TPU v7x, 32 devices: a whole 2x2x4 slice. The times are simulated.
32 devices in a mesh: slab: 2 (over y), wide: 4 (over z), narrow: 2 (over x), inner: 2 (over core).
Axes of the slice: x: 2, y: 2, z: 4, core: 2. Of those that a mesh axis runs over, the one named last changes fastest.
Arguments:
- templates: bfloat16 [16384, 1024], P(('slab', 'wide', 'narrow', 'inner')), parts along dimension 0, may hold values from -6 to 6
- leaf_inverse: bfloat16 [16384, 512], P(('slab', 'wide', 'narrow', 'inner')), parts along dimension 0, may hold values from -0.25 to 0.25
- v_basis: bfloat16 [4, 16384, 128], P(None, ('slab', 'wide', 'narrow', 'inner')), parts along dimension 1, may hold values from -0.09375 to 0.09375
- u_basis: bfloat16 [4, 16384, 128], P(None, ('slab', 'wide', 'narrow', 'inner')), parts along dimension 1, may hold values from -0.5 to 0.5
- coupling: bfloat16 [4, 32, 128, 256], P(None, ('slab', 'wide', 'narrow', 'inner')), parts along dimension 1, may hold values from -1 to 1, as said below
Outputs:
- filtered: bfloat16 [16384, 1024], P(('slab', 'wide', 'narrow', 'inner')), parts along dimension 0
There are 2 independent parts, one for each index of `slab`. A program takes and returns all parts, laid end to end along the dimension named above; each array names one. Nothing has to cross between parts.
Inputs may be any that keep to these rules, and one draw needn't show every extreme that they name: For each level, all leaves in the same child of a node hold the same rows of that node's coupling inverse (the first child the upper 128 rows, the second the lower).
All inputs are finite; a program needn't handle non-finite values.
Results may differ from a plain program's by a relative error of at most 0.013.
Values may be sent and summed in bfloat16 or wider, within the bound.
No kernel may reach another device: no remote copies, remote signals or barrier semaphores. Data moves between devices by JAX's collectives and lax.ppermute only.
A program may use at most 64 MiB of HBM per device.

v0:
```python
import jax
import jax.numpy as jnp
from jax import lax
from jax.sharding import PartitionSpec as P


def swapped(x, axis, stride):
    return lax.ppermute(x, axis, [(i, i ^ 1 << stride) for i in range(lax.axis_size(axis))])


def partner(value, bit, bits_inner, bits_narrow):
    if bit < bits_inner:
        return swapped(value, "inner", bit)
    if bit < bits_inner + bits_narrow:
        return swapped(value, "narrow", bit - bits_inner)
    return swapped(value, "wide", bit - bits_inner - bits_narrow)


def sibling(value, bit, bits_inner, bits_narrow):
    if bit < bits_inner:
        return swapped(value, "inner", bit)
    if bit < bits_inner + bits_narrow:
        return swapped(value, "narrow", bit - bits_inner)
    return swapped(value, "wide", bit - bits_inner - bits_narrow)


def side_bit(bit, bits_inner, bits_narrow):
    if bit < bits_inner:
        return lax.axis_index("inner") >> bit & 1
    if bit < bits_inner + bits_narrow:
        return lax.axis_index("narrow") >> bit - bits_inner & 1
    return lax.axis_index("wide") >> bit - bits_inner - bits_narrow & 1


def doubled(value, count, bits_inner, bits_narrow):
    for bit in range(count):
        value = value + partner(value, bit, bits_inner, bits_narrow)
    return value


def order_pair(mine, theirs, lower):
    first_part = jnp.where(lower, mine, theirs)
    second_part = jnp.where(lower, theirs, mine)
    return jnp.concatenate([first_part, second_part], axis=0)


def with_sibling(child, section, lower, bits_inner, bits_narrow):
    rounded_child = child.astype(jnp.bfloat16)
    return order_pair(
        rounded_child, sibling(rounded_child, section, bits_inner, bits_narrow), lower
    )


def on_device(templates, leaf_inverse, v_basis, u_basis, coupling):
    bits_inner = lax.axis_size("inner").bit_length() - 1
    bits_narrow = lax.axis_size("narrow").bit_length() - 1
    current = jnp.dot(leaf_inverse, templates, preferred_element_type=jnp.float32)
    for section in range(v_basis.shape[0]):
        projected = jnp.einsum(
            "ir,it->rt",
            v_basis[section],
            current.astype(jnp.bfloat16),
            preferred_element_type=jnp.float32,
        )
        lower = side_bit(section, bits_inner, bits_narrow) == 0
        child = doubled(projected, section, bits_inner, bits_narrow)
        stacked = with_sibling(child, section, lower, bits_inner, bits_narrow)
        coefficients = jnp.dot(
            coupling[section, 0], stacked, preferred_element_type=jnp.float32
        ).astype(jnp.bfloat16)
        current = current - jnp.dot(
            u_basis[section], coefficients, preferred_element_type=jnp.float32
        )
    return current.astype(jnp.bfloat16)


def solution(mesh):
    placed = (
        P(("slab", "wide", "narrow", "inner"), None),
        P(("slab", "wide", "narrow", "inner"), None),
        P(None, ("slab", "wide", "narrow", "inner"), None),
        P(None, ("slab", "wide", "narrow", "inner"), None),
        P(None, ("slab", "wide", "narrow", "inner"), None, None),
    )
    return jax.shard_map(
        on_device,
        mesh=mesh,
        in_specs=placed,
        out_specs=P(("slab", "wide", "narrow", "inner"), None),
        check_vma=False,
    )
```

profile of v0, /device:TPU:0, one launch (start us, length us, event | category | flops | bytes accessed | tf_op | source)
XLA Modules:
  0.0 107.7 jit_solution(5043891186207462237)
XLA Ops:
  1.2 1.8 %fusion.70 = f32[512,1024]{1,0:T(8,128)S(1)} fusion(bf16[512,512]{1,0:T(8,128)(2,1)} %param.6, bf16[512,1024]{1,0:T(8,128)(2,1)S(1)} %copy-done), kind=kOutput, calls=%fused_computation.69 | convolution fusion | flops 536870912 | bytes 3670016 | tf_op jit(solution)/shard_map/dot_general | solution.py:57
  8.0 2.6 %bitcast_subtract_fusion.3 = f32[512,1024]{1,0:T(8,128)S(1)} fusion(f32[512,1024]{1,0:T(8,128)} %copy-done.2, bf16[128,1024]{1,0:T(8,128)(2,1)} %get-tuple-element.12, bf16[128,1024]{1,0:T(8,128)(2,1)S(1)} %get-tuple-element.11, bf16[4,512,128]{2,1,0:T(8,128)(2,1)} %param.8, bf16[4,1,128,256]{3,2,1,0:T(8,128)(2,1)} %param.9), kind=kOutput, calls=%fused_computation.4 | convolution fusion | flops 203030528 | bytes 4915200 | tf_op jit(solution)/shard_map/dot_general | solution.py:71
  12.4 1.5 %collective-permute-done.1 = f32[128,1024]{1,0:T(8,128)S(1)} collective-permute-done((f32[128,1024]{1,0:T(8,128)S(1)}, f32[128,1024]{1,0:T(8,128)S(1)}, u32[]{:S(2)}, u32[]{:S(2)}) %collective-permute-start.1) | collective-permute-done | bytes 524320 | tf_op jit(solution)/shard_map/ppermute | solution.py:8
  14.0 2.9 %collective-permute-start.2 = (bf16[128,1024]{1,0:T(8,128)(2,1)S(1)}, bf16[128,1024]{1,0:T(8,128)(2,1)}, u32[]{:S(2)}, u32[]{:S(2)}) collective-permute-start(bf16[128,1024]{1,0:T(8,128)(2,1)S(1)} %add_convert_fusion.2), channel_id=1, source_target_pairs={{0,2},{2,0},{1,3},{3,1},{4,6},{6,4},{5,7},{7,5},{8,10},{10,8},{9,1... | collective-permute-start | bytes 786440 | tf_op jit(solution)/shard_map/ppermute | solution.py:8
  17.0 6.7 %collective-permute-done.2 = bf16[128,1024]{1,0:T(8,128)(2,1)} collective-permute-done((bf16[128,1024]{1,0:T(8,128)(2,1)S(1)}, bf16[128,1024]{1,0:T(8,128)(2,1)}, u32[]{:S(2)}, u32[]{:S(2)}) %collective-permute-start.2) | collective-permute-done | bytes 262176 | tf_op jit(solution)/shard_map/ppermute | solution.py:8
  23.7 1.8 %broadcast_select_fusion.5 = (bf16[128,1024]{1,0:T(8,128)(2,1)}, bf16[128,1024]{1,0:T(8,128)(2,1)}) fusion(bf16[128,1024]{1,0:T(8,128)(2,1)S(1)} %add_convert_fusion.2, bf16[128,1024]{1,0:T(8,128)(2,1)} %collective-permute-done.2, pred[]{:T(512)S(6)} %eq.13), kind=kLoop, calls=%fused_computation.38 | loop fusion | flops 262144 | bytes 1048577 | tf_op jit(solution)/shard_map/jit(_where)/select_n | solution.py:42
  25.5 2.6 %bitcast_subtract_fusion.2 = f32[512,1024]{1,0:T(8,128)S(1)} fusion(f32[512,1024]{1,0:T(8,128)} %copy-done.1, bf16[128,1024]{1,0:T(8,128)(2,1)} %get-tuple-element.10, bf16[128,1024]{1,0:T(8,128)(2,1)} %get-tuple-element.9, bf16[4,512,128]{2,1,0:T(8,128)(2,1)} %param.8, bf16[4,1,128,256]{3,2,1,0:T(8,128)(2,1)} %param.9), kind=kOutput, calls=%fused_computation.3 | convolution fusion | flops 203030528 | bytes 4915200 | tf_op jit(solution)/shard_map/dot_general | solution.py:71
  29.4 1.9 %collective-permute-done.3 = f32[128,1024]{1,0:T(8,128)S(1)} collective-permute-done((f32[128,1024]{1,0:T(8,128)S(1)}, f32[128,1024]{1,0:T(8,128)S(1)}, u32[]{:S(2)}, u32[]{:S(2)}) %collective-permute-start.3) | collective-permute-done | bytes 524320 | tf_op jit(solution)/shard_map/ppermute | solution.py:8
  31.4 1.8 %collective-permute-start.4 = (f32[128,1024]{1,0:T(8,128)S(1)}, f32[128,1024]{1,0:T(8,128)S(1)}, u32[]{:S(2)}, u32[]{:S(2)}) collective-permute-start(f32[128,1024]{1,0:T(8,128)S(1)} %add.19), channel_id=1, source_target_pairs={{0,2},{2,0},{1,3},{3,1},{4,6},{6,4},{5,7},{7,5},{8,10},{10,8},{9,1... | collective-permute-start | bytes 1572872 | tf_op jit(solution)/shard_map/ppermute | solution.py:8
  33.2 12.2 %collective-permute-done.4 = f32[128,1024]{1,0:T(8,128)S(1)} collective-permute-done((f32[128,1024]{1,0:T(8,128)S(1)}, f32[128,1024]{1,0:T(8,128)S(1)}, u32[]{:S(2)}, u32[]{:S(2)}) %collective-permute-start.4) | collective-permute-done | bytes 524320 | tf_op jit(solution)/shard_map/ppermute | solution.py:8
  45.5 1.9 %collective-permute-start.5 = (bf16[128,1024]{1,0:T(8,128)(2,1)S(1)}, bf16[128,1024]{1,0:T(8,128)(2,1)}, u32[]{:S(2)}, u32[]{:S(2)}) collective-permute-start(bf16[128,1024]{1,0:T(8,128)(2,1)S(1)} %add_convert_fusion.1), channel_id=1, source_target_pairs={{0,4},{4,0},{8,12},{12,8},{1,5},{5,1},{9,13},{13,9},{2,6},{6,2},{1... | collective-permute-start | bytes 786440 | tf_op jit(solution)/shard_map/ppermute | solution.py:8
  47.4 5.9 %collective-permute-done.5 = bf16[128,1024]{1,0:T(8,128)(2,1)} collective-permute-done((bf16[128,1024]{1,0:T(8,128)(2,1)S(1)}, bf16[128,1024]{1,0:T(8,128)(2,1)}, u32[]{:S(2)}, u32[]{:S(2)}) %collective-permute-start.5) | collective-permute-done | bytes 262176 | tf_op jit(solution)/shard_map/ppermute | solution.py:8
  53.3 1.8 %broadcast_select_fusion.3 = (bf16[128,1024]{1,0:T(8,128)(2,1)}, bf16[128,1024]{1,0:T(8,128)(2,1)}) fusion(bf16[128,1024]{1,0:T(8,128)(2,1)S(1)} %add_convert_fusion.1, bf16[128,1024]{1,0:T(8,128)(2,1)} %collective-permute-done.5, pred[]{:T(512)S(6)} %eq.14), kind=kLoop, calls=%fused_computation.36 | loop fusion | flops 262144 | bytes 1048577 | tf_op jit(solution)/shard_map/jit(_where)/select_n | solution.py:42
  55.1 3.2 %bitcast_subtract_fusion.1 = f32[512,1024]{1,0:T(8,128)} fusion(f32[512,1024]{1,0:T(8,128)S(1)} %bitcast_subtract_fusion.2, bf16[128,1024]{1,0:T(8,128)(2,1)} %get-tuple-element.8, bf16[128,1024]{1,0:T(8,128)(2,1)} %get-tuple-element.7, bf16[4,512,128]{2,1,0:T(8,128)(2,1)} %param.8, bf16[4,1,128,256]{3,2,1,0:T(8,128)(2,1)} %param.9), kind=kOutput, calls=%fused_computation.2 | convolution fusion | flops 203030528 | bytes 4915200 | tf_op jit(solution)/shard_map/dot_general | solution.py:71
  58.3 1.9 %convolution_bitcast_fusion = f32[128,1024]{1,0:T(8,128)S(1)} fusion(f32[512,1024]{1,0:T(8,128)} %bitcast_subtract_fusion.1, bf16[4,512,128]{2,1,0:T(8,128)(2,1)} %param.7), kind=kOutput, calls=%fused_computation.5 | convolution fusion | flops 134742016 | bytes 2752512 | tf_op jit(solution)/shard_map/ir,it->rt/dot_general | solution.py:59
  60.3 1.9 %collective-permute-done.6 = f32[128,1024]{1,0:T(8,128)S(1)} collective-permute-done((f32[128,1024]{1,0:T(8,128)S(1)}, f32[128,1024]{1,0:T(8,128)S(1)}, u32[]{:S(2)}, u32[]{:S(2)}) %collective-permute-start.6) | collective-permute-done | bytes 524320 | tf_op jit(solution)/shard_map/ppermute | solution.py:8
  62.3 1.7 %collective-permute-start.7 = (f32[128,1024]{1,0:T(8,128)S(1)}, f32[128,1024]{1,0:T(8,128)S(1)}, u32[]{:S(2)}, u32[]{:S(2)}) collective-permute-start(f32[128,1024]{1,0:T(8,128)S(1)} %add.21), channel_id=1, source_target_pairs={{0,2},{2,0},{1,3},{3,1},{4,6},{6,4},{5,7},{7,5},{8,10},{10,8},{9,1... | collective-permute-start | bytes 1572872 | tf_op jit(solution)/shard_map/ppermute | solution.py:8
  64.0 12.3 %collective-permute-done.7 = f32[128,1024]{1,0:T(8,128)S(1)} collective-permute-done((f32[128,1024]{1,0:T(8,128)S(1)}, f32[128,1024]{1,0:T(8,128)S(1)}, u32[]{:S(2)}, u32[]{:S(2)}) %collective-permute-start.7) | collective-permute-done | bytes 524320 | tf_op jit(solution)/shard_map/ppermute | solution.py:8
  76.4 1.8 %collective-permute-start.8 = (f32[128,1024]{1,0:T(8,128)S(1)}, f32[128,1024]{1,0:T(8,128)S(1)}, u32[]{:S(2)}, u32[]{:S(2)}) collective-permute-start(f32[128,1024]{1,0:T(8,128)S(1)} %add.22), channel_id=1, source_target_pairs={{0,4},{4,0},{8,12},{12,8},{1,5},{5,1},{9,13},{13,9},{2,6},{6,2},{1... | collective-permute-start | bytes 1572872 | tf_op jit(solution)/shard_map/ppermute | solution.py:8
  78.2 11.4 %collective-permute-done.8 = f32[128,1024]{1,0:T(8,128)S(1)} collective-permute-done((f32[128,1024]{1,0:T(8,128)S(1)}, f32[128,1024]{1,0:T(8,128)S(1)}, u32[]{:S(2)}, u32[]{:S(2)}) %collective-permute-start.8) | collective-permute-done | bytes 524320 | tf_op jit(solution)/shard_map/ppermute | solution.py:8
  89.6 2.8 %collective-permute-start.9 = (bf16[128,1024]{1,0:T(8,128)(2,1)S(1)}, bf16[128,1024]{1,0:T(8,128)(2,1)}, u32[]{:S(2)}, u32[]{:S(2)}) collective-permute-start(bf16[128,1024]{1,0:T(8,128)(2,1)S(1)} %add_convert_fusion), channel_id=1, source_target_pairs={{0,8},{4,12},{8,0},{12,4},{1,9},{5,13},{9,1},{13,5},{2,10},{6,14},... | collective-permute-start | bytes 786440 | tf_op jit(solution)/shard_map/ppermute | solution.py:8
  92.5 10.6 %collective-permute-done.9 = bf16[128,1024]{1,0:T(8,128)(2,1)} collective-permute-done((bf16[128,1024]{1,0:T(8,128)(2,1)S(1)}, bf16[128,1024]{1,0:T(8,128)(2,1)}, u32[]{:S(2)}, u32[]{:S(2)}) %collective-permute-start.9) | collective-permute-done | bytes 262176 | tf_op jit(solution)/shard_map/ppermute | solution.py:8
  103.0 1.8 %broadcast_select_fusion.1 = (bf16[128,1024]{1,0:T(8,128)(2,1)}, bf16[128,1024]{1,0:T(8,128)(2,1)}) fusion(bf16[128,1024]{1,0:T(8,128)(2,1)S(1)} %add_convert_fusion, bf16[128,1024]{1,0:T(8,128)(2,1)} %collective-permute-done.9, pred[]{:T(512)S(6)} %eq.15), kind=kLoop, calls=%fused_computation.34 | loop fusion | flops 262144 | bytes 1048577 | tf_op jit(solution)/shard_map/jit(_where)/select_n | solution.py:42
  104.8 2.8 %fusion = bf16[512,1024]{1,0:T(8,128)(2,1)} fusion(f32[512,1024]{1,0:T(8,128)S(1)} %copy-done.3, bf16[128,1024]{1,0:T(8,128)(2,1)} %get-tuple-element.6, bf16[128,1024]{1,0:T(8,128)(2,1)} %get-tuple-element.5, bf16[4,512,128]{2,1,0:T(8,128)(2,1)} %param.8, bf16[4,1,128,256]{3,2,1,0:T(8,128)(2,1)} %param.9), kind=kOutput, calls=%fused_computation.1 | convolution fusion | flops 203554816 | bytes 3866624 | tf_op jit(solution)/shard_map/dot_general | solution.py:71
  (23 shorter events, 9.9 us)
Async XLA Ops:
  0.0 1.2 %copy-start = (bf16[512,1024]{1,0:T(8,128)(2,1)S(1)}, bf16[512,1024]{1,0:T(8,128)(2,1)}, u32[]{:S(2)}) copy-start(bf16[512,1024]{1,0:T(8,128)(2,1)} %param.5) | copy-start | bytes 3145732
  3.0 1.3 %copy-start.2 = (f32[512,1024]{1,0:T(8,128)}, f32[512,1024]{1,0:T(8,128)S(1)}, u32[]{:S(2)}) copy-start(f32[512,1024]{1,0:T(8,128)S(1)} %fusion.70) | copy-start | bytes 6291460
  5.6 1.7 %collective-permute-start = (bf16[128,1024]{1,0:T(8,128)(2,1)S(1)}, bf16[128,1024]{1,0:T(8,128)(2,1)S(1)}, u32[]{:S(2)}, u32[]{:S(2)}) collective-permute-start(bf16[128,1024]{1,0:T(8,128)(2,1)S(1)} %fusion.1), channel_id=1, source_target_pairs={{0,1},{1,0},{2,3},{3,2},{4,5},{5,4},{6,7},{7,6},{8,9},{9,8},{10,11... | collective-permute-start | bytes 786440 | tf_op jit(solution)/shard_map/ppermute | solution.py:8
  10.6 14.9 %copy-start.1 = (f32[512,1024]{1,0:T(8,128)}, f32[512,1024]{1,0:T(8,128)S(1)}, u32[]{:S(2)}) copy-start(f32[512,1024]{1,0:T(8,128)S(1)} %bitcast_subtract_fusion.3) | copy-start | bytes 6291460
  12.0 2.0 %collective-permute-start.1 = (f32[128,1024]{1,0:T(8,128)S(1)}, f32[128,1024]{1,0:T(8,128)S(1)}, u32[]{:S(2)}, u32[]{:S(2)}) collective-permute-start(f32[128,1024]{1,0:T(8,128)S(1)} %convolution_bitcast_fusion.2), channel_id=1, source_target_pairs={{0,1},{1,0},{2,3},{3,2},{4,5},{5,4},{6,7},{7,6},{8,9},{9,8},{10,11... | collective-permute-start | bytes 1572872 | tf_op jit(solution)/shard_map/ppermute | solution.py:8
  14.0 9.6 %collective-permute-start.2 = (bf16[128,1024]{1,0:T(8,128)(2,1)S(1)}, bf16[128,1024]{1,0:T(8,128)(2,1)}, u32[]{:S(2)}, u32[]{:S(2)}) collective-permute-start(bf16[128,1024]{1,0:T(8,128)(2,1)S(1)} %add_convert_fusion.2), channel_id=1, source_target_pairs={{0,2},{2,0},{1,3},{3,1},{4,6},{6,4},{5,7},{7,5},{8,10},{10,8},{9,1... | collective-permute-start | bytes 786440 | tf_op jit(solution)/shard_map/ppermute | solution.py:8
  29.4 2.0 %collective-permute-start.3 = (f32[128,1024]{1,0:T(8,128)S(1)}, f32[128,1024]{1,0:T(8,128)S(1)}, u32[]{:S(2)}, u32[]{:S(2)}) collective-permute-start(f32[128,1024]{1,0:T(8,128)S(1)} %convolution_bitcast_fusion.1), channel_id=1, source_target_pairs={{0,1},{1,0},{2,3},{3,2},{4,5},{5,4},{6,7},{7,6},{8,9},{9,8},{10,11... | collective-permute-start | bytes 1572872 | tf_op jit(solution)/shard_map/ppermute | solution.py:8
  31.4 14.0 %collective-permute-start.4 = (f32[128,1024]{1,0:T(8,128)S(1)}, f32[128,1024]{1,0:T(8,128)S(1)}, u32[]{:S(2)}, u32[]{:S(2)}) collective-permute-start(f32[128,1024]{1,0:T(8,128)S(1)} %add.19), channel_id=1, source_target_pairs={{0,2},{2,0},{1,3},{3,1},{4,6},{6,4},{5,7},{7,5},{8,10},{10,8},{9,1... | collective-permute-start | bytes 1572872 | tf_op jit(solution)/shard_map/ppermute | solution.py:8
  45.5 7.8 %collective-permute-start.5 = (bf16[128,1024]{1,0:T(8,128)(2,1)S(1)}, bf16[128,1024]{1,0:T(8,128)(2,1)}, u32[]{:S(2)}, u32[]{:S(2)}) collective-permute-start(bf16[128,1024]{1,0:T(8,128)(2,1)S(1)} %add_convert_fusion.1), channel_id=1, source_target_pairs={{0,4},{4,0},{8,12},{12,8},{1,5},{5,1},{9,13},{13,9},{2,6},{6,2},{1... | collective-permute-start | bytes 786440 | tf_op jit(solution)/shard_map/ppermute | solution.py:8
  60.2 2.0 %collective-permute-start.6 = (f32[128,1024]{1,0:T(8,128)S(1)}, f32[128,1024]{1,0:T(8,128)S(1)}, u32[]{:S(2)}, u32[]{:S(2)}) collective-permute-start(f32[128,1024]{1,0:T(8,128)S(1)} %convolution_bitcast_fusion), channel_id=1, source_target_pairs={{0,1},{1,0},{2,3},{3,2},{4,5},{5,4},{6,7},{7,6},{8,9},{9,8},{10,11... | collective-permute-start | bytes 1572872 | tf_op jit(solution)/shard_map/ppermute | solution.py:8
  62.3 42.6 %copy-start.3 = (f32[512,1024]{1,0:T(8,128)S(1)}, f32[512,1024]{1,0:T(8,128)}, u32[]{:S(2)}) copy-start(f32[512,1024]{1,0:T(8,128)} %bitcast_subtract_fusion.1) | copy-start | bytes 6291460
  62.3 14.0 %collective-permute-start.7 = (f32[128,1024]{1,0:T(8,128)S(1)}, f32[128,1024]{1,0:T(8,128)S(1)}, u32[]{:S(2)}, u32[]{:S(2)}) collective-permute-start(f32[128,1024]{1,0:T(8,128)S(1)} %add.21), channel_id=1, source_target_pairs={{0,2},{2,0},{1,3},{3,1},{4,6},{6,4},{5,7},{7,5},{8,10},{10,8},{9,1... | collective-permute-start | bytes 1572872 | tf_op jit(solution)/shard_map/ppermute | solution.py:8
  76.4 13.2 %collective-permute-start.8 = (f32[128,1024]{1,0:T(8,128)S(1)}, f32[128,1024]{1,0:T(8,128)S(1)}, u32[]{:S(2)}, u32[]{:S(2)}) collective-permute-start(f32[128,1024]{1,0:T(8,128)S(1)} %add.22), channel_id=1, source_target_pairs={{0,4},{4,0},{8,12},{12,8},{1,5},{5,1},{9,13},{13,9},{2,6},{6,2},{1... | collective-permute-start | bytes 1572872 | tf_op jit(solution)/shard_map/ppermute | solution.py:8
  89.6 13.4 %collective-permute-start.9 = (bf16[128,1024]{1,0:T(8,128)(2,1)S(1)}, bf16[128,1024]{1,0:T(8,128)(2,1)}, u32[]{:S(2)}, u32[]{:S(2)}) collective-permute-start(bf16[128,1024]{1,0:T(8,128)(2,1)S(1)} %add_convert_fusion), channel_id=1, source_target_pairs={{0,8},{4,12},{8,0},{12,4},{1,9},{5,13},{9,1},{13,5},{2,10},{6,14},... | collective-permute-start | bytes 786440 | tf_op jit(solution)/shard_map/ppermute | solution.py:8
where the time goes:
time: 108 us
  waiting for transfers between devices  65.6 us (61%)
  matrix products  18.8 us (17%)
  starting transfers between devices  14.1 us (13%)
  other arithmetic  6.51 us (6%)
  local copies, waits for them, and re-layouts  2.57 us (2%)
    ppermute x10, waiting for transfers between devices, swapped(): lax.ppermute(x, axis, [(i, i ^ 1 << stride) for i in range(lax.axis_size(...  65.6 us
    ppermute x10, starting transfers between devices, swapped(): lax.ppermute(x, axis, [(i, i ^ 1 << stride) for i in range(lax.axis_size(...  14.1 us
    dot_general x4, matrix products, on_device(): jnp.dot(u_basis[section], coefficients, preferred_element_type=jnp.float32)  11.2 us
    select_n x4, other arithmetic, order_pair(): first_part = jnp.where(lower, mine, theirs)  6.11 us
    dot_general x4, matrix products, on_device(): jnp.einsum('ir,it->rt', v_basis[section], current.astype(jnp.bfloat16), p...  5.84 us
    unnamed x8, local copies, waits for them, and re-layouts  2.57 us
  transfers between devices with their start and end apart: 10, of which 10 were waited for; matrix products, arithmetic and copies ran while one was open for 0% of the time, Pallas kernels for 0%

commit v1 on v0

v1 whole, which is shorter than its diff:
```python
import jax
import jax.numpy as jnp
from jax import lax
from jax.sharding import PartitionSpec as P

F32 = jnp.float32
BF16 = jnp.bfloat16


def bit_axes():
    bits = []
    for axis in ("inner", "narrow", "wide"):
        for stride in range(lax.axis_size(axis).bit_length() - 1):
            bits.append((axis, stride))
    return bits


def swap(x, bit, bits):
    axis, stride = bits[bit]
    n = lax.axis_size(axis)
    return lax.ppermute(x, axis, [(i, i ^ (1 << stride)) for i in range(n)])


def side(bit, bits):
    axis, stride = bits[bit]
    return (lax.axis_index(axis) >> stride) & 1


def cols(x, start, width):
    return lax.dynamic_slice_in_dim(x, start, width, axis=x.ndim - 1)


def reduce_half(x, bit, bits):
    w = x.shape[-1] // 2
    h = side(bit, bits)
    keep = cols(x, h * w, w)
    send = cols(x, (1 - h) * w, w)
    return keep + swap(send, bit, bits)


def gather_half(x, bit, bits):
    w = x.shape[-1]
    h = side(bit, bits)
    both = jnp.concatenate([x, swap(x, bit, bits), x], axis=-1)
    return cols(both, h * w, 2 * w)


def hi_lo(w):
    hi = w.astype(BF16)
    lo = (w - hi.astype(F32)).astype(BF16)
    return hi, lo


def on_device(templates, leaf_inverse, v_basis, u_basis, coupling):
    bits = bit_axes()
    levels, pixels, rank = v_basis.shape
    c0 = jnp.dot(leaf_inverse, templates, preferred_element_type=F32)
    c0b = c0.astype(BF16)
    proj = jnp.einsum("lir,it->lrt", v_basis, c0b, preferred_element_type=F32)
    cross = jnp.einsum("lir,kis->lkrs", v_basis, u_basis, preferred_element_type=F32)

    couple = []
    for s in range(levels):
        lower = side(s, bits) == 0
        mine = coupling[s, 0]
        theirs = swap(mine, s, bits)
        rows = []
        for c in (mine, theirs):
            rolled = jnp.concatenate([c[:, rank:], c[:, :rank]], axis=1)
            rows.append(jnp.where(lower, c, rolled))
        couple.append(jnp.concatenate(rows, axis=0))

    weights = []
    for s in range(levels - 1):
        w = cross[s + 1:, s].reshape((levels - 1 - s) * rank, rank)
        for j in range(s):
            w = w + swap(w, j, bits)
        w_sib = swap(w, s, bits)
        parts = hi_lo(w) + hi_lo(w_sib)
        weights.append(jnp.concatenate(parts, axis=1))

    rest = proj[1:]
    if levels > 1:
        rest = reduce_half(rest, 0, bits)
    own_coefs = []
    for s in range(levels):
        if s == 0:
            mine = proj[0]
        else:
            mine = rest[0]
            rest = rest[1:]
            if rest.shape[0] > 0:
                rest = reduce_half(rest, s, bits)
        mine_b = mine.astype(BF16)
        stacked = jnp.concatenate([mine_b, swap(mine_b, s, bits)], axis=0)
        coefs = jnp.dot(couple[s], stacked, preferred_element_type=F32).astype(BF16)
        own_coefs.append(coefs[:rank])
        if s < levels - 1:
            w = coefs.shape[1] // 2
            half = cols(coefs, side(s, bits) * w, w)
            co, cs = half[:rank], half[rank:]
            fix = jnp.dot(
                weights[s],
                jnp.concatenate([co, co, cs, cs], axis=0),
                preferred_element_type=F32,
            )
            rest = rest - fix.reshape(rest.shape)

    full = []
    for s in range(levels):
        c = own_coefs[s]
        for j in reversed(range(s)):
            c = gather_half(c, j, bits)
        full.append(c)
    u_all = jnp.transpose(u_basis, (1, 0, 2)).reshape(pixels, levels * rank)
    early = levels - 1
    current = c0
    if early > 0:
        current = current - jnp.dot(
            u_all[:, : early * rank],
            jnp.concatenate(full[:early], axis=0),
            preferred_element_type=F32,
        )
    current = current - jnp.dot(
        u_basis[levels - 1], full[levels - 1], preferred_element_type=F32
    )
    return current.astype(BF16)


def solution(mesh):
    placed = (
        P(("slab", "wide", "narrow", "inner"), None),
        P(("slab", "wide", "narrow", "inner"), None),
        P(None, ("slab", "wide", "narrow", "inner"), None),
        P(None, ("slab", "wide", "narrow", "inner"), None),
        P(None, ("slab", "wide", "narrow", "inner"), None, None),
    )
    return jax.shard_map(
        on_device,
        mesh=mesh,
        in_specs=placed,
        out_specs=P(("slab", "wide", "narrow", "inner"), None),
        check_vma=False,
    )
```

time: 108 us -> 79.5 us (0.74)
  waiting for transfers between devices: 65.6 us -> 24.4 us
  local copies, waits for them, and re-layouts: 2.57 us -> 18.1 us
  matrix products: 18.8 us -> 10 us
  starting transfers between devices: 14.1 us -> 16.7 us
  other arithmetic: 6.51 us -> 8.72 us
    ppermute x10 -> x23, waiting for transfers between devices: 65.6 us -> 24.4 us  [swap(): return lax.ppermute(x, axis, [(i, i ^ 1 << stride) for i in range(n)])]
    dot_general x9 -> x11, matrix products: 18.8 us -> 9.3 us  [the longest x1 3.42 us: on_device(): jnp.dot(u_basis[levels - 1], full[levels - 1], preferred_element_type=F32)]
    slice x0 -> x19, local copies, waits for them, and re-layouts: none -> 8.53 us  [the longest x6 4.63 us: on_device(): rolled = jnp.concatenate([c[:, rank:], c[:, :rank]], axis=1)]
    ppermute x10 -> x23, starting transfers between devices: 14.1 us -> 16.7 us  [swap(): return lax.ppermute(x, axis, [(i, i ^ 1 << stride) for i in range(n)])]
    dynamic_slice x0 -> x6, local copies, waits for them, and re-layouts: none -> 2.15 us  [cols(): return lax.dynamic_slice_in_dim(x, start, width, axis=x.ndim - 1)]
    concatenate x0 -> x5, other arithmetic: none -> 1.78 us  [gather_half(): both = jnp.concatenate([x, swap(x, bit, bits), x], axis=-1)]
    squeeze x0 -> x1, local copies, waits for them, and re-layouts: none -> 1.77 us  [on_device(): mine = coupling[s, 0]]
    select_n x4 -> x5, other arithmetic: 6.11 us -> 4.36 us  [on_device(): rows.append(jnp.where(lower, c, rolled))]
  transfers between devices with their start and end apart: 10 -> 23, of which waited for: 10 -> 10; matrix products, arithmetic and copies ran while one was open for 0% -> 37% of each run, Pallas kernels for 0% -> 0%
where the time goes in v1:
time: 79.5 us; the launch traced here: 78.5 us
  waiting for transfers between devices  24.4 us (31%)
  local copies, waits for them, and re-layouts  18.1 us (23%)
  starting transfers between devices  16.7 us (21%)
  matrix products  10 us (13%)
  other arithmetic  8.72 us (11%)
    ppermute x23, waiting for transfers between devices, swap(): return lax.ppermute(x, axis, [(i, i ^ 1 << stride) for i in range(n)])  24.4 us
    ppermute x23, starting transfers between devices, swap(): return lax.ppermute(x, axis, [(i, i ^ 1 << stride) for i in range(n)])  16.7 us
    slice x6, local copies, waits for them, and re-layouts, on_device(): rolled = jnp.concatenate([c[:, rank:], c[:, :rank]], axis=1)  4.63 us
    select_n x5, other arithmetic, on_device(): rows.append(jnp.where(lower, c, rolled))  4.36 us
    unnamed x36, local copies, waits for them, and re-layouts  4.25 us
    dot_general x1, matrix products, on_device(): jnp.dot(u_basis[levels - 1], full[levels - 1], preferred_element_type=F32)  3.42 us
    dynamic_slice x6, local copies, waits for them, and re-layouts, cols(): return lax.dynamic_slice_in_dim(x, start, width, axis=x.ndim - 1)  2.15 us
    concatenate x5, other arithmetic, gather_half(): both = jnp.concatenate([x, swap(x, bit, bits), x], axis=-1)  1.78 us
  transfers between devices with their start and end apart: 23, of which 10 were waited for; matrix products, arithmetic and copies ran while one was open for 37% of the time, Pallas kernels for 0%

profile of v1, /device:TPU:0, one launch (start us, length us, event | category | flops | bytes accessed | tf_op | source)
XLA Modules:
  0.0 78.5 jit_solution(2608284480093480746)
XLA Ops:
  0.0 1.8 %slice_bitcast_fusion.1 = (bf16[128,256]{1,0:T(8,128)(2,1)}, bf16[128,256]{1,0:T(8,128)(2,1)}, bf16[128,256]{1,0:T(8,128)(2,1)}, bf16[128,256]{1,0:T(8,128)(2,1)}) fusion(bf16[4,1,128,256]{3,2,1,0:T(8,128)(2,1)} %param.9), kind=kLoop, calls=%fused_computation.139 | loop fusion | bytes 524288 | tf_op jit(solution)/shard_map/squeeze | solution.py:65
  1.8 4.0 %collective-permute-start.14 = (bf16[128,256]{1,0:T(8,128)(2,1)}, bf16[128,256]{1,0:T(8,128)(2,1)S(1)}, u32[]{:S(2)}, u32[]{:S(2)}) collective-permute-start(bf16[128,256]{1,0:T(8,128)(2,1)} %get-tuple-element.23), channel_id=1, source_target_pairs={{0,8},{4,12},{8,0},{12,4},{1,9},{5,13},{9,1},{13,5},{2,10},{6,14},... | collective-permute-start | bytes 196616 | tf_op jit(solution)/shard_map/ppermute | solution.py:21
  5.8 1.5 %collective-permute-start.2 = (bf16[128,256]{1,0:T(8,128)(2,1)}, bf16[128,256]{1,0:T(8,128)(2,1)}, u32[]{:S(2)}, u32[]{:S(2)}) collective-permute-start(bf16[128,256]{1,0:T(8,128)(2,1)} %get-tuple-element.24), channel_id=1, source_target_pairs={{0,2},{2,0},{1,3},{3,1},{4,6},{6,4},{5,7},{7,5},{8,10},{10,8},{9,1... | collective-permute-start | bytes 196616 | tf_op jit(solution)/shard_map/ppermute | solution.py:21
  7.3 1.6 %collective-permute-start.7 = (bf16[128,256]{1,0:T(8,128)(2,1)}, bf16[128,256]{1,0:T(8,128)(2,1)}, u32[]{:S(2)}, u32[]{:S(2)}) collective-permute-start(bf16[128,256]{1,0:T(8,128)(2,1)} %get-tuple-element.26), channel_id=1, source_target_pairs={{0,4},{4,0},{8,12},{12,8},{1,5},{5,1},{9,13},{13,9},{2,6},{6,2},{1... | collective-permute-start | bytes 196616 | tf_op jit(solution)/shard_map/ppermute | solution.py:21
  8.9 1.7 %convolution_bitcast_fusion = f32[4,4,128,128]{3,2,0,1:T(8,128)S(1)} fusion(bf16[4,512,128]{2,1,0:T(8,128)(2,1)} %param.8, bf16[4,512,128]{2,1,0:T(8,128)(2,1)} %param.7), kind=kOutput, calls=%fused_computation.3 | convolution fusion | flops 268435456 | bytes 2097152 | tf_op jit(solution)/shard_map/lir,kis->lkrs/dot_general | solution.py:60
  12.3 1.5 %fusion.113 = (bf16[128,128]{1,0:T(8,128)(2,1)}, bf16[128,128]{1,0:T(8,128)(2,1)}, bf16[128,128]{1,0:T(8,128)(2,1)}, bf16[128,128]{1,0:T(8,128)(2,1)}) fusion(bf16[128,256]{1,0:T(8,128)(2,1)} %get-tuple-element.25, bf16[128,256]{1,0:T(8,128)(2,1)} %get-tuple-element.26), kind=kLoop, calls=%fused_computation.170 | loop fusion | bytes 262144 | tf_op jit(solution)/shard_map/slice | solution.py:69
  13.8 1.0 %copy.10 = bf16[4,512,128]{1,2,0:T(8,128)(2,1)} copy(bf16[4,512,128]{2,1,0:T(8,128)(2,1)S(1)} %copy-done.4) | data formatting | bytes 1048576 | tf_op args[2]
  16.1 1.8 %fusion.117 = f32[512,1024]{1,0:T(8,128)S(1)} fusion(bf16[512,512]{1,0:T(8,128)(2,1)} %param.6, bf16[512,1024]{1,0:T(8,128)(2,1)S(1)} %copy-done), kind=kOutput, calls=%fused_computation.174 | convolution fusion | flops 536870912 | bytes 3670016 | tf_op jit(solution)/shard_map/dot_general | solution.py:57
  19.3 1.3 %slice.180 = f32[3,128,1024]{2,1,0:T(8,128)} slice(f32[4,128,1024]{2,1,0:T(8,128)S(1)} %bitcast.76), slice={[1:4], [0:128], [0:1024]} | slice | bytes 3145728 | tf_op jit(solution)/shard_map/slice | solution.py:82
  20.6 1.7 %maximum_select_fusion.6 = (bf16[128,256]{1,0:T(8,128)(2,1)}, bf16[128,256]{1,0:T(8,128)(2,1)}, bf16[128,256]{1,0:T(8,128)(2,1)}, bf16[128,256]{1,0:T(8,128)(2,1)}) fusion(bf16[128,128]{1,0:T(8,128)(2,1)S(1)} %get-tuple-element.32, bf16[128,128]{1,0:T(8,128)(2,1)S(1)} %get-tuple-element.31, pred[]{:T(512)S(6)} %eq.15, bf16[4,1,128,256]{3,2,1,0:T(8,128)(2,1)} %param.9, ...), kind=kLoop, calls=%fused_computation.131 | loop fusion | flops 655360 | bytes 786436 | tf_op jit(solution)/shard_map/jit(_where)/select_n | solution.py:70
  22.3 2.1 %constant_dynamic-slice_fusion.8 = f32[3,128,512]{2,1,0:T(8,128)} fusion(f32[3,128,1024]{2,1,0:T(8,128)} %slice.180, s32[]{:T(128)S(6)} %select_n.82), kind=kLoop, calls=%fused_computation.153 | loop fusion | bytes 1572868 | tf_op jit(solution)/shard_map/dynamic_slice | solution.py:30
  32.6 4.2 %collective-permute-done.17 = f32[128,128]{1,0:T(8,128)S(1)} collective-permute-done((f32[128,128]{1,0:T(8,128)S(1)}, f32[128,128]{1,0:T(8,128)S(1)}, u32[]{:S(2)}, u32[]{:S(2)}) %collective-permute-start.17) | collective-permute-done | bytes 65568 | tf_op jit(solution)/shard_map/ppermute | solution.py:21
  37.1 4.1 %collective-permute-done.18 = f32[128,128]{1,0:T(8,128)S(1)} collective-permute-done((f32[128,128]{1,0:T(8,128)S(1)}, f32[128,128]{1,0:T(8,128)S(1)}, u32[]{:S(2)}, u32[]{:S(2)}) %collective-permute-start.18) | collective-permute-done | bytes 65568 | tf_op jit(solution)/shard_map/ppermute | solution.py:21
  43.7 2.1 %collective-permute-start.8 = (f32[2,128,256]{2,1,0:T(8,128)S(1)}, f32[2,128,256]{2,1,0:T(8,128)S(1)}, u32[]{:S(2)}, u32[]{:S(2)}) collective-permute-start(f32[2,128,256]{2,1,0:T(8,128)S(1)} %constant_dynamic-slice_fusion.5), channel_id=1, source_target_pairs={{0,2},{2,0},{1,3},{3,1},{4,6},{6,4},{5,7},{7,5},{8,10},{10,8},{9,1... | collective-permute-start | bytes 786440 | tf_op jit(solution)/shard_map/ppermute | solution.py:21
  45.8 3.2 %collective-permute-done.5 = bf16[128,512]{1,0:T(8,128)(2,1)S(1)} collective-permute-done((bf16[128,512]{1,0:T(8,128)(2,1)S(1)}, bf16[128,512]{1,0:T(8,128)(2,1)S(1)}, u32[]{:S(2)}, u32[]{:S(2)}) %collective-permute-start.5) | collective-permute-done | bytes 131104 | tf_op jit(solution)/shard_map/ppermute | solution.py:21
  49.5 2.2 %collective-permute-done.8 = f32[2,128,256]{2,1,0:T(8,128)S(1)} collective-permute-done((f32[2,128,256]{2,1,0:T(8,128)S(1)}, f32[2,128,256]{2,1,0:T(8,128)S(1)}, u32[]{:S(2)}, u32[]{:S(2)}) %collective-permute-start.8) | collective-permute-done | bytes 262176 | tf_op jit(solution)/shard_map/ppermute | solution.py:21
  52.6 1.3 %collective-permute-start.15 = (f32[1,128,128]{2,1,0:T(8,128)S(1)}, f32[1,128,128]{2,1,0:T(8,128)S(1)}, u32[]{:S(2)}, u32[]{:S(2)}) collective-permute-start(f32[1,128,128]{2,1,0:T(8,128)S(1)} %constant_dynamic-slice_fusion.3), channel_id=1, source_target_pairs={{0,4},{4,0},{8,12},{12,8},{1,5},{5,1},{9,13},{13,9},{2,6},{6,2},{1... | collective-permute-start | bytes 196616 | tf_op jit(solution)/shard_map/ppermute | solution.py:21
  53.9 2.2 %collective-permute-done.11 = bf16[128,256]{1,0:T(8,128)(2,1)S(1)} collective-permute-done((bf16[128,256]{1,0:T(8,128)(2,1)S(1)}, bf16[128,256]{1,0:T(8,128)(2,1)S(1)}, u32[]{:S(2)}, u32[]{:S(2)}) %collective-permute-start.11) | collective-permute-done | bytes 65568 | tf_op jit(solution)/shard_map/ppermute | solution.py:21
  57.7 4.6 %collective-permute-done.19 = bf16[128,128]{1,0:T(8,128)(2,1)S(1)} collective-permute-done((bf16[128,128]{1,0:T(8,128)(2,1)S(1)}, bf16[128,128]{1,0:T(8,128)(2,1)S(1)}, u32[]{:S(2)}, u32[]{:S(2)}) %collective-permute-start.19) | collective-permute-done | bytes 32800 | tf_op jit(solution)/shard_map/ppermute | solution.py:21
  63.1 1.0 %collective-permute-start.20 = (bf16[128,128]{0,1:T(8,128)(2,1)}, bf16[128,128]{0,1:T(8,128)(2,1)}, u32[]{:S(2)}, u32[]{:S(2)}) collective-permute-start(bf16[128,128]{0,1:T(8,128)(2,1)} %slice.231), channel_id=1, source_target_pairs={{0,4},{4,0},{8,12},{12,8},{1,5},{5,1},{9,13},{13,9},{2,6},{6,2},{1... | collective-permute-start | bytes 98312 | tf_op jit(solution)/shard_map/ppermute | solution.py:21
  64.1 2.0 %copy.12 = bf16[4,512,128]{1,2,0:T(8,128)(2,1)} copy(bf16[4,512,128]{2,1,0:T(8,128)(2,1)} %param.8) | data formatting | bytes 1048576 | tf_op args[3]
  68.6 1.6 %collective-permute-start.21 = (bf16[128,256]{0,1:T(8,128)(2,1)S(1)}, bf16[128,256]{0,1:T(8,128)(2,1)S(1)}, u32[]{:S(2)}, u32[]{:S(2)}) collective-permute-start(bf16[128,256]{0,1:T(8,128)(2,1)S(1)} %fusion.88), channel_id=1, source_target_pairs={{0,2},{2,0},{1,3},{3,1},{4,6},{6,4},{5,7},{7,5},{8,10},{10,8},{9,1... | collective-permute-start | bytes 196616 | tf_op jit(solution)/shard_map/ppermute | solution.py:21
  70.2 1.8 %collective-permute-done.12 = bf16[128,256]{1,0:T(8,128)(2,1)S(1)} collective-permute-done((bf16[128,256]{1,0:T(8,128)(2,1)S(1)}, bf16[128,256]{1,0:T(8,128)(2,1)S(1)}, u32[]{:S(2)}, u32[]{:S(2)}) %collective-permute-start.12) | collective-permute-done | bytes 65568 | tf_op jit(solution)/shard_map/ppermute | solution.py:21
  75.1 3.4 %fusion = bf16[512,1024]{1,0:T(8,128)(2,1)} fusion(f32[512,1024]{1,0:T(8,128)S(1)} %fusion.117, f32[1024,512]{0,1:T(8,128)S(1)} %fusion.3, s32[]{:T(128)S(6)} %select_n.83, bf16[128,512]{0,1:T(8,128)(2,1)S(1)} %fusion.53, bf16[128,512]{0,1:T(8,128)(2,1)S(1)} %collective-permute-done.22, bf16[4,512,128]{2,1,0:T(8,128)(2,1)} %param.8), kind=kOutput, calls=%fused_computation.1 | convolution fusion | flops 136577024 | bytes 5636100 | tf_op jit(solution)/shard_map/dot_general | solution.py:124
  (120 shorter events, 24.4 us)
Async XLA Ops:
  1.8 30.7 %collective-permute-start.14 = (bf16[128,256]{1,0:T(8,128)(2,1)}, bf16[128,256]{1,0:T(8,128)(2,1)S(1)}, u32[]{:S(2)}, u32[]{:S(2)}) collective-permute-start(bf16[128,256]{1,0:T(8,128)(2,1)} %get-tuple-element.23), channel_id=1, source_target_pairs={{0,8},{4,12},{8,0},{12,4},{1,9},{5,13},{9,1},{13,5},{2,10},{6,14},... | collective-permute-start | bytes 196616 | tf_op jit(solution)/shard_map/ppermute | solution.py:21
  5.8 19.5 %collective-permute-start.2 = (bf16[128,256]{1,0:T(8,128)(2,1)}, bf16[128,256]{1,0:T(8,128)(2,1)}, u32[]{:S(2)}, u32[]{:S(2)}) collective-permute-start(bf16[128,256]{1,0:T(8,128)(2,1)} %get-tuple-element.24), channel_id=1, source_target_pairs={{0,2},{2,0},{1,3},{3,1},{4,6},{6,4},{5,7},{7,5},{8,10},{10,8},{9,1... | collective-permute-start | bytes 196616 | tf_op jit(solution)/shard_map/ppermute | solution.py:21
  7.3 19.1 %collective-permute-start = (bf16[128,256]{1,0:T(8,128)(2,1)}, bf16[128,256]{1,0:T(8,128)(2,1)}, u32[]{:S(2)}, u32[]{:S(2)}) collective-permute-start(bf16[128,256]{1,0:T(8,128)(2,1)} %get-tuple-element.25), channel_id=1, source_target_pairs={{0,1},{1,0},{2,3},{3,2},{4,5},{5,4},{6,7},{7,6},{8,9},{9,8},{10,11... | collective-permute-start | bytes 196616 | tf_op jit(solution)/shard_map/ppermute | solution.py:21
  7.3 20.2 %collective-permute-start.7 = (bf16[128,256]{1,0:T(8,128)(2,1)}, bf16[128,256]{1,0:T(8,128)(2,1)}, u32[]{:S(2)}, u32[]{:S(2)}) collective-permute-start(bf16[128,256]{1,0:T(8,128)(2,1)} %get-tuple-element.26), channel_id=1, source_target_pairs={{0,4},{4,0},{8,12},{12,8},{1,5},{5,1},{9,13},{13,9},{2,6},{6,2},{1... | collective-permute-start | bytes 196616 | tf_op jit(solution)/shard_map/ppermute | solution.py:21
  11.2 17.4 %collective-permute-start.16 = (f32[128,128]{1,0:T(8,128)}, f32[128,128]{1,0:T(8,128)}, u32[]{:S(2)}, u32[]{:S(2)}) collective-permute-start(f32[128,128]{1,0:T(8,128)} %slice_bitcast_fusion), channel_id=1, source_target_pairs={{0,1},{1,0},{2,3},{3,2},{4,5},{5,4},{6,7},{7,6},{8,9},{9,8},{10,11... | collective-permute-start | bytes 196616 | tf_op jit(solution)/shard_map/ppermute | solution.py:21
  25.3 11.6 %collective-permute-start.9 = (f32[256,128]{1,0:T(8,128)S(1)}, f32[256,128]{1,0:T(8,128)S(1)}, u32[]{:S(2)}, u32[]{:S(2)}) collective-permute-start(f32[256,128]{1,0:T(8,128)S(1)} %bitcast.81), channel_id=1, source_target_pairs={{0,1},{1,0},{2,3},{3,2},{4,5},{5,4},{6,7},{7,6},{8,9},{9,8},{10,11... | collective-permute-start | bytes 393224 | tf_op jit(solution)/shard_map/ppermute | solution.py:21
  26.4 14.8 %collective-permute-start.4 = (f32[384,128]{1,0:T(8,128)S(1)}, f32[384,128]{1,0:T(8,128)S(1)}, u32[]{:S(2)}, u32[]{:S(2)}) collective-permute-start(f32[384,128]{1,0:T(8,128)S(1)} %bitcast.78), channel_id=1, source_target_pairs={{0,1},{1,0},{2,3},{3,2},{4,5},{5,4},{6,7},{7,6},{8,9},{9,8},{10,11... | collective-permute-start | bytes 589832 | tf_op jit(solution)/shard_map/ppermute | solution.py:21
  27.5 13.8 %collective-permute-start.1 = (bf16[128,1024]{1,0:T(8,128)(2,1)}, bf16[128,1024]{1,0:T(8,128)(2,1)S(1)}, u32[]{:S(2)}, u32[]{:S(2)}) collective-permute-start(bf16[128,1024]{1,0:T(8,128)(2,1)} %fusion.35), channel_id=1, source_target_pairs={{0,1},{1,0},{2,3},{3,2},{4,5},{5,4},{6,7},{7,6},{8,9},{9,8},{10,11... | collective-permute-start | bytes 786440 | tf_op jit(solution)/shard_map/ppermute | solution.py:21
  28.7 13.8 %collective-permute-start.3 = (f32[3,128,512]{2,1,0:T(8,128)}, f32[3,128,512]{2,1,0:T(8,128)S(1)}, u32[]{:S(2)}, u32[]{:S(2)}) collective-permute-start(f32[3,128,512]{2,1,0:T(8,128)} %constant_dynamic-slice_fusion.8), channel_id=1, source_target_pairs={{0,1},{1,0},{2,3},{3,2},{4,5},{5,4},{6,7},{7,6},{8,9},{9,8},{10,11... | collective-permute-start | bytes 2359304 | tf_op jit(solution)/shard_map/ppermute | solution.py:21
  32.5 4.3 %collective-permute-start.17 = (f32[128,128]{1,0:T(8,128)S(1)}, f32[128,128]{1,0:T(8,128)S(1)}, u32[]{:S(2)}, u32[]{:S(2)}) collective-permute-start(f32[128,128]{1,0:T(8,128)S(1)} %fusion.108), channel_id=1, source_target_pairs={{0,2},{2,0},{1,3},{3,1},{4,6},{6,4},{5,7},{7,5},{8,10},{10,8},{9,1... | collective-permute-start | bytes 196616 | tf_op jit(solution)/shard_map/ppermute | solution.py:21
  36.9 4.3 %collective-permute-start.18 = (f32[128,128]{1,0:T(8,128)S(1)}, f32[128,128]{1,0:T(8,128)S(1)}, u32[]{:S(2)}, u32[]{:S(2)}) collective-permute-start(f32[128,128]{1,0:T(8,128)S(1)} %get-tuple-element.7), channel_id=1, source_target_pairs={{0,4},{4,0},{8,12},{12,8},{1,5},{5,1},{9,13},{13,9},{2,6},{6,2},{1... | collective-permute-start | bytes 196616 | tf_op jit(solution)/shard_map/ppermute | solution.py:21
  37.0 6.6 %collective-permute-start.10 = (f32[256,128]{1,0:T(8,128)S(1)}, f32[256,128]{1,0:T(8,128)S(1)}, u32[]{:S(2)}, u32[]{:S(2)}) collective-permute-start(f32[256,128]{1,0:T(8,128)S(1)} %get-tuple-element.14), channel_id=1, source_target_pairs={{0,2},{2,0},{1,3},{3,1},{4,6},{6,4},{5,7},{7,5},{8,10},{10,8},{9,1... | collective-permute-start | bytes 393224 | tf_op jit(solution)/shard_map/ppermute | solution.py:21
  43.5 5.4 %collective-permute-start.5 = (bf16[128,512]{1,0:T(8,128)(2,1)S(1)}, bf16[128,512]{1,0:T(8,128)(2,1)S(1)}, u32[]{:S(2)}, u32[]{:S(2)}) collective-permute-start(bf16[128,512]{1,0:T(8,128)(2,1)S(1)} %fusion.56), channel_id=1, source_target_pairs={{0,2},{2,0},{1,3},{3,1},{4,6},{6,4},{5,7},{7,5},{8,10},{10,8},{9,1... | collective-permute-start | bytes 393224 | tf_op jit(solution)/shard_map/ppermute | solution.py:21
  43.7 8.0 %collective-permute-start.8 = (f32[2,128,256]{2,1,0:T(8,128)S(1)}, f32[2,128,256]{2,1,0:T(8,128)S(1)}, u32[]{:S(2)}, u32[]{:S(2)}) collective-permute-start(f32[2,128,256]{2,1,0:T(8,128)S(1)} %constant_dynamic-slice_fusion.5), channel_id=1, source_target_pairs={{0,2},{2,0},{1,3},{3,1},{4,6},{6,4},{5,7},{7,5},{8,10},{10,8},{9,1... | collective-permute-start | bytes 786440 | tf_op jit(solution)/shard_map/ppermute | solution.py:21
  51.8 4.3 %collective-permute-start.11 = (bf16[128,256]{1,0:T(8,128)(2,1)S(1)}, bf16[128,256]{1,0:T(8,128)(2,1)S(1)}, u32[]{:S(2)}, u32[]{:S(2)}) collective-permute-start(bf16[128,256]{1,0:T(8,128)(2,1)S(1)} %fusion.89), channel_id=1, source_target_pairs={{0,4},{4,0},{8,12},{12,8},{1,5},{5,1},{9,13},{13,9},{2,6},{6,2},{1... | collective-permute-start | bytes 196616 | tf_op jit(solution)/shard_map/ppermute | solution.py:21
  52.6 4.6 %collective-permute-start.15 = (f32[1,128,128]{2,1,0:T(8,128)S(1)}, f32[1,128,128]{2,1,0:T(8,128)S(1)}, u32[]{:S(2)}, u32[]{:S(2)}) collective-permute-start(f32[1,128,128]{2,1,0:T(8,128)S(1)} %constant_dynamic-slice_fusion.3), channel_id=1, source_target_pairs={{0,4},{4,0},{8,12},{12,8},{1,5},{5,1},{9,13},{13,9},{2,6},{6,2},{1... | collective-permute-start | bytes 196616 | tf_op jit(solution)/shard_map/ppermute | solution.py:21
  57.4 4.9 %collective-permute-start.19 = (bf16[128,128]{1,0:T(8,128)(2,1)S(1)}, bf16[128,128]{1,0:T(8,128)(2,1)S(1)}, u32[]{:S(2)}, u32[]{:S(2)}) collective-permute-start(bf16[128,128]{1,0:T(8,128)(2,1)S(1)} %fusion.93), channel_id=1, source_target_pairs={{0,8},{4,12},{8,0},{12,4},{1,9},{5,13},{9,1},{13,5},{2,10},{6,14},... | collective-permute-start | bytes 98312 | tf_op jit(solution)/shard_map/ppermute | solution.py:21
  57.6 16.3 %slice-start = ((bf16[256,1024]{1,0:T(8,128)(2,1)}), bf16[128,1024]{1,0:T(8,128)(2,1)S(1)}, s32[]{:S(2)}) async-start(bf16[256,1024]{1,0:T(8,128)(2,1)} %copy-done.5), calls=%async_computation | async-start | bytes 524288 | tf_op jit(solution)/shard_map/slice | solution.py:97
  63.1 4.7 %collective-permute-start.20 = (bf16[128,128]{0,1:T(8,128)(2,1)}, bf16[128,128]{0,1:T(8,128)(2,1)}, u32[]{:S(2)}, u32[]{:S(2)}) collective-permute-start(bf16[128,128]{0,1:T(8,128)(2,1)} %slice.231), channel_id=1, source_target_pairs={{0,4},{4,0},{8,12},{12,8},{1,5},{5,1},{9,13},{13,9},{2,6},{6,2},{1... | collective-permute-start | bytes 98312 | tf_op jit(solution)/shard_map/ppermute | solution.py:21
  67.1 5.1 %collective-permute-start.6 = (bf16[128,512]{1,0:T(8,128)(2,1)S(1)}, bf16[128,512]{1,0:T(8,128)(2,1)S(1)}, u32[]{:S(2)}, u32[]{:S(2)}) collective-permute-start(bf16[128,512]{1,0:T(8,128)(2,1)S(1)} %slice.183), channel_id=1, source_target_pairs={{0,1},{1,0},{2,3},{3,2},{4,5},{5,4},{6,7},{7,6},{8,9},{9,8},{10,11... | collective-permute-start | bytes 393224 | tf_op jit(solution)/shard_map/ppermute | solution.py:21
  67.2 4.8 %collective-permute-start.12 = (bf16[128,256]{1,0:T(8,128)(2,1)S(1)}, bf16[128,256]{1,0:T(8,128)(2,1)S(1)}, u32[]{:S(2)}, u32[]{:S(2)}) collective-permute-start(bf16[128,256]{1,0:T(8,128)(2,1)S(1)} %slice.191), channel_id=1, source_target_pairs={{0,2},{2,0},{1,3},{3,1},{4,6},{6,4},{5,7},{7,5},{8,10},{10,8},{9,1... | collective-permute-start | bytes 196616 | tf_op jit(solution)/shard_map/ppermute | solution.py:21
  68.6 4.5 %collective-permute-start.21 = (bf16[128,256]{0,1:T(8,128)(2,1)S(1)}, bf16[128,256]{0,1:T(8,128)(2,1)S(1)}, u32[]{:S(2)}, u32[]{:S(2)}) collective-permute-start(bf16[128,256]{0,1:T(8,128)(2,1)S(1)} %fusion.88), channel_id=1, source_target_pairs={{0,2},{2,0},{1,3},{3,1},{4,6},{6,4},{5,7},{7,5},{8,10},{10,8},{9,1... | collective-permute-start | bytes 196616 | tf_op jit(solution)/shard_map/ppermute | solution.py:21
  72.1 1.7 %collective-permute-start.13 = (bf16[128,512]{1,0:T(8,128)(2,1)S(1)}, bf16[128,512]{1,0:T(8,128)(2,1)S(1)}, u32[]{:S(2)}, u32[]{:S(2)}) collective-permute-start(bf16[128,512]{1,0:T(8,128)(2,1)S(1)} %fusion.55), channel_id=1, source_target_pairs={{0,1},{1,0},{2,3},{3,2},{4,5},{5,4},{6,7},{7,6},{8,9},{9,8},{10,11... | collective-permute-start | bytes 393224 | tf_op jit(solution)/shard_map/ppermute | solution.py:21
  73.7 1.4 %collective-permute-start.22 = (bf16[128,512]{0,1:T(8,128)(2,1)S(1)}, bf16[128,512]{0,1:T(8,128)(2,1)S(1)}, u32[]{:S(2)}, u32[]{:S(2)}) collective-permute-start(bf16[128,512]{0,1:T(8,128)(2,1)S(1)} %fusion.53), channel_id=1, source_target_pairs={{0,1},{1,0},{2,3},{3,2},{4,5},{5,4},{6,7},{7,6},{8,9},{9,8},{10,11... | collective-permute-start | bytes 393224 | tf_op jit(solution)/shard_map/ppermute | solution.py:21
  (17 other events, 148.1 us)

commit v2 on v1

v2 whole, which is shorter than its diff:
```python
import jax
import jax.numpy as jnp
from jax import lax
from jax.sharding import PartitionSpec as P

F32 = jnp.float32
BF16 = jnp.bfloat16


def bit_axes():
    bits = []
    for axis in ("inner", "narrow", "wide"):
        for stride in range(lax.axis_size(axis).bit_length() - 1):
            bits.append((axis, stride))
    return bits


def swap(x, bit, bits):
    axis, stride = bits[bit]
    n = lax.axis_size(axis)
    return lax.ppermute(x, axis, [(i, i ^ (1 << stride)) for i in range(n)])


def side(bit, bits):
    axis, stride = bits[bit]
    return (lax.axis_index(axis) >> stride) & 1


def cols(x, start, width):
    return lax.dynamic_slice_in_dim(x, start, width, axis=x.ndim - 1)


def reduce_half(x, bit, bits):
    w = x.shape[-1] // 2
    h = side(bit, bits)
    keep = cols(x, h * w, w)
    send = cols(x, (1 - h) * w, w)
    return keep + swap(send, bit, bits)


def gather_half(x, bit, bits):
    w = x.shape[-1]
    h = side(bit, bits)
    both = jnp.concatenate([x, swap(x, bit, bits), x], axis=-1)
    return cols(both, h * w, 2 * w)


def on_device(templates, leaf_inverse, v_basis, u_basis, coupling):
    bits = bit_axes()
    levels, pixels, rank = v_basis.shape
    width = templates.shape[1]
    c0 = jnp.dot(leaf_inverse, templates, preferred_element_type=F32)
    c0b = c0.astype(BF16)

    cross = jnp.einsum("lir,kis->lkrs", v_basis, u_basis, preferred_element_type=F32)
    mine_c = coupling[:, 0]
    partial = [cross[s + 1:, s].reshape(-1, rank) for s in range(levels - 1)]
    w_own, theirs_c = [None] * levels, []
    for b in range(levels):
        c = mine_c[b]
        parts = [jnp.concatenate([c[:, :rank], c[:, rank:]], axis=0).astype(F32)]
        parts += partial[b:]
        got = swap(jnp.concatenate(parts, axis=0), b, bits)
        theirs = got[: 2 * rank].astype(BF16)
        theirs_c.append(jnp.concatenate([theirs[:rank], theirs[rank:]], axis=1))
        at = 2 * rank
        for s in range(b, levels - 1):
            n = partial[s].shape[0]
            recv = got[at : at + n]
            at += n
            if s == b:
                w_own[s] = jnp.concatenate([partial[s], recv], axis=1)
            else:
                partial[s] = partial[s] + recv
    theirs_c = jnp.stack(theirs_c)
    lower = jnp.stack([side(s, bits) == 0 for s in range(levels)])[:, None, None]
    first = jnp.concatenate([mine_c[:, :, :rank], theirs_c[:, :, :rank]], axis=1)
    second = jnp.concatenate([mine_c[:, :, rank:], theirs_c[:, :, rank:]], axis=1)
    couple = jnp.concatenate(
        [jnp.where(lower, first, second), jnp.where(lower, second, first)], axis=2
    )

    proj0 = jnp.dot(v_basis[0].T, c0b, preferred_element_type=F32)
    rest = None
    if levels > 1:
        half = width // 2
        h = side(0, bits)
        keep = jnp.einsum(
            "lir,it->lrt", v_basis[1:], cols(c0b, h * half, half),
            preferred_element_type=F32,
        )
        send = jnp.einsum(
            "lir,it->lrt", v_basis[1:], cols(c0b, (1 - h) * half, half),
            preferred_element_type=F32,
        )
        rest = keep + swap(send, 0, bits)
    own_coefs = []
    for s in range(levels):
        if s == 0:
            mine = proj0
        else:
            mine = rest[0]
            rest = rest[1:]
            if rest.shape[0] > 0:
                rest = reduce_half(rest, s, bits)
        mine_b = mine.astype(BF16)
        stacked = jnp.concatenate([mine_b, swap(mine_b, s, bits)], axis=0)
        coefs = jnp.dot(couple[s], stacked, preferred_element_type=F32).astype(BF16)
        own_coefs.append(coefs[:rank])
        if s < levels - 1:
            w = coefs.shape[1] // 2
            piece = cols(coefs, side(s, bits) * w, w).astype(F32)
            fix = jnp.dot(
                w_own[s], piece, preferred_element_type=F32,
                precision=lax.Precision.HIGHEST,
            )
            rest = rest - fix.reshape(rest.shape)

    full = [own_coefs[0]] + [None] * (levels - 1)
    pending = {s: own_coefs[s] for s in range(1, levels)}
    for j in reversed(range(levels - 1)):
        group = [s for s in range(j + 1, levels)]
        joined = gather_half(jnp.stack([pending[s] for s in group]), j, bits)
        for i, s in enumerate(group):
            pending[s] = joined[i]
    for s in range(1, levels):
        full[s] = pending[s]
    current = c0
    for s in range(levels):
        current = current - jnp.dot(u_basis[s], full[s], preferred_element_type=F32)
    return current.astype(BF16)


def solution(mesh):
    placed = (
        P(("slab", "wide", "narrow", "inner"), None),
        P(("slab", "wide", "narrow", "inner"), None),
        P(None, ("slab", "wide", "narrow", "inner"), None),
        P(None, ("slab", "wide", "narrow", "inner"), None),
        P(None, ("slab", "wide", "narrow", "inner"), None, None),
    )
    return jax.shard_map(
        on_device,
        mesh=mesh,
        in_specs=placed,
        out_specs=P(("slab", "wide", "narrow", "inner"), None),
        check_vma=False,
    )
```

time: 79.5 us -> 79.1 us (level)
  local copies, waits for them, and re-layouts: 18.1 us -> 6.41 us
  waiting for transfers between devices: 24.4 us -> 35.7 us
  starting transfers between devices: 16.7 us -> 14.2 us
  matrix products: 10 us -> 12.3 us
    ppermute x23 -> x14, waiting for transfers between devices: 24.4 us -> 35.7 us  [swap(): return lax.ppermute(x, axis, [(i, i ^ 1 << stride) for i in range(n)])]
    slice x17 -> x14, local copies, waits for them, and re-layouts: 8.49 us -> 2.78 us  [the longest x1 1.68 us: on_device(): mine_c[:, :, :rank]]
    select_n x5 -> x1, other arithmetic: 4.36 us -> 0.21 us  [on_device(): jnp.where(lower, second, first)]
    unnamed x36 -> x25, local copies, waits for them, and re-layouts: 4.25 us -> 1.65 us
    ppermute x23 -> x14, starting transfers between devices: 16.7 us -> 14.2 us  [swap(): return lax.ppermute(x, axis, [(i, i ^ 1 << stride) for i in range(n)])]
    sub x2, other arithmetic: 0.31 us -> 2.39 us  [on_device(): rest = rest - fix.reshape(rest.shape)]
    dynamic_slice x6 -> x2, local copies, waits for them, and re-layouts: 2.15 us -> 0.72 us  [cols(): return lax.dynamic_slice_in_dim(x, start, width, axis=x.ndim - 1)]
    another operation x0 -> x11, other arithmetic: none -> 1.35 us
  transfers between devices with their start and end apart: 23 -> 14, of which waited for: 10 -> 10; matrix products, arithmetic and copies ran while one was open for 37% -> 22% of each run, Pallas kernels for 0% -> 0%
where the time goes in v2:
time: 79.1 us; the launch traced here: 78.6 us
  waiting for transfers between devices  35.7 us (45%)
  starting transfers between devices  14.2 us (18%)
  matrix products  12.3 us (16%)
  other arithmetic  9.51 us (12%)
  local copies, waits for them, and re-layouts  6.41 us (8%)
    ppermute x14, waiting for transfers between devices, swap(): return lax.ppermute(x, axis, [(i, i ^ 1 << stride) for i in range(n)])  35.7 us
    ppermute x14, starting transfers between devices, swap(): return lax.ppermute(x, axis, [(i, i ^ 1 << stride) for i in range(n)])  14.2 us
    dot_general x4, matrix products, on_device(): current = current - jnp.dot(u_basis[s], full[s], preferred_element_type=F32)  2.84 us
    sub x2, other arithmetic, on_device(): rest = rest - fix.reshape(rest.shape)  2.39 us
    concatenate x3, other arithmetic, gather_half(): both = jnp.concatenate([x, swap(x, bit, bits), x], axis=-1)  2.09 us
    dot_general x1, matrix products, on_device(): c0 = jnp.dot(leaf_inverse, templates, preferred_element_type=F32)  2.08 us
    dot_general x4, matrix products, on_device(): coefs = jnp.dot(couple[s], stacked, preferred_element_type=F32).astype(BF16)  1.99 us
    add x3, other arithmetic, on_device(): partial[s] = partial[s] + recv  1.81 us
  transfers between devices with their start and end apart: 14, of which 10 were waited for; matrix products, arithmetic and copies ran while one was open for 22% of the time, Pallas kernels for 0%

profile of v2, /device:TPU:0, one launch (start us, length us, event | category | flops | bytes accessed | tf_op | source)
XLA Modules:
  0.0 78.6 jit_solution(18221576444839987345)
XLA Ops:
  1.7 4.0 %collective-permute-start.3 = (bf16[256,128]{1,0:T(8,128)(2,1)}, bf16[256,128]{1,0:T(8,128)(2,1)S(1)}, u32[]{:S(2)}, u32[]{:S(2)}) collective-permute-start(bf16[256,128]{1,0:T(8,128)(2,1)} %maximum_convert_fusion.3), channel_id=1, source_target_pairs={{0,8},{4,12},{8,0},{12,4},{1,9},{5,13},{9,1},{13,5},{2,10},{6,14},... | collective-permute-start | bytes 196616 | tf_op jit(solution)/shard_map/ppermute | solution.py:21
  5.7 1.7 %convolution_bitcast_fusion = f32[4,4,128,128]{3,2,0,1:T(8,128)S(1)} fusion(bf16[4,512,128]{2,1,0:T(8,128)(2,1)} %param.8, bf16[4,512,128]{2,1,0:T(8,128)(2,1)} %param.7), kind=kOutput, calls=%fused_computation.5 | convolution fusion | flops 268435456 | bytes 2097152 | tf_op jit(solution)/shard_map/lir,kis->lkrs/dot_general | solution.py:55
  8.6 2.1 %fusion.102 = (bf16[512,1024]{1,0:T(8,128)(2,1)S(1)}, f32[512,1024]{1,0:T(8,128)}) fusion(bf16[512,512]{1,0:T(8,128)(2,1)S(1)} %copy-done.7, bf16[512,1024]{1,0:T(8,128)(2,1)S(1)} %copy-done), kind=kOutput, calls=%fused_computation.165 | convolution fusion | flops 537395200 | bytes 4718592 | tf_op jit(solution)/shard_map/dot_general | solution.py:52
  12.2 1.3 %convolution_bitcast_fusion.1 = f32[3,128,512]{2,1,0:T(8,128)} fusion(bf16[512,1024]{1,0:T(8,128)(2,1)S(1)} %get-tuple-element.31, s32[]{:T(128)S(6)} %select_n.40, bf16[4,512,128]{2,1,0:T(8,128)(2,1)S(1)} %copy-done.2), kind=kOutput, calls=%fused_computation.6 | convolution fusion | flops 201326592 | bytes 1703940 | tf_op jit(solution)/shard_map/lir,it->lrt/dot_general | solution.py:92
  13.6 1.7 %fusion.92 = (bf16[4,128,128]{2,1,0:T(8,128)(2,1)}, bf16[4,128,128]{2,1,0:T(8,128)(2,1)}) fusion(bf16[4,128,256]{2,1,0:T(8,128)(2,1)} %bitcast.131), kind=kLoop, calls=%fused_computation.155 | loop fusion | bytes 524288 | tf_op jit(solution)/shard_map/slice | solution.py:77
  17.8 1.6 %collective-permute-start.1 = (f32[640,128]{1,0:T(8,128)S(1)}, f32[640,128]{1,0:T(8,128)S(1)}, u32[]{:S(2)}, u32[]{:S(2)}) collective-permute-start(f32[640,128]{1,0:T(8,128)S(1)} %pad_maximum_fusion.2), channel_id=1, source_target_pairs={{0,2},{2,0},{1,3},{3,1},{4,6},{6,4},{5,7},{7,5},{8,10},{10,8},{9,1... | collective-permute-start | bytes 983048 | tf_op jit(solution)/shard_map/ppermute | solution.py:21
  20.3 1.1 %convert.15 = bf16[1024,128]{1,0:T(8,128)(2,1)S(1)} convert(f32[1024,128]{1,0:T(8,128)} %collective-permute-done) | non-fusion elementwise | flops 131072 | bytes 786432 | tf_op jit(solution)/shard_map/convert.4
  21.5 6.5 %collective-permute-done.1 = f32[640,128]{1,0:T(8,128)S(1)} collective-permute-done((f32[640,128]{1,0:T(8,128)S(1)}, f32[640,128]{1,0:T(8,128)S(1)}, u32[]{:S(2)}, u32[]{:S(2)}) %collective-permute-start.1) | collective-permute-done | bytes 327712 | tf_op jit(solution)/shard_map/ppermute | solution.py:21
  28.1 1.6 %collective-permute-start.2 = (f32[384,128]{1,0:T(8,128)S(1)}, f32[384,128]{1,0:T(8,128)S(1)}, u32[]{:S(2)}, u32[]{:S(2)}) collective-permute-start(f32[384,128]{1,0:T(8,128)S(1)} %pad_maximum_fusion.6), channel_id=1, source_target_pairs={{0,4},{4,0},{8,12},{12,8},{1,5},{5,1},{9,13},{13,9},{2,6},{6,2},{1... | collective-permute-start | bytes 589832 | tf_op jit(solution)/shard_map/ppermute | solution.py:21
  29.8 4.9 %collective-permute-done.2 = f32[384,128]{1,0:T(8,128)S(1)} collective-permute-done((f32[384,128]{1,0:T(8,128)S(1)}, f32[384,128]{1,0:T(8,128)S(1)}, u32[]{:S(2)}, u32[]{:S(2)}) %collective-permute-start.2) | collective-permute-done | bytes 196640 | tf_op jit(solution)/shard_map/ppermute | solution.py:21
  35.7 1.3 %convolution_convert_fusion = bf16[256,1024]{1,0:T(8,128)(2,1)S(1)} fusion(bf16[128,1024]{1,0:T(8,128)(2,1)} %collective-permute-done.4, bf16[128,1024]{1,0:T(8,128)(2,1)} %fusion.1, bf16[4,256,128]{2,1,0:T(8,128)(2,1)S(1)} %get-tuple-element.6, bf16[4,256,128]{2,1,0:T(8,128)(2,1)S(1)} %get-tuple-element.5), kind=kOutput, calls=%fused_computation.7 | convolution fusion | flops 135790592 | bytes 1572864 | tf_op jit(solution)/shard_map/dot_general | solution.py:108
  37.5 1.4 %add_subtract_fusion = f32[3,128,512]{2,1,0:T(8,128)S(1)} fusion(f32[3,128,512]{2,1,0:T(8,128)S(1)} %bitcast.126, f32[3,128,512]{2,1,0:T(8,128)S(1)} %bitcast.125, f32[3,128,512]{2,1,0:T(8,128)} %collective-permute-done.5), kind=kLoop, calls=%fused_computation.22 | loop fusion | flops 393216 | bytes 3145728 | tf_op jit(solution)/shard_map/sub | solution.py:117
  39.0 1.5 %collective-permute-start.6 = (bf16[128,512]{1,0:T(8,128)(2,1)S(1)}, bf16[128,512]{1,0:T(8,128)(2,1)S(1)}, u32[]{:S(2)}, u32[]{:S(2)}) collective-permute-start(bf16[128,512]{1,0:T(8,128)(2,1)S(1)} %fusion.35), channel_id=1, source_target_pairs={{0,2},{2,0},{1,3},{3,1},{4,6},{6,4},{5,7},{7,5},{8,10},{10,8},{9,1... | collective-permute-start | bytes 393224 | tf_op jit(solution)/shard_map/ppermute | solution.py:21
  41.8 3.6 %collective-permute-done.6 = bf16[128,512]{1,0:T(8,128)(2,1)S(1)} collective-permute-done((bf16[128,512]{1,0:T(8,128)(2,1)S(1)}, bf16[128,512]{1,0:T(8,128)(2,1)S(1)}, u32[]{:S(2)}, u32[]{:S(2)}) %collective-permute-start.6) | collective-permute-done | bytes 131104 | tf_op jit(solution)/shard_map/ppermute | solution.py:21
  45.9 3.8 %collective-permute-done.7 = f32[2,128,256]{2,1,0:T(8,128)} collective-permute-done((f32[2,128,256]{2,1,0:T(8,128)}, f32[2,128,256]{2,1,0:T(8,128)}, u32[]{:S(2)}, u32[]{:S(2)}) %collective-permute-start.7) | collective-permute-done | bytes 262176 | tf_op jit(solution)/shard_map/ppermute | solution.py:21
  50.8 1.6 %collective-permute-start.8 = (bf16[128,256]{1,0:T(8,128)(2,1)S(1)}, bf16[128,256]{1,0:T(8,128)(2,1)S(1)}, u32[]{:S(2)}, u32[]{:S(2)}) collective-permute-start(bf16[128,256]{1,0:T(8,128)(2,1)S(1)} %fusion.68), channel_id=1, source_target_pairs={{0,4},{4,0},{8,12},{12,8},{1,5},{5,1},{9,13},{13,9},{2,6},{6,2},{1... | collective-permute-start | bytes 196616 | tf_op jit(solution)/shard_map/ppermute | solution.py:21
  52.9 2.2 %collective-permute-done.8 = bf16[128,256]{1,0:T(8,128)(2,1)S(1)} collective-permute-done((bf16[128,256]{1,0:T(8,128)(2,1)S(1)}, bf16[128,256]{1,0:T(8,128)(2,1)S(1)}, u32[]{:S(2)}, u32[]{:S(2)}) %collective-permute-start.8) | collective-permute-done | bytes 65568 | tf_op jit(solution)/shard_map/ppermute | solution.py:21
  55.4 1.4 %collective-permute-done.9 = f32[1,128,128]{2,1,0:T(8,128)S(1)} collective-permute-done((f32[1,128,128]{2,1,0:T(8,128)S(1)}, f32[1,128,128]{2,1,0:T(8,128)S(1)}, u32[]{:S(2)}, u32[]{:S(2)}) %collective-permute-start.9) | collective-permute-done | bytes 65568 | tf_op jit(solution)/shard_map/ppermute | solution.py:21
  57.3 4.5 %collective-permute-done.10 = bf16[128,128]{1,0:T(8,128)(2,1)S(1)} collective-permute-done((bf16[128,128]{1,0:T(8,128)(2,1)S(1)}, bf16[128,128]{1,0:T(8,128)(2,1)S(1)}, u32[]{:S(2)}, u32[]{:S(2)}) %collective-permute-start.10) | collective-permute-done | bytes 32800 | tf_op jit(solution)/shard_map/ppermute | solution.py:21
  63.1 3.0 %collective-permute-done.11 = bf16[1,128,128]{1,2,0:T(8,128)(2,1)S(1)} collective-permute-done((bf16[1,128,128]{1,2,0:T(8,128)(2,1)S(1)}, bf16[1,128,128]{1,2,0:T(8,128)(2,1)S(1)}, u32[]{:S(2)}, u32[]{:S(2)}) %collective-permute-start.11) | collective-permute-done | bytes 32800 | tf_op jit(solution)/shard_map/ppermute | solution.py:21
  67.4 4.1 %collective-permute-done.12 = bf16[2,128,256]{1,2,0:T(8,128)(2,1)S(1)} collective-permute-done((bf16[2,128,256]{1,2,0:T(8,128)(2,1)S(1)}, bf16[2,128,256]{1,2,0:T(8,128)(2,1)S(1)}, u32[]{:S(2)}, u32[]{:S(2)}) %collective-permute-start.12) | collective-permute-done | bytes 131104 | tf_op jit(solution)/shard_map/ppermute | solution.py:21
  72.2 1.7 %collective-permute-done.13 = bf16[3,128,512]{1,2,0:T(8,128)(2,1)S(1)} collective-permute-done((bf16[3,128,512]{1,2,0:T(8,128)(2,1)S(1)}, bf16[3,128,512]{1,2,0:T(8,128)(2,1)S(1)}, u32[]{:S(2)}, u32[]{:S(2)}) %collective-permute-start.13) | collective-permute-done | bytes 393248 | tf_op jit(solution)/shard_map/ppermute | solution.py:21
  73.9 1.2 %fusion.4 = bf16[3,128,1024]{1,2,0:T(8,128)(2,1)S(1)} fusion(s32[]{:T(128)S(6)} %select_n.47, bf16[1,128,512]{1,2,0:T(8,128)(2,1)S(1)} %copy.12, bf16[2,128,512]{1,2,0:T(8,128)(2,1)S(1)} %fusion.21, bf16[3,128,512]{1,2,0:T(8,128)(2,1)S(1)} %collective-permute-done.13), kind=kLoop, calls=%fused_computation.20 | loop fusion | flops 3932160 | bytes 1572868 | tf_op jit(solution)/shard_map/concatenate | solution.py:44
  77.1 1.5 %fusion = bf16[512,1024]{1,0:T(8,128)(2,1)} fusion(f32[1024,512]{0,1:T(8,128)S(1)} %fusion.23, f32[1024,512]{0,1:T(8,128)S(1)} %fusion.24, f32[1024,512]{0,1:T(8,128)S(1)} %fusion.25, f32[512,1024]{1,0:T(8,128)S(1)} %copy-done.1, bf16[256,1024]{1,0:T(8,128)(2,1)S(1)} %convolution_convert_fusion, bf16[4,512,128]{2,1,0:T(8,128)(2,1)S(1)} %copy-done.4), kind=kOutput, calls=%fused_computation.1 | convolution fusion | flops 136839168 | bytes 9830400 | tf_op jit(solution)/shard_map/dot_general | solution.py:130
  (98 shorter events, 18.7 us)
Async XLA Ops:
  0.0 8.6 %copy-start = (bf16[512,1024]{1,0:T(8,128)(2,1)S(1)}, bf16[512,1024]{1,0:T(8,128)(2,1)}, u32[]{:S(2)}) copy-start(bf16[512,1024]{1,0:T(8,128)(2,1)} %param.5) | copy-start | bytes 3145732
  1.7 6.9 %copy-start.7 = (bf16[512,512]{1,0:T(8,128)(2,1)S(1)}, bf16[512,512]{1,0:T(8,128)(2,1)}, u32[]{:S(2)}) copy-start(bf16[512,512]{1,0:T(8,128)(2,1)} %param.6) | copy-start | bytes 1572868
  1.7 14.3 %collective-permute-start.3 = (bf16[256,128]{1,0:T(8,128)(2,1)}, bf16[256,128]{1,0:T(8,128)(2,1)S(1)}, u32[]{:S(2)}, u32[]{:S(2)}) collective-permute-start(bf16[256,128]{1,0:T(8,128)(2,1)} %maximum_convert_fusion.3), channel_id=1, source_target_pairs={{0,8},{4,12},{8,0},{12,4},{1,9},{5,13},{9,1},{13,5},{2,10},{6,14},... | collective-permute-start | bytes 196616 | tf_op jit(solution)/shard_map/ppermute | solution.py:21
  8.6 2.1 %copy-start.2 = (bf16[4,512,128]{2,1,0:T(8,128)(2,1)S(1)}, bf16[4,512,128]{2,1,0:T(8,128)(2,1)}, u32[]{:S(2)}) copy-start(bf16[4,512,128]{2,1,0:T(8,128)(2,1)} %param.7) | copy-start | bytes 1572868
  8.6 7.4 %collective-permute-start = (f32[1024,128]{1,0:T(8,128)}, f32[1024,128]{1,0:T(8,128)}, u32[]{:S(2)}, u32[]{:S(2)}) collective-permute-start(f32[1024,128]{1,0:T(8,128)} %pad_maximum_fusion), channel_id=1, source_target_pairs={{0,1},{1,0},{2,3},{3,2},{4,5},{5,4},{6,7},{7,6},{8,9},{9,8},{10,11... | collective-permute-start | bytes 1572872 | tf_op jit(solution)/shard_map/ppermute | solution.py:21
  10.7 4.6 %slice-start = ((bf16[4,512,128]{2,1,0:T(8,128)(2,1)}), bf16[3,512,128]{2,1,0:T(8,128)(2,1)S(1)}, s32[]{:S(2)}) async-start(bf16[4,512,128]{2,1,0:T(8,128)(2,1)} %param.7), calls=%async_computation | async-start | bytes 786432
  11.7 23.9 %collective-permute-start.4 = (bf16[128,1024]{1,0:T(8,128)(2,1)}, bf16[128,1024]{1,0:T(8,128)(2,1)}, u32[]{:S(2)}, u32[]{:S(2)}) collective-permute-start(bf16[128,1024]{1,0:T(8,128)(2,1)} %fusion.1), channel_id=1, source_target_pairs={{0,1},{1,0},{2,3},{3,2},{4,5},{5,4},{6,7},{7,6},{8,9},{9,8},{10,11... | collective-permute-start | bytes 786440 | tf_op jit(solution)/shard_map/ppermute | solution.py:21
  13.5 24.0 %collective-permute-start.5 = (f32[3,128,512]{2,1,0:T(8,128)}, f32[3,128,512]{2,1,0:T(8,128)}, u32[]{:S(2)}, u32[]{:S(2)}) collective-permute-start(f32[3,128,512]{2,1,0:T(8,128)} %convolution_bitcast_fusion.1), channel_id=1, source_target_pairs={{0,1},{1,0},{2,3},{3,2},{4,5},{5,4},{6,7},{7,6},{8,9},{9,8},{10,11... | collective-permute-start | bytes 2359304 | tf_op jit(solution)/shard_map/ppermute | solution.py:21
  17.8 10.2 %collective-permute-start.1 = (f32[640,128]{1,0:T(8,128)S(1)}, f32[640,128]{1,0:T(8,128)S(1)}, u32[]{:S(2)}, u32[]{:S(2)}) collective-permute-start(f32[640,128]{1,0:T(8,128)S(1)} %pad_maximum_fusion.2), channel_id=1, source_target_pairs={{0,2},{2,0},{1,3},{3,1},{4,6},{6,4},{5,7},{7,5},{8,10},{10,8},{9,1... | collective-permute-start | bytes 983048 | tf_op jit(solution)/shard_map/ppermute | solution.py:21
  20.3 15.1 %copy-start.8 = (bf16[4,128,128]{2,1,0:T(8,128)(2,1)S(1)}, bf16[4,128,128]{2,1,0:T(8,128)(2,1)}, u32[]{:S(2)}) copy-start(bf16[4,128,128]{2,1,0:T(8,128)(2,1)} %get-tuple-element.7) | copy-start | bytes 393220
  20.3 15.1 %copy-start.9 = (bf16[4,128,128]{2,1,0:T(8,128)(2,1)S(1)}, bf16[4,128,128]{2,1,0:T(8,128)(2,1)}, u32[]{:S(2)}) copy-start(bf16[4,128,128]{2,1,0:T(8,128)(2,1)} %get-tuple-element.8) | copy-start | bytes 393220
  28.0 6.7 %copy-start.5 = (f32[128,128]{1,0:T(8,128)}, f32[128,128]{1,0:T(8,128)S(1)}, u32[]{:S(2)}) copy-start(f32[128,128]{1,0:T(8,128)S(1)} %slice_add_fusion.1) | copy-start | bytes 196612
  28.1 6.6 %collective-permute-start.2 = (f32[384,128]{1,0:T(8,128)S(1)}, f32[384,128]{1,0:T(8,128)S(1)}, u32[]{:S(2)}, u32[]{:S(2)}) collective-permute-start(f32[384,128]{1,0:T(8,128)S(1)} %pad_maximum_fusion.6), channel_id=1, source_target_pairs={{0,4},{4,0},{8,12},{12,8},{1,5},{5,1},{9,13},{13,9},{2,6},{6,2},{1... | collective-permute-start | bytes 589832 | tf_op jit(solution)/shard_map/ppermute | solution.py:21
  39.0 6.4 %collective-permute-start.6 = (bf16[128,512]{1,0:T(8,128)(2,1)S(1)}, bf16[128,512]{1,0:T(8,128)(2,1)S(1)}, u32[]{:S(2)}, u32[]{:S(2)}) collective-permute-start(bf16[128,512]{1,0:T(8,128)(2,1)S(1)} %fusion.35), channel_id=1, source_target_pairs={{0,2},{2,0},{1,3},{3,1},{4,6},{6,4},{5,7},{7,5},{8,10},{10,8},{9,1... | collective-permute-start | bytes 393224 | tf_op jit(solution)/shard_map/ppermute | solution.py:21
  41.3 8.5 %collective-permute-start.7 = (f32[2,128,256]{2,1,0:T(8,128)}, f32[2,128,256]{2,1,0:T(8,128)}, u32[]{:S(2)}, u32[]{:S(2)}) collective-permute-start(f32[2,128,256]{2,1,0:T(8,128)} %constant_dynamic-slice_fusion.1), channel_id=1, source_target_pairs={{0,2},{2,0},{1,3},{3,1},{4,6},{6,4},{5,7},{7,5},{8,10},{10,8},{9,1... | collective-permute-start | bytes 786440 | tf_op jit(solution)/shard_map/ppermute | solution.py:21
  41.8 14.9 %copy-start.6 = (f32[128,128]{1,0:T(8,128)S(1)}, f32[128,128]{1,0:T(8,128)}, u32[]{:S(2)}) copy-start(f32[128,128]{1,0:T(8,128)} %copy-done.5) | copy-start | bytes 196612
  41.8 14.9 %slice-start.1 = ((f32[384,128]{1,0:T(8,128)}), f32[128,128]{1,0:T(8,128)S(1)}, s32[]{:S(2)}) async-start(f32[384,128]{1,0:T(8,128)} %copy-done.10), calls=%async_computation.1 | async-start | bytes 131072 | tf_op jit(solution)/shard_map/slice | solution.py:69
  50.8 4.3 %collective-permute-start.8 = (bf16[128,256]{1,0:T(8,128)(2,1)S(1)}, bf16[128,256]{1,0:T(8,128)(2,1)S(1)}, u32[]{:S(2)}, u32[]{:S(2)}) collective-permute-start(bf16[128,256]{1,0:T(8,128)(2,1)S(1)} %fusion.68), channel_id=1, source_target_pairs={{0,4},{4,0},{8,12},{12,8},{1,5},{5,1},{9,13},{13,9},{2,6},{6,2},{1... | collective-permute-start | bytes 196616 | tf_op jit(solution)/shard_map/ppermute | solution.py:21
  52.4 4.3 %collective-permute-start.9 = (f32[1,128,128]{2,1,0:T(8,128)S(1)}, f32[1,128,128]{2,1,0:T(8,128)S(1)}, u32[]{:S(2)}, u32[]{:S(2)}) collective-permute-start(f32[1,128,128]{2,1,0:T(8,128)S(1)} %constant_dynamic-slice_fusion), channel_id=1, source_target_pairs={{0,4},{4,0},{8,12},{12,8},{1,5},{5,1},{9,13},{13,9},{2,6},{6,2},{1... | collective-permute-start | bytes 196616 | tf_op jit(solution)/shard_map/ppermute | solution.py:21
  57.0 4.9 %collective-permute-start.10 = (bf16[128,128]{1,0:T(8,128)(2,1)S(1)}, bf16[128,128]{1,0:T(8,128)(2,1)S(1)}, u32[]{:S(2)}, u32[]{:S(2)}) collective-permute-start(bf16[128,128]{1,0:T(8,128)(2,1)S(1)} %fusion.73), channel_id=1, source_target_pairs={{0,8},{4,12},{8,0},{12,4},{1,9},{5,13},{9,1},{13,5},{2,10},{6,14},... | collective-permute-start | bytes 98312 | tf_op jit(solution)/shard_map/ppermute | solution.py:21
  62.1 13.0 %copy-start.4 = (bf16[4,512,128]{2,1,0:T(8,128)(2,1)S(1)}, bf16[4,512,128]{2,1,0:T(8,128)(2,1)}, u32[]{:S(2)}) copy-start(bf16[4,512,128]{2,1,0:T(8,128)(2,1)} %param.8) | copy-start | bytes 1572868
  62.1 4.0 %collective-permute-start.11 = (bf16[1,128,128]{1,2,0:T(8,128)(2,1)S(1)}, bf16[1,128,128]{1,2,0:T(8,128)(2,1)S(1)}, u32[]{:S(2)}, u32[]{:S(2)}) collective-permute-start(bf16[1,128,128]{1,2,0:T(8,128)(2,1)S(1)} %fusion.74), channel_id=1, source_target_pairs={{0,4},{4,0},{8,12},{12,8},{1,5},{5,1},{9,13},{13,9},{2,6},{6,2},{1... | collective-permute-start | bytes 98312 | tf_op jit(solution)/shard_map/ppermute | solution.py:21
  66.4 5.0 %collective-permute-start.12 = (bf16[2,128,256]{1,2,0:T(8,128)(2,1)S(1)}, bf16[2,128,256]{1,2,0:T(8,128)(2,1)S(1)}, u32[]{:S(2)}, u32[]{:S(2)}) collective-permute-start(bf16[2,128,256]{1,2,0:T(8,128)(2,1)S(1)} %pad_maximum_fusion.8), channel_id=1, source_target_pairs={{0,2},{2,0},{1,3},{3,1},{4,6},{6,4},{5,7},{7,5},{8,10},{10,8},{9,1... | collective-permute-start | bytes 393224 | tf_op jit(solution)/shard_map/ppermute | solution.py:21
  72.1 1.8 %collective-permute-start.13 = (bf16[3,128,512]{1,2,0:T(8,128)(2,1)S(1)}, bf16[3,128,512]{1,2,0:T(8,128)(2,1)S(1)}, u32[]{:S(2)}, u32[]{:S(2)}) collective-permute-start(bf16[3,128,512]{1,2,0:T(8,128)(2,1)S(1)} %pad_maximum_fusion.1), channel_id=1, source_target_pairs={{0,1},{1,0},{2,3},{3,2},{4,5},{5,4},{6,7},{7,6},{8,9},{9,8},{10,11... | collective-permute-start | bytes 1179656 | tf_op jit(solution)/shard_map/ppermute | solution.py:21
  (3 other events, 3.4 us)

commit v3 on v2

--- a/solution.py
+++ b/solution.py
@@ -52,9 +52,13 @@
     c0 = jnp.dot(leaf_inverse, templates, preferred_element_type=F32)
     c0b = c0.astype(BF16)
 
-    cross = jnp.einsum("lir,kis->lkrs", v_basis, u_basis, preferred_element_type=F32)
     mine_c = coupling[:, 0]
-    partial = [cross[s + 1:, s].reshape(-1, rank) for s in range(levels - 1)]
+    partial = [
+        jnp.einsum(
+            "lir,is->lrs", v_basis[s + 1:], u_basis[s], preferred_element_type=F32
+        ).reshape(-1, rank)
+        for s in range(levels - 1)
+    ]
     w_own, theirs_c = [None] * levels, []
     for b in range(levels):
         c = mine_c[b]
@@ -72,13 +76,18 @@
                 w_own[s] = jnp.concatenate([partial[s], recv], axis=1)
             else:
                 partial[s] = partial[s] + recv
-    theirs_c = jnp.stack(theirs_c)
-    lower = jnp.stack([side(s, bits) == 0 for s in range(levels)])[:, None, None]
-    first = jnp.concatenate([mine_c[:, :, :rank], theirs_c[:, :, :rank]], axis=1)
-    second = jnp.concatenate([mine_c[:, :, rank:], theirs_c[:, :, rank:]], axis=1)
-    couple = jnp.concatenate(
-        [jnp.where(lower, first, second), jnp.where(lower, second, first)], axis=2
-    )
+    couple = []
+    for s in range(levels):
+        lower = side(s, bits) == 0
+        mine, theirs = mine_c[s], theirs_c[s]
+        first = jnp.concatenate([mine[:, :rank], theirs[:, :rank]], axis=0)
+        second = jnp.concatenate([mine[:, rank:], theirs[:, rank:]], axis=0)
+        couple.append(
+            jnp.concatenate(
+                [jnp.where(lower, first, second), jnp.where(lower, second, first)],
+                axis=1,
+            )
+        )
 
     proj0 = jnp.dot(v_basis[0].T, c0b, preferred_element_type=F32)
     rest = None

time: 79.1 us -> 68.1 us (0.86)
  waiting for transfers between devices: 35.7 us -> 24.2 us
  matrix products: 12.3 us -> 11.3 us
  local copies, waits for them, and re-layouts: 6.41 us -> 7.36 us
    ppermute x14, waiting for transfers between devices: 35.7 us -> 24.2 us  [swap(): return lax.ppermute(x, axis, [(i, i ^ 1 << stride) for i in range(n)])]
    slice x2, local copies, waits for them, and re-layouts: 0.05 us -> 2.12 us  [on_device(): parts = [jnp.concatenate([c[:, :rank], c[:, rank:]], axis=0).astype(F32)]]
    slice x4 -> x2, local copies, waits for them, and re-layouts: 1.75 us -> 0.01 us  [on_device(): v_basis[s + 1:]]
    convert_element_type x4, other arithmetic: 0.66 us -> 2.26 us  [on_device(): parts = [jnp.concatenate([c[:, :rank], c[:, rank:]], axis=0).astype(F32)]]
    dot_general x1 -> x3, matrix products: 1.68 us -> 0.69 us  [on_device(): jnp.einsum('lir,is->lrs', v_basis[s + 1:], u_basis[s], preferred_element_...]
    sub x2, other arithmetic: 2.39 us -> 1.44 us  [on_device(): rest = rest - fix.reshape(rest.shape)]
    unnamed x25 -> x46, local copies, waits for them, and re-layouts: 1.65 us -> 1.46 us
  transfers between devices with their start and end apart: 14 -> 14, of which waited for: 10 -> 8; matrix products, arithmetic and copies ran while one was open for 22% -> 28% of each run, Pallas kernels for 0% -> 0%
where the time goes in v3:
time: 68.1 us; the launch traced here: 67.5 us
  waiting for transfers between devices  24.2 us (36%)
  starting transfers between devices  14.2 us (21%)
  matrix products  11.3 us (17%)
  other arithmetic  9.77 us (14%)
  local copies, waits for them, and re-layouts  7.36 us (11%)
    ppermute x14, waiting for transfers between devices, swap(): return lax.ppermute(x, axis, [(i, i ^ 1 << stride) for i in range(n)])  24.2 us
    ppermute x14, starting transfers between devices, swap(): return lax.ppermute(x, axis, [(i, i ^ 1 << stride) for i in range(n)])  14.2 us
    dot_general x4, matrix products, on_device(): current = current - jnp.dot(u_basis[s], full[s], preferred_element_type=F32)  2.84 us
    convert_element_type x4, other arithmetic, on_device(): parts = [jnp.concatenate([c[:, :rank], c[:, rank:]], axis=0).astype(F32)]  2.26 us
    slice x2, local copies, waits for them, and re-layouts, on_device(): parts = [jnp.concatenate([c[:, :rank], c[:, rank:]], axis=0).astype(F32)]  2.12 us
    concatenate x3, other arithmetic, gather_half(): both = jnp.concatenate([x, swap(x, bit, bits), x], axis=-1)  2.09 us
    dot_general x1, matrix products, on_device(): c0 = jnp.dot(leaf_inverse, templates, preferred_element_type=F32)  2.06 us
    dot_general x4, matrix products, on_device(): coefs = jnp.dot(couple[s], stacked, preferred_element_type=F32).astype(BF16)  1.99 us
  transfers between devices with their start and end apart: 14, of which 8 were waited for; matrix products, arithmetic and copies ran while one was open for 28% of the time, Pallas kernels for 0%

profile of v3, /device:TPU:0, one launch (start us, length us, event | category | flops | bytes accessed | tf_op | source)
XLA Modules:
  0.0 67.5 jit_solution(8100020425821762656)
XLA Ops:
  0.0 1.8 %slice_bitcast_fusion.8 = (bf16[128,256]{1,0:T(8,128)(2,1)S(1)}, bf16[128,256]{1,0:T(8,128)(2,1)}, bf16[128,256]{1,0:T(8,128)(2,1)}, bf16[128,256]{1,0:T(8,128)(2,1)S(1)}) fusion(bf16[4,1,128,256]{3,2,1,0:T(8,128)(2,1)} %param.9), kind=kLoop, calls=%fused_computation.140 | loop fusion | bytes 524288 | tf_op jit(solution)/shard_map/squeeze | solution.py:82
  3.2 4.0 %collective-permute-start.8 = (bf16[256,128]{1,0:T(8,128)(2,1)}, bf16[256,128]{1,0:T(8,128)(2,1)}, u32[]{:S(2)}, u32[]{:S(2)}) collective-permute-start(bf16[256,128]{1,0:T(8,128)(2,1)} %fusion.75), channel_id=1, source_target_pairs={{0,8},{4,12},{8,0},{12,4},{1,9},{5,13},{9,1},{13,5},{2,10},{6,14},... | collective-permute-start | bytes 196616 | tf_op jit(solution)/shard_map/ppermute | solution.py:21
  8.3 1.4 %fusion.111 = (bf16[128,128]{1,0:T(8,128)(2,1)}, bf16[128,128]{1,0:T(8,128)(2,1)}, bf16[128,128]{1,0:T(8,128)(2,1)S(1)}, bf16[128,128]{1,0:T(8,128)(2,1)S(1)}) fusion(bf16[128,256]{1,0:T(8,128)(2,1)} %get-tuple-element.6, bf16[128,256]{1,0:T(8,128)(2,1)} %get-tuple-element.7), kind=kLoop, calls=%fused_computation.175 | loop fusion | bytes 262144 | tf_op jit(solution)/shard_map/slice | solution.py:65
  10.6 2.1 %fusion.113 = (bf16[512,1024]{1,0:T(8,128)(2,1)S(1)}, f32[512,1024]{1,0:T(8,128)}) fusion(bf16[512,512]{1,0:T(8,128)(2,1)S(1)} %copy-done.6, bf16[512,1024]{1,0:T(8,128)(2,1)S(1)} %copy-done), kind=kOutput, calls=%fused_computation.177 | convolution fusion | flops 537395200 | bytes 4718592 | tf_op jit(solution)/shard_map/dot_general | solution.py:52
  12.7 1.0 %fusion.1 = bf16[128,1024]{1,0:T(8,128)(2,1)} fusion(bf16[512,1024]{1,0:T(8,128)(2,1)S(1)} %get-tuple-element.33, bf16[4,512,128]{2,1,0:T(8,128)(2,1)S(1)} %copy-done.2), kind=kOutput, calls=%fused_computation.14 | convolution fusion | flops 134348800 | bytes 1441792 | tf_op jit(solution)/shard_map/dot_general | solution.py:92
  14.2 1.3 %convolution_bitcast_fusion = f32[3,128,512]{2,1,0:T(8,128)} fusion(bf16[512,1024]{1,0:T(8,128)(2,1)S(1)} %get-tuple-element.33, s32[]{:T(128)S(6)} %select_n.79, bf16[4,512,128]{2,1,0:T(8,128)(2,1)S(1)} %copy-done.2), kind=kOutput, calls=%fused_computation.5 | convolution fusion | flops 201326592 | bytes 1703940 | tf_op jit(solution)/shard_map/lir,it->lrt/dot_general | solution.py:101
  18.3 1.0 %slice_add_fusion = f32[256,128]{1,0:T(8,128)S(1)} fusion(f32[256,128]{1,0:T(8,128)} %copy-done.5, f32[1024,128]{1,0:T(8,128)} %collective-permute-done), kind=kLoop, calls=%fused_computation.66 | loop fusion | flops 32768 | bytes 393216 | tf_op jit(solution)/shard_map/add | solution.py:78
  20.2 1.6 %collective-permute-start.2 = (f32[640,128]{1,0:T(8,128)S(1)}, f32[640,128]{1,0:T(8,128)S(1)}, u32[]{:S(2)}, u32[]{:S(2)}) collective-permute-start(f32[640,128]{1,0:T(8,128)S(1)} %pad_maximum_fusion.2), channel_id=1, source_target_pairs={{0,2},{2,0},{1,3},{3,1},{4,6},{6,4},{5,7},{7,5},{8,10},{10,8},{9,1... | collective-permute-start | bytes 983048 | tf_op jit(solution)/shard_map/ppermute | solution.py:21
  22.7 1.1 %convert.15 = bf16[1024,128]{1,0:T(8,128)(2,1)S(1)} convert(f32[1024,128]{1,0:T(8,128)} %collective-permute-done) | non-fusion elementwise | flops 131072 | bytes 786432 | tf_op jit(solution)/shard_map/convert.4
  23.9 1.3 %convolution_convert_fusion = bf16[256,1024]{1,0:T(8,128)(2,1)S(1)} fusion(bf16[128,1024]{1,0:T(8,128)(2,1)} %collective-permute-done.1, bf16[128,1024]{1,0:T(8,128)(2,1)} %fusion.1, bf16[256,128]{1,0:T(8,128)(2,1)S(1)} %get-tuple-element.20, bf16[256,128]{1,0:T(8,128)(2,1)S(1)} %get-tuple-element.19), kind=kOutput, calls=%fused_computation.6 | convolution fusion | flops 135790592 | bytes 1179648 | tf_op jit(solution)/shard_map/dot_general | solution.py:117
  26.0 1.4 %add_subtract_fusion = f32[3,128,512]{2,1,0:T(8,128)S(1)} fusion(f32[3,128,512]{2,1,0:T(8,128)S(1)} %bitcast.103, f32[3,128,512]{2,1,0:T(8,128)S(1)} %bitcast.102, f32[3,128,512]{2,1,0:T(8,128)} %collective-permute-done.3), kind=kLoop, calls=%fused_computation.21 | loop fusion | flops 393216 | bytes 3145728 | tf_op jit(solution)/shard_map/sub | solution.py:126
  28.1 1.6 %collective-permute-start.6 = (f32[2,128,256]{2,1,0:T(8,128)S(1)}, f32[2,128,256]{2,1,0:T(8,128)S(1)}, u32[]{:S(2)}, u32[]{:S(2)}) collective-permute-start(f32[2,128,256]{2,1,0:T(8,128)S(1)} %constant_dynamic-slice_fusion.1), channel_id=1, source_target_pairs={{0,2},{2,0},{1,3},{3,1},{4,6},{6,4},{5,7},{7,5},{8,10},{10,8},{9,1... | collective-permute-start | bytes 786440 | tf_op jit(solution)/shard_map/ppermute | solution.py:21
  30.5 1.6 %collective-permute-start.5 = (f32[384,128]{1,0:T(8,128)S(1)}, f32[384,128]{1,0:T(8,128)S(1)}, u32[]{:S(2)}, u32[]{:S(2)}) collective-permute-start(f32[384,128]{1,0:T(8,128)S(1)} %pad_maximum_fusion.3), channel_id=1, source_target_pairs={{0,4},{4,0},{8,12},{12,8},{1,5},{5,1},{9,13},{13,9},{2,6},{6,2},{1... | collective-permute-start | bytes 589832 | tf_op jit(solution)/shard_map/ppermute | solution.py:21
  32.2 1.7 %collective-permute-done.4 = bf16[128,512]{1,0:T(8,128)(2,1)S(1)} collective-permute-done((bf16[128,512]{1,0:T(8,128)(2,1)S(1)}, bf16[128,512]{1,0:T(8,128)(2,1)S(1)}, u32[]{:S(2)}, u32[]{:S(2)}) %collective-permute-start.4) | collective-permute-done | bytes 131104 | tf_op jit(solution)/shard_map/ppermute | solution.py:21
  34.4 4.4 %collective-permute-done.6 = f32[2,128,256]{2,1,0:T(8,128)S(1)} collective-permute-done((f32[2,128,256]{2,1,0:T(8,128)S(1)}, f32[2,128,256]{2,1,0:T(8,128)S(1)}, u32[]{:S(2)}, u32[]{:S(2)}) %collective-permute-start.6) | collective-permute-done | bytes 262176 | tf_op jit(solution)/shard_map/ppermute | solution.py:21
  39.0 1.6 %collective-permute-start.9 = (f32[1,128,128]{2,1,0:T(8,128)S(1)}, f32[1,128,128]{2,1,0:T(8,128)S(1)}, u32[]{:S(2)}, u32[]{:S(2)}) collective-permute-start(f32[1,128,128]{2,1,0:T(8,128)S(1)} %constant_dynamic-slice_fusion), channel_id=1, source_target_pairs={{0,4},{4,0},{8,12},{12,8},{1,5},{5,1},{9,13},{13,9},{2,6},{6,2},{1... | collective-permute-start | bytes 196616 | tf_op jit(solution)/shard_map/ppermute | solution.py:21
  41.1 3.8 %collective-permute-done.7 = bf16[128,256]{1,0:T(8,128)(2,1)S(1)} collective-permute-done((bf16[128,256]{1,0:T(8,128)(2,1)S(1)}, bf16[128,256]{1,0:T(8,128)(2,1)S(1)}, u32[]{:S(2)}, u32[]{:S(2)}) %collective-permute-start.7) | collective-permute-done | bytes 65568 | tf_op jit(solution)/shard_map/ppermute | solution.py:21
  45.8 4.8 %collective-permute-done.10 = bf16[128,128]{1,0:T(8,128)(2,1)S(1)} collective-permute-done((bf16[128,128]{1,0:T(8,128)(2,1)S(1)}, bf16[128,128]{1,0:T(8,128)(2,1)S(1)}, u32[]{:S(2)}, u32[]{:S(2)}) %collective-permute-start.10) | collective-permute-done | bytes 32800 | tf_op jit(solution)/shard_map/ppermute | solution.py:21
  51.4 3.5 %collective-permute-done.11 = bf16[1,128,128]{1,2,0:T(8,128)(2,1)S(1)} collective-permute-done((bf16[1,128,128]{1,2,0:T(8,128)(2,1)S(1)}, bf16[1,128,128]{1,2,0:T(8,128)(2,1)S(1)}, u32[]{:S(2)}, u32[]{:S(2)}) %collective-permute-start.11) | collective-permute-done | bytes 32800 | tf_op jit(solution)/shard_map/ppermute | solution.py:21
  55.2 1.2 %collective-permute-start.12 = (bf16[2,128,256]{1,2,0:T(8,128)(2,1)S(1)}, bf16[2,128,256]{1,2,0:T(8,128)(2,1)S(1)}, u32[]{:S(2)}, u32[]{:S(2)}) collective-permute-start(bf16[2,128,256]{1,2,0:T(8,128)(2,1)S(1)} %pad_maximum_fusion.4), channel_id=1, source_target_pairs={{0,2},{2,0},{1,3},{3,1},{4,6},{6,4},{5,7},{7,5},{8,10},{10,8},{9,1... | collective-permute-start | bytes 393224 | tf_op jit(solution)/shard_map/ppermute | solution.py:21
  56.5 3.7 %collective-permute-done.12 = bf16[2,128,256]{1,2,0:T(8,128)(2,1)S(1)} collective-permute-done((bf16[2,128,256]{1,2,0:T(8,128)(2,1)S(1)}, bf16[2,128,256]{1,2,0:T(8,128)(2,1)S(1)}, u32[]{:S(2)}, u32[]{:S(2)}) %collective-permute-start.12) | collective-permute-done | bytes 131104 | tf_op jit(solution)/shard_map/ppermute | solution.py:21
  60.9 1.7 %collective-permute-done.13 = bf16[3,128,512]{1,2,0:T(8,128)(2,1)S(1)} collective-permute-done((bf16[3,128,512]{1,2,0:T(8,128)(2,1)S(1)}, bf16[3,128,512]{1,2,0:T(8,128)(2,1)S(1)}, u32[]{:S(2)}, u32[]{:S(2)}) %collective-permute-start.13) | collective-permute-done | bytes 393248 | tf_op jit(solution)/shard_map/ppermute | solution.py:21
  62.6 1.2 %fusion.4 = bf16[3,128,1024]{1,2,0:T(8,128)(2,1)S(1)} fusion(s32[]{:T(128)S(6)} %select_n.92, bf16[1,128,512]{1,2,0:T(8,128)(2,1)S(1)} %copy.21, bf16[2,128,512]{1,2,0:T(8,128)(2,1)S(1)} %fusion.19, bf16[3,128,512]{1,2,0:T(8,128)(2,1)S(1)} %collective-permute-done.13), kind=kLoop, calls=%fused_computation.19 | loop fusion | flops 3932160 | bytes 1572868 | tf_op jit(solution)/shard_map/concatenate | solution.py:44
  66.0 1.5 %fusion = bf16[512,1024]{1,0:T(8,128)(2,1)} fusion(f32[1024,512]{0,1:T(8,128)S(1)} %fusion.21, f32[1024,512]{0,1:T(8,128)S(1)} %fusion.22, f32[1024,512]{0,1:T(8,128)S(1)} %fusion.23, f32[512,1024]{1,0:T(8,128)S(1)} %copy-done.1, bf16[256,1024]{1,0:T(8,128)(2,1)S(1)} %copy-done.8, bf16[4,512,128]{2,1,0:T(8,128)(2,1)S(1)} %copy-done.4), kind=kOutput, calls=%fused_computation.1 | convolution fusion | flops 136839168 | bytes 9830400 | tf_op jit(solution)/shard_map/dot_general | solution.py:139
  (114 shorter events, 16.6 us)
Async XLA Ops:
  0.0 10.6 %copy-start = (bf16[512,1024]{1,0:T(8,128)(2,1)S(1)}, bf16[512,1024]{1,0:T(8,128)(2,1)}, u32[]{:S(2)}) copy-start(bf16[512,1024]{1,0:T(8,128)(2,1)} %param.5) | copy-start | bytes 3145732
  0.0 7.4 %slice-start = ((bf16[4,512,128]{2,1,0:T(8,128)(2,1)}), bf16[2,512,128]{2,1,0:T(8,128)(2,1)S(1)}, s32[]{:S(2)}) async-start(bf16[4,512,128]{2,1,0:T(8,128)(2,1)} %param.7), calls=%async_computation | async-start | bytes 524288 | tf_op jit(solution)/shard_map/slice | solution.py:58
  0.0 7.8 %slice-start.1 = ((bf16[4,512,128]{2,1,0:T(8,128)(2,1)}), bf16[3,512,128]{2,1,0:T(8,128)(2,1)S(1)}, s32[]{:S(2)}) async-start(bf16[4,512,128]{2,1,0:T(8,128)(2,1)} %param.7), calls=%async_computation.1 | async-start | bytes 786432
  3.2 14.4 %collective-permute-start.8 = (bf16[256,128]{1,0:T(8,128)(2,1)}, bf16[256,128]{1,0:T(8,128)(2,1)}, u32[]{:S(2)}, u32[]{:S(2)}) collective-permute-start(bf16[256,128]{1,0:T(8,128)(2,1)} %fusion.75), channel_id=1, source_target_pairs={{0,8},{4,12},{8,0},{12,4},{1,9},{5,13},{9,1},{13,5},{2,10},{6,14},... | collective-permute-start | bytes 196616 | tf_op jit(solution)/shard_map/ppermute | solution.py:21
  10.6 7.7 %collective-permute-start = (f32[1024,128]{1,0:T(8,128)}, f32[1024,128]{1,0:T(8,128)}, u32[]{:S(2)}, u32[]{:S(2)}) collective-permute-start(f32[1024,128]{1,0:T(8,128)} %pad_maximum_fusion), channel_id=1, source_target_pairs={{0,1},{1,0},{2,3},{3,2},{4,5},{5,4},{6,7},{7,6},{8,9},{9,8},{10,11... | collective-permute-start | bytes 1572872 | tf_op jit(solution)/shard_map/ppermute | solution.py:21
  13.7 10.1 %collective-permute-start.1 = (bf16[128,1024]{1,0:T(8,128)(2,1)}, bf16[128,1024]{1,0:T(8,128)(2,1)}, u32[]{:S(2)}, u32[]{:S(2)}) collective-permute-start(bf16[128,1024]{1,0:T(8,128)(2,1)} %fusion.1), channel_id=1, source_target_pairs={{0,1},{1,0},{2,3},{3,2},{4,5},{5,4},{6,7},{7,6},{8,9},{9,8},{10,11... | collective-permute-start | bytes 786440 | tf_op jit(solution)/shard_map/ppermute | solution.py:21
  15.5 10.2 %collective-permute-start.3 = (f32[3,128,512]{2,1,0:T(8,128)}, f32[3,128,512]{2,1,0:T(8,128)}, u32[]{:S(2)}, u32[]{:S(2)}) collective-permute-start(f32[3,128,512]{2,1,0:T(8,128)} %convolution_bitcast_fusion), channel_id=1, source_target_pairs={{0,1},{1,0},{2,3},{3,2},{4,5},{5,4},{6,7},{7,6},{8,9},{9,8},{10,11... | collective-permute-start | bytes 2359304 | tf_op jit(solution)/shard_map/ppermute | solution.py:21
  15.9 7.9 %copy-start.18 = (bf16[128,128]{1,0:T(8,128)(2,1)S(1)}, bf16[128,128]{1,0:T(8,128)(2,1)}, u32[]{:S(2)}) copy-start(bf16[128,128]{1,0:T(8,128)(2,1)} %copy-done.17) | copy-start | bytes 98308
  15.9 7.9 %copy-start.20 = (bf16[128,128]{1,0:T(8,128)(2,1)S(1)}, bf16[128,128]{1,0:T(8,128)(2,1)}, u32[]{:S(2)}) copy-start(bf16[128,128]{1,0:T(8,128)(2,1)} %copy-done.19) | copy-start | bytes 98308
  20.2 10.2 %collective-permute-start.2 = (f32[640,128]{1,0:T(8,128)S(1)}, f32[640,128]{1,0:T(8,128)S(1)}, u32[]{:S(2)}, u32[]{:S(2)}) collective-permute-start(f32[640,128]{1,0:T(8,128)S(1)} %pad_maximum_fusion.2), channel_id=1, source_target_pairs={{0,2},{2,0},{1,3},{3,1},{4,6},{6,4},{5,7},{7,5},{8,10},{10,8},{9,1... | collective-permute-start | bytes 983048 | tf_op jit(solution)/shard_map/ppermute | solution.py:21
  27.5 6.4 %collective-permute-start.4 = (bf16[128,512]{1,0:T(8,128)(2,1)S(1)}, bf16[128,512]{1,0:T(8,128)(2,1)S(1)}, u32[]{:S(2)}, u32[]{:S(2)}) collective-permute-start(bf16[128,512]{1,0:T(8,128)(2,1)S(1)} %fusion.33), channel_id=1, source_target_pairs={{0,2},{2,0},{1,3},{3,1},{4,6},{6,4},{5,7},{7,5},{8,10},{10,8},{9,1... | collective-permute-start | bytes 393224 | tf_op jit(solution)/shard_map/ppermute | solution.py:21
  28.1 10.7 %collective-permute-start.6 = (f32[2,128,256]{2,1,0:T(8,128)S(1)}, f32[2,128,256]{2,1,0:T(8,128)S(1)}, u32[]{:S(2)}, u32[]{:S(2)}) collective-permute-start(f32[2,128,256]{2,1,0:T(8,128)S(1)} %constant_dynamic-slice_fusion.1), channel_id=1, source_target_pairs={{0,2},{2,0},{1,3},{3,1},{4,6},{6,4},{5,7},{7,5},{8,10},{10,8},{9,1... | collective-permute-start | bytes 786440 | tf_op jit(solution)/shard_map/ppermute | solution.py:21
  30.5 10.6 %copy-start.13 = (bf16[128,128]{1,0:T(8,128)(2,1)S(1)}, bf16[128,128]{1,0:T(8,128)(2,1)}, u32[]{:S(2)}) copy-start(bf16[128,128]{1,0:T(8,128)(2,1)} %get-tuple-element.35) | copy-start | bytes 98308
  30.5 10.6 %copy-start.14 = (bf16[128,128]{1,0:T(8,128)(2,1)S(1)}, bf16[128,128]{1,0:T(8,128)(2,1)}, u32[]{:S(2)}) copy-start(bf16[128,128]{1,0:T(8,128)(2,1)} %get-tuple-element.36) | copy-start | bytes 98308
  30.5 8.4 %collective-permute-start.5 = (f32[384,128]{1,0:T(8,128)S(1)}, f32[384,128]{1,0:T(8,128)S(1)}, u32[]{:S(2)}, u32[]{:S(2)}) collective-permute-start(f32[384,128]{1,0:T(8,128)S(1)} %pad_maximum_fusion.3), channel_id=1, source_target_pairs={{0,4},{4,0},{8,12},{12,8},{1,5},{5,1},{9,13},{13,9},{2,6},{6,2},{1... | collective-permute-start | bytes 589832 | tf_op jit(solution)/shard_map/ppermute | solution.py:21
  34.1 11.7 %copy-start.10 = (bf16[128,128]{1,0:T(8,128)(2,1)S(1)}, bf16[128,128]{1,0:T(8,128)(2,1)}, u32[]{:S(2)}) copy-start(bf16[128,128]{1,0:T(8,128)(2,1)} %copy-done.9) | copy-start | bytes 98308
  34.1 11.7 %copy-start.12 = (bf16[128,128]{1,0:T(8,128)(2,1)S(1)}, bf16[128,128]{1,0:T(8,128)(2,1)}, u32[]{:S(2)}) copy-start(bf16[128,128]{1,0:T(8,128)(2,1)} %copy-done.11) | copy-start | bytes 98308
  39.0 6.1 %collective-permute-start.9 = (f32[1,128,128]{2,1,0:T(8,128)S(1)}, f32[1,128,128]{2,1,0:T(8,128)S(1)}, u32[]{:S(2)}, u32[]{:S(2)}) collective-permute-start(f32[1,128,128]{2,1,0:T(8,128)S(1)} %constant_dynamic-slice_fusion), channel_id=1, source_target_pairs={{0,4},{4,0},{8,12},{12,8},{1,5},{5,1},{9,13},{13,9},{2,6},{6,2},{1... | collective-permute-start | bytes 196616 | tf_op jit(solution)/shard_map/ppermute | solution.py:21
  40.6 4.3 %collective-permute-start.7 = (bf16[128,256]{1,0:T(8,128)(2,1)S(1)}, bf16[128,256]{1,0:T(8,128)(2,1)S(1)}, u32[]{:S(2)}, u32[]{:S(2)}) collective-permute-start(bf16[128,256]{1,0:T(8,128)(2,1)S(1)} %fusion.81), channel_id=1, source_target_pairs={{0,4},{4,0},{8,12},{12,8},{1,5},{5,1},{9,13},{13,9},{2,6},{6,2},{1... | collective-permute-start | bytes 196616 | tf_op jit(solution)/shard_map/ppermute | solution.py:21
  45.4 5.2 %collective-permute-start.10 = (bf16[128,128]{1,0:T(8,128)(2,1)S(1)}, bf16[128,128]{1,0:T(8,128)(2,1)S(1)}, u32[]{:S(2)}, u32[]{:S(2)}) collective-permute-start(bf16[128,128]{1,0:T(8,128)(2,1)S(1)} %fusion.86), channel_id=1, source_target_pairs={{0,8},{4,12},{8,0},{12,4},{1,9},{5,13},{9,1},{13,5},{2,10},{6,14},... | collective-permute-start | bytes 98312 | tf_op jit(solution)/shard_map/ppermute | solution.py:21
  50.6 13.2 %copy-start.4 = (bf16[4,512,128]{2,1,0:T(8,128)(2,1)S(1)}, bf16[4,512,128]{2,1,0:T(8,128)(2,1)}, u32[]{:S(2)}) copy-start(bf16[4,512,128]{2,1,0:T(8,128)(2,1)} %param.8) | copy-start | bytes 1572868
  50.9 4.0 %collective-permute-start.11 = (bf16[1,128,128]{1,2,0:T(8,128)(2,1)S(1)}, bf16[1,128,128]{1,2,0:T(8,128)(2,1)S(1)}, u32[]{:S(2)}, u32[]{:S(2)}) collective-permute-start(bf16[1,128,128]{1,2,0:T(8,128)(2,1)S(1)} %fusion.87), channel_id=1, source_target_pairs={{0,4},{4,0},{8,12},{12,8},{1,5},{5,1},{9,13},{13,9},{2,6},{6,2},{1... | collective-permute-start | bytes 98312 | tf_op jit(solution)/shard_map/ppermute | solution.py:21
  55.2 5.0 %collective-permute-start.12 = (bf16[2,128,256]{1,2,0:T(8,128)(2,1)S(1)}, bf16[2,128,256]{1,2,0:T(8,128)(2,1)S(1)}, u32[]{:S(2)}, u32[]{:S(2)}) collective-permute-start(bf16[2,128,256]{1,2,0:T(8,128)(2,1)S(1)} %pad_maximum_fusion.4), channel_id=1, source_target_pairs={{0,2},{2,0},{1,3},{3,1},{4,6},{6,4},{5,7},{7,5},{8,10},{10,8},{9,1... | collective-permute-start | bytes 393224 | tf_op jit(solution)/shard_map/ppermute | solution.py:21
  60.9 1.8 %collective-permute-start.13 = (bf16[3,128,512]{1,2,0:T(8,128)(2,1)S(1)}, bf16[3,128,512]{1,2,0:T(8,128)(2,1)S(1)}, u32[]{:S(2)}, u32[]{:S(2)}) collective-permute-start(bf16[3,128,512]{1,2,0:T(8,128)(2,1)S(1)} %pad_maximum_fusion.1), channel_id=1, source_target_pairs={{0,1},{1,0},{2,3},{3,2},{4,5},{5,4},{6,7},{7,6},{8,9},{9,8},{10,11... | collective-permute-start | bytes 1179656 | tf_op jit(solution)/shard_map/ppermute | solution.py:21
  (13 other events, 49.4 us)

commit v4 on v3

--- a/solution.py
+++ b/solution.py
@@ -106,14 +106,25 @@
     own_coefs = []
     for s in range(levels):
         if s == 0:
-            mine = proj0
+            mine_b = proj0.astype(BF16)
+            theirs_b = swap(mine_b, s, bits)
         else:
-            mine = rest[0]
+            mine_b = rest[0].astype(BF16)
             rest = rest[1:]
-            if rest.shape[0] > 0:
-                rest = reduce_half(rest, s, bits)
-        mine_b = mine.astype(BF16)
-        stacked = jnp.concatenate([mine_b, swap(mine_b, s, bits)], axis=0)
+            n = rest.shape[0]
+            w = mine_b.shape[1] // 2
+            parts = [mine_b[:, :w], mine_b[:, w:]]
+            if n > 0:
+                h = side(s, bits)
+                keep = cols(rest, h * w, w)
+                send = cols(rest, (1 - h) * w, w)
+                parts.append(send.astype(BF16).reshape(n * rank, w))
+            got = swap(jnp.concatenate(parts, axis=0), s, bits)
+            theirs_b = jnp.concatenate([got[:rank], got[rank : 2 * rank]], axis=1)
+            if n > 0:
+                recv = got[2 * rank :].reshape(n, rank, w).astype(F32)
+                rest = keep + recv
+        stacked = jnp.concatenate([mine_b, theirs_b], axis=0)
         coefs = jnp.dot(couple[s], stacked, preferred_element_type=F32).astype(BF16)
         own_coefs.append(coefs[:rank])
         if s < levels - 1:

time: 68.1 us -> 64.3 us (0.944)
  waiting for transfers between devices: 24.2 us -> 17.9 us
  matrix products: 11.3 us -> 14.4 us
  local copies, waits for them, and re-layouts: 7.36 us -> 8.57 us
  other arithmetic: 9.77 us -> 8.77 us
  starting transfers between devices: 14.2 us -> 13.3 us
    ppermute x14 -> x12, waiting for transfers between devices: 24.2 us -> 17.9 us  [swap(): return lax.ppermute(x, axis, [(i, i ^ 1 << stride) for i in range(n)])]
    slice x2, local copies, waits for them, and re-layouts: 2.12 us -> 0.05 us  [on_device(): parts = [jnp.concatenate([c[:, :rank], c[:, rank:]], axis=0).astype(F32)]]
    reshape x0 -> x4, local copies, waits for them, and re-layouts: none -> 1.62 us  [the longest x2 1.51 us: on_device(): rest = rest - fix.reshape(rest.shape)]
    dot_general x0 -> x1, matrix products: none -> 1.61 us  [on_device(): jnp.einsum('lir,it->lrt', v_basis[1:], cols(c0b, h * half, half), preferr...]
    sub x2 -> x1, other arithmetic: 1.44 us -> 0.04 us  [on_device(): rest = rest - fix.reshape(rest.shape)]
    dot_general x0 -> x2, local copies, waits for them, and re-layouts: none -> 1.2 us  [on_device(): jnp.einsum('lir,is->lrs', v_basis[s + 1:], u_basis[s], preferred_element_...]
    ppermute x14 -> x12, starting transfers between devices: 14.2 us -> 13.3 us  [swap(): return lax.ppermute(x, axis, [(i, i ^ 1 << stride) for i in range(n)])]
    convert_element_type x4, other arithmetic: 2.26 us -> 1.33 us  [on_device(): parts = [jnp.concatenate([c[:, :rank], c[:, rank:]], axis=0).astype(F32)]]
  transfers between devices with their start and end apart: 14 -> 12, of which waited for: 8 -> 7; matrix products, arithmetic and copies ran while one was open for 28% -> 36% of each run, Pallas kernels for 0% -> 0%
where the time goes in v4:
time: 64.3 us; the launch traced here: 63.7 us
  waiting for transfers between devices  17.9 us (28%)
  matrix products  14.4 us (22%)
  starting transfers between devices  13.3 us (21%)
  other arithmetic  8.77 us (14%)
  local copies, waits for them, and re-layouts  8.57 us (13%)
  between operations  0.81 us (1%)
    ppermute x12, waiting for transfers between devices, swap(): return lax.ppermute(x, axis, [(i, i ^ 1 << stride) for i in range(n)])  17.9 us
    ppermute x12, starting transfers between devices, swap(): return lax.ppermute(x, axis, [(i, i ^ 1 << stride) for i in range(n)])  13.3 us
    dot_general x4, matrix products, on_device(): coefs = jnp.dot(couple[s], stacked, preferred_element_type=F32).astype(BF16)  2.88 us
    dot_general x4, matrix products, on_device(): current = current - jnp.dot(u_basis[s], full[s], preferred_element_type=F32)  2.85 us
    concatenate x3, other arithmetic, gather_half(): both = jnp.concatenate([x, swap(x, bit, bits), x], axis=-1)  2.09 us
    dot_general x1, matrix products, on_device(): c0 = jnp.dot(leaf_inverse, templates, preferred_element_type=F32)  2.08 us
    dot_general x3, matrix products, on_device(): jnp.dot(w_own[s], piece, preferred_element_type=F32, precision=lax.Precis...  1.87 us
    add x3, other arithmetic, on_device(): partial[s] = partial[s] + recv  1.78 us
  transfers between devices with their start and end apart: 12, of which 7 were waited for; matrix products, arithmetic and copies ran while one was open for 36% of the time, Pallas kernels for 0%

profile of v4, /device:TPU:0, one launch (start us, length us, event | category | flops | bytes accessed | tf_op | source)
XLA Modules:
  0.0 63.7 jit_solution(5326701028189035494)
XLA Ops:
  0.0 1.1 %slice_bitcast_fusion.9 = (bf16[128,256]{1,0:T(8,128)(2,1)S(1)}, bf16[128,256]{1,0:T(8,128)(2,1)S(1)}, bf16[128,256]{1,0:T(8,128)(2,1)S(1)}, bf16[128,256]{1,0:T(8,128)(2,1)S(1)}) fusion(bf16[4,1,128,256]{3,2,1,0:T(8,128)(2,1)} %param.9), kind=kLoop, calls=%fused_computation.158 | loop fusion | bytes 524288 | tf_op jit(solution)/shard_map/squeeze | solution.py:82
  1.8 4.0 %collective-permute-start.7 = (bf16[256,128]{1,0:T(8,128)(2,1)}, bf16[256,128]{1,0:T(8,128)(2,1)}, u32[]{:S(2)}, u32[]{:S(2)}) collective-permute-start(bf16[256,128]{1,0:T(8,128)(2,1)} %fusion.83), channel_id=1, source_target_pairs={{0,8},{4,12},{8,0},{12,4},{1,9},{5,13},{9,1},{13,5},{2,10},{6,14},... | collective-permute-start | bytes 196616 | tf_op jit(solution)/shard_map/ppermute | solution.py:21
  9.5 2.1 %fusion.135 = (bf16[512,1024]{1,0:T(8,128)(2,1)S(1)}, f32[512,1024]{1,0:T(8,128)}) fusion(bf16[512,512]{1,0:T(8,128)(2,1)S(1)} %copy-done.8, bf16[512,1024]{1,0:T(8,128)(2,1)S(1)} %copy-done), kind=kOutput, calls=%fused_computation.201 | convolution fusion | flops 537395200 | bytes 4718592 | tf_op jit(solution)/shard_map/dot_general | solution.py:52
  11.6 1.1 %fusion.3 = bf16[128,1024]{1,0:T(8,128)(2,1)} fusion(bf16[512,1024]{1,0:T(8,128)(2,1)S(1)} %get-tuple-element.45, bf16[4,512,128]{2,1,0:T(8,128)(2,1)S(1)} %copy-done.2), kind=kOutput, calls=%fused_computation.17 | convolution fusion | flops 134348800 | bytes 1441792 | tf_op jit(solution)/shard_map/dot_general | solution.py:92
  13.1 1.4 %convolution_bitcast_fusion = f32[3,128,512]{1,2,0:T(8,128)} fusion(bf16[512,1024]{1,0:T(8,128)(2,1)S(1)} %get-tuple-element.45, s32[]{:T(128)S(6)} %select_n.79, bf16[4,512,128]{2,1,0:T(8,128)(2,1)S(1)} %copy-done.2), kind=kOutput, calls=%fused_computation.5 | convolution fusion | flops 201326592 | bytes 1703940 | tf_op jit(solution)/shard_map/lir,it->lrt/dot_general | solution.py:101
  15.2 1.4 %fusion.127 = (bf16[128,128]{1,0:T(8,128)(2,1)}, bf16[128,128]{1,0:T(8,128)(2,1)}) fusion(bf16[256,128]{1,0:T(8,128)(2,1)} %collective-permute-done.7), kind=kLoop, calls=%fused_computation.193 | loop fusion | bytes 131072 | tf_op jit(solution)/shard_map/slice | solution.py:69
  18.4 1.5 %collective-permute-start.2 = (f32[640,128]{1,0:T(8,128)}, f32[640,128]{1,0:T(8,128)}, u32[]{:S(2)}, u32[]{:S(2)}) collective-permute-start(f32[640,128]{1,0:T(8,128)} %pad_maximum_fusion.2), channel_id=1, source_target_pairs={{0,2},{2,0},{1,3},{3,1},{4,6},{6,4},{5,7},{7,5},{8,10},{10,8},{9,1... | collective-permute-start | bytes 983048 | tf_op jit(solution)/shard_map/ppermute | solution.py:21
  20.0 1.3 %convolution_convert_fusion = bf16[256,1024]{1,0:T(8,128)(2,1)S(1)} fusion(bf16[128,1024]{1,0:T(8,128)(2,1)} %collective-permute-done.1, bf16[128,1024]{1,0:T(8,128)(2,1)} %fusion.3, bf16[256,128]{1,0:T(8,128)(2,1)S(1)} %get-tuple-element.24, bf16[256,128]{1,0:T(8,128)(2,1)S(1)} %get-tuple-element.23), kind=kOutput, calls=%fused_computation.7 | convolution fusion | flops 135790592 | bytes 1179648 | tf_op jit(solution)/shard_map/dot_general | solution.py:128
  21.3 1.4 %fusion.15 = f32[384,512]{1,0:T(8,128)} fusion(f32[384,128]{1,0:T(8,128)S(1)} %slice.285, f32[384,128]{1,0:T(8,128)S(1)} %fusion.71, bf16[256,1024]{1,0:T(8,128)(2,1)S(1)} %convolution_convert_fusion, s32[]{:T(128)S(6)} %select_n.78), kind=kOutput, calls=%fused_computation.32 | convolution fusion | flops 604078080 | bytes 1441796 | tf_op jit(solution)/shard_map/dot_general | solution.py:133
  22.7 1.4 %copy.18 = f32[3,128,512]{1,2,0:T(8,128)S(1)} copy(f32[3,128,512]{2,1,0:T(8,128)} %bitcast.113) | data formatting | bytes 1572864 | tf_op jit(solution)/shard_map/reshape | solution.py:137
  24.1 1.6 %fusion.2 = f32[3,128,512]{1,2,0:T(8,128)S(1)} fusion(f32[3,128,512]{1,2,0:T(8,128)S(1)} %copy.18, f32[3,128,512]{1,2,0:T(8,128)} %collective-permute-done.3, bf16[512,1024]{1,0:T(8,128)(2,1)S(1)} %get-tuple-element.45, s32[]{:T(128)S(6)} %select_n.78, bf16[4,512,128]{2,1,0:T(8,128)(2,1)S(1)} %copy-done.2), kind=kOutput, calls=%fused_computation.9 | convolution fusion | flops 201719808 | bytes 3276804 | tf_op jit(solution)/shard_map/lir,it->lrt/dot_general | solution.py:97
  26.8 2.0 %collective-permute-done.2 = f32[640,128]{1,0:T(8,128)} collective-permute-done((f32[640,128]{1,0:T(8,128)}, f32[640,128]{1,0:T(8,128)}, u32[]{:S(2)}, u32[]{:S(2)}) %collective-permute-start.2) | collective-permute-done | bytes 327712 | tf_op jit(solution)/shard_map/ppermute | solution.py:21
  29.7 1.6 %collective-permute-start.5 = (f32[384,128]{1,0:T(8,128)S(1)}, f32[384,128]{1,0:T(8,128)S(1)}, u32[]{:S(2)}, u32[]{:S(2)}) collective-permute-start(f32[384,128]{1,0:T(8,128)S(1)} %pad_maximum_fusion.4), channel_id=1, source_target_pairs={{0,4},{4,0},{8,12},{12,8},{1,5},{5,1},{9,13},{13,9},{2,6},{6,2},{1... | collective-permute-start | bytes 589832 | tf_op jit(solution)/shard_map/ppermute | solution.py:21
  35.0 1.1 %convolution_convert_fusion.1 = bf16[256,512]{1,0:T(8,128)(2,1)S(1)} fusion(bf16[128,256]{0,1:T(8,128)(2,1)S(1)} %get-tuple-element.10, bf16[128,256]{0,1:T(8,128)(2,1)S(1)} %get-tuple-element.9, bf16[128,512]{0,1:T(8,128)(2,1)S(1)} %fusion.39, bf16[256,128]{1,0:T(8,128)(2,1)} %get-tuple-element.20, bf16[256,128]{1,0:T(8,128)(2,1)} %get-tuple-element.19), kind=kOutput, calls=%fused_computation.10 | convolution fusion | flops 68288512 | bytes 655360 | tf_op jit(solution)/shard_map/dot_general | solution.py:128
  36.8 1.6 %collective-permute-start.6 = (bf16[384,128]{0,1:T(8,128)(2,1)S(1)}, bf16[384,128]{0,1:T(8,128)(2,1)S(1)}, u32[]{:S(2)}, u32[]{:S(2)}) collective-permute-start(bf16[384,128]{0,1:T(8,128)(2,1)S(1)} %pad_maximum_fusion.6), channel_id=1, source_target_pairs={{0,4},{4,0},{8,12},{12,8},{1,5},{5,1},{9,13},{13,9},{2,6},{6,2},{1... | collective-permute-start | bytes 294920 | tf_op jit(solution)/shard_map/ppermute | solution.py:21
  38.5 3.0 %collective-permute-done.6 = bf16[384,128]{0,1:T(8,128)(2,1)S(1)} collective-permute-done((bf16[384,128]{0,1:T(8,128)(2,1)S(1)}, bf16[384,128]{0,1:T(8,128)(2,1)S(1)}, u32[]{:S(2)}, u32[]{:S(2)}) %collective-permute-start.6) | collective-permute-done | bytes 98336 | tf_op jit(solution)/shard_map/ppermute | solution.py:21
  42.4 4.4 %collective-permute-done.8 = bf16[256,64]{0,1:T(8,128)(2,1)S(1)} collective-permute-done((bf16[256,64]{0,1:T(8,128)(2,1)S(1)}, bf16[256,64]{0,1:T(8,128)(2,1)S(1)}, u32[]{:S(2)}, u32[]{:S(2)}) %collective-permute-start.8) | collective-permute-done | bytes 32800 | tf_op jit(solution)/shard_map/ppermute | solution.py:21
  47.1 1.6 %collective-permute-start.9 = (bf16[1,128,128]{1,2,0:T(8,128)(2,1)S(1)}, bf16[1,128,128]{1,2,0:T(8,128)(2,1)S(1)}, u32[]{:S(2)}, u32[]{:S(2)}) collective-permute-start(bf16[1,128,128]{1,2,0:T(8,128)(2,1)S(1)} %fusion.108), channel_id=1, source_target_pairs={{0,4},{4,0},{8,12},{12,8},{1,5},{5,1},{9,13},{13,9},{2,6},{6,2},{1... | collective-permute-start | bytes 98312 | tf_op jit(solution)/shard_map/ppermute | solution.py:21
  48.7 2.3 %collective-permute-done.9 = bf16[1,128,128]{1,2,0:T(8,128)(2,1)S(1)} collective-permute-done((bf16[1,128,128]{1,2,0:T(8,128)(2,1)S(1)}, bf16[1,128,128]{1,2,0:T(8,128)(2,1)S(1)}, u32[]{:S(2)}, u32[]{:S(2)}) %collective-permute-start.9) | collective-permute-done | bytes 32800 | tf_op jit(solution)/shard_map/ppermute | solution.py:21
  51.4 1.2 %collective-permute-start.10 = (bf16[2,128,256]{1,2,0:T(8,128)(2,1)S(1)}, bf16[2,128,256]{1,2,0:T(8,128)(2,1)S(1)}, u32[]{:S(2)}, u32[]{:S(2)}) collective-permute-start(bf16[2,128,256]{1,2,0:T(8,128)(2,1)S(1)} %pad_maximum_fusion.5), channel_id=1, source_target_pairs={{0,2},{2,0},{1,3},{3,1},{4,6},{6,4},{5,7},{7,5},{8,10},{10,8},{9,1... | collective-permute-start | bytes 393224 | tf_op jit(solution)/shard_map/ppermute | solution.py:21
  52.7 3.7 %collective-permute-done.10 = bf16[2,128,256]{1,2,0:T(8,128)(2,1)S(1)} collective-permute-done((bf16[2,128,256]{1,2,0:T(8,128)(2,1)S(1)}, bf16[2,128,256]{1,2,0:T(8,128)(2,1)S(1)}, u32[]{:S(2)}, u32[]{:S(2)}) %collective-permute-start.10) | collective-permute-done | bytes 131104 | tf_op jit(solution)/shard_map/ppermute | solution.py:21
  57.1 1.7 %collective-permute-done.11 = bf16[3,128,512]{1,2,0:T(8,128)(2,1)S(1)} collective-permute-done((bf16[3,128,512]{1,2,0:T(8,128)(2,1)S(1)}, bf16[3,128,512]{1,2,0:T(8,128)(2,1)S(1)}, u32[]{:S(2)}, u32[]{:S(2)}) %collective-permute-start.11) | collective-permute-done | bytes 393248 | tf_op jit(solution)/shard_map/ppermute | solution.py:21
  58.9 1.2 %fusion.6 = bf16[3,128,1024]{1,2,0:T(8,128)(2,1)S(1)} fusion(s32[]{:T(128)S(6)} %select_n.92, bf16[1,128,512]{1,2,0:T(8,128)(2,1)S(1)} %copy.24, bf16[2,128,512]{1,2,0:T(8,128)(2,1)S(1)} %fusion.23, bf16[3,128,512]{1,2,0:T(8,128)(2,1)S(1)} %collective-permute-done.11), kind=kLoop, calls=%fused_computation.22 | loop fusion | flops 3932160 | bytes 1572868 | tf_op jit(solution)/shard_map/concatenate | solution.py:44
  62.2 1.5 %fusion = bf16[512,1024]{1,0:T(8,128)(2,1)} fusion(f32[1024,512]{0,1:T(8,128)S(1)} %fusion.25, f32[1024,512]{0,1:T(8,128)S(1)} %fusion.26, f32[1024,512]{0,1:T(8,128)S(1)} %fusion.27, f32[512,1024]{1,0:T(8,128)S(1)} %copy-done.1, bf16[256,1024]{1,0:T(8,128)(2,1)S(1)} %copy-done.11, bf16[4,512,128]{2,1,0:T(8,128)(2,1)S(1)} %copy-done.4), kind=kOutput, calls=%fused_computation.1 | convolution fusion | flops 136839168 | bytes 9830400 | tf_op jit(solution)/shard_map/dot_general | solution.py:150
  (142 shorter events, 17.5 us)
Async XLA Ops:
  0.0 9.5 %copy-start = (bf16[512,1024]{1,0:T(8,128)(2,1)S(1)}, bf16[512,1024]{1,0:T(8,128)(2,1)}, u32[]{:S(2)}) copy-start(bf16[512,1024]{1,0:T(8,128)(2,1)} %param.5) | copy-start | bytes 3145732
  0.0 6.9 %copy-start.2 = (bf16[4,512,128]{2,1,0:T(8,128)(2,1)S(1)}, bf16[4,512,128]{2,1,0:T(8,128)(2,1)}, u32[]{:S(2)}) copy-start(bf16[4,512,128]{2,1,0:T(8,128)(2,1)} %param.7) | copy-start | bytes 1572868
  0.0 7.2 %slice-start = ((bf16[4,512,128]{2,1,0:T(8,128)(2,1)}), bf16[2,512,128]{2,1,0:T(8,128)(2,1)S(1)}, s32[]{:S(2)}) async-start(bf16[4,512,128]{2,1,0:T(8,128)(2,1)} %param.7), calls=%async_computation | async-start | bytes 524288 | tf_op jit(solution)/shard_map/slice | solution.py:58
  0.0 6.9 %copy-start.3 = (bf16[4,512,128]{2,1,0:T(8,128)(2,1)S(1)}, bf16[4,512,128]{2,1,0:T(8,128)(2,1)}, u32[]{:S(2)}) copy-start(bf16[4,512,128]{2,1,0:T(8,128)(2,1)} %param.8) | copy-start | bytes 1572868
  1.2 13.4 %copy-start.16 = (bf16[128,128]{1,0:T(8,128)(2,1)}, bf16[128,128]{1,0:T(8,128)(2,1)S(1)}, u32[]{:S(2)}) copy-start(bf16[128,128]{1,0:T(8,128)(2,1)S(1)} %get-tuple-element.47) | copy-start | bytes 98308
  1.2 13.4 %copy-start.18 = (bf16[128,128]{1,0:T(8,128)(2,1)}, bf16[128,128]{1,0:T(8,128)(2,1)S(1)}, u32[]{:S(2)}) copy-start(bf16[128,128]{1,0:T(8,128)(2,1)S(1)} %get-tuple-element.48) | copy-start | bytes 98308
  1.8 13.4 %collective-permute-start.7 = (bf16[256,128]{1,0:T(8,128)(2,1)}, bf16[256,128]{1,0:T(8,128)(2,1)}, u32[]{:S(2)}, u32[]{:S(2)}) collective-permute-start(bf16[256,128]{1,0:T(8,128)(2,1)} %fusion.83), channel_id=1, source_target_pairs={{0,8},{4,12},{8,0},{12,4},{1,9},{5,13},{9,1},{13,5},{2,10},{6,14},... | collective-permute-start | bytes 196616 | tf_op jit(solution)/shard_map/ppermute | solution.py:21
  8.1 7.1 %copy-start.20 = (bf16[128,128]{1,0:T(8,128)(2,1)}, bf16[128,128]{1,0:T(8,128)(2,1)S(1)}, u32[]{:S(2)}) copy-start(bf16[128,128]{1,0:T(8,128)(2,1)S(1)} %get-tuple-element.37) | copy-start | bytes 98308
  8.1 7.1 %copy-start.22 = (bf16[128,128]{1,0:T(8,128)(2,1)}, bf16[128,128]{1,0:T(8,128)(2,1)S(1)}, u32[]{:S(2)}) copy-start(bf16[128,128]{1,0:T(8,128)(2,1)S(1)} %get-tuple-element.38) | copy-start | bytes 98308
  9.5 7.1 %collective-permute-start = (f32[1024,128]{1,0:T(8,128)}, f32[1024,128]{1,0:T(8,128)S(1)}, u32[]{:S(2)}, u32[]{:S(2)}) collective-permute-start(f32[1024,128]{1,0:T(8,128)} %pad_maximum_fusion), channel_id=1, source_target_pairs={{0,1},{1,0},{2,3},{3,2},{4,5},{5,4},{6,7},{7,6},{8,9},{9,8},{10,11... | collective-permute-start | bytes 1572872 | tf_op jit(solution)/shard_map/ppermute | solution.py:21
  12.6 7.3 %collective-permute-start.1 = (bf16[128,1024]{1,0:T(8,128)(2,1)}, bf16[128,1024]{1,0:T(8,128)(2,1)}, u32[]{:S(2)}, u32[]{:S(2)}) collective-permute-start(bf16[128,1024]{1,0:T(8,128)(2,1)} %fusion.3), channel_id=1, source_target_pairs={{0,1},{1,0},{2,3},{3,2},{4,5},{5,4},{6,7},{7,6},{8,9},{9,8},{10,11... | collective-permute-start | bytes 786440 | tf_op jit(solution)/shard_map/ppermute | solution.py:21
  14.5 9.6 %collective-permute-start.3 = (f32[3,128,512]{1,2,0:T(8,128)}, f32[3,128,512]{1,2,0:T(8,128)}, u32[]{:S(2)}, u32[]{:S(2)}) collective-permute-start(f32[3,128,512]{1,2,0:T(8,128)} %convolution_bitcast_fusion), channel_id=1, source_target_pairs={{0,1},{1,0},{2,3},{3,2},{4,5},{5,4},{6,7},{7,6},{8,9},{9,8},{10,11... | collective-permute-start | bytes 2359304 | tf_op jit(solution)/shard_map/ppermute | solution.py:21
  18.4 10.4 %collective-permute-start.2 = (f32[640,128]{1,0:T(8,128)}, f32[640,128]{1,0:T(8,128)}, u32[]{:S(2)}, u32[]{:S(2)}) collective-permute-start(f32[640,128]{1,0:T(8,128)} %pad_maximum_fusion.2), channel_id=1, source_target_pairs={{0,2},{2,0},{1,3},{3,1},{4,6},{6,4},{5,7},{7,5},{8,10},{10,8},{9,1... | collective-permute-start | bytes 983048 | tf_op jit(solution)/shard_map/ppermute | solution.py:21
  25.8 7.5 %copy-start.21 = (bf16[128,128]{1,0:T(8,128)(2,1)S(1)}, bf16[128,128]{1,0:T(8,128)(2,1)}, u32[]{:S(2)}) copy-start(bf16[128,128]{1,0:T(8,128)(2,1)} %copy-done.20) | copy-start | bytes 98308
  25.8 7.5 %copy-start.23 = (bf16[128,128]{1,0:T(8,128)(2,1)S(1)}, bf16[128,128]{1,0:T(8,128)(2,1)}, u32[]{:S(2)}) copy-start(bf16[128,128]{1,0:T(8,128)(2,1)} %copy-done.22) | copy-start | bytes 98308
  26.2 8.5 %collective-permute-start.4 = (bf16[512,256]{0,1:T(8,128)(2,1)S(1)}, bf16[512,256]{0,1:T(8,128)(2,1)S(1)}, u32[]{:S(2)}, u32[]{:S(2)}) collective-permute-start(bf16[512,256]{0,1:T(8,128)(2,1)S(1)} %pad_maximum_fusion.3), channel_id=1, source_target_pairs={{0,2},{2,0},{1,3},{3,1},{4,6},{6,4},{5,7},{7,5},{8,10},{10,8},{9,1... | collective-permute-start | bytes 786440 | tf_op jit(solution)/shard_map/ppermute | solution.py:21
  29.7 7.0 %collective-permute-start.5 = (f32[384,128]{1,0:T(8,128)S(1)}, f32[384,128]{1,0:T(8,128)S(1)}, u32[]{:S(2)}, u32[]{:S(2)}) collective-permute-start(f32[384,128]{1,0:T(8,128)S(1)} %pad_maximum_fusion.4), channel_id=1, source_target_pairs={{0,4},{4,0},{8,12},{12,8},{1,5},{5,1},{9,13},{13,9},{2,6},{6,2},{1... | collective-permute-start | bytes 589832 | tf_op jit(solution)/shard_map/ppermute | solution.py:21
  36.4 5.9 %copy-start.13 = (bf16[128,128]{1,0:T(8,128)(2,1)S(1)}, bf16[128,128]{1,0:T(8,128)(2,1)}, u32[]{:S(2)}) copy-start(bf16[128,128]{1,0:T(8,128)(2,1)} %copy-done.12) | copy-start | bytes 98308
  36.8 4.7 %collective-permute-start.6 = (bf16[384,128]{0,1:T(8,128)(2,1)S(1)}, bf16[384,128]{0,1:T(8,128)(2,1)S(1)}, u32[]{:S(2)}, u32[]{:S(2)}) collective-permute-start(bf16[384,128]{0,1:T(8,128)(2,1)S(1)} %pad_maximum_fusion.6), channel_id=1, source_target_pairs={{0,4},{4,0},{8,12},{12,8},{1,5},{5,1},{9,13},{13,9},{2,6},{6,2},{1... | collective-permute-start | bytes 294920 | tf_op jit(solution)/shard_map/ppermute | solution.py:21
  42.0 4.9 %collective-permute-start.8 = (bf16[256,64]{0,1:T(8,128)(2,1)S(1)}, bf16[256,64]{0,1:T(8,128)(2,1)S(1)}, u32[]{:S(2)}, u32[]{:S(2)}) collective-permute-start(bf16[256,64]{0,1:T(8,128)(2,1)S(1)} %pad_maximum_fusion.19), channel_id=1, source_target_pairs={{0,8},{4,12},{8,0},{12,4},{1,9},{5,13},{9,1},{13,5},{2,10},{6,14},... | collective-permute-start | bytes 98312 | tf_op jit(solution)/shard_map/ppermute | solution.py:21
  47.1 13.0 %copy-start.4 = (bf16[4,512,128]{2,1,0:T(8,128)(2,1)S(1)}, bf16[4,512,128]{2,1,0:T(8,128)(2,1)}, u32[]{:S(2)}) copy-start(bf16[4,512,128]{2,1,0:T(8,128)(2,1)} %param.8) | copy-start | bytes 1572868
  47.1 4.0 %collective-permute-start.9 = (bf16[1,128,128]{1,2,0:T(8,128)(2,1)S(1)}, bf16[1,128,128]{1,2,0:T(8,128)(2,1)S(1)}, u32[]{:S(2)}, u32[]{:S(2)}) collective-permute-start(bf16[1,128,128]{1,2,0:T(8,128)(2,1)S(1)} %fusion.108), channel_id=1, source_target_pairs={{0,4},{4,0},{8,12},{12,8},{1,5},{5,1},{9,13},{13,9},{2,6},{6,2},{1... | collective-permute-start | bytes 98312 | tf_op jit(solution)/shard_map/ppermute | solution.py:21
  51.4 5.0 %collective-permute-start.10 = (bf16[2,128,256]{1,2,0:T(8,128)(2,1)S(1)}, bf16[2,128,256]{1,2,0:T(8,128)(2,1)S(1)}, u32[]{:S(2)}, u32[]{:S(2)}) collective-permute-start(bf16[2,128,256]{1,2,0:T(8,128)(2,1)S(1)} %pad_maximum_fusion.5), channel_id=1, source_target_pairs={{0,2},{2,0},{1,3},{3,1},{4,6},{6,4},{5,7},{7,5},{8,10},{10,8},{9,1... | collective-permute-start | bytes 393224 | tf_op jit(solution)/shard_map/ppermute | solution.py:21
  57.1 1.8 %collective-permute-start.11 = (bf16[3,128,512]{1,2,0:T(8,128)(2,1)S(1)}, bf16[3,128,512]{1,2,0:T(8,128)(2,1)S(1)}, u32[]{:S(2)}, u32[]{:S(2)}) collective-permute-start(bf16[3,128,512]{1,2,0:T(8,128)(2,1)S(1)} %pad_maximum_fusion.1), channel_id=1, source_target_pairs={{0,1},{1,0},{2,3},{3,2},{4,5},{5,4},{6,7},{7,6},{8,9},{9,8},{10,11... | collective-permute-start | bytes 1179656 | tf_op jit(solution)/shard_map/ppermute | solution.py:21
  (19 other events, 62.3 us)

commit v5 on v4

--- a/solution.py
+++ b/solution.py
@@ -52,22 +52,16 @@
     c0 = jnp.dot(leaf_inverse, templates, preferred_element_type=F32)
     c0b = c0.astype(BF16)
 
-    mine_c = coupling[:, 0]
     partial = [
         jnp.einsum(
             "lir,is->lrs", v_basis[s + 1:], u_basis[s], preferred_element_type=F32
         ).reshape(-1, rank)
         for s in range(levels - 1)
     ]
-    w_own, theirs_c = [None] * levels, []
-    for b in range(levels):
-        c = mine_c[b]
-        parts = [jnp.concatenate([c[:, :rank], c[:, rank:]], axis=0).astype(F32)]
-        parts += partial[b:]
-        got = swap(jnp.concatenate(parts, axis=0), b, bits)
-        theirs = got[: 2 * rank].astype(BF16)
-        theirs_c.append(jnp.concatenate([theirs[:rank], theirs[rank:]], axis=1))
-        at = 2 * rank
+    w_own = [None] * levels
+    for b in range(levels - 1):
+        got = swap(jnp.concatenate(partial[b:], axis=0), b, bits)
+        at = 0
         for s in range(b, levels - 1):
             n = partial[s].shape[0]
             recv = got[at : at + n]
@@ -76,18 +70,14 @@
                 w_own[s] = jnp.concatenate([partial[s], recv], axis=1)
             else:
                 partial[s] = partial[s] + recv
-    couple = []
+
+    couple_own, couple_send = [], []
     for s in range(levels):
         lower = side(s, bits) == 0
-        mine, theirs = mine_c[s], theirs_c[s]
-        first = jnp.concatenate([mine[:, :rank], theirs[:, :rank]], axis=0)
-        second = jnp.concatenate([mine[:, rank:], theirs[:, rank:]], axis=0)
-        couple.append(
-            jnp.concatenate(
-                [jnp.where(lower, first, second), jnp.where(lower, second, first)],
-                axis=1,
-            )
-        )
+        c = coupling[s, 0]
+        rolled = jnp.concatenate([c[:, rank:], c[:, :rank]], axis=1)
+        couple_own.append(jnp.where(lower, c, rolled))
+        couple_send.append(jnp.where(lower, rolled, c))
 
     proj0 = jnp.dot(v_basis[0].T, c0b, preferred_element_type=F32)
     rest = None
@@ -108,6 +98,7 @@
         if s == 0:
             mine_b = proj0.astype(BF16)
             theirs_b = swap(mine_b, s, bits)
+            couple_sib = swap(couple_send[0], s, bits)
         else:
             mine_b = rest[0].astype(BF16)
             rest = rest[1:]
@@ -119,13 +110,18 @@
                 keep = cols(rest, h * w, w)
                 send = cols(rest, (1 - h) * w, w)
                 parts.append(send.astype(BF16).reshape(n * rank, w))
+            parts.append(couple_send[s].reshape(-1, w))
             got = swap(jnp.concatenate(parts, axis=0), s, bits)
             theirs_b = jnp.concatenate([got[:rank], got[rank : 2 * rank]], axis=1)
+            at = 2 * rank
             if n > 0:
-                recv = got[2 * rank :].reshape(n, rank, w).astype(F32)
+                recv = got[at : at + n * rank].reshape(n, rank, w).astype(F32)
                 rest = keep + recv
+                at += n * rank
+            couple_sib = got[at:].reshape(rank, 2 * rank)
         stacked = jnp.concatenate([mine_b, theirs_b], axis=0)
-        coefs = jnp.dot(couple[s], stacked, preferred_element_type=F32).astype(BF16)
+        couple = jnp.concatenate([couple_own[s], couple_sib], axis=0)
+        coefs = jnp.dot(couple, stacked, preferred_element_type=F32).astype(BF16)
         own_coefs.append(coefs[:rank])
         if s < levels - 1:
             w = coefs.shape[1] // 2

time: 64.3 us -> 72.8 us (1.13)
  waiting for transfers between devices: 17.9 us -> 26.9 us
  starting transfers between devices: 13.3 us -> 12.2 us
    ppermute x12, waiting for transfers between devices: 17.9 us -> 26.9 us  [swap(): return lax.ppermute(x, axis, [(i, i ^ 1 << stride) for i in range(n)])]
    select_n x4, other arithmetic: 0.76 us -> 3.06 us  [the longest x2 2.38 us: on_device(): couple_own.append(jnp.where(lower, c, rolled))]
    concatenate x0 -> x4, local copies, waits for them, and re-layouts: none -> 1.82 us  [on_device(): rolled = jnp.concatenate([c[:, rank:], c[:, :rank]], axis=1)]
    convert_element_type x5 -> x1, other arithmetic: 1.35 us -> 0.02 us  [on_device(): recv = got[at:at + n * rank].reshape(n, rank, w).astype(F32)]
    ppermute x12, starting transfers between devices: 13.3 us -> 12.2 us  [swap(): return lax.ppermute(x, axis, [(i, i ^ 1 << stride) for i in range(n)])]
    dot_general x1, matrix products: 2.08 us -> 3.12 us  [on_device(): c0 = jnp.dot(leaf_inverse, templates, preferred_element_type=F32)]
    another operation x3 -> x0, other arithmetic: 1.03 us -> none
    dot_general x2, local copies, waits for them, and re-layouts: 1.2 us -> 0.21 us  [on_device(): jnp.einsum('lir,is->lrs', v_basis[s + 1:], u_basis[s], preferred_element_...]
  transfers between devices with their start and end apart: 12 -> 12, of which waited for: 7 -> 7; matrix products, arithmetic and copies ran while one was open for 36% -> 27% of each run, Pallas kernels for 0% -> 0%
where the time goes in v5:
time: 72.8 us; the launch traced here: 72.3 us
  waiting for transfers between devices  26.9 us (37%)
  matrix products  14 us (19%)
  starting transfers between devices  12.2 us (17%)
  other arithmetic  9.44 us (13%)
  local copies, waits for them, and re-layouts  9.11 us (13%)
    ppermute x12, waiting for transfers between devices, swap(): return lax.ppermute(x, axis, [(i, i ^ 1 << stride) for i in range(n)])  26.9 us
    ppermute x12, starting transfers between devices, swap(): return lax.ppermute(x, axis, [(i, i ^ 1 << stride) for i in range(n)])  12.2 us
    dot_general x1, matrix products, on_device(): c0 = jnp.dot(leaf_inverse, templates, preferred_element_type=F32)  3.12 us
    dot_general x4, matrix products, on_device(): current = current - jnp.dot(u_basis[s], full[s], preferred_element_type=F32)  2.85 us
    add x3, other arithmetic, on_device(): partial[s] = partial[s] + recv  2.47 us
    select_n x2, other arithmetic, on_device(): couple_own.append(jnp.where(lower, c, rolled))  2.38 us
    concatenate x3, other arithmetic, gather_half(): both = jnp.concatenate([x, swap(x, bit, bits), x], axis=-1)  2.09 us
    dot_general x4, matrix products, on_device(): coefs = jnp.dot(couple, stacked, preferred_element_type=F32).astype(BF16)  2.09 us
  transfers between devices with their start and end apart: 12, of which 7 were waited for; matrix products, arithmetic and copies ran while one was open for 27% of the time, Pallas kernels for 0%

profile of v5, /device:TPU:0, one launch (start us, length us, event | category | flops | bytes accessed | tf_op | source)
XLA Modules:
  0.0 72.3 jit_solution(5386808222527662154)
XLA Ops:
  0.0 1.1 %fusion.118 = (bf16[1,1,128,256]{3,2,1,0:T(8,128)(2,1)S(1)}, bf16[128,256]{1,0:T(8,128)(2,1)S(1)}, bf16[128,256]{1,0:T(8,128)(2,1)S(1)}, bf16[1,1,128,256]{3,2,1...) fusion(bf16[4,1,128,256]{3,2,1,0:T(8,128)(2,1)} %param.9), kind=kLoop, calls=%fused_computation.174 | loop fusion | bytes 655360 | tf_op jit(solution)/shard_map/slice | solution.py:77
  1.2 1.7 %broadcast_select_fusion.1 = (bf16[128,256]{1,0:T(8,128)(2,1)}, bf16[128,256]{1,0:T(8,128)(2,1)}, bf16[128,256]{1,0:T(8,128)(2,1)}, bf16[128,256]{1,0:T(8,128)(2...) fusion(pred[]{:T(512)S(6)} %eq.15, bf16[4,1,128,256]{3,2,1,0:T(8,128)(2,1)} %param.9, ...), kind=kLoop, calls=%fused_computation.149 | loop fusion | flops 524288 | bytes 786435 | tf_op jit(solution)/shard_map/jit(_where)/select_n | solution.py:79
  5.3 3.1 %fusion.128 = (bf16[512,1024]{1,0:T(8,128)(2,1)S(1)}, f32[512,1024]{1,0:T(8,128)}) fusion(bf16[512,512]{1,0:T(8,128)(2,1)} %param.6, bf16[512,1024]{1,0:T(8,128)(2,1)S(1)} %copy-done), kind=kOutput, calls=%fused_computation.184 | convolution fusion | flops 537395200 | bytes 4718592 | tf_op jit(solution)/shard_map/dot_general | solution.py:52
  9.3 1.4 %convolution_bitcast_fusion = f32[3,128,512]{1,2,0:T(8,128)} fusion(bf16[512,1024]{1,0:T(8,128)(2,1)S(1)} %get-tuple-element.42, s32[]{:T(128)S(6)} %select_n.84, bf16[4,512,128]{2,1,0:T(8,128)(2,1)S(1)} %copy-done.2), kind=kOutput, calls=%fused_computation.5 | convolution fusion | flops 201326592 | bytes 1703940 | tf_op jit(solution)/shard_map/lir,it->lrt/dot_general | solution.py:91
  15.1 1.4 %convolution_convert_fusion = bf16[256,1024]{1,0:T(8,128)(2,1)S(1)} fusion(bf16[128,1024]{1,0:T(8,128)(2,1)} %collective-permute-done.1, bf16[128,1024]{1,0:T(8,128)(2,1)} %copy-done.12, bf16[128,256]{1,0:T(8,128)(2,1)} %collective-permute-done, bf16[128,256]{1,0:T(8,128)(2,1)} %get-tuple-element.13), kind=kOutput, calls=%fused_computation.7 | convolution fusion | flops 135790592 | bytes 1179648 | tf_op jit(solution)/shard_map/dot_general | solution.py:124
  16.5 1.1 %slice.227 = f32[384,128]{1,0:T(8,128)S(1)} slice(f32[768,128]{1,0:T(8,128)} %collective-permute-done.3), slice={[0:384], [0:128]} | slice | bytes 393216 | tf_op jit(solution)/shard_map/slice | solution.py:67
  17.6 1.4 %fusion.15 = f32[384,512]{1,0:T(8,128)} fusion(f32[384,128]{1,0:T(8,128)S(1)} %slice.227, f32[384,128]{1,0:T(8,128)S(1)} %fusion.69, bf16[256,1024]{1,0:T(8,128)(2,1)S(1)} %convolution_convert_fusion, s32[]{:T(128)S(6)} %select_n.83), kind=kOutput, calls=%fused_computation.32 | convolution fusion | flops 604078080 | bytes 1441796 | tf_op jit(solution)/shard_map/dot_general | solution.py:129
  19.0 1.4 %copy.20 = f32[3,128,512]{1,2,0:T(8,128)S(1)} copy(f32[3,128,512]{2,1,0:T(8,128)} %bitcast.124) | data formatting | bytes 1572864 | tf_op jit(solution)/shard_map/reshape | solution.py:133
  20.4 1.5 %slice_add_fusion.2 = f32[128,128]{1,0:T(8,128)} fusion(f32[128,128]{1,0:T(8,128)S(1)} %fusion.63, f32[768,128]{1,0:T(8,128)} %collective-permute-done.3), kind=kLoop, calls=%fused_computation.131 | loop fusion | flops 16384 | bytes 196608 | tf_op jit(solution)/shard_map/add | solution.py:72
  21.9 1.0 %slice_add_fusion = f32[256,128]{1,0:T(8,128)S(1)} fusion(f32[256,128]{1,0:T(8,128)} %copy-done.5, f32[768,128]{1,0:T(8,128)} %collective-permute-done.3), kind=kLoop, calls=%fused_computation.74 | loop fusion | flops 32768 | bytes 393216 | tf_op jit(solution)/shard_map/add | solution.py:72
  22.9 1.6 %fusion.2 = f32[3,128,512]{1,2,0:T(8,128)S(1)} fusion(f32[3,128,512]{1,2,0:T(8,128)S(1)} %copy.20, f32[3,128,512]{1,2,0:T(8,128)} %collective-permute-done.2, bf16[512,1024]{1,0:T(8,128)(2,1)S(1)} %get-tuple-element.42, s32[]{:T(128)S(6)} %select_n.83, bf16[4,512,128]{2,1,0:T(8,128)(2,1)S(1)} %copy-done.2), kind=kOutput, calls=%fused_computation.9 | convolution fusion | flops 201719808 | bytes 3276804 | tf_op jit(solution)/shard_map/lir,it->lrt/dot_general | solution.py:87
  25.8 3.0 %collective-permute-start.4 = (bf16[640,256]{0,1:T(8,128)(2,1)S(1)}, bf16[640,256]{0,1:T(8,128)(2,1)S(1)}, u32[]{:S(2)}, u32[]{:S(2)}) collective-permute-start(bf16[640,256]{0,1:T(8,128)(2,1)S(1)} %pad_maximum_fusion.2), channel_id=1, source_target_pairs={{0,2},{2,0},{1,3},{3,1},{4,6},{6,4},{5,7},{7,5},{8,10},{10,8},{9,1... | collective-permute-start | bytes 983048 | tf_op jit(solution)/shard_map/ppermute | solution.py:21
  28.9 12.0 %collective-permute-done.5 = f32[384,128]{1,0:T(8,128)S(1)} collective-permute-done((f32[384,128]{1,0:T(8,128)S(1)}, f32[384,128]{1,0:T(8,128)S(1)}, u32[]{:S(2)}, u32[]{:S(2)}) %collective-permute-start.5) | collective-permute-done | bytes 196640 | tf_op jit(solution)/shard_map/ppermute | solution.py:21
  42.2 1.9 %collective-permute-start.6 = (bf16[640,128]{0,1:T(8,128)(2,1)S(1)}, bf16[640,128]{0,1:T(8,128)(2,1)S(1)}, u32[]{:S(2)}, u32[]{:S(2)}) collective-permute-start(bf16[640,128]{0,1:T(8,128)(2,1)S(1)} %pad_maximum_fusion.4), channel_id=1, source_target_pairs={{0,4},{4,0},{8,12},{12,8},{1,5},{5,1},{9,13},{13,9},{2,6},{6,2},{1... | collective-permute-start | bytes 491528 | tf_op jit(solution)/shard_map/ppermute | solution.py:21
  44.3 4.2 %collective-permute-done.6 = bf16[640,128]{0,1:T(8,128)(2,1)S(1)} collective-permute-done((bf16[640,128]{0,1:T(8,128)(2,1)S(1)}, bf16[640,128]{0,1:T(8,128)(2,1)S(1)}, u32[]{:S(2)}, u32[]{:S(2)}) %collective-permute-start.6) | collective-permute-done | bytes 163872 | tf_op jit(solution)/shard_map/ppermute | solution.py:21
  49.5 2.6 %collective-permute-start.8 = (bf16[768,64]{0,1:T(8,128)(2,1)S(1)}, bf16[768,64]{0,1:T(8,128)(2,1)S(1)}, u32[]{:S(2)}, u32[]{:S(2)}) collective-permute-start(bf16[768,64]{0,1:T(8,128)(2,1)S(1)} %pad_maximum_fusion.6), channel_id=1, source_target_pairs={{0,8},{4,12},{8,0},{12,4},{1,9},{5,13},{9,1},{13,5},{2,10},{6,14},... | collective-permute-start | bytes 294920 | tf_op jit(solution)/shard_map/ppermute | solution.py:21
  52.1 3.0 %collective-permute-done.8 = bf16[768,64]{0,1:T(8,128)(2,1)S(1)} collective-permute-done((bf16[768,64]{0,1:T(8,128)(2,1)S(1)}, bf16[768,64]{0,1:T(8,128)(2,1)S(1)}, u32[]{:S(2)}, u32[]{:S(2)}) %collective-permute-start.8) | collective-permute-done | bytes 98336 | tf_op jit(solution)/shard_map/ppermute | solution.py:21
  55.6 1.7 %collective-permute-start.9 = (bf16[1,128,128]{1,2,0:T(8,128)(2,1)S(1)}, bf16[1,128,128]{1,2,0:T(8,128)(2,1)S(1)}, u32[]{:S(2)}, u32[]{:S(2)}) collective-permute-start(bf16[1,128,128]{1,2,0:T(8,128)(2,1)S(1)} %fusion.104), channel_id=1, source_target_pairs={{0,4},{4,0},{8,12},{12,8},{1,5},{5,1},{9,13},{13,9},{2,6},{6,2},{1... | collective-permute-start | bytes 98312 | tf_op jit(solution)/shard_map/ppermute | solution.py:21
  57.4 2.3 %collective-permute-done.9 = bf16[1,128,128]{1,2,0:T(8,128)(2,1)S(1)} collective-permute-done((bf16[1,128,128]{1,2,0:T(8,128)(2,1)S(1)}, bf16[1,128,128]{1,2,0:T(8,128)(2,1)S(1)}, u32[]{:S(2)}, u32[]{:S(2)}) %collective-permute-start.9) | collective-permute-done | bytes 32800 | tf_op jit(solution)/shard_map/ppermute | solution.py:21
  59.9 1.5 %collective-permute-start.10 = (bf16[2,128,256]{1,2,0:T(8,128)(2,1)S(1)}, bf16[2,128,256]{1,2,0:T(8,128)(2,1)S(1)}, u32[]{:S(2)}, u32[]{:S(2)}) collective-permute-start(bf16[2,128,256]{1,2,0:T(8,128)(2,1)S(1)} %pad_maximum_fusion.5), channel_id=1, source_target_pairs={{0,2},{2,0},{1,3},{3,1},{4,6},{6,4},{5,7},{7,5},{8,10},{10,8},{9,1... | collective-permute-start | bytes 393224 | tf_op jit(solution)/shard_map/ppermute | solution.py:21
  61.6 3.4 %collective-permute-done.10 = bf16[2,128,256]{1,2,0:T(8,128)(2,1)S(1)} collective-permute-done((bf16[2,128,256]{1,2,0:T(8,128)(2,1)S(1)}, bf16[2,128,256]{1,2,0:T(8,128)(2,1)S(1)}, u32[]{:S(2)}, u32[]{:S(2)}) %collective-permute-start.10) | collective-permute-done | bytes 131104 | tf_op jit(solution)/shard_map/ppermute | solution.py:21
  65.7 1.7 %collective-permute-done.11 = bf16[3,128,512]{1,2,0:T(8,128)(2,1)S(1)} collective-permute-done((bf16[3,128,512]{1,2,0:T(8,128)(2,1)S(1)}, bf16[3,128,512]{1,2,0:T(8,128)(2,1)S(1)}, u32[]{:S(2)}, u32[]{:S(2)}) %collective-permute-start.11) | collective-permute-done | bytes 393248 | tf_op jit(solution)/shard_map/ppermute | solution.py:21
  67.4 1.2 %fusion.6 = bf16[3,128,1024]{1,2,0:T(8,128)(2,1)S(1)} fusion(s32[]{:T(128)S(6)} %select_n.100, bf16[1,128,512]{1,2,0:T(8,128)(2,1)S(1)} %copy.32, bf16[2,128,512]{1,2,0:T(8,128)(2,1)S(1)} %fusion.23, bf16[3,128,512]{1,2,0:T(8,128)(2,1)S(1)} %collective-permute-done.11), kind=kLoop, calls=%fused_computation.22 | loop fusion | flops 3932160 | bytes 1572868 | tf_op jit(solution)/shard_map/concatenate | solution.py:44
  70.8 1.5 %fusion = bf16[512,1024]{1,0:T(8,128)(2,1)} fusion(f32[1024,512]{0,1:T(8,128)S(1)} %fusion.25, f32[1024,512]{0,1:T(8,128)S(1)} %fusion.26, f32[1024,512]{0,1:T(8,128)S(1)} %fusion.27, f32[512,1024]{1,0:T(8,128)S(1)} %copy-done.1, bf16[256,1024]{1,0:T(8,128)(2,1)S(1)} %copy-done.8, bf16[4,512,128]{2,1,0:T(8,128)(2,1)S(1)} %copy-done.4), kind=kOutput, calls=%fused_computation.1 | convolution fusion | flops 136839168 | bytes 9830400 | tf_op jit(solution)/shard_map/dot_general | solution.py:146
  (117 shorter events, 14.9 us)
Async XLA Ops:
  0.0 5.3 %copy-start = (bf16[512,1024]{1,0:T(8,128)(2,1)S(1)}, bf16[512,1024]{1,0:T(8,128)(2,1)}, u32[]{:S(2)}) copy-start(bf16[512,1024]{1,0:T(8,128)(2,1)} %param.5) | copy-start | bytes 3145732
  0.0 3.3 %copy-start.2 = (bf16[4,512,128]{2,1,0:T(8,128)(2,1)S(1)}, bf16[4,512,128]{2,1,0:T(8,128)(2,1)}, u32[]{:S(2)}) copy-start(bf16[4,512,128]{2,1,0:T(8,128)(2,1)} %param.7) | copy-start | bytes 1572868
  0.0 3.6 %slice-start = ((bf16[4,512,128]{2,1,0:T(8,128)(2,1)}), bf16[2,512,128]{2,1,0:T(8,128)(2,1)S(1)}, s32[]{:S(2)}) async-start(bf16[4,512,128]{2,1,0:T(8,128)(2,1)} %param.7), calls=%async_computation | async-start | bytes 524288 | tf_op jit(solution)/shard_map/slice | solution.py:57
  0.0 3.4 %copy-start.3 = (bf16[4,512,128]{2,1,0:T(8,128)(2,1)S(1)}, bf16[4,512,128]{2,1,0:T(8,128)(2,1)}, u32[]{:S(2)}) copy-start(bf16[4,512,128]{2,1,0:T(8,128)(2,1)} %param.8) | copy-start | bytes 1572868
  2.9 12.2 %collective-permute-start = (bf16[128,256]{1,0:T(8,128)(2,1)}, bf16[128,256]{1,0:T(8,128)(2,1)}, u32[]{:S(2)}, u32[]{:S(2)}) collective-permute-start(bf16[128,256]{1,0:T(8,128)(2,1)} %get-tuple-element.12), channel_id=1, source_target_pairs={{0,1},{1,0},{2,3},{3,2},{4,5},{5,4},{6,7},{7,6},{8,9},{9,8},{10,11... | collective-permute-start | bytes 196616 | tf_op jit(solution)/shard_map/ppermute | solution.py:21
  5.2 11.2 %collective-permute-start.3 = (f32[768,128]{1,0:T(8,128)}, f32[768,128]{1,0:T(8,128)}, u32[]{:S(2)}, u32[]{:S(2)}) collective-permute-start(f32[768,128]{1,0:T(8,128)} %pad_maximum_fusion), channel_id=1, source_target_pairs={{0,1},{1,0},{2,3},{3,2},{4,5},{5,4},{6,7},{7,6},{8,9},{9,8},{10,11... | collective-permute-start | bytes 1179656 | tf_op jit(solution)/shard_map/ppermute | solution.py:21
  8.8 6.3 %copy-start.12 = (bf16[128,1024]{1,0:T(8,128)(2,1)}, bf16[128,1024]{1,0:T(8,128)(2,1)S(1)}, u32[]{:S(2)}) copy-start(bf16[128,1024]{1,0:T(8,128)(2,1)S(1)} %fusion.3) | copy-start | bytes 786436
  8.8 6.3 %collective-permute-start.1 = (bf16[128,1024]{1,0:T(8,128)(2,1)S(1)}, bf16[128,1024]{1,0:T(8,128)(2,1)}, u32[]{:S(2)}, u32[]{:S(2)}) collective-permute-start(bf16[128,1024]{1,0:T(8,128)(2,1)S(1)} %fusion.3), channel_id=1, source_target_pairs={{0,1},{1,0},{2,3},{3,2},{4,5},{5,4},{6,7},{7,6},{8,9},{9,8},{10,11... | collective-permute-start | bytes 786440 | tf_op jit(solution)/shard_map/ppermute | solution.py:21
  10.7 12.2 %collective-permute-start.2 = (f32[3,128,512]{1,2,0:T(8,128)}, f32[3,128,512]{1,2,0:T(8,128)}, u32[]{:S(2)}, u32[]{:S(2)}) collective-permute-start(f32[3,128,512]{1,2,0:T(8,128)} %convolution_bitcast_fusion), channel_id=1, source_target_pairs={{0,1},{1,0},{2,3},{3,2},{4,5},{5,4},{6,7},{7,6},{8,9},{9,8},{10,11... | collective-permute-start | bytes 2359304 | tf_op jit(solution)/shard_map/ppermute | solution.py:21
  24.5 4.3 %copy-start.6 = (f32[128,128]{1,0:T(8,128)S(1)}, f32[128,128]{1,0:T(8,128)}, u32[]{:S(2)}) copy-start(f32[128,128]{1,0:T(8,128)} %slice_add_fusion.2) | copy-start | bytes 196612
  24.5 4.4 %copy-start.10 = (bf16[512,64]{0,1:T(8,128)(2,1)S(1)}, bf16[512,64]{0,1:T(8,128)(2,1)}, u32[]{:S(2)}) copy-start(bf16[512,64]{0,1:T(8,128)(2,1)} %copy.30) | copy-start | bytes 196612
  24.5 4.4 %copy-start.11 = (bf16[512,64]{0,1:T(8,128)(2,1)S(1)}, bf16[512,64]{0,1:T(8,128)(2,1)}, u32[]{:S(2)}) copy-start(bf16[512,64]{0,1:T(8,128)(2,1)} %copy.29) | copy-start | bytes 196612
  24.6 16.6 %copy-start.13 = (bf16[128,256]{0,1:T(8,128)(2,1)S(1)}, bf16[128,256]{0,1:T(8,128)(2,1)}, u32[]{:S(2)}) copy-start(bf16[128,256]{0,1:T(8,128)(2,1)} %get-tuple-element.22) | copy-start | bytes 196612
  25.8 15.2 %collective-permute-start.4 = (bf16[640,256]{0,1:T(8,128)(2,1)S(1)}, bf16[640,256]{0,1:T(8,128)(2,1)S(1)}, u32[]{:S(2)}, u32[]{:S(2)}) collective-permute-start(bf16[640,256]{0,1:T(8,128)(2,1)S(1)} %pad_maximum_fusion.2), channel_id=1, source_target_pairs={{0,2},{2,0},{1,3},{3,1},{4,6},{6,4},{5,7},{7,5},{8,10},{10,8},{9,1... | collective-permute-start | bytes 983048 | tf_op jit(solution)/shard_map/ppermute | solution.py:21
  28.8 12.1 %collective-permute-start.5 = (f32[384,128]{1,0:T(8,128)S(1)}, f32[384,128]{1,0:T(8,128)S(1)}, u32[]{:S(2)}, u32[]{:S(2)}) collective-permute-start(f32[384,128]{1,0:T(8,128)S(1)} %pad_maximum_fusion.3), channel_id=1, source_target_pairs={{0,2},{2,0},{1,3},{3,1},{4,6},{6,4},{5,7},{7,5},{8,10},{10,8},{9,1... | collective-permute-start | bytes 589832 | tf_op jit(solution)/shard_map/ppermute | solution.py:21
  41.8 6.9 %copy-start.15 = (bf16[128,256]{1,0:T(8,128)(2,1)S(1)}, bf16[128,256]{1,0:T(8,128)(2,1)}, u32[]{:S(2)}) copy-start(bf16[128,256]{1,0:T(8,128)(2,1)} %get-tuple-element.11) | copy-start | bytes 196612
  42.0 13.4 %copy-start.14 = (bf16[128,256]{1,0:T(8,128)(2,1)S(1)}, bf16[128,256]{1,0:T(8,128)(2,1)}, u32[]{:S(2)}) copy-start(bf16[128,256]{1,0:T(8,128)(2,1)} %get-tuple-element.10) | copy-start | bytes 196612
  42.2 6.4 %collective-permute-start.6 = (bf16[640,128]{0,1:T(8,128)(2,1)S(1)}, bf16[640,128]{0,1:T(8,128)(2,1)S(1)}, u32[]{:S(2)}, u32[]{:S(2)}) collective-permute-start(bf16[640,128]{0,1:T(8,128)(2,1)S(1)} %pad_maximum_fusion.4), channel_id=1, source_target_pairs={{0,4},{4,0},{8,12},{12,8},{1,5},{5,1},{9,13},{13,9},{2,6},{6,2},{1... | collective-permute-start | bytes 491528 | tf_op jit(solution)/shard_map/ppermute | solution.py:21
  44.1 5.2 %collective-permute-start.7 = (f32[128,128]{1,0:T(8,128)S(1)}, f32[128,128]{1,0:T(8,128)S(1)}, u32[]{:S(2)}, u32[]{:S(2)}) collective-permute-start(f32[128,128]{1,0:T(8,128)S(1)} %slice_add_fusion.1), channel_id=1, source_target_pairs={{0,4},{4,0},{8,12},{12,8},{1,5},{5,1},{9,13},{13,9},{2,6},{6,2},{1... | collective-permute-start | bytes 196616 | tf_op jit(solution)/shard_map/ppermute | solution.py:21
  49.5 5.6 %collective-permute-start.8 = (bf16[768,64]{0,1:T(8,128)(2,1)S(1)}, bf16[768,64]{0,1:T(8,128)(2,1)S(1)}, u32[]{:S(2)}, u32[]{:S(2)}) collective-permute-start(bf16[768,64]{0,1:T(8,128)(2,1)S(1)} %pad_maximum_fusion.6), channel_id=1, source_target_pairs={{0,8},{4,12},{8,0},{12,4},{1,9},{5,13},{9,1},{13,5},{2,10},{6,14},... | collective-permute-start | bytes 294920 | tf_op jit(solution)/shard_map/ppermute | solution.py:21
  55.6 13.0 %copy-start.4 = (bf16[4,512,128]{2,1,0:T(8,128)(2,1)S(1)}, bf16[4,512,128]{2,1,0:T(8,128)(2,1)}, u32[]{:S(2)}) copy-start(bf16[4,512,128]{2,1,0:T(8,128)(2,1)} %param.8) | copy-start | bytes 1572868
  55.6 4.0 %collective-permute-start.9 = (bf16[1,128,128]{1,2,0:T(8,128)(2,1)S(1)}, bf16[1,128,128]{1,2,0:T(8,128)(2,1)S(1)}, u32[]{:S(2)}, u32[]{:S(2)}) collective-permute-start(bf16[1,128,128]{1,2,0:T(8,128)(2,1)S(1)} %fusion.104), channel_id=1, source_target_pairs={{0,4},{4,0},{8,12},{12,8},{1,5},{5,1},{9,13},{13,9},{2,6},{6,2},{1... | collective-permute-start | bytes 98312 | tf_op jit(solution)/shard_map/ppermute | solution.py:21
  59.9 5.0 %collective-permute-start.10 = (bf16[2,128,256]{1,2,0:T(8,128)(2,1)S(1)}, bf16[2,128,256]{1,2,0:T(8,128)(2,1)S(1)}, u32[]{:S(2)}, u32[]{:S(2)}) collective-permute-start(bf16[2,128,256]{1,2,0:T(8,128)(2,1)S(1)} %pad_maximum_fusion.5), channel_id=1, source_target_pairs={{0,2},{2,0},{1,3},{3,1},{4,6},{6,4},{5,7},{7,5},{8,10},{10,8},{9,1... | collective-permute-start | bytes 393224 | tf_op jit(solution)/shard_map/ppermute | solution.py:21
  65.6 1.8 %collective-permute-start.11 = (bf16[3,128,512]{1,2,0:T(8,128)(2,1)S(1)}, bf16[3,128,512]{1,2,0:T(8,128)(2,1)S(1)}, u32[]{:S(2)}, u32[]{:S(2)}) collective-permute-start(bf16[3,128,512]{1,2,0:T(8,128)(2,1)S(1)} %pad_maximum_fusion.1), channel_id=1, source_target_pairs={{0,1},{1,0},{2,3},{3,2},{4,5},{5,4},{6,7},{7,6},{8,9},{9,8},{10,11... | collective-permute-start | bytes 1179656 | tf_op jit(solution)/shard_map/ppermute | solution.py:21
  (5 other events, 7.9 us)

commit v6 on v5

--- a/solution.py
+++ b/solution.py
@@ -111,7 +111,10 @@
                 send = cols(rest, (1 - h) * w, w)
                 parts.append(send.astype(BF16).reshape(n * rank, w))
             parts.append(couple_send[s].reshape(-1, w))
-            got = swap(jnp.concatenate(parts, axis=0), s, bits)
+            payload = jnp.concatenate(parts, axis=0)
+            if s < levels - 1:
+                payload, w_own[s] = lax.optimization_barrier((payload, w_own[s]))
+            got = swap(payload, s, bits)
             theirs_b = jnp.concatenate([got[:rank], got[rank : 2 * rank]], axis=1)
             at = 2 * rank
             if n > 0:

time: 72.8 us -> 72.9 us (level)
  waiting for transfers between devices: 26.9 us -> 23.3 us
  other arithmetic: 9.44 us -> 11 us
  local copies, waits for them, and re-layouts: 9.11 us -> 10.6 us
    ppermute x12, waiting for transfers between devices: 26.9 us -> 23.3 us  [swap(): return lax.ppermute(x, axis, [(i, i ^ 1 << stride) for i in range(n)])]
    slice x2, local copies, waits for them, and re-layouts: 1.14 us -> 2.04 us  [on_device(): recv = got[at:at + n]]
    add x3, other arithmetic: 2.47 us -> 3.28 us  [on_device(): partial[s] = partial[s] + recv]
    concatenate x3 -> x5, other arithmetic: 0.91 us -> 1.69 us  [the longest x2 1.62 us: on_device(): w_own[s] = jnp.concatenate([partial[s], recv], axis=1)]
  transfers between devices with their start and end apart: 12 -> 12, of which waited for: 7 -> 7; matrix products, arithmetic and copies ran while one was open for 27% -> 33% of each run, Pallas kernels for 0% -> 0%
where the time goes in v6:
time: 72.9 us; the launch traced here: 72.3 us
  waiting for transfers between devices  23.3 us (32%)
  matrix products  13.9 us (19%)
  starting transfers between devices  12.7 us (17%)
  other arithmetic  11 us (15%)
  local copies, waits for them, and re-layouts  10.6 us (15%)
    ppermute x12, waiting for transfers between devices, swap(): return lax.ppermute(x, axis, [(i, i ^ 1 << stride) for i in range(n)])  23.3 us
    ppermute x12, starting transfers between devices, swap(): return lax.ppermute(x, axis, [(i, i ^ 1 << stride) for i in range(n)])  12.7 us
    add x3, other arithmetic, on_device(): partial[s] = partial[s] + recv  3.28 us
    dot_general x1, matrix products, on_device(): c0 = jnp.dot(leaf_inverse, templates, preferred_element_type=F32)  3.12 us
    dot_general x4, matrix products, on_device(): current = current - jnp.dot(u_basis[s], full[s], preferred_element_type=F32)  2.85 us
    select_n x2, other arithmetic, on_device(): couple_own.append(jnp.where(lower, c, rolled))  2.35 us
    concatenate x3, other arithmetic, gather_half(): both = jnp.concatenate([x, swap(x, bit, bits), x], axis=-1)  2.09 us
    slice x2, local copies, waits for them, and re-layouts, on_device(): recv = got[at:at + n]  2.04 us
  transfers between devices with their start and end apart: 12, of which 7 were waited for; matrix products, arithmetic and copies ran while one was open for 33% of the time, Pallas kernels for 0%

profile of v6, /device:TPU:0, one launch (start us, length us, event | category | flops | bytes accessed | tf_op | source)
XLA Modules:
  0.0 72.3 jit_solution(9352647021032729307)
XLA Ops:
  0.0 1.7 %fusion.106 = (bf16[1,1,128,256]{3,2,1,0:T(8,128)(2,1)}, bf16[128,256]{1,0:T(8,128)(2,1)S(1)}, bf16[128,256]{1,0:T(8,128)(2,1)S(1)}, bf16[1,1,128,256]{3,2,1,0:T...) fusion(bf16[4,1,128,256]{3,2,1,0:T(8,128)(2,1)} %param.9), kind=kLoop, calls=%fused_computation.168 | loop fusion | bytes 655360 | tf_op jit(solution)/shard_map/slice | solution.py:77
  1.8 1.7 %broadcast_select_fusion.1 = (bf16[128,256]{1,0:T(8,128)(2,1)}, bf16[128,256]{1,0:T(8,128)(2,1)}, bf16[128,256]{1,0:T(8,128)(2,1)}, bf16[128,256]{1,0:T(8,128)(2...) fusion(pred[]{:T(512)S(6)} %eq.15, bf16[4,1,128,256]{3,2,1,0:T(8,128)(2,1)} %param.9, ...), kind=kLoop, calls=%fused_computation.145 | loop fusion | flops 524288 | bytes 786435 | tf_op jit(solution)/shard_map/jit(_where)/select_n | solution.py:79
  5.9 3.1 %fusion.116 = (bf16[512,1024]{1,0:T(8,128)(2,1)S(1)}, f32[512,1024]{1,0:T(8,128)}) fusion(bf16[512,512]{1,0:T(8,128)(2,1)} %param.6, bf16[512,1024]{1,0:T(8,128)(2,1)S(1)} %copy-done), kind=kOutput, calls=%fused_computation.178 | convolution fusion | flops 537395200 | bytes 4718592 | tf_op jit(solution)/shard_map/dot_general | solution.py:52
  9.9 1.4 %convolution_bitcast_fusion = f32[3,128,512]{1,2,0:T(8,128)} fusion(bf16[512,1024]{1,0:T(8,128)(2,1)S(1)} %get-tuple-element.50, s32[]{:T(128)S(6)} %select_n.84, bf16[4,512,128]{2,1,0:T(8,128)(2,1)S(1)} %copy-done.2), kind=kOutput, calls=%fused_computation.5 | convolution fusion | flops 201326592 | bytes 1703940 | tf_op jit(solution)/shard_map/lir,it->lrt/dot_general | solution.py:91
  14.5 0.9 %slice_add_fusion = f32[256,128]{1,0:T(8,128)S(1)} fusion(f32[256,128]{1,0:T(8,128)S(1)} %fusion.60, f32[768,128]{1,0:T(8,128)} %collective-permute-done.3), kind=kLoop, calls=%fused_computation.73 | loop fusion | flops 32768 | bytes 393216 | tf_op jit(solution)/shard_map/add | solution.py:72
  16.9 3.0 %collective-permute-start.4 = (f32[384,128]{1,0:T(8,128)}, f32[384,128]{1,0:T(8,128)}, u32[]{:S(2)}, u32[]{:S(2)}) collective-permute-start(f32[384,128]{1,0:T(8,128)} %pad_maximum_fusion.4), channel_id=1, source_target_pairs={{0,2},{2,0},{1,3},{3,1},{4,6},{6,4},{5,7},{7,5},{8,10},{10,8},{9,1... | collective-permute-start | bytes 589832 | tf_op jit(solution)/shard_map/ppermute | solution.py:21
  19.9 1.3 %convolution_convert_fusion = bf16[256,1024]{1,0:T(8,128)(2,1)S(1)} fusion(bf16[128,1024]{1,0:T(8,128)(2,1)} %collective-permute-done.1, bf16[128,1024]{1,0:T(8,128)(2,1)S(1)} %fusion.3, bf16[128,256]{1,0:T(8,128)(2,1)} %collective-permute-done, bf16[128,256]{1,0:T(8,128)(2,1)} %get-tuple-element.21), kind=kOutput, calls=%fused_computation.7 | convolution fusion | flops 135790592 | bytes 1179648 | tf_op jit(solution)/shard_map/dot_general | solution.py:127
  21.3 1.1 %slice.227 = f32[384,128]{1,0:T(8,128)S(1)} slice(f32[768,128]{1,0:T(8,128)} %collective-permute-done.3), slice={[0:384], [0:128]} | slice | bytes 393216 | tf_op jit(solution)/shard_map/slice | solution.py:67
  22.4 1.4 %fusion.15 = f32[384,512]{1,0:T(8,128)} fusion(f32[384,128]{1,0:T(8,128)S(1)} %slice.227, f32[384,128]{1,0:T(8,128)S(1)} %fusion.62, bf16[256,1024]{1,0:T(8,128)(2,1)S(1)} %convolution_convert_fusion, s32[]{:T(128)S(6)} %select_n.83), kind=kOutput, calls=%fused_computation.32 | convolution fusion | flops 604078080 | bytes 1441796 | tf_op jit(solution)/shard_map/dot_general | solution.py:132
  23.8 1.4 %copy.20 = f32[3,128,512]{1,2,0:T(8,128)S(1)} copy(f32[3,128,512]{2,1,0:T(8,128)} %bitcast.126) | data formatting | bytes 1572864 | tf_op jit(solution)/shard_map/reshape | solution.py:136
  25.3 1.5 %slice_add_fusion.1 = f32[128,128]{1,0:T(8,128)} fusion(f32[128,128]{1,0:T(8,128)} %copy-done.6, f32[384,128]{1,0:T(8,128)} %collective-permute-done.4), kind=kLoop, calls=%fused_computation.126 | loop fusion | flops 16384 | bytes 196608 | tf_op jit(solution)/shard_map/add | solution.py:72
  26.8 1.8 %collective-permute-start.6 = (f32[128,128]{1,0:T(8,128)}, f32[128,128]{1,0:T(8,128)}, u32[]{:S(2)}, u32[]{:S(2)}) collective-permute-start(f32[128,128]{1,0:T(8,128)} %slice_add_fusion.1), channel_id=1, source_target_pairs={{0,4},{4,0},{8,12},{12,8},{1,5},{5,1},{9,13},{13,9},{2,6},{6,2},{1... | collective-permute-start | bytes 196616 | tf_op jit(solution)/shard_map/ppermute | solution.py:21
  30.3 1.6 %fusion.2 = f32[3,128,512]{1,2,0:T(8,128)S(1)} fusion(f32[3,128,512]{1,2,0:T(8,128)S(1)} %copy.20, f32[3,128,512]{1,2,0:T(8,128)} %collective-permute-done.2, bf16[512,1024]{1,0:T(8,128)(2,1)S(1)} %get-tuple-element.50, s32[]{:T(128)S(6)} %select_n.83, bf16[4,512,128]{2,1,0:T(8,128)(2,1)S(1)} %copy-done.2), kind=kOutput, calls=%fused_computation.9 | convolution fusion | flops 201719808 | bytes 3276804 | tf_op jit(solution)/shard_map/lir,it->lrt/dot_general | solution.py:87
  32.4 1.6 %collective-permute-start.5 = (bf16[640,256]{0,1:T(8,128)(2,1)S(1)}, bf16[640,256]{0,1:T(8,128)(2,1)S(1)}, u32[]{:S(2)}, u32[]{:S(2)}) collective-permute-start(bf16[640,256]{0,1:T(8,128)(2,1)S(1)} %pad_maximum_fusion.2), channel_id=1, source_target_pairs={{0,2},{2,0},{1,3},{3,1},{4,6},{6,4},{5,7},{7,5},{8,10},{10,8},{9,1... | collective-permute-start | bytes 983048 | tf_op jit(solution)/shard_map/ppermute | solution.py:21
  35.4 5.8 %collective-permute-done.5 = bf16[640,256]{0,1:T(8,128)(2,1)S(1)} collective-permute-done((bf16[640,256]{0,1:T(8,128)(2,1)S(1)}, bf16[640,256]{0,1:T(8,128)(2,1)S(1)}, u32[]{:S(2)}, u32[]{:S(2)}) %collective-permute-start.5) | collective-permute-done | bytes 327712 | tf_op jit(solution)/shard_map/ppermute | solution.py:21
  42.9 4.9 %collective-permute-done.7 = bf16[640,128]{0,1:T(8,128)(2,1)S(1)} collective-permute-done((bf16[640,128]{0,1:T(8,128)(2,1)S(1)}, bf16[640,128]{0,1:T(8,128)(2,1)S(1)}, u32[]{:S(2)}, u32[]{:S(2)}) %collective-permute-start.7) | collective-permute-done | bytes 163872 | tf_op jit(solution)/shard_map/ppermute | solution.py:21
  48.5 3.2 %collective-permute-start.8 = (bf16[768,64]{0,1:T(8,128)(2,1)S(1)}, bf16[768,64]{0,1:T(8,128)(2,1)S(1)}, u32[]{:S(2)}, u32[]{:S(2)}) collective-permute-start(bf16[768,64]{0,1:T(8,128)(2,1)S(1)} %pad_maximum_fusion.8), channel_id=1, source_target_pairs={{0,8},{4,12},{8,0},{12,4},{1,9},{5,13},{9,1},{13,5},{2,10},{6,14},... | collective-permute-start | bytes 294920 | tf_op jit(solution)/shard_map/ppermute | solution.py:21
  51.7 3.4 %collective-permute-done.8 = bf16[768,64]{0,1:T(8,128)(2,1)S(1)} collective-permute-done((bf16[768,64]{0,1:T(8,128)(2,1)S(1)}, bf16[768,64]{0,1:T(8,128)(2,1)S(1)}, u32[]{:S(2)}, u32[]{:S(2)}) %collective-permute-start.8) | collective-permute-done | bytes 98336 | tf_op jit(solution)/shard_map/ppermute | solution.py:21
  55.7 3.9 %collective-permute-done.9 = bf16[1,128,128]{1,2,0:T(8,128)(2,1)S(1)} collective-permute-done((bf16[1,128,128]{1,2,0:T(8,128)(2,1)S(1)}, bf16[1,128,128]{1,2,0:T(8,128)(2,1)S(1)}, u32[]{:S(2)}, u32[]{:S(2)}) %collective-permute-start.9) | collective-permute-done | bytes 32800 | tf_op jit(solution)/shard_map/ppermute | solution.py:21
  59.9 1.4 %collective-permute-start.10 = (bf16[2,128,256]{1,2,0:T(8,128)(2,1)S(1)}, bf16[2,128,256]{1,2,0:T(8,128)(2,1)S(1)}, u32[]{:S(2)}, u32[]{:S(2)}) collective-permute-start(bf16[2,128,256]{1,2,0:T(8,128)(2,1)S(1)} %pad_maximum_fusion.7), channel_id=1, source_target_pairs={{0,2},{2,0},{1,3},{3,1},{4,6},{6,4},{5,7},{7,5},{8,10},{10,8},{9,1... | collective-permute-start | bytes 393224 | tf_op jit(solution)/shard_map/ppermute | solution.py:21
  61.5 3.5 %collective-permute-done.10 = bf16[2,128,256]{1,2,0:T(8,128)(2,1)S(1)} collective-permute-done((bf16[2,128,256]{1,2,0:T(8,128)(2,1)S(1)}, bf16[2,128,256]{1,2,0:T(8,128)(2,1)S(1)}, u32[]{:S(2)}, u32[]{:S(2)}) %collective-permute-start.10) | collective-permute-done | bytes 131104 | tf_op jit(solution)/shard_map/ppermute | solution.py:21
  65.7 1.7 %collective-permute-done.11 = bf16[3,128,512]{1,2,0:T(8,128)(2,1)S(1)} collective-permute-done((bf16[3,128,512]{1,2,0:T(8,128)(2,1)S(1)}, bf16[3,128,512]{1,2,0:T(8,128)(2,1)S(1)}, u32[]{:S(2)}, u32[]{:S(2)}) %collective-permute-start.11) | collective-permute-done | bytes 393248 | tf_op jit(solution)/shard_map/ppermute | solution.py:21
  67.4 1.2 %fusion.6 = bf16[3,128,1024]{1,2,0:T(8,128)(2,1)S(1)} fusion(s32[]{:T(128)S(6)} %select_n.100, bf16[1,128,512]{1,2,0:T(8,128)(2,1)S(1)} %copy.32, bf16[2,128,512]{1,2,0:T(8,128)(2,1)S(1)} %fusion.23, bf16[3,128,512]{1,2,0:T(8,128)(2,1)S(1)} %collective-permute-done.11), kind=kLoop, calls=%fused_computation.22 | loop fusion | flops 3932160 | bytes 1572868 | tf_op jit(solution)/shard_map/concatenate | solution.py:44
  70.7 1.5 %fusion = bf16[512,1024]{1,0:T(8,128)(2,1)} fusion(f32[1024,512]{0,1:T(8,128)S(1)} %fusion.25, f32[1024,512]{0,1:T(8,128)S(1)} %fusion.26, f32[1024,512]{0,1:T(8,128)S(1)} %fusion.27, f32[512,1024]{1,0:T(8,128)S(1)} %copy-done.1, bf16[256,1024]{1,0:T(8,128)(2,1)S(1)} %copy-done.8, bf16[4,512,128]{2,1,0:T(8,128)(2,1)S(1)} %copy-done.4), kind=kOutput, calls=%fused_computation.1 | convolution fusion | flops 136839168 | bytes 9830400 | tf_op jit(solution)/shard_map/dot_general | solution.py:149
  (121 shorter events, 17.5 us)
Async XLA Ops:
  0.0 5.9 %copy-start = (bf16[512,1024]{1,0:T(8,128)(2,1)S(1)}, bf16[512,1024]{1,0:T(8,128)(2,1)}, u32[]{:S(2)}) copy-start(bf16[512,1024]{1,0:T(8,128)(2,1)} %param.5) | copy-start | bytes 3145732
  0.0 3.9 %copy-start.2 = (bf16[4,512,128]{2,1,0:T(8,128)(2,1)S(1)}, bf16[4,512,128]{2,1,0:T(8,128)(2,1)}, u32[]{:S(2)}) copy-start(bf16[4,512,128]{2,1,0:T(8,128)(2,1)} %param.7) | copy-start | bytes 1572868
  0.0 4.2 %slice-start = ((bf16[4,512,128]{2,1,0:T(8,128)(2,1)}), bf16[2,512,128]{2,1,0:T(8,128)(2,1)S(1)}, s32[]{:S(2)}) async-start(bf16[4,512,128]{2,1,0:T(8,128)(2,1)} %param.7), calls=%async_computation | async-start | bytes 524288 | tf_op jit(solution)/shard_map/slice | solution.py:57
  0.0 4.0 %copy-start.3 = (bf16[4,512,128]{2,1,0:T(8,128)(2,1)S(1)}, bf16[4,512,128]{2,1,0:T(8,128)(2,1)}, u32[]{:S(2)}) copy-start(bf16[4,512,128]{2,1,0:T(8,128)(2,1)} %param.8) | copy-start | bytes 1572868
  3.5 16.4 %collective-permute-start = (bf16[128,256]{1,0:T(8,128)(2,1)}, bf16[128,256]{1,0:T(8,128)(2,1)}, u32[]{:S(2)}, u32[]{:S(2)}) collective-permute-start(bf16[128,256]{1,0:T(8,128)(2,1)} %get-tuple-element.20), channel_id=1, source_target_pairs={{0,1},{1,0},{2,3},{3,2},{4,5},{5,4},{6,7},{7,6},{8,9},{9,8},{10,11... | collective-permute-start | bytes 196616 | tf_op jit(solution)/shard_map/ppermute | solution.py:21
  5.8 8.6 %collective-permute-start.3 = (f32[768,128]{1,0:T(8,128)}, f32[768,128]{1,0:T(8,128)}, u32[]{:S(2)}, u32[]{:S(2)}) collective-permute-start(f32[768,128]{1,0:T(8,128)} %pad_maximum_fusion), channel_id=1, source_target_pairs={{0,1},{1,0},{2,3},{3,2},{4,5},{5,4},{6,7},{7,6},{8,9},{9,8},{10,11... | collective-permute-start | bytes 1179656 | tf_op jit(solution)/shard_map/ppermute | solution.py:21
  9.3 10.6 %collective-permute-start.1 = (bf16[128,1024]{1,0:T(8,128)(2,1)S(1)}, bf16[128,1024]{1,0:T(8,128)(2,1)}, u32[]{:S(2)}, u32[]{:S(2)}) collective-permute-start(bf16[128,1024]{1,0:T(8,128)(2,1)S(1)} %fusion.3), channel_id=1, source_target_pairs={{0,1},{1,0},{2,3},{3,2},{4,5},{5,4},{6,7},{7,6},{8,9},{9,8},{10,11... | collective-permute-start | bytes 786440 | tf_op jit(solution)/shard_map/ppermute | solution.py:21
  11.3 19.0 %collective-permute-start.2 = (f32[3,128,512]{1,2,0:T(8,128)}, f32[3,128,512]{1,2,0:T(8,128)}, u32[]{:S(2)}, u32[]{:S(2)}) collective-permute-start(f32[3,128,512]{1,2,0:T(8,128)} %convolution_bitcast_fusion), channel_id=1, source_target_pairs={{0,1},{1,0},{2,3},{3,2},{4,5},{5,4},{6,7},{7,6},{8,9},{9,8},{10,11... | collective-permute-start | bytes 2359304 | tf_op jit(solution)/shard_map/ppermute | solution.py:21
  16.2 3.7 %copy-start.6 = (f32[128,128]{1,0:T(8,128)}, f32[128,128]{1,0:T(8,128)S(1)}, u32[]{:S(2)}) copy-start(f32[128,128]{1,0:T(8,128)S(1)} %slice_add_fusion.2) | copy-start | bytes 196612
  16.9 8.4 %collective-permute-start.4 = (f32[384,128]{1,0:T(8,128)}, f32[384,128]{1,0:T(8,128)}, u32[]{:S(2)}, u32[]{:S(2)}) collective-permute-start(f32[384,128]{1,0:T(8,128)} %pad_maximum_fusion.4), channel_id=1, source_target_pairs={{0,2},{2,0},{1,3},{3,1},{4,6},{6,4},{5,7},{7,5},{8,10},{10,8},{9,1... | collective-permute-start | bytes 589832 | tf_op jit(solution)/shard_map/ppermute | solution.py:21
  21.2 2.5 %copy-start.7 = (bf16[256,1024]{1,0:T(8,128)(2,1)}, bf16[256,1024]{1,0:T(8,128)(2,1)S(1)}, u32[]{:S(2)}) copy-start(bf16[256,1024]{1,0:T(8,128)(2,1)S(1)} %convolution_convert_fusion) | copy-start | bytes 1572868
  26.8 7.7 %collective-permute-start.6 = (f32[128,128]{1,0:T(8,128)}, f32[128,128]{1,0:T(8,128)}, u32[]{:S(2)}, u32[]{:S(2)}) collective-permute-start(f32[128,128]{1,0:T(8,128)} %slice_add_fusion.1), channel_id=1, source_target_pairs={{0,4},{4,0},{8,12},{12,8},{1,5},{5,1},{9,13},{13,9},{2,6},{6,2},{1... | collective-permute-start | bytes 196616 | tf_op jit(solution)/shard_map/ppermute | solution.py:21
  32.0 2.3 %copy-start.13 = (bf16[128,256]{1,0:T(8,128)(2,1)S(1)}, bf16[128,256]{1,0:T(8,128)(2,1)}, u32[]{:S(2)}) copy-start(bf16[128,256]{1,0:T(8,128)(2,1)} %get-tuple-element.37) | copy-start | bytes 196612
  32.2 9.3 %copy-start.14 = (bf16[128,256]{0,1:T(8,128)(2,1)S(1)}, bf16[128,256]{0,1:T(8,128)(2,1)}, u32[]{:S(2)}) copy-start(bf16[128,256]{0,1:T(8,128)(2,1)} %get-tuple-element.30) | copy-start | bytes 196612
  32.4 9.4 %copy-start.5 = (f32[256,256]{1,0:T(8,128)S(1)}, f32[256,256]{1,0:T(8,128)}, u32[]{:S(2)}) copy-start(f32[256,256]{1,0:T(8,128)} %pad_maximum_fusion.3) | copy-start | bytes 786436
  32.4 8.8 %collective-permute-start.5 = (bf16[640,256]{0,1:T(8,128)(2,1)S(1)}, bf16[640,256]{0,1:T(8,128)(2,1)S(1)}, u32[]{:S(2)}, u32[]{:S(2)}) collective-permute-start(bf16[640,256]{0,1:T(8,128)(2,1)S(1)} %pad_maximum_fusion.2), channel_id=1, source_target_pairs={{0,2},{2,0},{1,3},{3,1},{4,6},{6,4},{5,7},{7,5},{8,10},{10,8},{9,1... | collective-permute-start | bytes 983048 | tf_op jit(solution)/shard_map/ppermute | solution.py:21
  41.8 6.2 %copy-start.16 = (bf16[128,256]{1,0:T(8,128)(2,1)S(1)}, bf16[128,256]{1,0:T(8,128)(2,1)}, u32[]{:S(2)}) copy-start(bf16[128,256]{1,0:T(8,128)(2,1)} %get-tuple-element.19) | copy-start | bytes 196612
  42.2 13.1 %copy-start.15 = (bf16[128,256]{1,0:T(8,128)(2,1)S(1)}, bf16[128,256]{1,0:T(8,128)(2,1)}, u32[]{:S(2)}) copy-start(bf16[128,256]{1,0:T(8,128)(2,1)} %get-tuple-element.18) | copy-start | bytes 196612
  42.4 5.4 %collective-permute-start.7 = (bf16[640,128]{0,1:T(8,128)(2,1)S(1)}, bf16[640,128]{0,1:T(8,128)(2,1)S(1)}, u32[]{:S(2)}, u32[]{:S(2)}) collective-permute-start(bf16[640,128]{0,1:T(8,128)(2,1)S(1)} %pad_maximum_fusion.5), channel_id=1, source_target_pairs={{0,4},{4,0},{8,12},{12,8},{1,5},{5,1},{9,13},{13,9},{2,6},{6,2},{1... | collective-permute-start | bytes 491528 | tf_op jit(solution)/shard_map/ppermute | solution.py:21
  48.5 6.6 %collective-permute-start.8 = (bf16[768,64]{0,1:T(8,128)(2,1)S(1)}, bf16[768,64]{0,1:T(8,128)(2,1)S(1)}, u32[]{:S(2)}, u32[]{:S(2)}) collective-permute-start(bf16[768,64]{0,1:T(8,128)(2,1)S(1)} %pad_maximum_fusion.8), channel_id=1, source_target_pairs={{0,8},{4,12},{8,0},{12,4},{1,9},{5,13},{9,1},{13,5},{2,10},{6,14},... | collective-permute-start | bytes 294920 | tf_op jit(solution)/shard_map/ppermute | solution.py:21
  55.6 13.0 %copy-start.4 = (bf16[4,512,128]{2,1,0:T(8,128)(2,1)S(1)}, bf16[4,512,128]{2,1,0:T(8,128)(2,1)}, u32[]{:S(2)}) copy-start(bf16[4,512,128]{2,1,0:T(8,128)(2,1)} %param.8) | copy-start | bytes 1572868
  55.6 4.0 %collective-permute-start.9 = (bf16[1,128,128]{1,2,0:T(8,128)(2,1)S(1)}, bf16[1,128,128]{1,2,0:T(8,128)(2,1)S(1)}, u32[]{:S(2)}, u32[]{:S(2)}) collective-permute-start(bf16[1,128,128]{1,2,0:T(8,128)(2,1)S(1)} %fusion.94), channel_id=1, source_target_pairs={{0,4},{4,0},{8,12},{12,8},{1,5},{5,1},{9,13},{13,9},{2,6},{6,2},{1... | collective-permute-start | bytes 98312 | tf_op jit(solution)/shard_map/ppermute | solution.py:21
  59.9 5.0 %collective-permute-start.10 = (bf16[2,128,256]{1,2,0:T(8,128)(2,1)S(1)}, bf16[2,128,256]{1,2,0:T(8,128)(2,1)S(1)}, u32[]{:S(2)}, u32[]{:S(2)}) collective-permute-start(bf16[2,128,256]{1,2,0:T(8,128)(2,1)S(1)} %pad_maximum_fusion.7), channel_id=1, source_target_pairs={{0,2},{2,0},{1,3},{3,1},{4,6},{6,4},{5,7},{7,5},{8,10},{10,8},{9,1... | collective-permute-start | bytes 393224 | tf_op jit(solution)/shard_map/ppermute | solution.py:21
  65.6 1.8 %collective-permute-start.11 = (bf16[3,128,512]{1,2,0:T(8,128)(2,1)S(1)}, bf16[3,128,512]{1,2,0:T(8,128)(2,1)S(1)}, u32[]{:S(2)}, u32[]{:S(2)}) collective-permute-start(bf16[3,128,512]{1,2,0:T(8,128)(2,1)S(1)} %pad_maximum_fusion.1), channel_id=1, source_target_pairs={{0,1},{1,0},{2,3},{3,2},{4,5},{5,4},{6,7},{7,6},{8,9},{9,8},{10,11... | collective-permute-start | bytes 1179656 | tf_op jit(solution)/shard_map/ppermute | solution.py:21
  (6 other events, 11.4 us)

commit v7 on v6

v7 whole, which is shorter than its diff:
```python
import jax
import jax.numpy as jnp
from jax import lax
from jax.sharding import PartitionSpec as P

F32 = jnp.float32
BF16 = jnp.bfloat16


def bit_axes():
    bits = []
    for axis in ("inner", "narrow", "wide"):
        for stride in range(lax.axis_size(axis).bit_length() - 1):
            bits.append((axis, stride))
    return bits


def swap(x, bit, bits):
    axis, stride = bits[bit]
    n = lax.axis_size(axis)
    return lax.ppermute(x, axis, [(i, i ^ (1 << stride)) for i in range(n)])


def side(bit, bits):
    axis, stride = bits[bit]
    return (lax.axis_index(axis) >> stride) & 1


def cols(x, start, width):
    return lax.dynamic_slice_in_dim(x, start, width, axis=x.ndim - 1)


def gather_half(x, bit, bits):
    w = x.shape[-1]
    h = side(bit, bits)
    both = jnp.concatenate([x, swap(x, bit, bits), x], axis=-1)
    return cols(both, h * w, 2 * w)


def on_device(templates, leaf_inverse, v_basis, u_basis, coupling):
    bits = bit_axes()
    levels, pixels, rank = v_basis.shape
    width = templates.shape[1]
    c0 = jnp.dot(leaf_inverse, templates, preferred_element_type=F32)
    c0b = c0.astype(BF16)

    cross = jnp.einsum("kis,lir->klrs", u_basis, v_basis, preferred_element_type=F32)
    counts = [levels - 1 - k for k in range(levels - 1)]
    suffix = jnp.concatenate(
        [cross[k, k + 1 :].reshape(-1, rank) for k in range(levels - 1)], axis=0
    )
    w_own, w_sib = [None] * levels, [None] * levels
    for b in range(levels - 1):
        n = counts[b] * rank
        got = swap(suffix, b, bits)
        w_own[b] = suffix[:n].reshape(counts[b], rank, rank)
        w_sib[b] = got[:n].reshape(counts[b], rank, rank)
        suffix = suffix[n:] + got[n:]
    couple_sib = [swap(coupling[s, 0], s, bits) for s in range(levels)]

    proj0 = jnp.dot(v_basis[0].T, c0b, preferred_element_type=F32)
    rest = None
    if levels > 1:
        half = width // 2
        h = side(0, bits)
        keep = jnp.einsum(
            "lir,it->lrt", v_basis[1:], cols(c0b, h * half, half),
            preferred_element_type=F32,
        )
        send = jnp.einsum(
            "lir,it->lrt", v_basis[1:], cols(c0b, (1 - h) * half, half),
            preferred_element_type=F32,
        )
        rest = keep + swap(send, 0, bits)
    own_coefs = []
    for s in range(levels):
        if s == 0:
            mine_b = proj0.astype(BF16)
            theirs_b = swap(mine_b, s, bits)
        else:
            mine_b = rest[0].astype(BF16)
            rest = rest[1:]
            n = rest.shape[0]
            w = mine_b.shape[1] // 2
            parts = [mine_b[:, :w], mine_b[:, w:]]
            if n > 0:
                h = side(s, bits)
                keep = cols(rest, h * w, w)
                send = cols(rest, (1 - h) * w, w)
                parts.append(send.astype(BF16).reshape(n * rank, w))
            payload = jnp.concatenate(parts, axis=0)
            if s < levels - 1:
                payload, w_sib[s] = lax.optimization_barrier((payload, w_sib[s]))
            got = swap(payload, s, bits)
            theirs_b = jnp.concatenate([got[:rank], got[rank : 2 * rank]], axis=1)
            if n > 0:
                recv = got[2 * rank :].reshape(n, rank, w).astype(F32)
                rest = keep + recv
        lower = side(s, bits) == 0
        stacked = jnp.where(
            lower,
            jnp.concatenate([mine_b, theirs_b], axis=0),
            jnp.concatenate([theirs_b, mine_b], axis=0),
        )
        couple = jnp.concatenate([coupling[s, 0], couple_sib[s]], axis=0)
        coefs = jnp.dot(couple, stacked, preferred_element_type=F32).astype(BF16)
        own_coefs.append(coefs[:rank])
        if s < levels - 1:
            w = coefs.shape[1] // 2
            piece = cols(coefs, side(s, bits) * w, w).astype(F32)
            fix = jnp.einsum(
                "nrs,st->nrt", w_own[s], piece[:rank],
                preferred_element_type=F32, precision=lax.Precision.HIGHEST,
            ) + jnp.einsum(
                "nrs,st->nrt", w_sib[s], piece[rank:],
                preferred_element_type=F32, precision=lax.Precision.HIGHEST,
            )
            rest = rest - fix

    pending = {s: own_coefs[s] for s in range(1, levels)}
    for j in reversed(range(levels - 1)):
        group = [s for s in range(j + 1, levels)]
        joined = gather_half(jnp.stack([pending[s] for s in group]), j, bits)
        for i, s in enumerate(group):
            pending[s] = joined[i]
    full = [own_coefs[0]] + [pending[s] for s in range(1, levels)]
    current = c0
    for s in range(levels):
        current = current - jnp.dot(u_basis[s], full[s], preferred_element_type=F32)
    return current.astype(BF16)


def solution(mesh):
    placed = (
        P(("slab", "wide", "narrow", "inner"), None),
        P(("slab", "wide", "narrow", "inner"), None),
        P(None, ("slab", "wide", "narrow", "inner"), None),
        P(None, ("slab", "wide", "narrow", "inner"), None),
        P(None, ("slab", "wide", "narrow", "inner"), None, None),
    )
    return jax.shard_map(
        on_device,
        mesh=mesh,
        in_specs=placed,
        out_specs=P(("slab", "wide", "narrow", "inner"), None),
        check_vma=False,
    )
```

time: 72.9 us -> 72.2 us (level)
  other arithmetic: 11 us -> 4.07 us
  matrix products: 13.9 us -> 18.8 us
  local copies, waits for them, and re-layouts: 10.6 us -> 6.54 us
  waiting for transfers between devices: 23.3 us -> 26.9 us
  starting transfers between devices: 12.7 us -> 15.1 us
    ppermute x12 -> x15, waiting for transfers between devices: 23.3 us -> 26.9 us  [swap(): return lax.ppermute(x, axis, [(i, i ^ 1 << stride) for i in range(n)])]
    slice x13 -> x5, local copies, waits for them, and re-layouts: 4.09 us -> 0.69 us  [the longest x1 0.66 us: on_device(): w_own[b] = suffix[:n].reshape(counts[b], rank, rank)]
    dot_general x4, matrix products: 2.01 us -> 5.05 us  [on_device(): coefs = jnp.dot(couple, stacked, preferred_element_type=F32).astype(BF16)]
    select_n x4 -> x0, other arithmetic: 2.37 us -> none  [the longest x2 2.35 us: on_device(): couple_own.append(jnp.where(lower, c, rolled))]
    ppermute x12 -> x15, starting transfers between devices: 12.7 us -> 15.1 us  [swap(): return lax.ppermute(x, axis, [(i, i ^ 1 << stride) for i in range(n)])]
    concatenate x4 -> x1, other arithmetic: 3.09 us -> 0.8 us  [on_device(): jnp.concatenate([cross[k, k + 1:].reshape(-1, rank) for k in range(levels...]
    add x3 -> x2, other arithmetic: 3.28 us -> 1.07 us  [on_device(): suffix = suffix[n:] + got[n:]]
    concatenate x4 -> x0, local copies, waits for them, and re-layouts: 1.82 us -> none  [on_device(): rolled = jnp.concatenate([c[:, rank:], c[:, :rank]], axis=1)]
  transfers between devices with their start and end apart: 12 -> 15, of which waited for: 7 -> 9; matrix products, arithmetic and copies ran while one was open for 33% -> 22% of each run, Pallas kernels for 0% -> 0%
where the time goes in v7:
time: 72.2 us; the launch traced here: 71.8 us
  waiting for transfers between devices  26.9 us (37%)
  matrix products  18.8 us (26%)
  starting transfers between devices  15.1 us (21%)
  local copies, waits for them, and re-layouts  6.54 us (9%)
  other arithmetic  4.07 us (6%)
    ppermute x15, waiting for transfers between devices, swap(): return lax.ppermute(x, axis, [(i, i ^ 1 << stride) for i in range(n)])  26.9 us
    ppermute x15, starting transfers between devices, swap(): return lax.ppermute(x, axis, [(i, i ^ 1 << stride) for i in range(n)])  15.1 us
    dot_general x4, matrix products, on_device(): coefs = jnp.dot(couple, stacked, preferred_element_type=F32).astype(BF16)  5.05 us
    dot_general x1, matrix products, on_device(): c0 = jnp.dot(leaf_inverse, templates, preferred_element_type=F32)  3.11 us
    dot_general x4, matrix products, on_device(): current = current - jnp.dot(u_basis[s], full[s], preferred_element_type=F32)  2.85 us
    unnamed x24, local copies, waits for them, and re-layouts  2.72 us
    dot_general x3, matrix products, on_device(): jnp.einsum('nrs,st->nrt', w_own[s], piece[:rank], preferred_element_type=...  2.2 us
    concatenate x3, other arithmetic, gather_half(): both = jnp.concatenate([x, swap(x, bit, bits), x], axis=-1)  2.09 us
  transfers between devices with their start and end apart: 15, of which 9 were waited for; matrix products, arithmetic and copies ran while one was open for 22% of the time, Pallas kernels for 0%

profile of v7, /device:TPU:0, one launch (start us, length us, event | category | flops | bytes accessed | tf_op | source)
XLA Modules:
  0.0 71.8 jit_solution(11480323635829032446)
XLA Ops:
  0.0 1.7 %slice_bitcast_fusion.9 = (bf16[128,256]{1,0:T(8,128)(2,1)}, bf16[128,256]{1,0:T(8,128)(2,1)}, bf16[128,256]{1,0:T(8,128)(2,1)S(1)}, bf16[128,256]{1,0:T(8,128)(2,1)}) fusion(bf16[4,1,128,256]{3,2,1,0:T(8,128)(2,1)} %param.9), kind=kLoop, calls=%fused_computation.149 | loop fusion | bytes 524288 | tf_op jit(solution)/shard_map/squeeze | solution.py:105
  2.2 3.1 %fusion.118 = (bf16[512,1024]{1,0:T(8,128)(2,1)S(1)}, f32[512,1024]{1,0:T(8,128)}) fusion(bf16[512,512]{1,0:T(8,128)(2,1)} %param.6, bf16[512,1024]{1,0:T(8,128)(2,1)S(1)} %copy-done), kind=kOutput, calls=%fused_computation.178 | convolution fusion | flops 537395200 | bytes 4718592 | tf_op jit(solution)/shard_map/dot_general | solution.py:44
  9.1 1.4 %convolution_bitcast_fusion.1 = f32[3,128,512]{1,2,0:T(8,128)} fusion(bf16[512,1024]{1,0:T(8,128)(2,1)S(1)} %get-tuple-element.31, s32[]{:T(128)S(6)} %select_n.66, bf16[4,512,128]{2,1,0:T(8,128)(2,1)S(1)} %copy-done.2), kind=kOutput, calls=%fused_computation.6 | convolution fusion | flops 201326592 | bytes 1703940 | tf_op jit(solution)/shard_map/lir,it->lrt/dot_general | solution.py:70
  10.6 1.5 %convolution_convert_fusion = bf16[256,1024]{1,0:T(8,128)(2,1)S(1)} fusion(bf16[128,1024]{1,0:T(8,128)(2,1)} %collective-permute-done.1, bf16[128,1024]{1,0:T(8,128)(2,1)} %fusion.3, pred[]{:T(512)S(6)} %eq.12, bf16[128,256]{1,0:T(8,128)(2,1)S(1)} %collective-permute-done, bf16[128,256]{1,0:T(8,128)(2,1)S(1)} %get-tuple-element.17), kind=kOutput, calls=%fused_computation.8 | convolution fusion | flops 137101312 | bytes 1179649 | tf_op jit(solution)/shard_map/dot_general | solution.py:106
  12.1 1.6 %fusion.41 = f32[3,128,512]{1,2,0:T(8,128)S(1)} fusion(bf16[256,1024]{1,0:T(8,128)(2,1)S(1)} %convolution_convert_fusion, s32[]{:T(128)S(6)} %select_n.65, f32[4,4,128,128]{3,2,0,1:T(8,128)} %copy-done.3), kind=kOutput, calls=%fused_computation.77 | convolution fusion | flops 301989888 | bytes 1114116 | tf_op jit(solution)/shard_map/nrs,st->nrt/dot_general | solution.py:111
  14.9 2.9 %collective-permute-start.5 = (f32[384,128]{1,0:T(8,128)S(1)}, f32[384,128]{1,0:T(8,128)S(1)}, u32[]{:S(2)}, u32[]{:S(2)}) collective-permute-start(f32[384,128]{1,0:T(8,128)S(1)} %get-tuple-element.13), channel_id=1, source_target_pairs={{0,2},{2,0},{1,3},{3,1},{4,6},{6,4},{5,7},{7,5},{8,10},{10,8},{9,1... | collective-permute-start | bytes 589832 | tf_op jit(solution)/shard_map/ppermute | solution.py:21
  18.3 4.6 %collective-permute-done.5 = f32[384,128]{1,0:T(8,128)S(1)} collective-permute-done((f32[384,128]{1,0:T(8,128)S(1)}, f32[384,128]{1,0:T(8,128)S(1)}, u32[]{:S(2)}, u32[]{:S(2)}) %collective-permute-start.5) | collective-permute-done | bytes 196640 | tf_op jit(solution)/shard_map/ppermute | solution.py:21
  23.7 1.6 %fusion.2 = f32[3,128,512]{1,2,0:T(8,128)S(1)} fusion(f32[3,128,512]{1,2,0:T(8,128)S(1)} %convolution_add_fusion, f32[3,128,512]{1,2,0:T(8,128)} %collective-permute-done.3, bf16[512,1024]{1,0:T(8,128)(2,1)S(1)} %get-tuple-element.31, s32[]{:T(128)S(6)} %select_n.65, bf16[4,512,128]{2,1,0:T(8,128)(2,1)S(1)} %copy-done.2), kind=kOutput, calls=%fused_computation.10 | convolution fusion | flops 201719808 | bytes 3276804 | tf_op jit(solution)/shard_map/lir,it->lrt/dot_general | solution.py:66
  26.0 1.8 %collective-permute-start.6 = (bf16[512,256]{0,1:T(8,128)(2,1)S(1)}, bf16[512,256]{0,1:T(8,128)(2,1)S(1)}, u32[]{:S(2)}, u32[]{:S(2)}) collective-permute-start(bf16[512,256]{0,1:T(8,128)(2,1)S(1)} %pad_maximum_fusion.2), channel_id=1, source_target_pairs={{0,2},{2,0},{1,3},{3,1},{4,6},{6,4},{5,7},{7,5},{8,10},{10,8},{9,1... | collective-permute-start | bytes 786440 | tf_op jit(solution)/shard_map/ppermute | solution.py:21
  28.8 1.9 %collective-permute-start.8 = (f32[128,128]{1,0:T(8,128)S(1)}, f32[128,128]{1,0:T(8,128)S(1)}, u32[]{:S(2)}, u32[]{:S(2)}) collective-permute-start(f32[128,128]{1,0:T(8,128)S(1)} %slice_add_fusion.1), channel_id=1, source_target_pairs={{0,4},{4,0},{8,12},{12,8},{1,5},{5,1},{9,13},{13,9},{2,6},{6,2},{1... | collective-permute-start | bytes 196616 | tf_op jit(solution)/shard_map/ppermute | solution.py:21
  30.7 3.9 %collective-permute-done.6 = bf16[512,256]{0,1:T(8,128)(2,1)S(1)} collective-permute-done((bf16[512,256]{0,1:T(8,128)(2,1)S(1)}, bf16[512,256]{0,1:T(8,128)(2,1)S(1)}, u32[]{:S(2)}, u32[]{:S(2)}) %collective-permute-start.6) | collective-permute-done | bytes 262176 | tf_op jit(solution)/shard_map/ppermute | solution.py:21
  35.6 1.4 %convolution_convert_fusion.1 = bf16[256,512]{1,0:T(8,128)(2,1)S(1)} fusion(bf16[128,256]{0,1:T(8,128)(2,1)} %get-tuple-element.20, bf16[128,256]{0,1:T(8,128)(2,1)} %get-tuple-element.19, bf16[128,512]{0,1:T(8,128)(2,1)} %copy-done.9, pred[]{:T(512)S(6)} %eq.13, bf16[128,256]{1,0:T(8,128)(2,1)} %collective-permute-done.2, ...), kind=kOutput, calls=%fused_computation.12 | convolution fusion | flops 69206016 | bytes 655361 | tf_op jit(solution)/shard_map/dot_general | solution.py:106
  37.8 1.6 %collective-permute-start.9 = (bf16[384,128]{0,1:T(8,128)(2,1)S(1)}, bf16[384,128]{0,1:T(8,128)(2,1)S(1)}, u32[]{:S(2)}, u32[]{:S(2)}) collective-permute-start(bf16[384,128]{0,1:T(8,128)(2,1)S(1)} %pad_maximum_fusion.4), channel_id=1, source_target_pairs={{0,4},{4,0},{8,12},{12,8},{1,5},{5,1},{9,13},{13,9},{2,6},{6,2},{1... | collective-permute-start | bytes 294920 | tf_op jit(solution)/shard_map/ppermute | solution.py:21
  39.9 2.6 %collective-permute-done.9 = bf16[384,128]{0,1:T(8,128)(2,1)S(1)} collective-permute-done((bf16[384,128]{0,1:T(8,128)(2,1)S(1)}, bf16[384,128]{0,1:T(8,128)(2,1)S(1)}, u32[]{:S(2)}, u32[]{:S(2)}) %collective-permute-start.9) | collective-permute-done | bytes 98336 | tf_op jit(solution)/shard_map/ppermute | solution.py:21
  42.5 1.4 %collective-permute-done.7 = bf16[128,256]{1,0:T(8,128)(2,1)S(1)} collective-permute-done((bf16[128,256]{1,0:T(8,128)(2,1)}, bf16[128,256]{1,0:T(8,128)(2,1)S(1)}, u32[]{:S(2)}, u32[]{:S(2)}) %collective-permute-start.7) | collective-permute-done | bytes 65568 | tf_op jit(solution)/shard_map/ppermute | solution.py:21
  45.4 2.6 %collective-permute-start.11 = (bf16[256,64]{0,1:T(8,128)(2,1)S(1)}, bf16[256,64]{0,1:T(8,128)(2,1)S(1)}, u32[]{:S(2)}, u32[]{:S(2)}) collective-permute-start(bf16[256,64]{0,1:T(8,128)(2,1)S(1)} %pad_maximum_fusion.5), channel_id=1, source_target_pairs={{0,8},{4,12},{8,0},{12,4},{1,9},{5,13},{9,1},{13,5},{2,10},{6,14},... | collective-permute-start | bytes 98312 | tf_op jit(solution)/shard_map/ppermute | solution.py:21
  48.4 1.9 %collective-permute-done.11 = bf16[256,64]{0,1:T(8,128)(2,1)S(1)} collective-permute-done((bf16[256,64]{0,1:T(8,128)(2,1)S(1)}, bf16[256,64]{0,1:T(8,128)(2,1)S(1)}, u32[]{:S(2)}, u32[]{:S(2)}) %collective-permute-start.11) | collective-permute-done | bytes 32800 | tf_op jit(solution)/shard_map/ppermute | solution.py:21
  50.3 3.8 %collective-permute-done.10 = bf16[128,256]{1,0:T(8,128)(2,1)S(1)} collective-permute-done((bf16[128,256]{1,0:T(8,128)(2,1)}, bf16[128,256]{1,0:T(8,128)(2,1)S(1)}, u32[]{:S(2)}, u32[]{:S(2)}) %collective-permute-start.10) | collective-permute-done | bytes 65568 | tf_op jit(solution)/shard_map/ppermute | solution.py:21
  55.5 3.6 %collective-permute-done.12 = bf16[1,128,128]{1,2,0:T(8,128)(2,1)S(1)} collective-permute-done((bf16[1,128,128]{1,2,0:T(8,128)(2,1)S(1)}, bf16[1,128,128]{1,2,0:T(8,128)(2,1)S(1)}, u32[]{:S(2)}, u32[]{:S(2)}) %collective-permute-start.12) | collective-permute-done | bytes 32800 | tf_op jit(solution)/shard_map/ppermute | solution.py:21
  59.5 1.6 %collective-permute-start.13 = (bf16[2,128,256]{1,2,0:T(8,128)(2,1)S(1)}, bf16[2,128,256]{1,2,0:T(8,128)(2,1)S(1)}, u32[]{:S(2)}, u32[]{:S(2)}) collective-permute-start(bf16[2,128,256]{1,2,0:T(8,128)(2,1)S(1)} %pad_maximum_fusion.3), channel_id=1, source_target_pairs={{0,2},{2,0},{1,3},{3,1},{4,6},{6,4},{5,7},{7,5},{8,10},{10,8},{9,1... | collective-permute-start | bytes 393224 | tf_op jit(solution)/shard_map/ppermute | solution.py:21
  61.2 3.3 %collective-permute-done.13 = bf16[2,128,256]{1,2,0:T(8,128)(2,1)S(1)} collective-permute-done((bf16[2,128,256]{1,2,0:T(8,128)(2,1)S(1)}, bf16[2,128,256]{1,2,0:T(8,128)(2,1)S(1)}, u32[]{:S(2)}, u32[]{:S(2)}) %collective-permute-start.13) | collective-permute-done | bytes 131104 | tf_op jit(solution)/shard_map/ppermute | solution.py:21
  65.2 1.7 %collective-permute-done.14 = bf16[3,128,512]{1,2,0:T(8,128)(2,1)S(1)} collective-permute-done((bf16[3,128,512]{1,2,0:T(8,128)(2,1)S(1)}, bf16[3,128,512]{1,2,0:T(8,128)(2,1)S(1)}, u32[]{:S(2)}, u32[]{:S(2)}) %collective-permute-start.14) | collective-permute-done | bytes 393248 | tf_op jit(solution)/shard_map/ppermute | solution.py:21
  66.9 1.2 %fusion.7 = bf16[3,128,1024]{1,2,0:T(8,128)(2,1)S(1)} fusion(s32[]{:T(128)S(6)} %select_n.78, bf16[1,128,512]{1,2,0:T(8,128)(2,1)S(1)} %copy.30, bf16[2,128,512]{1,2,0:T(8,128)(2,1)S(1)} %fusion.25, bf16[3,128,512]{1,2,0:T(8,128)(2,1)S(1)} %collective-permute-done.14), kind=kLoop, calls=%fused_computation.26 | loop fusion | flops 3932160 | bytes 1572868 | tf_op jit(solution)/shard_map/concatenate | solution.py:36
  70.3 1.5 %fusion = bf16[512,1024]{1,0:T(8,128)(2,1)} fusion(f32[1024,512]{0,1:T(8,128)S(1)} %fusion.27, f32[1024,512]{0,1:T(8,128)S(1)} %fusion.28, f32[1024,512]{0,1:T(8,128)S(1)} %fusion.29, f32[512,1024]{1,0:T(8,128)S(1)} %copy-done.1, bf16[256,1024]{1,0:T(8,128)(2,1)S(1)} %copy-done.8, bf16[4,512,128]{2,1,0:T(8,128)(2,1)S(1)} %copy-done.4), kind=kOutput, calls=%fused_computation.1 | convolution fusion | flops 136839168 | bytes 9830400 | tf_op jit(solution)/shard_map/dot_general | solution.py:129
  (88 shorter events, 16.9 us)
Async XLA Ops:
  0.0 2.2 %copy-start = (bf16[512,1024]{1,0:T(8,128)(2,1)S(1)}, bf16[512,1024]{1,0:T(8,128)(2,1)}, u32[]{:S(2)}) copy-start(bf16[512,1024]{1,0:T(8,128)(2,1)} %param.5) | copy-start | bytes 3145732
  1.7 3.6 %copy-start.2 = (bf16[4,512,128]{2,1,0:T(8,128)(2,1)S(1)}, bf16[4,512,128]{2,1,0:T(8,128)(2,1)}, u32[]{:S(2)}) copy-start(bf16[4,512,128]{2,1,0:T(8,128)(2,1)} %param.7) | copy-start | bytes 1572868
  1.7 4.8 %copy-start.4 = (bf16[4,512,128]{2,1,0:T(8,128)(2,1)S(1)}, bf16[4,512,128]{2,1,0:T(8,128)(2,1)}, u32[]{:S(2)}) copy-start(bf16[4,512,128]{2,1,0:T(8,128)(2,1)} %param.8) | copy-start | bytes 1572868
  1.7 8.9 %collective-permute-start = (bf16[128,256]{1,0:T(8,128)(2,1)S(1)}, bf16[128,256]{1,0:T(8,128)(2,1)S(1)}, u32[]{:S(2)}, u32[]{:S(2)}) collective-permute-start(bf16[128,256]{1,0:T(8,128)(2,1)S(1)} %get-tuple-element.17), channel_id=1, source_target_pairs={{0,1},{1,0},{2,3},{3,2},{4,5},{5,4},{6,7},{7,6},{8,9},{9,8},{10,11... | collective-permute-start | bytes 196616 | tf_op jit(solution)/shard_map/ppermute | solution.py:21
  6.3 4.3 %collective-permute-start.1 = (bf16[128,1024]{1,0:T(8,128)(2,1)}, bf16[128,1024]{1,0:T(8,128)(2,1)}, u32[]{:S(2)}, u32[]{:S(2)}) collective-permute-start(bf16[128,1024]{1,0:T(8,128)(2,1)} %fusion.3), channel_id=1, source_target_pairs={{0,1},{1,0},{2,3},{3,2},{4,5},{5,4},{6,7},{7,6},{8,9},{9,8},{10,11... | collective-permute-start | bytes 786440 | tf_op jit(solution)/shard_map/ppermute | solution.py:21
  8.7 5.1 %collective-permute-start.4 = (f32[768,128]{1,0:T(8,128)}, f32[768,128]{1,0:T(8,128)}, u32[]{:S(2)}, u32[]{:S(2)}) collective-permute-start(f32[768,128]{1,0:T(8,128)} %pad_maximum_fusion), channel_id=1, source_target_pairs={{0,1},{1,0},{2,3},{3,2},{4,5},{5,4},{6,7},{7,6},{8,9},{9,8},{10,11... | collective-permute-start | bytes 1179656 | tf_op jit(solution)/shard_map/ppermute | solution.py:21
  10.5 13.2 %collective-permute-start.3 = (f32[3,128,512]{1,2,0:T(8,128)}, f32[3,128,512]{1,2,0:T(8,128)}, u32[]{:S(2)}, u32[]{:S(2)}) collective-permute-start(f32[3,128,512]{1,2,0:T(8,128)} %convolution_bitcast_fusion.1), channel_id=1, source_target_pairs={{0,1},{1,0},{2,3},{3,2},{4,5},{5,4},{6,7},{7,6},{8,9},{9,8},{10,11... | collective-permute-start | bytes 2359304 | tf_op jit(solution)/shard_map/ppermute | solution.py:21
  12.1 10.9 %copy-start.7 = (bf16[256,1024]{1,0:T(8,128)(2,1)}, bf16[256,1024]{1,0:T(8,128)(2,1)S(1)}, u32[]{:S(2)}) copy-start(bf16[256,1024]{1,0:T(8,128)(2,1)S(1)} %convolution_convert_fusion) | copy-start | bytes 1572868
  14.9 8.1 %collective-permute-start.5 = (f32[384,128]{1,0:T(8,128)S(1)}, f32[384,128]{1,0:T(8,128)S(1)}, u32[]{:S(2)}, u32[]{:S(2)}) collective-permute-start(f32[384,128]{1,0:T(8,128)S(1)} %get-tuple-element.13), channel_id=1, source_target_pairs={{0,2},{2,0},{1,3},{3,1},{4,6},{6,4},{5,7},{7,5},{8,10},{10,8},{9,1... | collective-permute-start | bytes 589832 | tf_op jit(solution)/shard_map/ppermute | solution.py:21
  25.3 2.5 %copy-start.11 = (bf16[128,256]{1,0:T(8,128)(2,1)S(1)}, bf16[128,256]{1,0:T(8,128)(2,1)}, u32[]{:S(2)}) copy-start(bf16[128,256]{1,0:T(8,128)(2,1)} %get-tuple-element.16) | copy-start | bytes 196612
  25.3 3.5 %copy-start.6 = (f32[384,128]{1,0:T(8,128)S(1)}, f32[384,128]{1,0:T(8,128)}, u32[]{:S(2)}) copy-start(f32[384,128]{1,0:T(8,128)} %copy-done.5) | copy-start | bytes 589828
  26.0 11.0 %slice-start = ((f32[384,128]{1,0:T(8,128)}), f32[256,128]{1,0:T(8,128)S(1)}, s32[]{:S(2)}) async-start(f32[384,128]{1,0:T(8,128)} %copy-done.5), calls=%async_computation | async-start | bytes 262144 | tf_op jit(solution)/shard_map/slice | solution.py:57
  26.0 8.6 %collective-permute-start.6 = (bf16[512,256]{0,1:T(8,128)(2,1)S(1)}, bf16[512,256]{0,1:T(8,128)(2,1)S(1)}, u32[]{:S(2)}, u32[]{:S(2)}) collective-permute-start(bf16[512,256]{0,1:T(8,128)(2,1)S(1)} %pad_maximum_fusion.2), channel_id=1, source_target_pairs={{0,2},{2,0},{1,3},{3,1},{4,6},{6,4},{5,7},{7,5},{8,10},{10,8},{9,1... | collective-permute-start | bytes 786440 | tf_op jit(solution)/shard_map/ppermute | solution.py:21
  27.8 7.7 %collective-permute-start.2 = (bf16[128,256]{1,0:T(8,128)(2,1)S(1)}, bf16[128,256]{1,0:T(8,128)(2,1)}, u32[]{:S(2)}, u32[]{:S(2)}) collective-permute-start(bf16[128,256]{1,0:T(8,128)(2,1)S(1)} %copy-done.11), channel_id=1, source_target_pairs={{0,2},{2,0},{1,3},{3,1},{4,6},{6,4},{5,7},{7,5},{8,10},{10,8},{9,1... | collective-permute-start | bytes 196616 | tf_op jit(solution)/shard_map/ppermute | solution.py:21
  28.8 8.6 %copy-start.10 = (f32[256,128]{1,0:T(8,128)S(1)}, f32[256,128]{1,0:T(8,128)}, u32[]{:S(2)}) copy-start(f32[256,128]{1,0:T(8,128)} %slice.227) | copy-start | bytes 393220
  28.8 9.0 %collective-permute-start.8 = (f32[128,128]{1,0:T(8,128)S(1)}, f32[128,128]{1,0:T(8,128)S(1)}, u32[]{:S(2)}, u32[]{:S(2)}) collective-permute-start(f32[128,128]{1,0:T(8,128)S(1)} %slice_add_fusion.1), channel_id=1, source_target_pairs={{0,4},{4,0},{8,12},{12,8},{1,5},{5,1},{9,13},{13,9},{2,6},{6,2},{1... | collective-permute-start | bytes 196616 | tf_op jit(solution)/shard_map/ppermute | solution.py:21
  37.8 4.7 %collective-permute-start.9 = (bf16[384,128]{0,1:T(8,128)(2,1)S(1)}, bf16[384,128]{0,1:T(8,128)(2,1)S(1)}, u32[]{:S(2)}, u32[]{:S(2)}) collective-permute-start(bf16[384,128]{0,1:T(8,128)(2,1)S(1)} %pad_maximum_fusion.4), channel_id=1, source_target_pairs={{0,4},{4,0},{8,12},{12,8},{1,5},{5,1},{9,13},{13,9},{2,6},{6,2},{1... | collective-permute-start | bytes 294920 | tf_op jit(solution)/shard_map/ppermute | solution.py:21
  39.4 4.5 %collective-permute-start.7 = (bf16[128,256]{1,0:T(8,128)(2,1)}, bf16[128,256]{1,0:T(8,128)(2,1)S(1)}, u32[]{:S(2)}, u32[]{:S(2)}) collective-permute-start(bf16[128,256]{1,0:T(8,128)(2,1)} %get-tuple-element.18), channel_id=1, source_target_pairs={{0,4},{4,0},{8,12},{12,8},{1,5},{5,1},{9,13},{13,9},{2,6},{6,2},{1... | collective-permute-start | bytes 196616 | tf_op jit(solution)/shard_map/ppermute | solution.py:21
  45.4 4.9 %collective-permute-start.11 = (bf16[256,64]{0,1:T(8,128)(2,1)S(1)}, bf16[256,64]{0,1:T(8,128)(2,1)S(1)}, u32[]{:S(2)}, u32[]{:S(2)}) collective-permute-start(bf16[256,64]{0,1:T(8,128)(2,1)S(1)} %pad_maximum_fusion.5), channel_id=1, source_target_pairs={{0,8},{4,12},{8,0},{12,4},{1,9},{5,13},{9,1},{13,5},{2,10},{6,14},... | collective-permute-start | bytes 98312 | tf_op jit(solution)/shard_map/ppermute | solution.py:21
  48.0 6.1 %collective-permute-start.10 = (bf16[128,256]{1,0:T(8,128)(2,1)}, bf16[128,256]{1,0:T(8,128)(2,1)S(1)}, u32[]{:S(2)}, u32[]{:S(2)}) collective-permute-start(bf16[128,256]{1,0:T(8,128)(2,1)} %get-tuple-element.15), channel_id=1, source_target_pairs={{0,8},{4,12},{8,0},{12,4},{1,9},{5,13},{9,1},{13,5},{2,10},{6,14},... | collective-permute-start | bytes 196616 | tf_op jit(solution)/shard_map/ppermute | solution.py:21
  55.2 4.0 %collective-permute-start.12 = (bf16[1,128,128]{1,2,0:T(8,128)(2,1)S(1)}, bf16[1,128,128]{1,2,0:T(8,128)(2,1)S(1)}, u32[]{:S(2)}, u32[]{:S(2)}) collective-permute-start(bf16[1,128,128]{1,2,0:T(8,128)(2,1)S(1)} %fusion.97), channel_id=1, source_target_pairs={{0,4},{4,0},{8,12},{12,8},{1,5},{5,1},{9,13},{13,9},{2,6},{6,2},{1... | collective-permute-start | bytes 98312 | tf_op jit(solution)/shard_map/ppermute | solution.py:21
  59.5 5.0 %collective-permute-start.13 = (bf16[2,128,256]{1,2,0:T(8,128)(2,1)S(1)}, bf16[2,128,256]{1,2,0:T(8,128)(2,1)S(1)}, u32[]{:S(2)}, u32[]{:S(2)}) collective-permute-start(bf16[2,128,256]{1,2,0:T(8,128)(2,1)S(1)} %pad_maximum_fusion.3), channel_id=1, source_target_pairs={{0,2},{2,0},{1,3},{3,1},{4,6},{6,4},{5,7},{7,5},{8,10},{10,8},{9,1... | collective-permute-start | bytes 393224 | tf_op jit(solution)/shard_map/ppermute | solution.py:21
  65.2 1.8 %collective-permute-start.14 = (bf16[3,128,512]{1,2,0:T(8,128)(2,1)S(1)}, bf16[3,128,512]{1,2,0:T(8,128)(2,1)S(1)}, u32[]{:S(2)}, u32[]{:S(2)}) collective-permute-start(bf16[3,128,512]{1,2,0:T(8,128)(2,1)S(1)} %pad_maximum_fusion.1), channel_id=1, source_target_pairs={{0,1},{1,0},{2,3},{3,2},{4,5},{5,4},{6,7},{7,6},{8,9},{9,8},{10,11... | collective-permute-start | bytes 1179656 | tf_op jit(solution)/shard_map/ppermute | solution.py:21
  68.6 1.7 %copy-start.8 = (bf16[256,1024]{1,0:T(8,128)(2,1)S(1)}, bf16[256,1024]{1,0:T(8,128)(2,1)}, u32[]{:S(2)}) copy-start(bf16[256,1024]{1,0:T(8,128)(2,1)} %copy-done.7) | copy-start | bytes 1572868
  (4 other events, 3.9 us)

commit v8 on v7

--- a/solution.py
+++ b/solution.py
@@ -41,23 +41,30 @@
     bits = bit_axes()
     levels, pixels, rank = v_basis.shape
     width = templates.shape[1]
-    c0 = jnp.dot(leaf_inverse, templates, preferred_element_type=F32)
-    c0b = c0.astype(BF16)
-
     cross = jnp.einsum("kis,lir->klrs", u_basis, v_basis, preferred_element_type=F32)
     counts = [levels - 1 - k for k in range(levels - 1)]
     suffix = jnp.concatenate(
         [cross[k, k + 1 :].reshape(-1, rank) for k in range(levels - 1)], axis=0
     )
-    w_own, w_sib = [None] * levels, [None] * levels
+    w_own, m_sib = [None] * levels, [None] * levels
     for b in range(levels - 1):
         n = counts[b] * rank
-        got = swap(suffix, b, bits)
         w_own[b] = suffix[:n].reshape(counts[b], rank, rank)
-        w_sib[b] = got[:n].reshape(counts[b], rank, rank)
-        suffix = suffix[n:] + got[n:]
-    couple_sib = [swap(coupling[s, 0], s, bits) for s in range(levels)]
+        m = jnp.einsum(
+            "nrs,sk->nrk", w_own[b], coupling[b, 0].astype(F32),
+            preferred_element_type=F32, precision=lax.Precision.HIGHEST,
+        )
+        later = suffix[n:]
+        payload = jnp.concatenate([later, m.reshape(-1, rank)], axis=0)
+        if b == 0:
+            payload, templates = lax.optimization_barrier((payload, templates))
+        got = swap(payload, b, bits)
+        k = later.shape[0]
+        m_sib[b] = got[k:].reshape(counts[b], rank, 2 * rank)
+        suffix = later + got[:k]
 
+    c0 = jnp.dot(leaf_inverse, templates, preferred_element_type=F32)
+    c0b = c0.astype(BF16)
     proj0 = jnp.dot(v_basis[0].T, c0b, preferred_element_type=F32)
     rest = None
     if levels > 1:
@@ -90,7 +97,7 @@
                 parts.append(send.astype(BF16).reshape(n * rank, w))
             payload = jnp.concatenate(parts, axis=0)
             if s < levels - 1:
-                payload, w_sib[s] = lax.optimization_barrier((payload, w_sib[s]))
+                payload, m_sib[s] = lax.optimization_barrier((payload, m_sib[s]))
             got = swap(payload, s, bits)
             theirs_b = jnp.concatenate([got[:rank], got[rank : 2 * rank]], axis=1)
             if n > 0:
@@ -102,17 +109,16 @@
             jnp.concatenate([mine_b, theirs_b], axis=0),
             jnp.concatenate([theirs_b, mine_b], axis=0),
         )
-        couple = jnp.concatenate([coupling[s, 0], couple_sib[s]], axis=0)
-        coefs = jnp.dot(couple, stacked, preferred_element_type=F32).astype(BF16)
-        own_coefs.append(coefs[:rank])
+        coefs = jnp.dot(coupling[s, 0], stacked, preferred_element_type=F32).astype(BF16)
+        own_coefs.append(coefs)
         if s < levels - 1:
             w = coefs.shape[1] // 2
-            piece = cols(coefs, side(s, bits) * w, w).astype(F32)
+            h = side(s, bits)
             fix = jnp.einsum(
-                "nrs,st->nrt", w_own[s], piece[:rank],
+                "nrs,st->nrt", w_own[s], cols(coefs, h * w, w).astype(F32),
                 preferred_element_type=F32, precision=lax.Precision.HIGHEST,
             ) + jnp.einsum(
-                "nrs,st->nrt", w_sib[s], piece[rank:],
+                "nrk,kt->nrt", m_sib[s], cols(stacked, h * w, w).astype(F32),
                 preferred_element_type=F32, precision=lax.Precision.HIGHEST,
             )
             rest = rest - fix

time: 72.2 us -> 78.6 us (1.089)
  local copies, waits for them, and re-layouts: 6.54 us -> 13.9 us
  waiting for transfers between devices: 26.9 us -> 22 us
  other arithmetic: 4.07 us -> 7.14 us
  matrix products: 18.8 us -> 21 us
  starting transfers between devices: 15.1 us -> 13.4 us
    reshape x0 -> x6, local copies, waits for them, and re-layouts: none -> 5.23 us  [the longest x3 2.89 us: on_device(): m_sib[b] = got[k:].reshape(counts[b], rank, 2 * rank)]
    ppermute x15 -> x11, waiting for transfers between devices: 26.9 us -> 22 us  [swap(): return lax.ppermute(x, axis, [(i, i ^ 1 << stride) for i in range(n)])]
    dot_general x10 -> x13, matrix products: 8.33 us -> 11.8 us  [the longest x3 3.98 us: on_device(): jnp.einsum('nrs,sk->nrk', w_own[b], coupling[b, 0].astype(F32), preferred...]
    slice x2 -> x3, local copies, waits for them, and re-layouts: 0.01 us -> 3.43 us  [the longest x2 2.74 us: on_device(): m_sib[b] = got[k:].reshape(counts[b], rank, 2 * rank)]
    concatenate x1 -> x2, other arithmetic: 0.8 us -> 2.59 us  [on_device(): payload = jnp.concatenate([later, m.reshape(-1, rank)], axis=0)]
    squeeze x1 -> x0, local copies, waits for them, and re-layouts: 1.72 us -> none  [on_device(): couple = jnp.concatenate([coupling[s, 0], couple_sib[s]], axis=0)]
    ppermute x15 -> x11, starting transfers between devices: 15.1 us -> 13.4 us  [swap(): return lax.ppermute(x, axis, [(i, i ^ 1 << stride) for i in range(n)])]
    select_n x0 -> x3, other arithmetic: none -> 1.38 us  [on_device(): jnp.where(lower, jnp.concatenate([mine_b, theirs_b], axis=0), jnp.concate...]
  transfers between devices with their start and end apart: 15 -> 11, of which waited for: 9 -> 7; matrix products, arithmetic and copies ran while one was open for 22% -> 30% of each run, Pallas kernels for 0% -> 0%
where the time goes in v8:
time: 78.6 us; the launch traced here: 77.8 us
  waiting for transfers between devices  22 us (28%)
  matrix products  21 us (27%)
  local copies, waits for them, and re-layouts  13.9 us (18%)
  starting transfers between devices  13.4 us (17%)
  other arithmetic  7.14 us (9%)
    ppermute x11, waiting for transfers between devices, swap(): return lax.ppermute(x, axis, [(i, i ^ 1 << stride) for i in range(n)])  22 us
    ppermute x11, starting transfers between devices, swap(): return lax.ppermute(x, axis, [(i, i ^ 1 << stride) for i in range(n)])  13.4 us
    dot_general x3, matrix products, on_device(): jnp.einsum('nrs,sk->nrk', w_own[b], coupling[b, 0].astype(F32), preferred...  3.98 us
    dot_general x3, matrix products, on_device(): jnp.einsum('nrs,st->nrt', w_own[s], cols(coefs, h * w, w).astype(F32), pr...  3.63 us
    reshape x3, local copies, waits for them, and re-layouts, on_device(): m_sib[b] = got[k:].reshape(counts[b], rank, 2 * rank)  2.89 us
    slice x2, local copies, waits for them, and re-layouts, on_device(): m_sib[b] = got[k:].reshape(counts[b], rank, 2 * rank)  2.74 us
    concatenate x2, other arithmetic, on_device(): payload = jnp.concatenate([later, m.reshape(-1, rank)], axis=0)  2.59 us
    dot_general x3, matrix products, on_device(): jnp.einsum('nrk,kt->nrt', m_sib[s], cols(stacked, h * w, w).astype(F32),...  2.46 us
  transfers between devices with their start and end apart: 11, of which 7 were waited for; matrix products, arithmetic and copies ran while one was open for 30% of the time, Pallas kernels for 0%

profile of v8, /device:TPU:0, one launch (start us, length us, event | category | flops | bytes accessed | tf_op | source)
XLA Modules:
  0.0 77.8 jit_solution(15890022415082628327)
XLA Ops:
  0.0 1.8 %convolution_bitcast_fusion = f32[4,4,128,128]{3,2,0,1:T(8,128)S(1)} fusion(bf16[4,512,128]{2,1,0:T(8,128)(2,1)} %param.7, bf16[4,512,128]{2,1,0:T(8,128)(2,1)} %param.8), kind=kOutput, calls=%fused_computation.2 | convolution fusion | flops 268435456 | bytes 2097152 | tf_op jit(solution)/shard_map/kis,lir->klrs/dot_general | solution.py:44
  4.9 2.1 %fusion.105 = (bf16[1024,512]{1,0:T(8,128)(2,1)S(1)}, f32[1024,512]{1,0:T(8,128)}) fusion(bf16[512,1024]{1,0:T(8,128)(2,1)S(1)} %copy-done, bf16[512,512]{1,0:T(8,128)(2,1)S(1)} %copy-done.9), kind=kOutput, calls=%fused_computation.152 | convolution fusion | flops 537395200 | bytes 4718592 | tf_op jit(solution)/shard_map/dot_general | solution.py:66
  8.0 1.3 %convolution_bitcast_fusion.1 = f32[3,128,512]{1,2,0:T(8,128)} fusion(bf16[1024,512]{1,0:T(8,128)(2,1)S(1)} %get-tuple-element.29, s32[]{:T(128)S(6)} %select_n.69, bf16[4,512,128]{2,1,0:T(8,128)(2,1)S(1)} %copy-done.2), kind=kOutput, calls=%fused_computation.4 | convolution fusion | flops 201326592 | bytes 1703940 | tf_op jit(solution)/shard_map/lir,it->lrt/dot_general | solution.py:77
  12.3 2.3 %fusion.26 = f32[3,128,512]{1,2,0:T(8,128)} fusion(f32[4,4,128,128]{3,2,0,1:T(8,128)} %copy-done.3, bf16[1024,128]{1,0:T(8,128)(2,1)S(1)} %convolution_convert_fusion, s32[]{:T(128)S(6)} %select_n.68), kind=kOutput, calls=%fused_computation.62 | convolution fusion | flops 301989888 | bytes 1114116 | tf_op jit(solution)/shard_map/nrs,st->nrt/dot_general | solution.py:117
  16.3 1.8 %slice.172 = f32[768,128]{1,0:T(8,128)} slice(f32[1152,128]{1,0:T(8,128)} %collective-permute-done.2), slice={[384:1152], [0:128]} | slice | bytes 786432 | tf_op jit(solution)/shard_map/slice | solution.py:63
  18.0 1.9 %reshape.50 = f32[3,128,256]{2,1,0:T(8,128)} reshape(f32[768,128]{1,0:T(8,128)} %slice.172) | data formatting | bytes 786432 | tf_op jit(solution)/shard_map/reshape | solution.py:63
  19.9 1.8 %fusion.61 = f32[2,128,256]{2,1,0:T(8,128)} fusion(f32[2,128,128]{2,1,0:T(8,128)S(1)} %bitcast.143, bf16[4,1,128,256]{3,2,1,0:T(8,128)(2,1)} %param.9), kind=kOutput, calls=%fused_computation.109 | convolution fusion | flops 100663296 | bytes 458752 | tf_op jit(solution)/shard_map/nrs,sk->nrk/dot_general | solution.py:53
  21.7 1.7 %reshape.53 = f32[512,128]{1,0:T(8,128)} reshape(f32[2,128,256]{2,1,0:T(8,128)} %fusion.61) | data formatting | bytes 524288 | tf_op jit(solution)/shard_map/reshape | solution.py:58
  23.3 1.7 %pad_maximum_fusion.2 = f32[640,128]{1,0:T(8,128)} fusion(f32[512,128]{1,0:T(8,128)} %reshape.53, f32[128,128]{1,0:T(8,128)} %slice.178), kind=kLoop, calls=%fused_computation.43 | loop fusion | flops 81920 | bytes 655360 | tf_op jit(solution)/shard_map/concatenate | solution.py:58
  25.0 2.6 %collective-permute-start.3 = (f32[640,128]{1,0:T(8,128)}, f32[640,128]{1,0:T(8,128)}, u32[]{:S(2)}, u32[]{:S(2)}) collective-permute-start(f32[640,128]{1,0:T(8,128)} %pad_maximum_fusion.2), channel_id=1, source_target_pairs={{0,2},{2,0},{1,3},{3,1},{4,6},{6,4},{5,7},{7,5},{8,10},{10,8},{9,1... | collective-permute-start | bytes 983048 | tf_op jit(solution)/shard_map/ppermute | solution.py:21
  27.6 1.9 %convolution_add_fusion = f32[3,128,512]{1,2,0:T(8,128)S(1)} fusion(f32[3,128,512]{1,2,0:T(8,128)} %fusion.26, f32[3,128,256]{2,1,0:T(8,128)} %reshape.50, bf16[256,1024]{1,0:T(8,128)(2,1)S(1)} %maximum_select_fusion, s32[]{:T(128)S(6)} %select_n.68), kind=kOutput, calls=%fused_computation.3 | convolution fusion | flops 604176384 | bytes 2228228 | tf_op jit(solution)/shard_map/nrk,kt->nrt/dot_general | solution.py:120
  29.5 1.6 %fusion.2 = f32[3,128,512]{1,2,0:T(8,128)S(1)} fusion(f32[3,128,512]{1,2,0:T(8,128)S(1)} %convolution_add_fusion, f32[3,128,512]{1,2,0:T(8,128)} %collective-permute-done.1, bf16[1024,512]{1,0:T(8,128)(2,1)S(1)} %get-tuple-element.29, s32[]{:T(128)S(6)} %select_n.68, bf16[4,512,128]{2,1,0:T(8,128)(2,1)S(1)} %copy-done.2), kind=kOutput, calls=%fused_computation.7 | convolution fusion | flops 201719808 | bytes 3276804 | tf_op jit(solution)/shard_map/lir,it->lrt/dot_general | solution.py:73
  31.5 4.7 %collective-permute-done.3 = f32[640,128]{1,0:T(8,128)} collective-permute-done((f32[640,128]{1,0:T(8,128)}, f32[640,128]{1,0:T(8,128)}, u32[]{:S(2)}, u32[]{:S(2)}) %collective-permute-start.3) | collective-permute-done | bytes 327712 | tf_op jit(solution)/shard_map/ppermute | solution.py:21
  37.3 1.8 %collective-permute-start.4 = (bf16[512,256]{0,1:T(8,128)(2,1)S(1)}, bf16[512,256]{0,1:T(8,128)(2,1)S(1)}, u32[]{:S(2)}, u32[]{:S(2)}) collective-permute-start(bf16[512,256]{0,1:T(8,128)(2,1)S(1)} %pad_maximum_fusion.3), channel_id=1, source_target_pairs={{0,2},{2,0},{1,3},{3,1},{4,6},{6,4},{5,7},{7,5},{8,10},{10,8},{9,1... | collective-permute-start | bytes 786440 | tf_op jit(solution)/shard_map/ppermute | solution.py:21
  40.8 1.6 %collective-permute-start.5 = (f32[256,128]{1,0:T(8,128)}, f32[256,128]{1,0:T(8,128)}, u32[]{:S(2)}, u32[]{:S(2)}) collective-permute-start(f32[256,128]{1,0:T(8,128)} %reshape.56), channel_id=1, source_target_pairs={{0,4},{4,0},{8,12},{12,8},{1,5},{5,1},{9,13},{13,9},{2,6},{6,2},{1... | collective-permute-start | bytes 393224 | tf_op jit(solution)/shard_map/ppermute | solution.py:21
  42.4 3.7 %collective-permute-done.5 = f32[256,128]{1,0:T(8,128)} collective-permute-done((f32[256,128]{1,0:T(8,128)}, f32[256,128]{1,0:T(8,128)}, u32[]{:S(2)}, u32[]{:S(2)}) %collective-permute-start.5) | collective-permute-done | bytes 131104 | tf_op jit(solution)/shard_map/ppermute | solution.py:21
  50.0 1.6 %collective-permute-start.6 = (bf16[384,128]{0,1:T(8,128)(2,1)S(1)}, bf16[384,128]{0,1:T(8,128)(2,1)S(1)}, u32[]{:S(2)}, u32[]{:S(2)}) collective-permute-start(bf16[384,128]{0,1:T(8,128)(2,1)S(1)} %pad_maximum_fusion.5), channel_id=1, source_target_pairs={{0,4},{4,0},{8,12},{12,8},{1,5},{5,1},{9,13},{13,9},{2,6},{6,2},{1... | collective-permute-start | bytes 294920 | tf_op jit(solution)/shard_map/ppermute | solution.py:21
  51.7 3.0 %collective-permute-done.6 = bf16[384,128]{0,1:T(8,128)(2,1)S(1)} collective-permute-done((bf16[384,128]{0,1:T(8,128)(2,1)S(1)}, bf16[384,128]{0,1:T(8,128)(2,1)S(1)}, u32[]{:S(2)}, u32[]{:S(2)}) %collective-permute-start.6) | collective-permute-done | bytes 98336 | tf_op jit(solution)/shard_map/ppermute | solution.py:21
  56.3 2.6 %collective-permute-start.7 = (bf16[256,64]{0,1:T(8,128)(2,1)S(1)}, bf16[256,64]{0,1:T(8,128)(2,1)S(1)}, u32[]{:S(2)}, u32[]{:S(2)}) collective-permute-start(bf16[256,64]{0,1:T(8,128)(2,1)S(1)} %pad_maximum_fusion.6), channel_id=1, source_target_pairs={{0,8},{4,12},{8,0},{12,4},{1,9},{5,13},{9,1},{13,5},{2,10},{6,14},... | collective-permute-start | bytes 98312 | tf_op jit(solution)/shard_map/ppermute | solution.py:21
  58.9 2.2 %collective-permute-done.7 = bf16[256,64]{0,1:T(8,128)(2,1)S(1)} collective-permute-done((bf16[256,64]{0,1:T(8,128)(2,1)S(1)}, bf16[256,64]{0,1:T(8,128)(2,1)S(1)}, u32[]{:S(2)}, u32[]{:S(2)}) %collective-permute-start.7) | collective-permute-done | bytes 32800 | tf_op jit(solution)/shard_map/ppermute | solution.py:21
  61.3 1.6 %collective-permute-start.8 = (bf16[1,128,128]{1,2,0:T(8,128)(2,1)S(1)}, bf16[1,128,128]{1,2,0:T(8,128)(2,1)S(1)}, u32[]{:S(2)}, u32[]{:S(2)}) collective-permute-start(bf16[1,128,128]{1,2,0:T(8,128)(2,1)S(1)} %fusion.5), channel_id=1, source_target_pairs={{0,4},{4,0},{8,12},{12,8},{1,5},{5,1},{9,13},{13,9},{2,6},{6,2},{1... | collective-permute-start | bytes 98312 | tf_op jit(solution)/shard_map/ppermute | solution.py:21
  62.9 2.3 %collective-permute-done.8 = bf16[1,128,128]{1,2,0:T(8,128)(2,1)S(1)} collective-permute-done((bf16[1,128,128]{1,2,0:T(8,128)(2,1)S(1)}, bf16[1,128,128]{1,2,0:T(8,128)(2,1)S(1)}, u32[]{:S(2)}, u32[]{:S(2)}) %collective-permute-start.8) | collective-permute-done | bytes 32800 | tf_op jit(solution)/shard_map/ppermute | solution.py:21
  66.0 4.7 %collective-permute-done.9 = bf16[2,128,256]{1,2,0:T(8,128)(2,1)S(1)} collective-permute-done((bf16[2,128,256]{1,2,0:T(8,128)(2,1)S(1)}, bf16[2,128,256]{1,2,0:T(8,128)(2,1)S(1)}, u32[]{:S(2)}, u32[]{:S(2)}) %collective-permute-start.9) | collective-permute-done | bytes 131104 | tf_op jit(solution)/shard_map/ppermute | solution.py:21
  76.5 1.3 %copy.23 = bf16[512,1024]{1,0:T(8,128)(2,1)} copy(bf16[512,1024]{0,1:T(8,128)(2,1)S(1)} %fusion) | data formatting | bytes 2097152 | tf_op jit(solution)/shard_map/sub | solution.py:135
  (86 shorter events, 23.7 us)
Async XLA Ops:
  0.0 4.8 %copy-start = (bf16[512,1024]{1,0:T(8,128)(2,1)S(1)}, bf16[512,1024]{1,0:T(8,128)(2,1)}, u32[]{:S(2)}) copy-start(bf16[512,1024]{1,0:T(8,128)(2,1)} %param.5) | copy-start | bytes 3145732
  0.0 4.8 %copy-start.9 = (bf16[512,512]{1,0:T(8,128)(2,1)S(1)}, bf16[512,512]{1,0:T(8,128)(2,1)}, u32[]{:S(2)}) copy-start(bf16[512,512]{1,0:T(8,128)(2,1)} %param.6) | copy-start | bytes 1572868
  1.8 1.0 %copy-start.3 = (f32[4,4,128,128]{3,2,0,1:T(8,128)}, f32[4,4,128,128]{3,2,0,1:T(8,128)S(1)}, u32[]{:S(2)}) copy-start(f32[4,4,128,128]{3,2,0,1:T(8,128)S(1)} %convolution_bitcast_fusion) | copy-start | bytes 3145732
  1.8 5.1 %copy-start.7 = (f32[128,128]{1,0:T(8,128)}, f32[128,128]{1,0:T(8,128)S(1)}, u32[]{:S(2)}) copy-start(f32[128,128]{1,0:T(8,128)S(1)} %slice_bitcast_fusion.9) | copy-start | bytes 196612
  4.9 2.1 %copy-start.2 = (bf16[4,512,128]{2,1,0:T(8,128)(2,1)S(1)}, bf16[4,512,128]{2,1,0:T(8,128)(2,1)}, u32[]{:S(2)}) copy-start(bf16[4,512,128]{2,1,0:T(8,128)(2,1)} %param.7) | copy-start | bytes 1572868
  7.5 2.4 %collective-permute-start = (bf16[128,1024]{1,0:T(8,128)(2,1)S(1)}, bf16[128,1024]{1,0:T(8,128)(2,1)}, u32[]{:S(2)}, u32[]{:S(2)}) collective-permute-start(bf16[128,1024]{1,0:T(8,128)(2,1)S(1)} %fusion.3), channel_id=1, source_target_pairs={{0,1},{1,0},{2,3},{3,2},{4,5},{5,4},{6,7},{7,6},{8,9},{9,8},{10,11... | collective-permute-start | bytes 786440 | tf_op jit(solution)/shard_map/ppermute | solution.py:21
  8.0 6.6 %collective-permute-start.2 = (f32[1152,128]{1,0:T(8,128)}, f32[1152,128]{1,0:T(8,128)}, u32[]{:S(2)}, u32[]{:S(2)}) collective-permute-start(f32[1152,128]{1,0:T(8,128)} %pad_maximum_fusion), channel_id=1, source_target_pairs={{0,1},{1,0},{2,3},{3,2},{4,5},{5,4},{6,7},{7,6},{8,9},{9,8},{10,11... | collective-permute-start | bytes 1769480 | tf_op jit(solution)/shard_map/ppermute | solution.py:21
  9.4 20.2 %collective-permute-start.1 = (f32[3,128,512]{1,2,0:T(8,128)}, f32[3,128,512]{1,2,0:T(8,128)}, u32[]{:S(2)}, u32[]{:S(2)}) collective-permute-start(f32[3,128,512]{1,2,0:T(8,128)} %convolution_bitcast_fusion.1), channel_id=1, source_target_pairs={{0,1},{1,0},{2,3},{3,2},{4,5},{5,4},{6,7},{7,6},{8,9},{9,8},{10,11... | collective-permute-start | bytes 2359304 | tf_op jit(solution)/shard_map/ppermute | solution.py:21
  15.5 0.7 copy-start.5
  25.0 11.2 %collective-permute-start.3 = (f32[640,128]{1,0:T(8,128)}, f32[640,128]{1,0:T(8,128)}, u32[]{:S(2)}, u32[]{:S(2)}) collective-permute-start(f32[640,128]{1,0:T(8,128)} %pad_maximum_fusion.2), channel_id=1, source_target_pairs={{0,2},{2,0},{1,3},{3,1},{4,6},{6,4},{5,7},{7,5},{8,10},{10,8},{9,1... | collective-permute-start | bytes 983048 | tf_op jit(solution)/shard_map/ppermute | solution.py:21
  31.1 8.0 %copy-start.6 = (f32[384,128]{1,0:T(8,128)S(1)}, f32[384,128]{1,0:T(8,128)}, u32[]{:S(2)}) copy-start(f32[384,128]{1,0:T(8,128)} %copy-done.5) | copy-start | bytes 589828
  31.1 8.0 %copy-start.8 = (bf16[4,1,128,256]{3,2,1,0:T(8,128)(2,1)S(1)}, bf16[4,1,128,256]{3,2,1,0:T(8,128)(2,1)}, u32[]{:S(2)}) copy-start(bf16[4,1,128,256]{3,2,1,0:T(8,128)(2,1)} %param.9) | copy-start | bytes 786436
  37.3 9.8 %collective-permute-start.4 = (bf16[512,256]{0,1:T(8,128)(2,1)S(1)}, bf16[512,256]{0,1:T(8,128)(2,1)S(1)}, u32[]{:S(2)}, u32[]{:S(2)}) collective-permute-start(bf16[512,256]{0,1:T(8,128)(2,1)S(1)} %pad_maximum_fusion.3), channel_id=1, source_target_pairs={{0,2},{2,0},{1,3},{3,1},{4,6},{6,4},{5,7},{7,5},{8,10},{10,8},{9,1... | collective-permute-start | bytes 786440 | tf_op jit(solution)/shard_map/ppermute | solution.py:21
  40.8 5.3 %collective-permute-start.5 = (f32[256,128]{1,0:T(8,128)}, f32[256,128]{1,0:T(8,128)}, u32[]{:S(2)}, u32[]{:S(2)}) collective-permute-start(f32[256,128]{1,0:T(8,128)} %reshape.56), channel_id=1, source_target_pairs={{0,4},{4,0},{8,12},{12,8},{1,5},{5,1},{9,13},{13,9},{2,6},{6,2},{1... | collective-permute-start | bytes 393224 | tf_op jit(solution)/shard_map/ppermute | solution.py:21
  47.1 0.7 copy-start.10
  49.9 21.4 %copy-start.4 = (bf16[4,512,128]{2,1,0:T(8,128)(2,1)S(1)}, bf16[4,512,128]{2,1,0:T(8,128)(2,1)}, u32[]{:S(2)}) copy-start(bf16[4,512,128]{2,1,0:T(8,128)(2,1)} %param.8) | copy-start | bytes 1572868
  50.0 4.7 %collective-permute-start.6 = (bf16[384,128]{0,1:T(8,128)(2,1)S(1)}, bf16[384,128]{0,1:T(8,128)(2,1)S(1)}, u32[]{:S(2)}, u32[]{:S(2)}) collective-permute-start(bf16[384,128]{0,1:T(8,128)(2,1)S(1)} %pad_maximum_fusion.5), channel_id=1, source_target_pairs={{0,4},{4,0},{8,12},{12,8},{1,5},{5,1},{9,13},{13,9},{2,6},{6,2},{1... | collective-permute-start | bytes 294920 | tf_op jit(solution)/shard_map/ppermute | solution.py:21
  56.3 4.9 %collective-permute-start.7 = (bf16[256,64]{0,1:T(8,128)(2,1)S(1)}, bf16[256,64]{0,1:T(8,128)(2,1)S(1)}, u32[]{:S(2)}, u32[]{:S(2)}) collective-permute-start(bf16[256,64]{0,1:T(8,128)(2,1)S(1)} %pad_maximum_fusion.6), channel_id=1, source_target_pairs={{0,8},{4,12},{8,0},{12,4},{1,9},{5,13},{9,1},{13,5},{2,10},{6,14},... | collective-permute-start | bytes 98312 | tf_op jit(solution)/shard_map/ppermute | solution.py:21
  61.3 4.0 %collective-permute-start.8 = (bf16[1,128,128]{1,2,0:T(8,128)(2,1)S(1)}, bf16[1,128,128]{1,2,0:T(8,128)(2,1)S(1)}, u32[]{:S(2)}, u32[]{:S(2)}) collective-permute-start(bf16[1,128,128]{1,2,0:T(8,128)(2,1)S(1)} %fusion.5), channel_id=1, source_target_pairs={{0,4},{4,0},{8,12},{12,8},{1,5},{5,1},{9,13},{13,9},{2,6},{6,2},{1... | collective-permute-start | bytes 98312 | tf_op jit(solution)/shard_map/ppermute | solution.py:21
  65.6 5.0 %collective-permute-start.9 = (bf16[2,128,256]{1,2,0:T(8,128)(2,1)S(1)}, bf16[2,128,256]{1,2,0:T(8,128)(2,1)S(1)}, u32[]{:S(2)}, u32[]{:S(2)}) collective-permute-start(bf16[2,128,256]{1,2,0:T(8,128)(2,1)S(1)} %pad_maximum_fusion.4), channel_id=1, source_target_pairs={{0,2},{2,0},{1,3},{3,1},{4,6},{6,4},{5,7},{7,5},{8,10},{10,8},{9,1... | collective-permute-start | bytes 393224 | tf_op jit(solution)/shard_map/ppermute | solution.py:21
  71.3 1.8 %collective-permute-start.10 = (bf16[3,128,512]{1,2,0:T(8,128)(2,1)S(1)}, bf16[3,128,512]{1,2,0:T(8,128)(2,1)S(1)}, u32[]{:S(2)}, u32[]{:S(2)}) collective-permute-start(bf16[3,128,512]{1,2,0:T(8,128)(2,1)S(1)} %pad_maximum_fusion.1), channel_id=1, source_target_pairs={{0,1},{1,0},{2,3},{3,2},{4,5},{5,4},{6,7},{7,6},{8,9},{9,8},{10,11... | collective-permute-start | bytes 1179656 | tf_op jit(solution)/shard_map/ppermute | solution.py:21
  74.3 1.6 %copy-start.1 = (f32[1024,512]{1,0:T(8,128)S(1)}, f32[1024,512]{1,0:T(8,128)}, u32[]{:S(2)}) copy-start(f32[1024,512]{1,0:T(8,128)} %get-tuple-element.30) | copy-start | bytes 6291460

commit v9 on v8

--- a/solution.py
+++ b/solution.py
@@ -51,7 +51,7 @@
         n = counts[b] * rank
         w_own[b] = suffix[:n].reshape(counts[b], rank, rank)
         m = jnp.einsum(
-            "nrs,sk->nrk", w_own[b], coupling[b, 0].astype(F32),
+            "nrs,sk->nkr", w_own[b], coupling[b, 0].astype(F32),
             preferred_element_type=F32, precision=lax.Precision.HIGHEST,
         )
         later = suffix[n:]
@@ -60,7 +60,7 @@
             payload, templates = lax.optimization_barrier((payload, templates))
         got = swap(payload, b, bits)
         k = later.shape[0]
-        m_sib[b] = got[k:].reshape(counts[b], rank, 2 * rank)
+        m_sib[b] = got[k:].reshape(counts[b], 2 * rank, rank)
         suffix = later + got[:k]
 
     c0 = jnp.dot(leaf_inverse, templates, preferred_element_type=F32)
@@ -118,7 +118,7 @@
                 "nrs,st->nrt", w_own[s], cols(coefs, h * w, w).astype(F32),
                 preferred_element_type=F32, precision=lax.Precision.HIGHEST,
             ) + jnp.einsum(
-                "nrk,kt->nrt", m_sib[s], cols(stacked, h * w, w).astype(F32),
+                "nkr,kt->nrt", m_sib[s], cols(stacked, h * w, w).astype(F32),
                 preferred_element_type=F32, precision=lax.Precision.HIGHEST,
             )
             rest = rest - fix

time: 78.6 us -> 76.2 us (0.969)
  local copies, waits for them, and re-layouts: 13.9 us -> 9.85 us
  matrix products: 21 us -> 24.1 us
  waiting for transfers between devices: 22 us -> 19 us
  starting transfers between devices: 13.4 us -> 14.7 us
    reshape x6 -> x0, local copies, waits for them, and re-layouts: 5.23 us -> none  [the longest x3 2.89 us: on_device(): m_sib[b] = got[k:].reshape(counts[b], rank, 2 * rank)]
    ppermute x11, waiting for transfers between devices: 22 us -> 19 us  [swap(): return lax.ppermute(x, axis, [(i, i ^ 1 << stride) for i in range(n)])]
    transpose x0 -> x2, local copies, waits for them, and re-layouts: none -> 1.96 us  [on_device(): jnp.einsum('nrs,sk->nkr', w_own[b], coupling[b, 0].astype(F32), preferred...]
    dot_general x4, matrix products: 1.75 us -> 3.43 us  [on_device(): jnp.dot(coupling[s, 0], stacked, preferred_element_type=F32).astype(BF16)]
    dot_general x6, matrix products: 6.44 us -> 7.86 us  [the longest x3 4.64 us: on_device(): jnp.einsum('nrs,sk->nkr', w_own[b], coupling[b, 0].astype(F32), preferred...]
    ppermute x11, starting transfers between devices: 13.4 us -> 14.7 us  [swap(): return lax.ppermute(x, axis, [(i, i ^ 1 << stride) for i in range(n)])]
  transfers between devices with their start and end apart: 11 -> 11, of which waited for: 7 -> 7; matrix products, arithmetic and copies ran while one was open for 30% -> 29% of each run, Pallas kernels for 0% -> 0%
where the time goes in v9:
time: 76.2 us; the launch traced here: 75.3 us
  matrix products  24.1 us (32%)
  waiting for transfers between devices  19 us (25%)
  starting transfers between devices  14.7 us (19%)
  local copies, waits for them, and re-layouts  9.85 us (13%)
  other arithmetic  7.14 us (9%)
    ppermute x11, waiting for transfers between devices, swap(): return lax.ppermute(x, axis, [(i, i ^ 1 << stride) for i in range(n)])  19 us
    ppermute x11, starting transfers between devices, swap(): return lax.ppermute(x, axis, [(i, i ^ 1 << stride) for i in range(n)])  14.7 us
    dot_general x3, matrix products, on_device(): jnp.einsum('nrs,sk->nkr', w_own[b], coupling[b, 0].astype(F32), preferred...  4.64 us
    dot_general x3, matrix products, on_device(): jnp.einsum('nrs,st->nrt', w_own[s], cols(coefs, h * w, w).astype(F32), pr...  3.63 us
    dot_general x4, matrix products, on_device(): jnp.dot(coupling[s, 0], stacked, preferred_element_type=F32).astype(BF16)  3.43 us
    dot_general x3, matrix products, on_device(): jnp.einsum('nkr,kt->nrt', m_sib[s], cols(stacked, h * w, w).astype(F32),...  3.22 us
    concatenate x2, other arithmetic, on_device(): payload = jnp.concatenate([later, m.reshape(-1, rank)], axis=0)  2.59 us
    unnamed x22, local copies, waits for them, and re-layouts  2.39 us
  transfers between devices with their start and end apart: 11, of which 7 were waited for; matrix products, arithmetic and copies ran while one was open for 29% of the time, Pallas kernels for 0%

profile of v9, /device:TPU:0, one launch (start us, length us, event | category | flops | bytes accessed | tf_op | source)
XLA Modules:
  0.0 75.3 jit_solution(5410207400476479267)
XLA Ops:
  0.0 1.8 %convolution_bitcast_fusion = f32[4,4,128,128]{3,2,0,1:T(8,128)S(1)} fusion(bf16[4,512,128]{2,1,0:T(8,128)(2,1)} %param.7, bf16[4,512,128]{2,1,0:T(8,128)(2,1)} %param.8), kind=kOutput, calls=%fused_computation.2 | convolution fusion | flops 268435456 | bytes 2097152 | tf_op jit(solution)/shard_map/kis,lir->klrs/dot_general | solution.py:44
  5.0 2.1 %fusion.102 = (bf16[1024,512]{1,0:T(8,128)(2,1)S(1)}, f32[1024,512]{1,0:T(8,128)}) fusion(bf16[512,1024]{1,0:T(8,128)(2,1)S(1)} %copy-done, bf16[512,512]{1,0:T(8,128)(2,1)S(1)} %copy-done.9), kind=kOutput, calls=%fused_computation.152 | convolution fusion | flops 537395200 | bytes 4718592 | tf_op jit(solution)/shard_map/dot_general | solution.py:66
  8.2 1.3 %convolution_bitcast_fusion.1 = f32[3,128,512]{1,2,0:T(8,128)} fusion(bf16[1024,512]{1,0:T(8,128)(2,1)S(1)} %get-tuple-element.29, s32[]{:T(128)S(6)} %select_n.69, bf16[4,512,128]{2,1,0:T(8,128)(2,1)S(1)} %copy-done.2), kind=kOutput, calls=%fused_computation.4 | convolution fusion | flops 201326592 | bytes 1703940 | tf_op jit(solution)/shard_map/lir,it->lrt/dot_general | solution.py:77
  12.4 2.3 %fusion.26 = f32[3,128,512]{1,2,0:T(8,128)} fusion(f32[4,4,128,128]{3,2,0,1:T(8,128)} %copy-done.3, bf16[1024,128]{1,0:T(8,128)(2,1)S(1)} %convolution_convert_fusion, s32[]{:T(128)S(6)} %select_n.68), kind=kOutput, calls=%fused_computation.65 | convolution fusion | flops 301989888 | bytes 1114116 | tf_op jit(solution)/shard_map/nrs,st->nrt/dot_general | solution.py:117
  16.4 1.8 %convolution_bitcast_fusion.4 = f32[2,256,128]{1,2,0:T(8,128)} fusion(f32[2,128,128]{2,1,0:T(8,128)S(1)} %bitcast.156, bf16[4,1,128,256]{3,2,1,0:T(8,128)(2,1)} %param.9), kind=kOutput, calls=%fused_computation.18 | convolution fusion | flops 100663296 | bytes 458752 | tf_op jit(solution)/shard_map/nrs,sk->nkr/dot_general | solution.py:53
  18.2 1.8 %copy.20 = f32[2,256,128]{2,1,0:T(8,128)} copy(f32[2,256,128]{1,2,0:T(8,128)} %convolution_bitcast_fusion.4) | data formatting | bytes 524288 | tf_op jit(solution)/shard_map/nrs,sk->nkr/transpose | solution.py:53
  20.0 1.7 %pad_maximum_fusion.2 = f32[640,128]{1,0:T(8,128)} fusion(f32[512,128]{1,0:T(8,128)} %bitcast.159, f32[128,128]{1,0:T(8,128)} %slice.178), kind=kLoop, calls=%fused_computation.46 | loop fusion | flops 81920 | bytes 655360 | tf_op jit(solution)/shard_map/concatenate | solution.py:58
  21.7 2.6 %collective-permute-start.3 = (f32[640,128]{1,0:T(8,128)}, f32[640,128]{1,0:T(8,128)}, u32[]{:S(2)}, u32[]{:S(2)}) collective-permute-start(f32[640,128]{1,0:T(8,128)} %pad_maximum_fusion.2), channel_id=1, source_target_pairs={{0,2},{2,0},{1,3},{3,1},{4,6},{6,4},{5,7},{7,5},{8,10},{10,8},{9,1... | collective-permute-start | bytes 983048 | tf_op jit(solution)/shard_map/ppermute | solution.py:21
  25.3 1.8 %convolution_add_fusion = f32[3,128,512]{1,2,0:T(8,128)S(1)} fusion(f32[3,128,512]{1,2,0:T(8,128)} %fusion.26, f32[3,256,128]{2,1,0:T(8,128)S(1)} %bitcast.152, bf16[256,1024]{1,0:T(8,128)(2,1)S(1)} %maximum_select_fusion, s32[]{:T(128)S(6)} %select_n.68), kind=kOutput, calls=%fused_computation.3 | convolution fusion | flops 604176384 | bytes 2228228 | tf_op jit(solution)/shard_map/nkr,kt->nrt/dot_general | solution.py:120
  27.1 1.6 %fusion.2 = f32[3,128,512]{1,2,0:T(8,128)S(1)} fusion(f32[3,128,512]{1,2,0:T(8,128)S(1)} %convolution_add_fusion, f32[3,128,512]{1,2,0:T(8,128)} %collective-permute-done.1, bf16[1024,512]{1,0:T(8,128)(2,1)S(1)} %get-tuple-element.29, s32[]{:T(128)S(6)} %select_n.68, bf16[4,512,128]{2,1,0:T(8,128)(2,1)S(1)} %copy-done.2), kind=kOutput, calls=%fused_computation.7 | convolution fusion | flops 201719808 | bytes 3276804 | tf_op jit(solution)/shard_map/lir,it->lrt/dot_general | solution.py:73
  29.1 3.8 %collective-permute-done.3 = f32[640,128]{1,0:T(8,128)} collective-permute-done((f32[640,128]{1,0:T(8,128)}, f32[640,128]{1,0:T(8,128)}, u32[]{:S(2)}, u32[]{:S(2)}) %collective-permute-start.3) | collective-permute-done | bytes 327712 | tf_op jit(solution)/shard_map/ppermute | solution.py:21
  33.9 1.8 %collective-permute-start.4 = (bf16[512,256]{0,1:T(8,128)(2,1)S(1)}, bf16[512,256]{0,1:T(8,128)(2,1)S(1)}, u32[]{:S(2)}, u32[]{:S(2)}) collective-permute-start(bf16[512,256]{0,1:T(8,128)(2,1)S(1)} %pad_maximum_fusion.3), channel_id=1, source_target_pairs={{0,2},{2,0},{1,3},{3,1},{4,6},{6,4},{5,7},{7,5},{8,10},{10,8},{9,1... | collective-permute-start | bytes 786440 | tf_op jit(solution)/shard_map/ppermute | solution.py:21
  35.7 1.7 %convolution_bitcast_fusion.5 = f32[256,128]{0,1:T(8,128)} fusion(bf16[4,1,128,256]{3,2,1,0:T(8,128)(2,1)S(1)} %copy-done.8, f32[640,128]{1,0:T(8,128)} %collective-permute-done.3, f32[384,128]{1,0:T(8,128)S(1)} %copy-done.6), kind=kOutput, calls=%fused_computation.20 | convolution fusion | flops 50348032 | bytes 327680 | tf_op jit(solution)/shard_map/nrs,sk->nkr/dot_general | solution.py:53
  37.4 1.6 %collective-permute-start.5 = (f32[256,128]{0,1:T(8,128)}, f32[256,128]{0,1:T(8,128)}, u32[]{:S(2)}, u32[]{:S(2)}) collective-permute-start(f32[256,128]{0,1:T(8,128)} %convolution_bitcast_fusion.5), channel_id=1, source_target_pairs={{0,4},{4,0},{8,12},{12,8},{1,5},{5,1},{9,13},{13,9},{2,6},{6,2},{1... | collective-permute-start | bytes 393224 | tf_op jit(solution)/shard_map/ppermute | solution.py:21
  38.9 3.1 %collective-permute-done.4 = bf16[512,256]{0,1:T(8,128)(2,1)S(1)} collective-permute-done((bf16[512,256]{0,1:T(8,128)(2,1)S(1)}, bf16[512,256]{0,1:T(8,128)(2,1)S(1)}, u32[]{:S(2)}, u32[]{:S(2)}) %collective-permute-start.4) | collective-permute-done | bytes 262176 | tf_op jit(solution)/shard_map/ppermute | solution.py:21
  44.9 1.7 %collective-permute-start.6 = (bf16[384,128]{0,1:T(8,128)(2,1)S(1)}, bf16[384,128]{0,1:T(8,128)(2,1)S(1)}, u32[]{:S(2)}, u32[]{:S(2)}) collective-permute-start(bf16[384,128]{0,1:T(8,128)(2,1)S(1)} %pad_maximum_fusion.5), channel_id=1, source_target_pairs={{0,4},{4,0},{8,12},{12,8},{1,5},{5,1},{9,13},{13,9},{2,6},{6,2},{1... | collective-permute-start | bytes 294920 | tf_op jit(solution)/shard_map/ppermute | solution.py:21
  46.6 3.0 %collective-permute-done.6 = bf16[384,128]{0,1:T(8,128)(2,1)S(1)} collective-permute-done((bf16[384,128]{0,1:T(8,128)(2,1)S(1)}, bf16[384,128]{0,1:T(8,128)(2,1)S(1)}, u32[]{:S(2)}, u32[]{:S(2)}) %collective-permute-start.6) | collective-permute-done | bytes 98336 | tf_op jit(solution)/shard_map/ppermute | solution.py:21
  52.9 2.7 %collective-permute-start.7 = (bf16[256,64]{0,1:T(8,128)(2,1)S(1)}, bf16[256,64]{0,1:T(8,128)(2,1)S(1)}, u32[]{:S(2)}, u32[]{:S(2)}) collective-permute-start(bf16[256,64]{0,1:T(8,128)(2,1)S(1)} %pad_maximum_fusion.6), channel_id=1, source_target_pairs={{0,8},{4,12},{8,0},{12,4},{1,9},{5,13},{9,1},{13,5},{2,10},{6,14},... | collective-permute-start | bytes 98312 | tf_op jit(solution)/shard_map/ppermute | solution.py:21
  55.6 2.2 %collective-permute-done.7 = bf16[256,64]{0,1:T(8,128)(2,1)S(1)} collective-permute-done((bf16[256,64]{0,1:T(8,128)(2,1)S(1)}, bf16[256,64]{0,1:T(8,128)(2,1)S(1)}, u32[]{:S(2)}, u32[]{:S(2)}) %collective-permute-start.7) | collective-permute-done | bytes 32800 | tf_op jit(solution)/shard_map/ppermute | solution.py:21
  58.8 1.7 %collective-permute-start.8 = (bf16[1,128,128]{1,2,0:T(8,128)(2,1)S(1)}, bf16[1,128,128]{1,2,0:T(8,128)(2,1)S(1)}, u32[]{:S(2)}, u32[]{:S(2)}) collective-permute-start(bf16[1,128,128]{1,2,0:T(8,128)(2,1)S(1)} %fusion.5), channel_id=1, source_target_pairs={{0,4},{4,0},{8,12},{12,8},{1,5},{5,1},{9,13},{13,9},{2,6},{6,2},{1... | collective-permute-start | bytes 98312 | tf_op jit(solution)/shard_map/ppermute | solution.py:21
  60.5 2.3 %collective-permute-done.8 = bf16[1,128,128]{1,2,0:T(8,128)(2,1)S(1)} collective-permute-done((bf16[1,128,128]{1,2,0:T(8,128)(2,1)S(1)}, bf16[1,128,128]{1,2,0:T(8,128)(2,1)S(1)}, u32[]{:S(2)}, u32[]{:S(2)}) %collective-permute-start.8) | collective-permute-done | bytes 32800 | tf_op jit(solution)/shard_map/ppermute | solution.py:21
  63.1 1.6 %collective-permute-start.9 = (bf16[2,128,256]{1,2,0:T(8,128)(2,1)S(1)}, bf16[2,128,256]{1,2,0:T(8,128)(2,1)S(1)}, u32[]{:S(2)}, u32[]{:S(2)}) collective-permute-start(bf16[2,128,256]{1,2,0:T(8,128)(2,1)S(1)} %pad_maximum_fusion.4), channel_id=1, source_target_pairs={{0,2},{2,0},{1,3},{3,1},{4,6},{6,4},{5,7},{7,5},{8,10},{10,8},{9,1... | collective-permute-start | bytes 393224 | tf_op jit(solution)/shard_map/ppermute | solution.py:21
  64.7 3.4 %collective-permute-done.9 = bf16[2,128,256]{1,2,0:T(8,128)(2,1)S(1)} collective-permute-done((bf16[2,128,256]{1,2,0:T(8,128)(2,1)S(1)}, bf16[2,128,256]{1,2,0:T(8,128)(2,1)S(1)}, u32[]{:S(2)}, u32[]{:S(2)}) %collective-permute-start.9) | collective-permute-done | bytes 131104 | tf_op jit(solution)/shard_map/ppermute | solution.py:21
  74.0 1.3 %copy.27 = bf16[512,1024]{1,0:T(8,128)(2,1)} copy(bf16[512,1024]{0,1:T(8,128)(2,1)S(1)} %fusion) | data formatting | bytes 2097152 | tf_op jit(solution)/shard_map/sub | solution.py:135
  (82 shorter events, 24.3 us)
Async XLA Ops:
  0.0 5.0 %copy-start = (bf16[512,1024]{1,0:T(8,128)(2,1)S(1)}, bf16[512,1024]{1,0:T(8,128)(2,1)}, u32[]{:S(2)}) copy-start(bf16[512,1024]{1,0:T(8,128)(2,1)} %param.5) | copy-start | bytes 3145732
  0.0 5.0 %copy-start.9 = (bf16[512,512]{1,0:T(8,128)(2,1)S(1)}, bf16[512,512]{1,0:T(8,128)(2,1)}, u32[]{:S(2)}) copy-start(bf16[512,512]{1,0:T(8,128)(2,1)} %param.6) | copy-start | bytes 1572868
  1.8 1.0 %copy-start.3 = (f32[4,4,128,128]{3,2,0,1:T(8,128)}, f32[4,4,128,128]{3,2,0,1:T(8,128)S(1)}, u32[]{:S(2)}) copy-start(f32[4,4,128,128]{3,2,0,1:T(8,128)S(1)} %convolution_bitcast_fusion) | copy-start | bytes 3145732
  1.8 2.3 %copy-start.7 = (f32[128,128]{1,0:T(8,128)}, f32[128,128]{1,0:T(8,128)S(1)}, u32[]{:S(2)}) copy-start(f32[128,128]{1,0:T(8,128)S(1)} %slice_bitcast_fusion.9) | copy-start | bytes 196612
  5.0 2.1 %copy-start.2 = (bf16[4,512,128]{2,1,0:T(8,128)(2,1)S(1)}, bf16[4,512,128]{2,1,0:T(8,128)(2,1)}, u32[]{:S(2)}) copy-start(bf16[4,512,128]{2,1,0:T(8,128)(2,1)} %param.7) | copy-start | bytes 1572868
  7.6 2.4 %collective-permute-start = (bf16[128,1024]{1,0:T(8,128)(2,1)S(1)}, bf16[128,1024]{1,0:T(8,128)(2,1)}, u32[]{:S(2)}, u32[]{:S(2)}) collective-permute-start(bf16[128,1024]{1,0:T(8,128)(2,1)S(1)} %fusion.3), channel_id=1, source_target_pairs={{0,1},{1,0},{2,3},{3,2},{4,5},{5,4},{6,7},{7,6},{8,9},{9,8},{10,11... | collective-permute-start | bytes 786440 | tf_op jit(solution)/shard_map/ppermute | solution.py:21
  8.1 6.6 %collective-permute-start.2 = (f32[1152,128]{1,0:T(8,128)}, f32[1152,128]{1,0:T(8,128)}, u32[]{:S(2)}, u32[]{:S(2)}) collective-permute-start(f32[1152,128]{1,0:T(8,128)} %pad_maximum_fusion), channel_id=1, source_target_pairs={{0,1},{1,0},{2,3},{3,2},{4,5},{5,4},{6,7},{7,6},{8,9},{9,8},{10,11... | collective-permute-start | bytes 1769480 | tf_op jit(solution)/shard_map/ppermute | solution.py:21
  9.5 17.6 %collective-permute-start.1 = (f32[3,128,512]{1,2,0:T(8,128)}, f32[3,128,512]{1,2,0:T(8,128)}, u32[]{:S(2)}, u32[]{:S(2)}) collective-permute-start(f32[3,128,512]{1,2,0:T(8,128)} %convolution_bitcast_fusion.1), channel_id=1, source_target_pairs={{0,1},{1,0},{2,3},{3,2},{4,5},{5,4},{6,7},{7,6},{8,9},{9,8},{10,11... | collective-permute-start | bytes 2359304 | tf_op jit(solution)/shard_map/ppermute | solution.py:21
  15.7 0.7 copy-start.5
  21.7 11.2 %collective-permute-start.3 = (f32[640,128]{1,0:T(8,128)}, f32[640,128]{1,0:T(8,128)}, u32[]{:S(2)}, u32[]{:S(2)}) collective-permute-start(f32[640,128]{1,0:T(8,128)} %pad_maximum_fusion.2), channel_id=1, source_target_pairs={{0,2},{2,0},{1,3},{3,1},{4,6},{6,4},{5,7},{7,5},{8,10},{10,8},{9,1... | collective-permute-start | bytes 983048 | tf_op jit(solution)/shard_map/ppermute | solution.py:21
  28.7 7.0 %copy-start.6 = (f32[384,128]{1,0:T(8,128)S(1)}, f32[384,128]{1,0:T(8,128)}, u32[]{:S(2)}) copy-start(f32[384,128]{1,0:T(8,128)} %copy-done.5) | copy-start | bytes 589828
  28.7 7.0 %copy-start.8 = (bf16[4,1,128,256]{3,2,1,0:T(8,128)(2,1)S(1)}, bf16[4,1,128,256]{3,2,1,0:T(8,128)(2,1)}, u32[]{:S(2)}) copy-start(bf16[4,1,128,256]{3,2,1,0:T(8,128)(2,1)} %param.9) | copy-start | bytes 786436
  33.9 8.1 %collective-permute-start.4 = (bf16[512,256]{0,1:T(8,128)(2,1)S(1)}, bf16[512,256]{0,1:T(8,128)(2,1)S(1)}, u32[]{:S(2)}, u32[]{:S(2)}) collective-permute-start(bf16[512,256]{0,1:T(8,128)(2,1)S(1)} %pad_maximum_fusion.3), channel_id=1, source_target_pairs={{0,2},{2,0},{1,3},{3,1},{4,6},{6,4},{5,7},{7,5},{8,10},{10,8},{9,1... | collective-permute-start | bytes 786440 | tf_op jit(solution)/shard_map/ppermute | solution.py:21
  37.4 7.5 %collective-permute-start.5 = (f32[256,128]{0,1:T(8,128)}, f32[256,128]{0,1:T(8,128)}, u32[]{:S(2)}, u32[]{:S(2)}) collective-permute-start(f32[256,128]{0,1:T(8,128)} %convolution_bitcast_fusion.5), channel_id=1, source_target_pairs={{0,4},{4,0},{8,12},{12,8},{1,5},{5,1},{9,13},{13,9},{2,6},{6,2},{1... | collective-permute-start | bytes 393224 | tf_op jit(solution)/shard_map/ppermute | solution.py:21
  42.0 0.7 copy-start.10
  44.8 24.0 %copy-start.4 = (bf16[4,512,128]{2,1,0:T(8,128)(2,1)S(1)}, bf16[4,512,128]{2,1,0:T(8,128)(2,1)}, u32[]{:S(2)}) copy-start(bf16[4,512,128]{2,1,0:T(8,128)(2,1)} %param.8) | copy-start | bytes 1572868
  44.9 4.7 %collective-permute-start.6 = (bf16[384,128]{0,1:T(8,128)(2,1)S(1)}, bf16[384,128]{0,1:T(8,128)(2,1)S(1)}, u32[]{:S(2)}, u32[]{:S(2)}) collective-permute-start(bf16[384,128]{0,1:T(8,128)(2,1)S(1)} %pad_maximum_fusion.5), channel_id=1, source_target_pairs={{0,4},{4,0},{8,12},{12,8},{1,5},{5,1},{9,13},{13,9},{2,6},{6,2},{1... | collective-permute-start | bytes 294920 | tf_op jit(solution)/shard_map/ppermute | solution.py:21
  52.9 4.9 %collective-permute-start.7 = (bf16[256,64]{0,1:T(8,128)(2,1)S(1)}, bf16[256,64]{0,1:T(8,128)(2,1)S(1)}, u32[]{:S(2)}, u32[]{:S(2)}) collective-permute-start(bf16[256,64]{0,1:T(8,128)(2,1)S(1)} %pad_maximum_fusion.6), channel_id=1, source_target_pairs={{0,8},{4,12},{8,0},{12,4},{1,9},{5,13},{9,1},{13,5},{2,10},{6,14},... | collective-permute-start | bytes 98312 | tf_op jit(solution)/shard_map/ppermute | solution.py:21
  58.8 4.0 %collective-permute-start.8 = (bf16[1,128,128]{1,2,0:T(8,128)(2,1)S(1)}, bf16[1,128,128]{1,2,0:T(8,128)(2,1)S(1)}, u32[]{:S(2)}, u32[]{:S(2)}) collective-permute-start(bf16[1,128,128]{1,2,0:T(8,128)(2,1)S(1)} %fusion.5), channel_id=1, source_target_pairs={{0,4},{4,0},{8,12},{12,8},{1,5},{5,1},{9,13},{13,9},{2,6},{6,2},{1... | collective-permute-start | bytes 98312 | tf_op jit(solution)/shard_map/ppermute | solution.py:21
  63.1 5.0 %collective-permute-start.9 = (bf16[2,128,256]{1,2,0:T(8,128)(2,1)S(1)}, bf16[2,128,256]{1,2,0:T(8,128)(2,1)S(1)}, u32[]{:S(2)}, u32[]{:S(2)}) collective-permute-start(bf16[2,128,256]{1,2,0:T(8,128)(2,1)S(1)} %pad_maximum_fusion.4), channel_id=1, source_target_pairs={{0,2},{2,0},{1,3},{3,1},{4,6},{6,4},{5,7},{7,5},{8,10},{10,8},{9,1... | collective-permute-start | bytes 393224 | tf_op jit(solution)/shard_map/ppermute | solution.py:21
  68.8 1.8 %collective-permute-start.10 = (bf16[3,128,512]{1,2,0:T(8,128)(2,1)S(1)}, bf16[3,128,512]{1,2,0:T(8,128)(2,1)S(1)}, u32[]{:S(2)}, u32[]{:S(2)}) collective-permute-start(bf16[3,128,512]{1,2,0:T(8,128)(2,1)S(1)} %pad_maximum_fusion.1), channel_id=1, source_target_pairs={{0,1},{1,0},{2,3},{3,2},{4,5},{5,4},{6,7},{7,6},{8,9},{9,8},{10,11... | collective-permute-start | bytes 1179656 | tf_op jit(solution)/shard_map/ppermute | solution.py:21
  71.8 1.6 %copy-start.1 = (f32[1024,512]{1,0:T(8,128)S(1)}, f32[1024,512]{1,0:T(8,128)}, u32[]{:S(2)}) copy-start(f32[1024,512]{1,0:T(8,128)} %get-tuple-element.30) | copy-start | bytes 6291460

commit v10 on v4

--- a/solution.py
+++ b/solution.py
@@ -114,14 +114,21 @@
             n = rest.shape[0]
             w = mine_b.shape[1] // 2
             parts = [mine_b[:, :w], mine_b[:, w:]]
-            if n > 0:
+            summed = n == 1 and s == levels - 2
+            if summed:
+                last = rest[0].astype(BF16)
+                parts += [last[:, :w], last[:, w:]]
+            elif n > 0:
                 h = side(s, bits)
                 keep = cols(rest, h * w, w)
                 send = cols(rest, (1 - h) * w, w)
                 parts.append(send.astype(BF16).reshape(n * rank, w))
             got = swap(jnp.concatenate(parts, axis=0), s, bits)
             theirs_b = jnp.concatenate([got[:rank], got[rank : 2 * rank]], axis=1)
-            if n > 0:
+            if summed:
+                recv = jnp.concatenate([got[2 * rank : 3 * rank], got[3 * rank :]], axis=1)
+                rest = rest + recv.astype(F32)[None]
+            elif n > 0:
                 recv = got[2 * rank :].reshape(n, rank, w).astype(F32)
                 rest = keep + recv
         stacked = jnp.concatenate([mine_b, theirs_b], axis=0)
@@ -129,7 +136,10 @@
         own_coefs.append(coefs[:rank])
         if s < levels - 1:
             w = coefs.shape[1] // 2
-            piece = cols(coefs, side(s, bits) * w, w).astype(F32)
+            if rest.shape[-1] == coefs.shape[1]:
+                piece = coefs.astype(F32)
+            else:
+                piece = cols(coefs, side(s, bits) * w, w).astype(F32)
             fix = jnp.dot(
                 w_own[s], piece, preferred_element_type=F32,
                 precision=lax.Precision.HIGHEST,
@@ -138,8 +148,13 @@
 
     full = [own_coefs[0]] + [None] * (levels - 1)
     pending = {s: own_coefs[s] for s in range(1, levels)}
+    top = {s: s - 1 for s in range(1, levels)}
+    if levels > 2:
+        top[levels - 1] = levels - 3
     for j in reversed(range(levels - 1)):
-        group = [s for s in range(j + 1, levels)]
+        group = [s for s in range(1, levels) if top[s] >= j]
+        if not group:
+            continue
         joined = gather_half(jnp.stack([pending[s] for s in group]), j, bits)
         for i, s in enumerate(group):
             pending[s] = joined[i]

time: 64.3 us -> 57.8 us (0.90)
  matrix products: 14.4 us -> 11.4 us
  local copies, waits for them, and re-layouts: 8.57 us -> 5.77 us
  waiting for transfers between devices: 17.9 us -> 19.7 us
  starting transfers between devices: 13.3 us -> 11.9 us
  other arithmetic: 8.77 us -> 7.9 us
    ppermute x12 -> x11, waiting for transfers between devices: 17.9 us -> 19.7 us  [swap(): return lax.ppermute(x, axis, [(i, i ^ 1 << stride) for i in range(n)])]
    reshape x4 -> x0, local copies, waits for them, and re-layouts: 1.62 us -> none  [the longest x2 1.51 us: on_device(): rest = rest - fix.reshape(rest.shape)]
    dot_general x1 -> x0, matrix products: 1.61 us -> none  [on_device(): jnp.einsum('lir,it->lrt', v_basis[1:], cols(c0b, h * half, half), preferr...]
    sub x1 -> x2, other arithmetic: 0.04 us -> 1.44 us  [on_device(): rest = rest - fix.reshape(rest.shape)]
    ppermute x12 -> x11, starting transfers between devices: 13.3 us -> 11.9 us  [swap(): return lax.ppermute(x, axis, [(i, i ^ 1 << stride) for i in range(n)])]
    dot_general x2 -> x0, local copies, waits for them, and re-layouts: 1.2 us -> none  [on_device(): jnp.einsum('lir,is->lrs', v_basis[s + 1:], u_basis[s], preferred_element_...]
    dot_general x4, matrix products: 2.88 us -> 2.01 us  [on_device(): coefs = jnp.dot(couple[s], stacked, preferred_element_type=F32).astype(BF16)]
    dot_general x3, matrix products: 1.87 us -> 1.07 us  [on_device(): jnp.dot(w_own[s], piece, preferred_element_type=F32, precision=lax.Precis...]
  transfers between devices with their start and end apart: 12 -> 11, of which waited for: 7 -> 6; matrix products, arithmetic and copies ran while one was open for 36% -> 29% of each run, Pallas kernels for 0% -> 0%
where the time goes in v10:
time: 57.8 us; the launch traced here: 57.3 us
  waiting for transfers between devices  19.7 us (34%)
  starting transfers between devices  11.9 us (21%)
  matrix products  11.4 us (20%)
  other arithmetic  7.9 us (14%)
  local copies, waits for them, and re-layouts  5.77 us (10%)
  between operations  0.61 us (1%)
    ppermute x11, waiting for transfers between devices, swap(): return lax.ppermute(x, axis, [(i, i ^ 1 << stride) for i in range(n)])  19.7 us
    ppermute x11, starting transfers between devices, swap(): return lax.ppermute(x, axis, [(i, i ^ 1 << stride) for i in range(n)])  11.9 us
    dot_general x4, matrix products, on_device(): current = current - jnp.dot(u_basis[s], full[s], preferred_element_type=F32)  2.84 us
    dot_general x1, matrix products, on_device(): c0 = jnp.dot(leaf_inverse, templates, preferred_element_type=F32)  2.05 us
    dot_general x4, matrix products, on_device(): coefs = jnp.dot(couple[s], stacked, preferred_element_type=F32).astype(BF16)  2.01 us
    concatenate x2, other arithmetic, gather_half(): both = jnp.concatenate([x, swap(x, bit, bits), x], axis=-1)  1.79 us
    add x3, other arithmetic, on_device(): partial[s] = partial[s] + recv  1.78 us
    squeeze x1, local copies, waits for them, and re-layouts, on_device(): mine, theirs = (mine_c[s], theirs_c[s])  1.76 us
  transfers between devices with their start and end apart: 11, of which 6 were waited for; matrix products, arithmetic and copies ran while one was open for 29% of the time, Pallas kernels for 0%

profile of v10, /device:TPU:0, one launch (start us, length us, event | category | flops | bytes accessed | tf_op | source)
XLA Modules:
  0.0 57.3 jit_solution(9422060588810820043)
XLA Ops:
  0.0 1.8 %slice_bitcast_fusion.8 = (bf16[128,256]{1,0:T(8,128)(2,1)S(1)}, bf16[128,256]{1,0:T(8,128)(2,1)}, bf16[128,256]{1,0:T(8,128)(2,1)}, bf16[128,256]{1,0:T(8,128)(2,1)S(1)}) fusion(bf16[4,1,128,256]{3,2,1,0:T(8,128)(2,1)} %param.9), kind=kLoop, calls=%fused_computation.150 | loop fusion | bytes 524288 | tf_op jit(solution)/shard_map/squeeze | solution.py:82
  2.5 4.0 %collective-permute-start.7 = (bf16[256,128]{1,0:T(8,128)(2,1)}, bf16[256,128]{1,0:T(8,128)(2,1)}, u32[]{:S(2)}, u32[]{:S(2)}) collective-permute-start(bf16[256,128]{1,0:T(8,128)(2,1)} %fusion.88), channel_id=1, source_target_pairs={{0,8},{4,12},{8,0},{12,4},{1,9},{5,13},{9,1},{13,5},{2,10},{6,14},... | collective-permute-start | bytes 196616 | tf_op jit(solution)/shard_map/ppermute | solution.py:21
  8.5 0.8 %pad_maximum_fusion = f32[1024,128]{1,0:T(8,128)} fusion(f32[128,128]{1,0:T(8,128)S(1)} %fusion.69, f32[256,128]{1,0:T(8,128)S(1)} %fusion.73, f32[384,128]{1,0:T(8,128)S(1)} %fusion.76, f32[256,128]{1,0:T(8,128)S(1)} %fusion.91), kind=kLoop, calls=%fused_computation.25 | loop fusion | flops 393216 | bytes 1048576 | tf_op jit(solution)/shard_map/concatenate | solution.py:67
  9.4 2.1 %fusion.121 = (bf16[512,1024]{1,0:T(8,128)(2,1)S(1)}, f32[512,1024]{1,0:T(8,128)}) fusion(bf16[512,512]{1,0:T(8,128)(2,1)S(1)} %copy-done.5, bf16[512,1024]{1,0:T(8,128)(2,1)S(1)} %copy-done), kind=kOutput, calls=%fused_computation.190 | convolution fusion | flops 537395200 | bytes 4718592 | tf_op jit(solution)/shard_map/dot_general | solution.py:52
  11.4 1.1 %fusion.1 = bf16[128,1024]{1,0:T(8,128)(2,1)} fusion(bf16[512,1024]{1,0:T(8,128)(2,1)S(1)} %get-tuple-element.51, bf16[4,512,128]{2,1,0:T(8,128)(2,1)S(1)} %copy-done.2), kind=kOutput, calls=%fused_computation.14 | convolution fusion | flops 134348800 | bytes 1441792 | tf_op jit(solution)/shard_map/dot_general | solution.py:92
  13.0 1.3 %convolution_bitcast_fusion = f32[3,128,512]{2,1,0:T(8,128)} fusion(bf16[512,1024]{1,0:T(8,128)(2,1)S(1)} %get-tuple-element.51, s32[]{:T(128)S(6)} %select_n.69, bf16[4,512,128]{2,1,0:T(8,128)(2,1)S(1)} %copy-done.2), kind=kOutput, calls=%fused_computation.5 | convolution fusion | flops 201326592 | bytes 1703940 | tf_op jit(solution)/shard_map/lir,it->lrt/dot_general | solution.py:101
  15.6 0.9 %slice_add_fusion = f32[256,128]{1,0:T(8,128)S(1)} fusion(f32[256,128]{1,0:T(8,128)S(1)} %fusion.73, f32[1024,128]{1,0:T(8,128)} %collective-permute-done), kind=kLoop, calls=%fused_computation.75 | loop fusion | flops 32768 | bytes 393216 | tf_op jit(solution)/shard_map/add | solution.py:78
  16.5 0.8 %slice_add_fusion.2 = f32[128,128]{1,0:T(8,128)S(1)} fusion(f32[128,128]{1,0:T(8,128)S(1)} %fusion.69, f32[1024,128]{1,0:T(8,128)} %collective-permute-done), kind=kLoop, calls=%fused_computation.144 | loop fusion | flops 16384 | bytes 196608 | tf_op jit(solution)/shard_map/add | solution.py:78
  17.4 1.6 %collective-permute-start.2 = (f32[640,128]{1,0:T(8,128)S(1)}, f32[640,128]{1,0:T(8,128)S(1)}, u32[]{:S(2)}, u32[]{:S(2)}) collective-permute-start(f32[640,128]{1,0:T(8,128)S(1)} %pad_maximum_fusion.2), channel_id=1, source_target_pairs={{0,2},{2,0},{1,3},{3,1},{4,6},{6,4},{5,7},{7,5},{8,10},{10,8},{9,1... | collective-permute-start | bytes 983048 | tf_op jit(solution)/shard_map/ppermute | solution.py:21
  18.9 0.9 %slice.297 = f32[384,128]{1,0:T(8,128)S(1)} slice(f32[1024,128]{1,0:T(8,128)} %collective-permute-done), slice={[256:640], [0:128]} | slice | bytes 393216 | tf_op jit(solution)/shard_map/slice | solution.py:73
  19.9 1.1 %convert.16 = bf16[1024,128]{1,0:T(8,128)(2,1)S(1)} convert(f32[1024,128]{1,0:T(8,128)} %collective-permute-done) | non-fusion elementwise | flops 131072 | bytes 786432 | tf_op jit(solution)/shard_map/convert.5
  21.0 1.3 %convolution_convert_fusion = bf16[256,1024]{1,0:T(8,128)(2,1)S(1)} fusion(bf16[128,1024]{1,0:T(8,128)(2,1)} %collective-permute-done.1, bf16[128,1024]{1,0:T(8,128)(2,1)} %fusion.1, bf16[256,128]{1,0:T(8,128)(2,1)S(1)} %get-tuple-element.30, bf16[256,128]{1,0:T(8,128)(2,1)S(1)} %get-tuple-element.29), kind=kOutput, calls=%fused_computation.6 | convolution fusion | flops 135790592 | bytes 1179648 | tf_op jit(solution)/shard_map/dot_general | solution.py:135
  22.9 1.4 %add_subtract_fusion = f32[3,128,512]{2,1,0:T(8,128)S(1)} fusion(f32[3,128,512]{2,1,0:T(8,128)S(1)} %bitcast.117, f32[3,128,512]{2,1,0:T(8,128)S(1)} %bitcast.116, f32[3,128,512]{2,1,0:T(8,128)} %collective-permute-done.3), kind=kLoop, calls=%fused_computation.24 | loop fusion | flops 393216 | bytes 3145728 | tf_op jit(solution)/shard_map/sub | solution.py:147
  25.0 2.7 %collective-permute-done.2 = f32[640,128]{1,0:T(8,128)S(1)} collective-permute-done((f32[640,128]{1,0:T(8,128)S(1)}, f32[640,128]{1,0:T(8,128)S(1)}, u32[]{:S(2)}, u32[]{:S(2)}) %collective-permute-start.2) | collective-permute-done | bytes 327712 | tf_op jit(solution)/shard_map/ppermute | solution.py:21
  27.8 1.6 %collective-permute-start.5 = (f32[384,128]{1,0:T(8,128)S(1)}, f32[384,128]{1,0:T(8,128)S(1)}, u32[]{:S(2)}, u32[]{:S(2)}) collective-permute-start(f32[384,128]{1,0:T(8,128)S(1)} %pad_maximum_fusion.4), channel_id=1, source_target_pairs={{0,4},{4,0},{8,12},{12,8},{1,5},{5,1},{9,13},{13,9},{2,6},{6,2},{1... | collective-permute-start | bytes 589832 | tf_op jit(solution)/shard_map/ppermute | solution.py:21
  29.5 3.7 %collective-permute-done.4 = bf16[512,256]{1,0:T(8,128)(2,1)S(1)} collective-permute-done((bf16[512,256]{1,0:T(8,128)(2,1)S(1)}, bf16[512,256]{1,0:T(8,128)(2,1)S(1)}, u32[]{:S(2)}, u32[]{:S(2)}) %collective-permute-start.4) | collective-permute-done | bytes 262176 | tf_op jit(solution)/shard_map/ppermute | solution.py:21
  33.9 1.6 %collective-permute-start.6 = (bf16[512,128]{1,0:T(8,128)(2,1)S(1)}, bf16[512,128]{1,0:T(8,128)(2,1)S(1)}, u32[]{:S(2)}, u32[]{:S(2)}) collective-permute-start(bf16[512,128]{1,0:T(8,128)(2,1)S(1)} %pad_maximum_fusion.5), channel_id=1, source_target_pairs={{0,4},{4,0},{8,12},{12,8},{1,5},{5,1},{9,13},{13,9},{2,6},{6,2},{1... | collective-permute-start | bytes 393224 | tf_op jit(solution)/shard_map/ppermute | solution.py:21
  35.6 3.4 %collective-permute-done.6 = bf16[512,128]{1,0:T(8,128)(2,1)S(1)} collective-permute-done((bf16[512,128]{1,0:T(8,128)(2,1)S(1)}, bf16[512,128]{1,0:T(8,128)(2,1)S(1)}, u32[]{:S(2)}, u32[]{:S(2)}) %collective-permute-start.6) | collective-permute-done | bytes 131104 | tf_op jit(solution)/shard_map/ppermute | solution.py:21
  39.8 5.0 %collective-permute-done.8 = bf16[256,128]{1,0:T(8,128)(2,1)S(1)} collective-permute-done((bf16[256,128]{1,0:T(8,128)(2,1)S(1)}, bf16[256,128]{1,0:T(8,128)(2,1)S(1)}, u32[]{:S(2)}, u32[]{:S(2)}) %collective-permute-start.8) | collective-permute-done | bytes 65568 | tf_op jit(solution)/shard_map/ppermute | solution.py:21
  45.1 1.6 %collective-permute-start.9 = (bf16[2,128,256]{1,2,0:T(8,128)(2,1)S(1)}, bf16[2,128,256]{1,2,0:T(8,128)(2,1)S(1)}, u32[]{:S(2)}, u32[]{:S(2)}) collective-permute-start(bf16[2,128,256]{1,2,0:T(8,128)(2,1)S(1)} %pad_maximum_fusion.6), channel_id=1, source_target_pairs={{0,2},{2,0},{1,3},{3,1},{4,6},{6,4},{5,7},{7,5},{8,10},{10,8},{9,1... | collective-permute-start | bytes 393224 | tf_op jit(solution)/shard_map/ppermute | solution.py:21
  46.8 3.3 %collective-permute-done.9 = bf16[2,128,256]{1,2,0:T(8,128)(2,1)S(1)} collective-permute-done((bf16[2,128,256]{1,2,0:T(8,128)(2,1)S(1)}, bf16[2,128,256]{1,2,0:T(8,128)(2,1)S(1)}, u32[]{:S(2)}, u32[]{:S(2)}) %collective-permute-start.9) | collective-permute-done | bytes 131104 | tf_op jit(solution)/shard_map/ppermute | solution.py:21
  50.8 1.7 %collective-permute-done.10 = bf16[3,128,512]{1,2,0:T(8,128)(2,1)S(1)} collective-permute-done((bf16[3,128,512]{1,2,0:T(8,128)(2,1)S(1)}, bf16[3,128,512]{1,2,0:T(8,128)(2,1)S(1)}, u32[]{:S(2)}, u32[]{:S(2)}) %collective-permute-start.10) | collective-permute-done | bytes 393248 | tf_op jit(solution)/shard_map/ppermute | solution.py:21
  52.5 1.2 %fusion.7 = bf16[3,128,1024]{1,2,0:T(8,128)(2,1)S(1)} fusion(s32[]{:T(128)S(6)} %select_n.79, bf16[1,128,512]{1,2,0:T(8,128)(2,1)S(1)} %copy.21, bf16[2,128,512]{1,2,0:T(8,128)(2,1)S(1)} %fusion.22, bf16[3,128,512]{1,2,0:T(8,128)(2,1)S(1)} %collective-permute-done.10), kind=kLoop, calls=%fused_computation.22 | loop fusion | flops 3932160 | bytes 1572868 | tf_op jit(solution)/shard_map/concatenate | solution.py:44
  55.8 1.5 %fusion = bf16[512,1024]{1,0:T(8,128)(2,1)} fusion(f32[1024,512]{0,1:T(8,128)S(1)} %fusion.24, f32[1024,512]{0,1:T(8,128)S(1)} %fusion.25, f32[1024,512]{0,1:T(8,128)S(1)} %fusion.26, f32[512,1024]{1,0:T(8,128)S(1)} %copy-done.1, bf16[256,1024]{1,0:T(8,128)(2,1)S(1)} %convolution_convert_fusion, bf16[4,512,128]{2,1,0:T(8,128)(2,1)S(1)} %copy-done.4), kind=kOutput, calls=%fused_computation.1 | convolution fusion | flops 136839168 | bytes 9830400 | tf_op jit(solution)/shard_map/dot_general | solution.py:165
  (102 shorter events, 10.2 us)
Async XLA Ops:
  0.0 9.4 %copy-start = (bf16[512,1024]{1,0:T(8,128)(2,1)S(1)}, bf16[512,1024]{1,0:T(8,128)(2,1)}, u32[]{:S(2)}) copy-start(bf16[512,1024]{1,0:T(8,128)(2,1)} %param.5) | copy-start | bytes 3145732
  0.0 6.5 %copy-start.2 = (bf16[4,512,128]{2,1,0:T(8,128)(2,1)S(1)}, bf16[4,512,128]{2,1,0:T(8,128)(2,1)}, u32[]{:S(2)}) copy-start(bf16[4,512,128]{2,1,0:T(8,128)(2,1)} %param.7) | copy-start | bytes 1572868
  0.0 6.8 %slice-start = ((bf16[4,512,128]{2,1,0:T(8,128)(2,1)}), bf16[2,512,128]{2,1,0:T(8,128)(2,1)S(1)}, s32[]{:S(2)}) async-start(bf16[4,512,128]{2,1,0:T(8,128)(2,1)} %param.7), calls=%async_computation | async-start | bytes 524288 | tf_op jit(solution)/shard_map/slice | solution.py:58
  0.0 7.2 %slice-start.1 = ((bf16[4,512,128]{2,1,0:T(8,128)(2,1)}), bf16[3,512,128]{2,1,0:T(8,128)(2,1)S(1)}, s32[]{:S(2)}) async-start(bf16[4,512,128]{2,1,0:T(8,128)(2,1)} %param.7), calls=%async_computation.1 | async-start | bytes 786432
  0.0 6.5 %copy-start.3 = (bf16[4,512,128]{2,1,0:T(8,128)(2,1)S(1)}, bf16[4,512,128]{2,1,0:T(8,128)(2,1)}, u32[]{:S(2)}) copy-start(bf16[4,512,128]{2,1,0:T(8,128)(2,1)} %param.8) | copy-start | bytes 1572868
  1.8 5.1 %copy-start.10 = (bf16[128,128]{1,0:T(8,128)(2,1)}, bf16[128,128]{1,0:T(8,128)(2,1)S(1)}, u32[]{:S(2)}) copy-start(bf16[128,128]{1,0:T(8,128)(2,1)S(1)} %get-tuple-element.39) | copy-start | bytes 98308
  1.8 5.1 %copy-start.12 = (bf16[128,128]{1,0:T(8,128)(2,1)}, bf16[128,128]{1,0:T(8,128)(2,1)S(1)}, u32[]{:S(2)}) copy-start(bf16[128,128]{1,0:T(8,128)(2,1)S(1)} %get-tuple-element.40) | copy-start | bytes 98308
  2.5 12.3 %collective-permute-start.7 = (bf16[256,128]{1,0:T(8,128)(2,1)}, bf16[256,128]{1,0:T(8,128)(2,1)}, u32[]{:S(2)}, u32[]{:S(2)}) collective-permute-start(bf16[256,128]{1,0:T(8,128)(2,1)} %fusion.88), channel_id=1, source_target_pairs={{0,8},{4,12},{8,0},{12,4},{1,9},{5,13},{9,1},{13,5},{2,10},{6,14},... | collective-permute-start | bytes 196616 | tf_op jit(solution)/shard_map/ppermute | solution.py:21
  7.4 2.0 %copy-start.5 = (bf16[512,512]{1,0:T(8,128)(2,1)S(1)}, bf16[512,512]{1,0:T(8,128)(2,1)}, u32[]{:S(2)}) copy-start(bf16[512,512]{1,0:T(8,128)(2,1)} %param.6) | copy-start | bytes 1572868
  9.3 6.2 %collective-permute-start = (f32[1024,128]{1,0:T(8,128)}, f32[1024,128]{1,0:T(8,128)}, u32[]{:S(2)}, u32[]{:S(2)}) collective-permute-start(f32[1024,128]{1,0:T(8,128)} %pad_maximum_fusion), channel_id=1, source_target_pairs={{0,1},{1,0},{2,3},{3,2},{4,5},{5,4},{6,7},{7,6},{8,9},{9,8},{10,11... | collective-permute-start | bytes 1572872 | tf_op jit(solution)/shard_map/ppermute | solution.py:21
  12.5 8.6 %collective-permute-start.1 = (bf16[128,1024]{1,0:T(8,128)(2,1)}, bf16[128,1024]{1,0:T(8,128)(2,1)}, u32[]{:S(2)}, u32[]{:S(2)}) collective-permute-start(bf16[128,1024]{1,0:T(8,128)(2,1)} %fusion.1), channel_id=1, source_target_pairs={{0,1},{1,0},{2,3},{3,2},{4,5},{5,4},{6,7},{7,6},{8,9},{9,8},{10,11... | collective-permute-start | bytes 786440 | tf_op jit(solution)/shard_map/ppermute | solution.py:21
  14.3 1.3 %copy-start.13 = (bf16[128,128]{1,0:T(8,128)(2,1)S(1)}, bf16[128,128]{1,0:T(8,128)(2,1)}, u32[]{:S(2)}) copy-start(bf16[128,128]{1,0:T(8,128)(2,1)} %copy-done.12) | copy-start | bytes 98308
  14.3 8.6 %collective-permute-start.3 = (f32[3,128,512]{2,1,0:T(8,128)}, f32[3,128,512]{2,1,0:T(8,128)}, u32[]{:S(2)}, u32[]{:S(2)}) collective-permute-start(f32[3,128,512]{2,1,0:T(8,128)} %convolution_bitcast_fusion), channel_id=1, source_target_pairs={{0,1},{1,0},{2,3},{3,2},{4,5},{5,4},{6,7},{7,6},{8,9},{9,8},{10,11... | collective-permute-start | bytes 2359304 | tf_op jit(solution)/shard_map/ppermute | solution.py:21
  14.7 6.3 %copy-start.7 = (bf16[128,128]{1,0:T(8,128)(2,1)S(1)}, bf16[128,128]{1,0:T(8,128)(2,1)}, u32[]{:S(2)}) copy-start(bf16[128,128]{1,0:T(8,128)(2,1)} %copy-done.6) | copy-start | bytes 98308
  14.7 6.3 %copy-start.9 = (bf16[128,128]{1,0:T(8,128)(2,1)S(1)}, bf16[128,128]{1,0:T(8,128)(2,1)}, u32[]{:S(2)}) copy-start(bf16[128,128]{1,0:T(8,128)(2,1)} %copy-done.8) | copy-start | bytes 98308
  17.4 10.4 %collective-permute-start.2 = (f32[640,128]{1,0:T(8,128)S(1)}, f32[640,128]{1,0:T(8,128)S(1)}, u32[]{:S(2)}, u32[]{:S(2)}) collective-permute-start(f32[640,128]{1,0:T(8,128)S(1)} %pad_maximum_fusion.2), channel_id=1, source_target_pairs={{0,2},{2,0},{1,3},{3,1},{4,6},{6,4},{5,7},{7,5},{8,10},{10,8},{9,1... | collective-permute-start | bytes 983048 | tf_op jit(solution)/shard_map/ppermute | solution.py:21
  24.4 8.7 %collective-permute-start.4 = (bf16[512,256]{1,0:T(8,128)(2,1)S(1)}, bf16[512,256]{1,0:T(8,128)(2,1)S(1)}, u32[]{:S(2)}, u32[]{:S(2)}) collective-permute-start(bf16[512,256]{1,0:T(8,128)(2,1)S(1)} %pad_maximum_fusion.3), channel_id=1, source_target_pairs={{0,2},{2,0},{1,3},{3,1},{4,6},{6,4},{5,7},{7,5},{8,10},{10,8},{9,1... | collective-permute-start | bytes 786440 | tf_op jit(solution)/shard_map/ppermute | solution.py:21
  27.8 7.7 %collective-permute-start.5 = (f32[384,128]{1,0:T(8,128)S(1)}, f32[384,128]{1,0:T(8,128)S(1)}, u32[]{:S(2)}, u32[]{:S(2)}) collective-permute-start(f32[384,128]{1,0:T(8,128)S(1)} %pad_maximum_fusion.4), channel_id=1, source_target_pairs={{0,4},{4,0},{8,12},{12,8},{1,5},{5,1},{9,13},{13,9},{2,6},{6,2},{1... | collective-permute-start | bytes 589832 | tf_op jit(solution)/shard_map/ppermute | solution.py:21
  33.9 5.1 %collective-permute-start.6 = (bf16[512,128]{1,0:T(8,128)(2,1)S(1)}, bf16[512,128]{1,0:T(8,128)(2,1)S(1)}, u32[]{:S(2)}, u32[]{:S(2)}) collective-permute-start(bf16[512,128]{1,0:T(8,128)(2,1)S(1)} %pad_maximum_fusion.5), channel_id=1, source_target_pairs={{0,4},{4,0},{8,12},{12,8},{1,5},{5,1},{9,13},{13,9},{2,6},{6,2},{1... | collective-permute-start | bytes 393224 | tf_op jit(solution)/shard_map/ppermute | solution.py:21
  39.6 5.2 %collective-permute-start.8 = (bf16[256,128]{1,0:T(8,128)(2,1)S(1)}, bf16[256,128]{1,0:T(8,128)(2,1)S(1)}, u32[]{:S(2)}, u32[]{:S(2)}) collective-permute-start(bf16[256,128]{1,0:T(8,128)(2,1)S(1)} %pad_maximum_fusion.19), channel_id=1, source_target_pairs={{0,8},{4,12},{8,0},{12,4},{1,9},{5,13},{9,1},{13,5},{2,10},{6,14},... | collective-permute-start | bytes 196616 | tf_op jit(solution)/shard_map/ppermute | solution.py:21
  44.8 9.0 %copy-start.4 = (bf16[4,512,128]{2,1,0:T(8,128)(2,1)S(1)}, bf16[4,512,128]{2,1,0:T(8,128)(2,1)}, u32[]{:S(2)}) copy-start(bf16[4,512,128]{2,1,0:T(8,128)(2,1)} %param.8) | copy-start | bytes 1572868
  45.1 5.0 %collective-permute-start.9 = (bf16[2,128,256]{1,2,0:T(8,128)(2,1)S(1)}, bf16[2,128,256]{1,2,0:T(8,128)(2,1)S(1)}, u32[]{:S(2)}, u32[]{:S(2)}) collective-permute-start(bf16[2,128,256]{1,2,0:T(8,128)(2,1)S(1)} %pad_maximum_fusion.6), channel_id=1, source_target_pairs={{0,2},{2,0},{1,3},{3,1},{4,6},{6,4},{5,7},{7,5},{8,10},{10,8},{9,1... | collective-permute-start | bytes 393224 | tf_op jit(solution)/shard_map/ppermute | solution.py:21
  50.8 1.8 %collective-permute-start.10 = (bf16[3,128,512]{1,2,0:T(8,128)(2,1)S(1)}, bf16[3,128,512]{1,2,0:T(8,128)(2,1)S(1)}, u32[]{:S(2)}, u32[]{:S(2)}) collective-permute-start(bf16[3,128,512]{1,2,0:T(8,128)(2,1)S(1)} %pad_maximum_fusion.1), channel_id=1, source_target_pairs={{0,1},{1,0},{2,3},{3,2},{4,5},{5,4},{6,7},{7,6},{8,9},{9,8},{10,11... | collective-permute-start | bytes 1179656 | tf_op jit(solution)/shard_map/ppermute | solution.py:21
  54.2 1.6 %copy-start.1 = (f32[512,1024]{1,0:T(8,128)S(1)}, f32[512,1024]{1,0:T(8,128)}, u32[]{:S(2)}) copy-start(f32[512,1024]{1,0:T(8,128)} %get-tuple-element.52) | copy-start | bytes 6291460
  (3 other events, 3.0 us)

commit v11 on v7

--- a/solution.py
+++ b/solution.py
@@ -30,6 +30,14 @@
     return lax.dynamic_slice_in_dim(x, start, width, axis=x.ndim - 1)
 
 
+def reduce_half(x, bit, bits):
+    w = x.shape[-1] // 2
+    h = side(bit, bits)
+    keep = cols(x, h * w, w)
+    send = cols(x, (1 - h) * w, w)
+    return keep + swap(send, bit, bits)
+
+
 def gather_half(x, bit, bits):
     w = x.shape[-1]
     h = side(bit, bits)
@@ -41,23 +49,25 @@
     bits = bit_axes()
     levels, pixels, rank = v_basis.shape
     width = templates.shape[1]
-    c0 = jnp.dot(leaf_inverse, templates, preferred_element_type=F32)
-    c0b = c0.astype(BF16)
-
     cross = jnp.einsum("kis,lir->klrs", u_basis, v_basis, preferred_element_type=F32)
     counts = [levels - 1 - k for k in range(levels - 1)]
     suffix = jnp.concatenate(
         [cross[k, k + 1 :].reshape(-1, rank) for k in range(levels - 1)], axis=0
     )
-    w_own, w_sib = [None] * levels, [None] * levels
+    w_own, w_sib, sent = [None] * levels, [None] * levels, [None] * levels
     for b in range(levels - 1):
         n = counts[b] * rank
+        if b == 0:
+            suffix, templates = lax.optimization_barrier((suffix, templates))
+        sent[b] = suffix
         got = swap(suffix, b, bits)
         w_own[b] = suffix[:n].reshape(counts[b], rank, rank)
         w_sib[b] = got[:n].reshape(counts[b], rank, rank)
         suffix = suffix[n:] + got[n:]
     couple_sib = [swap(coupling[s, 0], s, bits) for s in range(levels)]
 
+    c0 = jnp.dot(leaf_inverse, templates, preferred_element_type=F32)
+    c0b = c0.astype(BF16)
     proj0 = jnp.dot(v_basis[0].T, c0b, preferred_element_type=F32)
     rest = None
     if levels > 1:
@@ -83,7 +93,11 @@
             n = rest.shape[0]
             w = mine_b.shape[1] // 2
             parts = [mine_b[:, :w], mine_b[:, w:]]
-            if n > 0:
+            summed = n == 1 and s == levels - 2
+            if summed:
+                last = rest[0].astype(BF16)
+                parts += [last[:, :w], last[:, w:]]
+            elif n > 0:
                 h = side(s, bits)
                 keep = cols(rest, h * w, w)
                 send = cols(rest, (1 - h) * w, w)
@@ -93,7 +107,10 @@
                 payload, w_sib[s] = lax.optimization_barrier((payload, w_sib[s]))
             got = swap(payload, s, bits)
             theirs_b = jnp.concatenate([got[:rank], got[rank : 2 * rank]], axis=1)
-            if n > 0:
+            if summed:
+                recv = jnp.concatenate([got[2 * rank : 3 * rank], got[3 * rank :]], axis=1)
+                rest = rest + recv.astype(F32)[None]
+            elif n > 0:
                 recv = got[2 * rank :].reshape(n, rank, w).astype(F32)
                 rest = keep + recv
         lower = side(s, bits) == 0
@@ -102,28 +119,41 @@
             jnp.concatenate([mine_b, theirs_b], axis=0),
             jnp.concatenate([theirs_b, mine_b], axis=0),
         )
-        couple = jnp.concatenate([coupling[s, 0], couple_sib[s]], axis=0)
-        coefs = jnp.dot(couple, stacked, preferred_element_type=F32).astype(BF16)
-        own_coefs.append(coefs[:rank])
+        if s == 0 and levels > 2:
+            stacked, sent[1] = lax.optimization_barrier((stacked, sent[1]))
+        coefs = jnp.dot(coupling[s, 0], stacked, preferred_element_type=F32).astype(BF16)
+        own_coefs.append(coefs)
         if s < levels - 1:
+            sib = jnp.dot(couple_sib[s], stacked, preferred_element_type=F32).astype(BF16)
             w = coefs.shape[1] // 2
-            piece = cols(coefs, side(s, bits) * w, w).astype(F32)
+            if rest.shape[-1] == coefs.shape[1]:
+                co, cs = coefs, sib
+            else:
+                h = side(s, bits)
+                co, cs = cols(coefs, h * w, w), cols(sib, h * w, w)
             fix = jnp.einsum(
-                "nrs,st->nrt", w_own[s], piece[:rank],
+                "nrs,st->nrt", w_own[s], co.astype(F32),
                 preferred_element_type=F32, precision=lax.Precision.HIGHEST,
             ) + jnp.einsum(
-                "nrs,st->nrt", w_sib[s], piece[rank:],
+                "nrs,st->nrt", w_sib[s], cs.astype(F32),
                 preferred_element_type=F32, precision=lax.Precision.HIGHEST,
             )
-            rest = rest - fix
+            rest = rest - fix.reshape(rest.shape)
 
+    full = [own_coefs[0]] + [None] * (levels - 1)
     pending = {s: own_coefs[s] for s in range(1, levels)}
+    top = {s: s - 1 for s in range(1, levels)}
+    if levels > 2:
+        top[levels - 1] = levels - 3
     for j in reversed(range(levels - 1)):
-        group = [s for s in range(j + 1, levels)]
+        group = [s for s in range(1, levels) if top[s] >= j]
+        if not group:
+            continue
         joined = gather_half(jnp.stack([pending[s] for s in group]), j, bits)
         for i, s in enumerate(group):
             pending[s] = joined[i]
-    full = [own_coefs[0]] + [pending[s] for s in range(1, levels)]
+    for s in range(1, levels):
+        full[s] = pending[s]
     current = c0
     for s in range(levels):
         current = current - jnp.dot(u_basis[s], full[s], preferred_element_type=F32)

time: 72.2 us -> 59 us (0.82)
  waiting for transfers between devices: 26.9 us -> 18 us
  local copies, waits for them, and re-layouts: 6.54 us -> 4.12 us
  matrix products: 18.8 us -> 17.2 us
    ppermute x15 -> x13, waiting for transfers between devices: 26.9 us -> 18 us  [swap(): return lax.ppermute(x, axis, [(i, i ^ 1 << stride) for i in range(n)])]
    unnamed x24 -> x19, local copies, waits for them, and re-layouts: 2.72 us -> 0.93 us
    select_n x0 -> x1, other arithmetic: none -> 1.43 us  [on_device(): jnp.where(lower, jnp.concatenate([mine_b, theirs_b], axis=0), jnp.concate...]
    dot_general x11 -> x13, matrix products: 9.94 us -> 8.57 us  [the longest x3 3.09 us: on_device(): jnp.einsum('nrs,st->nrt', w_sib[s], cs.astype(F32), preferred_element_typ...]
    sub x0 -> x1, local copies, waits for them, and re-layouts: none -> 1.32 us  [on_device(): current = current - jnp.dot(u_basis[s], full[s], preferred_element_type=F32)]
    dot_general x1, matrix products: 0.46 us -> 1.66 us  [on_device(): jnp.einsum('kis,lir->klrs', u_basis, v_basis, preferred_element_type=F32)]
    slice x0 -> x1, other arithmetic: none -> 1.07 us  [on_device(): w_sib[b] = got[:n].reshape(counts[b], rank, rank)]
    add x2 -> x1, other arithmetic: 1.07 us -> 0.01 us  [on_device(): suffix = suffix[n:] + got[n:]]
  transfers between devices with their start and end apart: 15 -> 13, of which waited for: 9 -> 8; matrix products, arithmetic and copies ran while one was open for 22% -> 26% of each run, Pallas kernels for 0% -> 0%
where the time goes in v11:
time: 59 us; the launch traced here: 58.6 us
  waiting for transfers between devices  18 us (31%)
  matrix products  17.2 us (29%)
  starting transfers between devices  14.4 us (24%)
  other arithmetic  4.42 us (7%)
  local copies, waits for them, and re-layouts  4.12 us (7%)
    ppermute x13, waiting for transfers between devices, swap(): return lax.ppermute(x, axis, [(i, i ^ 1 << stride) for i in range(n)])  18 us
    ppermute x13, starting transfers between devices, swap(): return lax.ppermute(x, axis, [(i, i ^ 1 << stride) for i in range(n)])  14.4 us
    dot_general x3, matrix products, on_device(): jnp.einsum('nrs,st->nrt', w_sib[s], cs.astype(F32), preferred_element_typ...  3.09 us
    dot_general x3, matrix products, on_device(): jnp.dot(couple_sib[s], stacked, preferred_element_type=F32).astype(BF16)  2.54 us
    dot_general x1, matrix products, on_device(): c0 = jnp.dot(leaf_inverse, templates, preferred_element_type=F32)  2.11 us
    dot_general x4, matrix products, on_device(): current = current - jnp.dot(u_basis[s], full[s], preferred_element_type=F32)  1.95 us
    dot_general x4, matrix products, on_device(): jnp.dot(coupling[s, 0], stacked, preferred_element_type=F32).astype(BF16)  1.94 us
    concatenate x2, other arithmetic, gather_half(): both = jnp.concatenate([x, swap(x, bit, bits), x], axis=-1)  1.79 us
  transfers between devices with their start and end apart: 13, of which 8 were waited for; matrix products, arithmetic and copies ran while one was open for 26% of the time, Pallas kernels for 0%

profile of v11, /device:TPU:0, one launch (start us, length us, event | category | flops | bytes accessed | tf_op | source)
XLA Modules:
  0.0 58.6 jit_solution(15856944226841389335)
XLA Ops:
  0.0 1.7 %slice_bitcast_fusion.7 = (bf16[128,256]{1,0:T(8,128)(2,1)S(1)}, bf16[128,256]{1,0:T(8,128)(2,1)}, bf16[128,256]{1,0:T(8,128)(2,1)S(1)}) fusion(bf16[4,1,128,256]{3,2,1,0:T(8,128)(2,1)} %param.9), kind=kLoop, calls=%fused_computation.105 | loop fusion | bytes 393216 | tf_op jit(solution)/shard_map/squeeze | solution.py:124
  2.1 1.7 %convolution_bitcast_fusion = f32[4,4,128,128]{3,2,0,1:T(8,128)S(1)} fusion(bf16[4,512,128]{2,1,0:T(8,128)(2,1)} %param.7, bf16[4,512,128]{2,1,0:T(8,128)(2,1)} %param.8), kind=kOutput, calls=%fused_computation.2 | convolution fusion | flops 268435456 | bytes 2097152 | tf_op jit(solution)/shard_map/kis,lir->klrs/dot_general | solution.py:52
  4.0 2.1 %fusion.82 = (bf16[1024,512]{1,0:T(8,128)(2,1)S(1)}, f32[1024,512]{1,0:T(8,128)}) fusion(bf16[512,1024]{1,0:T(8,128)(2,1)S(1)} %copy-done, bf16[512,512]{1,0:T(8,128)(2,1)S(1)} %copy-done.4), kind=kOutput, calls=%fused_computation.127 | convolution fusion | flops 537395200 | bytes 4718592 | tf_op jit(solution)/shard_map/dot_general | solution.py:69
  6.1 1.2 %fusion.1 = bf16[128,1024]{1,0:T(8,128)(2,1)} fusion(bf16[1024,512]{1,0:T(8,128)(2,1)S(1)} %get-tuple-element.43, bf16[4,512,128]{2,1,0:T(8,128)(2,1)S(1)} %copy-done.2), kind=kOutput, calls=%fused_computation.13 | convolution fusion | flops 134348800 | bytes 1441792 | tf_op jit(solution)/shard_map/dot_general | solution.py:71
  7.8 1.3 %convolution_bitcast_fusion.1 = f32[3,128,512]{2,1,0:T(8,128)} fusion(bf16[1024,512]{1,0:T(8,128)(2,1)S(1)} %get-tuple-element.43, s32[]{:T(128)S(6)} %select_n.56, bf16[4,512,128]{2,1,0:T(8,128)(2,1)S(1)} %copy-done.2), kind=kOutput, calls=%fused_computation.3 | convolution fusion | flops 201326592 | bytes 1703940 | tf_op jit(solution)/shard_map/lir,it->lrt/dot_general | solution.py:80
  9.7 1.4 %maximum_select_fusion = bf16[256,1024]{1,0:T(8,128)(2,1)S(1)} fusion(bf16[128,1024]{1,0:T(8,128)(2,1)} %collective-permute-done, bf16[128,1024]{1,0:T(8,128)(2,1)} %fusion.1, pred[]{:T(512)S(6)} %eq.12), kind=kLoop, calls=%fused_computation.29 | loop fusion | flops 2359296 | bytes 1048577 | tf_op jit(solution)/shard_map/jit(_where)/select_n | solution.py:117
  12.3 3.0 %collective-permute-start.4 = (f32[384,128]{1,0:T(8,128)S(1)}, f32[384,128]{1,0:T(8,128)S(1)}, u32[]{:S(2)}, u32[]{:S(2)}) collective-permute-start(f32[384,128]{1,0:T(8,128)S(1)} %get-tuple-element.20), channel_id=1, source_target_pairs={{0,2},{2,0},{1,3},{3,1},{4,6},{6,4},{5,7},{7,5},{8,10},{10,8},{9,1... | collective-permute-start | bytes 589832 | tf_op jit(solution)/shard_map/ppermute | solution.py:21
  15.3 1.2 %convolution_convert_fusion = bf16[1024,128]{1,0:T(8,128)(2,1)S(1)} fusion(bf16[256,1024]{1,0:T(8,128)(2,1)S(1)} %maximum_select_fusion, bf16[4,1,128,256]{3,2,1,0:T(8,128)(2,1)} %param.9), kind=kOutput, calls=%fused_computation.5 | convolution fusion | flops 67239936 | bytes 851968 | tf_op jit(solution)/shard_map/dot_general | solution.py:124
  17.0 1.2 %fusion.83 = bf16[1024,128]{1,0:T(8,128)(2,1)S(1)} fusion(bf16[256,1024]{1,0:T(8,128)(2,1)S(1)} %maximum_select_fusion, bf16[128,256]{1,0:T(8,128)(2,1)} %collective-permute-done.3), kind=kOutput, calls=%fused_computation.128 | convolution fusion | flops 67108864 | bytes 851968 | tf_op jit(solution)/shard_map/dot_general | solution.py:127
  18.2 2.2 %collective-permute-done.4 = f32[384,128]{1,0:T(8,128)S(1)} collective-permute-done((f32[384,128]{1,0:T(8,128)S(1)}, f32[384,128]{1,0:T(8,128)S(1)}, u32[]{:S(2)}, u32[]{:S(2)}) %collective-permute-start.4) | collective-permute-done | bytes 196640 | tf_op jit(solution)/shard_map/ppermute | solution.py:21
  20.4 1.7 %add_subtract_fusion = f32[3,128,512]{2,1,0:T(8,128)S(1)} fusion(f32[3,128,512]{2,1,0:T(8,128)S(1)} %bitcast.139, f32[3,128,512]{2,1,0:T(8,128)} %collective-permute-done.2, f32[3,128,512]{2,1,0:T(8,128)S(1)} %fusion.41, f32[3,128,128]{2,1,0:T(8,128)S(1)} %bitcast.144, bf16[1024,128]{1,0:T(8,128)(2,1)S(1)} %fusion.83, s32[]{:T(128)S(6)} %select_n.55), kind=kOutput, calls=%fused_computation.28 | convolution fusion | flops 302579712 | bytes 3473412 | tf_op jit(solution)/shard_map/nrs,st->nrt/dot_general | solution.py:137
  22.3 1.8 %collective-permute-start.5 = (bf16[512,256]{1,0:T(8,128)(2,1)S(1)}, bf16[512,256]{1,0:T(8,128)(2,1)S(1)}, u32[]{:S(2)}, u32[]{:S(2)}) collective-permute-start(bf16[512,256]{1,0:T(8,128)(2,1)S(1)} %pad_maximum_fusion.2), channel_id=1, source_target_pairs={{0,2},{2,0},{1,3},{3,1},{4,6},{6,4},{5,7},{7,5},{8,10},{10,8},{9,1... | collective-permute-start | bytes 786440 | tf_op jit(solution)/shard_map/ppermute | solution.py:21
  24.4 1.9 %collective-permute-start.7 = (f32[128,128]{1,0:T(8,128)S(1)}, f32[128,128]{1,0:T(8,128)S(1)}, u32[]{:S(2)}, u32[]{:S(2)}) collective-permute-start(f32[128,128]{1,0:T(8,128)S(1)} %slice_add_fusion.1), channel_id=1, source_target_pairs={{0,4},{4,0},{8,12},{12,8},{1,5},{5,1},{9,13},{13,9},{2,6},{6,2},{1... | collective-permute-start | bytes 196616 | tf_op jit(solution)/shard_map/ppermute | solution.py:21
  26.3 4.4 %collective-permute-done.5 = bf16[512,256]{1,0:T(8,128)(2,1)S(1)} collective-permute-done((bf16[512,256]{1,0:T(8,128)(2,1)S(1)}, bf16[512,256]{1,0:T(8,128)(2,1)S(1)}, u32[]{:S(2)}, u32[]{:S(2)}) %collective-permute-start.5) | collective-permute-done | bytes 262176 | tf_op jit(solution)/shard_map/ppermute | solution.py:21
  31.6 1.1 %fusion.74 = bf16[512,128]{1,0:T(8,128)(2,1)S(1)} fusion(bf16[128,256]{1,0:T(8,128)(2,1)} %collective-permute-done.6, bf16[128,256]{1,0:T(8,128)(2,1)S(1)} %get-tuple-element.28, bf16[128,256]{1,0:T(8,128)(2,1)S(1)} %get-tuple-element.27, bf16[128,512]{1,0:T(8,128)(2,1)S(1)} %fusion.28, pred[]{:T(512)S(6)} %eq.13), kind=kOutput, calls=%fused_computation.119 | convolution fusion | flops 35258368 | bytes 458753 | tf_op jit(solution)/shard_map/dot_general | solution.py:127
  33.4 1.6 %collective-permute-start.8 = (bf16[512,128]{1,0:T(8,128)(2,1)S(1)}, bf16[512,128]{1,0:T(8,128)(2,1)S(1)}, u32[]{:S(2)}, u32[]{:S(2)}) collective-permute-start(bf16[512,128]{1,0:T(8,128)(2,1)S(1)} %pad_maximum_fusion.3), channel_id=1, source_target_pairs={{0,4},{4,0},{8,12},{12,8},{1,5},{5,1},{9,13},{13,9},{2,6},{6,2},{1... | collective-permute-start | bytes 393224 | tf_op jit(solution)/shard_map/ppermute | solution.py:21
  35.5 2.9 %collective-permute-done.8 = bf16[512,128]{1,0:T(8,128)(2,1)S(1)} collective-permute-done((bf16[512,128]{1,0:T(8,128)(2,1)S(1)}, bf16[512,128]{1,0:T(8,128)(2,1)S(1)}, u32[]{:S(2)}, u32[]{:S(2)}) %collective-permute-start.8) | collective-permute-done | bytes 131104 | tf_op jit(solution)/shard_map/ppermute | solution.py:21
  40.8 2.6 %collective-permute-start.10 = (bf16[256,128]{1,0:T(8,128)(2,1)S(1)}, bf16[256,128]{1,0:T(8,128)(2,1)S(1)}, u32[]{:S(2)}, u32[]{:S(2)}) collective-permute-start(bf16[256,128]{1,0:T(8,128)(2,1)S(1)} %pad_maximum_fusion.5), channel_id=1, source_target_pairs={{0,8},{4,12},{8,0},{12,4},{1,9},{5,13},{9,1},{13,5},{2,10},{6,14},... | collective-permute-start | bytes 196616 | tf_op jit(solution)/shard_map/ppermute | solution.py:21
  43.5 2.6 %collective-permute-done.10 = bf16[256,128]{1,0:T(8,128)(2,1)S(1)} collective-permute-done((bf16[256,128]{1,0:T(8,128)(2,1)S(1)}, bf16[256,128]{1,0:T(8,128)(2,1)S(1)}, u32[]{:S(2)}, u32[]{:S(2)}) %collective-permute-start.10) | collective-permute-done | bytes 65568 | tf_op jit(solution)/shard_map/ppermute | solution.py:21
  46.3 1.5 %collective-permute-start.11 = (bf16[2,128,256]{1,2,0:T(8,128)(2,1)S(1)}, bf16[2,128,256]{1,2,0:T(8,128)(2,1)S(1)}, u32[]{:S(2)}, u32[]{:S(2)}) collective-permute-start(bf16[2,128,256]{1,2,0:T(8,128)(2,1)S(1)} %pad_maximum_fusion.4), channel_id=1, source_target_pairs={{0,2},{2,0},{1,3},{3,1},{4,6},{6,4},{5,7},{7,5},{8,10},{10,8},{9,1... | collective-permute-start | bytes 393224 | tf_op jit(solution)/shard_map/ppermute | solution.py:21
  47.9 3.5 %collective-permute-done.11 = bf16[2,128,256]{1,2,0:T(8,128)(2,1)S(1)} collective-permute-done((bf16[2,128,256]{1,2,0:T(8,128)(2,1)S(1)}, bf16[2,128,256]{1,2,0:T(8,128)(2,1)S(1)}, u32[]{:S(2)}, u32[]{:S(2)}) %collective-permute-start.11) | collective-permute-done | bytes 131104 | tf_op jit(solution)/shard_map/ppermute | solution.py:21
  52.5 1.3 %collective-permute-done.12 = bf16[3,128,512]{1,2,0:T(8,128)(2,1)S(1)} collective-permute-done((bf16[3,128,512]{1,2,0:T(8,128)(2,1)S(1)}, bf16[3,128,512]{1,2,0:T(8,128)(2,1)S(1)}, u32[]{:S(2)}, u32[]{:S(2)}) %collective-permute-start.12) | collective-permute-done | bytes 393248 | tf_op jit(solution)/shard_map/ppermute | solution.py:21
  53.8 1.2 %fusion.9 = bf16[3,128,1024]{1,2,0:T(8,128)(2,1)S(1)} fusion(s32[]{:T(128)S(6)} %select_n.65, bf16[1,128,512]{1,2,0:T(8,128)(2,1)S(1)} %bitcast.142, bf16[2,128,512]{1,2,0:T(8,128)(2,1)S(1)} %fusion.19, bf16[3,128,512]{1,2,0:T(8,128)(2,1)S(1)} %collective-permute-done.12), kind=kLoop, calls=%fused_computation.26 | loop fusion | flops 3932160 | bytes 1572868 | tf_op jit(solution)/shard_map/concatenate | solution.py:44
  57.3 1.3 %copy.10 = bf16[512,1024]{1,0:T(8,128)(2,1)} copy(bf16[512,1024]{0,1:T(8,128)(2,1)S(1)} %fusion) | data formatting | bytes 2097152 | tf_op jit(solution)/shard_map/sub | solution.py:159
  (73 shorter events, 11.6 us)
Async XLA Ops:
  0.0 4.0 %copy-start = (bf16[512,1024]{1,0:T(8,128)(2,1)S(1)}, bf16[512,1024]{1,0:T(8,128)(2,1)}, u32[]{:S(2)}) copy-start(bf16[512,1024]{1,0:T(8,128)(2,1)} %param.5) | copy-start | bytes 3145732
  0.0 4.0 %copy-start.4 = (bf16[512,512]{1,0:T(8,128)(2,1)S(1)}, bf16[512,512]{1,0:T(8,128)(2,1)}, u32[]{:S(2)}) copy-start(bf16[512,512]{1,0:T(8,128)(2,1)} %param.6) | copy-start | bytes 1572868
  1.7 15.3 %collective-permute-start.3 = (bf16[128,256]{1,0:T(8,128)(2,1)S(1)}, bf16[128,256]{1,0:T(8,128)(2,1)}, u32[]{:S(2)}, u32[]{:S(2)}) collective-permute-start(bf16[128,256]{1,0:T(8,128)(2,1)S(1)} %get-tuple-element.24), channel_id=1, source_target_pairs={{0,1},{1,0},{2,3},{3,2},{4,5},{5,4},{6,7},{7,6},{8,9},{9,8},{10,11... | collective-permute-start | bytes 196616 | tf_op jit(solution)/shard_map/ppermute | solution.py:21
  3.9 2.3 %copy-start.2 = (bf16[4,512,128]{2,1,0:T(8,128)(2,1)S(1)}, bf16[4,512,128]{2,1,0:T(8,128)(2,1)}, u32[]{:S(2)}) copy-start(bf16[4,512,128]{2,1,0:T(8,128)(2,1)} %param.7) | copy-start | bytes 1572868
  3.9 7.3 %collective-permute-start.1 = (f32[768,128]{1,0:T(8,128)S(1)}, f32[768,128]{1,0:T(8,128)}, u32[]{:S(2)}, u32[]{:S(2)}) collective-permute-start(f32[768,128]{1,0:T(8,128)S(1)} %pad_maximum_fusion), channel_id=1, source_target_pairs={{0,1},{1,0},{2,3},{3,2},{4,5},{5,4},{6,7},{7,6},{8,9},{9,8},{10,11... | collective-permute-start | bytes 1179656 | tf_op jit(solution)/shard_map/ppermute | solution.py:21
  6.1 3.0 %slice-start = ((bf16[4,512,128]{2,1,0:T(8,128)(2,1)}), bf16[3,512,128]{2,1,0:T(8,128)(2,1)S(1)}, s32[]{:S(2)}) async-start(bf16[4,512,128]{2,1,0:T(8,128)(2,1)} %param.7), calls=%async_computation | async-start | bytes 786432
  7.3 2.4 %collective-permute-start = (bf16[128,1024]{1,0:T(8,128)(2,1)}, bf16[128,1024]{1,0:T(8,128)(2,1)}, u32[]{:S(2)}, u32[]{:S(2)}) collective-permute-start(bf16[128,1024]{1,0:T(8,128)(2,1)} %fusion.1), channel_id=1, source_target_pairs={{0,1},{1,0},{2,3},{3,2},{4,5},{5,4},{6,7},{7,6},{8,9},{9,8},{10,11... | collective-permute-start | bytes 786440 | tf_op jit(solution)/shard_map/ppermute | solution.py:21
  9.1 11.3 %collective-permute-start.2 = (f32[3,128,512]{2,1,0:T(8,128)}, f32[3,128,512]{2,1,0:T(8,128)}, u32[]{:S(2)}, u32[]{:S(2)}) collective-permute-start(f32[3,128,512]{2,1,0:T(8,128)} %convolution_bitcast_fusion.1), channel_id=1, source_target_pairs={{0,1},{1,0},{2,3},{3,2},{4,5},{5,4},{6,7},{7,6},{8,9},{9,8},{10,11... | collective-permute-start | bytes 2359304 | tf_op jit(solution)/shard_map/ppermute | solution.py:21
  12.3 8.1 %collective-permute-start.4 = (f32[384,128]{1,0:T(8,128)S(1)}, f32[384,128]{1,0:T(8,128)S(1)}, u32[]{:S(2)}, u32[]{:S(2)}) collective-permute-start(f32[384,128]{1,0:T(8,128)S(1)} %get-tuple-element.20), channel_id=1, source_target_pairs={{0,2},{2,0},{1,3},{3,1},{4,6},{6,4},{5,7},{7,5},{8,10},{10,8},{9,1... | collective-permute-start | bytes 589832 | tf_op jit(solution)/shard_map/ppermute | solution.py:21
  20.4 4.0 %copy-start.5 = (f32[384,128]{1,0:T(8,128)}, f32[384,128]{1,0:T(8,128)S(1)}, u32[]{:S(2)}) copy-start(f32[384,128]{1,0:T(8,128)S(1)} %collective-permute-done.4) | copy-start | bytes 589828
  22.1 8.7 %copy-start.6 = (bf16[4,1,128,256]{3,2,1,0:T(8,128)(2,1)S(1)}, bf16[4,1,128,256]{3,2,1,0:T(8,128)(2,1)}, u32[]{:S(2)}) copy-start(bf16[4,1,128,256]{3,2,1,0:T(8,128)(2,1)} %param.9) | copy-start | bytes 786436
  22.3 8.5 %collective-permute-start.5 = (bf16[512,256]{1,0:T(8,128)(2,1)S(1)}, bf16[512,256]{1,0:T(8,128)(2,1)S(1)}, u32[]{:S(2)}, u32[]{:S(2)}) collective-permute-start(bf16[512,256]{1,0:T(8,128)(2,1)S(1)} %pad_maximum_fusion.2), channel_id=1, source_target_pairs={{0,2},{2,0},{1,3},{3,1},{4,6},{6,4},{5,7},{7,5},{8,10},{10,8},{9,1... | collective-permute-start | bytes 786440 | tf_op jit(solution)/shard_map/ppermute | solution.py:21
  24.1 7.5 %collective-permute-start.6 = (bf16[128,256]{1,0:T(8,128)(2,1)}, bf16[128,256]{1,0:T(8,128)(2,1)}, u32[]{:S(2)}, u32[]{:S(2)}) collective-permute-start(bf16[128,256]{1,0:T(8,128)(2,1)} %get-tuple-element.23), channel_id=1, source_target_pairs={{0,2},{2,0},{1,3},{3,1},{4,6},{6,4},{5,7},{7,5},{8,10},{10,8},{9,1... | collective-permute-start | bytes 196616 | tf_op jit(solution)/shard_map/ppermute | solution.py:21
  24.4 8.3 %slice-start.1 = ((f32[384,128]{1,0:T(8,128)}), f32[256,128]{1,0:T(8,128)S(1)}, s32[]{:S(2)}) async-start(f32[384,128]{1,0:T(8,128)} %copy-done.5), calls=%async_computation.1 | async-start | bytes 262144 | tf_op jit(solution)/shard_map/slice | solution.py:65
  24.4 9.0 %collective-permute-start.7 = (f32[128,128]{1,0:T(8,128)S(1)}, f32[128,128]{1,0:T(8,128)S(1)}, u32[]{:S(2)}, u32[]{:S(2)}) collective-permute-start(f32[128,128]{1,0:T(8,128)S(1)} %slice_add_fusion.1), channel_id=1, source_target_pairs={{0,4},{4,0},{8,12},{12,8},{1,5},{5,1},{9,13},{13,9},{2,6},{6,2},{1... | collective-permute-start | bytes 196616 | tf_op jit(solution)/shard_map/ppermute | solution.py:21
  33.4 5.1 %copy-start.7 = (f32[128,128]{1,0:T(8,128)}, f32[128,128]{1,0:T(8,128)S(1)}, u32[]{:S(2)}) copy-start(f32[128,128]{1,0:T(8,128)S(1)} %collective-permute-done.7) | copy-start | bytes 196612
  33.4 5.0 %collective-permute-start.8 = (bf16[512,128]{1,0:T(8,128)(2,1)S(1)}, bf16[512,128]{1,0:T(8,128)(2,1)S(1)}, u32[]{:S(2)}, u32[]{:S(2)}) collective-permute-start(bf16[512,128]{1,0:T(8,128)(2,1)S(1)} %pad_maximum_fusion.3), channel_id=1, source_target_pairs={{0,4},{4,0},{8,12},{12,8},{1,5},{5,1},{9,13},{13,9},{2,6},{6,2},{1... | collective-permute-start | bytes 393224 | tf_op jit(solution)/shard_map/ppermute | solution.py:21
  35.0 4.3 %collective-permute-start.9 = (bf16[128,256]{1,0:T(8,128)(2,1)S(1)}, bf16[128,256]{1,0:T(8,128)(2,1)S(1)}, u32[]{:S(2)}, u32[]{:S(2)}) collective-permute-start(bf16[128,256]{1,0:T(8,128)(2,1)S(1)} %get-tuple-element.22), channel_id=1, source_target_pairs={{0,4},{4,0},{8,12},{12,8},{1,5},{5,1},{9,13},{13,9},{2,6},{6,2},{1... | collective-permute-start | bytes 196616 | tf_op jit(solution)/shard_map/ppermute | solution.py:21
  38.7 13.4 %copy-start.3 = (bf16[4,512,128]{2,1,0:T(8,128)(2,1)S(1)}, bf16[4,512,128]{2,1,0:T(8,128)(2,1)}, u32[]{:S(2)}) copy-start(bf16[4,512,128]{2,1,0:T(8,128)(2,1)} %param.8) | copy-start | bytes 1572868
  40.8 5.2 %collective-permute-start.10 = (bf16[256,128]{1,0:T(8,128)(2,1)S(1)}, bf16[256,128]{1,0:T(8,128)(2,1)S(1)}, u32[]{:S(2)}, u32[]{:S(2)}) collective-permute-start(bf16[256,128]{1,0:T(8,128)(2,1)S(1)} %pad_maximum_fusion.5), channel_id=1, source_target_pairs={{0,8},{4,12},{8,0},{12,4},{1,9},{5,13},{9,1},{13,5},{2,10},{6,14},... | collective-permute-start | bytes 196616 | tf_op jit(solution)/shard_map/ppermute | solution.py:21
  46.3 5.0 %collective-permute-start.11 = (bf16[2,128,256]{1,2,0:T(8,128)(2,1)S(1)}, bf16[2,128,256]{1,2,0:T(8,128)(2,1)S(1)}, u32[]{:S(2)}, u32[]{:S(2)}) collective-permute-start(bf16[2,128,256]{1,2,0:T(8,128)(2,1)S(1)} %pad_maximum_fusion.4), channel_id=1, source_target_pairs={{0,2},{2,0},{1,3},{3,1},{4,6},{6,4},{5,7},{7,5},{8,10},{10,8},{9,1... | collective-permute-start | bytes 393224 | tf_op jit(solution)/shard_map/ppermute | solution.py:21
  52.0 1.8 %collective-permute-start.12 = (bf16[3,128,512]{1,2,0:T(8,128)(2,1)S(1)}, bf16[3,128,512]{1,2,0:T(8,128)(2,1)S(1)}, u32[]{:S(2)}, u32[]{:S(2)}) collective-permute-start(bf16[3,128,512]{1,2,0:T(8,128)(2,1)S(1)} %pad_maximum_fusion.1), channel_id=1, source_target_pairs={{0,1},{1,0},{2,3},{3,2},{4,5},{5,4},{6,7},{7,6},{8,9},{9,8},{10,11... | collective-permute-start | bytes 1179656 | tf_op jit(solution)/shard_map/ppermute | solution.py:21
  55.0 1.6 %copy-start.1 = (f32[1024,512]{1,0:T(8,128)S(1)}, f32[1024,512]{1,0:T(8,128)}, u32[]{:S(2)}) copy-start(f32[1024,512]{1,0:T(8,128)} %get-tuple-element.44) | copy-start | bytes 6291460

commit v12 on v10

--- a/solution.py
+++ b/solution.py
@@ -151,6 +151,8 @@
     top = {s: s - 1 for s in range(1, levels)}
     if levels > 2:
         top[levels - 1] = levels - 3
+    early = c0 - jnp.dot(u_basis[0], own_coefs[0], preferred_element_type=F32)
+    joined = None
     for j in reversed(range(levels - 1)):
         group = [s for s in range(1, levels) if top[s] >= j]
         if not group:
@@ -158,11 +160,11 @@
         joined = gather_half(jnp.stack([pending[s] for s in group]), j, bits)
         for i, s in enumerate(group):
             pending[s] = joined[i]
-    for s in range(1, levels):
-        full[s] = pending[s]
-    current = c0
-    for s in range(levels):
-        current = current - jnp.dot(u_basis[s], full[s], preferred_element_type=F32)
+    if joined is None:
+        joined = jnp.stack([pending[s] for s in range(1, levels)])
+    current = early - jnp.einsum(
+        "lir,lrt->it", u_basis[1:], joined, preferred_element_type=F32
+    )
     return current.astype(BF16)
 
 

time: 57.8 us -> 58.4 us (1.010)
  matrix products: 11.4 us -> 14.4 us
  waiting for transfers between devices: 19.7 us -> 18.6 us
  local copies, waits for them, and re-layouts: 5.77 us -> 5.04 us
    dot_general x4 -> x2, matrix products: 2.84 us -> 4.89 us  [the longest x1 3.4 us: on_device(): jnp.einsum('lir,lrt->it', u_basis[1:], joined, preferred_element_type=F32)]
    concatenate x2 -> x1, other arithmetic: 1.79 us -> 0.6 us  [gather_half(): both = jnp.concatenate([x, swap(x, bit, bits), x], axis=-1)]
    ppermute x11, waiting for transfers between devices: 19.7 us -> 18.6 us  [swap(): return lax.ppermute(x, axis, [(i, i ^ 1 << stride) for i in range(n)])]
    dot_general x3, matrix products: 0.69 us -> 1.64 us  [on_device(): jnp.einsum('lir,is->lrs', v_basis[s + 1:], u_basis[s], preferred_element_...]
    another operation x2, other arithmetic: 0.05 us -> 0.8 us  [on_device(): joined = gather_half(jnp.stack([pending[s] for s in group]), j, bits)]
    unnamed x32 -> x34, local copies, waits for them, and re-layouts: 1.09 us -> 0.39 us
  transfers between devices with their start and end apart: 11 -> 11, of which waited for: 6 -> 6; matrix products, arithmetic and copies ran while one was open for 29% -> 32% of each run, Pallas kernels for 0% -> 0%
where the time goes in v12:
time: 58.4 us; the launch traced here: 57.9 us
  waiting for transfers between devices  18.6 us (32%)
  matrix products  14.4 us (25%)
  starting transfers between devices  11.9 us (20%)
  other arithmetic  7.44 us (13%)
  local copies, waits for them, and re-layouts  5.04 us (9%)
    ppermute x11, waiting for transfers between devices, swap(): return lax.ppermute(x, axis, [(i, i ^ 1 << stride) for i in range(n)])  18.6 us
    ppermute x11, starting transfers between devices, swap(): return lax.ppermute(x, axis, [(i, i ^ 1 << stride) for i in range(n)])  11.9 us
    dot_general x1, matrix products, on_device(): jnp.einsum('lir,lrt->it', u_basis[1:], joined, preferred_element_type=F32)  3.4 us
    dot_general x1, matrix products, on_device(): c0 = jnp.dot(leaf_inverse, templates, preferred_element_type=F32)  2.05 us
    dot_general x4, matrix products, on_device(): coefs = jnp.dot(couple[s], stacked, preferred_element_type=F32).astype(BF16)  2.01 us
    add x3, other arithmetic, on_device(): partial[s] = partial[s] + recv  1.78 us
    squeeze x1, local copies, waits for them, and re-layouts, on_device(): mine, theirs = (mine_c[s], theirs_c[s])  1.74 us
    dot_general x3, matrix products, on_device(): jnp.einsum('lir,is->lrs', v_basis[s + 1:], u_basis[s], preferred_element_...  1.64 us
  transfers between devices with their start and end apart: 11, of which 6 were waited for; matrix products, arithmetic and copies ran while one was open for 32% of the time, Pallas kernels for 0%

profile of v12, /device:TPU:0, one launch (start us, length us, event | category | flops | bytes accessed | tf_op | source)
XLA Modules:
  0.0 57.9 jit_solution(1302682267700569995)
XLA Ops:
  0.0 1.7 %slice_bitcast_fusion.2 = (bf16[128,256]{1,0:T(8,128)(2,1)S(1)}, bf16[128,256]{1,0:T(8,128)(2,1)}, bf16[128,256]{1,0:T(8,128)(2,1)}, bf16[128,256]{1,0:T(8,128)(2,1)S(1)}) fusion(bf16[4,1,128,256]{3,2,1,0:T(8,128)(2,1)} %param.9), kind=kLoop, calls=%fused_computation.138 | loop fusion | bytes 524288 | tf_op jit(solution)/shard_map/squeeze | solution.py:82
  2.5 4.0 %collective-permute-start.7 = (bf16[256,128]{1,0:T(8,128)(2,1)}, bf16[256,128]{1,0:T(8,128)(2,1)}, u32[]{:S(2)}, u32[]{:S(2)}) collective-permute-start(bf16[256,128]{1,0:T(8,128)(2,1)} %fusion.83), channel_id=1, source_target_pairs={{0,8},{4,12},{8,0},{12,4},{1,9},{5,13},{9,1},{13,5},{2,10},{6,14},... | collective-permute-start | bytes 196616 | tf_op jit(solution)/shard_map/ppermute | solution.py:21
  7.3 1.2 %fusion.74 = f32[384,128]{1,0:T(8,128)S(1)} fusion(bf16[384,512]{1,0:T(8,128)(2,1)S(1)} %bitcast.92, bf16[4,512,128]{2,1,0:T(8,128)(2,1)} %param.8), kind=kOutput, calls=%fused_computation.105 | convolution fusion | flops 50331648 | bytes 720896 | tf_op jit(solution)/shard_map/lir,is->lrs/dot_general | solution.py:57
  9.4 0.8 %pad_maximum_fusion = f32[1024,128]{1,0:T(8,128)} fusion(f32[128,128]{1,0:T(8,128)S(1)} %fusion.68, f32[256,128]{1,0:T(8,128)S(1)} %fusion.71, f32[384,128]{1,0:T(8,128)S(1)} %fusion.74, f32[256,128]{1,0:T(8,128)S(1)} %fusion.86), kind=kLoop, calls=%fused_computation.23 | loop fusion | flops 393216 | bytes 1048576 | tf_op jit(solution)/shard_map/concatenate | solution.py:67
  10.3 2.0 %fusion.118 = (bf16[512,1024]{1,0:T(8,128)(2,1)S(1)}, f32[512,1024]{1,0:T(8,128)}) fusion(bf16[512,512]{1,0:T(8,128)(2,1)S(1)} %copy-done.3, bf16[512,1024]{1,0:T(8,128)(2,1)S(1)} %copy-done), kind=kOutput, calls=%fused_computation.180 | convolution fusion | flops 537395200 | bytes 4718592 | tf_op jit(solution)/shard_map/dot_general | solution.py:52
  12.3 1.1 %fusion.1 = bf16[128,1024]{1,0:T(8,128)(2,1)} fusion(bf16[512,1024]{1,0:T(8,128)(2,1)S(1)} %get-tuple-element.51, bf16[4,512,128]{2,1,0:T(8,128)(2,1)S(1)} %copy-done.1), kind=kOutput, calls=%fused_computation.12 | convolution fusion | flops 134348800 | bytes 1441792 | tf_op jit(solution)/shard_map/dot_general | solution.py:92
  13.9 1.3 %convolution_bitcast_fusion = f32[3,128,512]{2,1,0:T(8,128)} fusion(bf16[512,1024]{1,0:T(8,128)(2,1)S(1)} %get-tuple-element.51, s32[]{:T(128)S(6)} %select_n.69, bf16[4,512,128]{2,1,0:T(8,128)(2,1)S(1)} %copy-done.1), kind=kOutput, calls=%fused_computation.3 | convolution fusion | flops 201326592 | bytes 1703940 | tf_op jit(solution)/shard_map/lir,it->lrt/dot_general | solution.py:101
  16.5 0.9 %slice_add_fusion = f32[256,128]{1,0:T(8,128)S(1)} fusion(f32[256,128]{1,0:T(8,128)S(1)} %fusion.71, f32[1024,128]{1,0:T(8,128)} %collective-permute-done), kind=kLoop, calls=%fused_computation.69 | loop fusion | flops 32768 | bytes 393216 | tf_op jit(solution)/shard_map/add | solution.py:78
  17.4 0.8 %slice_add_fusion.2 = f32[128,128]{1,0:T(8,128)S(1)} fusion(f32[128,128]{1,0:T(8,128)S(1)} %fusion.68, f32[1024,128]{1,0:T(8,128)} %collective-permute-done), kind=kLoop, calls=%fused_computation.132 | loop fusion | flops 16384 | bytes 196608 | tf_op jit(solution)/shard_map/add | solution.py:78
  18.3 1.6 %collective-permute-start.2 = (f32[640,128]{1,0:T(8,128)S(1)}, f32[640,128]{1,0:T(8,128)S(1)}, u32[]{:S(2)}, u32[]{:S(2)}) collective-permute-start(f32[640,128]{1,0:T(8,128)S(1)} %pad_maximum_fusion.2), channel_id=1, source_target_pairs={{0,2},{2,0},{1,3},{3,1},{4,6},{6,4},{5,7},{7,5},{8,10},{10,8},{9,1... | collective-permute-start | bytes 983048 | tf_op jit(solution)/shard_map/ppermute | solution.py:21
  19.9 0.9 %slice.283 = f32[384,128]{1,0:T(8,128)S(1)} slice(f32[1024,128]{1,0:T(8,128)} %collective-permute-done), slice={[256:640], [0:128]} | slice | bytes 393216 | tf_op jit(solution)/shard_map/slice | solution.py:73
  20.8 1.1 %convert.16 = bf16[1024,128]{1,0:T(8,128)(2,1)S(1)} convert(f32[1024,128]{1,0:T(8,128)} %collective-permute-done) | non-fusion elementwise | flops 131072 | bytes 786432 | tf_op jit(solution)/shard_map/convert.5
  21.9 1.3 %convolution_convert_fusion = bf16[256,1024]{1,0:T(8,128)(2,1)S(1)} fusion(bf16[128,1024]{1,0:T(8,128)(2,1)} %collective-permute-done.1, bf16[128,1024]{1,0:T(8,128)(2,1)} %fusion.1, bf16[256,128]{1,0:T(8,128)(2,1)S(1)} %get-tuple-element.30, bf16[256,128]{1,0:T(8,128)(2,1)S(1)} %get-tuple-element.29), kind=kOutput, calls=%fused_computation.4 | convolution fusion | flops 135790592 | bytes 1179648 | tf_op jit(solution)/shard_map/dot_general | solution.py:135
  23.8 1.4 %add_subtract_fusion = f32[3,128,512]{2,1,0:T(8,128)S(1)} fusion(f32[3,128,512]{2,1,0:T(8,128)S(1)} %bitcast.95, f32[3,128,512]{2,1,0:T(8,128)S(1)} %bitcast.94, f32[3,128,512]{2,1,0:T(8,128)} %collective-permute-done.3), kind=kLoop, calls=%fused_computation.22 | loop fusion | flops 393216 | bytes 3145728 | tf_op jit(solution)/shard_map/sub | solution.py:147
  26.0 2.7 %collective-permute-done.2 = f32[640,128]{1,0:T(8,128)S(1)} collective-permute-done((f32[640,128]{1,0:T(8,128)S(1)}, f32[640,128]{1,0:T(8,128)S(1)}, u32[]{:S(2)}, u32[]{:S(2)}) %collective-permute-start.2) | collective-permute-done | bytes 327712 | tf_op jit(solution)/shard_map/ppermute | solution.py:21
  28.7 1.6 %collective-permute-start.5 = (f32[384,128]{1,0:T(8,128)S(1)}, f32[384,128]{1,0:T(8,128)S(1)}, u32[]{:S(2)}, u32[]{:S(2)}) collective-permute-start(f32[384,128]{1,0:T(8,128)S(1)} %pad_maximum_fusion.4), channel_id=1, source_target_pairs={{0,4},{4,0},{8,12},{12,8},{1,5},{5,1},{9,13},{13,9},{2,6},{6,2},{1... | collective-permute-start | bytes 589832 | tf_op jit(solution)/shard_map/ppermute | solution.py:21
  30.4 3.7 %collective-permute-done.4 = bf16[512,256]{1,0:T(8,128)(2,1)S(1)} collective-permute-done((bf16[512,256]{1,0:T(8,128)(2,1)S(1)}, bf16[512,256]{1,0:T(8,128)(2,1)S(1)}, u32[]{:S(2)}, u32[]{:S(2)}) %collective-permute-start.4) | collective-permute-done | bytes 262176 | tf_op jit(solution)/shard_map/ppermute | solution.py:21
  34.8 1.6 %collective-permute-start.6 = (bf16[512,128]{1,0:T(8,128)(2,1)S(1)}, bf16[512,128]{1,0:T(8,128)(2,1)S(1)}, u32[]{:S(2)}, u32[]{:S(2)}) collective-permute-start(bf16[512,128]{1,0:T(8,128)(2,1)S(1)} %pad_maximum_fusion.5), channel_id=1, source_target_pairs={{0,4},{4,0},{8,12},{12,8},{1,5},{5,1},{9,13},{13,9},{2,6},{6,2},{1... | collective-permute-start | bytes 393224 | tf_op jit(solution)/shard_map/ppermute | solution.py:21
  36.5 3.4 %collective-permute-done.6 = bf16[512,128]{1,0:T(8,128)(2,1)S(1)} collective-permute-done((bf16[512,128]{1,0:T(8,128)(2,1)S(1)}, bf16[512,128]{1,0:T(8,128)(2,1)S(1)}, u32[]{:S(2)}, u32[]{:S(2)}) %collective-permute-start.6) | collective-permute-done | bytes 131104 | tf_op jit(solution)/shard_map/ppermute | solution.py:21
  40.7 5.0 %collective-permute-done.8 = bf16[256,128]{1,0:T(8,128)(2,1)S(1)} collective-permute-done((bf16[256,128]{1,0:T(8,128)(2,1)S(1)}, bf16[256,128]{1,0:T(8,128)(2,1)S(1)}, u32[]{:S(2)}, u32[]{:S(2)}) %collective-permute-start.8) | collective-permute-done | bytes 65568 | tf_op jit(solution)/shard_map/ppermute | solution.py:21
  46.0 1.6 %collective-permute-start.9 = (bf16[2,128,256]{1,2,0:T(8,128)(2,1)S(1)}, bf16[2,128,256]{1,2,0:T(8,128)(2,1)S(1)}, u32[]{:S(2)}, u32[]{:S(2)}) collective-permute-start(bf16[2,128,256]{1,2,0:T(8,128)(2,1)S(1)} %pad_maximum_fusion.6), channel_id=1, source_target_pairs={{0,2},{2,0},{1,3},{3,1},{4,6},{6,4},{5,7},{7,5},{8,10},{10,8},{9,1... | collective-permute-start | bytes 393224 | tf_op jit(solution)/shard_map/ppermute | solution.py:21
  47.7 3.3 %collective-permute-done.9 = bf16[2,128,256]{1,2,0:T(8,128)(2,1)S(1)} collective-permute-done((bf16[2,128,256]{1,2,0:T(8,128)(2,1)S(1)}, bf16[2,128,256]{1,2,0:T(8,128)(2,1)S(1)}, u32[]{:S(2)}, u32[]{:S(2)}) %collective-permute-start.9) | collective-permute-done | bytes 131104 | tf_op jit(solution)/shard_map/ppermute | solution.py:21
  52.4 1.5 %fusion.27 = f32[1024,512]{0,1:T(8,128)S(1)} fusion(bf16[256,1024]{1,0:T(8,128)(2,1)} %copy-done.6, bf16[4,512,128]{2,1,0:T(8,128)(2,1)} %param.8), kind=kOutput, calls=%fused_computation.48 | convolution fusion | flops 134217728 | bytes 2490368 | tf_op jit(solution)/shard_map/dot_general | solution.py:154
  54.5 3.4 %fusion = bf16[512,1024]{1,0:T(8,128)(2,1)} fusion(f32[512,1024]{1,0:T(8,128)S(1)} %copy-done.2, f32[1024,512]{0,1:T(8,128)S(1)} %fusion.27, s32[]{:T(128)S(6)} %select_n.79, bf16[1,128,512]{1,2,0:T(8,128)(2,1)S(1)} %copy.19, bf16[2,128,512]{1,2,0:T(8,128)(2,1)S(1)} %fusion.25, bf16[3,128,512]{1,2,0:T(8,128)(2,1)} %collective-permute-done.10, ...), kind=kOutput, calls=%fused_computation.1 | convolution fusion | flops 408158208 | bytes 6422532 | tf_op jit(solution)/shard_map/lir,lrt->it/dot_general | solution.py:165
  (101 shorter events, 9.2 us)
Async XLA Ops:
  0.0 10.3 %copy-start = (bf16[512,1024]{1,0:T(8,128)(2,1)S(1)}, bf16[512,1024]{1,0:T(8,128)(2,1)}, u32[]{:S(2)}) copy-start(bf16[512,1024]{1,0:T(8,128)(2,1)} %param.5) | copy-start | bytes 3145732
  0.0 6.5 %copy-start.1 = (bf16[4,512,128]{2,1,0:T(8,128)(2,1)S(1)}, bf16[4,512,128]{2,1,0:T(8,128)(2,1)}, u32[]{:S(2)}) copy-start(bf16[4,512,128]{2,1,0:T(8,128)(2,1)} %param.7) | copy-start | bytes 1572868
  0.0 6.7 %slice-start = ((bf16[4,512,128]{2,1,0:T(8,128)(2,1)}), bf16[2,512,128]{2,1,0:T(8,128)(2,1)S(1)}, s32[]{:S(2)}) async-start(bf16[4,512,128]{2,1,0:T(8,128)(2,1)} %param.7), calls=%async_computation | async-start | bytes 524288 | tf_op jit(solution)/shard_map/slice | solution.py:58
  0.0 6.5 %copy-start.4 = (bf16[4,512,128]{2,1,0:T(8,128)(2,1)S(1)}, bf16[4,512,128]{2,1,0:T(8,128)(2,1)}, u32[]{:S(2)}) copy-start(bf16[4,512,128]{2,1,0:T(8,128)(2,1)} %param.8) | copy-start | bytes 1572868
  1.8 5.4 %slice-start.1 = ((bf16[4,512,128]{2,1,0:T(8,128)(2,1)}), bf16[3,512,128]{2,1,0:T(8,128)(2,1)S(1)}, s32[]{:S(2)}) async-start(bf16[4,512,128]{2,1,0:T(8,128)(2,1)} %param.7), calls=%async_computation.1 | async-start | bytes 786432
  1.8 5.1 %copy-start.11 = (bf16[128,128]{1,0:T(8,128)(2,1)}, bf16[128,128]{1,0:T(8,128)(2,1)S(1)}, u32[]{:S(2)}) copy-start(bf16[128,128]{1,0:T(8,128)(2,1)S(1)} %get-tuple-element.39) | copy-start | bytes 98308
  1.8 5.1 %copy-start.13 = (bf16[128,128]{1,0:T(8,128)(2,1)}, bf16[128,128]{1,0:T(8,128)(2,1)S(1)}, u32[]{:S(2)}) copy-start(bf16[128,128]{1,0:T(8,128)(2,1)S(1)} %get-tuple-element.40) | copy-start | bytes 98308
  2.5 13.2 %collective-permute-start.7 = (bf16[256,128]{1,0:T(8,128)(2,1)}, bf16[256,128]{1,0:T(8,128)(2,1)}, u32[]{:S(2)}, u32[]{:S(2)}) collective-permute-start(bf16[256,128]{1,0:T(8,128)(2,1)} %fusion.83), channel_id=1, source_target_pairs={{0,8},{4,12},{8,0},{12,4},{1,9},{5,13},{9,1},{13,5},{2,10},{6,14},... | collective-permute-start | bytes 196616 | tf_op jit(solution)/shard_map/ppermute | solution.py:21
  7.3 3.0 %copy-start.3 = (bf16[512,512]{1,0:T(8,128)(2,1)S(1)}, bf16[512,512]{1,0:T(8,128)(2,1)}, u32[]{:S(2)}) copy-start(bf16[512,512]{1,0:T(8,128)(2,1)} %param.6) | copy-start | bytes 1572868
  10.3 6.2 %collective-permute-start = (f32[1024,128]{1,0:T(8,128)}, f32[1024,128]{1,0:T(8,128)}, u32[]{:S(2)}, u32[]{:S(2)}) collective-permute-start(f32[1024,128]{1,0:T(8,128)} %pad_maximum_fusion), channel_id=1, source_target_pairs={{0,1},{1,0},{2,3},{3,2},{4,5},{5,4},{6,7},{7,6},{8,9},{9,8},{10,11... | collective-permute-start | bytes 1572872 | tf_op jit(solution)/shard_map/ppermute | solution.py:21
  13.4 8.6 %collective-permute-start.1 = (bf16[128,1024]{1,0:T(8,128)(2,1)}, bf16[128,1024]{1,0:T(8,128)(2,1)}, u32[]{:S(2)}, u32[]{:S(2)}) collective-permute-start(bf16[128,1024]{1,0:T(8,128)(2,1)} %fusion.1), channel_id=1, source_target_pairs={{0,1},{1,0},{2,3},{3,2},{4,5},{5,4},{6,7},{7,6},{8,9},{9,8},{10,11... | collective-permute-start | bytes 786440 | tf_op jit(solution)/shard_map/ppermute | solution.py:21
  15.2 8.6 %collective-permute-start.3 = (f32[3,128,512]{2,1,0:T(8,128)}, f32[3,128,512]{2,1,0:T(8,128)}, u32[]{:S(2)}, u32[]{:S(2)}) collective-permute-start(f32[3,128,512]{2,1,0:T(8,128)} %convolution_bitcast_fusion), channel_id=1, source_target_pairs={{0,1},{1,0},{2,3},{3,2},{4,5},{5,4},{6,7},{7,6},{8,9},{9,8},{10,11... | collective-permute-start | bytes 2359304 | tf_op jit(solution)/shard_map/ppermute | solution.py:21
  15.6 6.3 %copy-start.8 = (bf16[128,128]{1,0:T(8,128)(2,1)S(1)}, bf16[128,128]{1,0:T(8,128)(2,1)}, u32[]{:S(2)}) copy-start(bf16[128,128]{1,0:T(8,128)(2,1)} %copy-done.7) | copy-start | bytes 98308
  15.6 6.3 %copy-start.10 = (bf16[128,128]{1,0:T(8,128)(2,1)S(1)}, bf16[128,128]{1,0:T(8,128)(2,1)}, u32[]{:S(2)}) copy-start(bf16[128,128]{1,0:T(8,128)(2,1)} %copy-done.9) | copy-start | bytes 98308
  18.3 10.4 %collective-permute-start.2 = (f32[640,128]{1,0:T(8,128)S(1)}, f32[640,128]{1,0:T(8,128)S(1)}, u32[]{:S(2)}, u32[]{:S(2)}) collective-permute-start(f32[640,128]{1,0:T(8,128)S(1)} %pad_maximum_fusion.2), channel_id=1, source_target_pairs={{0,2},{2,0},{1,3},{3,1},{4,6},{6,4},{5,7},{7,5},{8,10},{10,8},{9,1... | collective-permute-start | bytes 983048 | tf_op jit(solution)/shard_map/ppermute | solution.py:21
  23.3 1.9 %copy-start.6 = (bf16[256,1024]{1,0:T(8,128)(2,1)}, bf16[256,1024]{1,0:T(8,128)(2,1)S(1)}, u32[]{:S(2)}) copy-start(bf16[256,1024]{1,0:T(8,128)(2,1)S(1)} %convolution_convert_fusion) | copy-start | bytes 1572868
  25.3 8.7 %collective-permute-start.4 = (bf16[512,256]{1,0:T(8,128)(2,1)S(1)}, bf16[512,256]{1,0:T(8,128)(2,1)S(1)}, u32[]{:S(2)}, u32[]{:S(2)}) collective-permute-start(bf16[512,256]{1,0:T(8,128)(2,1)S(1)} %pad_maximum_fusion.3), channel_id=1, source_target_pairs={{0,2},{2,0},{1,3},{3,1},{4,6},{6,4},{5,7},{7,5},{8,10},{10,8},{9,1... | collective-permute-start | bytes 786440 | tf_op jit(solution)/shard_map/ppermute | solution.py:21
  28.7 7.7 %collective-permute-start.5 = (f32[384,128]{1,0:T(8,128)S(1)}, f32[384,128]{1,0:T(8,128)S(1)}, u32[]{:S(2)}, u32[]{:S(2)}) collective-permute-start(f32[384,128]{1,0:T(8,128)S(1)} %pad_maximum_fusion.4), channel_id=1, source_target_pairs={{0,4},{4,0},{8,12},{12,8},{1,5},{5,1},{9,13},{13,9},{2,6},{6,2},{1... | collective-permute-start | bytes 589832 | tf_op jit(solution)/shard_map/ppermute | solution.py:21
  34.8 5.1 %collective-permute-start.6 = (bf16[512,128]{1,0:T(8,128)(2,1)S(1)}, bf16[512,128]{1,0:T(8,128)(2,1)S(1)}, u32[]{:S(2)}, u32[]{:S(2)}) collective-permute-start(bf16[512,128]{1,0:T(8,128)(2,1)S(1)} %pad_maximum_fusion.5), channel_id=1, source_target_pairs={{0,4},{4,0},{8,12},{12,8},{1,5},{5,1},{9,13},{13,9},{2,6},{6,2},{1... | collective-permute-start | bytes 393224 | tf_op jit(solution)/shard_map/ppermute | solution.py:21
  40.5 5.2 %collective-permute-start.8 = (bf16[256,128]{1,0:T(8,128)(2,1)S(1)}, bf16[256,128]{1,0:T(8,128)(2,1)S(1)}, u32[]{:S(2)}, u32[]{:S(2)}) collective-permute-start(bf16[256,128]{1,0:T(8,128)(2,1)S(1)} %pad_maximum_fusion.19), channel_id=1, source_target_pairs={{0,8},{4,12},{8,0},{12,4},{1,9},{5,13},{9,1},{13,5},{2,10},{6,14},... | collective-permute-start | bytes 196616 | tf_op jit(solution)/shard_map/ppermute | solution.py:21
  46.0 5.0 %collective-permute-start.9 = (bf16[2,128,256]{1,2,0:T(8,128)(2,1)S(1)}, bf16[2,128,256]{1,2,0:T(8,128)(2,1)S(1)}, u32[]{:S(2)}, u32[]{:S(2)}) collective-permute-start(bf16[2,128,256]{1,2,0:T(8,128)(2,1)S(1)} %pad_maximum_fusion.6), channel_id=1, source_target_pairs={{0,2},{2,0},{1,3},{3,1},{4,6},{6,4},{5,7},{7,5},{8,10},{10,8},{9,1... | collective-permute-start | bytes 393224 | tf_op jit(solution)/shard_map/ppermute | solution.py:21
  51.6 2.9 %copy-start.2 = (f32[512,1024]{1,0:T(8,128)S(1)}, f32[512,1024]{1,0:T(8,128)}, u32[]{:S(2)}) copy-start(f32[512,1024]{1,0:T(8,128)} %get-tuple-element.52) | copy-start | bytes 6291460
  52.4 2.1 %collective-permute-start.10 = (bf16[3,128,512]{1,2,0:T(8,128)(2,1)}, bf16[3,128,512]{1,2,0:T(8,128)(2,1)}, u32[]{:S(2)}, u32[]{:S(2)}) collective-permute-start(bf16[3,128,512]{1,2,0:T(8,128)(2,1)} %pad_maximum_fusion.1), channel_id=1, source_target_pairs={{0,1},{1,0},{2,3},{3,2},{4,5},{5,4},{6,7},{7,6},{8,9},{9,8},{10,11... | collective-permute-start | bytes 1179656 | tf_op jit(solution)/shard_map/ppermute | solution.py:21
  52.4 2.1 %copy-start.5 = (bf16[4,512,128]{2,1,0:T(8,128)(2,1)S(1)}, bf16[4,512,128]{2,1,0:T(8,128)(2,1)}, u32[]{:S(2)}) copy-start(bf16[4,512,128]{2,1,0:T(8,128)(2,1)} %param.8) | copy-start | bytes 1572868
  (4 other events, 4.2 us)

commit v13 on v10

--- a/solution.py
+++ b/solution.py
@@ -50,7 +50,6 @@
     levels, pixels, rank = v_basis.shape
     width = templates.shape[1]
     c0 = jnp.dot(leaf_inverse, templates, preferred_element_type=F32)
-    c0b = c0.astype(BF16)
 
     mine_c = coupling[:, 0]
     partial = [
@@ -89,19 +88,22 @@
             )
         )
 
-    proj0 = jnp.dot(v_basis[0].T, c0b, preferred_element_type=F32)
+    vl = jnp.einsum("lir,ij->lrj", v_basis, leaf_inverse, preferred_element_type=F32)
+    vl_hi = vl.astype(BF16)
+    vl_lo = (vl - vl_hi.astype(F32)).astype(BF16)
+
+    def project(lv, x):
+        return jnp.einsum(
+            "lrj,jt->lrt", vl_hi[lv], x, preferred_element_type=F32
+        ) + jnp.einsum("lrj,jt->lrt", vl_lo[lv], x, preferred_element_type=F32)
+
+    proj0 = project(slice(0, 1), templates)[0]
     rest = None
     if levels > 1:
         half = width // 2
         h = side(0, bits)
-        keep = jnp.einsum(
-            "lir,it->lrt", v_basis[1:], cols(c0b, h * half, half),
-            preferred_element_type=F32,
-        )
-        send = jnp.einsum(
-            "lir,it->lrt", v_basis[1:], cols(c0b, (1 - h) * half, half),
-            preferred_element_type=F32,
-        )
+        keep = project(slice(1, levels), cols(templates, h * half, half))
+        send = project(slice(1, levels), cols(templates, (1 - h) * half, half))
         rest = keep + swap(send, 0, bits)
     own_coefs = []
     for s in range(levels):

time: 57.8 us -> 57.1 us (0.988)
  matrix products: 11.4 us -> 13.7 us
  local copies, waits for them, and re-layouts: 5.77 us -> 4.07 us
  waiting for transfers between devices: 19.7 us -> 18.9 us
  other arithmetic: 7.9 us -> 7.28 us
    dot_general x2 -> x7, matrix products: 2.36 us -> 6.33 us  [the longest x3 3.79 us: project(): jnp.einsum('lrj,jt->lrt', vl_lo[lv], x, preferred_element_type=F32)]
    sub x2 -> x1, other arithmetic: 1.44 us -> 0.06 us  [on_device(): rest = rest - fix.reshape(rest.shape)]
    dot_general x4, matrix products: 2.84 us -> 1.73 us  [on_device(): current = current - jnp.dot(u_basis[s], full[s], preferred_element_type=F32)]
    ppermute x11, waiting for transfers between devices: 19.7 us -> 18.9 us  [swap(): return lax.ppermute(x, axis, [(i, i ^ 1 << stride) for i in range(n)])]
    slice x2, local copies, waits for them, and re-layouts: 0.84 us -> 0.05 us  [on_device(): parts = [jnp.concatenate([c[:, :rank], c[:, rank:]], axis=0).astype(F32)]]
    select_n x4, other arithmetic: 0.13 us -> 0.9 us  [on_device(): jnp.where(lower, first, second)]
    squeeze x1, local copies, waits for them, and re-layouts: 1.76 us -> 1.12 us  [on_device(): mine, theirs = (mine_c[s], theirs_c[s])]
  transfers between devices with their start and end apart: 11 -> 11, of which waited for: 6 -> 6; matrix products, arithmetic and copies ran while one was open for 29% -> 30% of each run, Pallas kernels for 0% -> 0%
where the time goes in v13:
time: 57.1 us; the launch traced here: 56.6 us
  waiting for transfers between devices  18.9 us (33%)
  matrix products  13.7 us (24%)
  starting transfers between devices  12 us (21%)
  other arithmetic  7.28 us (13%)
  local copies, waits for them, and re-layouts  4.07 us (7%)
  between operations  0.67 us (1%)
    ppermute x11, waiting for transfers between devices, swap(): return lax.ppermute(x, axis, [(i, i ^ 1 << stride) for i in range(n)])  18.9 us
    ppermute x11, starting transfers between devices, swap(): return lax.ppermute(x, axis, [(i, i ^ 1 << stride) for i in range(n)])  12 us
    dot_general x3, matrix products, project(): jnp.einsum('lrj,jt->lrt', vl_lo[lv], x, preferred_element_type=F32)  3.79 us
    dot_general x4, matrix products, on_device(): coefs = jnp.dot(couple[s], stacked, preferred_element_type=F32).astype(BF16)  2 us
    dot_general x1, matrix products, on_device(): c0 = jnp.dot(leaf_inverse, templates, preferred_element_type=F32)  1.83 us
    concatenate x2, other arithmetic, gather_half(): both = jnp.concatenate([x, swap(x, bit, bits), x], axis=-1)  1.79 us
    add x3, other arithmetic, on_device(): partial[s] = partial[s] + recv  1.78 us
    dot_general x4, matrix products, on_device(): current = current - jnp.dot(u_basis[s], full[s], preferred_element_type=F32)  1.73 us
  transfers between devices with their start and end apart: 11, of which 6 were waited for; matrix products, arithmetic and copies ran while one was open for 30% of the time, Pallas kernels for 0%

profile of v13, /device:TPU:0, one launch (start us, length us, event | category | flops | bytes accessed | tf_op | source)
XLA Modules:
  0.0 56.6 jit_solution(18245260790736689294)
XLA Ops:
  0.0 1.1 %slice_bitcast_fusion.12 = (bf16[128,256]{1,0:T(8,128)(2,1)S(1)}, bf16[128,256]{1,0:T(8,128)(2,1)S(1)}, bf16[128,256]{1,0:T(8,128)(2,1)S(1)}, bf16[128,256]{1,0:T(8,128)(2,1)S(1)}) fusion(bf16[4,1,128,256]{3,2,1,0:T(8,128)(2,1)} %param.9), kind=kLoop, calls=%fused_computation.163 | loop fusion | bytes 524288 | tf_op jit(solution)/shard_map/squeeze | solution.py:81
  1.8 4.0 %collective-permute-start.7 = (bf16[256,128]{1,0:T(8,128)(2,1)}, bf16[256,128]{1,0:T(8,128)(2,1)}, u32[]{:S(2)}, u32[]{:S(2)}) collective-permute-start(bf16[256,128]{1,0:T(8,128)(2,1)} %fusion.98), channel_id=1, source_target_pairs={{0,8},{4,12},{8,0},{12,4},{1,9},{5,13},{9,1},{13,5},{2,10},{6,14},... | collective-permute-start | bytes 196616 | tf_op jit(solution)/shard_map/ppermute | solution.py:21
  7.0 0.8 %pad_maximum_fusion = f32[1024,128]{1,0:T(8,128)} fusion(f32[128,128]{1,0:T(8,128)S(1)} %fusion.80, f32[256,128]{1,0:T(8,128)S(1)} %fusion.84, f32[384,128]{1,0:T(8,128)S(1)} %fusion.87, f32[256,128]{1,0:T(8,128)S(1)} %fusion.101), kind=kLoop, calls=%fused_computation.28 | loop fusion | flops 393216 | bytes 1048576 | tf_op jit(solution)/shard_map/concatenate | solution.py:66
  7.9 1.5 %subtract_convert_fusion = (bf16[4,128,512]{2,1,0:T(8,128)(2,1)S(1)}, bf16[4,128,512]{2,1,0:T(8,128)(2,1)S(1)}) fusion(bf16[4,512,128]{2,1,0:T(8,128)(2,1)S(1)} %copy-done.1, bf16[512,512]{1,0:T(8,128)(2,1)} %param.6), kind=kOutput, calls=%fused_computation.23 | convolution fusion | flops 269484032 | bytes 2097152 | tf_op jit(solution)/shard_map/lir,ij->lrj/dot_general | solution.py:91
  9.7 1.0 %fusion.3 = bf16[128,1024]{1,0:T(8,128)(2,1)} fusion(f32[128,1024]{1,0:T(8,128)S(1)} %fusion.51, bf16[512,1024]{1,0:T(8,128)(2,1)S(1)} %copy-done, bf16[4,128,512]{2,1,0:T(8,128)(2,1)S(1)} %get-tuple-element.5), kind=kOutput, calls=%fused_computation.11 | convolution fusion | flops 134479872 | bytes 1966080 | tf_op jit(solution)/shard_map/lrj,jt->lrt/dot_general | solution.py:98
  11.6 1.3 %convolution_add_fusion = f32[3,128,512]{2,1,0:T(8,128)} fusion(f32[3,128,512]{2,1,0:T(8,128)S(1)} %fusion.15, bf16[4,128,512]{2,1,0:T(8,128)(2,1)S(1)} %get-tuple-element.5, bf16[512,1024]{1,0:T(8,128)(2,1)S(1)} %copy-done, s32[]{:T(128)S(6)} %select_n.69), kind=kOutput, calls=%fused_computation.6 | convolution fusion | flops 201523200 | bytes 2621444 | tf_op jit(solution)/shard_map/lrj,jt->lrt/dot_general | solution.py:98
  15.0 0.9 %slice_add_fusion = f32[256,128]{1,0:T(8,128)S(1)} fusion(f32[256,128]{1,0:T(8,128)S(1)} %fusion.84, f32[1024,128]{1,0:T(8,128)} %collective-permute-done), kind=kLoop, calls=%fused_computation.87 | loop fusion | flops 32768 | bytes 393216 | tf_op jit(solution)/shard_map/add | solution.py:77
  15.9 0.8 %slice_add_fusion.2 = f32[128,128]{1,0:T(8,128)S(1)} fusion(f32[128,128]{1,0:T(8,128)S(1)} %fusion.80, f32[1024,128]{1,0:T(8,128)} %collective-permute-done), kind=kLoop, calls=%fused_computation.157 | loop fusion | flops 16384 | bytes 196608 | tf_op jit(solution)/shard_map/add | solution.py:77
  16.8 1.6 %collective-permute-start.2 = (f32[640,128]{1,0:T(8,128)S(1)}, f32[640,128]{1,0:T(8,128)S(1)}, u32[]{:S(2)}, u32[]{:S(2)}) collective-permute-start(f32[640,128]{1,0:T(8,128)S(1)} %pad_maximum_fusion.2), channel_id=1, source_target_pairs={{0,2},{2,0},{1,3},{3,1},{4,6},{6,4},{5,7},{7,5},{8,10},{10,8},{9,1... | collective-permute-start | bytes 983048 | tf_op jit(solution)/shard_map/ppermute | solution.py:21
  18.3 0.9 %slice.311 = f32[384,128]{1,0:T(8,128)S(1)} slice(f32[1024,128]{1,0:T(8,128)} %collective-permute-done), slice={[256:640], [0:128]} | slice | bytes 393216 | tf_op jit(solution)/shard_map/slice | solution.py:72
  19.3 1.1 %convert.16 = bf16[1024,128]{1,0:T(8,128)(2,1)S(1)} convert(f32[1024,128]{1,0:T(8,128)} %collective-permute-done) | non-fusion elementwise | flops 131072 | bytes 786432 | tf_op jit(solution)/shard_map/convert.5
  20.4 1.3 %convolution_convert_fusion = bf16[256,1024]{1,0:T(8,128)(2,1)S(1)} fusion(bf16[128,1024]{1,0:T(8,128)(2,1)} %collective-permute-done.1, bf16[128,1024]{1,0:T(8,128)(2,1)} %fusion.3, bf16[256,128]{1,0:T(8,128)(2,1)S(1)} %get-tuple-element.32, bf16[256,128]{1,0:T(8,128)(2,1)S(1)} %get-tuple-element.31), kind=kOutput, calls=%fused_computation.5 | convolution fusion | flops 135790592 | bytes 1179648 | tf_op jit(solution)/shard_map/dot_general | solution.py:137
  22.6 1.5 %fusion.2 = f32[3,128,512]{2,1,0:T(8,128)S(1)} fusion(f32[3,128,512]{2,1,0:T(8,128)S(1)} %bitcast.124, f32[3,128,512]{2,1,0:T(8,128)} %collective-permute-done.3, f32[3,128,512]{2,1,0:T(8,128)S(1)} %fusion.18, bf16[4,128,512]{2,1,0:T(8,128)(2,1)S(1)} %get-tuple-element.5, bf16[512,1024]{1,0:T(8,128)(2,1)S(1)} %copy-done, s32[]{:T(128)S(6)} %select_n.68), kind=kOutput, calls=%fused_computation.9 | convolution fusion | flops 201916416 | bytes 4194308 | tf_op jit(solution)/shard_map/lrj,jt->lrt/dot_general | solution.py:98
  24.8 2.1 %collective-permute-done.2 = f32[640,128]{1,0:T(8,128)S(1)} collective-permute-done((f32[640,128]{1,0:T(8,128)S(1)}, f32[640,128]{1,0:T(8,128)S(1)}, u32[]{:S(2)}, u32[]{:S(2)}) %collective-permute-start.2) | collective-permute-done | bytes 327712 | tf_op jit(solution)/shard_map/ppermute | solution.py:21
  27.0 1.6 %collective-permute-start.5 = (f32[384,128]{1,0:T(8,128)S(1)}, f32[384,128]{1,0:T(8,128)S(1)}, u32[]{:S(2)}, u32[]{:S(2)}) collective-permute-start(f32[384,128]{1,0:T(8,128)S(1)} %pad_maximum_fusion.4), channel_id=1, source_target_pairs={{0,4},{4,0},{8,12},{12,8},{1,5},{5,1},{9,13},{13,9},{2,6},{6,2},{1... | collective-permute-start | bytes 589832 | tf_op jit(solution)/shard_map/ppermute | solution.py:21
  28.7 4.0 %collective-permute-done.4 = bf16[512,256]{1,0:T(8,128)(2,1)S(1)} collective-permute-done((bf16[512,256]{1,0:T(8,128)(2,1)S(1)}, bf16[512,256]{1,0:T(8,128)(2,1)S(1)}, u32[]{:S(2)}, u32[]{:S(2)}) %collective-permute-start.4) | collective-permute-done | bytes 262176 | tf_op jit(solution)/shard_map/ppermute | solution.py:21
  33.4 1.7 %collective-permute-start.6 = (bf16[512,128]{1,0:T(8,128)(2,1)S(1)}, bf16[512,128]{1,0:T(8,128)(2,1)S(1)}, u32[]{:S(2)}, u32[]{:S(2)}) collective-permute-start(bf16[512,128]{1,0:T(8,128)(2,1)S(1)} %pad_maximum_fusion.5), channel_id=1, source_target_pairs={{0,4},{4,0},{8,12},{12,8},{1,5},{5,1},{9,13},{13,9},{2,6},{6,2},{1... | collective-permute-start | bytes 393224 | tf_op jit(solution)/shard_map/ppermute | solution.py:21
  35.2 3.3 %collective-permute-done.6 = bf16[512,128]{1,0:T(8,128)(2,1)S(1)} collective-permute-done((bf16[512,128]{1,0:T(8,128)(2,1)S(1)}, bf16[512,128]{1,0:T(8,128)(2,1)S(1)}, u32[]{:S(2)}, u32[]{:S(2)}) %collective-permute-start.6) | collective-permute-done | bytes 131104 | tf_op jit(solution)/shard_map/ppermute | solution.py:21
  39.5 4.8 %collective-permute-done.8 = bf16[256,128]{1,0:T(8,128)(2,1)S(1)} collective-permute-done((bf16[256,128]{1,0:T(8,128)(2,1)S(1)}, bf16[256,128]{1,0:T(8,128)(2,1)S(1)}, u32[]{:S(2)}, u32[]{:S(2)}) %collective-permute-start.8) | collective-permute-done | bytes 65568 | tf_op jit(solution)/shard_map/ppermute | solution.py:21
  44.6 1.5 %collective-permute-start.9 = (bf16[2,128,256]{1,2,0:T(8,128)(2,1)S(1)}, bf16[2,128,256]{1,2,0:T(8,128)(2,1)S(1)}, u32[]{:S(2)}, u32[]{:S(2)}) collective-permute-start(bf16[2,128,256]{1,2,0:T(8,128)(2,1)S(1)} %pad_maximum_fusion.6), channel_id=1, source_target_pairs={{0,2},{2,0},{1,3},{3,1},{4,6},{6,4},{5,7},{7,5},{8,10},{10,8},{9,1... | collective-permute-start | bytes 393224 | tf_op jit(solution)/shard_map/ppermute | solution.py:21
  46.2 3.4 %collective-permute-done.9 = bf16[2,128,256]{1,2,0:T(8,128)(2,1)S(1)} collective-permute-done((bf16[2,128,256]{1,2,0:T(8,128)(2,1)S(1)}, bf16[2,128,256]{1,2,0:T(8,128)(2,1)S(1)}, u32[]{:S(2)}, u32[]{:S(2)}) %collective-permute-start.9) | collective-permute-done | bytes 131104 | tf_op jit(solution)/shard_map/ppermute | solution.py:21
  50.8 1.3 %collective-permute-done.10 = bf16[3,128,512]{1,2,0:T(8,128)(2,1)S(1)} collective-permute-done((bf16[3,128,512]{1,2,0:T(8,128)(2,1)S(1)}, bf16[3,128,512]{1,2,0:T(8,128)(2,1)S(1)}, u32[]{:S(2)}, u32[]{:S(2)}) %collective-permute-start.10) | collective-permute-done | bytes 393248 | tf_op jit(solution)/shard_map/ppermute | solution.py:21
  52.0 1.2 %fusion.9 = bf16[3,128,1024]{1,2,0:T(8,128)(2,1)S(1)} fusion(s32[]{:T(128)S(6)} %select_n.79, bf16[1,128,512]{1,2,0:T(8,128)(2,1)S(1)} %copy.16, bf16[2,128,512]{1,2,0:T(8,128)(2,1)S(1)} %fusion.32, bf16[3,128,512]{1,2,0:T(8,128)(2,1)S(1)} %collective-permute-done.10), kind=kLoop, calls=%fused_computation.26 | loop fusion | flops 3932160 | bytes 1572868 | tf_op jit(solution)/shard_map/concatenate | solution.py:44
  54.7 1.8 %fusion = bf16[512,1024]{1,0:T(8,128)(2,1)} fusion(f32[1024,512]{0,1:T(8,128)S(1)} %fusion.34, f32[1024,512]{0,1:T(8,128)S(1)} %fusion.35, f32[1024,512]{0,1:T(8,128)S(1)} %fusion.36, f32[1024,512]{0,1:T(8,128)S(1)} %fusion.37, bf16[512,512]{1,0:T(8,128)(2,1)S(1)} %copy-done.2, bf16[512,1024]{1,0:T(8,128)(2,1)S(1)} %copy-done), kind=kOutput, calls=%fused_computation.1 | convolution fusion | flops 539492352 | bytes 11010048 | tf_op jit(solution)/shard_map/dot_general | solution.py:52
  (103 shorter events, 11.2 us)
Async XLA Ops:
  0.0 9.4 %copy-start = (bf16[512,1024]{1,0:T(8,128)(2,1)S(1)}, bf16[512,1024]{1,0:T(8,128)(2,1)}, u32[]{:S(2)}) copy-start(bf16[512,1024]{1,0:T(8,128)(2,1)} %param.5) | copy-start | bytes 3145732
  0.0 5.9 %copy-start.1 = (bf16[4,512,128]{2,1,0:T(8,128)(2,1)S(1)}, bf16[4,512,128]{2,1,0:T(8,128)(2,1)}, u32[]{:S(2)}) copy-start(bf16[4,512,128]{2,1,0:T(8,128)(2,1)} %param.7) | copy-start | bytes 1572868
  0.0 6.1 %slice-start = ((bf16[4,512,128]{2,1,0:T(8,128)(2,1)}), bf16[2,512,128]{2,1,0:T(8,128)(2,1)S(1)}, s32[]{:S(2)}) async-start(bf16[4,512,128]{2,1,0:T(8,128)(2,1)} %param.7), calls=%async_computation | async-start | bytes 524288 | tf_op jit(solution)/shard_map/slice | solution.py:57
  0.0 6.5 %slice-start.1 = ((bf16[4,512,128]{2,1,0:T(8,128)(2,1)}), bf16[3,512,128]{2,1,0:T(8,128)(2,1)S(1)}, s32[]{:S(2)}) async-start(bf16[4,512,128]{2,1,0:T(8,128)(2,1)} %param.7), calls=%async_computation.1 | async-start | bytes 786432 | tf_op jit(solution)/shard_map/slice | solution.py:57
  0.0 5.9 %copy-start.3 = (bf16[4,512,128]{2,1,0:T(8,128)(2,1)S(1)}, bf16[4,512,128]{2,1,0:T(8,128)(2,1)}, u32[]{:S(2)}) copy-start(bf16[4,512,128]{2,1,0:T(8,128)(2,1)} %param.8) | copy-start | bytes 1572868
  1.2 5.1 %copy-start.11 = (bf16[128,128]{1,0:T(8,128)(2,1)}, bf16[128,128]{1,0:T(8,128)(2,1)S(1)}, u32[]{:S(2)}) copy-start(bf16[128,128]{1,0:T(8,128)(2,1)S(1)} %get-tuple-element.41) | copy-start | bytes 98308
  1.2 5.1 %copy-start.12 = (bf16[128,128]{1,0:T(8,128)(2,1)}, bf16[128,128]{1,0:T(8,128)(2,1)S(1)}, u32[]{:S(2)}) copy-start(bf16[128,128]{1,0:T(8,128)(2,1)S(1)} %get-tuple-element.42) | copy-start | bytes 98308
  1.8 11.5 %collective-permute-start.7 = (bf16[256,128]{1,0:T(8,128)(2,1)}, bf16[256,128]{1,0:T(8,128)(2,1)}, u32[]{:S(2)}, u32[]{:S(2)}) collective-permute-start(bf16[256,128]{1,0:T(8,128)(2,1)} %fusion.98), channel_id=1, source_target_pairs={{0,8},{4,12},{8,0},{12,4},{1,9},{5,13},{9,1},{13,5},{2,10},{6,14},... | collective-permute-start | bytes 196616 | tf_op jit(solution)/shard_map/ppermute | solution.py:21
  7.0 2.7 %copy-start.7 = (bf16[128,128]{1,0:T(8,128)(2,1)}, bf16[128,128]{1,0:T(8,128)(2,1)S(1)}, u32[]{:S(2)}) copy-start(bf16[128,128]{1,0:T(8,128)(2,1)S(1)} %get-tuple-element.55) | copy-start | bytes 98308
  7.0 2.7 %copy-start.9 = (bf16[128,128]{1,0:T(8,128)(2,1)}, bf16[128,128]{1,0:T(8,128)(2,1)S(1)}, u32[]{:S(2)}) copy-start(bf16[128,128]{1,0:T(8,128)(2,1)S(1)} %get-tuple-element.56) | copy-start | bytes 98308
  7.9 7.1 %collective-permute-start = (f32[1024,128]{1,0:T(8,128)}, f32[1024,128]{1,0:T(8,128)}, u32[]{:S(2)}, u32[]{:S(2)}) collective-permute-start(f32[1024,128]{1,0:T(8,128)} %pad_maximum_fusion), channel_id=1, source_target_pairs={{0,1},{1,0},{2,3},{3,2},{4,5},{5,4},{6,7},{7,6},{8,9},{9,8},{10,11... | collective-permute-start | bytes 1572872 | tf_op jit(solution)/shard_map/ppermute | solution.py:21
  10.8 9.6 %collective-permute-start.1 = (bf16[128,1024]{1,0:T(8,128)(2,1)}, bf16[128,1024]{1,0:T(8,128)(2,1)}, u32[]{:S(2)}, u32[]{:S(2)}) collective-permute-start(bf16[128,1024]{1,0:T(8,128)(2,1)} %fusion.3), channel_id=1, source_target_pairs={{0,1},{1,0},{2,3},{3,2},{4,5},{5,4},{6,7},{7,6},{8,9},{9,8},{10,11... | collective-permute-start | bytes 786440 | tf_op jit(solution)/shard_map/ppermute | solution.py:21
  12.9 9.3 %collective-permute-start.3 = (f32[3,128,512]{2,1,0:T(8,128)}, f32[3,128,512]{2,1,0:T(8,128)}, u32[]{:S(2)}, u32[]{:S(2)}) collective-permute-start(f32[3,128,512]{2,1,0:T(8,128)} %convolution_add_fusion), channel_id=1, source_target_pairs={{0,1},{1,0},{2,3},{3,2},{4,5},{5,4},{6,7},{7,6},{8,9},{9,8},{10,11... | collective-permute-start | bytes 2359304 | tf_op jit(solution)/shard_map/ppermute | solution.py:21
  13.3 7.1 %copy-start.8 = (bf16[128,128]{1,0:T(8,128)(2,1)S(1)}, bf16[128,128]{1,0:T(8,128)(2,1)}, u32[]{:S(2)}) copy-start(bf16[128,128]{1,0:T(8,128)(2,1)} %copy-done.7) | copy-start | bytes 98308
  13.3 7.1 %copy-start.10 = (bf16[128,128]{1,0:T(8,128)(2,1)S(1)}, bf16[128,128]{1,0:T(8,128)(2,1)}, u32[]{:S(2)}) copy-start(bf16[128,128]{1,0:T(8,128)(2,1)} %copy-done.9) | copy-start | bytes 98308
  16.8 10.2 %collective-permute-start.2 = (f32[640,128]{1,0:T(8,128)S(1)}, f32[640,128]{1,0:T(8,128)S(1)}, u32[]{:S(2)}, u32[]{:S(2)}) collective-permute-start(f32[640,128]{1,0:T(8,128)S(1)} %pad_maximum_fusion.2), channel_id=1, source_target_pairs={{0,2},{2,0},{1,3},{3,1},{4,6},{6,4},{5,7},{7,5},{8,10},{10,8},{9,1... | collective-permute-start | bytes 983048 | tf_op jit(solution)/shard_map/ppermute | solution.py:21
  24.2 8.5 %collective-permute-start.4 = (bf16[512,256]{1,0:T(8,128)(2,1)S(1)}, bf16[512,256]{1,0:T(8,128)(2,1)S(1)}, u32[]{:S(2)}, u32[]{:S(2)}) collective-permute-start(bf16[512,256]{1,0:T(8,128)(2,1)S(1)} %pad_maximum_fusion.3), channel_id=1, source_target_pairs={{0,2},{2,0},{1,3},{3,1},{4,6},{6,4},{5,7},{7,5},{8,10},{10,8},{9,1... | collective-permute-start | bytes 786440 | tf_op jit(solution)/shard_map/ppermute | solution.py:21
  27.0 8.1 %collective-permute-start.5 = (f32[384,128]{1,0:T(8,128)S(1)}, f32[384,128]{1,0:T(8,128)S(1)}, u32[]{:S(2)}, u32[]{:S(2)}) collective-permute-start(f32[384,128]{1,0:T(8,128)S(1)} %pad_maximum_fusion.4), channel_id=1, source_target_pairs={{0,4},{4,0},{8,12},{12,8},{1,5},{5,1},{9,13},{13,9},{2,6},{6,2},{1... | collective-permute-start | bytes 589832 | tf_op jit(solution)/shard_map/ppermute | solution.py:21
  33.4 5.0 %collective-permute-start.6 = (bf16[512,128]{1,0:T(8,128)(2,1)S(1)}, bf16[512,128]{1,0:T(8,128)(2,1)S(1)}, u32[]{:S(2)}, u32[]{:S(2)}) collective-permute-start(bf16[512,128]{1,0:T(8,128)(2,1)S(1)} %pad_maximum_fusion.5), channel_id=1, source_target_pairs={{0,4},{4,0},{8,12},{12,8},{1,5},{5,1},{9,13},{13,9},{2,6},{6,2},{1... | collective-permute-start | bytes 393224 | tf_op jit(solution)/shard_map/ppermute | solution.py:21
  38.5 11.9 %copy-start.4 = (bf16[4,512,128]{2,1,0:T(8,128)(2,1)S(1)}, bf16[4,512,128]{2,1,0:T(8,128)(2,1)}, u32[]{:S(2)}) copy-start(bf16[4,512,128]{2,1,0:T(8,128)(2,1)} %param.8) | copy-start | bytes 1572868
  38.5 11.9 %copy-start.6 = (bf16[256,1024]{1,0:T(8,128)(2,1)S(1)}, bf16[256,1024]{1,0:T(8,128)(2,1)}, u32[]{:S(2)}) copy-start(bf16[256,1024]{1,0:T(8,128)(2,1)} %copy-done.5) | copy-start | bytes 1572868
  39.1 5.2 %collective-permute-start.8 = (bf16[256,128]{1,0:T(8,128)(2,1)S(1)}, bf16[256,128]{1,0:T(8,128)(2,1)S(1)}, u32[]{:S(2)}, u32[]{:S(2)}) collective-permute-start(bf16[256,128]{1,0:T(8,128)(2,1)S(1)} %pad_maximum_fusion.19), channel_id=1, source_target_pairs={{0,8},{4,12},{8,0},{12,4},{1,9},{5,13},{9,1},{13,5},{2,10},{6,14},... | collective-permute-start | bytes 196616 | tf_op jit(solution)/shard_map/ppermute | solution.py:21
  44.6 5.0 %collective-permute-start.9 = (bf16[2,128,256]{1,2,0:T(8,128)(2,1)S(1)}, bf16[2,128,256]{1,2,0:T(8,128)(2,1)S(1)}, u32[]{:S(2)}, u32[]{:S(2)}) collective-permute-start(bf16[2,128,256]{1,2,0:T(8,128)(2,1)S(1)} %pad_maximum_fusion.6), channel_id=1, source_target_pairs={{0,2},{2,0},{1,3},{3,1},{4,6},{6,4},{5,7},{7,5},{8,10},{10,8},{9,1... | collective-permute-start | bytes 393224 | tf_op jit(solution)/shard_map/ppermute | solution.py:21
  50.3 1.8 %collective-permute-start.10 = (bf16[3,128,512]{1,2,0:T(8,128)(2,1)S(1)}, bf16[3,128,512]{1,2,0:T(8,128)(2,1)S(1)}, u32[]{:S(2)}, u32[]{:S(2)}) collective-permute-start(bf16[3,128,512]{1,2,0:T(8,128)(2,1)S(1)} %pad_maximum_fusion.1), channel_id=1, source_target_pairs={{0,1},{1,0},{2,3},{3,2},{4,5},{5,4},{6,7},{7,6},{8,9},{9,8},{10,11... | collective-permute-start | bytes 1179656 | tf_op jit(solution)/shard_map/ppermute | solution.py:21
  (2 other events, 1.9 us)

commit v14 on v11

--- a/solution.py
+++ b/solution.py
@@ -49,38 +49,38 @@
     bits = bit_axes()
     levels, pixels, rank = v_basis.shape
     width = templates.shape[1]
+    c0 = jnp.dot(leaf_inverse, templates, preferred_element_type=F32)
+
     cross = jnp.einsum("kis,lir->klrs", u_basis, v_basis, preferred_element_type=F32)
     counts = [levels - 1 - k for k in range(levels - 1)]
     suffix = jnp.concatenate(
         [cross[k, k + 1 :].reshape(-1, rank) for k in range(levels - 1)], axis=0
     )
-    w_own, w_sib, sent = [None] * levels, [None] * levels, [None] * levels
+    w_own, w_sib = [None] * levels, [None] * levels
     for b in range(levels - 1):
         n = counts[b] * rank
-        if b == 0:
-            suffix, templates = lax.optimization_barrier((suffix, templates))
-        sent[b] = suffix
         got = swap(suffix, b, bits)
         w_own[b] = suffix[:n].reshape(counts[b], rank, rank)
         w_sib[b] = got[:n].reshape(counts[b], rank, rank)
         suffix = suffix[n:] + got[n:]
-    couple_sib = [swap(coupling[s, 0], s, bits) for s in range(levels)]
+    couple_sib = [swap(coupling[s, 0], s, bits) for s in range(levels - 1)]
 
-    c0 = jnp.dot(leaf_inverse, templates, preferred_element_type=F32)
-    c0b = c0.astype(BF16)
-    proj0 = jnp.dot(v_basis[0].T, c0b, preferred_element_type=F32)
+    vl = jnp.einsum("lir,ij->lrj", v_basis, leaf_inverse, preferred_element_type=F32)
+    vl_hi = vl.astype(BF16)
+    vl_lo = (vl - vl_hi.astype(F32)).astype(BF16)
+
+    def project(lv, x):
+        return jnp.einsum(
+            "lrj,jt->lrt", vl_hi[lv], x, preferred_element_type=F32
+        ) + jnp.einsum("lrj,jt->lrt", vl_lo[lv], x, preferred_element_type=F32)
+
+    proj0 = project(slice(0, 1), templates)[0]
     rest = None
     if levels > 1:
         half = width // 2
         h = side(0, bits)
-        keep = jnp.einsum(
-            "lir,it->lrt", v_basis[1:], cols(c0b, h * half, half),
-            preferred_element_type=F32,
-        )
-        send = jnp.einsum(
-            "lir,it->lrt", v_basis[1:], cols(c0b, (1 - h) * half, half),
-            preferred_element_type=F32,
-        )
+        keep = project(slice(1, levels), cols(templates, h * half, half))
+        send = project(slice(1, levels), cols(templates, (1 - h) * half, half))
         rest = keep + swap(send, 0, bits)
     own_coefs = []
     for s in range(levels):
@@ -119,8 +119,8 @@
             jnp.concatenate([mine_b, theirs_b], axis=0),
             jnp.concatenate([theirs_b, mine_b], axis=0),
         )
-        if s == 0 and levels > 2:
-            stacked, sent[1] = lax.optimization_barrier((stacked, sent[1]))
+        if s == 0:
+            stacked, couple_sib = lax.optimization_barrier((stacked, couple_sib))
         coefs = jnp.dot(coupling[s, 0], stacked, preferred_element_type=F32).astype(BF16)
         own_coefs.append(coefs)
         if s < levels - 1:

time: 59 us -> 60.5 us (1.025)
  waiting for transfers between devices: 18 us -> 25.8 us
  starting transfers between devices: 14.4 us -> 10.9 us
  local copies, waits for them, and re-layouts: 4.12 us -> 2.14 us
  matrix products: 17.2 us -> 15.8 us
    ppermute x13, waiting for transfers between devices: 18 us -> 25.8 us  [swap(): return lax.ppermute(x, axis, [(i, i ^ 1 << stride) for i in range(n)])]
    ppermute x13, starting transfers between devices: 14.4 us -> 10.9 us  [swap(): return lax.ppermute(x, axis, [(i, i ^ 1 << stride) for i in range(n)])]
    dot_general x3, matrix products: 3.09 us -> 0.94 us  [on_device(): jnp.einsum('nrs,st->nrt', w_sib[s], cs.astype(F32), preferred_element_typ...]
    sub x1 -> x0, local copies, waits for them, and re-layouts: 1.32 us -> none  [on_device(): current = current - jnp.dot(u_basis[s], full[s], preferred_element_type=F32)]
    slice x1 -> x0, other arithmetic: 1.07 us -> none  [on_device(): w_sib[b] = got[:n].reshape(counts[b], rank, rank)]
    add x1 -> x2, other arithmetic: 0.01 us -> 1.07 us  [on_device(): suffix = suffix[n:] + got[n:]]
    dot_general x2 -> x7, matrix products: 2.49 us -> 3.46 us  [the longest x3 1.95 us: project(): jnp.einsum('lrj,jt->lrt', vl_lo[lv], x, preferred_element_type=F32)]
    concatenate x1, other arithmetic: 0.03 us -> 0.79 us  [on_device(): jnp.concatenate([cross[k, k + 1:].reshape(-1, rank) for k in range(levels...]
  transfers between devices with their start and end apart: 13 -> 13, of which waited for: 8 -> 6; matrix products, arithmetic and copies ran while one was open for 26% -> 23% of each run, Pallas kernels for 0% -> 0%
where the time goes in v14:
time: 60.5 us; the launch traced here: 60.1 us
  waiting for transfers between devices  25.8 us (43%)
  matrix products  15.8 us (26%)
  starting transfers between devices  10.9 us (18%)
  other arithmetic  4.99 us (8%)
  local copies, waits for them, and re-layouts  2.14 us (4%)
    ppermute x13, waiting for transfers between devices, swap(): return lax.ppermute(x, axis, [(i, i ^ 1 << stride) for i in range(n)])  25.8 us
    ppermute x13, starting transfers between devices, swap(): return lax.ppermute(x, axis, [(i, i ^ 1 << stride) for i in range(n)])  10.9 us
    dot_general x3, matrix products, on_device(): jnp.dot(couple_sib[s], stacked, preferred_element_type=F32).astype(BF16)  3.19 us
    dot_general x3, matrix products, project(): jnp.einsum('lrj,jt->lrt', vl_lo[lv], x, preferred_element_type=F32)  1.95 us
    dot_general x4, matrix products, on_device(): jnp.dot(coupling[s, 0], stacked, preferred_element_type=F32).astype(BF16)  1.94 us
    dot_general x1, matrix products, on_device(): c0 = jnp.dot(leaf_inverse, templates, preferred_element_type=F32)  1.83 us
    concatenate x2, other arithmetic, gather_half(): both = jnp.concatenate([x, swap(x, bit, bits), x], axis=-1)  1.79 us
    dot_general x4, matrix products, on_device(): current = current - jnp.dot(u_basis[s], full[s], preferred_element_type=F32)  1.74 us
  transfers between devices with their start and end apart: 13, of which 6 were waited for; matrix products, arithmetic and copies ran while one was open for 23% of the time, Pallas kernels for 0%

profile of v14, /device:TPU:0, one launch (start us, length us, event | category | flops | bytes accessed | tf_op | source)
XLA Modules:
  0.0 60.1 jit_solution(6318486887887884015)
XLA Ops:
  0.0 1.7 %slice_bitcast_fusion.11 = (bf16[128,256]{1,0:T(8,128)(2,1)}, bf16[128,256]{1,0:T(8,128)(2,1)}, bf16[128,256]{1,0:T(8,128)(2,1)}) fusion(bf16[4,1,128,256]{3,2,1,0:T(8,128)(2,1)} %param.9), kind=kLoop, calls=%fused_computation.123 | loop fusion | bytes 393216 | tf_op jit(solution)/shard_map/squeeze | solution.py:66
  1.7 3.0 %collective-permute-start.3 = (bf16[128,256]{1,0:T(8,128)(2,1)}, bf16[128,256]{1,0:T(8,128)(2,1)}, u32[]{:S(2)}, u32[]{:S(2)}) collective-permute-start(bf16[128,256]{1,0:T(8,128)(2,1)} %get-tuple-element.29), channel_id=1, source_target_pairs={{0,4},{4,0},{8,12},{12,8},{1,5},{5,1},{9,13},{13,9},{2,6},{6,2},{1... | collective-permute-start | bytes 196616 | tf_op jit(solution)/shard_map/ppermute | solution.py:21
  4.8 1.5 %collective-permute-start.2 = (bf16[128,256]{1,0:T(8,128)(2,1)}, bf16[128,256]{1,0:T(8,128)(2,1)}, u32[]{:S(2)}, u32[]{:S(2)}) collective-permute-start(bf16[128,256]{1,0:T(8,128)(2,1)} %get-tuple-element.30), channel_id=1, source_target_pairs={{0,2},{2,0},{1,3},{3,1},{4,6},{6,4},{5,7},{7,5},{8,10},{10,8},{9,1... | collective-permute-start | bytes 196616 | tf_op jit(solution)/shard_map/ppermute | solution.py:21
  6.3 1.7 %convolution_bitcast_fusion = f32[4,4,128,128]{3,2,0,1:T(8,128)S(1)} fusion(bf16[4,512,128]{2,1,0:T(8,128)(2,1)} %param.7, bf16[4,512,128]{2,1,0:T(8,128)(2,1)} %param.8), kind=kOutput, calls=%fused_computation.5 | convolution fusion | flops 268435456 | bytes 2097152 | tf_op jit(solution)/shard_map/kis,lir->klrs/dot_general | solution.py:54
  8.0 0.8 %pad_maximum_fusion = f32[768,128]{1,0:T(8,128)} fusion(f32[128,128]{1,0:T(8,128)S(1)} %slice_bitcast_fusion.10, f32[256,128]{1,0:T(8,128)S(1)} %bitcast.162, f32[384,128]{1,0:T(8,128)S(1)} %bitcast.166), kind=kLoop, calls=%fused_computation.50 | loop fusion | flops 196608 | bytes 786432 | tf_op jit(solution)/shard_map/concatenate | solution.py:56
  10.9 1.3 %convolution_add_fusion = f32[3,128,512]{2,1,0:T(8,128)} fusion(f32[3,128,512]{2,1,0:T(8,128)S(1)} %fusion.16, bf16[4,128,512]{2,1,0:T(8,128)(2,1)S(1)} %get-tuple-element.21, bf16[512,1024]{1,0:T(8,128)(2,1)S(1)} %copy-done, s32[]{:T(128)S(6)} %select_n.56), kind=kOutput, calls=%fused_computation.6 | convolution fusion | flops 201523200 | bytes 2621444 | tf_op jit(solution)/shard_map/lrj,jt->lrt/dot_general | solution.py:75
  13.1 1.3 %maximum_select_fusion = bf16[256,1024]{1,0:T(8,128)(2,1)S(1)} fusion(bf16[128,1024]{1,0:T(8,128)(2,1)} %collective-permute-done, bf16[128,1024]{1,0:T(8,128)(2,1)S(1)} %fusion.3, pred[]{:T(512)S(6)} %eq.12), kind=kLoop, calls=%fused_computation.35 | loop fusion | flops 2359296 | bytes 1048577 | tf_op jit(solution)/shard_map/jit(_where)/select_n | solution.py:117
  14.4 1.2 %convolution_convert_fusion = bf16[1024,128]{1,0:T(8,128)(2,1)S(1)} fusion(bf16[256,1024]{1,0:T(8,128)(2,1)S(1)} %maximum_select_fusion, bf16[4,1,128,256]{3,2,1,0:T(8,128)(2,1)} %param.9), kind=kOutput, calls=%fused_computation.13 | convolution fusion | flops 67239936 | bytes 851968 | tf_op jit(solution)/shard_map/dot_general | solution.py:124
  15.6 1.1 %fusion.92 = bf16[128,1024]{1,0:T(8,128)(2,1)S(1)} fusion(bf16[128,256]{1,0:T(8,128)(2,1)} %collective-permute-done.1, bf16[256,1024]{1,0:T(8,128)(2,1)S(1)} %maximum_select_fusion), kind=kOutput, calls=%fused_computation.145 | convolution fusion | flops 67108864 | bytes 851968 | tf_op jit(solution)/shard_map/dot_general | solution.py:127
  17.2 1.1 %slice_add_fusion = (f32[384,128]{1,0:T(8,128)S(1)}, f32[384,128]{1,0:T(8,128)S(1)}) fusion(f32[768,128]{1,0:T(8,128)} %collective-permute-done.5, f32[128,128]{1,0:T(8,128)S(1)} %copy-done.6, f32[256,128]{1,0:T(8,128)S(1)} %bitcast.163), kind=kLoop, calls=%fused_computation.74 | loop fusion | flops 98304 | bytes 983040 | tf_op jit(solution)/shard_map/add | solution.py:65
  18.2 0.6 %collective-permute-start.6 = (f32[384,128]{1,0:T(8,128)S(1)}, f32[384,128]{1,0:T(8,128)S(1)}, u32[]{:S(2)}, u32[]{:S(2)}) collective-permute-start(f32[384,128]{1,0:T(8,128)S(1)} %get-tuple-element.23), channel_id=1, source_target_pairs={{0,2},{2,0},{1,3},{3,1},{4,6},{6,4},{5,7},{7,5},{8,10},{10,8},{9,1... | collective-permute-start | bytes 589832 | tf_op jit(solution)/shard_map/ppermute | solution.py:21
  19.3 5.8 %collective-permute-done.6 = f32[384,128]{1,0:T(8,128)S(1)} collective-permute-done((f32[384,128]{1,0:T(8,128)S(1)}, f32[384,128]{1,0:T(8,128)S(1)}, u32[]{:S(2)}, u32[]{:S(2)}) %collective-permute-start.6) | collective-permute-done | bytes 196640 | tf_op jit(solution)/shard_map/ppermute | solution.py:21
  25.7 0.6 %collective-permute-start.7 = (bf16[512,256]{1,0:T(8,128)(2,1)S(1)}, bf16[512,256]{1,0:T(8,128)(2,1)S(1)}, u32[]{:S(2)}, u32[]{:S(2)}) collective-permute-start(bf16[512,256]{1,0:T(8,128)(2,1)S(1)} %pad_maximum_fusion.2), channel_id=1, source_target_pairs={{0,2},{2,0},{1,3},{3,1},{4,6},{6,4},{5,7},{7,5},{8,10},{10,8},{9,1... | collective-permute-start | bytes 786440 | tf_op jit(solution)/shard_map/ppermute | solution.py:21
  26.6 6.5 %collective-permute-done.7 = bf16[512,256]{1,0:T(8,128)(2,1)S(1)} collective-permute-done((bf16[512,256]{1,0:T(8,128)(2,1)S(1)}, bf16[512,256]{1,0:T(8,128)(2,1)S(1)}, u32[]{:S(2)}, u32[]{:S(2)}) %collective-permute-start.7) | collective-permute-done | bytes 262176 | tf_op jit(solution)/shard_map/ppermute | solution.py:21
  33.5 1.1 %fusion.85 = bf16[128,512]{1,0:T(8,128)(2,1)S(1)} fusion(bf16[128,256]{1,0:T(8,128)(2,1)} %collective-permute-done.2, bf16[128,256]{1,0:T(8,128)(2,1)S(1)} %get-tuple-element.28, bf16[128,256]{1,0:T(8,128)(2,1)S(1)} %get-tuple-element.27, bf16[128,512]{1,0:T(8,128)(2,1)S(1)} %fusion.39, pred[]{:T(512)S(6)} %eq.13), kind=kOutput, calls=%fused_computation.138 | convolution fusion | flops 35258368 | bytes 458753 | tf_op jit(solution)/shard_map/dot_general | solution.py:127
  35.7 4.5 %collective-permute-done.9 = bf16[512,128]{1,0:T(8,128)(2,1)S(1)} collective-permute-done((bf16[512,128]{1,0:T(8,128)(2,1)S(1)}, bf16[512,128]{1,0:T(8,128)(2,1)S(1)}, u32[]{:S(2)}, u32[]{:S(2)}) %collective-permute-start.9) | collective-permute-done | bytes 131104 | tf_op jit(solution)/shard_map/ppermute | solution.py:21
  40.5 1.1 %convolution_convert_fusion.3 = bf16[128,256]{1,0:T(8,128)(2,1)S(1)} fusion(bf16[128,256]{1,0:T(8,128)(2,1)} %collective-permute-done.3, bf16[128,128]{1,0:T(8,128)(2,1)S(1)} %get-tuple-element.34, bf16[128,128]{1,0:T(8,128)(2,1)S(1)} %get-tuple-element.35, bf16[128,256]{1,0:T(8,128)(2,1)S(1)} %get-tuple-element.25, pred[]{:T(512)S(6)} %eq.14), kind=kOutput, calls=%fused_computation.26 | convolution fusion | flops 17661952 | bytes 262145 | tf_op jit(solution)/shard_map/dot_general | solution.py:127
  42.1 2.7 %collective-permute-start.10 = (bf16[256,128]{1,0:T(8,128)(2,1)S(1)}, bf16[256,128]{1,0:T(8,128)(2,1)S(1)}, u32[]{:S(2)}, u32[]{:S(2)}) collective-permute-start(bf16[256,128]{1,0:T(8,128)(2,1)S(1)} %pad_maximum_fusion.5), channel_id=1, source_target_pairs={{0,8},{4,12},{8,0},{12,4},{1,9},{5,13},{9,1},{13,5},{2,10},{6,14},... | collective-permute-start | bytes 196616 | tf_op jit(solution)/shard_map/ppermute | solution.py:21
  44.7 3.2 %collective-permute-done.10 = bf16[256,128]{1,0:T(8,128)(2,1)S(1)} collective-permute-done((bf16[256,128]{1,0:T(8,128)(2,1)S(1)}, bf16[256,128]{1,0:T(8,128)(2,1)S(1)}, u32[]{:S(2)}, u32[]{:S(2)}) %collective-permute-start.10) | collective-permute-done | bytes 65568 | tf_op jit(solution)/shard_map/ppermute | solution.py:21
  48.7 4.5 %collective-permute-done.11 = bf16[2,128,256]{1,2,0:T(8,128)(2,1)S(1)} collective-permute-done((bf16[2,128,256]{1,2,0:T(8,128)(2,1)S(1)}, bf16[2,128,256]{1,2,0:T(8,128)(2,1)S(1)}, u32[]{:S(2)}, u32[]{:S(2)}) %collective-permute-start.11) | collective-permute-done | bytes 131104 | tf_op jit(solution)/shard_map/ppermute | solution.py:21
  53.2 0.6 fusion.29
  54.4 1.3 %collective-permute-done.12 = bf16[3,128,512]{1,2,0:T(8,128)(2,1)S(1)} collective-permute-done((bf16[3,128,512]{1,2,0:T(8,128)(2,1)S(1)}, bf16[3,128,512]{1,2,0:T(8,128)(2,1)S(1)}, u32[]{:S(2)}, u32[]{:S(2)}) %collective-permute-start.12) | collective-permute-done | bytes 393248 | tf_op jit(solution)/shard_map/ppermute | solution.py:21
  55.6 1.2 %fusion.11 = bf16[3,128,1024]{1,2,0:T(8,128)(2,1)S(1)} fusion(s32[]{:T(128)S(6)} %select_n.65, bf16[1,128,512]{1,2,0:T(8,128)(2,1)S(1)} %bitcast.165, bf16[2,128,512]{1,2,0:T(8,128)(2,1)S(1)} %fusion.29, bf16[3,128,512]{1,2,0:T(8,128)(2,1)S(1)} %collective-permute-done.12), kind=kLoop, calls=%fused_computation.33 | loop fusion | flops 3932160 | bytes 1572868 | tf_op jit(solution)/shard_map/concatenate | solution.py:44
  58.3 1.8 %fusion = bf16[512,1024]{1,0:T(8,128)(2,1)} fusion(f32[1024,512]{0,1:T(8,128)S(1)} %fusion.31, f32[1024,512]{0,1:T(8,128)S(1)} %fusion.32, f32[1024,512]{0,1:T(8,128)S(1)} %fusion.33, f32[1024,512]{0,1:T(8,128)S(1)} %fusion.54, bf16[512,512]{1,0:T(8,128)(2,1)S(1)} %copy-done.4, bf16[512,1024]{1,0:T(8,128)(2,1)S(1)} %copy-done), kind=kOutput, calls=%fused_computation.1 | convolution fusion | flops 539492352 | bytes 11010048 | tf_op jit(solution)/shard_map/dot_general | solution.py:52
  (75 shorter events, 9.8 us)
Async XLA Ops:
  0.0 9.8 %copy-start = (bf16[512,1024]{1,0:T(8,128)(2,1)S(1)}, bf16[512,1024]{1,0:T(8,128)(2,1)}, u32[]{:S(2)}) copy-start(bf16[512,1024]{1,0:T(8,128)(2,1)} %param.5) | copy-start | bytes 3145732
  0.0 9.3 %copy-start.2 = (bf16[4,512,128]{2,1,0:T(8,128)(2,1)S(1)}, bf16[4,512,128]{2,1,0:T(8,128)(2,1)}, u32[]{:S(2)}) copy-start(bf16[4,512,128]{2,1,0:T(8,128)(2,1)} %param.7) | copy-start | bytes 1572868
  0.0 9.3 %copy-start.3 = (bf16[512,512]{1,0:T(8,128)(2,1)S(1)}, bf16[512,512]{1,0:T(8,128)(2,1)}, u32[]{:S(2)}) copy-start(bf16[512,512]{1,0:T(8,128)(2,1)} %param.6) | copy-start | bytes 1572868
  1.7 12.6 %collective-permute-start.3 = (bf16[128,256]{1,0:T(8,128)(2,1)}, bf16[128,256]{1,0:T(8,128)(2,1)}, u32[]{:S(2)}, u32[]{:S(2)}) collective-permute-start(bf16[128,256]{1,0:T(8,128)(2,1)} %get-tuple-element.29), channel_id=1, source_target_pairs={{0,4},{4,0},{8,12},{12,8},{1,5},{5,1},{9,13},{13,9},{2,6},{6,2},{1... | collective-permute-start | bytes 196616 | tf_op jit(solution)/shard_map/ppermute | solution.py:21
  4.8 9.6 %collective-permute-start.2 = (bf16[128,256]{1,0:T(8,128)(2,1)}, bf16[128,256]{1,0:T(8,128)(2,1)}, u32[]{:S(2)}, u32[]{:S(2)}) collective-permute-start(bf16[128,256]{1,0:T(8,128)(2,1)} %get-tuple-element.30), channel_id=1, source_target_pairs={{0,2},{2,0},{1,3},{3,1},{4,6},{6,4},{5,7},{7,5},{8,10},{10,8},{9,1... | collective-permute-start | bytes 196616 | tf_op jit(solution)/shard_map/ppermute | solution.py:21
  6.2 8.1 %collective-permute-start.1 = (bf16[128,256]{1,0:T(8,128)(2,1)}, bf16[128,256]{1,0:T(8,128)(2,1)}, u32[]{:S(2)}, u32[]{:S(2)}) collective-permute-start(bf16[128,256]{1,0:T(8,128)(2,1)} %get-tuple-element.31), channel_id=1, source_target_pairs={{0,1},{1,0},{2,3},{3,2},{4,5},{5,4},{6,7},{7,6},{8,9},{9,8},{10,11... | collective-permute-start | bytes 196616 | tf_op jit(solution)/shard_map/ppermute | solution.py:21
  7.9 2.2 %copy-start.5 = (f32[128,128]{1,0:T(8,128)}, f32[128,128]{1,0:T(8,128)S(1)}, u32[]{:S(2)}) copy-start(f32[128,128]{1,0:T(8,128)S(1)} %slice_bitcast_fusion.10) | copy-start | bytes 196612
  8.8 8.4 %collective-permute-start.5 = (f32[768,128]{1,0:T(8,128)}, f32[768,128]{1,0:T(8,128)}, u32[]{:S(2)}, u32[]{:S(2)}) collective-permute-start(f32[768,128]{1,0:T(8,128)} %pad_maximum_fusion), channel_id=1, source_target_pairs={{0,1},{1,0},{2,3},{3,2},{4,5},{5,4},{6,7},{7,6},{8,9},{9,8},{10,11... | collective-permute-start | bytes 1179656 | tf_op jit(solution)/shard_map/ppermute | solution.py:21
  10.4 2.1 %collective-permute-start = (bf16[128,1024]{1,0:T(8,128)(2,1)S(1)}, bf16[128,1024]{1,0:T(8,128)(2,1)}, u32[]{:S(2)}, u32[]{:S(2)}) collective-permute-start(bf16[128,1024]{1,0:T(8,128)(2,1)S(1)} %fusion.3), channel_id=1, source_target_pairs={{0,1},{1,0},{2,3},{3,2},{4,5},{5,4},{6,7},{7,6},{8,9},{9,8},{10,11... | collective-permute-start | bytes 786440 | tf_op jit(solution)/shard_map/ppermute | solution.py:21
  12.5 4.6 %copy-start.6 = (f32[128,128]{1,0:T(8,128)S(1)}, f32[128,128]{1,0:T(8,128)}, u32[]{:S(2)}) copy-start(f32[128,128]{1,0:T(8,128)} %copy-done.5) | copy-start | bytes 196612
  12.5 12.6 %collective-permute-start.4 = (f32[3,128,512]{2,1,0:T(8,128)}, f32[3,128,512]{2,1,0:T(8,128)S(1)}, u32[]{:S(2)}, u32[]{:S(2)}) collective-permute-start(f32[3,128,512]{2,1,0:T(8,128)} %convolution_add_fusion), channel_id=1, source_target_pairs={{0,1},{1,0},{2,3},{3,2},{4,5},{5,4},{6,7},{7,6},{8,9},{9,8},{10,11... | collective-permute-start | bytes 2359304 | tf_op jit(solution)/shard_map/ppermute | solution.py:21
  18.2 6.9 %collective-permute-start.6 = (f32[384,128]{1,0:T(8,128)S(1)}, f32[384,128]{1,0:T(8,128)S(1)}, u32[]{:S(2)}, u32[]{:S(2)}) collective-permute-start(f32[384,128]{1,0:T(8,128)S(1)} %get-tuple-element.23), channel_id=1, source_target_pairs={{0,2},{2,0},{1,3},{3,1},{4,6},{6,4},{5,7},{7,5},{8,10},{10,8},{9,1... | collective-permute-start | bytes 589832 | tf_op jit(solution)/shard_map/ppermute | solution.py:21
  25.1 1.2 %copy-start.7 = (f32[384,128]{1,0:T(8,128)}, f32[384,128]{1,0:T(8,128)S(1)}, u32[]{:S(2)}) copy-start(f32[384,128]{1,0:T(8,128)S(1)} %collective-permute-done.6) | copy-start | bytes 589828
  25.5 7.6 %copy-start.8 = (bf16[4,1,128,256]{3,2,1,0:T(8,128)(2,1)S(1)}, bf16[4,1,128,256]{3,2,1,0:T(8,128)(2,1)}, u32[]{:S(2)}) copy-start(bf16[4,1,128,256]{3,2,1,0:T(8,128)(2,1)} %param.9) | copy-start | bytes 786436
  25.7 7.5 %collective-permute-start.7 = (bf16[512,256]{1,0:T(8,128)(2,1)S(1)}, bf16[512,256]{1,0:T(8,128)(2,1)S(1)}, u32[]{:S(2)}, u32[]{:S(2)}) collective-permute-start(bf16[512,256]{1,0:T(8,128)(2,1)S(1)} %pad_maximum_fusion.2), channel_id=1, source_target_pairs={{0,2},{2,0},{1,3},{3,1},{4,6},{6,4},{5,7},{7,5},{8,10},{10,8},{9,1... | collective-permute-start | bytes 786440 | tf_op jit(solution)/shard_map/ppermute | solution.py:21
  26.3 8.2 %slice-start = ((f32[384,128]{1,0:T(8,128)}), f32[256,128]{1,0:T(8,128)S(1)}, s32[]{:S(2)}) async-start(f32[384,128]{1,0:T(8,128)} %copy-done.7), calls=%async_computation | async-start | bytes 262144 | tf_op jit(solution)/shard_map/slice | solution.py:64
  26.3 8.9 %collective-permute-start.8 = (f32[128,128]{1,0:T(8,128)S(1)}, f32[128,128]{1,0:T(8,128)S(1)}, u32[]{:S(2)}, u32[]{:S(2)}) collective-permute-start(f32[128,128]{1,0:T(8,128)S(1)} %slice_add_fusion.1), channel_id=1, source_target_pairs={{0,4},{4,0},{8,12},{12,8},{1,5},{5,1},{9,13},{13,9},{2,6},{6,2},{1... | collective-permute-start | bytes 196616 | tf_op jit(solution)/shard_map/ppermute | solution.py:21
  35.2 5.0 %collective-permute-start.9 = (bf16[512,128]{1,0:T(8,128)(2,1)S(1)}, bf16[512,128]{1,0:T(8,128)(2,1)S(1)}, u32[]{:S(2)}, u32[]{:S(2)}) collective-permute-start(bf16[512,128]{1,0:T(8,128)(2,1)S(1)} %pad_maximum_fusion.3), channel_id=1, source_target_pairs={{0,4},{4,0},{8,12},{12,8},{1,5},{5,1},{9,13},{13,9},{2,6},{6,2},{1... | collective-permute-start | bytes 393224 | tf_op jit(solution)/shard_map/ppermute | solution.py:21
  40.5 13.4 %copy-start.1 = (bf16[4,512,128]{2,1,0:T(8,128)(2,1)S(1)}, bf16[4,512,128]{2,1,0:T(8,128)(2,1)}, u32[]{:S(2)}) copy-start(bf16[4,512,128]{2,1,0:T(8,128)(2,1)} %param.8) | copy-start | bytes 1572868
  42.1 5.8 %collective-permute-start.10 = (bf16[256,128]{1,0:T(8,128)(2,1)S(1)}, bf16[256,128]{1,0:T(8,128)(2,1)S(1)}, u32[]{:S(2)}, u32[]{:S(2)}) collective-permute-start(bf16[256,128]{1,0:T(8,128)(2,1)S(1)} %pad_maximum_fusion.5), channel_id=1, source_target_pairs={{0,8},{4,12},{8,0},{12,4},{1,9},{5,13},{9,1},{13,5},{2,10},{6,14},... | collective-permute-start | bytes 196616 | tf_op jit(solution)/shard_map/ppermute | solution.py:21
  48.2 5.0 %collective-permute-start.11 = (bf16[2,128,256]{1,2,0:T(8,128)(2,1)S(1)}, bf16[2,128,256]{1,2,0:T(8,128)(2,1)S(1)}, u32[]{:S(2)}, u32[]{:S(2)}) collective-permute-start(bf16[2,128,256]{1,2,0:T(8,128)(2,1)S(1)} %pad_maximum_fusion.4), channel_id=1, source_target_pairs={{0,2},{2,0},{1,3},{3,1},{4,6},{6,4},{5,7},{7,5},{8,10},{10,8},{9,1... | collective-permute-start | bytes 393224 | tf_op jit(solution)/shard_map/ppermute | solution.py:21
  53.8 1.8 %collective-permute-start.12 = (bf16[3,128,512]{1,2,0:T(8,128)(2,1)S(1)}, bf16[3,128,512]{1,2,0:T(8,128)(2,1)S(1)}, u32[]{:S(2)}, u32[]{:S(2)}) collective-permute-start(bf16[3,128,512]{1,2,0:T(8,128)(2,1)S(1)} %pad_maximum_fusion.1), channel_id=1, source_target_pairs={{0,1},{1,0},{2,3},{3,2},{4,5},{5,4},{6,7},{7,6},{8,9},{9,8},{10,11... | collective-permute-start | bytes 1179656 | tf_op jit(solution)/shard_map/ppermute | solution.py:21
  57.3 1.0 %copy-start.4 = (bf16[512,512]{1,0:T(8,128)(2,1)S(1)}, bf16[512,512]{1,0:T(8,128)(2,1)}, u32[]{:S(2)}) copy-start(bf16[512,512]{1,0:T(8,128)(2,1)} %param.6) | copy-start | bytes 1572868

commit v15 on v13

--- a/solution.py
+++ b/solution.py
@@ -97,19 +97,30 @@
             "lrj,jt->lrt", vl_hi[lv], x, preferred_element_type=F32
         ) + jnp.einsum("lrj,jt->lrt", vl_lo[lv], x, preferred_element_type=F32)
 
-    proj0 = project(slice(0, 1), templates)[0]
+    proj0 = project(slice(0, 1), templates)[0].astype(BF16)
     rest = None
+    half = width // 2
     if levels > 1:
-        half = width // 2
         h = side(0, bits)
         keep = project(slice(1, levels), cols(templates, h * half, half))
         send = project(slice(1, levels), cols(templates, (1 - h) * half, half))
-        rest = keep + swap(send, 0, bits)
+        got0 = swap(
+            jnp.concatenate(
+                [proj0[:, :half], proj0[:, half:],
+                 send.astype(BF16).reshape((levels - 1) * rank, half)],
+                axis=0,
+            ),
+            0,
+            bits,
+        )
+        theirs0 = jnp.concatenate([got0[:rank], got0[rank : 2 * rank]], axis=1)
+        rest = keep + got0[2 * rank :].reshape(levels - 1, rank, half).astype(F32)
+    else:
+        theirs0 = swap(proj0, 0, bits)
     own_coefs = []
     for s in range(levels):
         if s == 0:
-            mine_b = proj0.astype(BF16)
-            theirs_b = swap(mine_b, s, bits)
+            mine_b, theirs_b = proj0, theirs0
         else:
             mine_b = rest[0].astype(BF16)
             rest = rest[1:]

time: 57.1 us -> 57.8 us (1.012)
  matrix products: 13.7 us -> 8.88 us
  local copies, waits for them, and re-layouts: 4.07 us -> 8.51 us
  other arithmetic: 7.28 us -> 8.21 us
    slice x0 -> x3, local copies, waits for them, and re-layouts: none -> 2.75 us  [the longest x1 1.02 us: on_device(): rest = keep + got0[2 * rank:].reshape(levels - 1, rank, half).astype(F32)]
    dot_general x3, matrix products: 3.79 us -> 1.07 us  [project(): jnp.einsum('lrj,jt->lrt', vl_lo[lv], x, preferred_element_type=F32)]
    slice x2, local copies, waits for them, and re-layouts: 0.05 us -> 1.29 us  [on_device(): parts = [jnp.concatenate([c[:, :rank], c[:, rank:]], axis=0).astype(F32)]]
    dot_general x1, matrix products: 1.5 us -> 0.47 us  [on_device(): jnp.einsum('lir,ij->lrj', v_basis, leaf_inverse, preferred_element_type=F32)]
    dot_general x4, matrix products: 2 us -> 0.99 us  [on_device(): coefs = jnp.dot(couple[s], stacked, preferred_element_type=F32).astype(BF16)]
    concatenate x0 -> x1, other arithmetic: none -> 0.88 us  [on_device(): jnp.concatenate([proj0[:, :half], proj0[:, half:], send.astype(BF16).resh...]
    select_n x4, other arithmetic: 0.9 us -> 0.13 us  [on_device(): jnp.where(lower, first, second)]
    concatenate x2, other arithmetic: 1.79 us -> 2.38 us  [gather_half(): both = jnp.concatenate([x, swap(x, bit, bits), x], axis=-1)]
  transfers between devices with their start and end apart: 11 -> 10, of which waited for: 6 -> 6; matrix products, arithmetic and copies ran while one was open for 30% -> 28% of each run, Pallas kernels for 0% -> 0%
where the time goes in v15:
time: 57.8 us; the launch traced here: 57.3 us
  waiting for transfers between devices  19.1 us (33%)
  starting transfers between devices  11.8 us (20%)
  matrix products  8.88 us (15%)
  local copies, waits for them, and re-layouts  8.51 us (15%)
  other arithmetic  8.21 us (14%)
  between operations  0.79 us (1%)
    ppermute x10, waiting for transfers between devices, swap(): return lax.ppermute(x, axis, [(i, i ^ 1 << stride) for i in range(n)])  19.1 us
    ppermute x10, starting transfers between devices, swap(): return lax.ppermute(x, axis, [(i, i ^ 1 << stride) for i in range(n)])  11.8 us
    concatenate x2, other arithmetic, gather_half(): both = jnp.concatenate([x, swap(x, bit, bits), x], axis=-1)  2.38 us
    dot_general x1, matrix products, on_device(): c0 = jnp.dot(leaf_inverse, templates, preferred_element_type=F32)  1.84 us
    add x3, other arithmetic, on_device(): partial[s] = partial[s] + recv  1.82 us
    dot_general x4, matrix products, on_device(): current = current - jnp.dot(u_basis[s], full[s], preferred_element_type=F32)  1.73 us
    unnamed x54, local copies, waits for them, and re-layouts  1.29 us
    slice x2, local copies, waits for them, and re-layouts, on_device(): parts = [jnp.concatenate([c[:, :rank], c[:, rank:]], axis=0).astype(F32)]  1.29 us
  transfers between devices with their start and end apart: 10, of which 6 were waited for; matrix products, arithmetic and copies ran while one was open for 28% of the time, Pallas kernels for 0%

profile of v15, /device:TPU:0, one launch (start us, length us, event | category | flops | bytes accessed | tf_op | source)
XLA Modules:
  0.0 57.3 jit_solution(17253790786156872091)
XLA Ops:
  0.0 1.1 %slice_bitcast_fusion.12 = (bf16[128,256]{1,0:T(8,128)(2,1)S(1)}, bf16[128,256]{1,0:T(8,128)(2,1)S(1)}, bf16[128,256]{1,0:T(8,128)(2,1)S(1)}, bf16[128,256]{1,0:T(8,128)(2,1)S(1)}) fusion(bf16[4,1,128,256]{3,2,1,0:T(8,128)(2,1)} %param.9), kind=kLoop, calls=%fused_computation.167 | loop fusion | bytes 524288 | tf_op jit(solution)/shard_map/squeeze | solution.py:81
  2.4 4.0 %collective-permute-start.6 = (bf16[256,128]{1,0:T(8,128)(2,1)}, bf16[256,128]{1,0:T(8,128)(2,1)}, u32[]{:S(2)}, u32[]{:S(2)}) collective-permute-start(bf16[256,128]{1,0:T(8,128)(2,1)} %fusion.100), channel_id=1, source_target_pairs={{0,8},{4,12},{8,0},{12,4},{1,9},{5,13},{9,1},{13,5},{2,10},{6,14},... | collective-permute-start | bytes 196616 | tf_op jit(solution)/shard_map/ppermute | solution.py:21
  8.2 0.8 %pad_maximum_fusion.1 = f32[1024,128]{1,0:T(8,128)} fusion(f32[128,128]{1,0:T(8,128)S(1)} %fusion.82, f32[256,128]{1,0:T(8,128)S(1)} %fusion.86, f32[384,128]{1,0:T(8,128)S(1)} %fusion.89, f32[256,128]{1,0:T(8,128)S(1)} %fusion.103), kind=kLoop, calls=%fused_computation.30 | loop fusion | flops 393216 | bytes 1048576 | tf_op jit(solution)/shard_map/concatenate | solution.py:66
  10.2 0.7 %fusion.123 = (bf16[128,512]{1,0:T(8,128)(2,1)S(1)}, bf16[128,512]{1,0:T(8,128)(2,1)}) fusion(bf16[128,1024]{1,0:T(8,128)(2,1)S(1)} %fusion.2), kind=kLoop, calls=%fused_computation.197 | loop fusion | bytes 524288 | tf_op jit(solution)/shard_map/slice | solution.py:109
  12.2 0.9 %pad_maximum_fusion = bf16[640,512]{1,0:T(8,128)(2,1)} fusion(bf16[384,512]{1,0:T(8,128)(2,1)S(1)} %bitcast.128, bf16[128,512]{1,0:T(8,128)(2,1)S(1)} %copy-done.9, bf16[128,512]{1,0:T(8,128)(2,1)S(1)} %get-tuple-element.19), kind=kLoop, calls=%fused_computation.29 | loop fusion | flops 1966080 | bytes 1310720 | tf_op jit(solution)/shard_map/concatenate | solution.py:108
  14.8 0.8 %fusion.129 = (bf16[128,128]{1,0:T(8,128)(2,1)S(1)}, bf16[128,128]{1,0:T(8,128)(2,1)S(1)}) fusion(bf16[256,128]{1,0:T(8,128)(2,1)} %collective-permute-done.6), kind=kLoop, calls=%fused_computation.203 | loop fusion | bytes 131072 | tf_op jit(solution)/shard_map/slice | solution.py:68
  15.7 0.9 %slice_add_fusion = f32[256,128]{1,0:T(8,128)S(1)} fusion(f32[256,128]{1,0:T(8,128)S(1)} %fusion.86, f32[1024,128]{1,0:T(8,128)} %collective-permute-done), kind=kLoop, calls=%fused_computation.91 | loop fusion | flops 32768 | bytes 393216 | tf_op jit(solution)/shard_map/add | solution.py:77
  16.6 0.9 %slice_add_fusion.2 = f32[128,128]{1,0:T(8,128)S(1)} fusion(f32[128,128]{1,0:T(8,128)S(1)} %fusion.82, f32[1024,128]{1,0:T(8,128)} %collective-permute-done), kind=kLoop, calls=%fused_computation.161 | loop fusion | flops 16384 | bytes 196608 | tf_op jit(solution)/shard_map/add | solution.py:77
  17.5 1.6 %collective-permute-start.2 = (f32[640,128]{1,0:T(8,128)S(1)}, f32[640,128]{1,0:T(8,128)S(1)}, u32[]{:S(2)}, u32[]{:S(2)}) collective-permute-start(f32[640,128]{1,0:T(8,128)S(1)} %pad_maximum_fusion.3), channel_id=1, source_target_pairs={{0,2},{2,0},{1,3},{3,1},{4,6},{6,4},{5,7},{7,5},{8,10},{10,8},{9,1... | collective-permute-start | bytes 983048 | tf_op jit(solution)/shard_map/ppermute | solution.py:21
  19.1 0.9 %slice.336 = f32[384,128]{1,0:T(8,128)S(1)} slice(f32[1024,128]{1,0:T(8,128)} %collective-permute-done), slice={[256:640], [0:128]} | slice | bytes 393216 | tf_op jit(solution)/shard_map/slice | solution.py:72
  20.0 1.1 %convert.17 = bf16[1024,128]{1,0:T(8,128)(2,1)S(1)} convert(f32[1024,128]{1,0:T(8,128)} %collective-permute-done) | non-fusion elementwise | flops 131072 | bytes 786432 | tf_op jit(solution)/shard_map/convert.6
  21.2 1.0 %fusion.120 = (bf16[128,512]{1,0:T(8,128)(2,1)S(1)}, bf16[128,512]{1,0:T(8,128)(2,1)S(1)}) fusion(bf16[640,512]{1,0:T(8,128)(2,1)} %collective-permute-done.1), kind=kLoop, calls=%fused_computation.194 | loop fusion | bytes 524288 | tf_op jit(solution)/shard_map/slice | solution.py:116
  23.0 1.0 %slice.335 = bf16[384,512]{1,0:T(8,128)(2,1)S(1)} slice(bf16[640,512]{1,0:T(8,128)(2,1)} %collective-permute-done.1), slice={[256:640], [0:512]} | slice | bytes 786432 | tf_op jit(solution)/shard_map/slice | solution.py:117
  25.0 2.5 %collective-permute-done.2 = f32[640,128]{1,0:T(8,128)S(1)} collective-permute-done((f32[640,128]{1,0:T(8,128)S(1)}, f32[640,128]{1,0:T(8,128)S(1)}, u32[]{:S(2)}, u32[]{:S(2)}) %collective-permute-start.2) | collective-permute-done | bytes 327712 | tf_op jit(solution)/shard_map/ppermute | solution.py:21
  27.6 1.6 %collective-permute-start.4 = (f32[384,128]{1,0:T(8,128)S(1)}, f32[384,128]{1,0:T(8,128)S(1)}, u32[]{:S(2)}, u32[]{:S(2)}) collective-permute-start(f32[384,128]{1,0:T(8,128)S(1)} %pad_maximum_fusion.5), channel_id=1, source_target_pairs={{0,4},{4,0},{8,12},{12,8},{1,5},{5,1},{9,13},{13,9},{2,6},{6,2},{1... | collective-permute-start | bytes 589832 | tf_op jit(solution)/shard_map/ppermute | solution.py:21
  29.4 3.5 %collective-permute-done.3 = bf16[512,256]{1,0:T(8,128)(2,1)S(1)} collective-permute-done((bf16[512,256]{1,0:T(8,128)(2,1)S(1)}, bf16[512,256]{1,0:T(8,128)(2,1)S(1)}, u32[]{:S(2)}, u32[]{:S(2)}) %collective-permute-start.3) | collective-permute-done | bytes 262176 | tf_op jit(solution)/shard_map/ppermute | solution.py:21
  33.6 1.6 %collective-permute-start.5 = (bf16[512,128]{1,0:T(8,128)(2,1)S(1)}, bf16[512,128]{1,0:T(8,128)(2,1)S(1)}, u32[]{:S(2)}, u32[]{:S(2)}) collective-permute-start(bf16[512,128]{1,0:T(8,128)(2,1)S(1)} %pad_maximum_fusion.6), channel_id=1, source_target_pairs={{0,4},{4,0},{8,12},{12,8},{1,5},{5,1},{9,13},{13,9},{2,6},{6,2},{1... | collective-permute-start | bytes 393224 | tf_op jit(solution)/shard_map/ppermute | solution.py:21
  35.3 3.3 %collective-permute-done.5 = bf16[512,128]{1,0:T(8,128)(2,1)S(1)} collective-permute-done((bf16[512,128]{1,0:T(8,128)(2,1)S(1)}, bf16[512,128]{1,0:T(8,128)(2,1)S(1)}, u32[]{:S(2)}, u32[]{:S(2)}) %collective-permute-start.5) | collective-permute-done | bytes 131104 | tf_op jit(solution)/shard_map/ppermute | solution.py:21
  39.4 5.1 %collective-permute-done.7 = bf16[256,128]{1,0:T(8,128)(2,1)S(1)} collective-permute-done((bf16[256,128]{1,0:T(8,128)(2,1)S(1)}, bf16[256,128]{1,0:T(8,128)(2,1)S(1)}, u32[]{:S(2)}, u32[]{:S(2)}) %collective-permute-start.7) | collective-permute-done | bytes 65568 | tf_op jit(solution)/shard_map/ppermute | solution.py:21
  44.7 1.6 %collective-permute-start.8 = (bf16[2,128,256]{1,2,0:T(8,128)(2,1)S(1)}, bf16[2,128,256]{1,2,0:T(8,128)(2,1)S(1)}, u32[]{:S(2)}, u32[]{:S(2)}) collective-permute-start(bf16[2,128,256]{1,2,0:T(8,128)(2,1)S(1)} %pad_maximum_fusion.7), channel_id=1, source_target_pairs={{0,2},{2,0},{1,3},{3,1},{4,6},{6,4},{5,7},{7,5},{8,10},{10,8},{9,1... | collective-permute-start | bytes 393224 | tf_op jit(solution)/shard_map/ppermute | solution.py:21
  46.4 3.3 %collective-permute-done.8 = bf16[2,128,256]{1,2,0:T(8,128)(2,1)S(1)} collective-permute-done((bf16[2,128,256]{1,2,0:T(8,128)(2,1)S(1)}, bf16[2,128,256]{1,2,0:T(8,128)(2,1)S(1)}, u32[]{:S(2)}, u32[]{:S(2)}) %collective-permute-start.8) | collective-permute-done | bytes 131104 | tf_op jit(solution)/shard_map/ppermute | solution.py:21
  50.9 1.4 %collective-permute-done.9 = bf16[3,128,512]{1,2,0:T(8,128)(2,1)} collective-permute-done((bf16[3,128,512]{1,2,0:T(8,128)(2,1)S(1)}, bf16[3,128,512]{1,2,0:T(8,128)(2,1)}, u32[]{:S(2)}, u32[]{:S(2)}) %collective-permute-start.9) | collective-permute-done | bytes 393248 | tf_op jit(solution)/shard_map/ppermute | solution.py:21
  52.3 1.8 %fusion.8 = bf16[3,128,1024]{1,2,0:T(8,128)(2,1)S(1)} fusion(s32[]{:T(128)S(6)} %select_n.79, bf16[1,128,512]{1,2,0:T(8,128)(2,1)S(1)} %copy.16, bf16[2,128,512]{1,2,0:T(8,128)(2,1)S(1)} %fusion.34, bf16[3,128,512]{1,2,0:T(8,128)(2,1)} %collective-permute-done.9), kind=kLoop, calls=%fused_computation.25 | loop fusion | flops 3932160 | bytes 1572868 | tf_op jit(solution)/shard_map/concatenate | solution.py:44
  55.4 1.8 %fusion = bf16[512,1024]{1,0:T(8,128)(2,1)} fusion(f32[1024,512]{0,1:T(8,128)S(1)} %fusion.36, f32[1024,512]{0,1:T(8,128)S(1)} %fusion.37, f32[1024,512]{0,1:T(8,128)S(1)} %fusion.38, f32[1024,512]{0,1:T(8,128)S(1)} %fusion.39, bf16[512,512]{1,0:T(8,128)(2,1)S(1)} %copy-done.2, bf16[512,1024]{1,0:T(8,128)(2,1)S(1)} %copy-done), kind=kOutput, calls=%fused_computation.1 | convolution fusion | flops 539492352 | bytes 11010048 | tf_op jit(solution)/shard_map/dot_general | solution.py:52
  (132 shorter events, 13.2 us)
Async XLA Ops:
  0.0 9.6 %copy-start = (bf16[512,1024]{1,0:T(8,128)(2,1)S(1)}, bf16[512,1024]{1,0:T(8,128)(2,1)}, u32[]{:S(2)}) copy-start(bf16[512,1024]{1,0:T(8,128)(2,1)} %param.5) | copy-start | bytes 3145732
  0.0 6.5 %copy-start.1 = (bf16[4,512,128]{2,1,0:T(8,128)(2,1)S(1)}, bf16[4,512,128]{2,1,0:T(8,128)(2,1)}, u32[]{:S(2)}) copy-start(bf16[4,512,128]{2,1,0:T(8,128)(2,1)} %param.7) | copy-start | bytes 1572868
  0.0 6.7 %slice-start = ((bf16[4,512,128]{2,1,0:T(8,128)(2,1)}), bf16[2,512,128]{2,1,0:T(8,128)(2,1)S(1)}, s32[]{:S(2)}) async-start(bf16[4,512,128]{2,1,0:T(8,128)(2,1)} %param.7), calls=%async_computation | async-start | bytes 524288 | tf_op jit(solution)/shard_map/slice | solution.py:57
  0.0 6.5 %copy-start.3 = (bf16[4,512,128]{2,1,0:T(8,128)(2,1)S(1)}, bf16[4,512,128]{2,1,0:T(8,128)(2,1)}, u32[]{:S(2)}) copy-start(bf16[4,512,128]{2,1,0:T(8,128)(2,1)} %param.8) | copy-start | bytes 1572868
  1.1 6.0 %slice-start.1 = ((bf16[4,512,128]{2,1,0:T(8,128)(2,1)}), bf16[3,512,128]{2,1,0:T(8,128)(2,1)S(1)}, s32[]{:S(2)}) async-start(bf16[4,512,128]{2,1,0:T(8,128)(2,1)} %param.7), calls=%async_computation.1 | async-start | bytes 786432 | tf_op jit(solution)/shard_map/slice | solution.py:57
  1.8 4.7 %copy-start.22 = (bf16[128,128]{1,0:T(8,128)(2,1)}, bf16[128,128]{1,0:T(8,128)(2,1)S(1)}, u32[]{:S(2)}) copy-start(bf16[128,128]{1,0:T(8,128)(2,1)S(1)} %get-tuple-element.45) | copy-start | bytes 98308
  1.8 4.7 %copy-start.24 = (bf16[128,128]{1,0:T(8,128)(2,1)}, bf16[128,128]{1,0:T(8,128)(2,1)S(1)}, u32[]{:S(2)}) copy-start(bf16[128,128]{1,0:T(8,128)(2,1)S(1)} %get-tuple-element.46) | copy-start | bytes 98308
  2.4 12.4 %collective-permute-start.6 = (bf16[256,128]{1,0:T(8,128)(2,1)}, bf16[256,128]{1,0:T(8,128)(2,1)}, u32[]{:S(2)}, u32[]{:S(2)}) collective-permute-start(bf16[256,128]{1,0:T(8,128)(2,1)} %fusion.100), channel_id=1, source_target_pairs={{0,8},{4,12},{8,0},{12,4},{1,9},{5,13},{9,1},{13,5},{2,10},{6,14},... | collective-permute-start | bytes 196616 | tf_op jit(solution)/shard_map/ppermute | solution.py:21
  9.1 6.6 %collective-permute-start = (f32[1024,128]{1,0:T(8,128)}, f32[1024,128]{1,0:T(8,128)}, u32[]{:S(2)}, u32[]{:S(2)}) collective-permute-start(f32[1024,128]{1,0:T(8,128)} %pad_maximum_fusion.1), channel_id=1, source_target_pairs={{0,1},{1,0},{2,3},{3,2},{4,5},{5,4},{6,7},{7,6},{8,9},{9,8},{10,11... | collective-permute-start | bytes 1572872 | tf_op jit(solution)/shard_map/ppermute | solution.py:21
  13.1 8.1 %collective-permute-start.1 = (bf16[640,512]{1,0:T(8,128)(2,1)}, bf16[640,512]{1,0:T(8,128)(2,1)}, u32[]{:S(2)}, u32[]{:S(2)}) collective-permute-start(bf16[640,512]{1,0:T(8,128)(2,1)} %pad_maximum_fusion), channel_id=1, source_target_pairs={{0,1},{1,0},{2,3},{3,2},{4,5},{5,4},{6,7},{7,6},{8,9},{9,8},{10,11... | collective-permute-start | bytes 1966088 | tf_op jit(solution)/shard_map/ppermute | solution.py:21
  14.8 6.3 %copy-start.19 = (bf16[128,128]{1,0:T(8,128)(2,1)S(1)}, bf16[128,128]{1,0:T(8,128)(2,1)}, u32[]{:S(2)}) copy-start(bf16[128,128]{1,0:T(8,128)(2,1)} %copy-done.18) | copy-start | bytes 98308
  14.8 6.3 %copy-start.21 = (bf16[128,128]{1,0:T(8,128)(2,1)S(1)}, bf16[128,128]{1,0:T(8,128)(2,1)}, u32[]{:S(2)}) copy-start(bf16[128,128]{1,0:T(8,128)(2,1)} %copy-done.20) | copy-start | bytes 98308
  16.6 5.6 %copy-start.6 = (bf16[128,1024]{1,0:T(8,128)(2,1)S(1)}, bf16[128,1024]{1,0:T(8,128)(2,1)}, u32[]{:S(2)}) copy-start(bf16[128,1024]{1,0:T(8,128)(2,1)} %copy-done.5) | copy-start | bytes 786436
  17.5 10.0 %collective-permute-start.2 = (f32[640,128]{1,0:T(8,128)S(1)}, f32[640,128]{1,0:T(8,128)S(1)}, u32[]{:S(2)}, u32[]{:S(2)}) collective-permute-start(f32[640,128]{1,0:T(8,128)S(1)} %pad_maximum_fusion.3), channel_id=1, source_target_pairs={{0,2},{2,0},{1,3},{3,1},{4,6},{6,4},{5,7},{7,5},{8,10},{10,8},{9,1... | collective-permute-start | bytes 983048 | tf_op jit(solution)/shard_map/ppermute | solution.py:21
  24.3 5.0 %copy-start.15 = (bf16[128,128]{1,0:T(8,128)(2,1)S(1)}, bf16[128,128]{1,0:T(8,128)(2,1)}, u32[]{:S(2)}) copy-start(bf16[128,128]{1,0:T(8,128)(2,1)} %get-tuple-element.53) | copy-start | bytes 98308
  24.3 5.0 %copy-start.17 = (bf16[128,128]{1,0:T(8,128)(2,1)S(1)}, bf16[128,128]{1,0:T(8,128)(2,1)}, u32[]{:S(2)}) copy-start(bf16[128,128]{1,0:T(8,128)(2,1)} %get-tuple-element.54) | copy-start | bytes 98308
  24.4 8.4 %collective-permute-start.3 = (bf16[512,256]{1,0:T(8,128)(2,1)S(1)}, bf16[512,256]{1,0:T(8,128)(2,1)S(1)}, u32[]{:S(2)}, u32[]{:S(2)}) collective-permute-start(bf16[512,256]{1,0:T(8,128)(2,1)S(1)} %pad_maximum_fusion.4), channel_id=1, source_target_pairs={{0,2},{2,0},{1,3},{3,1},{4,6},{6,4},{5,7},{7,5},{8,10},{10,8},{9,1... | collective-permute-start | bytes 786440 | tf_op jit(solution)/shard_map/ppermute | solution.py:21
  27.6 7.6 %collective-permute-start.4 = (f32[384,128]{1,0:T(8,128)S(1)}, f32[384,128]{1,0:T(8,128)S(1)}, u32[]{:S(2)}, u32[]{:S(2)}) collective-permute-start(f32[384,128]{1,0:T(8,128)S(1)} %pad_maximum_fusion.5), channel_id=1, source_target_pairs={{0,4},{4,0},{8,12},{12,8},{1,5},{5,1},{9,13},{13,9},{2,6},{6,2},{1... | collective-permute-start | bytes 589832 | tf_op jit(solution)/shard_map/ppermute | solution.py:21
  33.6 5.0 %collective-permute-start.5 = (bf16[512,128]{1,0:T(8,128)(2,1)S(1)}, bf16[512,128]{1,0:T(8,128)(2,1)S(1)}, u32[]{:S(2)}, u32[]{:S(2)}) collective-permute-start(bf16[512,128]{1,0:T(8,128)(2,1)S(1)} %pad_maximum_fusion.6), channel_id=1, source_target_pairs={{0,4},{4,0},{8,12},{12,8},{1,5},{5,1},{9,13},{13,9},{2,6},{6,2},{1... | collective-permute-start | bytes 393224 | tf_op jit(solution)/shard_map/ppermute | solution.py:21
  39.2 11.3 %copy-start.4 = (bf16[4,512,128]{2,1,0:T(8,128)(2,1)S(1)}, bf16[4,512,128]{2,1,0:T(8,128)(2,1)}, u32[]{:S(2)}) copy-start(bf16[4,512,128]{2,1,0:T(8,128)(2,1)} %param.8) | copy-start | bytes 1572868
  39.2 11.3 %copy-start.8 = (bf16[256,1024]{1,0:T(8,128)(2,1)S(1)}, bf16[256,1024]{1,0:T(8,128)(2,1)}, u32[]{:S(2)}) copy-start(bf16[256,1024]{1,0:T(8,128)(2,1)} %copy-done.7) | copy-start | bytes 1572868
  39.2 5.2 %collective-permute-start.7 = (bf16[256,128]{1,0:T(8,128)(2,1)S(1)}, bf16[256,128]{1,0:T(8,128)(2,1)S(1)}, u32[]{:S(2)}, u32[]{:S(2)}) collective-permute-start(bf16[256,128]{1,0:T(8,128)(2,1)S(1)} %pad_maximum_fusion.20), channel_id=1, source_target_pairs={{0,8},{4,12},{8,0},{12,4},{1,9},{5,13},{9,1},{13,5},{2,10},{6,14},... | collective-permute-start | bytes 196616 | tf_op jit(solution)/shard_map/ppermute | solution.py:21
  44.7 5.0 %collective-permute-start.8 = (bf16[2,128,256]{1,2,0:T(8,128)(2,1)S(1)}, bf16[2,128,256]{1,2,0:T(8,128)(2,1)S(1)}, u32[]{:S(2)}, u32[]{:S(2)}) collective-permute-start(bf16[2,128,256]{1,2,0:T(8,128)(2,1)S(1)} %pad_maximum_fusion.7), channel_id=1, source_target_pairs={{0,2},{2,0},{1,3},{3,1},{4,6},{6,4},{5,7},{7,5},{8,10},{10,8},{9,1... | collective-permute-start | bytes 393224 | tf_op jit(solution)/shard_map/ppermute | solution.py:21
  50.4 1.9 %collective-permute-start.9 = (bf16[3,128,512]{1,2,0:T(8,128)(2,1)S(1)}, bf16[3,128,512]{1,2,0:T(8,128)(2,1)}, u32[]{:S(2)}, u32[]{:S(2)}) collective-permute-start(bf16[3,128,512]{1,2,0:T(8,128)(2,1)S(1)} %pad_maximum_fusion.2), channel_id=1, source_target_pairs={{0,1},{1,0},{2,3},{3,2},{4,5},{5,4},{6,7},{7,6},{8,9},{9,8},{10,11... | collective-permute-start | bytes 1179656 | tf_op jit(solution)/shard_map/ppermute | solution.py:21
  (14 other events, 17.3 us)

commit v16 on v14

--- a/solution.py
+++ b/solution.py
@@ -56,6 +56,7 @@
     suffix = jnp.concatenate(
         [cross[k, k + 1 :].reshape(-1, rank) for k in range(levels - 1)], axis=0
     )
+    first_prep = suffix
     w_own, w_sib = [None] * levels, [None] * levels
     for b in range(levels - 1):
         n = counts[b] * rank
@@ -74,19 +75,28 @@
             "lrj,jt->lrt", vl_hi[lv], x, preferred_element_type=F32
         ) + jnp.einsum("lrj,jt->lrt", vl_lo[lv], x, preferred_element_type=F32)
 
-    proj0 = project(slice(0, 1), templates)[0]
+    proj0 = project(slice(0, 1), templates)[0].astype(BF16)
     rest = None
+    half = width // 2
     if levels > 1:
-        half = width // 2
         h = side(0, bits)
         keep = project(slice(1, levels), cols(templates, h * half, half))
         send = project(slice(1, levels), cols(templates, (1 - h) * half, half))
-        rest = keep + swap(send, 0, bits)
+        payload0 = jnp.concatenate(
+            [proj0[:, :half], proj0[:, half:],
+             send.astype(BF16).reshape((levels - 1) * rank, half)],
+            axis=0,
+        )
+        payload0, first_prep = lax.optimization_barrier((payload0, first_prep))
+        got0 = swap(payload0, 0, bits)
+        theirs0 = jnp.concatenate([got0[:rank], got0[rank : 2 * rank]], axis=1)
+        rest = keep + got0[2 * rank :].reshape(levels - 1, rank, half).astype(F32)
+    else:
+        theirs0 = swap(proj0, 0, bits)
     own_coefs = []
     for s in range(levels):
         if s == 0:
-            mine_b = proj0.astype(BF16)
-            theirs_b = swap(mine_b, s, bits)
+            mine_b, theirs_b = proj0, theirs0
         else:
             mine_b = rest[0].astype(BF16)
             rest = rest[1:]

time: 60.5 us -> 65.6 us (1.084)
  local copies, waits for them, and re-layouts: 2.14 us -> 5.71 us
  waiting for transfers between devices: 25.8 us -> 27 us
  matrix products: 15.8 us -> 16.9 us
  starting transfers between devices: 10.9 us -> 10.2 us
    slice x0 -> x3, local copies, waits for them, and re-layouts: none -> 2.1 us  [the longest x1 1.06 us: on_device(): theirs0 = jnp.concatenate([got0[:rank], got0[rank:2 * rank]], axis=1)]
    unnamed x18, local copies, waits for them, and re-layouts: 0.19 us -> 1.7 us
    ppermute x13 -> x12, waiting for transfers between devices: 25.8 us -> 27 us  [swap(): return lax.ppermute(x, axis, [(i, i ^ 1 << stride) for i in range(n)])]
    dot_general x1, matrix products: 0.47 us -> 1.66 us  [on_device(): jnp.einsum('lir,ij->lrj', v_basis, leaf_inverse, preferred_element_type=F32)]
    select_n x1, other arithmetic: 1.25 us -> 0.12 us  [on_device(): jnp.where(lower, jnp.concatenate([mine_b, theirs_b], axis=0), jnp.concate...]
    dot_general x3, matrix products: 1.95 us -> 1.06 us  [project(): jnp.einsum('lrj,jt->lrt', vl_lo[lv], x, preferred_element_type=F32)]
    concatenate x0 -> x1, other arithmetic: none -> 0.88 us  [on_device(): jnp.concatenate([proj0[:, :half], proj0[:, half:], send.astype(BF16).resh...]
    dot_general x4, matrix products: 1.94 us -> 2.8 us  [on_device(): jnp.dot(coupling[s, 0], stacked, preferred_element_type=F32).astype(BF16)]
  transfers between devices with their start and end apart: 13 -> 12, of which waited for: 6 -> 6; matrix products, arithmetic and copies ran while one was open for 23% -> 19% of each run, Pallas kernels for 0% -> 0%
where the time goes in v16:
time: 65.6 us; the launch traced here: 65.1 us
  waiting for transfers between devices  27 us (41%)
  matrix products  16.9 us (26%)
  starting transfers between devices  10.2 us (16%)
  local copies, waits for them, and re-layouts  5.71 us (9%)
  other arithmetic  4.74 us (7%)
    ppermute x12, waiting for transfers between devices, swap(): return lax.ppermute(x, axis, [(i, i ^ 1 << stride) for i in range(n)])  27 us
    ppermute x12, starting transfers between devices, swap(): return lax.ppermute(x, axis, [(i, i ^ 1 << stride) for i in range(n)])  10.2 us
    dot_general x3, matrix products, on_device(): jnp.dot(couple_sib[s], stacked, preferred_element_type=F32).astype(BF16)  3.13 us
    dot_general x4, matrix products, on_device(): jnp.dot(coupling[s, 0], stacked, preferred_element_type=F32).astype(BF16)  2.8 us
    dot_general x1, matrix products, on_device(): c0 = jnp.dot(leaf_inverse, templates, preferred_element_type=F32)  1.83 us
    concatenate x2, other arithmetic, gather_half(): both = jnp.concatenate([x, swap(x, bit, bits), x], axis=-1)  1.79 us
    dot_general x4, matrix products, on_device(): current = current - jnp.dot(u_basis[s], full[s], preferred_element_type=F32)  1.75 us
    unnamed x18, local copies, waits for them, and re-layouts  1.7 us
  transfers between devices with their start and end apart: 12, of which 6 were waited for; matrix products, arithmetic and copies ran while one was open for 19% of the time, Pallas kernels for 0%

profile of v16, /device:TPU:0, one launch (start us, length us, event | category | flops | bytes accessed | tf_op | source)
XLA Modules:
  0.0 65.1 jit_solution(17383138334939009550)
XLA Ops:
  0.0 1.7 %slice_bitcast_fusion.11 = (bf16[128,256]{1,0:T(8,128)(2,1)}, bf16[128,256]{1,0:T(8,128)(2,1)}, bf16[128,256]{1,0:T(8,128)(2,1)}) fusion(bf16[4,1,128,256]{3,2,1,0:T(8,128)(2,1)} %param.9), kind=kLoop, calls=%fused_computation.125 | loop fusion | bytes 393216 | tf_op jit(solution)/shard_map/squeeze | solution.py:67
  1.7 3.0 %collective-permute-start.3 = (bf16[128,256]{1,0:T(8,128)(2,1)}, bf16[128,256]{1,0:T(8,128)(2,1)}, u32[]{:S(2)}, u32[]{:S(2)}) collective-permute-start(bf16[128,256]{1,0:T(8,128)(2,1)} %get-tuple-element.33), channel_id=1, source_target_pairs={{0,4},{4,0},{8,12},{12,8},{1,5},{5,1},{9,13},{13,9},{2,6},{6,2},{1... | collective-permute-start | bytes 196616 | tf_op jit(solution)/shard_map/ppermute | solution.py:21
  4.7 1.5 %collective-permute-start.2 = (bf16[128,256]{1,0:T(8,128)(2,1)}, bf16[128,256]{1,0:T(8,128)(2,1)}, u32[]{:S(2)}, u32[]{:S(2)}) collective-permute-start(bf16[128,256]{1,0:T(8,128)(2,1)} %get-tuple-element.34), channel_id=1, source_target_pairs={{0,2},{2,0},{1,3},{3,1},{4,6},{6,4},{5,7},{7,5},{8,10},{10,8},{9,1... | collective-permute-start | bytes 196616 | tf_op jit(solution)/shard_map/ppermute | solution.py:21
  6.2 1.7 %convolution_bitcast_fusion = f32[4,4,128,128]{3,2,0,1:T(8,128)S(1)} fusion(bf16[4,512,128]{2,1,0:T(8,128)(2,1)} %param.7, bf16[4,512,128]{2,1,0:T(8,128)(2,1)} %param.8), kind=kOutput, calls=%fused_computation.5 | convolution fusion | flops 268435456 | bytes 2097152 | tf_op jit(solution)/shard_map/kis,lir->klrs/dot_general | solution.py:54
  7.9 0.8 %pad_maximum_fusion.1 = f32[768,128]{1,0:T(8,128)} fusion(f32[128,128]{1,0:T(8,128)S(1)} %slice_bitcast_fusion.10, f32[256,128]{1,0:T(8,128)S(1)} %bitcast.169, f32[384,128]{1,0:T(8,128)S(1)} %bitcast.173), kind=kLoop, calls=%fused_computation.52 | loop fusion | flops 196608 | bytes 786432 | tf_op jit(solution)/shard_map/concatenate | solution.py:56
  9.2 1.7 %subtract_convert_fusion = (bf16[4,128,512]{2,1,0:T(8,128)(2,1)S(1)}, bf16[4,128,512]{2,1,0:T(8,128)(2,1)S(1)}) fusion(bf16[4,512,128]{2,1,0:T(8,128)(2,1)} %param.7, bf16[512,512]{1,0:T(8,128)(2,1)} %param.6), kind=kOutput, calls=%fused_computation.29 | convolution fusion | flops 269484032 | bytes 2097152 | tf_op jit(solution)/shard_map/lir,ij->lrj/dot_general | solution.py:69
  12.3 0.9 %pad_maximum_fusion = bf16[640,512]{1,0:T(8,128)(2,1)} fusion(bf16[384,512]{1,0:T(8,128)(2,1)S(1)} %bitcast.168, bf16[128,512]{1,0:T(8,128)(2,1)S(1)} %get-tuple-element.37, bf16[128,512]{1,0:T(8,128)(2,1)S(1)} %get-tuple-element.36), kind=kLoop, calls=%fused_computation.36 | loop fusion | flops 1966080 | bytes 1310720 | tf_op jit(solution)/shard_map/concatenate | solution.py:85
  14.1 1.1 %slice_add_fusion = (f32[384,128]{1,0:T(8,128)S(1)}, f32[384,128]{1,0:T(8,128)S(1)}) fusion(f32[768,128]{1,0:T(8,128)} %collective-permute-done.4, f32[128,128]{1,0:T(8,128)S(1)} %copy-done.4, f32[256,128]{1,0:T(8,128)S(1)} %bitcast.170), kind=kLoop, calls=%fused_computation.76 | loop fusion | flops 98304 | bytes 983040 | tf_op jit(solution)/shard_map/add | solution.py:66
  16.1 6.4 %collective-permute-done.5 = f32[384,128]{1,0:T(8,128)S(1)} collective-permute-done((f32[384,128]{1,0:T(8,128)S(1)}, f32[384,128]{1,0:T(8,128)S(1)}, u32[]{:S(2)}, u32[]{:S(2)}) %collective-permute-start.5) | collective-permute-done | bytes 196640 | tf_op jit(solution)/shard_map/ppermute | solution.py:21
  22.5 1.1 %fusion.88 = (bf16[128,512]{1,0:T(8,128)(2,1)S(1)}, bf16[128,512]{1,0:T(8,128)(2,1)S(1)}) fusion(bf16[640,512]{1,0:T(8,128)(2,1)} %collective-permute-done), kind=kLoop, calls=%fused_computation.141 | loop fusion | bytes 524288 | tf_op jit(solution)/shard_map/slice | solution.py:92
  23.7 1.2 %convolution_convert_fusion = bf16[1024,128]{1,0:T(8,128)(2,1)S(1)} fusion(bf16[256,1024]{1,0:T(8,128)(2,1)S(1)} %maximum_select_fusion, bf16[4,1,128,256]{3,2,1,0:T(8,128)(2,1)} %param.9), kind=kOutput, calls=%fused_computation.12 | convolution fusion | flops 67239936 | bytes 851968 | tf_op jit(solution)/shard_map/dot_general | solution.py:134
  24.9 1.1 %fusion.96 = bf16[128,1024]{1,0:T(8,128)(2,1)S(1)} fusion(bf16[128,256]{1,0:T(8,128)(2,1)} %collective-permute-done.1, bf16[256,1024]{1,0:T(8,128)(2,1)S(1)} %maximum_select_fusion), kind=kOutput, calls=%fused_computation.149 | convolution fusion | flops 67108864 | bytes 851968 | tf_op jit(solution)/shard_map/dot_general | solution.py:137
  26.5 1.0 %slice.221 = bf16[384,512]{1,0:T(8,128)(2,1)S(1)} slice(bf16[640,512]{1,0:T(8,128)(2,1)} %collective-permute-done), slice={[256:640], [0:512]} | slice | bytes 786432 | tf_op jit(solution)/shard_map/slice | solution.py:93
  29.1 7.1 %collective-permute-done.6 = bf16[512,256]{1,0:T(8,128)(2,1)S(1)} collective-permute-done((bf16[512,256]{1,0:T(8,128)(2,1)S(1)}, bf16[512,256]{1,0:T(8,128)(2,1)S(1)}, u32[]{:S(2)}, u32[]{:S(2)}) %collective-permute-start.6) | collective-permute-done | bytes 262176 | tf_op jit(solution)/shard_map/ppermute | solution.py:21
  36.2 1.1 %convolution_convert_fusion.1 = bf16[512,128]{1,0:T(8,128)(2,1)S(1)} fusion(bf16[4,1,128,256]{3,2,1,0:T(8,128)(2,1)} %param.9, bf16[128,256]{1,0:T(8,128)(2,1)S(1)} %get-tuple-element.32, bf16[128,256]{1,0:T(8,128)(2,1)S(1)} %get-tuple-element.31, bf16[128,512]{1,0:T(8,128)(2,1)S(1)} %fusion.41, pred[]{:T(512)S(6)} %eq.13), kind=kOutput, calls=%fused_computation.19 | convolution fusion | flops 35323904 | bytes 458753 | tf_op jit(solution)/shard_map/dot_general | solution.py:134
  37.4 1.1 %fusion.87 = bf16[128,512]{1,0:T(8,128)(2,1)S(1)} fusion(bf16[128,256]{1,0:T(8,128)(2,1)} %collective-permute-done.2, bf16[128,256]{1,0:T(8,128)(2,1)S(1)} %get-tuple-element.32, bf16[128,256]{1,0:T(8,128)(2,1)S(1)} %get-tuple-element.31, bf16[128,512]{1,0:T(8,128)(2,1)S(1)} %fusion.41, pred[]{:T(512)S(6)} %eq.13), kind=kOutput, calls=%fused_computation.140 | convolution fusion | flops 35258368 | bytes 458753 | tf_op jit(solution)/shard_map/dot_general | solution.py:137
  40.3 4.5 %collective-permute-done.8 = bf16[512,128]{1,0:T(8,128)(2,1)S(1)} collective-permute-done((bf16[512,128]{1,0:T(8,128)(2,1)S(1)}, bf16[512,128]{1,0:T(8,128)(2,1)S(1)}, u32[]{:S(2)}, u32[]{:S(2)}) %collective-permute-start.8) | collective-permute-done | bytes 131104 | tf_op jit(solution)/shard_map/ppermute | solution.py:21
  45.0 1.0 %convolution_convert_fusion.3 = bf16[128,256]{1,0:T(8,128)(2,1)S(1)} fusion(bf16[128,256]{1,0:T(8,128)(2,1)} %collective-permute-done.3, bf16[128,128]{1,0:T(8,128)(2,1)S(1)} %get-tuple-element.40, bf16[128,128]{1,0:T(8,128)(2,1)S(1)} %get-tuple-element.41, bf16[128,256]{1,0:T(8,128)(2,1)S(1)} %get-tuple-element.29, pred[]{:T(512)S(6)} %eq.14), kind=kOutput, calls=%fused_computation.25 | convolution fusion | flops 17661952 | bytes 262145 | tf_op jit(solution)/shard_map/dot_general | solution.py:137
  46.5 2.7 %collective-permute-start.9 = (bf16[256,128]{1,0:T(8,128)(2,1)S(1)}, bf16[256,128]{1,0:T(8,128)(2,1)S(1)}, u32[]{:S(2)}, u32[]{:S(2)}) collective-permute-start(bf16[256,128]{1,0:T(8,128)(2,1)S(1)} %pad_maximum_fusion.6), channel_id=1, source_target_pairs={{0,8},{4,12},{8,0},{12,4},{1,9},{5,13},{9,1},{13,5},{2,10},{6,14},... | collective-permute-start | bytes 196616 | tf_op jit(solution)/shard_map/ppermute | solution.py:21
  49.2 3.2 %collective-permute-done.9 = bf16[256,128]{1,0:T(8,128)(2,1)S(1)} collective-permute-done((bf16[256,128]{1,0:T(8,128)(2,1)S(1)}, bf16[256,128]{1,0:T(8,128)(2,1)S(1)}, u32[]{:S(2)}, u32[]{:S(2)}) %collective-permute-start.9) | collective-permute-done | bytes 65568 | tf_op jit(solution)/shard_map/ppermute | solution.py:21
  53.1 4.6 %collective-permute-done.10 = bf16[2,128,256]{1,2,0:T(8,128)(2,1)S(1)} collective-permute-done((bf16[2,128,256]{1,2,0:T(8,128)(2,1)S(1)}, bf16[2,128,256]{1,2,0:T(8,128)(2,1)S(1)}, u32[]{:S(2)}, u32[]{:S(2)}) %collective-permute-start.10) | collective-permute-done | bytes 131104 | tf_op jit(solution)/shard_map/ppermute | solution.py:21
  58.8 1.3 %collective-permute-done.11 = bf16[3,128,512]{1,2,0:T(8,128)(2,1)S(1)} collective-permute-done((bf16[3,128,512]{1,2,0:T(8,128)(2,1)S(1)}, bf16[3,128,512]{1,2,0:T(8,128)(2,1)S(1)}, u32[]{:S(2)}, u32[]{:S(2)}) %collective-permute-start.11) | collective-permute-done | bytes 393248 | tf_op jit(solution)/shard_map/ppermute | solution.py:21
  60.1 1.2 %fusion.10 = bf16[3,128,1024]{1,2,0:T(8,128)(2,1)S(1)} fusion(s32[]{:T(128)S(6)} %select_n.65, bf16[1,128,512]{1,2,0:T(8,128)(2,1)S(1)} %bitcast.172, bf16[2,128,512]{1,2,0:T(8,128)(2,1)S(1)} %fusion.29, bf16[3,128,512]{1,2,0:T(8,128)(2,1)S(1)} %collective-permute-done.11), kind=kLoop, calls=%fused_computation.32 | loop fusion | flops 3932160 | bytes 1572868 | tf_op jit(solution)/shard_map/concatenate | solution.py:44
  63.2 1.8 %fusion = bf16[512,1024]{1,0:T(8,128)(2,1)} fusion(f32[1024,512]{0,1:T(8,128)S(1)} %fusion.31, f32[1024,512]{0,1:T(8,128)S(1)} %fusion.32, f32[1024,512]{0,1:T(8,128)S(1)} %fusion.33, f32[1024,512]{0,1:T(8,128)S(1)} %fusion.56, bf16[512,512]{1,0:T(8,128)(2,1)S(1)} %copy-done.2, bf16[512,1024]{1,0:T(8,128)(2,1)S(1)} %copy-done), kind=kOutput, calls=%fused_computation.1 | convolution fusion | flops 539492352 | bytes 11010048 | tf_op jit(solution)/shard_map/dot_general | solution.py:52
  (77 shorter events, 12.1 us)
Async XLA Ops:
  0.0 10.9 %copy-start = (bf16[512,1024]{1,0:T(8,128)(2,1)S(1)}, bf16[512,1024]{1,0:T(8,128)(2,1)}, u32[]{:S(2)}) copy-start(bf16[512,1024]{1,0:T(8,128)(2,1)} %param.5) | copy-start | bytes 3145732
  1.7 22.0 %collective-permute-start.3 = (bf16[128,256]{1,0:T(8,128)(2,1)}, bf16[128,256]{1,0:T(8,128)(2,1)}, u32[]{:S(2)}, u32[]{:S(2)}) collective-permute-start(bf16[128,256]{1,0:T(8,128)(2,1)} %get-tuple-element.33), channel_id=1, source_target_pairs={{0,4},{4,0},{8,12},{12,8},{1,5},{5,1},{9,13},{13,9},{2,6},{6,2},{1... | collective-permute-start | bytes 196616 | tf_op jit(solution)/shard_map/ppermute | solution.py:21
  4.7 19.0 %collective-permute-start.2 = (bf16[128,256]{1,0:T(8,128)(2,1)}, bf16[128,256]{1,0:T(8,128)(2,1)}, u32[]{:S(2)}, u32[]{:S(2)}) collective-permute-start(bf16[128,256]{1,0:T(8,128)(2,1)} %get-tuple-element.34), channel_id=1, source_target_pairs={{0,2},{2,0},{1,3},{3,1},{4,6},{6,4},{5,7},{7,5},{8,10},{10,8},{9,1... | collective-permute-start | bytes 196616 | tf_op jit(solution)/shard_map/ppermute | solution.py:21
  6.2 17.5 %collective-permute-start.1 = (bf16[128,256]{1,0:T(8,128)(2,1)}, bf16[128,256]{1,0:T(8,128)(2,1)}, u32[]{:S(2)}, u32[]{:S(2)}) collective-permute-start(bf16[128,256]{1,0:T(8,128)(2,1)} %get-tuple-element.35), channel_id=1, source_target_pairs={{0,1},{1,0},{2,3},{3,2},{4,5},{5,4},{6,7},{7,6},{8,9},{9,8},{10,11... | collective-permute-start | bytes 196616 | tf_op jit(solution)/shard_map/ppermute | solution.py:21
  7.9 3.0 %copy-start.3 = (f32[128,128]{1,0:T(8,128)}, f32[128,128]{1,0:T(8,128)S(1)}, u32[]{:S(2)}) copy-start(f32[128,128]{1,0:T(8,128)S(1)} %slice_bitcast_fusion.10) | copy-start | bytes 196612
  8.7 4.9 %collective-permute-start.4 = (f32[768,128]{1,0:T(8,128)}, f32[768,128]{1,0:T(8,128)}, u32[]{:S(2)}, u32[]{:S(2)}) collective-permute-start(f32[768,128]{1,0:T(8,128)} %pad_maximum_fusion.1), channel_id=1, source_target_pairs={{0,1},{1,0},{2,3},{3,2},{4,5},{5,4},{6,7},{7,6},{8,9},{9,8},{10,11... | collective-permute-start | bytes 1179656 | tf_op jit(solution)/shard_map/ppermute | solution.py:21
  13.2 9.3 %collective-permute-start = (bf16[640,512]{1,0:T(8,128)(2,1)}, bf16[640,512]{1,0:T(8,128)(2,1)}, u32[]{:S(2)}, u32[]{:S(2)}) collective-permute-start(bf16[640,512]{1,0:T(8,128)(2,1)} %pad_maximum_fusion), channel_id=1, source_target_pairs={{0,1},{1,0},{2,3},{3,2},{4,5},{5,4},{6,7},{7,6},{8,9},{9,8},{10,11... | collective-permute-start | bytes 1966088 | tf_op jit(solution)/shard_map/ppermute | solution.py:21
  13.2 0.8 %copy-start.4 = (f32[128,128]{1,0:T(8,128)S(1)}, f32[128,128]{1,0:T(8,128)}, u32[]{:S(2)}) copy-start(f32[128,128]{1,0:T(8,128)} %copy-done.3) | copy-start | bytes 196612
  15.1 7.4 %collective-permute-start.5 = (f32[384,128]{1,0:T(8,128)S(1)}, f32[384,128]{1,0:T(8,128)S(1)}, u32[]{:S(2)}, u32[]{:S(2)}) collective-permute-start(f32[384,128]{1,0:T(8,128)S(1)} %get-tuple-element.27), channel_id=1, source_target_pairs={{0,2},{2,0},{1,3},{3,1},{4,6},{6,4},{5,7},{7,5},{8,10},{10,8},{9,1... | collective-permute-start | bytes 589832 | tf_op jit(solution)/shard_map/ppermute | solution.py:21
  22.5 6.3 %copy-start.5 = (f32[384,128]{1,0:T(8,128)}, f32[384,128]{1,0:T(8,128)S(1)}, u32[]{:S(2)}) copy-start(f32[384,128]{1,0:T(8,128)S(1)} %collective-permute-done.5) | copy-start | bytes 589828
  28.2 8.0 %collective-permute-start.6 = (bf16[512,256]{1,0:T(8,128)(2,1)S(1)}, bf16[512,256]{1,0:T(8,128)(2,1)S(1)}, u32[]{:S(2)}, u32[]{:S(2)}) collective-permute-start(bf16[512,256]{1,0:T(8,128)(2,1)S(1)} %pad_maximum_fusion.3), channel_id=1, source_target_pairs={{0,2},{2,0},{1,3},{3,1},{4,6},{6,4},{5,7},{7,5},{8,10},{10,8},{9,1... | collective-permute-start | bytes 786440 | tf_op jit(solution)/shard_map/ppermute | solution.py:21
  28.9 10.3 %collective-permute-start.7 = (f32[128,128]{1,0:T(8,128)S(1)}, f32[128,128]{1,0:T(8,128)S(1)}, u32[]{:S(2)}, u32[]{:S(2)}) collective-permute-start(f32[128,128]{1,0:T(8,128)S(1)} %slice_add_fusion.1), channel_id=1, source_target_pairs={{0,4},{4,0},{8,12},{12,8},{1,5},{5,1},{9,13},{13,9},{2,6},{6,2},{1... | collective-permute-start | bytes 196616 | tf_op jit(solution)/shard_map/ppermute | solution.py:21
  36.2 2.2 %slice-start = ((f32[384,128]{1,0:T(8,128)}), f32[256,128]{1,0:T(8,128)S(1)}, s32[]{:S(2)}) async-start(f32[384,128]{1,0:T(8,128)} %copy-done.5), calls=%async_computation | async-start | bytes 262144 | tf_op jit(solution)/shard_map/slice | solution.py:65
  38.5 6.3 %copy-start.6 = (bf16[4,1,128,256]{3,2,1,0:T(8,128)(2,1)S(1)}, bf16[4,1,128,256]{3,2,1,0:T(8,128)(2,1)}, u32[]{:S(2)}) copy-start(bf16[4,1,128,256]{3,2,1,0:T(8,128)(2,1)} %param.9) | copy-start | bytes 786436
  39.2 0.6 copy-start.7
  39.8 6.2 %copy-start.8 = (f32[128,128]{1,0:T(8,128)S(1)}, f32[128,128]{1,0:T(8,128)}, u32[]{:S(2)}) copy-start(f32[128,128]{1,0:T(8,128)} %copy-done.7) | copy-start | bytes 196612
  39.8 5.0 %collective-permute-start.8 = (bf16[512,128]{1,0:T(8,128)(2,1)S(1)}, bf16[512,128]{1,0:T(8,128)(2,1)S(1)}, u32[]{:S(2)}, u32[]{:S(2)}) collective-permute-start(bf16[512,128]{1,0:T(8,128)(2,1)S(1)} %pad_maximum_fusion.4), channel_id=1, source_target_pairs={{0,4},{4,0},{8,12},{12,8},{1,5},{5,1},{9,13},{13,9},{2,6},{6,2},{1... | collective-permute-start | bytes 393224 | tf_op jit(solution)/shard_map/ppermute | solution.py:21
  46.2 12.1 %copy-start.1 = (bf16[4,512,128]{2,1,0:T(8,128)(2,1)S(1)}, bf16[4,512,128]{2,1,0:T(8,128)(2,1)}, u32[]{:S(2)}) copy-start(bf16[4,512,128]{2,1,0:T(8,128)(2,1)} %param.8) | copy-start | bytes 1572868
  46.5 5.8 %collective-permute-start.9 = (bf16[256,128]{1,0:T(8,128)(2,1)S(1)}, bf16[256,128]{1,0:T(8,128)(2,1)S(1)}, u32[]{:S(2)}, u32[]{:S(2)}) collective-permute-start(bf16[256,128]{1,0:T(8,128)(2,1)S(1)} %pad_maximum_fusion.6), channel_id=1, source_target_pairs={{0,8},{4,12},{8,0},{12,4},{1,9},{5,13},{9,1},{13,5},{2,10},{6,14},... | collective-permute-start | bytes 196616 | tf_op jit(solution)/shard_map/ppermute | solution.py:21
  52.6 5.0 %collective-permute-start.10 = (bf16[2,128,256]{1,2,0:T(8,128)(2,1)S(1)}, bf16[2,128,256]{1,2,0:T(8,128)(2,1)S(1)}, u32[]{:S(2)}, u32[]{:S(2)}) collective-permute-start(bf16[2,128,256]{1,2,0:T(8,128)(2,1)S(1)} %pad_maximum_fusion.5), channel_id=1, source_target_pairs={{0,2},{2,0},{1,3},{3,1},{4,6},{6,4},{5,7},{7,5},{8,10},{10,8},{9,1... | collective-permute-start | bytes 393224 | tf_op jit(solution)/shard_map/ppermute | solution.py:21
  58.3 1.8 %collective-permute-start.11 = (bf16[3,128,512]{1,2,0:T(8,128)(2,1)S(1)}, bf16[3,128,512]{1,2,0:T(8,128)(2,1)S(1)}, u32[]{:S(2)}, u32[]{:S(2)}) collective-permute-start(bf16[3,128,512]{1,2,0:T(8,128)(2,1)S(1)} %pad_maximum_fusion.2), channel_id=1, source_target_pairs={{0,1},{1,0},{2,3},{3,2},{4,5},{5,4},{6,7},{7,6},{8,9},{9,8},{10,11... | collective-permute-start | bytes 1179656 | tf_op jit(solution)/shard_map/ppermute | solution.py:21
  62.2 1.0 %copy-start.2 = (bf16[512,512]{1,0:T(8,128)(2,1)S(1)}, bf16[512,512]{1,0:T(8,128)(2,1)}, u32[]{:S(2)}) copy-start(bf16[512,512]{1,0:T(8,128)(2,1)} %param.6) | copy-start | bytes 1572868

commit v17 on v13

--- a/solution.py
+++ b/solution.py
@@ -153,6 +153,9 @@
     top = {s: s - 1 for s in range(1, levels)}
     if levels > 2:
         top[levels - 1] = levels - 3
+    early = c0 - jnp.dot(u_basis[0], own_coefs[0], preferred_element_type=F32)
+    u_rest = jnp.transpose(u_basis[1:], (1, 0, 2)).reshape(pixels, (levels - 1) * rank)
+    joined = None
     for j in reversed(range(levels - 1)):
         group = [s for s in range(1, levels) if top[s] >= j]
         if not group:
@@ -160,11 +163,11 @@
         joined = gather_half(jnp.stack([pending[s] for s in group]), j, bits)
         for i, s in enumerate(group):
             pending[s] = joined[i]
-    for s in range(1, levels):
-        full[s] = pending[s]
-    current = c0
-    for s in range(levels):
-        current = current - jnp.dot(u_basis[s], full[s], preferred_element_type=F32)
+    if joined is None:
+        joined = jnp.stack([pending[s] for s in range(1, levels)])
+    current = early - jnp.dot(
+        u_rest, joined.reshape((levels - 1) * rank, width), preferred_element_type=F32
+    )
     return current.astype(BF16)
 
 

time: 57.1 us -> 58.7 us (1.028)
  matrix products: 13.7 us -> 15.7 us
  waiting for transfers between devices: 18.9 us -> 17.6 us
  local copies, waits for them, and re-layouts: 4.07 us -> 5.3 us
    dot_general x4 -> x2, matrix products: 1.73 us -> 4.9 us  [the longest x1 3.42 us: on_device(): jnp.dot(u_rest, joined.reshape((levels - 1) * rank, width), preferred_ele...]
    ppermute x11, waiting for transfers between devices: 18.9 us -> 17.6 us  [swap(): return lax.ppermute(x, axis, [(i, i ^ 1 << stride) for i in range(n)])]
    concatenate x2 -> x1, other arithmetic: 1.79 us -> 0.6 us  [gather_half(): both = jnp.concatenate([x, swap(x, bit, bits), x], axis=-1)]
    dot_general x1, matrix products: 1.5 us -> 0.46 us  [on_device(): jnp.einsum('lir,ij->lrj', v_basis, leaf_inverse, preferred_element_type=F32)]
    slice x2, local copies, waits for them, and re-layouts: 0.05 us -> 0.82 us  [on_device(): parts = [jnp.concatenate([c[:, :rank], c[:, rank:]], axis=0).astype(F32)]]
    another operation x2, other arithmetic: 0.05 us -> 0.8 us  [on_device(): joined = gather_half(jnp.stack([pending[s] for s in group]), j, bits)]
    squeeze x1, local copies, waits for them, and re-layouts: 1.12 us -> 1.73 us  [on_device(): mine, theirs = (mine_c[s], theirs_c[s])]
  transfers between devices with their start and end apart: 11 -> 11, of which waited for: 6 -> 5; matrix products, arithmetic and copies ran while one was open for 30% -> 34% of each run, Pallas kernels for 0% -> 0%
where the time goes in v17:
time: 58.7 us; the launch traced here: 58.1 us
  waiting for transfers between devices  17.6 us (30%)
  matrix products  15.7 us (27%)
  starting transfers between devices  11.9 us (20%)
  other arithmetic  6.84 us (12%)
  local copies, waits for them, and re-layouts  5.3 us (9%)
  between operations  0.62 us (1%)
    ppermute x11, waiting for transfers between devices, swap(): return lax.ppermute(x, axis, [(i, i ^ 1 << stride) for i in range(n)])  17.6 us
    ppermute x11, starting transfers between devices, swap(): return lax.ppermute(x, axis, [(i, i ^ 1 << stride) for i in range(n)])  11.9 us
    dot_general x3, matrix products, project(): jnp.einsum('lrj,jt->lrt', vl_lo[lv], x, preferred_element_type=F32)  3.79 us
    dot_general x1, matrix products, on_device(): jnp.dot(u_rest, joined.reshape((levels - 1) * rank, width), preferred_ele...  3.42 us
    dot_general x4, matrix products, on_device(): coefs = jnp.dot(couple[s], stacked, preferred_element_type=F32).astype(BF16)  2.01 us
    add x3, other arithmetic, on_device(): partial[s] = partial[s] + recv  1.78 us
    dot_general x1, matrix products, on_device(): c0 = jnp.dot(leaf_inverse, templates, preferred_element_type=F32)  1.75 us
    squeeze x1, local copies, waits for them, and re-layouts, on_device(): mine, theirs = (mine_c[s], theirs_c[s])  1.73 us
  transfers between devices with their start and end apart: 11, of which 5 were waited for; matrix products, arithmetic and copies ran while one was open for 34% of the time, Pallas kernels for 0%

profile of v17, /device:TPU:0, one launch (start us, length us, event | category | flops | bytes accessed | tf_op | source)
XLA Modules:
  0.0 58.1 jit_solution(2937888590692903540)
XLA Ops:
  0.0 1.7 %slice_bitcast_fusion.6 = (bf16[128,256]{1,0:T(8,128)(2,1)S(1)}, bf16[128,256]{1,0:T(8,128)(2,1)S(1)}, bf16[128,256]{1,0:T(8,128)(2,1)}, bf16[128,256]{1,0:T(8,128)(2,1)S(1)}) fusion(bf16[4,1,128,256]{3,2,1,0:T(8,128)(2,1)} %param.9), kind=kLoop, calls=%fused_computation.151 | loop fusion | bytes 524288 | tf_op jit(solution)/shard_map/squeeze | solution.py:81
  2.4 4.0 %collective-permute-start.7 = (bf16[256,128]{1,0:T(8,128)(2,1)}, bf16[256,128]{1,0:T(8,128)(2,1)}, u32[]{:S(2)}, u32[]{:S(2)}) collective-permute-start(bf16[256,128]{1,0:T(8,128)(2,1)} %fusion.93), channel_id=1, source_target_pairs={{0,8},{4,12},{8,0},{12,4},{1,9},{5,13},{9,1},{13,5},{2,10},{6,14},... | collective-permute-start | bytes 196616 | tf_op jit(solution)/shard_map/ppermute | solution.py:21
  8.4 0.9 %pad_maximum_fusion = f32[1024,128]{1,0:T(8,128)} fusion(f32[128,128]{1,0:T(8,128)S(1)} %fusion.79, f32[256,128]{1,0:T(8,128)S(1)} %fusion.82, f32[384,128]{1,0:T(8,128)S(1)} %fusion.85, f32[256,128]{1,0:T(8,128)S(1)} %fusion.96), kind=kLoop, calls=%fused_computation.26 | loop fusion | flops 393216 | bytes 1048576 | tf_op jit(solution)/shard_map/concatenate | solution.py:66
  10.1 1.0 %fusion.3 = bf16[128,1024]{1,0:T(8,128)(2,1)} fusion(f32[128,1024]{1,0:T(8,128)S(1)} %fusion.52, bf16[512,1024]{1,0:T(8,128)(2,1)S(1)} %copy-done, bf16[4,128,512]{2,1,0:T(8,128)(2,1)S(1)} %get-tuple-element.5), kind=kOutput, calls=%fused_computation.9 | convolution fusion | flops 134479872 | bytes 1966080 | tf_op jit(solution)/shard_map/lrj,jt->lrt/dot_general | solution.py:98
  12.0 1.3 %convolution_add_fusion = f32[3,128,512]{2,1,0:T(8,128)} fusion(f32[3,128,512]{2,1,0:T(8,128)S(1)} %fusion.17, bf16[4,128,512]{2,1,0:T(8,128)(2,1)S(1)} %get-tuple-element.5, bf16[512,1024]{1,0:T(8,128)(2,1)S(1)} %copy-done, s32[]{:T(128)S(6)} %select_n.69), kind=kOutput, calls=%fused_computation.4 | convolution fusion | flops 201523200 | bytes 2621444 | tf_op jit(solution)/shard_map/lrj,jt->lrt/dot_general | solution.py:98
  14.5 0.8 %broadcast_select_fusion.1 = (bf16[256,128]{1,0:T(8,128)(2,1)S(1)}, bf16[256,128]{1,0:T(8,128)(2,1)S(1)}) fusion(pred[]{:T(512)S(6)} %eq.15, bf16[128,128]{1,0:T(8,128)(2,1)S(1)} %get-tuple-element.40, bf16[128,128]{1,0:T(8,128)(2,1)} %copy-done.10, bf16[128,128]{1,0:T(8,128)(2,1)S(1)} %get-tuple-element.39, bf16[128,128]{1,0:T(8,128)(2,1)} %copy-done.11), kind=kLoop, calls=%fused_computation.156 | loop fusion | flops 327680 | bytes 262145 | tf_op jit(solution)/shard_map/jit(_where)/select_n | solution.py:86
  15.3 0.9 %slice_add_fusion = f32[256,128]{1,0:T(8,128)S(1)} fusion(f32[256,128]{1,0:T(8,128)S(1)} %fusion.82, f32[1024,128]{1,0:T(8,128)} %collective-permute-done), kind=kLoop, calls=%fused_computation.81 | loop fusion | flops 32768 | bytes 393216 | tf_op jit(solution)/shard_map/add | solution.py:77
  16.2 0.8 %slice_add_fusion.2 = f32[128,128]{1,0:T(8,128)S(1)} fusion(f32[128,128]{1,0:T(8,128)S(1)} %fusion.79, f32[1024,128]{1,0:T(8,128)} %collective-permute-done), kind=kLoop, calls=%fused_computation.145 | loop fusion | flops 16384 | bytes 196608 | tf_op jit(solution)/shard_map/add | solution.py:77
  17.1 1.6 %collective-permute-start.2 = (f32[640,128]{1,0:T(8,128)S(1)}, f32[640,128]{1,0:T(8,128)S(1)}, u32[]{:S(2)}, u32[]{:S(2)}) collective-permute-start(f32[640,128]{1,0:T(8,128)S(1)} %pad_maximum_fusion.2), channel_id=1, source_target_pairs={{0,2},{2,0},{1,3},{3,1},{4,6},{6,4},{5,7},{7,5},{8,10},{10,8},{9,1... | collective-permute-start | bytes 983048 | tf_op jit(solution)/shard_map/ppermute | solution.py:21
  18.7 0.9 %slice.297 = f32[384,128]{1,0:T(8,128)S(1)} slice(f32[1024,128]{1,0:T(8,128)} %collective-permute-done), slice={[256:640], [0:128]} | slice | bytes 393216 | tf_op jit(solution)/shard_map/slice | solution.py:72
  19.6 1.1 %convert.16 = bf16[1024,128]{1,0:T(8,128)(2,1)S(1)} convert(f32[1024,128]{1,0:T(8,128)} %collective-permute-done) | non-fusion elementwise | flops 131072 | bytes 786432 | tf_op jit(solution)/shard_map/convert.5
  20.8 1.3 %convolution_convert_fusion = bf16[256,1024]{1,0:T(8,128)(2,1)S(1)} fusion(bf16[128,1024]{1,0:T(8,128)(2,1)} %collective-permute-done.1, bf16[128,1024]{1,0:T(8,128)(2,1)} %fusion.3, bf16[256,128]{1,0:T(8,128)(2,1)S(1)} %get-tuple-element.32, bf16[256,128]{1,0:T(8,128)(2,1)S(1)} %get-tuple-element.31), kind=kOutput, calls=%fused_computation.3 | convolution fusion | flops 135790592 | bytes 1179648 | tf_op jit(solution)/shard_map/dot_general | solution.py:137
  22.9 1.5 %fusion.2 = f32[3,128,512]{2,1,0:T(8,128)S(1)} fusion(f32[3,128,512]{2,1,0:T(8,128)S(1)} %bitcast.105, f32[3,128,512]{2,1,0:T(8,128)} %collective-permute-done.3, f32[3,128,512]{2,1,0:T(8,128)S(1)} %fusion.20, bf16[4,128,512]{2,1,0:T(8,128)(2,1)S(1)} %get-tuple-element.5, bf16[512,1024]{1,0:T(8,128)(2,1)S(1)} %copy-done, s32[]{:T(128)S(6)} %select_n.68), kind=kOutput, calls=%fused_computation.7 | convolution fusion | flops 201916416 | bytes 4194308 | tf_op jit(solution)/shard_map/lrj,jt->lrt/dot_general | solution.py:98
  25.2 2.1 %collective-permute-done.2 = f32[640,128]{1,0:T(8,128)S(1)} collective-permute-done((f32[640,128]{1,0:T(8,128)S(1)}, f32[640,128]{1,0:T(8,128)S(1)}, u32[]{:S(2)}, u32[]{:S(2)}) %collective-permute-start.2) | collective-permute-done | bytes 327712 | tf_op jit(solution)/shard_map/ppermute | solution.py:21
  27.4 1.6 %collective-permute-start.5 = (f32[384,128]{1,0:T(8,128)S(1)}, f32[384,128]{1,0:T(8,128)S(1)}, u32[]{:S(2)}, u32[]{:S(2)}) collective-permute-start(f32[384,128]{1,0:T(8,128)S(1)} %pad_maximum_fusion.4), channel_id=1, source_target_pairs={{0,4},{4,0},{8,12},{12,8},{1,5},{5,1},{9,13},{13,9},{2,6},{6,2},{1... | collective-permute-start | bytes 589832 | tf_op jit(solution)/shard_map/ppermute | solution.py:21
  29.1 4.0 %collective-permute-done.4 = bf16[512,256]{1,0:T(8,128)(2,1)S(1)} collective-permute-done((bf16[512,256]{1,0:T(8,128)(2,1)S(1)}, bf16[512,256]{1,0:T(8,128)(2,1)S(1)}, u32[]{:S(2)}, u32[]{:S(2)}) %collective-permute-start.4) | collective-permute-done | bytes 262176 | tf_op jit(solution)/shard_map/ppermute | solution.py:21
  33.8 1.6 %collective-permute-start.6 = (bf16[512,128]{1,0:T(8,128)(2,1)S(1)}, bf16[512,128]{1,0:T(8,128)(2,1)S(1)}, u32[]{:S(2)}, u32[]{:S(2)}) collective-permute-start(bf16[512,128]{1,0:T(8,128)(2,1)S(1)} %pad_maximum_fusion.5), channel_id=1, source_target_pairs={{0,4},{4,0},{8,12},{12,8},{1,5},{5,1},{9,13},{13,9},{2,6},{6,2},{1... | collective-permute-start | bytes 393224 | tf_op jit(solution)/shard_map/ppermute | solution.py:21
  35.5 3.3 %collective-permute-done.6 = bf16[512,128]{1,0:T(8,128)(2,1)S(1)} collective-permute-done((bf16[512,128]{1,0:T(8,128)(2,1)S(1)}, bf16[512,128]{1,0:T(8,128)(2,1)S(1)}, u32[]{:S(2)}, u32[]{:S(2)}) %collective-permute-start.6) | collective-permute-done | bytes 131104 | tf_op jit(solution)/shard_map/ppermute | solution.py:21
  39.8 4.8 %collective-permute-done.8 = bf16[256,128]{1,0:T(8,128)(2,1)S(1)} collective-permute-done((bf16[256,128]{1,0:T(8,128)(2,1)S(1)}, bf16[256,128]{1,0:T(8,128)(2,1)S(1)}, u32[]{:S(2)}, u32[]{:S(2)}) %collective-permute-start.8) | collective-permute-done | bytes 65568 | tf_op jit(solution)/shard_map/ppermute | solution.py:21
  44.9 1.5 %collective-permute-start.9 = (bf16[2,128,256]{1,2,0:T(8,128)(2,1)S(1)}, bf16[2,128,256]{1,2,0:T(8,128)(2,1)S(1)}, u32[]{:S(2)}, u32[]{:S(2)}) collective-permute-start(bf16[2,128,256]{1,2,0:T(8,128)(2,1)S(1)} %pad_maximum_fusion.6), channel_id=1, source_target_pairs={{0,2},{2,0},{1,3},{3,1},{4,6},{6,4},{5,7},{7,5},{8,10},{10,8},{9,1... | collective-permute-start | bytes 393224 | tf_op jit(solution)/shard_map/ppermute | solution.py:21
  46.6 3.4 %collective-permute-done.9 = bf16[2,128,256]{1,2,0:T(8,128)(2,1)S(1)} collective-permute-done((bf16[2,128,256]{1,2,0:T(8,128)(2,1)S(1)}, bf16[2,128,256]{1,2,0:T(8,128)(2,1)S(1)}, u32[]{:S(2)}, u32[]{:S(2)}) %collective-permute-start.9) | collective-permute-done | bytes 131104 | tf_op jit(solution)/shard_map/ppermute | solution.py:21
  51.4 1.8 %fusion.129 = f32[512,1024]{1,0:T(8,128)S(1)} fusion(bf16[512,512]{1,0:T(8,128)(2,1)} %param.6, bf16[512,1024]{1,0:T(8,128)(2,1)S(1)} %copy-done), kind=kOutput, calls=%fused_computation.194 | convolution fusion | flops 536870912 | bytes 3670016 | tf_op jit(solution)/shard_map/dot_general | solution.py:52
  53.1 1.5 %fusion.38 = f32[1024,512]{0,1:T(8,128)S(1)} fusion(bf16[256,1024]{1,0:T(8,128)(2,1)} %copy-done.5, bf16[4,512,128]{2,1,0:T(8,128)(2,1)} %param.8), kind=kOutput, calls=%fused_computation.60 | convolution fusion | flops 134217728 | bytes 2490368 | tf_op jit(solution)/shard_map/dot_general | solution.py:156
  54.6 3.4 %fusion = bf16[512,1024]{1,0:T(8,128)(2,1)} fusion(f32[512,1024]{1,0:T(8,128)S(1)} %fusion.129, f32[1024,512]{0,1:T(8,128)S(1)} %fusion.38, s32[]{:T(128)S(6)} %select_n.79, bf16[1,128,512]{1,2,0:T(8,128)(2,1)S(1)} %copy.14, bf16[2,128,512]{1,2,0:T(8,128)(2,1)S(1)} %fusion.36, bf16[3,128,512]{1,2,0:T(8,128)(2,1)} %collective-permute-done.10, ...), kind=kOutput, calls=%fused_computation.1 | convolution fusion | flops 408158208 | bytes 6422532 | tf_op jit(solution)/shard_map/dot_general | solution.py:168
  (98 shorter events, 10.5 us)
Async XLA Ops:
  0.0 9.8 %copy-start = (bf16[512,1024]{1,0:T(8,128)(2,1)S(1)}, bf16[512,1024]{1,0:T(8,128)(2,1)}, u32[]{:S(2)}) copy-start(bf16[512,1024]{1,0:T(8,128)(2,1)} %param.5) | copy-start | bytes 3145732
  0.0 6.5 %copy-start.1 = (bf16[4,512,128]{2,1,0:T(8,128)(2,1)S(1)}, bf16[4,512,128]{2,1,0:T(8,128)(2,1)}, u32[]{:S(2)}) copy-start(bf16[4,512,128]{2,1,0:T(8,128)(2,1)} %param.7) | copy-start | bytes 1572868
  0.0 6.7 %slice-start = ((bf16[4,512,128]{2,1,0:T(8,128)(2,1)}), bf16[2,512,128]{2,1,0:T(8,128)(2,1)S(1)}, s32[]{:S(2)}) async-start(bf16[4,512,128]{2,1,0:T(8,128)(2,1)} %param.7), calls=%async_computation | async-start | bytes 524288 | tf_op jit(solution)/shard_map/slice | solution.py:57
  0.0 6.5 %copy-start.3 = (bf16[4,512,128]{2,1,0:T(8,128)(2,1)S(1)}, bf16[4,512,128]{2,1,0:T(8,128)(2,1)}, u32[]{:S(2)}) copy-start(bf16[4,512,128]{2,1,0:T(8,128)(2,1)} %param.8) | copy-start | bytes 1572868
  1.7 5.4 %slice-start.1 = ((bf16[4,512,128]{2,1,0:T(8,128)(2,1)}), bf16[3,512,128]{2,1,0:T(8,128)(2,1)S(1)}, s32[]{:S(2)}) async-start(bf16[4,512,128]{2,1,0:T(8,128)(2,1)} %param.7), calls=%async_computation.1 | async-start | bytes 786432 | tf_op jit(solution)/shard_map/slice | solution.py:57
  1.8 5.5 %copy-start.10 = (bf16[128,128]{1,0:T(8,128)(2,1)}, bf16[128,128]{1,0:T(8,128)(2,1)S(1)}, u32[]{:S(2)}) copy-start(bf16[128,128]{1,0:T(8,128)(2,1)S(1)} %get-tuple-element.41) | copy-start | bytes 98308
  1.8 5.5 %copy-start.11 = (bf16[128,128]{1,0:T(8,128)(2,1)}, bf16[128,128]{1,0:T(8,128)(2,1)S(1)}, u32[]{:S(2)}) copy-start(bf16[128,128]{1,0:T(8,128)(2,1)S(1)} %get-tuple-element.42) | copy-start | bytes 98308
  2.4 11.3 %collective-permute-start.7 = (bf16[256,128]{1,0:T(8,128)(2,1)}, bf16[256,128]{1,0:T(8,128)(2,1)}, u32[]{:S(2)}, u32[]{:S(2)}) collective-permute-start(bf16[256,128]{1,0:T(8,128)(2,1)} %fusion.93), channel_id=1, source_target_pairs={{0,8},{4,12},{8,0},{12,4},{1,9},{5,13},{9,1},{13,5},{2,10},{6,14},... | collective-permute-start | bytes 196616 | tf_op jit(solution)/shard_map/ppermute | solution.py:21
  7.3 2.0 %copy-start.2 = (bf16[512,512]{1,0:T(8,128)(2,1)S(1)}, bf16[512,512]{1,0:T(8,128)(2,1)}, u32[]{:S(2)}) copy-start(bf16[512,512]{1,0:T(8,128)(2,1)} %param.6) | copy-start | bytes 1572868
  8.4 1.4 %copy-start.6 = (bf16[128,128]{1,0:T(8,128)(2,1)}, bf16[128,128]{1,0:T(8,128)(2,1)S(1)}, u32[]{:S(2)}) copy-start(bf16[128,128]{1,0:T(8,128)(2,1)S(1)} %get-tuple-element.55) | copy-start | bytes 98308
  8.4 1.4 %copy-start.8 = (bf16[128,128]{1,0:T(8,128)(2,1)}, bf16[128,128]{1,0:T(8,128)(2,1)S(1)}, u32[]{:S(2)}) copy-start(bf16[128,128]{1,0:T(8,128)(2,1)S(1)} %get-tuple-element.56) | copy-start | bytes 98308
  9.3 6.0 %collective-permute-start = (f32[1024,128]{1,0:T(8,128)}, f32[1024,128]{1,0:T(8,128)}, u32[]{:S(2)}, u32[]{:S(2)}) collective-permute-start(f32[1024,128]{1,0:T(8,128)} %pad_maximum_fusion), channel_id=1, source_target_pairs={{0,1},{1,0},{2,3},{3,2},{4,5},{5,4},{6,7},{7,6},{8,9},{9,8},{10,11... | collective-permute-start | bytes 1572872 | tf_op jit(solution)/shard_map/ppermute | solution.py:21
  11.1 9.6 %collective-permute-start.1 = (bf16[128,1024]{1,0:T(8,128)(2,1)}, bf16[128,1024]{1,0:T(8,128)(2,1)}, u32[]{:S(2)}, u32[]{:S(2)}) collective-permute-start(bf16[128,1024]{1,0:T(8,128)(2,1)} %fusion.3), channel_id=1, source_target_pairs={{0,1},{1,0},{2,3},{3,2},{4,5},{5,4},{6,7},{7,6},{8,9},{9,8},{10,11... | collective-permute-start | bytes 786440 | tf_op jit(solution)/shard_map/ppermute | solution.py:21
  13.3 9.3 %collective-permute-start.3 = (f32[3,128,512]{2,1,0:T(8,128)}, f32[3,128,512]{2,1,0:T(8,128)}, u32[]{:S(2)}, u32[]{:S(2)}) collective-permute-start(f32[3,128,512]{2,1,0:T(8,128)} %convolution_add_fusion), channel_id=1, source_target_pairs={{0,1},{1,0},{2,3},{3,2},{4,5},{5,4},{6,7},{7,6},{8,9},{9,8},{10,11... | collective-permute-start | bytes 2359304 | tf_op jit(solution)/shard_map/ppermute | solution.py:21
  13.7 7.0 %copy-start.7 = (bf16[128,128]{1,0:T(8,128)(2,1)S(1)}, bf16[128,128]{1,0:T(8,128)(2,1)}, u32[]{:S(2)}) copy-start(bf16[128,128]{1,0:T(8,128)(2,1)} %copy-done.6) | copy-start | bytes 98308
  13.7 7.0 %copy-start.9 = (bf16[128,128]{1,0:T(8,128)(2,1)S(1)}, bf16[128,128]{1,0:T(8,128)(2,1)}, u32[]{:S(2)}) copy-start(bf16[128,128]{1,0:T(8,128)(2,1)} %copy-done.8) | copy-start | bytes 98308
  17.1 10.2 %collective-permute-start.2 = (f32[640,128]{1,0:T(8,128)S(1)}, f32[640,128]{1,0:T(8,128)S(1)}, u32[]{:S(2)}, u32[]{:S(2)}) collective-permute-start(f32[640,128]{1,0:T(8,128)S(1)} %pad_maximum_fusion.2), channel_id=1, source_target_pairs={{0,2},{2,0},{1,3},{3,1},{4,6},{6,4},{5,7},{7,5},{8,10},{10,8},{9,1... | collective-permute-start | bytes 983048 | tf_op jit(solution)/shard_map/ppermute | solution.py:21
  24.6 8.5 %collective-permute-start.4 = (bf16[512,256]{1,0:T(8,128)(2,1)S(1)}, bf16[512,256]{1,0:T(8,128)(2,1)S(1)}, u32[]{:S(2)}, u32[]{:S(2)}) collective-permute-start(bf16[512,256]{1,0:T(8,128)(2,1)S(1)} %pad_maximum_fusion.3), channel_id=1, source_target_pairs={{0,2},{2,0},{1,3},{3,1},{4,6},{6,4},{5,7},{7,5},{8,10},{10,8},{9,1... | collective-permute-start | bytes 786440 | tf_op jit(solution)/shard_map/ppermute | solution.py:21
  27.4 8.1 %collective-permute-start.5 = (f32[384,128]{1,0:T(8,128)S(1)}, f32[384,128]{1,0:T(8,128)S(1)}, u32[]{:S(2)}, u32[]{:S(2)}) collective-permute-start(f32[384,128]{1,0:T(8,128)S(1)} %pad_maximum_fusion.4), channel_id=1, source_target_pairs={{0,4},{4,0},{8,12},{12,8},{1,5},{5,1},{9,13},{13,9},{2,6},{6,2},{1... | collective-permute-start | bytes 589832 | tf_op jit(solution)/shard_map/ppermute | solution.py:21
  33.8 5.0 %collective-permute-start.6 = (bf16[512,128]{1,0:T(8,128)(2,1)S(1)}, bf16[512,128]{1,0:T(8,128)(2,1)S(1)}, u32[]{:S(2)}, u32[]{:S(2)}) collective-permute-start(bf16[512,128]{1,0:T(8,128)(2,1)S(1)} %pad_maximum_fusion.5), channel_id=1, source_target_pairs={{0,4},{4,0},{8,12},{12,8},{1,5},{5,1},{9,13},{13,9},{2,6},{6,2},{1... | collective-permute-start | bytes 393224 | tf_op jit(solution)/shard_map/ppermute | solution.py:21
  39.4 5.2 %collective-permute-start.8 = (bf16[256,128]{1,0:T(8,128)(2,1)S(1)}, bf16[256,128]{1,0:T(8,128)(2,1)S(1)}, u32[]{:S(2)}, u32[]{:S(2)}) collective-permute-start(bf16[256,128]{1,0:T(8,128)(2,1)S(1)} %pad_maximum_fusion.19), channel_id=1, source_target_pairs={{0,8},{4,12},{8,0},{12,4},{1,9},{5,13},{9,1},{13,5},{2,10},{6,14},... | collective-permute-start | bytes 196616 | tf_op jit(solution)/shard_map/ppermute | solution.py:21
  44.9 5.0 %collective-permute-start.9 = (bf16[2,128,256]{1,2,0:T(8,128)(2,1)S(1)}, bf16[2,128,256]{1,2,0:T(8,128)(2,1)S(1)}, u32[]{:S(2)}, u32[]{:S(2)}) collective-permute-start(bf16[2,128,256]{1,2,0:T(8,128)(2,1)S(1)} %pad_maximum_fusion.6), channel_id=1, source_target_pairs={{0,2},{2,0},{1,3},{3,1},{4,6},{6,4},{5,7},{7,5},{8,10},{10,8},{9,1... | collective-permute-start | bytes 393224 | tf_op jit(solution)/shard_map/ppermute | solution.py:21
  51.4 3.3 %collective-permute-start.10 = (bf16[3,128,512]{1,2,0:T(8,128)(2,1)}, bf16[3,128,512]{1,2,0:T(8,128)(2,1)}, u32[]{:S(2)}, u32[]{:S(2)}) collective-permute-start(bf16[3,128,512]{1,2,0:T(8,128)(2,1)} %pad_maximum_fusion.1), channel_id=1, source_target_pairs={{0,1},{1,0},{2,3},{3,2},{4,5},{5,4},{6,7},{7,6},{8,9},{9,8},{10,11... | collective-permute-start | bytes 1179656 | tf_op jit(solution)/shard_map/ppermute | solution.py:21
  53.1 1.5 %copy-start.4 = (bf16[4,512,128]{2,1,0:T(8,128)(2,1)S(1)}, bf16[4,512,128]{2,1,0:T(8,128)(2,1)}, u32[]{:S(2)}) copy-start(bf16[4,512,128]{2,1,0:T(8,128)(2,1)} %param.8) | copy-start | bytes 1572868
  (1 other events, 0.8 us)

commit v18 on v13

--- a/solution.py
+++ b/solution.py
@@ -58,15 +58,10 @@
         ).reshape(-1, rank)
         for s in range(levels - 1)
     ]
-    w_own, theirs_c = [None] * levels, []
-    for b in range(levels):
-        c = mine_c[b]
-        parts = [jnp.concatenate([c[:, :rank], c[:, rank:]], axis=0).astype(F32)]
-        parts += partial[b:]
-        got = swap(jnp.concatenate(parts, axis=0), b, bits)
-        theirs = got[: 2 * rank].astype(BF16)
-        theirs_c.append(jnp.concatenate([theirs[:rank], theirs[rank:]], axis=1))
-        at = 2 * rank
+    w_own = [None] * levels
+    for b in range(levels - 1):
+        got = swap(jnp.concatenate(partial[b:], axis=0), b, bits)
+        at = 0
         for s in range(b, levels - 1):
             n = partial[s].shape[0]
             recv = got[at : at + n]
@@ -75,17 +70,16 @@
                 w_own[s] = jnp.concatenate([partial[s], recv], axis=1)
             else:
                 partial[s] = partial[s] + recv
-    couple = []
-    for s in range(levels):
+    theirs_c = [swap(mine_c[s], s, bits) for s in range(levels)]
+
+    def ordered(s, theirs):
         lower = side(s, bits) == 0
-        mine, theirs = mine_c[s], theirs_c[s]
+        mine = mine_c[s]
         first = jnp.concatenate([mine[:, :rank], theirs[:, :rank]], axis=0)
         second = jnp.concatenate([mine[:, rank:], theirs[:, rank:]], axis=0)
-        couple.append(
-            jnp.concatenate(
-                [jnp.where(lower, first, second), jnp.where(lower, second, first)],
-                axis=1,
-            )
+        return jnp.concatenate(
+            [jnp.where(lower, first, second), jnp.where(lower, second, first)],
+            axis=1,
         )
 
     vl = jnp.einsum("lir,ij->lrj", v_basis, leaf_inverse, preferred_element_type=F32)
@@ -134,7 +128,10 @@
                 recv = got[2 * rank :].reshape(n, rank, w).astype(F32)
                 rest = keep + recv
         stacked = jnp.concatenate([mine_b, theirs_b], axis=0)
-        coefs = jnp.dot(couple[s], stacked, preferred_element_type=F32).astype(BF16)
+        if s == 0:
+            stacked, theirs_c = lax.optimization_barrier((stacked, theirs_c))
+        couple = ordered(s, theirs_c[s])
+        coefs = jnp.dot(couple, stacked, preferred_element_type=F32).astype(BF16)
         own_coefs.append(coefs[:rank])
         if s < levels - 1:
             w = coefs.shape[1] // 2

time: 57.1 us -> 64.6 us (1.13)
  waiting for transfers between devices: 18.9 us -> 25.4 us
  other arithmetic: 7.28 us -> 3.13 us
  local copies, waits for them, and re-layouts: 4.07 us -> 7.17 us
  starting transfers between devices: 12 us -> 13.4 us
    ppermute x11 -> x14, waiting for transfers between devices: 18.9 us -> 25.4 us  [swap(): return lax.ppermute(x, axis, [(i, i ^ 1 << stride) for i in range(n)])]
    slice x6 -> x4, local copies, waits for them, and re-layouts: 0.85 us -> 4.55 us  [ordered(): first = jnp.concatenate([mine[:, :rank], theirs[:, :rank]], axis=0)]
    dot_general x3, matrix products: 0.69 us -> 4.01 us  [on_device(): jnp.einsum('lir,is->lrs', v_basis[s + 1:], u_basis[s], preferred_element_...]
    dot_general x3, matrix products: 3.79 us -> 1.96 us  [project(): jnp.einsum('lrj,jt->lrt', vl_lo[lv], x, preferred_element_type=F32)]
    add x3, other arithmetic: 1.78 us -> 0.04 us  [on_device(): partial[s] = partial[s] + recv]
    ppermute x11 -> x14, starting transfers between devices: 12 us -> 13.4 us  [swap(): return lax.ppermute(x, axis, [(i, i ^ 1 << stride) for i in range(n)])]
    another operation x3 -> x0, other arithmetic: 1.1 us -> none
    dot_general x4, matrix products: 2 us -> 0.98 us  [on_device(): coefs = jnp.dot(couple, stacked, preferred_element_type=F32).astype(BF16)]
  transfers between devices with their start and end apart: 11 -> 14, of which waited for: 6 -> 6; matrix products, arithmetic and copies ran while one was open for 30% -> 25% of each run, Pallas kernels for 0% -> 0%
where the time goes in v18:
time: 64.6 us; the launch traced here: 64.1 us
  waiting for transfers between devices  25.4 us (39%)
  matrix products  14.3 us (22%)
  starting transfers between devices  13.4 us (21%)
  local copies, waits for them, and re-layouts  7.17 us (11%)
  other arithmetic  3.13 us (5%)
  between operations  0.65 us (1%)
    ppermute x14, waiting for transfers between devices, swap(): return lax.ppermute(x, axis, [(i, i ^ 1 << stride) for i in range(n)])  25.4 us
    ppermute x14, starting transfers between devices, swap(): return lax.ppermute(x, axis, [(i, i ^ 1 << stride) for i in range(n)])  13.4 us
    slice x4, local copies, waits for them, and re-layouts, ordered(): first = jnp.concatenate([mine[:, :rank], theirs[:, :rank]], axis=0)  4.55 us
    dot_general x3, matrix products, on_device(): jnp.einsum('lir,is->lrs', v_basis[s + 1:], u_basis[s], preferred_element_...  4.01 us
    dot_general x3, matrix products, project(): jnp.einsum('lrj,jt->lrt', vl_lo[lv], x, preferred_element_type=F32)  1.96 us
    dot_general x1, matrix products, on_device(): c0 = jnp.dot(leaf_inverse, templates, preferred_element_type=F32)  1.83 us
    concatenate x2, other arithmetic, gather_half(): both = jnp.concatenate([x, swap(x, bit, bits), x], axis=-1)  1.79 us
    squeeze x1, local copies, waits for them, and re-layouts, on_device(): theirs_c = [swap(mine_c[s], s, bits) for s in range(levels)]  1.74 us
  transfers between devices with their start and end apart: 14, of which 6 were waited for; matrix products, arithmetic and copies ran while one was open for 25% of the time, Pallas kernels for 0%

profile of v18, /device:TPU:0, one launch (start us, length us, event | category | flops | bytes accessed | tf_op | source)
XLA Modules:
  0.0 64.1 jit_solution(9334648623929581637)
XLA Ops:
  0.0 1.7 %slice_bitcast_fusion.12 = (bf16[128,256]{1,0:T(8,128)(2,1)}, bf16[128,256]{1,0:T(8,128)(2,1)}, bf16[128,256]{1,0:T(8,128)(2,1)}, bf16[128,256]{1,0:T(8,128)(2,1)}) fusion(bf16[4,1,128,256]{3,2,1,0:T(8,128)(2,1)} %param.9), kind=kLoop, calls=%fused_computation.152 | loop fusion | bytes 524288 | tf_op jit(solution)/shard_map/squeeze | solution.py:73
  1.7 4.0 %collective-permute-start.4 = (bf16[128,256]{1,0:T(8,128)(2,1)}, bf16[128,256]{1,0:T(8,128)(2,1)}, u32[]{:S(2)}, u32[]{:S(2)}) collective-permute-start(bf16[128,256]{1,0:T(8,128)(2,1)} %get-tuple-element.21), channel_id=1, source_target_pairs={{0,8},{4,12},{8,0},{12,4},{1,9},{5,13},{9,1},{13,5},{2,10},{6,14},... | collective-permute-start | bytes 196616 | tf_op jit(solution)/shard_map/ppermute | solution.py:21
  5.8 1.5 %collective-permute-start.2 = (bf16[128,256]{1,0:T(8,128)(2,1)}, bf16[128,256]{1,0:T(8,128)(2,1)}, u32[]{:S(2)}, u32[]{:S(2)}) collective-permute-start(bf16[128,256]{1,0:T(8,128)(2,1)} %get-tuple-element.22), channel_id=1, source_target_pairs={{0,2},{2,0},{1,3},{3,1},{4,6},{6,4},{5,7},{7,5},{8,10},{10,8},{9,1... | collective-permute-start | bytes 196616 | tf_op jit(solution)/shard_map/ppermute | solution.py:21
  7.3 1.6 %collective-permute-start.3 = (bf16[128,256]{1,0:T(8,128)(2,1)}, bf16[128,256]{1,0:T(8,128)(2,1)}, u32[]{:S(2)}, u32[]{:S(2)}) collective-permute-start(bf16[128,256]{1,0:T(8,128)(2,1)} %get-tuple-element.24), channel_id=1, source_target_pairs={{0,4},{4,0},{8,12},{12,8},{1,5},{5,1},{9,13},{13,9},{2,6},{6,2},{1... | collective-permute-start | bytes 196616 | tf_op jit(solution)/shard_map/ppermute | solution.py:21
  8.8 1.7 %subtract_convert_fusion = (bf16[4,128,512]{2,1,0:T(8,128)(2,1)S(1)}, bf16[4,128,512]{2,1,0:T(8,128)(2,1)S(1)}) fusion(bf16[4,512,128]{2,1,0:T(8,128)(2,1)} %param.7, bf16[512,512]{1,0:T(8,128)(2,1)} %param.6), kind=kOutput, calls=%fused_computation.23 | convolution fusion | flops 269484032 | bytes 2097152 | tf_op jit(solution)/shard_map/lir,ij->lrj/dot_general | solution.py:85
  11.5 1.5 %fusion.115 = (bf16[128,128]{1,0:T(8,128)(2,1)}, bf16[128,128]{1,0:T(8,128)(2,1)}, bf16[128,128]{1,0:T(8,128)(2,1)}, bf16[128,128]{1,0:T(8,128)(2,1)}) fusion(bf16[128,256]{1,0:T(8,128)(2,1)} %get-tuple-element.21, bf16[128,256]{1,0:T(8,128)(2,1)} %get-tuple-element.24), kind=kLoop, calls=%fused_computation.183 | loop fusion | bytes 262144 | tf_op jit(solution)/shard_map/slice | solution.py:78
  13.0 1.4 %fusion.121 = (bf16[128,128]{1,0:T(8,128)(2,1)}, bf16[128,128]{1,0:T(8,128)(2,1)}, bf16[128,128]{1,0:T(8,128)(2,1)}, bf16[128,128]{1,0:T(8,128)(2,1)}) fusion(bf16[128,256]{1,0:T(8,128)(2,1)} %get-tuple-element.22, bf16[128,256]{1,0:T(8,128)(2,1)} %get-tuple-element.23), kind=kLoop, calls=%fused_computation.189 | loop fusion | bytes 262144 | tf_op jit(solution)/shard_map/slice | solution.py:78
  14.4 1.7 %fusion.77 = f32[128,128]{1,0:T(8,128)} fusion(bf16[4,512,128]{2,1,0:T(8,128)(2,1)S(1)} %copy-done.1, bf16[4,512,128]{2,1,0:T(8,128)(2,1)} %param.8), kind=kOutput, calls=%fused_computation.118 | convolution fusion | flops 16777216 | bytes 327680 | tf_op jit(solution)/shard_map/lir,is->lrs/dot_general | solution.py:56
  16.3 1.1 %fusion.81 = f32[256,128]{1,0:T(8,128)S(1)} fusion(bf16[256,512]{1,0:T(8,128)(2,1)S(1)} %bitcast.128, bf16[4,512,128]{2,1,0:T(8,128)(2,1)} %param.8), kind=kOutput, calls=%fused_computation.122 | convolution fusion | flops 33554432 | bytes 524288 | tf_op jit(solution)/shard_map/lir,is->lrs/dot_general | solution.py:56
  17.6 1.2 %fusion.83 = f32[384,128]{1,0:T(8,128)S(1)} fusion(bf16[384,512]{1,0:T(8,128)(2,1)S(1)} %bitcast.126, bf16[4,512,128]{2,1,0:T(8,128)(2,1)} %param.8), kind=kOutput, calls=%fused_computation.124 | convolution fusion | flops 50331648 | bytes 720896 | tf_op jit(solution)/shard_map/lir,is->lrs/dot_general | solution.py:56
  19.2 1.3 %convolution_add_fusion = f32[3,128,512]{2,1,0:T(8,128)} fusion(f32[3,128,512]{2,1,0:T(8,128)S(1)} %fusion.12, bf16[4,128,512]{2,1,0:T(8,128)(2,1)S(1)} %get-tuple-element.15, bf16[512,1024]{1,0:T(8,128)(2,1)S(1)} %copy-done, s32[]{:T(128)S(6)} %select_n.69), kind=kOutput, calls=%fused_computation.6 | convolution fusion | flops 201523200 | bytes 2621444 | tf_op jit(solution)/shard_map/lrj,jt->lrt/dot_general | solution.py:92
  21.3 1.0 %pad_maximum_fusion = bf16[256,1024]{1,0:T(8,128)(2,1)S(1)} fusion(bf16[128,1024]{1,0:T(8,128)(2,1)} %collective-permute-done, bf16[128,1024]{1,0:T(8,128)(2,1)S(1)} %fusion.3), kind=kLoop, calls=%fused_computation.28 | loop fusion | flops 1048576 | bytes 1048576 | tf_op jit(solution)/shard_map/concatenate | solution.py:130
  22.6 0.8 %fusion.122 = (bf16[128,128]{1,0:T(8,128)(2,1)S(1)}, bf16[128,128]{1,0:T(8,128)(2,1)S(1)}, bf16[128,128]{1,0:T(8,128)(2,1)S(1)}, bf16[128,128]{1,0:T(8,128)(2,1)S(1)}) fusion(bf16[128,256]{1,0:T(8,128)(2,1)} %collective-permute-done.2, bf16[128,256]{1,0:T(8,128)(2,1)} %collective-permute-done.1), kind=kLoop, calls=%fused_computation.190 | loop fusion | bytes 262144 | tf_op jit(solution)/shard_map/slice | solution.py:78
  23.8 0.8 %fusion.116 = (bf16[128,128]{1,0:T(8,128)(2,1)S(1)}, bf16[128,128]{1,0:T(8,128)(2,1)S(1)}, bf16[128,128]{1,0:T(8,128)(2,1)S(1)}, bf16[128,128]{1,0:T(8,128)(2,1)S(1)}) fusion(bf16[128,256]{1,0:T(8,128)(2,1)} %collective-permute-done.4, bf16[128,256]{1,0:T(8,128)(2,1)} %collective-permute-done.3), kind=kLoop, calls=%fused_computation.184 | loop fusion | bytes 262144 | tf_op jit(solution)/shard_map/slice | solution.py:78
  26.4 1.6 %collective-permute-start.8 = (f32[384,128]{1,0:T(8,128)S(1)}, f32[384,128]{1,0:T(8,128)S(1)}, u32[]{:S(2)}, u32[]{:S(2)}) collective-permute-start(f32[384,128]{1,0:T(8,128)S(1)} %pad_maximum_fusion.4), channel_id=1, source_target_pairs={{0,2},{2,0},{1,3},{3,1},{4,6},{6,4},{5,7},{7,5},{8,10},{10,8},{9,1... | collective-permute-start | bytes 589832 | tf_op jit(solution)/shard_map/ppermute | solution.py:21
  28.1 10.5 %collective-permute-done.8 = f32[384,128]{1,0:T(8,128)S(1)} collective-permute-done((f32[384,128]{1,0:T(8,128)S(1)}, f32[384,128]{1,0:T(8,128)S(1)}, u32[]{:S(2)}, u32[]{:S(2)}) %collective-permute-start.8) | collective-permute-done | bytes 196640 | tf_op jit(solution)/shard_map/ppermute | solution.py:21
  39.9 1.6 %collective-permute-start.10 = (f32[128,128]{1,0:T(8,128)S(1)}, f32[128,128]{1,0:T(8,128)S(1)}, u32[]{:S(2)}, u32[]{:S(2)}) collective-permute-start(f32[128,128]{1,0:T(8,128)S(1)} %slice_add_fusion.1), channel_id=1, source_target_pairs={{0,4},{4,0},{8,12},{12,8},{1,5},{5,1},{9,13},{13,9},{2,6},{6,2},{1... | collective-permute-start | bytes 196616 | tf_op jit(solution)/shard_map/ppermute | solution.py:21
  41.5 3.5 %collective-permute-done.9 = bf16[512,128]{1,0:T(8,128)(2,1)S(1)} collective-permute-done((bf16[512,128]{1,0:T(8,128)(2,1)S(1)}, bf16[512,128]{1,0:T(8,128)(2,1)S(1)}, u32[]{:S(2)}, u32[]{:S(2)}) %collective-permute-start.9) | collective-permute-done | bytes 131104 | tf_op jit(solution)/shard_map/ppermute | solution.py:21
  46.4 5.4 %collective-permute-done.11 = bf16[256,128]{1,0:T(8,128)(2,1)S(1)} collective-permute-done((bf16[256,128]{1,0:T(8,128)(2,1)S(1)}, bf16[256,128]{1,0:T(8,128)(2,1)S(1)}, u32[]{:S(2)}, u32[]{:S(2)}) %collective-permute-start.11) | collective-permute-done | bytes 65568 | tf_op jit(solution)/shard_map/ppermute | solution.py:21
  52.1 0.6 collective-permute-start.12
  52.8 4.3 %collective-permute-done.12 = bf16[2,128,256]{1,2,0:T(8,128)(2,1)S(1)} collective-permute-done((bf16[2,128,256]{1,2,0:T(8,128)(2,1)S(1)}, bf16[2,128,256]{1,2,0:T(8,128)(2,1)S(1)}, u32[]{:S(2)}, u32[]{:S(2)}) %collective-permute-start.12) | collective-permute-done | bytes 131104 | tf_op jit(solution)/shard_map/ppermute | solution.py:21
  58.3 1.3 %collective-permute-done.13 = bf16[3,128,512]{1,2,0:T(8,128)(2,1)S(1)} collective-permute-done((bf16[3,128,512]{1,2,0:T(8,128)(2,1)S(1)}, bf16[3,128,512]{1,2,0:T(8,128)(2,1)S(1)}, u32[]{:S(2)}, u32[]{:S(2)}) %collective-permute-start.13) | collective-permute-done | bytes 393248 | tf_op jit(solution)/shard_map/ppermute | solution.py:21
  59.6 1.2 %fusion.9 = bf16[3,128,1024]{1,2,0:T(8,128)(2,1)S(1)} fusion(s32[]{:T(128)S(6)} %select_n.79, bf16[1,128,512]{1,2,0:T(8,128)(2,1)S(1)} %copy.16, bf16[2,128,512]{1,2,0:T(8,128)(2,1)S(1)} %fusion.29, bf16[3,128,512]{1,2,0:T(8,128)(2,1)S(1)} %collective-permute-done.13), kind=kLoop, calls=%fused_computation.26 | loop fusion | flops 3932160 | bytes 1572868 | tf_op jit(solution)/shard_map/concatenate | solution.py:44
  62.2 1.8 %fusion = bf16[512,1024]{1,0:T(8,128)(2,1)} fusion(f32[1024,512]{0,1:T(8,128)S(1)} %fusion.31, f32[1024,512]{0,1:T(8,128)S(1)} %fusion.32, f32[1024,512]{0,1:T(8,128)S(1)} %fusion.33, f32[1024,512]{0,1:T(8,128)S(1)} %fusion.34, bf16[512,512]{1,0:T(8,128)(2,1)S(1)} %copy-done.2, bf16[512,1024]{1,0:T(8,128)(2,1)S(1)} %copy-done), kind=kOutput, calls=%fused_computation.1 | convolution fusion | flops 539492352 | bytes 11010048 | tf_op jit(solution)/shard_map/dot_general | solution.py:52
  (101 shorter events, 10.3 us)
Async XLA Ops:
  0.0 10.5 %copy-start = (bf16[512,1024]{1,0:T(8,128)(2,1)S(1)}, bf16[512,1024]{1,0:T(8,128)(2,1)}, u32[]{:S(2)}) copy-start(bf16[512,1024]{1,0:T(8,128)(2,1)} %param.5) | copy-start | bytes 3145732
  1.7 20.5 %collective-permute-start.4 = (bf16[128,256]{1,0:T(8,128)(2,1)}, bf16[128,256]{1,0:T(8,128)(2,1)}, u32[]{:S(2)}, u32[]{:S(2)}) collective-permute-start(bf16[128,256]{1,0:T(8,128)(2,1)} %get-tuple-element.21), channel_id=1, source_target_pairs={{0,8},{4,12},{8,0},{12,4},{1,9},{5,13},{9,1},{13,5},{2,10},{6,14},... | collective-permute-start | bytes 196616 | tf_op jit(solution)/shard_map/ppermute | solution.py:21
  5.8 16.8 %collective-permute-start.2 = (bf16[128,256]{1,0:T(8,128)(2,1)}, bf16[128,256]{1,0:T(8,128)(2,1)}, u32[]{:S(2)}, u32[]{:S(2)}) collective-permute-start(bf16[128,256]{1,0:T(8,128)(2,1)} %get-tuple-element.22), channel_id=1, source_target_pairs={{0,2},{2,0},{1,3},{3,1},{4,6},{6,4},{5,7},{7,5},{8,10},{10,8},{9,1... | collective-permute-start | bytes 196616 | tf_op jit(solution)/shard_map/ppermute | solution.py:21
  7.3 15.3 %collective-permute-start.1 = (bf16[128,256]{1,0:T(8,128)(2,1)}, bf16[128,256]{1,0:T(8,128)(2,1)}, u32[]{:S(2)}, u32[]{:S(2)}) collective-permute-start(bf16[128,256]{1,0:T(8,128)(2,1)} %get-tuple-element.23), channel_id=1, source_target_pairs={{0,1},{1,0},{2,3},{3,2},{4,5},{5,4},{6,7},{7,6},{8,9},{9,8},{10,11... | collective-permute-start | bytes 196616 | tf_op jit(solution)/shard_map/ppermute | solution.py:21
  7.3 15.3 %collective-permute-start.3 = (bf16[128,256]{1,0:T(8,128)(2,1)}, bf16[128,256]{1,0:T(8,128)(2,1)}, u32[]{:S(2)}, u32[]{:S(2)}) collective-permute-start(bf16[128,256]{1,0:T(8,128)(2,1)} %get-tuple-element.24), channel_id=1, source_target_pairs={{0,4},{4,0},{8,12},{12,8},{1,5},{5,1},{9,13},{13,9},{2,6},{6,2},{1... | collective-permute-start | bytes 196616 | tf_op jit(solution)/shard_map/ppermute | solution.py:21
  10.8 3.6 %copy-start.1 = (bf16[4,512,128]{2,1,0:T(8,128)(2,1)S(1)}, bf16[4,512,128]{2,1,0:T(8,128)(2,1)}, u32[]{:S(2)}) copy-start(bf16[4,512,128]{2,1,0:T(8,128)(2,1)} %param.7) | copy-start | bytes 1572868
  10.9 5.3 %slice-start = ((bf16[4,512,128]{2,1,0:T(8,128)(2,1)}), bf16[2,512,128]{2,1,0:T(8,128)(2,1)S(1)}, s32[]{:S(2)}) async-start(bf16[4,512,128]{2,1,0:T(8,128)(2,1)} %param.7), calls=%async_computation | async-start | bytes 524288 | tf_op jit(solution)/shard_map/slice | solution.py:57
  11.2 6.2 %slice-start.1 = ((bf16[4,512,128]{2,1,0:T(8,128)(2,1)}), bf16[3,512,128]{2,1,0:T(8,128)(2,1)S(1)}, s32[]{:S(2)}) async-start(bf16[4,512,128]{2,1,0:T(8,128)(2,1)} %param.7), calls=%async_computation.1 | async-start | bytes 786432 | tf_op jit(solution)/shard_map/slice | solution.py:57
  11.2 9.7 %collective-permute-start = (bf16[128,1024]{1,0:T(8,128)(2,1)S(1)}, bf16[128,1024]{1,0:T(8,128)(2,1)}, u32[]{:S(2)}, u32[]{:S(2)}) collective-permute-start(bf16[128,1024]{1,0:T(8,128)(2,1)S(1)} %fusion.3), channel_id=1, source_target_pairs={{0,1},{1,0},{2,3},{3,2},{4,5},{5,4},{6,7},{7,6},{8,9},{9,8},{10,11... | collective-permute-start | bytes 786440 | tf_op jit(solution)/shard_map/ppermute | solution.py:21
  20.4 3.0 %copy-start.12 = (bf16[128,128]{1,0:T(8,128)(2,1)S(1)}, bf16[128,128]{1,0:T(8,128)(2,1)}, u32[]{:S(2)}) copy-start(bf16[128,128]{1,0:T(8,128)(2,1)} %get-tuple-element.65) | copy-start | bytes 98308
  20.4 3.0 %copy-start.13 = (bf16[128,128]{1,0:T(8,128)(2,1)S(1)}, bf16[128,128]{1,0:T(8,128)(2,1)}, u32[]{:S(2)}) copy-start(bf16[128,128]{1,0:T(8,128)(2,1)} %get-tuple-element.66) | copy-start | bytes 98308
  20.5 3.3 %copy-start.10 = (bf16[128,128]{1,0:T(8,128)(2,1)S(1)}, bf16[128,128]{1,0:T(8,128)(2,1)}, u32[]{:S(2)}) copy-start(bf16[128,128]{1,0:T(8,128)(2,1)} %get-tuple-element.55) | copy-start | bytes 98308
  20.5 3.3 %copy-start.11 = (bf16[128,128]{1,0:T(8,128)(2,1)S(1)}, bf16[128,128]{1,0:T(8,128)(2,1)}, u32[]{:S(2)}) copy-start(bf16[128,128]{1,0:T(8,128)(2,1)} %get-tuple-element.56) | copy-start | bytes 98308
  20.9 3.7 %collective-permute-start.6 = (f32[768,128]{1,0:T(8,128)S(1)}, f32[768,128]{1,0:T(8,128)S(1)}, u32[]{:S(2)}, u32[]{:S(2)}) collective-permute-start(f32[768,128]{1,0:T(8,128)S(1)} %pad_maximum_fusion.1), channel_id=1, source_target_pairs={{0,1},{1,0},{2,3},{3,2},{4,5},{5,4},{6,7},{7,6},{8,9},{9,8},{10,11... | collective-permute-start | bytes 1179656 | tf_op jit(solution)/shard_map/ppermute | solution.py:21
  22.3 3.0 %collective-permute-start.5 = (f32[3,128,512]{2,1,0:T(8,128)S(1)}, f32[3,128,512]{2,1,0:T(8,128)S(1)}, u32[]{:S(2)}, u32[]{:S(2)}) collective-permute-start(f32[3,128,512]{2,1,0:T(8,128)S(1)} %copy-done.4), channel_id=1, source_target_pairs={{0,1},{1,0},{2,3},{3,2},{4,5},{5,4},{6,7},{7,6},{8,9},{9,8},{10,11... | collective-permute-start | bytes 2359304 | tf_op jit(solution)/shard_map/ppermute | solution.py:21
  25.7 2.4 %copy-start.6 = (bf16[128,128]{1,0:T(8,128)(2,1)S(1)}, bf16[128,128]{1,0:T(8,128)(2,1)}, u32[]{:S(2)}) copy-start(bf16[128,128]{1,0:T(8,128)(2,1)} %get-tuple-element.63) | copy-start | bytes 98308
  25.8 12.8 %collective-permute-start.7 = (bf16[512,256]{1,0:T(8,128)(2,1)S(1)}, bf16[512,256]{1,0:T(8,128)(2,1)S(1)}, u32[]{:S(2)}, u32[]{:S(2)}) collective-permute-start(bf16[512,256]{1,0:T(8,128)(2,1)S(1)} %pad_maximum_fusion.3), channel_id=1, source_target_pairs={{0,2},{2,0},{1,3},{3,1},{4,6},{6,4},{5,7},{7,5},{8,10},{10,8},{9,1... | collective-permute-start | bytes 786440 | tf_op jit(solution)/shard_map/ppermute | solution.py:21
  26.4 12.2 %collective-permute-start.8 = (f32[384,128]{1,0:T(8,128)S(1)}, f32[384,128]{1,0:T(8,128)S(1)}, u32[]{:S(2)}, u32[]{:S(2)}) collective-permute-start(f32[384,128]{1,0:T(8,128)S(1)} %pad_maximum_fusion.4), channel_id=1, source_target_pairs={{0,2},{2,0},{1,3},{3,1},{4,6},{6,4},{5,7},{7,5},{8,10},{10,8},{9,1... | collective-permute-start | bytes 589832 | tf_op jit(solution)/shard_map/ppermute | solution.py:21
  39.3 5.6 %collective-permute-start.9 = (bf16[512,128]{1,0:T(8,128)(2,1)S(1)}, bf16[512,128]{1,0:T(8,128)(2,1)S(1)}, u32[]{:S(2)}, u32[]{:S(2)}) collective-permute-start(bf16[512,128]{1,0:T(8,128)(2,1)S(1)} %pad_maximum_fusion.5), channel_id=1, source_target_pairs={{0,4},{4,0},{8,12},{12,8},{1,5},{5,1},{9,13},{13,9},{2,6},{6,2},{1... | collective-permute-start | bytes 393224 | tf_op jit(solution)/shard_map/ppermute | solution.py:21
  39.9 5.8 %collective-permute-start.10 = (f32[128,128]{1,0:T(8,128)S(1)}, f32[128,128]{1,0:T(8,128)S(1)}, u32[]{:S(2)}, u32[]{:S(2)}) collective-permute-start(f32[128,128]{1,0:T(8,128)S(1)} %slice_add_fusion.1), channel_id=1, source_target_pairs={{0,4},{4,0},{8,12},{12,8},{1,5},{5,1},{9,13},{13,9},{2,6},{6,2},{1... | collective-permute-start | bytes 196616 | tf_op jit(solution)/shard_map/ppermute | solution.py:21
  45.0 12.9 %copy-start.3 = (bf16[4,512,128]{2,1,0:T(8,128)(2,1)S(1)}, bf16[4,512,128]{2,1,0:T(8,128)(2,1)}, u32[]{:S(2)}) copy-start(bf16[4,512,128]{2,1,0:T(8,128)(2,1)} %param.8) | copy-start | bytes 1572868
  46.0 5.8 %collective-permute-start.11 = (bf16[256,128]{1,0:T(8,128)(2,1)S(1)}, bf16[256,128]{1,0:T(8,128)(2,1)S(1)}, u32[]{:S(2)}, u32[]{:S(2)}) collective-permute-start(bf16[256,128]{1,0:T(8,128)(2,1)S(1)} %pad_maximum_fusion.15), channel_id=1, source_target_pairs={{0,8},{4,12},{8,0},{12,4},{1,9},{5,13},{9,1},{13,5},{2,10},{6,14},... | collective-permute-start | bytes 196616 | tf_op jit(solution)/shard_map/ppermute | solution.py:21
  52.1 5.0 %collective-permute-start.12 = (bf16[2,128,256]{1,2,0:T(8,128)(2,1)S(1)}, bf16[2,128,256]{1,2,0:T(8,128)(2,1)S(1)}, u32[]{:S(2)}, u32[]{:S(2)}) collective-permute-start(bf16[2,128,256]{1,2,0:T(8,128)(2,1)S(1)} %pad_maximum_fusion.6), channel_id=1, source_target_pairs={{0,2},{2,0},{1,3},{3,1},{4,6},{6,4},{5,7},{7,5},{8,10},{10,8},{9,1... | collective-permute-start | bytes 393224 | tf_op jit(solution)/shard_map/ppermute | solution.py:21
  57.8 1.8 %collective-permute-start.13 = (bf16[3,128,512]{1,2,0:T(8,128)(2,1)S(1)}, bf16[3,128,512]{1,2,0:T(8,128)(2,1)S(1)}, u32[]{:S(2)}, u32[]{:S(2)}) collective-permute-start(bf16[3,128,512]{1,2,0:T(8,128)(2,1)S(1)} %pad_maximum_fusion.2), channel_id=1, source_target_pairs={{0,1},{1,0},{2,3},{3,2},{4,5},{5,4},{6,7},{7,6},{8,9},{9,8},{10,11... | collective-permute-start | bytes 1179656 | tf_op jit(solution)/shard_map/ppermute | solution.py:21
  (6 other events, 11.6 us)

commit v19 on v13

--- a/solution.py
+++ b/solution.py
@@ -126,6 +126,11 @@
                 send = cols(rest, (1 - h) * w, w)
                 parts.append(send.astype(BF16).reshape(n * rank, w))
             got = swap(jnp.concatenate(parts, axis=0), s, bits)
+            if s == levels - 1:
+                early = c0 - jnp.dot(
+                    u_basis[0], own_coefs[0], preferred_element_type=F32
+                )
+                got, early = lax.optimization_barrier((got, early))
             theirs_b = jnp.concatenate([got[:rank], got[rank : 2 * rank]], axis=1)
             if summed:
                 recv = jnp.concatenate([got[2 * rank : 3 * rank], got[3 * rank :]], axis=1)
@@ -162,8 +167,8 @@
             pending[s] = joined[i]
     for s in range(1, levels):
         full[s] = pending[s]
-    current = c0
-    for s in range(levels):
+    current = early
+    for s in range(1, levels):
         current = current - jnp.dot(u_basis[s], full[s], preferred_element_type=F32)
     return current.astype(BF16)
 

time: 57.1 us -> 59.2 us (1.037)
  matrix products: 13.7 us -> 15.5 us
  other arithmetic: 7.28 us -> 5.62 us
  waiting for transfers between devices: 18.9 us -> 20.1 us
  local copies, waits for them, and re-layouts: 4.07 us -> 5.16 us
    add x3, other arithmetic: 1.78 us -> 0.04 us  [on_device(): partial[s] = partial[s] + recv]
    dot_general x4 -> x3, matrix products: 1.73 us -> 3.29 us  [on_device(): current = current - jnp.dot(u_basis[s], full[s], preferred_element_type=F32)]
    dot_general x0 -> x1, matrix products: none -> 1.32 us  [on_device(): early = c0 - jnp.dot(u_basis[0], own_coefs[0], preferred_element_type=F32)]
    slice x2, local copies, waits for them, and re-layouts: 0.05 us -> 1.31 us  [on_device(): parts = [jnp.concatenate([c[:, :rank], c[:, rank:]], axis=0).astype(F32)]]
    ppermute x11, waiting for transfers between devices: 18.9 us -> 20.1 us  [swap(): return lax.ppermute(x, axis, [(i, i ^ 1 << stride) for i in range(n)])]
    concatenate x2, other arithmetic: 1.79 us -> 2.94 us  [gather_half(): both = jnp.concatenate([x, swap(x, bit, bits), x], axis=-1)]
    dot_general x1, matrix products: 1.83 us -> 0.71 us  [on_device(): c0 = jnp.dot(leaf_inverse, templates, preferred_element_type=F32)]
    another operation x3, other arithmetic: 1.1 us -> 0.06 us
  transfers between devices with their start and end apart: 11 -> 11, of which waited for: 6 -> 6; matrix products, arithmetic and copies ran while one was open for 30% -> 25% of each run, Pallas kernels for 0% -> 0%
where the time goes in v19:
time: 59.2 us; the launch traced here: 58.8 us
  waiting for transfers between devices  20.1 us (34%)
  matrix products  15.5 us (26%)
  starting transfers between devices  11.7 us (20%)
  other arithmetic  5.62 us (9%)
  local copies, waits for them, and re-layouts  5.16 us (9%)
  between operations  0.75 us (1%)
    ppermute x11, waiting for transfers between devices, swap(): return lax.ppermute(x, axis, [(i, i ^ 1 << stride) for i in range(n)])  20.1 us
    ppermute x11, starting transfers between devices, swap(): return lax.ppermute(x, axis, [(i, i ^ 1 << stride) for i in range(n)])  11.7 us
    dot_general x3, matrix products, on_device(): current = current - jnp.dot(u_basis[s], full[s], preferred_element_type=F32)  3.29 us
    dot_general x3, matrix products, project(): jnp.einsum('lrj,jt->lrt', vl_lo[lv], x, preferred_element_type=F32)  3.09 us
    concatenate x2, other arithmetic, gather_half(): both = jnp.concatenate([x, swap(x, bit, bits), x], axis=-1)  2.94 us
    dot_general x4, matrix products, on_device(): coefs = jnp.dot(couple[s], stacked, preferred_element_type=F32).astype(BF16)  1.93 us
    dot_general x3, matrix products, project(): jnp.einsum('lrj,jt->lrt', vl_hi[lv], x, preferred_element_type=F32)  1.93 us
    unnamed x54, local copies, waits for them, and re-layouts  1.59 us
  transfers between devices with their start and end apart: 11, of which 6 were waited for; matrix products, arithmetic and copies ran while one was open for 25% of the time, Pallas kernels for 0%

profile of v19, /device:TPU:0, one launch (start us, length us, event | category | flops | bytes accessed | tf_op | source)
XLA Modules:
  0.0 58.8 jit_solution(17426063414788565638)
XLA Ops:
  0.0 1.1 %slice_bitcast_fusion.14 = (bf16[128,256]{1,0:T(8,128)(2,1)S(1)}, bf16[128,256]{1,0:T(8,128)(2,1)S(1)}, bf16[128,256]{1,0:T(8,128)(2,1)S(1)}, bf16[128,256]{1,0:T(8,128)(2,1)S(1)}) fusion(bf16[4,1,128,256]{3,2,1,0:T(8,128)(2,1)} %param.9), kind=kLoop, calls=%fused_computation.163 | loop fusion | bytes 524288 | tf_op jit(solution)/shard_map/squeeze | solution.py:81
  2.4 4.0 %collective-permute-start.8 = (bf16[256,128]{1,0:T(8,128)(2,1)}, bf16[256,128]{1,0:T(8,128)(2,1)}, u32[]{:S(2)}, u32[]{:S(2)}) collective-permute-start(bf16[256,128]{1,0:T(8,128)(2,1)} %fusion.98), channel_id=1, source_target_pairs={{0,8},{4,12},{8,0},{12,4},{1,9},{5,13},{9,1},{13,5},{2,10},{6,14},... | collective-permute-start | bytes 196616 | tf_op jit(solution)/shard_map/ppermute | solution.py:21
  8.9 0.8 %pad_maximum_fusion = f32[1024,128]{1,0:T(8,128)} fusion(f32[128,128]{1,0:T(8,128)S(1)} %fusion.80, f32[256,128]{1,0:T(8,128)S(1)} %fusion.84, f32[384,128]{1,0:T(8,128)S(1)} %fusion.87, f32[256,128]{1,0:T(8,128)S(1)} %fusion.101), kind=kLoop, calls=%fused_computation.28 | loop fusion | flops 393216 | bytes 1048576 | tf_op jit(solution)/shard_map/concatenate | solution.py:66
  9.7 1.5 %subtract_convert_fusion = (bf16[4,128,512]{2,1,0:T(8,128)(2,1)S(1)}, bf16[4,128,512]{2,1,0:T(8,128)(2,1)S(1)}) fusion(bf16[4,512,128]{2,1,0:T(8,128)(2,1)S(1)} %copy-done.3, bf16[512,512]{1,0:T(8,128)(2,1)} %param.6), kind=kOutput, calls=%fused_computation.23 | convolution fusion | flops 269484032 | bytes 2097152 | tf_op jit(solution)/shard_map/lir,ij->lrj/dot_general | solution.py:91
  12.9 1.3 %convolution_add_fusion = f32[3,128,512]{2,1,0:T(8,128)} fusion(f32[3,128,512]{2,1,0:T(8,128)S(1)} %fusion.15, bf16[4,128,512]{2,1,0:T(8,128)(2,1)S(1)} %get-tuple-element.9, bf16[512,1024]{1,0:T(8,128)(2,1)S(1)} %copy-done, s32[]{:T(128)S(6)} %select_n.63), kind=kOutput, calls=%fused_computation.6 | convolution fusion | flops 201523200 | bytes 2621444 | tf_op jit(solution)/shard_map/lrj,jt->lrt/dot_general | solution.py:98
  14.2 1.3 %fusion.18 = f32[3,128,512]{2,1,0:T(8,128)} fusion(bf16[4,128,512]{2,1,0:T(8,128)(2,1)S(1)} %get-tuple-element.10, bf16[512,1024]{1,0:T(8,128)(2,1)S(1)} %copy-done, s32[]{:T(128)S(6)} %select_n.62), kind=kOutput, calls=%fused_computation.36 | convolution fusion | flops 201326592 | bytes 1835012 | tf_op jit(solution)/shard_map/lrj,jt->lrt/dot_general | solution.py:96
  16.4 1.6 %collective-permute-start.4 = (f32[640,128]{1,0:T(8,128)S(1)}, f32[640,128]{1,0:T(8,128)S(1)}, u32[]{:S(2)}, u32[]{:S(2)}) collective-permute-start(f32[640,128]{1,0:T(8,128)S(1)} %pad_maximum_fusion.2), channel_id=1, source_target_pairs={{0,2},{2,0},{1,3},{3,1},{4,6},{6,4},{5,7},{7,5},{8,10},{10,8},{9,1... | collective-permute-start | bytes 983048 | tf_op jit(solution)/shard_map/ppermute | solution.py:21
  18.1 1.3 %convolution_convert_fusion = bf16[256,1024]{1,0:T(8,128)(2,1)S(1)} fusion(bf16[128,1024]{1,0:T(8,128)(2,1)} %collective-permute-done.2, bf16[128,1024]{1,0:T(8,128)(2,1)S(1)} %fusion.3, bf16[256,128]{1,0:T(8,128)(2,1)S(1)} %get-tuple-element.36, bf16[256,128]{1,0:T(8,128)(2,1)S(1)} %get-tuple-element.35), kind=kOutput, calls=%fused_computation.5 | convolution fusion | flops 135790592 | bytes 1179648 | tf_op jit(solution)/shard_map/dot_general | solution.py:142
  19.9 1.3 %fusion.37 = f32[1024,512]{0,1:T(8,128)S(1)} fusion(bf16[256,1024]{1,0:T(8,128)(2,1)S(1)} %convolution_convert_fusion, bf16[4,512,128]{2,1,0:T(8,128)(2,1)} %param.8), kind=kOutput, calls=%fused_computation.65 | convolution fusion | flops 134217728 | bytes 2490368 | tf_op jit(solution)/shard_map/dot_general | solution.py:130
  22.5 1.5 %fusion.2 = f32[3,128,512]{2,1,0:T(8,128)S(1)} fusion(f32[3,128,512]{2,1,0:T(8,128)S(1)} %bitcast.124, f32[3,128,512]{2,1,0:T(8,128)} %collective-permute-done, f32[3,128,512]{2,1,0:T(8,128)S(1)} %copy-done.4, bf16[4,128,512]{2,1,0:T(8,128)(2,1)S(1)} %copy-done.2, bf16[512,1024]{1,0:T(8,128)(2,1)S(1)} %copy-done, s32[]{:T(128)S(6)} %select_n.62), kind=kOutput, calls=%fused_computation.9 | convolution fusion | flops 201916416 | bytes 4194308 | tf_op jit(solution)/shard_map/lrj,jt->lrt/dot_general | solution.py:98
  24.8 1.8 %collective-permute-done.4 = f32[640,128]{1,0:T(8,128)S(1)} collective-permute-done((f32[640,128]{1,0:T(8,128)S(1)}, f32[640,128]{1,0:T(8,128)S(1)}, u32[]{:S(2)}, u32[]{:S(2)}) %collective-permute-start.4) | collective-permute-done | bytes 327712 | tf_op jit(solution)/shard_map/ppermute | solution.py:21
  26.6 1.6 %collective-permute-start.6 = (f32[384,128]{1,0:T(8,128)S(1)}, f32[384,128]{1,0:T(8,128)S(1)}, u32[]{:S(2)}, u32[]{:S(2)}) collective-permute-start(f32[384,128]{1,0:T(8,128)S(1)} %pad_maximum_fusion.4), channel_id=1, source_target_pairs={{0,4},{4,0},{8,12},{12,8},{1,5},{5,1},{9,13},{13,9},{2,6},{6,2},{1... | collective-permute-start | bytes 589832 | tf_op jit(solution)/shard_map/ppermute | solution.py:21
  28.4 4.3 %collective-permute-done.3 = bf16[512,256]{1,0:T(8,128)(2,1)S(1)} collective-permute-done((bf16[512,256]{1,0:T(8,128)(2,1)S(1)}, bf16[512,256]{1,0:T(8,128)(2,1)S(1)}, u32[]{:S(2)}, u32[]{:S(2)}) %collective-permute-start.3) | collective-permute-done | bytes 262176 | tf_op jit(solution)/shard_map/ppermute | solution.py:21
  33.4 1.6 %collective-permute-start.5 = (bf16[512,128]{1,0:T(8,128)(2,1)S(1)}, bf16[512,128]{1,0:T(8,128)(2,1)S(1)}, u32[]{:S(2)}, u32[]{:S(2)}) collective-permute-start(bf16[512,128]{1,0:T(8,128)(2,1)S(1)} %pad_maximum_fusion.5), channel_id=1, source_target_pairs={{0,4},{4,0},{8,12},{12,8},{1,5},{5,1},{9,13},{13,9},{2,6},{6,2},{1... | collective-permute-start | bytes 393224 | tf_op jit(solution)/shard_map/ppermute | solution.py:21
  35.2 3.3 %collective-permute-done.5 = bf16[512,128]{1,0:T(8,128)(2,1)S(1)} collective-permute-done((bf16[512,128]{1,0:T(8,128)(2,1)S(1)}, bf16[512,128]{1,0:T(8,128)(2,1)S(1)}, u32[]{:S(2)}, u32[]{:S(2)}) %collective-permute-start.5) | collective-permute-done | bytes 131104 | tf_op jit(solution)/shard_map/ppermute | solution.py:21
  39.5 4.8 %collective-permute-done.7 = bf16[256,128]{1,0:T(8,128)(2,1)S(1)} collective-permute-done((bf16[256,128]{1,0:T(8,128)(2,1)S(1)}, bf16[256,128]{1,0:T(8,128)(2,1)S(1)}, u32[]{:S(2)}, u32[]{:S(2)}) %collective-permute-start.7) | collective-permute-done | bytes 65568 | tf_op jit(solution)/shard_map/ppermute | solution.py:21
  44.6 1.2 %collective-permute-start.9 = (bf16[2,128,256]{1,2,0:T(8,128)(2,1)S(1)}, bf16[2,128,256]{1,2,0:T(8,128)(2,1)}, u32[]{:S(2)}, u32[]{:S(2)}) collective-permute-start(bf16[2,128,256]{1,2,0:T(8,128)(2,1)S(1)} %pad_maximum_fusion.6), channel_id=1, source_target_pairs={{0,2},{2,0},{1,3},{3,1},{4,6},{6,4},{5,7},{7,5},{8,10},{10,8},{9,1... | collective-permute-start | bytes 393224 | tf_op jit(solution)/shard_map/ppermute | solution.py:21
  45.9 3.8 %collective-permute-done.9 = bf16[2,128,256]{1,2,0:T(8,128)(2,1)} collective-permute-done((bf16[2,128,256]{1,2,0:T(8,128)(2,1)S(1)}, bf16[2,128,256]{1,2,0:T(8,128)(2,1)}, u32[]{:S(2)}, u32[]{:S(2)}) %collective-permute-start.9) | collective-permute-done | bytes 131104 | tf_op jit(solution)/shard_map/ppermute | solution.py:21
  49.7 1.1 %fusion.32 = bf16[2,128,512]{1,2,0:T(8,128)(2,1)S(1)} fusion(s32[]{:T(128)S(6)} %select_n.78, bf16[1,128,256]{1,2,0:T(8,128)(2,1)} %copy-done.8, bf16[1,128,256]{1,2,0:T(8,128)(2,1)} %copy-done.9, bf16[2,128,256]{1,2,0:T(8,128)(2,1)} %collective-permute-done.9), kind=kLoop, calls=%fused_computation.57 | loop fusion | flops 1310720 | bytes 524292 | tf_op jit(solution)/shard_map/concatenate | solution.py:44
  50.9 0.8 %pad_maximum_fusion.1 = bf16[3,128,512]{1,2,0:T(8,128)(2,1)} fusion(bf16[2,128,512]{1,2,0:T(8,128)(2,1)S(1)} %fusion.32, bf16[1,128,512]{1,2,0:T(8,128)(2,1)S(1)} %copy.16), kind=kLoop, calls=%fused_computation.53 | loop fusion | flops 196608 | bytes 786432 | tf_op jit(solution)/shard_map/stack | solution.py:165
  51.6 2.1 %collective-permute-done.10 = bf16[3,128,512]{1,2,0:T(8,128)(2,1)} collective-permute-done((bf16[3,128,512]{1,2,0:T(8,128)(2,1)}, bf16[3,128,512]{1,2,0:T(8,128)(2,1)}, u32[]{:S(2)}, u32[]{:S(2)}) %collective-permute-start.10) | collective-permute-done | bytes 393248 | tf_op jit(solution)/shard_map/ppermute | solution.py:21
  53.7 1.8 %fusion.9 = bf16[3,128,1024]{1,2,0:T(8,128)(2,1)S(1)} fusion(s32[]{:T(128)S(6)} %select_n.79, bf16[1,128,512]{1,2,0:T(8,128)(2,1)S(1)} %copy.16, bf16[2,128,512]{1,2,0:T(8,128)(2,1)S(1)} %fusion.32, bf16[3,128,512]{1,2,0:T(8,128)(2,1)} %collective-permute-done.10), kind=kLoop, calls=%fused_computation.26 | loop fusion | flops 3932160 | bytes 1572868 | tf_op jit(solution)/shard_map/concatenate | solution.py:44
  55.5 1.3 %fusion.35 = f32[1024,512]{0,1:T(8,128)S(1)} fusion(bf16[3,128,1024]{1,2,0:T(8,128)(2,1)S(1)} %fusion.9, bf16[4,512,128]{2,1,0:T(8,128)(2,1)} %param.8), kind=kOutput, calls=%fused_computation.62 | convolution fusion | flops 134217728 | bytes 2490368 | tf_op jit(solution)/shard_map/dot_general | solution.py:172
  57.3 1.5 %fusion = bf16[512,1024]{1,0:T(8,128)(2,1)} fusion(f32[1024,512]{0,1:T(8,128)S(1)} %fusion.35, f32[512,1024]{1,0:T(8,128)S(1)} %bitcast_subtract_fusion.3, f32[1024,512]{0,1:T(8,128)S(1)} %fusion.36, bf16[3,128,1024]{1,2,0:T(8,128)(2,1)S(1)} %fusion.9, bf16[4,512,128]{2,1,0:T(8,128)(2,1)S(1)} %copy-done.7), kind=kOutput, calls=%fused_computation.1 | convolution fusion | flops 136314880 | bytes 7733248 | tf_op jit(solution)/shard_map/dot_general | solution.py:172
  (129 shorter events, 11.3 us)
Async XLA Ops:
  0.0 11.2 %copy-start = (bf16[512,1024]{1,0:T(8,128)(2,1)S(1)}, bf16[512,1024]{1,0:T(8,128)(2,1)}, u32[]{:S(2)}) copy-start(bf16[512,1024]{1,0:T(8,128)(2,1)} %param.5) | copy-start | bytes 3145732
  0.0 6.5 %copy-start.3 = (bf16[4,512,128]{2,1,0:T(8,128)(2,1)S(1)}, bf16[4,512,128]{2,1,0:T(8,128)(2,1)}, u32[]{:S(2)}) copy-start(bf16[4,512,128]{2,1,0:T(8,128)(2,1)} %param.7) | copy-start | bytes 1572868
  0.0 6.7 %slice-start = ((bf16[4,512,128]{2,1,0:T(8,128)(2,1)}), bf16[2,512,128]{2,1,0:T(8,128)(2,1)S(1)}, s32[]{:S(2)}) async-start(bf16[4,512,128]{2,1,0:T(8,128)(2,1)} %param.7), calls=%async_computation | async-start | bytes 524288 | tf_op jit(solution)/shard_map/slice | solution.py:57
  0.0 7.1 %slice-start.1 = ((bf16[4,512,128]{2,1,0:T(8,128)(2,1)}), bf16[3,512,128]{2,1,0:T(8,128)(2,1)S(1)}, s32[]{:S(2)}) async-start(bf16[4,512,128]{2,1,0:T(8,128)(2,1)} %param.7), calls=%async_computation.1 | async-start | bytes 786432 | tf_op jit(solution)/shard_map/slice | solution.py:57
  0.0 6.5 %copy-start.6 = (bf16[4,512,128]{2,1,0:T(8,128)(2,1)S(1)}, bf16[4,512,128]{2,1,0:T(8,128)(2,1)}, u32[]{:S(2)}) copy-start(bf16[4,512,128]{2,1,0:T(8,128)(2,1)} %param.8) | copy-start | bytes 1572868
  1.8 4.7 %copy-start.22 = (bf16[128,128]{1,0:T(8,128)(2,1)}, bf16[128,128]{1,0:T(8,128)(2,1)S(1)}, u32[]{:S(2)}) copy-start(bf16[128,128]{1,0:T(8,128)(2,1)S(1)} %get-tuple-element.45) | copy-start | bytes 98308
  1.8 4.7 %copy-start.24 = (bf16[128,128]{1,0:T(8,128)(2,1)}, bf16[128,128]{1,0:T(8,128)(2,1)S(1)}, u32[]{:S(2)}) copy-start(bf16[128,128]{1,0:T(8,128)(2,1)S(1)} %get-tuple-element.46) | copy-start | bytes 98308
  2.4 13.1 %collective-permute-start.8 = (bf16[256,128]{1,0:T(8,128)(2,1)}, bf16[256,128]{1,0:T(8,128)(2,1)}, u32[]{:S(2)}, u32[]{:S(2)}) collective-permute-start(bf16[256,128]{1,0:T(8,128)(2,1)} %fusion.98), channel_id=1, source_target_pairs={{0,8},{4,12},{8,0},{12,4},{1,9},{5,13},{9,1},{13,5},{2,10},{6,14},... | collective-permute-start | bytes 196616 | tf_op jit(solution)/shard_map/ppermute | solution.py:21
  9.7 6.6 %collective-permute-start.1 = (f32[1024,128]{1,0:T(8,128)}, f32[1024,128]{1,0:T(8,128)S(1)}, u32[]{:S(2)}, u32[]{:S(2)}) collective-permute-start(f32[1024,128]{1,0:T(8,128)} %pad_maximum_fusion), channel_id=1, source_target_pairs={{0,1},{1,0},{2,3},{3,2},{4,5},{5,4},{6,7},{7,6},{8,9},{9,8},{10,11... | collective-permute-start | bytes 1572872 | tf_op jit(solution)/shard_map/ppermute | solution.py:21
  11.9 6.2 %collective-permute-start.2 = (bf16[128,1024]{1,0:T(8,128)(2,1)S(1)}, bf16[128,1024]{1,0:T(8,128)(2,1)}, u32[]{:S(2)}, u32[]{:S(2)}) collective-permute-start(bf16[128,1024]{1,0:T(8,128)(2,1)S(1)} %fusion.3), channel_id=1, source_target_pairs={{0,1},{1,0},{2,3},{3,2},{4,5},{5,4},{6,7},{7,6},{8,9},{9,8},{10,11... | collective-permute-start | bytes 786440 | tf_op jit(solution)/shard_map/ppermute | solution.py:21
  12.9 3.4 %copy-start.23 = (bf16[128,128]{1,0:T(8,128)(2,1)S(1)}, bf16[128,128]{1,0:T(8,128)(2,1)}, u32[]{:S(2)}) copy-start(bf16[128,128]{1,0:T(8,128)(2,1)} %copy-done.22) | copy-start | bytes 98308
  12.9 3.4 %copy-start.25 = (bf16[128,128]{1,0:T(8,128)(2,1)S(1)}, bf16[128,128]{1,0:T(8,128)(2,1)}, u32[]{:S(2)}) copy-start(bf16[128,128]{1,0:T(8,128)(2,1)} %copy-done.24) | copy-start | bytes 98308
  14.2 7.8 %collective-permute-start = (f32[3,128,512]{2,1,0:T(8,128)}, f32[3,128,512]{2,1,0:T(8,128)}, u32[]{:S(2)}, u32[]{:S(2)}) collective-permute-start(f32[3,128,512]{2,1,0:T(8,128)} %convolution_add_fusion), channel_id=1, source_target_pairs={{0,1},{1,0},{2,3},{3,2},{4,5},{5,4},{6,7},{7,6},{8,9},{9,8},{10,11... | collective-permute-start | bytes 2359304 | tf_op jit(solution)/shard_map/ppermute | solution.py:21
  16.4 10.2 %collective-permute-start.4 = (f32[640,128]{1,0:T(8,128)S(1)}, f32[640,128]{1,0:T(8,128)S(1)}, u32[]{:S(2)}, u32[]{:S(2)}) collective-permute-start(f32[640,128]{1,0:T(8,128)S(1)} %pad_maximum_fusion.2), channel_id=1, source_target_pairs={{0,2},{2,0},{1,3},{3,1},{4,6},{6,4},{5,7},{7,5},{8,10},{10,8},{9,1... | collective-permute-start | bytes 983048 | tf_op jit(solution)/shard_map/ppermute | solution.py:21
  24.1 4.3 %copy-start.15 = (bf16[128,128]{1,0:T(8,128)(2,1)S(1)}, bf16[128,128]{1,0:T(8,128)(2,1)}, u32[]{:S(2)}) copy-start(bf16[128,128]{1,0:T(8,128)(2,1)} %get-tuple-element.53) | copy-start | bytes 98308
  24.1 4.3 %copy-start.17 = (bf16[128,128]{1,0:T(8,128)(2,1)S(1)}, bf16[128,128]{1,0:T(8,128)(2,1)}, u32[]{:S(2)}) copy-start(bf16[128,128]{1,0:T(8,128)(2,1)} %get-tuple-element.54) | copy-start | bytes 98308
  24.2 8.5 %collective-permute-start.3 = (bf16[512,256]{1,0:T(8,128)(2,1)S(1)}, bf16[512,256]{1,0:T(8,128)(2,1)S(1)}, u32[]{:S(2)}, u32[]{:S(2)}) collective-permute-start(bf16[512,256]{1,0:T(8,128)(2,1)S(1)} %pad_maximum_fusion.3), channel_id=1, source_target_pairs={{0,2},{2,0},{1,3},{3,1},{4,6},{6,4},{5,7},{7,5},{8,10},{10,8},{9,1... | collective-permute-start | bytes 786440 | tf_op jit(solution)/shard_map/ppermute | solution.py:21
  26.6 8.4 %collective-permute-start.6 = (f32[384,128]{1,0:T(8,128)S(1)}, f32[384,128]{1,0:T(8,128)S(1)}, u32[]{:S(2)}, u32[]{:S(2)}) collective-permute-start(f32[384,128]{1,0:T(8,128)S(1)} %pad_maximum_fusion.4), channel_id=1, source_target_pairs={{0,4},{4,0},{8,12},{12,8},{1,5},{5,1},{9,13},{13,9},{2,6},{6,2},{1... | collective-permute-start | bytes 589832 | tf_op jit(solution)/shard_map/ppermute | solution.py:21
  33.4 5.0 %collective-permute-start.5 = (bf16[512,128]{1,0:T(8,128)(2,1)S(1)}, bf16[512,128]{1,0:T(8,128)(2,1)S(1)}, u32[]{:S(2)}, u32[]{:S(2)}) collective-permute-start(bf16[512,128]{1,0:T(8,128)(2,1)S(1)} %pad_maximum_fusion.5), channel_id=1, source_target_pairs={{0,4},{4,0},{8,12},{12,8},{1,5},{5,1},{9,13},{13,9},{2,6},{6,2},{1... | collective-permute-start | bytes 393224 | tf_op jit(solution)/shard_map/ppermute | solution.py:21
  39.0 5.2 %collective-permute-start.7 = (bf16[256,128]{1,0:T(8,128)(2,1)S(1)}, bf16[256,128]{1,0:T(8,128)(2,1)S(1)}, u32[]{:S(2)}, u32[]{:S(2)}) collective-permute-start(bf16[256,128]{1,0:T(8,128)(2,1)S(1)} %pad_maximum_fusion.18), channel_id=1, source_target_pairs={{0,8},{4,12},{8,0},{12,4},{1,9},{5,13},{9,1},{13,5},{2,10},{6,14},... | collective-permute-start | bytes 196616 | tf_op jit(solution)/shard_map/ppermute | solution.py:21
  39.5 6.3 %copy-start.8 = (bf16[1,128,256]{1,2,0:T(8,128)(2,1)}, bf16[1,128,256]{1,2,0:T(8,128)(2,1)S(1)}, u32[]{:S(2)}) copy-start(bf16[1,128,256]{1,2,0:T(8,128)(2,1)S(1)} %slice_bitcast_fusion.13) | copy-start | bytes 196612
  44.6 5.1 %collective-permute-start.9 = (bf16[2,128,256]{1,2,0:T(8,128)(2,1)S(1)}, bf16[2,128,256]{1,2,0:T(8,128)(2,1)}, u32[]{:S(2)}, u32[]{:S(2)}) collective-permute-start(bf16[2,128,256]{1,2,0:T(8,128)(2,1)S(1)} %pad_maximum_fusion.6), channel_id=1, source_target_pairs={{0,2},{2,0},{1,3},{3,1},{4,6},{6,4},{5,7},{7,5},{8,10},{10,8},{9,1... | collective-permute-start | bytes 393224 | tf_op jit(solution)/shard_map/ppermute | solution.py:21
  51.6 2.1 %collective-permute-start.10 = (bf16[3,128,512]{1,2,0:T(8,128)(2,1)}, bf16[3,128,512]{1,2,0:T(8,128)(2,1)}, u32[]{:S(2)}, u32[]{:S(2)}) collective-permute-start(bf16[3,128,512]{1,2,0:T(8,128)(2,1)} %pad_maximum_fusion.1), channel_id=1, source_target_pairs={{0,1},{1,0},{2,3},{3,2},{4,5},{5,4},{6,7},{7,6},{8,9},{9,8},{10,11... | collective-permute-start | bytes 1179656 | tf_op jit(solution)/shard_map/ppermute | solution.py:21
  51.6 5.2 %copy-start.7 = (bf16[4,512,128]{2,1,0:T(8,128)(2,1)S(1)}, bf16[4,512,128]{2,1,0:T(8,128)(2,1)}, u32[]{:S(2)}) copy-start(bf16[4,512,128]{2,1,0:T(8,128)(2,1)} %param.8) | copy-start | bytes 1572868
  (15 other events, 28.8 us)

commit v20 on v19

--- a/solution.py
+++ b/solution.py
@@ -125,11 +125,16 @@
                 keep = cols(rest, h * w, w)
                 send = cols(rest, (1 - h) * w, w)
                 parts.append(send.astype(BF16).reshape(n * rank, w))
-            got = swap(jnp.concatenate(parts, axis=0), s, bits)
+            payload = jnp.concatenate(parts, axis=0)
             if s == levels - 1:
-                early = c0 - jnp.dot(
-                    u_basis[0], own_coefs[0], preferred_element_type=F32
+                payload, lin, tin, first = lax.optimization_barrier(
+                    (payload, leaf_inverse, templates, own_coefs[0])
                 )
+                early = jnp.dot(lin, tin, preferred_element_type=F32) - jnp.dot(
+                    u_basis[0], first, preferred_element_type=F32
+                )
+            got = swap(payload, s, bits)
+            if s == levels - 1:
                 got, early = lax.optimization_barrier((got, early))
             theirs_b = jnp.concatenate([got[:rank], got[rank : 2 * rank]], axis=1)
             if summed:

time: 59.2 us -> 60.2 us (1.017)
  other arithmetic: 5.62 us -> 9.96 us
  waiting for transfers between devices: 20.1 us -> 18.5 us
  local copies, waits for them, and re-layouts: 5.16 us -> 3.82 us
    add x3, other arithmetic: 0.04 us -> 1.78 us  [on_device(): partial[s] = partial[s] + recv]
    ppermute x11, waiting for transfers between devices: 20.1 us -> 18.5 us  [swap(): return lax.ppermute(x, axis, [(i, i ^ 1 << stride) for i in range(n)])]
    select_n x4, other arithmetic: 0.13 us -> 1.68 us  [on_device(): jnp.where(lower, first, second)]
    slice x2, local copies, waits for them, and re-layouts: 1.31 us -> 0.05 us  [on_device(): parts = [jnp.concatenate([c[:, :rank], c[:, rank:]], axis=0).astype(F32)]]
    unnamed x54 -> x26, local copies, waits for them, and re-layouts: 1.59 us -> 0.38 us
    slice x3, local copies, waits for them, and re-layouts: 0.03 us -> 1.15 us  [on_device(): recv = got[at:at + n]]
    another operation x3, other arithmetic: 0.06 us -> 1.1 us
    dot_general x3, matrix products: 1.93 us -> 1.04 us  [project(): jnp.einsum('lrj,jt->lrt', vl_hi[lv], x, preferred_element_type=F32)]
  transfers between devices with their start and end apart: 11 -> 11, of which waited for: 6 -> 6; matrix products, arithmetic and copies ran while one was open for 25% -> 33% of each run, Pallas kernels for 0% -> 0%
where the time goes in v20:
time: 60.2 us; the launch traced here: 59.5 us
  waiting for transfers between devices  18.5 us (31%)
  matrix products  15.4 us (26%)
  starting transfers between devices  11.1 us (18%)
  other arithmetic  9.96 us (17%)
  local copies, waits for them, and re-layouts  3.82 us (6%)
  between operations  0.64 us (1%)
    ppermute x11, waiting for transfers between devices, swap(): return lax.ppermute(x, axis, [(i, i ^ 1 << stride) for i in range(n)])  18.5 us
    ppermute x11, starting transfers between devices, swap(): return lax.ppermute(x, axis, [(i, i ^ 1 << stride) for i in range(n)])  11.1 us
    dot_general x3, matrix products, project(): jnp.einsum('lrj,jt->lrt', vl_lo[lv], x, preferred_element_type=F32)  3.81 us
    dot_general x3, matrix products, on_device(): current = current - jnp.dot(u_basis[s], full[s], preferred_element_type=F32)  3.29 us
    concatenate x2, other arithmetic, gather_half(): both = jnp.concatenate([x, swap(x, bit, bits), x], axis=-1)  2.94 us
    dot_general x4, matrix products, on_device(): coefs = jnp.dot(couple[s], stacked, preferred_element_type=F32).astype(BF16)  2.01 us
    add x3, other arithmetic, on_device(): partial[s] = partial[s] + recv  1.78 us
    select_n x4, other arithmetic, on_device(): jnp.where(lower, first, second)  1.68 us
  transfers between devices with their start and end apart: 11, of which 6 were waited for; matrix products, arithmetic and copies ran while one was open for 33% of the time, Pallas kernels for 0%

profile of v20, /device:TPU:0, one launch (start us, length us, event | category | flops | bytes accessed | tf_op | source)
XLA Modules:
  0.0 59.5 jit_solution(14625382818077424964)
XLA Ops:
  0.0 1.1 %slice_bitcast_fusion.14 = (bf16[128,256]{1,0:T(8,128)(2,1)S(1)}, bf16[128,256]{1,0:T(8,128)(2,1)S(1)}, bf16[128,256]{1,0:T(8,128)(2,1)S(1)}, bf16[128,256]{1,0:T(8,128)(2,1)S(1)}) fusion(bf16[4,1,128,256]{3,2,1,0:T(8,128)(2,1)} %param.9), kind=kLoop, calls=%fused_computation.162 | loop fusion | bytes 524288 | tf_op jit(solution)/shard_map/squeeze | solution.py:81
  1.9 4.0 %collective-permute-start.8 = (bf16[256,128]{1,0:T(8,128)(2,1)}, bf16[256,128]{1,0:T(8,128)(2,1)}, u32[]{:S(2)}, u32[]{:S(2)}) collective-permute-start(bf16[256,128]{1,0:T(8,128)(2,1)} %fusion.97), channel_id=1, source_target_pairs={{0,8},{4,12},{8,0},{12,4},{1,9},{5,13},{9,1},{13,5},{2,10},{6,14},... | collective-permute-start | bytes 196616 | tf_op jit(solution)/shard_map/ppermute | solution.py:21
  7.9 1.5 %subtract_convert_fusion = (bf16[4,128,512]{2,1,0:T(8,128)(2,1)S(1)}, bf16[4,128,512]{2,1,0:T(8,128)(2,1)S(1)}) fusion(bf16[4,512,128]{2,1,0:T(8,128)(2,1)S(1)} %copy-done.1, bf16[512,512]{1,0:T(8,128)(2,1)} %param.6), kind=kOutput, calls=%fused_computation.23 | convolution fusion | flops 269484032 | bytes 2097152 | tf_op jit(solution)/shard_map/lir,ij->lrj/dot_general | solution.py:91
  9.8 1.0 %fusion.3 = bf16[128,1024]{1,0:T(8,128)(2,1)} fusion(f32[128,1024]{1,0:T(8,128)S(1)} %fusion.49, bf16[512,1024]{1,0:T(8,128)(2,1)S(1)} %copy-done, bf16[4,128,512]{2,1,0:T(8,128)(2,1)S(1)} %get-tuple-element.17), kind=kOutput, calls=%fused_computation.11 | convolution fusion | flops 134479872 | bytes 1966080 | tf_op jit(solution)/shard_map/lrj,jt->lrt/dot_general | solution.py:98
  11.7 1.3 %convolution_add_fusion = f32[3,128,512]{2,1,0:T(8,128)} fusion(f32[3,128,512]{2,1,0:T(8,128)S(1)} %fusion.15, bf16[4,128,512]{2,1,0:T(8,128)(2,1)S(1)} %get-tuple-element.17, bf16[512,1024]{1,0:T(8,128)(2,1)S(1)} %copy-done, s32[]{:T(128)S(6)} %select_n.63), kind=kOutput, calls=%fused_computation.6 | convolution fusion | flops 201523200 | bytes 2621444 | tf_op jit(solution)/shard_map/lrj,jt->lrt/dot_general | solution.py:98
  15.0 0.9 %slice_add_fusion = f32[256,128]{1,0:T(8,128)S(1)} fusion(f32[256,128]{1,0:T(8,128)S(1)} %fusion.82, f32[1024,128]{1,0:T(8,128)} %collective-permute-done.1), kind=kLoop, calls=%fused_computation.85 | loop fusion | flops 32768 | bytes 393216 | tf_op jit(solution)/shard_map/add | solution.py:77
  16.8 1.6 %collective-permute-start.4 = (f32[640,128]{1,0:T(8,128)S(1)}, f32[640,128]{1,0:T(8,128)S(1)}, u32[]{:S(2)}, u32[]{:S(2)}) collective-permute-start(f32[640,128]{1,0:T(8,128)S(1)} %pad_maximum_fusion.2), channel_id=1, source_target_pairs={{0,2},{2,0},{1,3},{3,1},{4,6},{6,4},{5,7},{7,5},{8,10},{10,8},{9,1... | collective-permute-start | bytes 983048 | tf_op jit(solution)/shard_map/ppermute | solution.py:21
  18.3 1.1 %convert.16 = bf16[1024,128]{1,0:T(8,128)(2,1)S(1)} convert(f32[1024,128]{1,0:T(8,128)} %collective-permute-done.1) | non-fusion elementwise | flops 131072 | bytes 786432 | tf_op jit(solution)/shard_map/convert.5
  20.2 1.3 %convolution_convert_fusion = bf16[256,1024]{1,0:T(8,128)(2,1)S(1)} fusion(bf16[128,1024]{1,0:T(8,128)(2,1)} %collective-permute-done.2, bf16[128,1024]{1,0:T(8,128)(2,1)} %fusion.3, bf16[256,128]{1,0:T(8,128)(2,1)S(1)} %get-tuple-element.44, bf16[256,128]{1,0:T(8,128)(2,1)S(1)} %get-tuple-element.43), kind=kOutput, calls=%fused_computation.5 | convolution fusion | flops 135790592 | bytes 1179648 | tf_op jit(solution)/shard_map/dot_general | solution.py:147
  21.6 1.1 %slice.300 = f32[384,128]{1,0:T(8,128)S(1)} slice(f32[1024,128]{1,0:T(8,128)} %collective-permute-done.1), slice={[256:640], [0:128]} | slice | bytes 393216 | tf_op jit(solution)/shard_map/slice | solution.py:72
  23.2 1.5 %fusion.2 = f32[3,128,512]{2,1,0:T(8,128)S(1)} fusion(f32[3,128,512]{2,1,0:T(8,128)S(1)} %bitcast.125, f32[3,128,512]{2,1,0:T(8,128)} %collective-permute-done, f32[3,128,512]{2,1,0:T(8,128)S(1)} %fusion.18, bf16[4,128,512]{2,1,0:T(8,128)(2,1)S(1)} %get-tuple-element.17, bf16[512,1024]{1,0:T(8,128)(2,1)S(1)} %copy-done, s32[]{:T(128)S(6)} %select_n.62), kind=kOutput, calls=%fused_computation.9 | convolution fusion | flops 201916416 | bytes 4194308 | tf_op jit(solution)/shard_map/lrj,jt->lrt/dot_general | solution.py:98
  25.5 1.4 %collective-permute-done.4 = f32[640,128]{1,0:T(8,128)S(1)} collective-permute-done((f32[640,128]{1,0:T(8,128)S(1)}, f32[640,128]{1,0:T(8,128)S(1)}, u32[]{:S(2)}, u32[]{:S(2)}) %collective-permute-start.4) | collective-permute-done | bytes 327712 | tf_op jit(solution)/shard_map/ppermute | solution.py:21
  27.0 1.6 %collective-permute-start.6 = (f32[384,128]{1,0:T(8,128)S(1)}, f32[384,128]{1,0:T(8,128)S(1)}, u32[]{:S(2)}, u32[]{:S(2)}) collective-permute-start(f32[384,128]{1,0:T(8,128)S(1)} %pad_maximum_fusion.4), channel_id=1, source_target_pairs={{0,4},{4,0},{8,12},{12,8},{1,5},{5,1},{9,13},{13,9},{2,6},{6,2},{1... | collective-permute-start | bytes 589832 | tf_op jit(solution)/shard_map/ppermute | solution.py:21
  28.7 4.7 %collective-permute-done.3 = bf16[512,256]{1,0:T(8,128)(2,1)S(1)} collective-permute-done((bf16[512,256]{1,0:T(8,128)(2,1)S(1)}, bf16[512,256]{1,0:T(8,128)(2,1)S(1)}, u32[]{:S(2)}, u32[]{:S(2)}) %collective-permute-start.3) | collective-permute-done | bytes 262176 | tf_op jit(solution)/shard_map/ppermute | solution.py:21
  34.1 1.6 %collective-permute-start.5 = (bf16[512,128]{1,0:T(8,128)(2,1)S(1)}, bf16[512,128]{1,0:T(8,128)(2,1)S(1)}, u32[]{:S(2)}, u32[]{:S(2)}) collective-permute-start(bf16[512,128]{1,0:T(8,128)(2,1)S(1)} %pad_maximum_fusion.5), channel_id=1, source_target_pairs={{0,4},{4,0},{8,12},{12,8},{1,5},{5,1},{9,13},{13,9},{2,6},{6,2},{1... | collective-permute-start | bytes 393224 | tf_op jit(solution)/shard_map/ppermute | solution.py:21
  35.9 3.3 %collective-permute-done.5 = bf16[512,128]{1,0:T(8,128)(2,1)S(1)} collective-permute-done((bf16[512,128]{1,0:T(8,128)(2,1)S(1)}, bf16[512,128]{1,0:T(8,128)(2,1)S(1)}, u32[]{:S(2)}, u32[]{:S(2)}) %collective-permute-start.5) | collective-permute-done | bytes 131104 | tf_op jit(solution)/shard_map/ppermute | solution.py:21
  40.1 1.3 %fusion.84 = f32[1024,512]{0,1:T(8,128)S(1)} fusion(bf16[128,1024]{1,0:T(8,128)(2,1)S(1)} %slice-done.2, bf16[4,512,128]{2,1,0:T(8,128)(2,1)} %param.8), kind=kOutput, calls=%fused_computation.125 | convolution fusion | flops 134217728 | bytes 2490368 | tf_op jit(solution)/shard_map/dot_general | solution.py:133
  42.2 2.7 %collective-permute-done.7 = bf16[256,128]{1,0:T(8,128)(2,1)S(1)} collective-permute-done((bf16[256,128]{1,0:T(8,128)(2,1)S(1)}, bf16[256,128]{1,0:T(8,128)(2,1)S(1)}, u32[]{:S(2)}, u32[]{:S(2)}) %collective-permute-start.7) | collective-permute-done | bytes 65568 | tf_op jit(solution)/shard_map/ppermute | solution.py:21
  46.1 4.3 %collective-permute-done.9 = bf16[2,128,256]{1,2,0:T(8,128)(2,1)} collective-permute-done((bf16[2,128,256]{1,2,0:T(8,128)(2,1)S(1)}, bf16[2,128,256]{1,2,0:T(8,128)(2,1)}, u32[]{:S(2)}, u32[]{:S(2)}) %collective-permute-start.9) | collective-permute-done | bytes 131104 | tf_op jit(solution)/shard_map/ppermute | solution.py:21
  50.4 1.1 %fusion.32 = bf16[2,128,512]{1,2,0:T(8,128)(2,1)S(1)} fusion(s32[]{:T(128)S(6)} %select_n.78, bf16[1,128,256]{1,2,0:T(8,128)(2,1)} %copy-done.6, bf16[1,128,256]{1,2,0:T(8,128)(2,1)} %copy-done.7, bf16[2,128,256]{1,2,0:T(8,128)(2,1)} %collective-permute-done.9), kind=kLoop, calls=%fused_computation.57 | loop fusion | flops 1310720 | bytes 524292 | tf_op jit(solution)/shard_map/concatenate | solution.py:44
  52.3 2.1 %collective-permute-done.10 = bf16[3,128,512]{1,2,0:T(8,128)(2,1)} collective-permute-done((bf16[3,128,512]{1,2,0:T(8,128)(2,1)}, bf16[3,128,512]{1,2,0:T(8,128)(2,1)}, u32[]{:S(2)}, u32[]{:S(2)}) %collective-permute-start.10) | collective-permute-done | bytes 393248 | tf_op jit(solution)/shard_map/ppermute | solution.py:21
  54.4 1.8 %fusion.9 = bf16[3,128,1024]{1,2,0:T(8,128)(2,1)S(1)} fusion(s32[]{:T(128)S(6)} %select_n.79, bf16[1,128,512]{1,2,0:T(8,128)(2,1)S(1)} %copy.16, bf16[2,128,512]{1,2,0:T(8,128)(2,1)S(1)} %fusion.32, bf16[3,128,512]{1,2,0:T(8,128)(2,1)} %collective-permute-done.10), kind=kLoop, calls=%fused_computation.26 | loop fusion | flops 3932160 | bytes 1572868 | tf_op jit(solution)/shard_map/concatenate | solution.py:44
  56.2 1.3 %fusion.35 = f32[1024,512]{0,1:T(8,128)S(1)} fusion(bf16[3,128,1024]{1,2,0:T(8,128)(2,1)S(1)} %fusion.9, bf16[4,512,128]{2,1,0:T(8,128)(2,1)} %param.8), kind=kOutput, calls=%fused_computation.62 | convolution fusion | flops 134217728 | bytes 2490368 | tf_op jit(solution)/shard_map/dot_general | solution.py:177
  58.0 1.5 %fusion = bf16[512,1024]{1,0:T(8,128)(2,1)} fusion(f32[1024,512]{0,1:T(8,128)S(1)} %fusion.35, f32[512,1024]{1,0:T(8,128)S(1)} %bitcast_subtract_fusion.3, f32[1024,512]{0,1:T(8,128)S(1)} %fusion.36, bf16[3,128,1024]{1,2,0:T(8,128)(2,1)S(1)} %fusion.9, bf16[4,512,128]{2,1,0:T(8,128)(2,1)S(1)} %copy-done.4), kind=kOutput, calls=%fused_computation.1 | convolution fusion | flops 136314880 | bytes 7733248 | tf_op jit(solution)/shard_map/dot_general | solution.py:177
  (103 shorter events, 13.5 us)
Async XLA Ops:
  0.0 9.4 %copy-start = (bf16[512,1024]{1,0:T(8,128)(2,1)S(1)}, bf16[512,1024]{1,0:T(8,128)(2,1)}, u32[]{:S(2)}) copy-start(bf16[512,1024]{1,0:T(8,128)(2,1)} %param.5) | copy-start | bytes 3145732
  0.0 5.9 %copy-start.1 = (bf16[4,512,128]{2,1,0:T(8,128)(2,1)S(1)}, bf16[4,512,128]{2,1,0:T(8,128)(2,1)}, u32[]{:S(2)}) copy-start(bf16[4,512,128]{2,1,0:T(8,128)(2,1)} %param.7) | copy-start | bytes 1572868
  0.0 6.1 %slice-start = ((bf16[4,512,128]{2,1,0:T(8,128)(2,1)}), bf16[2,512,128]{2,1,0:T(8,128)(2,1)S(1)}, s32[]{:S(2)}) async-start(bf16[4,512,128]{2,1,0:T(8,128)(2,1)} %param.7), calls=%async_computation | async-start | bytes 524288 | tf_op jit(solution)/shard_map/slice | solution.py:57
  0.0 6.5 %slice-start.1 = ((bf16[4,512,128]{2,1,0:T(8,128)(2,1)}), bf16[3,512,128]{2,1,0:T(8,128)(2,1)S(1)}, s32[]{:S(2)}) async-start(bf16[4,512,128]{2,1,0:T(8,128)(2,1)} %param.7), calls=%async_computation.1 | async-start | bytes 786432 | tf_op jit(solution)/shard_map/slice | solution.py:57
  0.0 5.9 %copy-start.3 = (bf16[4,512,128]{2,1,0:T(8,128)(2,1)S(1)}, bf16[4,512,128]{2,1,0:T(8,128)(2,1)}, u32[]{:S(2)}) copy-start(bf16[4,512,128]{2,1,0:T(8,128)(2,1)} %param.8) | copy-start | bytes 1572868
  1.2 5.1 %copy-start.10 = (bf16[128,128]{1,0:T(8,128)(2,1)}, bf16[128,128]{1,0:T(8,128)(2,1)S(1)}, u32[]{:S(2)}) copy-start(bf16[128,128]{1,0:T(8,128)(2,1)S(1)} %get-tuple-element.53) | copy-start | bytes 98308
  1.2 5.1 %copy-start.11 = (bf16[128,128]{1,0:T(8,128)(2,1)}, bf16[128,128]{1,0:T(8,128)(2,1)S(1)}, u32[]{:S(2)}) copy-start(bf16[128,128]{1,0:T(8,128)(2,1)S(1)} %get-tuple-element.54) | copy-start | bytes 98308
  1.9 11.5 %collective-permute-start.8 = (bf16[256,128]{1,0:T(8,128)(2,1)}, bf16[256,128]{1,0:T(8,128)(2,1)}, u32[]{:S(2)}, u32[]{:S(2)}) collective-permute-start(bf16[256,128]{1,0:T(8,128)(2,1)} %fusion.97), channel_id=1, source_target_pairs={{0,8},{4,12},{8,0},{12,4},{1,9},{5,13},{9,1},{13,5},{2,10},{6,14},... | collective-permute-start | bytes 196616 | tf_op jit(solution)/shard_map/ppermute | solution.py:21
  7.0 2.7 %copy-start.8 = (bf16[128,128]{1,0:T(8,128)(2,1)}, bf16[128,128]{1,0:T(8,128)(2,1)S(1)}, u32[]{:S(2)}) copy-start(bf16[128,128]{1,0:T(8,128)(2,1)S(1)} %get-tuple-element.67) | copy-start | bytes 98308
  7.9 7.1 %collective-permute-start.1 = (f32[1024,128]{1,0:T(8,128)}, f32[1024,128]{1,0:T(8,128)}, u32[]{:S(2)}, u32[]{:S(2)}) collective-permute-start(f32[1024,128]{1,0:T(8,128)} %pad_maximum_fusion), channel_id=1, source_target_pairs={{0,1},{1,0},{2,3},{3,2},{4,5},{5,4},{6,7},{7,6},{8,9},{9,8},{10,11... | collective-permute-start | bytes 1572872 | tf_op jit(solution)/shard_map/ppermute | solution.py:21
  10.8 9.4 %collective-permute-start.2 = (bf16[128,1024]{1,0:T(8,128)(2,1)}, bf16[128,1024]{1,0:T(8,128)(2,1)}, u32[]{:S(2)}, u32[]{:S(2)}) collective-permute-start(bf16[128,1024]{1,0:T(8,128)(2,1)} %fusion.3), channel_id=1, source_target_pairs={{0,1},{1,0},{2,3},{3,2},{4,5},{5,4},{6,7},{7,6},{8,9},{9,8},{10,11... | collective-permute-start | bytes 786440 | tf_op jit(solution)/shard_map/ppermute | solution.py:21
  12.9 10.3 %collective-permute-start = (f32[3,128,512]{2,1,0:T(8,128)}, f32[3,128,512]{2,1,0:T(8,128)}, u32[]{:S(2)}, u32[]{:S(2)}) collective-permute-start(f32[3,128,512]{2,1,0:T(8,128)} %convolution_add_fusion), channel_id=1, source_target_pairs={{0,1},{1,0},{2,3},{3,2},{4,5},{5,4},{6,7},{7,6},{8,9},{9,8},{10,11... | collective-permute-start | bytes 2359304 | tf_op jit(solution)/shard_map/ppermute | solution.py:21
  16.8 10.2 %collective-permute-start.4 = (f32[640,128]{1,0:T(8,128)S(1)}, f32[640,128]{1,0:T(8,128)S(1)}, u32[]{:S(2)}, u32[]{:S(2)}) collective-permute-start(f32[640,128]{1,0:T(8,128)S(1)} %pad_maximum_fusion.2), channel_id=1, source_target_pairs={{0,2},{2,0},{1,3},{3,1},{4,6},{6,4},{5,7},{7,5},{8,10},{10,8},{9,1... | collective-permute-start | bytes 983048 | tf_op jit(solution)/shard_map/ppermute | solution.py:21
  21.6 3.2 %copy-start.5 = (bf16[256,1024]{1,0:T(8,128)(2,1)}, bf16[256,1024]{1,0:T(8,128)(2,1)S(1)}, u32[]{:S(2)}) copy-start(bf16[256,1024]{1,0:T(8,128)(2,1)S(1)} %convolution_convert_fusion) | copy-start | bytes 1572868
  24.9 8.5 %collective-permute-start.3 = (bf16[512,256]{1,0:T(8,128)(2,1)S(1)}, bf16[512,256]{1,0:T(8,128)(2,1)S(1)}, u32[]{:S(2)}, u32[]{:S(2)}) collective-permute-start(bf16[512,256]{1,0:T(8,128)(2,1)S(1)} %pad_maximum_fusion.3), channel_id=1, source_target_pairs={{0,2},{2,0},{1,3},{3,1},{4,6},{6,4},{5,7},{7,5},{8,10},{10,8},{9,1... | collective-permute-start | bytes 786440 | tf_op jit(solution)/shard_map/ppermute | solution.py:21
  27.0 8.8 %collective-permute-start.6 = (f32[384,128]{1,0:T(8,128)S(1)}, f32[384,128]{1,0:T(8,128)S(1)}, u32[]{:S(2)}, u32[]{:S(2)}) collective-permute-start(f32[384,128]{1,0:T(8,128)S(1)} %pad_maximum_fusion.4), channel_id=1, source_target_pairs={{0,4},{4,0},{8,12},{12,8},{1,5},{5,1},{9,13},{13,9},{2,6},{6,2},{1... | collective-permute-start | bytes 589832 | tf_op jit(solution)/shard_map/ppermute | solution.py:21
  34.0 6.2 %slice-start.2 = ((bf16[256,1024]{1,0:T(8,128)(2,1)}), bf16[128,1024]{1,0:T(8,128)(2,1)S(1)}, s32[]{:S(2)}) async-start(bf16[256,1024]{1,0:T(8,128)(2,1)} %copy-done.5), calls=%async_computation.2 | async-start | bytes 524288 | tf_op jit(solution)/shard_map/slice | solution.py:148
  34.1 5.0 %collective-permute-start.5 = (bf16[512,128]{1,0:T(8,128)(2,1)S(1)}, bf16[512,128]{1,0:T(8,128)(2,1)S(1)}, u32[]{:S(2)}, u32[]{:S(2)}) collective-permute-start(bf16[512,128]{1,0:T(8,128)(2,1)S(1)} %pad_maximum_fusion.5), channel_id=1, source_target_pairs={{0,4},{4,0},{8,12},{12,8},{1,5},{5,1},{9,13},{13,9},{2,6},{6,2},{1... | collective-permute-start | bytes 393224 | tf_op jit(solution)/shard_map/ppermute | solution.py:21
  35.9 5.6 %copy-start.2 = (bf16[512,512]{1,0:T(8,128)(2,1)S(1)}, bf16[512,512]{1,0:T(8,128)(2,1)}, u32[]{:S(2)}) copy-start(bf16[512,512]{1,0:T(8,128)(2,1)} %param.6) | copy-start | bytes 1572868
  39.7 5.2 %collective-permute-start.7 = (bf16[256,128]{1,0:T(8,128)(2,1)S(1)}, bf16[256,128]{1,0:T(8,128)(2,1)S(1)}, u32[]{:S(2)}, u32[]{:S(2)}) collective-permute-start(bf16[256,128]{1,0:T(8,128)(2,1)S(1)} %pad_maximum_fusion.18), channel_id=1, source_target_pairs={{0,8},{4,12},{8,0},{12,4},{1,9},{5,13},{9,1},{13,5},{2,10},{6,14},... | collective-permute-start | bytes 196616 | tf_op jit(solution)/shard_map/ppermute | solution.py:21
  42.2 3.8 %copy-start.6 = (bf16[1,128,256]{1,2,0:T(8,128)(2,1)}, bf16[1,128,256]{1,2,0:T(8,128)(2,1)S(1)}, u32[]{:S(2)}) copy-start(bf16[1,128,256]{1,2,0:T(8,128)(2,1)S(1)} %slice_bitcast_fusion.13) | copy-start | bytes 196612
  45.2 5.1 %collective-permute-start.9 = (bf16[2,128,256]{1,2,0:T(8,128)(2,1)S(1)}, bf16[2,128,256]{1,2,0:T(8,128)(2,1)}, u32[]{:S(2)}, u32[]{:S(2)}) collective-permute-start(bf16[2,128,256]{1,2,0:T(8,128)(2,1)S(1)} %pad_maximum_fusion.6), channel_id=1, source_target_pairs={{0,2},{2,0},{1,3},{3,1},{4,6},{6,4},{5,7},{7,5},{8,10},{10,8},{9,1... | collective-permute-start | bytes 393224 | tf_op jit(solution)/shard_map/ppermute | solution.py:21
  52.3 2.1 %collective-permute-start.10 = (bf16[3,128,512]{1,2,0:T(8,128)(2,1)}, bf16[3,128,512]{1,2,0:T(8,128)(2,1)}, u32[]{:S(2)}, u32[]{:S(2)}) collective-permute-start(bf16[3,128,512]{1,2,0:T(8,128)(2,1)} %pad_maximum_fusion.1), channel_id=1, source_target_pairs={{0,1},{1,0},{2,3},{3,2},{4,5},{5,4},{6,7},{7,6},{8,9},{9,8},{10,11... | collective-permute-start | bytes 1179656 | tf_op jit(solution)/shard_map/ppermute | solution.py:21
  52.3 5.2 %copy-start.4 = (bf16[4,512,128]{2,1,0:T(8,128)(2,1)S(1)}, bf16[4,512,128]{2,1,0:T(8,128)(2,1)}, u32[]{:S(2)}) copy-start(bf16[4,512,128]{2,1,0:T(8,128)(2,1)} %param.8) | copy-start | bytes 1572868
  (2 other events, 3.5 us)

commit v21 on v13

--- a/solution.py
+++ b/solution.py
@@ -148,23 +148,36 @@
             )
             rest = rest - fix.reshape(rest.shape)
 
-    full = [own_coefs[0]] + [None] * (levels - 1)
     pending = {s: own_coefs[s] for s in range(1, levels)}
     top = {s: s - 1 for s in range(1, levels)}
     if levels > 2:
         top[levels - 1] = levels - 3
-    for j in reversed(range(levels - 1)):
+    for j in reversed(range(1, levels - 1)):
         group = [s for s in range(1, levels) if top[s] >= j]
         if not group:
             continue
         joined = gather_half(jnp.stack([pending[s] for s in group]), j, bits)
         for i, s in enumerate(group):
             pending[s] = joined[i]
-    for s in range(1, levels):
-        full[s] = pending[s]
-    current = c0
-    for s in range(levels):
-        current = current - jnp.dot(u_basis[s], full[s], preferred_element_type=F32)
+    half = width // 2
+    h = side(0, bits)
+    base = c0 - jnp.dot(u_basis[0], own_coefs[0], preferred_element_type=F32)
+    mine = jnp.stack([pending[s] for s in range(1, levels)])
+    theirs = swap(mine, 0, bits)
+
+    def part(pieces, start):
+        acc = cols(base, start, half)
+        for i, s in enumerate(range(1, levels)):
+            acc = acc - jnp.dot(u_basis[s], pieces[i], preferred_element_type=F32)
+        return acc
+
+    p_mine = part(mine, h * half)
+    p_theirs = part(theirs, (1 - h) * half)
+    current = jnp.where(
+        h == 0,
+        jnp.concatenate([p_mine, p_theirs], axis=1),
+        jnp.concatenate([p_theirs, p_mine], axis=1),
+    )
     return current.astype(BF16)
 
 

time: 57.1 us -> 63.5 us (1.11)
  local copies, waits for them, and re-layouts: 4.07 us -> 10 us
  waiting for transfers between devices: 18.9 us -> 15 us
  starting transfers between devices: 12 us -> 14.4 us
  matrix products: 13.7 us -> 14.7 us
  other arithmetic: 7.28 us -> 7.99 us
    ppermute x11, waiting for transfers between devices: 18.9 us -> 15 us  [swap(): return lax.ppermute(x, axis, [(i, i ^ 1 << stride) for i in range(n)])]
    ppermute x11, starting transfers between devices: 12 us -> 14.4 us  [swap(): return lax.ppermute(x, axis, [(i, i ^ 1 << stride) for i in range(n)])]
    another operation x0 -> x2, local copies, waits for them, and re-layouts: none -> 2.31 us  [on_device(): mine = jnp.stack([pending[s] for s in range(1, levels)])]
    convert_element_type x0 -> x1, other arithmetic: none -> 1.26 us  [on_device(): return current.astype(BF16)]
    concatenate x2 -> x1, other arithmetic: 1.79 us -> 0.6 us  [gather_half(): both = jnp.concatenate([x, swap(x, bit, bits), x], axis=-1)]
    dot_general x1, matrix products: 1.83 us -> 0.71 us  [on_device(): c0 = jnp.dot(leaf_inverse, templates, preferred_element_type=F32)]
    unnamed x28 -> x52, local copies, waits for them, and re-layouts: 0.83 us -> 1.77 us
    slice x3, local copies, waits for them, and re-layouts: 0.96 us -> 1.88 us  [on_device(): recv = got[at:at + n]]
  transfers between devices with their start and end apart: 11 -> 11, of which waited for: 6 -> 5; matrix products, arithmetic and copies ran while one was open for 30% -> 35% of each run, Pallas kernels for 0% -> 0%
where the time goes in v21:
time: 63.5 us; the launch traced here: 62.8 us
  waiting for transfers between devices  15 us (24%)
  matrix products  14.7 us (23%)
  starting transfers between devices  14.4 us (23%)
  local copies, waits for them, and re-layouts  10 us (16%)
  other arithmetic  7.99 us (13%)
  between operations  0.66 us (1%)
    ppermute x11, waiting for transfers between devices, swap(): return lax.ppermute(x, axis, [(i, i ^ 1 << stride) for i in range(n)])  15 us
    ppermute x11, starting transfers between devices, swap(): return lax.ppermute(x, axis, [(i, i ^ 1 << stride) for i in range(n)])  14.4 us
    dot_general x3, matrix products, project(): jnp.einsum('lrj,jt->lrt', vl_lo[lv], x, preferred_element_type=F32)  3.78 us
    dot_general x4, matrix products, on_device(): coefs = jnp.dot(couple[s], stacked, preferred_element_type=F32).astype(BF16)  2.85 us
    another operation x2, local copies, waits for them, and re-layouts, on_device(): mine = jnp.stack([pending[s] for s in range(1, levels)])  2.31 us
    dot_general x3, matrix products, project(): jnp.einsum('lrj,jt->lrt', vl_hi[lv], x, preferred_element_type=F32)  1.91 us
    slice x3, local copies, waits for them, and re-layouts, on_device(): recv = got[at:at + n]  1.88 us
    add x3, other arithmetic, on_device(): partial[s] = partial[s] + recv  1.78 us
  transfers between devices with their start and end apart: 11, of which 5 were waited for; matrix products, arithmetic and copies ran while one was open for 35% of the time, Pallas kernels for 0%

profile of v21, /device:TPU:0, one launch (start us, length us, event | category | flops | bytes accessed | tf_op | source)
XLA Modules:
  0.0 62.8 jit_solution(14581531938441618544)
XLA Ops:
  0.0 1.8 %slice_bitcast_fusion.16 = (bf16[128,256]{1,0:T(8,128)(2,1)}, bf16[128,256]{1,0:T(8,128)(2,1)S(1)}, bf16[128,256]{1,0:T(8,128)(2,1)S(1)}, bf16[128,256]{1,0:T(8,128)(2,1)}) fusion(bf16[4,1,128,256]{3,2,1,0:T(8,128)(2,1)} %param.9), kind=kLoop, calls=%fused_computation.170 | loop fusion | bytes 524288 | tf_op jit(solution)/shard_map/squeeze | solution.py:81
  4.8 1.5 %subtract_convert_fusion = (bf16[4,128,512]{2,1,0:T(8,128)(2,1)S(1)}, bf16[4,128,512]{2,1,0:T(8,128)(2,1)S(1)}) fusion(bf16[4,512,128]{2,1,0:T(8,128)(2,1)S(1)} %copy-done.5, bf16[512,512]{1,0:T(8,128)(2,1)} %param.6), kind=kOutput, calls=%fused_computation.28 | convolution fusion | flops 269484032 | bytes 2097152 | tf_op jit(solution)/shard_map/lir,ij->lrj/dot_general | solution.py:91
  6.7 1.0 %fusion.9 = bf16[128,1024]{1,0:T(8,128)(2,1)} fusion(f32[128,1024]{1,0:T(8,128)S(1)} %fusion.50, bf16[512,1024]{1,0:T(8,128)(2,1)S(1)} %copy-done, bf16[4,128,512]{2,1,0:T(8,128)(2,1)S(1)} %get-tuple-element.5), kind=kOutput, calls=%fused_computation.21 | convolution fusion | flops 134479872 | bytes 1966080 | tf_op jit(solution)/shard_map/lrj,jt->lrt/dot_general | solution.py:98
  8.1 1.3 %convolution_add_fusion = f32[3,128,512]{2,1,0:T(8,128)} fusion(f32[3,128,512]{2,1,0:T(8,128)S(1)} %fusion.17, bf16[4,128,512]{2,1,0:T(8,128)(2,1)S(1)} %get-tuple-element.5, bf16[512,1024]{1,0:T(8,128)(2,1)S(1)} %copy-done, s32[]{:T(128)S(6)} %select_n.77), kind=kOutput, calls=%fused_computation.16 | convolution fusion | flops 201523200 | bytes 2621444 | tf_op jit(solution)/shard_map/lrj,jt->lrt/dot_general | solution.py:98
  9.9 3.7 %collective-permute-start.7 = (bf16[256,128]{1,0:T(8,128)(2,1)S(1)}, bf16[256,128]{1,0:T(8,128)(2,1)S(1)}, u32[]{:S(2)}, u32[]{:S(2)}) collective-permute-start(bf16[256,128]{1,0:T(8,128)(2,1)S(1)} %fusion.104), channel_id=1, source_target_pairs={{0,8},{4,12},{8,0},{12,4},{1,9},{5,13},{9,1},{13,5},{2,10},{6,14},... | collective-permute-start | bytes 196616 | tf_op jit(solution)/shard_map/ppermute | solution.py:21
  13.6 1.2 %fusion.20 = f32[3,128,512]{2,1,0:T(8,128)} fusion(bf16[4,128,512]{2,1,0:T(8,128)(2,1)S(1)} %get-tuple-element.6, bf16[512,1024]{1,0:T(8,128)(2,1)S(1)} %copy-done, s32[]{:T(128)S(6)} %select_n.73), kind=kOutput, calls=%fused_computation.37 | convolution fusion | flops 201326592 | bytes 1835012 | tf_op jit(solution)/shard_map/lrj,jt->lrt/dot_general | solution.py:96
  14.9 2.9 %collective-permute-done.7 = bf16[256,128]{1,0:T(8,128)(2,1)S(1)} collective-permute-done((bf16[256,128]{1,0:T(8,128)(2,1)S(1)}, bf16[256,128]{1,0:T(8,128)(2,1)S(1)}, u32[]{:S(2)}, u32[]{:S(2)}) %collective-permute-start.7) | collective-permute-done | bytes 65568 | tf_op jit(solution)/shard_map/ppermute | solution.py:21
  18.4 0.9 %slice_add_fusion = f32[256,128]{1,0:T(8,128)S(1)} fusion(f32[256,128]{1,0:T(8,128)S(1)} %fusion.86, f32[1024,128]{1,0:T(8,128)} %collective-permute-done), kind=kLoop, calls=%fused_computation.86 | loop fusion | flops 32768 | bytes 393216 | tf_op jit(solution)/shard_map/add | solution.py:77
  20.2 1.6 %collective-permute-start.2 = (f32[640,128]{1,0:T(8,128)S(1)}, f32[640,128]{1,0:T(8,128)S(1)}, u32[]{:S(2)}, u32[]{:S(2)}) collective-permute-start(f32[640,128]{1,0:T(8,128)S(1)} %pad_maximum_fusion.2), channel_id=1, source_target_pairs={{0,2},{2,0},{1,3},{3,1},{4,6},{6,4},{5,7},{7,5},{8,10},{10,8},{9,1... | collective-permute-start | bytes 983048 | tf_op jit(solution)/shard_map/ppermute | solution.py:21
  21.9 1.1 %convert.16 = bf16[1024,128]{1,0:T(8,128)(2,1)S(1)} convert(f32[1024,128]{1,0:T(8,128)} %collective-permute-done) | non-fusion elementwise | flops 131072 | bytes 786432 | tf_op jit(solution)/shard_map/convert.5
  22.9 0.9 %slice.320 = f32[384,128]{1,0:T(8,128)S(1)} slice(f32[1024,128]{1,0:T(8,128)} %collective-permute-done), slice={[256:640], [0:128]} | slice | bytes 393216 | tf_op jit(solution)/shard_map/slice | solution.py:72
  24.0 1.3 %convolution_convert_fusion = bf16[256,1024]{1,0:T(8,128)(2,1)S(1)} fusion(bf16[128,1024]{1,0:T(8,128)(2,1)} %collective-permute-done.1, bf16[128,1024]{1,0:T(8,128)(2,1)} %fusion.9, bf16[256,128]{1,0:T(8,128)(2,1)S(1)} %get-tuple-element.30, bf16[256,128]{1,0:T(8,128)(2,1)S(1)} %get-tuple-element.29), kind=kOutput, calls=%fused_computation.15 | convolution fusion | flops 135790592 | bytes 1179648 | tf_op jit(solution)/shard_map/dot_general | solution.py:137
  27.6 1.5 %fusion.8 = f32[3,128,512]{2,1,0:T(8,128)S(1)} fusion(f32[3,128,512]{2,1,0:T(8,128)S(1)} %bitcast.146, f32[3,128,512]{2,1,0:T(8,128)} %collective-permute-done.3, f32[3,128,512]{2,1,0:T(8,128)S(1)} %copy-done.6, bf16[4,128,512]{2,1,0:T(8,128)(2,1)S(1)} %copy-done.2, bf16[512,1024]{1,0:T(8,128)(2,1)S(1)} %copy-done, s32[]{:T(128)S(6)} %select_n.73), kind=kOutput, calls=%fused_computation.19 | convolution fusion | flops 201916416 | bytes 4194308 | tf_op jit(solution)/shard_map/lrj,jt->lrt/dot_general | solution.py:98
  30.9 5.1 %collective-permute-done.4 = bf16[512,256]{1,0:T(8,128)(2,1)S(1)} collective-permute-done((bf16[512,256]{1,0:T(8,128)(2,1)S(1)}, bf16[512,256]{1,0:T(8,128)(2,1)S(1)}, u32[]{:S(2)}, u32[]{:S(2)}) %collective-permute-start.4) | collective-permute-done | bytes 262176 | tf_op jit(solution)/shard_map/ppermute | solution.py:21
  37.3 2.1 %collective-permute-start.6 = (bf16[512,128]{1,0:T(8,128)(2,1)}, bf16[512,128]{1,0:T(8,128)(2,1)}, u32[]{:S(2)}, u32[]{:S(2)}) collective-permute-start(bf16[512,128]{1,0:T(8,128)(2,1)} %pad_maximum_fusion.5), channel_id=1, source_target_pairs={{0,4},{4,0},{8,12},{12,8},{1,5},{5,1},{9,13},{13,9},{2,6},{6,2},{1... | collective-permute-start | bytes 393224 | tf_op jit(solution)/shard_map/ppermute | solution.py:21
  41.4 1.7 %copy.22 = bf16[1,128,512]{1,2,0:T(8,128)(2,1)} copy(bf16[1,128,512]{2,1,0:T(8,128)(2,1)} %slice_bitcast_fusion.14) | data formatting | bytes 262144 | tf_op jit(solution)/shard_map/stack | solution.py:165
  43.1 0.9 %slice.350 = f32[128,128]{1,0:T(8,128)S(1)} slice(f32[384,128]{1,0:T(8,128)} %copy-done.11), slice={[256:384], [0:128]} | slice | bytes 131072 | tf_op jit(solution)/shard_map/slice | solution.py:72
  45.6 1.1 %convolution_convert_fusion.2 = bf16[256,256]{0,1:T(8,128)(2,1)S(1)} fusion(bf16[256,128]{1,0:T(8,128)(2,1)S(1)} %get-tuple-element.32, bf16[256,128]{1,0:T(8,128)(2,1)S(1)} %get-tuple-element.31, bf16[128,128]{1,0:T(8,128)(2,1)S(1)} %get-tuple-element.21, bf16[128,128]{1,0:T(8,128)(2,1)S(1)} %get-tuple-element.22, bf16[128,256]{1,0:T(8,128)(2,1)} %copy-done.20), kind=kOutput, calls=%fused_computation.23 | convolution fusion | flops 34275328 | bytes 393216 | tf_op jit(solution)/shard_map/dot_general | solution.py:137
  47.1 3.4 %collective-permute-start.8 = (bf16[256,128]{1,0:T(8,128)(2,1)S(1)}, bf16[256,128]{1,0:T(8,128)(2,1)S(1)}, u32[]{:S(2)}, u32[]{:S(2)}) collective-permute-start(bf16[256,128]{1,0:T(8,128)(2,1)S(1)} %pad_maximum_fusion.19), channel_id=1, source_target_pairs={{0,8},{4,12},{8,0},{12,4},{1,9},{5,13},{9,1},{13,5},{2,10},{6,14},... | collective-permute-start | bytes 196616 | tf_op jit(solution)/shard_map/ppermute | solution.py:21
  50.5 2.4 %collective-permute-done.8 = bf16[256,128]{1,0:T(8,128)(2,1)S(1)} collective-permute-done((bf16[256,128]{1,0:T(8,128)(2,1)S(1)}, bf16[256,128]{1,0:T(8,128)(2,1)S(1)}, u32[]{:S(2)}, u32[]{:S(2)}) %collective-permute-start.8) | collective-permute-done | bytes 65568 | tf_op jit(solution)/shard_map/ppermute | solution.py:21
  53.2 1.2 %collective-permute-start.9 = (bf16[2,128,256]{1,2,0:T(8,128)(2,1)S(1)}, bf16[2,128,256]{1,2,0:T(8,128)(2,1)S(1)}, u32[]{:S(2)}, u32[]{:S(2)}) collective-permute-start(bf16[2,128,256]{1,2,0:T(8,128)(2,1)S(1)} %pad_maximum_fusion.6), channel_id=1, source_target_pairs={{0,2},{2,0},{1,3},{3,1},{4,6},{6,4},{5,7},{7,5},{8,10},{10,8},{9,1... | collective-permute-start | bytes 393224 | tf_op jit(solution)/shard_map/ppermute | solution.py:21
  54.6 3.6 %collective-permute-done.9 = bf16[2,128,256]{1,2,0:T(8,128)(2,1)S(1)} collective-permute-done((bf16[2,128,256]{1,2,0:T(8,128)(2,1)S(1)}, bf16[2,128,256]{1,2,0:T(8,128)(2,1)S(1)}, u32[]{:S(2)}, u32[]{:S(2)}) %collective-permute-start.9) | collective-permute-done | bytes 131104 | tf_op jit(solution)/shard_map/ppermute | solution.py:21
  59.5 1.1 %collective-permute-done.10 = bf16[3,128,512]{1,2,0:T(8,128)(2,1)S(1)} collective-permute-done((bf16[3,128,512]{1,2,0:T(8,128)(2,1)S(1)}, bf16[3,128,512]{1,2,0:T(8,128)(2,1)S(1)}, u32[]{:S(2)}, u32[]{:S(2)}) %collective-permute-start.10) | collective-permute-done | bytes 393248 | tf_op jit(solution)/shard_map/ppermute | solution.py:21
  61.6 1.3 %fusion = bf16[512,1024]{1,0:T(8,128)(2,1)} fusion(bf16[512,512]{1,0:T(8,128)(2,1)S(1)} %fusion.6, bf16[512,512]{1,0:T(8,128)(2,1)S(1)} %fusion.4, pred[]{:T(512)S(6)} %eq.13), kind=kLoop, calls=%fused_computation.1 | loop fusion | flops 4718592 | bytes 2097153 | tf_op jit(solution)/shard_map/convert_element_type | solution.py:181
  (130 shorter events, 17.8 us)
Async XLA Ops:
  0.0 6.4 %copy-start = (bf16[512,1024]{1,0:T(8,128)(2,1)S(1)}, bf16[512,1024]{1,0:T(8,128)(2,1)}, u32[]{:S(2)}) copy-start(bf16[512,1024]{1,0:T(8,128)(2,1)} %param.5) | copy-start | bytes 3145732
  0.0 2.5 %slice-start.1 = ((bf16[4,512,128]{2,1,0:T(8,128)(2,1)}), bf16[2,512,128]{2,1,0:T(8,128)(2,1)S(1)}, s32[]{:S(2)}) async-start(bf16[4,512,128]{2,1,0:T(8,128)(2,1)} %param.7), calls=%async_computation.1 | async-start | bytes 524288 | tf_op jit(solution)/shard_map/slice | solution.py:57
  4.4 14.1 %collective-permute-start = (f32[1024,128]{1,0:T(8,128)}, f32[1024,128]{1,0:T(8,128)}, u32[]{:S(2)}, u32[]{:S(2)}) collective-permute-start(f32[1024,128]{1,0:T(8,128)} %pad_maximum_fusion), channel_id=1, source_target_pairs={{0,1},{1,0},{2,3},{3,2},{4,5},{5,4},{6,7},{7,6},{8,9},{9,8},{10,11... | collective-permute-start | bytes 1572872 | tf_op jit(solution)/shard_map/ppermute | solution.py:21
  7.7 16.3 %collective-permute-start.1 = (bf16[128,1024]{1,0:T(8,128)(2,1)}, bf16[128,1024]{1,0:T(8,128)(2,1)}, u32[]{:S(2)}, u32[]{:S(2)}) collective-permute-start(bf16[128,1024]{1,0:T(8,128)(2,1)} %fusion.9), channel_id=1, source_target_pairs={{0,1},{1,0},{2,3},{3,2},{4,5},{5,4},{6,7},{7,6},{8,9},{9,8},{10,11... | collective-permute-start | bytes 786440 | tf_op jit(solution)/shard_map/ppermute | solution.py:21
  8.1 6.7 %copy-start.12 = (bf16[128,128]{1,0:T(8,128)(2,1)S(1)}, bf16[128,128]{1,0:T(8,128)(2,1)}, u32[]{:S(2)}) copy-start(bf16[128,128]{1,0:T(8,128)(2,1)} %get-tuple-element.49) | copy-start | bytes 98308
  8.1 6.7 %copy-start.14 = (bf16[128,128]{1,0:T(8,128)(2,1)S(1)}, bf16[128,128]{1,0:T(8,128)(2,1)}, u32[]{:S(2)}) copy-start(bf16[128,128]{1,0:T(8,128)(2,1)} %get-tuple-element.50) | copy-start | bytes 98308
  9.4 17.6 %collective-permute-start.3 = (f32[3,128,512]{2,1,0:T(8,128)}, f32[3,128,512]{2,1,0:T(8,128)}, u32[]{:S(2)}, u32[]{:S(2)}) collective-permute-start(f32[3,128,512]{2,1,0:T(8,128)} %convolution_add_fusion), channel_id=1, source_target_pairs={{0,1},{1,0},{2,3},{3,2},{4,5},{5,4},{6,7},{7,6},{8,9},{9,8},{10,11... | collective-permute-start | bytes 2359304 | tf_op jit(solution)/shard_map/ppermute | solution.py:21
  9.9 7.8 %collective-permute-start.7 = (bf16[256,128]{1,0:T(8,128)(2,1)S(1)}, bf16[256,128]{1,0:T(8,128)(2,1)S(1)}, u32[]{:S(2)}, u32[]{:S(2)}) collective-permute-start(bf16[256,128]{1,0:T(8,128)(2,1)S(1)} %fusion.104), channel_id=1, source_target_pairs={{0,8},{4,12},{8,0},{12,4},{1,9},{5,13},{9,1},{13,5},{2,10},{6,14},... | collective-permute-start | bytes 196616 | tf_op jit(solution)/shard_map/ppermute | solution.py:21
  14.8 9.1 %copy-start.17 = (bf16[128,128]{1,0:T(8,128)(2,1)S(1)}, bf16[128,128]{1,0:T(8,128)(2,1)}, u32[]{:S(2)}) copy-start(bf16[128,128]{1,0:T(8,128)(2,1)} %copy-done.16) | copy-start | bytes 98308
  14.8 9.1 %copy-start.19 = (bf16[128,128]{1,0:T(8,128)(2,1)S(1)}, bf16[128,128]{1,0:T(8,128)(2,1)}, u32[]{:S(2)}) copy-start(bf16[128,128]{1,0:T(8,128)(2,1)} %copy-done.18) | copy-start | bytes 98308
  20.2 9.6 %collective-permute-start.2 = (f32[640,128]{1,0:T(8,128)S(1)}, f32[640,128]{1,0:T(8,128)S(1)}, u32[]{:S(2)}, u32[]{:S(2)}) collective-permute-start(f32[640,128]{1,0:T(8,128)S(1)} %pad_maximum_fusion.2), channel_id=1, source_target_pairs={{0,2},{2,0},{1,3},{3,1},{4,6},{6,4},{5,7},{7,5},{8,10},{10,8},{9,1... | collective-permute-start | bytes 983048 | tf_op jit(solution)/shard_map/ppermute | solution.py:21
  29.3 6.7 %collective-permute-start.4 = (bf16[512,256]{1,0:T(8,128)(2,1)S(1)}, bf16[512,256]{1,0:T(8,128)(2,1)S(1)}, u32[]{:S(2)}, u32[]{:S(2)}) collective-permute-start(bf16[512,256]{1,0:T(8,128)(2,1)S(1)} %pad_maximum_fusion.3), channel_id=1, source_target_pairs={{0,2},{2,0},{1,3},{3,1},{4,6},{6,4},{5,7},{7,5},{8,10},{10,8},{9,1... | collective-permute-start | bytes 786440 | tf_op jit(solution)/shard_map/ppermute | solution.py:21
  29.9 10.2 %collective-permute-start.5 = (f32[384,128]{1,0:T(8,128)S(1)}, f32[384,128]{1,0:T(8,128)S(1)}, u32[]{:S(2)}, u32[]{:S(2)}) collective-permute-start(f32[384,128]{1,0:T(8,128)S(1)} %pad_maximum_fusion.4), channel_id=1, source_target_pairs={{0,4},{4,0},{8,12},{12,8},{1,5},{5,1},{9,13},{13,9},{2,6},{6,2},{1... | collective-permute-start | bytes 589832 | tf_op jit(solution)/shard_map/ppermute | solution.py:21
  36.2 3.2 %copy-start.8 = (bf16[256,512]{1,0:T(8,128)(2,1)}, bf16[256,512]{1,0:T(8,128)(2,1)S(1)}, u32[]{:S(2)}) copy-start(bf16[256,512]{1,0:T(8,128)(2,1)S(1)} %convolution_convert_fusion.1) | copy-start | bytes 786436
  36.6 4.1 %copy-start.20 = (bf16[128,256]{1,0:T(8,128)(2,1)}, bf16[128,256]{1,0:T(8,128)(2,1)S(1)}, u32[]{:S(2)}) copy-start(bf16[128,256]{1,0:T(8,128)(2,1)S(1)} %get-tuple-element.11) | copy-start | bytes 196612
  37.3 7.5 %collective-permute-start.6 = (bf16[512,128]{1,0:T(8,128)(2,1)}, bf16[512,128]{1,0:T(8,128)(2,1)}, u32[]{:S(2)}, u32[]{:S(2)}) collective-permute-start(bf16[512,128]{1,0:T(8,128)(2,1)} %pad_maximum_fusion.5), channel_id=1, source_target_pairs={{0,4},{4,0},{8,12},{12,8},{1,5},{5,1},{9,13},{13,9},{2,6},{6,2},{1... | collective-permute-start | bytes 393224 | tf_op jit(solution)/shard_map/ppermute | solution.py:21
  43.1 9.8 %copy-start.23 = (bf16[256,128]{1,0:T(8,128)(2,1)S(1)}, bf16[256,128]{1,0:T(8,128)(2,1)}, u32[]{:S(2)}) copy-start(bf16[256,128]{1,0:T(8,128)(2,1)} %get-tuple-element.23) | copy-start | bytes 196612
  43.1 9.8 %copy-start.24 = (bf16[256,128]{1,0:T(8,128)(2,1)S(1)}, bf16[256,128]{1,0:T(8,128)(2,1)}, u32[]{:S(2)}) copy-start(bf16[256,128]{1,0:T(8,128)(2,1)} %get-tuple-element.24) | copy-start | bytes 196612
  43.1 11.3 %copy-start.4 = (bf16[4,512,128]{2,1,0:T(8,128)(2,1)S(1)}, bf16[4,512,128]{2,1,0:T(8,128)(2,1)}, u32[]{:S(2)}) copy-start(bf16[4,512,128]{2,1,0:T(8,128)(2,1)} %param.8) | copy-start | bytes 1572868
  43.1 11.3 %copy-start.9 = (bf16[256,512]{1,0:T(8,128)(2,1)S(1)}, bf16[256,512]{1,0:T(8,128)(2,1)}, u32[]{:S(2)}) copy-start(bf16[256,512]{1,0:T(8,128)(2,1)} %copy-done.8) | copy-start | bytes 786436
  47.0 11.8 %copy-start.10 = (bf16[1,128,512]{1,2,0:T(8,128)(2,1)S(1)}, bf16[1,128,512]{1,2,0:T(8,128)(2,1)}, u32[]{:S(2)}) copy-start(bf16[1,128,512]{1,2,0:T(8,128)(2,1)} %copy.22) | copy-start | bytes 393220
  47.1 5.8 %collective-permute-start.8 = (bf16[256,128]{1,0:T(8,128)(2,1)S(1)}, bf16[256,128]{1,0:T(8,128)(2,1)S(1)}, u32[]{:S(2)}, u32[]{:S(2)}) collective-permute-start(bf16[256,128]{1,0:T(8,128)(2,1)S(1)} %pad_maximum_fusion.19), channel_id=1, source_target_pairs={{0,8},{4,12},{8,0},{12,4},{1,9},{5,13},{9,1},{13,5},{2,10},{6,14},... | collective-permute-start | bytes 196616 | tf_op jit(solution)/shard_map/ppermute | solution.py:21
  53.2 5.0 %collective-permute-start.9 = (bf16[2,128,256]{1,2,0:T(8,128)(2,1)S(1)}, bf16[2,128,256]{1,2,0:T(8,128)(2,1)S(1)}, u32[]{:S(2)}, u32[]{:S(2)}) collective-permute-start(bf16[2,128,256]{1,2,0:T(8,128)(2,1)S(1)} %pad_maximum_fusion.6), channel_id=1, source_target_pairs={{0,2},{2,0},{1,3},{3,1},{4,6},{6,4},{5,7},{7,5},{8,10},{10,8},{9,1... | collective-permute-start | bytes 393224 | tf_op jit(solution)/shard_map/ppermute | solution.py:21
  58.9 1.8 %collective-permute-start.10 = (bf16[3,128,512]{1,2,0:T(8,128)(2,1)S(1)}, bf16[3,128,512]{1,2,0:T(8,128)(2,1)S(1)}, u32[]{:S(2)}, u32[]{:S(2)}) collective-permute-start(bf16[3,128,512]{1,2,0:T(8,128)(2,1)S(1)} %pad_maximum_fusion.1), channel_id=1, source_target_pairs={{0,1},{1,0},{2,3},{3,2},{4,5},{5,4},{6,7},{7,6},{8,9},{9,8},{10,11... | collective-permute-start | bytes 1179656 | tf_op jit(solution)/shard_map/ppermute | solution.py:21
  (14 other events, 21.0 us)

commit v22 on v13

--- a/solution.py
+++ b/solution.py
@@ -116,10 +116,11 @@
             n = rest.shape[0]
             w = mine_b.shape[1] // 2
             parts = [mine_b[:, :w], mine_b[:, w:]]
-            summed = n == 1 and s == levels - 2
+            summed = n > 0
             if summed:
-                last = rest[0].astype(BF16)
-                parts += [last[:, :w], last[:, w:]]
+                later = rest.astype(BF16)
+                parts += [later[:, :, :w].reshape(n * rank, w),
+                          later[:, :, w:].reshape(n * rank, w)]
             elif n > 0:
                 h = side(s, bits)
                 keep = cols(rest, h * w, w)
@@ -128,8 +129,9 @@
             got = swap(jnp.concatenate(parts, axis=0), s, bits)
             theirs_b = jnp.concatenate([got[:rank], got[rank : 2 * rank]], axis=1)
             if summed:
-                recv = jnp.concatenate([got[2 * rank : 3 * rank], got[3 * rank :]], axis=1)
-                rest = rest + recv.astype(F32)[None]
+                lo = got[2 * rank : (2 + n) * rank].reshape(n, rank, w)
+                hi = got[(2 + n) * rank :].reshape(n, rank, w)
+                rest = rest + jnp.concatenate([lo, hi], axis=2).astype(F32)
             elif n > 0:
                 recv = got[2 * rank :].reshape(n, rank, w).astype(F32)
                 rest = keep + recv
@@ -150,9 +152,7 @@
 
     full = [own_coefs[0]] + [None] * (levels - 1)
     pending = {s: own_coefs[s] for s in range(1, levels)}
-    top = {s: s - 1 for s in range(1, levels)}
-    if levels > 2:
-        top[levels - 1] = levels - 3
+    top = {s: 0 for s in range(1, levels)}
     for j in reversed(range(levels - 1)):
         group = [s for s in range(1, levels) if top[s] >= j]
         if not group:

time: 57.1 us -> 57.5 us (level)
  waiting for transfers between devices: 18.9 us -> 21.5 us
  other arithmetic: 7.28 us -> 5.23 us
  starting transfers between devices: 12 us -> 10.5 us
  local copies, waits for them, and re-layouts: 4.07 us -> 5.4 us
    ppermute x11 -> x10, waiting for transfers between devices: 18.9 us -> 21.5 us  [swap(): return lax.ppermute(x, axis, [(i, i ^ 1 << stride) for i in range(n)])]
    ppermute x11 -> x10, starting transfers between devices: 12 us -> 10.5 us  [swap(): return lax.ppermute(x, axis, [(i, i ^ 1 << stride) for i in range(n)])]
    concatenate x2 -> x1, other arithmetic: 1.79 us -> 0.43 us  [gather_half(): both = jnp.concatenate([x, swap(x, bit, bits), x], axis=-1)]
    slice x2, local copies, waits for them, and re-layouts: 0.05 us -> 1.32 us  [on_device(): parts = [jnp.concatenate([c[:, :rank], c[:, rank:]], axis=0).astype(F32)]]
    dot_general x1, matrix products: 1.5 us -> 0.47 us  [on_device(): jnp.einsum('lir,ij->lrj', v_basis, leaf_inverse, preferred_element_type=F32)]
    dot_general x4, matrix products: 1.73 us -> 2.63 us  [on_device(): current = current - jnp.dot(u_basis[s], full[s], preferred_element_type=F32)]
    select_n x4, other arithmetic: 0.9 us -> 0.12 us  [on_device(): jnp.where(lower, first, second)]
  transfers between devices with their start and end apart: 11 -> 10, of which waited for: 6 -> 6; matrix products, arithmetic and copies ran while one was open for 30% -> 28% of each run, Pallas kernels for 0% -> 0%
where the time goes in v22:
time: 57.5 us; the launch traced here: 57 us
  waiting for transfers between devices  21.5 us (37%)
  matrix products  13.6 us (24%)
  starting transfers between devices  10.5 us (18%)
  local copies, waits for them, and re-layouts  5.4 us (9%)
  other arithmetic  5.23 us (9%)
  between operations  0.69 us (1%)
    ppermute x10, waiting for transfers between devices, swap(): return lax.ppermute(x, axis, [(i, i ^ 1 << stride) for i in range(n)])  21.5 us
    ppermute x10, starting transfers between devices, swap(): return lax.ppermute(x, axis, [(i, i ^ 1 << stride) for i in range(n)])  10.5 us
    dot_general x3, matrix products, project(): jnp.einsum('lrj,jt->lrt', vl_lo[lv], x, preferred_element_type=F32)  3.79 us
    dot_general x4, matrix products, on_device(): current = current - jnp.dot(u_basis[s], full[s], preferred_element_type=F32)  2.63 us
    dot_general x4, matrix products, on_device(): coefs = jnp.dot(couple[s], stacked, preferred_element_type=F32).astype(BF16)  2 us
    dot_general x1, matrix products, on_device(): c0 = jnp.dot(leaf_inverse, templates, preferred_element_type=F32)  1.84 us
    add x3, other arithmetic, on_device(): partial[s] = partial[s] + recv  1.78 us
    slice x2, local copies, waits for them, and re-layouts, on_device(): parts = [jnp.concatenate([c[:, :rank], c[:, rank:]], axis=0).astype(F32)]  1.32 us
  transfers between devices with their start and end apart: 10, of which 6 were waited for; matrix products, arithmetic and copies ran while one was open for 28% of the time, Pallas kernels for 0%

profile of v22, /device:TPU:0, one launch (start us, length us, event | category | flops | bytes accessed | tf_op | source)
XLA Modules:
  0.0 57.0 jit_solution(8486824926600432880)
XLA Ops:
  0.0 1.1 %slice_bitcast_fusion.16 = (bf16[128,256]{1,0:T(8,128)(2,1)S(1)}, bf16[128,256]{1,0:T(8,128)(2,1)S(1)}, bf16[128,256]{1,0:T(8,128)(2,1)S(1)}, bf16[128,256]{1,0:T(8,128)(2,1)S(1)}) fusion(bf16[4,1,128,256]{3,2,1,0:T(8,128)(2,1)} %param.9), kind=kLoop, calls=%fused_computation.158 | loop fusion | bytes 524288 | tf_op jit(solution)/shard_map/squeeze | solution.py:81
  1.1 0.7 %fusion.123 = (bf16[128,128]{1,0:T(8,128)(2,1)S(1)}, bf16[128,128]{1,0:T(8,128)(2,1)S(1)}, bf16[128,128]{1,0:T(8,128)(2,1)}, bf16[128,128]{1,0:T(8,128)(2,1)}) fusion(bf16[128,256]{1,0:T(8,128)(2,1)S(1)} %get-tuple-element.13, bf16[128,256]{1,0:T(8,128)(2,1)S(1)} %get-tuple-element.16), kind=kLoop, calls=%fused_computation.193 | loop fusion | bytes 262144 | tf_op jit(solution)/shard_map/slice | solution.py:64
  2.4 4.0 %collective-permute-start.7 = (bf16[256,128]{1,0:T(8,128)(2,1)}, bf16[256,128]{1,0:T(8,128)(2,1)}, u32[]{:S(2)}, u32[]{:S(2)}) collective-permute-start(bf16[256,128]{1,0:T(8,128)(2,1)} %fusion.96), channel_id=1, source_target_pairs={{0,8},{4,12},{8,0},{12,4},{1,9},{5,13},{9,1},{13,5},{2,10},{6,14},... | collective-permute-start | bytes 196616 | tf_op jit(solution)/shard_map/ppermute | solution.py:21
  7.6 0.7 %fusion.125 = (bf16[128,128]{1,0:T(8,128)(2,1)}, bf16[128,128]{1,0:T(8,128)(2,1)}, bf16[128,128]{1,0:T(8,128)(2,1)S(1)}, bf16[128,128]{1,0:T(8,128)(2,1)S(1)}) fusion(bf16[128,256]{1,0:T(8,128)(2,1)S(1)} %get-tuple-element.14, bf16[128,256]{1,0:T(8,128)(2,1)S(1)} %get-tuple-element.15), kind=kLoop, calls=%fused_computation.195 | loop fusion | bytes 262144 | tf_op jit(solution)/shard_map/slice | solution.py:64
  8.3 0.8 %pad_maximum_fusion = f32[1024,128]{1,0:T(8,128)} fusion(f32[128,128]{1,0:T(8,128)S(1)} %fusion.79, f32[256,128]{1,0:T(8,128)S(1)} %fusion.83, f32[384,128]{1,0:T(8,128)S(1)} %fusion.86, f32[256,128]{1,0:T(8,128)S(1)} %fusion.99), kind=kLoop, calls=%fused_computation.32 | loop fusion | flops 393216 | bytes 1048576 | tf_op jit(solution)/shard_map/concatenate | solution.py:66
  9.9 1.0 %fusion.3 = bf16[128,1024]{1,0:T(8,128)(2,1)} fusion(f32[128,1024]{1,0:T(8,128)S(1)} %fusion.61, bf16[512,1024]{1,0:T(8,128)(2,1)S(1)} %copy-done, bf16[4,128,512]{2,1,0:T(8,128)(2,1)S(1)} %get-tuple-element.5), kind=kOutput, calls=%fused_computation.11 | convolution fusion | flops 134479872 | bytes 1966080 | tf_op jit(solution)/shard_map/lrj,jt->lrt/dot_general | solution.py:98
  11.8 1.3 %convolution_add_fusion = f32[3,128,512]{2,1,0:T(8,128)} fusion(f32[3,128,512]{2,1,0:T(8,128)S(1)} %fusion.17, bf16[4,128,512]{2,1,0:T(8,128)(2,1)S(1)} %get-tuple-element.5, bf16[512,1024]{1,0:T(8,128)(2,1)S(1)} %copy-done, s32[]{:T(128)S(6)} %select_n.59), kind=kOutput, calls=%fused_computation.6 | convolution fusion | flops 201523200 | bytes 2621444 | tf_op jit(solution)/shard_map/lrj,jt->lrt/dot_general | solution.py:98
  13.9 0.8 %fusion.122 = (bf16[128,128]{1,0:T(8,128)(2,1)S(1)}, bf16[128,128]{1,0:T(8,128)(2,1)S(1)}) fusion(bf16[256,128]{1,0:T(8,128)(2,1)} %collective-permute-done.7), kind=kLoop, calls=%fused_computation.192 | loop fusion | bytes 131072 | tf_op jit(solution)/shard_map/slice | solution.py:68
  14.8 0.9 %slice_add_fusion = f32[256,128]{1,0:T(8,128)S(1)} fusion(f32[256,128]{1,0:T(8,128)S(1)} %fusion.83, f32[1024,128]{1,0:T(8,128)} %collective-permute-done), kind=kLoop, calls=%fused_computation.97 | loop fusion | flops 32768 | bytes 393216 | tf_op jit(solution)/shard_map/add | solution.py:77
  15.7 0.8 %slice_add_fusion.2 = f32[128,128]{1,0:T(8,128)S(1)} fusion(f32[128,128]{1,0:T(8,128)S(1)} %fusion.79, f32[1024,128]{1,0:T(8,128)} %collective-permute-done), kind=kLoop, calls=%fused_computation.153 | loop fusion | flops 16384 | bytes 196608 | tf_op jit(solution)/shard_map/add | solution.py:77
  16.6 1.6 %collective-permute-start.2 = (f32[640,128]{1,0:T(8,128)S(1)}, f32[640,128]{1,0:T(8,128)S(1)}, u32[]{:S(2)}, u32[]{:S(2)}) collective-permute-start(f32[640,128]{1,0:T(8,128)S(1)} %pad_maximum_fusion.3), channel_id=1, source_target_pairs={{0,2},{2,0},{1,3},{3,1},{4,6},{6,4},{5,7},{7,5},{8,10},{10,8},{9,1... | collective-permute-start | bytes 983048 | tf_op jit(solution)/shard_map/ppermute | solution.py:21
  18.2 0.9 %slice.320 = f32[384,128]{1,0:T(8,128)S(1)} slice(f32[1024,128]{1,0:T(8,128)} %collective-permute-done), slice={[256:640], [0:128]} | slice | bytes 393216 | tf_op jit(solution)/shard_map/slice | solution.py:72
  19.1 1.1 %convert.15 = bf16[1024,128]{1,0:T(8,128)(2,1)S(1)} convert(f32[1024,128]{1,0:T(8,128)} %collective-permute-done) | non-fusion elementwise | flops 131072 | bytes 786432 | tf_op jit(solution)/shard_map/convert.4
  20.3 1.3 %convolution_convert_fusion = bf16[256,1024]{1,0:T(8,128)(2,1)S(1)} fusion(bf16[128,1024]{1,0:T(8,128)(2,1)} %collective-permute-done.1, bf16[128,1024]{1,0:T(8,128)(2,1)} %fusion.3, bf16[256,128]{1,0:T(8,128)(2,1)S(1)} %get-tuple-element.44, bf16[256,128]{1,0:T(8,128)(2,1)S(1)} %get-tuple-element.43), kind=kOutput, calls=%fused_computation.5 | convolution fusion | flops 135790592 | bytes 1179648 | tf_op jit(solution)/shard_map/dot_general | solution.py:139
  22.4 1.5 %fusion.2 = f32[3,128,512]{2,1,0:T(8,128)S(1)} fusion(f32[3,128,512]{2,1,0:T(8,128)S(1)} %bitcast.128, f32[3,128,512]{2,1,0:T(8,128)} %collective-permute-done.3, f32[3,128,512]{2,1,0:T(8,128)S(1)} %fusion.20, bf16[4,128,512]{2,1,0:T(8,128)(2,1)S(1)} %get-tuple-element.5, bf16[512,1024]{1,0:T(8,128)(2,1)S(1)} %copy-done, s32[]{:T(128)S(6)} %select_n.58), kind=kOutput, calls=%fused_computation.9 | convolution fusion | flops 201916416 | bytes 4194308 | tf_op jit(solution)/shard_map/lrj,jt->lrt/dot_general | solution.py:98
  24.7 1.8 %collective-permute-done.2 = f32[640,128]{1,0:T(8,128)S(1)} collective-permute-done((f32[640,128]{1,0:T(8,128)S(1)}, f32[640,128]{1,0:T(8,128)S(1)}, u32[]{:S(2)}, u32[]{:S(2)}) %collective-permute-start.2) | collective-permute-done | bytes 327712 | tf_op jit(solution)/shard_map/ppermute | solution.py:21
  26.5 1.6 %collective-permute-start.5 = (f32[384,128]{1,0:T(8,128)S(1)}, f32[384,128]{1,0:T(8,128)S(1)}, u32[]{:S(2)}, u32[]{:S(2)}) collective-permute-start(f32[384,128]{1,0:T(8,128)S(1)} %pad_maximum_fusion.5), channel_id=1, source_target_pairs={{0,4},{4,0},{8,12},{12,8},{1,5},{5,1},{9,13},{13,9},{2,6},{6,2},{1... | collective-permute-start | bytes 589832 | tf_op jit(solution)/shard_map/ppermute | solution.py:21
  28.3 4.5 %collective-permute-done.5 = f32[384,128]{1,0:T(8,128)S(1)} collective-permute-done((f32[384,128]{1,0:T(8,128)S(1)}, f32[384,128]{1,0:T(8,128)S(1)}, u32[]{:S(2)}, u32[]{:S(2)}) %collective-permute-start.5) | collective-permute-done | bytes 196640 | tf_op jit(solution)/shard_map/ppermute | solution.py:21
  32.9 2.3 %collective-permute-done.4 = bf16[768,256]{1,0:T(8,128)(2,1)S(1)} collective-permute-done((bf16[768,256]{1,0:T(8,128)(2,1)S(1)}, bf16[768,256]{1,0:T(8,128)(2,1)S(1)}, u32[]{:S(2)}, u32[]{:S(2)}) %collective-permute-start.4) | collective-permute-done | bytes 393248 | tf_op jit(solution)/shard_map/ppermute | solution.py:21
  36.0 1.6 %collective-permute-start.6 = (bf16[512,256]{1,0:T(8,128)(2,1)S(1)}, bf16[512,256]{1,0:T(8,128)(2,1)S(1)}, u32[]{:S(2)}, u32[]{:S(2)}) collective-permute-start(bf16[512,256]{1,0:T(8,128)(2,1)S(1)} %pad_maximum_fusion.4), channel_id=1, source_target_pairs={{0,4},{4,0},{8,12},{12,8},{1,5},{5,1},{9,13},{13,9},{2,6},{6,2},{1... | collective-permute-start | bytes 786440 | tf_op jit(solution)/shard_map/ppermute | solution.py:21
  37.8 5.6 %collective-permute-done.6 = bf16[512,256]{1,0:T(8,128)(2,1)S(1)} collective-permute-done((bf16[512,256]{1,0:T(8,128)(2,1)S(1)}, bf16[512,256]{1,0:T(8,128)(2,1)S(1)}, u32[]{:S(2)}, u32[]{:S(2)}) %collective-permute-start.6) | collective-permute-done | bytes 262176 | tf_op jit(solution)/shard_map/ppermute | solution.py:21
  44.4 6.9 %collective-permute-done.8 = bf16[256,256]{1,0:T(8,128)(2,1)S(1)} collective-permute-done((bf16[256,256]{1,0:T(8,128)(2,1)S(1)}, bf16[256,256]{1,0:T(8,128)(2,1)S(1)}, u32[]{:S(2)}, u32[]{:S(2)}) %collective-permute-start.8) | collective-permute-done | bytes 131104 | tf_op jit(solution)/shard_map/ppermute | solution.py:21
  51.8 1.4 %fusion.35 = f32[1024,512]{0,1:T(8,128)S(1)} fusion(bf16[256,1024]{1,0:T(8,128)(2,1)} %copy-done.5, bf16[4,512,128]{2,1,0:T(8,128)(2,1)S(1)} %copy-done.4), kind=kOutput, calls=%fused_computation.66 | convolution fusion | flops 134217728 | bytes 2490368 | tf_op jit(solution)/shard_map/dot_general | solution.py:167
  55.2 1.8 %fusion = bf16[512,1024]{1,0:T(8,128)(2,1)} fusion(f32[1024,512]{0,1:T(8,128)S(1)} %fusion.32, f32[1024,512]{0,1:T(8,128)S(1)} %fusion.33, f32[1024,512]{0,1:T(8,128)S(1)} %fusion.34, f32[1024,512]{0,1:T(8,128)S(1)} %fusion.35, bf16[512,512]{1,0:T(8,128)(2,1)S(1)} %copy-done.2, bf16[512,1024]{1,0:T(8,128)(2,1)S(1)} %copy-done), kind=kOutput, calls=%fused_computation.1 | convolution fusion | flops 539492352 | bytes 11010048 | tf_op jit(solution)/shard_map/dot_general | solution.py:52
  (119 shorter events, 10.1 us)
Async XLA Ops:
  0.0 9.6 %copy-start = (bf16[512,1024]{1,0:T(8,128)(2,1)S(1)}, bf16[512,1024]{1,0:T(8,128)(2,1)}, u32[]{:S(2)}) copy-start(bf16[512,1024]{1,0:T(8,128)(2,1)} %param.5) | copy-start | bytes 3145732
  0.0 6.5 %copy-start.1 = (bf16[4,512,128]{2,1,0:T(8,128)(2,1)S(1)}, bf16[4,512,128]{2,1,0:T(8,128)(2,1)}, u32[]{:S(2)}) copy-start(bf16[4,512,128]{2,1,0:T(8,128)(2,1)} %param.7) | copy-start | bytes 1572868
  0.0 6.7 %slice-start = ((bf16[4,512,128]{2,1,0:T(8,128)(2,1)}), bf16[2,512,128]{2,1,0:T(8,128)(2,1)S(1)}, s32[]{:S(2)}) async-start(bf16[4,512,128]{2,1,0:T(8,128)(2,1)} %param.7), calls=%async_computation | async-start | bytes 524288 | tf_op jit(solution)/shard_map/slice | solution.py:57
  0.0 6.5 %copy-start.3 = (bf16[4,512,128]{2,1,0:T(8,128)(2,1)S(1)}, bf16[4,512,128]{2,1,0:T(8,128)(2,1)}, u32[]{:S(2)}) copy-start(bf16[4,512,128]{2,1,0:T(8,128)(2,1)} %param.8) | copy-start | bytes 1572868
  1.1 6.0 %slice-start.1 = ((bf16[4,512,128]{2,1,0:T(8,128)(2,1)}), bf16[3,512,128]{2,1,0:T(8,128)(2,1)S(1)}, s32[]{:S(2)}) async-start(bf16[4,512,128]{2,1,0:T(8,128)(2,1)} %param.7), calls=%async_computation.1 | async-start | bytes 786432 | tf_op jit(solution)/shard_map/slice | solution.py:57
  1.8 4.7 %copy-start.19 = (bf16[128,128]{1,0:T(8,128)(2,1)}, bf16[128,128]{1,0:T(8,128)(2,1)S(1)}, u32[]{:S(2)}) copy-start(bf16[128,128]{1,0:T(8,128)(2,1)S(1)} %get-tuple-element.49) | copy-start | bytes 98308
  1.8 4.7 %copy-start.21 = (bf16[128,128]{1,0:T(8,128)(2,1)}, bf16[128,128]{1,0:T(8,128)(2,1)S(1)}, u32[]{:S(2)}) copy-start(bf16[128,128]{1,0:T(8,128)(2,1)S(1)} %get-tuple-element.50) | copy-start | bytes 98308
  2.4 11.5 %collective-permute-start.7 = (bf16[256,128]{1,0:T(8,128)(2,1)}, bf16[256,128]{1,0:T(8,128)(2,1)}, u32[]{:S(2)}, u32[]{:S(2)}) collective-permute-start(bf16[256,128]{1,0:T(8,128)(2,1)} %fusion.96), channel_id=1, source_target_pairs={{0,8},{4,12},{8,0},{12,4},{1,9},{5,13},{9,1},{13,5},{2,10},{6,14},... | collective-permute-start | bytes 196616 | tf_op jit(solution)/shard_map/ppermute | solution.py:21
  9.1 5.7 %collective-permute-start = (f32[1024,128]{1,0:T(8,128)}, f32[1024,128]{1,0:T(8,128)}, u32[]{:S(2)}, u32[]{:S(2)}) collective-permute-start(f32[1024,128]{1,0:T(8,128)} %pad_maximum_fusion), channel_id=1, source_target_pairs={{0,1},{1,0},{2,3},{3,2},{4,5},{5,4},{6,7},{7,6},{8,9},{9,8},{10,11... | collective-permute-start | bytes 1572872 | tf_op jit(solution)/shard_map/ppermute | solution.py:21
  11.0 9.3 %collective-permute-start.1 = (bf16[128,1024]{1,0:T(8,128)(2,1)}, bf16[128,1024]{1,0:T(8,128)(2,1)}, u32[]{:S(2)}, u32[]{:S(2)}) collective-permute-start(bf16[128,1024]{1,0:T(8,128)(2,1)} %fusion.3), channel_id=1, source_target_pairs={{0,1},{1,0},{2,3},{3,2},{4,5},{5,4},{6,7},{7,6},{8,9},{9,8},{10,11... | collective-permute-start | bytes 786440 | tf_op jit(solution)/shard_map/ppermute | solution.py:21
  13.1 9.0 %collective-permute-start.3 = (f32[3,128,512]{2,1,0:T(8,128)}, f32[3,128,512]{2,1,0:T(8,128)}, u32[]{:S(2)}, u32[]{:S(2)}) collective-permute-start(f32[3,128,512]{2,1,0:T(8,128)} %convolution_add_fusion), channel_id=1, source_target_pairs={{0,1},{1,0},{2,3},{3,2},{4,5},{5,4},{6,7},{7,6},{8,9},{9,8},{10,11... | collective-permute-start | bytes 2359304 | tf_op jit(solution)/shard_map/ppermute | solution.py:21
  13.9 6.3 %copy-start.16 = (bf16[128,128]{1,0:T(8,128)(2,1)S(1)}, bf16[128,128]{1,0:T(8,128)(2,1)}, u32[]{:S(2)}) copy-start(bf16[128,128]{1,0:T(8,128)(2,1)} %copy-done.15) | copy-start | bytes 98308
  13.9 6.3 %copy-start.18 = (bf16[128,128]{1,0:T(8,128)(2,1)S(1)}, bf16[128,128]{1,0:T(8,128)(2,1)}, u32[]{:S(2)}) copy-start(bf16[128,128]{1,0:T(8,128)(2,1)} %copy-done.17) | copy-start | bytes 98308
  16.6 9.9 %collective-permute-start.2 = (f32[640,128]{1,0:T(8,128)S(1)}, f32[640,128]{1,0:T(8,128)S(1)}, u32[]{:S(2)}, u32[]{:S(2)}) collective-permute-start(f32[640,128]{1,0:T(8,128)S(1)} %pad_maximum_fusion.3), channel_id=1, source_target_pairs={{0,2},{2,0},{1,3},{3,1},{4,6},{6,4},{5,7},{7,5},{8,10},{10,8},{9,1... | collective-permute-start | bytes 983048 | tf_op jit(solution)/shard_map/ppermute | solution.py:21
  24.0 4.3 %copy-start.12 = (bf16[128,128]{1,0:T(8,128)(2,1)S(1)}, bf16[128,128]{1,0:T(8,128)(2,1)}, u32[]{:S(2)}) copy-start(bf16[128,128]{1,0:T(8,128)(2,1)} %get-tuple-element.53) | copy-start | bytes 98308
  24.0 4.3 %copy-start.14 = (bf16[128,128]{1,0:T(8,128)(2,1)S(1)}, bf16[128,128]{1,0:T(8,128)(2,1)}, u32[]{:S(2)}) copy-start(bf16[128,128]{1,0:T(8,128)(2,1)} %get-tuple-element.54) | copy-start | bytes 98308
  24.1 11.0 %collective-permute-start.4 = (bf16[768,256]{1,0:T(8,128)(2,1)S(1)}, bf16[768,256]{1,0:T(8,128)(2,1)S(1)}, u32[]{:S(2)}, u32[]{:S(2)}) collective-permute-start(bf16[768,256]{1,0:T(8,128)(2,1)S(1)} %pad_maximum_fusion.1), channel_id=1, source_target_pairs={{0,2},{2,0},{1,3},{3,1},{4,6},{6,4},{5,7},{7,5},{8,10},{10,8},{9,1... | collective-permute-start | bytes 1179656 | tf_op jit(solution)/shard_map/ppermute | solution.py:21
  26.5 6.3 %collective-permute-start.5 = (f32[384,128]{1,0:T(8,128)S(1)}, f32[384,128]{1,0:T(8,128)S(1)}, u32[]{:S(2)}, u32[]{:S(2)}) collective-permute-start(f32[384,128]{1,0:T(8,128)S(1)} %pad_maximum_fusion.5), channel_id=1, source_target_pairs={{0,4},{4,0},{8,12},{12,8},{1,5},{5,1},{9,13},{13,9},{2,6},{6,2},{1... | collective-permute-start | bytes 589832 | tf_op jit(solution)/shard_map/ppermute | solution.py:21
  32.8 4.9 %copy-start.6 = (f32[384,128]{1,0:T(8,128)}, f32[384,128]{1,0:T(8,128)S(1)}, u32[]{:S(2)}) copy-start(f32[384,128]{1,0:T(8,128)S(1)} %collective-permute-done.5) | copy-start | bytes 589828
  36.0 7.4 %collective-permute-start.6 = (bf16[512,256]{1,0:T(8,128)(2,1)S(1)}, bf16[512,256]{1,0:T(8,128)(2,1)S(1)}, u32[]{:S(2)}, u32[]{:S(2)}) collective-permute-start(bf16[512,256]{1,0:T(8,128)(2,1)S(1)} %pad_maximum_fusion.4), channel_id=1, source_target_pairs={{0,4},{4,0},{8,12},{12,8},{1,5},{5,1},{9,13},{13,9},{2,6},{6,2},{1... | collective-permute-start | bytes 786440 | tf_op jit(solution)/shard_map/ppermute | solution.py:21
  37.7 5.9 %slice-start.2 = ((f32[384,128]{1,0:T(8,128)}), f32[128,128]{1,0:T(8,128)S(1)}, s32[]{:S(2)}) async-start(f32[384,128]{1,0:T(8,128)} %copy-done.6), calls=%async_computation.2 | async-start | bytes 131072 | tf_op jit(solution)/shard_map/slice | solution.py:72
  44.0 7.8 %copy-start.4 = (bf16[4,512,128]{2,1,0:T(8,128)(2,1)S(1)}, bf16[4,512,128]{2,1,0:T(8,128)(2,1)}, u32[]{:S(2)}) copy-start(bf16[4,512,128]{2,1,0:T(8,128)(2,1)} %param.8) | copy-start | bytes 1572868
  44.0 7.3 %collective-permute-start.8 = (bf16[256,256]{1,0:T(8,128)(2,1)S(1)}, bf16[256,256]{1,0:T(8,128)(2,1)S(1)}, u32[]{:S(2)}, u32[]{:S(2)}) collective-permute-start(bf16[256,256]{1,0:T(8,128)(2,1)S(1)} %pad_maximum_fusion.6), channel_id=1, source_target_pairs={{0,8},{4,12},{8,0},{12,4},{1,9},{5,13},{9,1},{13,5},{2,10},{6,14},... | collective-permute-start | bytes 393224 | tf_op jit(solution)/shard_map/ppermute | solution.py:21
  51.7 1.8 %collective-permute-start.9 = (bf16[3,128,512]{2,1,0:T(8,128)(2,1)S(1)}, bf16[3,128,512]{2,1,0:T(8,128)(2,1)S(1)}, u32[]{:S(2)}, u32[]{:S(2)}) collective-permute-start(bf16[3,128,512]{2,1,0:T(8,128)(2,1)S(1)} %pad_maximum_fusion.2), channel_id=1, source_target_pairs={{0,1},{1,0},{2,3},{3,2},{4,5},{5,4},{6,7},{7,6},{8,9},{9,8},{10,11... | collective-permute-start | bytes 1179656 | tf_op jit(solution)/shard_map/ppermute | solution.py:21
  (12 other events, 14.5 us)

commit v23 on v13

--- a/solution.py
+++ b/solution.py
@@ -64,7 +64,7 @@
         parts = [jnp.concatenate([c[:, :rank], c[:, rank:]], axis=0).astype(F32)]
         parts += partial[b:]
         got = swap(jnp.concatenate(parts, axis=0), b, bits)
-        theirs = got[: 2 * rank].astype(BF16)
+        theirs = got[: 2 * rank]
         theirs_c.append(jnp.concatenate([theirs[:rank], theirs[rank:]], axis=1))
         at = 2 * rank
         for s in range(b, levels - 1):

time: 57.1 us -> 56.1 us (0.982)
  other arithmetic: 7.28 us -> 5.39 us
  local copies, waits for them, and re-layouts: 4.07 us -> 4.95 us
    another operation x3 -> x0, other arithmetic: 1.1 us -> none
    slice x4, local copies, waits for them, and re-layouts: 0.8 us -> 1.69 us  [on_device(): theirs_c.append(jnp.concatenate([theirs[:rank], theirs[rank:]], axis=1))]
    select_n x4, other arithmetic: 0.9 us -> 0.13 us  [on_device(): jnp.where(lower, first, second)]
  transfers between devices with their start and end apart: 11 -> 11, of which waited for: 6 -> 6; matrix products, arithmetic and copies ran while one was open for 30% -> 29% of each run, Pallas kernels for 0% -> 0%
where the time goes in v23:
time: 56.1 us; the launch traced here: 55.6 us
  waiting for transfers between devices  18.8 us (34%)
  matrix products  13.6 us (24%)
  starting transfers between devices  12.2 us (22%)
  other arithmetic  5.39 us (10%)
  local copies, waits for them, and re-layouts  4.95 us (9%)
  between operations  0.66 us (1%)
    ppermute x11, waiting for transfers between devices, swap(): return lax.ppermute(x, axis, [(i, i ^ 1 << stride) for i in range(n)])  18.8 us
    ppermute x11, starting transfers between devices, swap(): return lax.ppermute(x, axis, [(i, i ^ 1 << stride) for i in range(n)])  12.2 us
    dot_general x3, matrix products, project(): jnp.einsum('lrj,jt->lrt', vl_lo[lv], x, preferred_element_type=F32)  3.8 us
    dot_general x4, matrix products, on_device(): coefs = jnp.dot(couple[s], stacked, preferred_element_type=F32).astype(BF16)  2.01 us
    dot_general x1, matrix products, on_device(): c0 = jnp.dot(leaf_inverse, templates, preferred_element_type=F32)  1.83 us
    concatenate x2, other arithmetic, gather_half(): both = jnp.concatenate([x, swap(x, bit, bits), x], axis=-1)  1.79 us
    add x3, other arithmetic, on_device(): partial[s] = partial[s] + recv  1.78 us
    dot_general x4, matrix products, on_device(): current = current - jnp.dot(u_basis[s], full[s], preferred_element_type=F32)  1.73 us
  transfers between devices with their start and end apart: 11, of which 6 were waited for; matrix products, arithmetic and copies ran while one was open for 29% of the time, Pallas kernels for 0%

profile of v23, /device:TPU:0, one launch (start us, length us, event | category | flops | bytes accessed | tf_op | source)
XLA Modules:
  0.0 55.6 jit_solution(3093651355032881845)
XLA Ops:
  0.0 1.1 %slice_bitcast_fusion.12 = (bf16[128,256]{1,0:T(8,128)(2,1)S(1)}, bf16[128,256]{1,0:T(8,128)(2,1)S(1)}, bf16[128,256]{1,0:T(8,128)(2,1)S(1)}, bf16[128,256]{1,0:T(8,128)(2,1)S(1)}) fusion(bf16[4,1,128,256]{3,2,1,0:T(8,128)(2,1)} %param.9), kind=kLoop, calls=%fused_computation.167 | loop fusion | bytes 524288 | tf_op jit(solution)/shard_map/squeeze | solution.py:81
  1.8 4.0 %collective-permute-start.7 = (bf16[256,128]{1,0:T(8,128)(2,1)}, bf16[256,128]{1,0:T(8,128)(2,1)}, u32[]{:S(2)}, u32[]{:S(2)}) collective-permute-start(bf16[256,128]{1,0:T(8,128)(2,1)} %maximum_convert_fusion.3), channel_id=1, source_target_pairs={{0,8},{4,12},{8,0},{12,4},{1,9},{5,13},{9,1},{13,5},{2,10},{6,14},... | collective-permute-start | bytes 196616 | tf_op jit(solution)/shard_map/ppermute | solution.py:21
  7.0 0.8 %pad_maximum_fusion = f32[1024,128]{1,0:T(8,128)} fusion(f32[128,128]{1,0:T(8,128)S(1)} %fusion.80, f32[256,128]{1,0:T(8,128)S(1)} %fusion.84, f32[384,128]{1,0:T(8,128)S(1)} %fusion.87, f32[256,128]{1,0:T(8,128)S(1)} %maximum_convert_fusion), kind=kLoop, calls=%fused_computation.28 | loop fusion | flops 393216 | bytes 1048576 | tf_op jit(solution)/shard_map/concatenate | solution.py:66
  7.9 1.5 %subtract_convert_fusion = (bf16[4,128,512]{2,1,0:T(8,128)(2,1)S(1)}, bf16[4,128,512]{2,1,0:T(8,128)(2,1)S(1)}) fusion(bf16[4,512,128]{2,1,0:T(8,128)(2,1)S(1)} %copy-done.1, bf16[512,512]{1,0:T(8,128)(2,1)} %param.6), kind=kOutput, calls=%fused_computation.23 | convolution fusion | flops 269484032 | bytes 2097152 | tf_op jit(solution)/shard_map/lir,ij->lrj/dot_general | solution.py:91
  9.7 1.0 %fusion.3 = bf16[128,1024]{1,0:T(8,128)(2,1)} fusion(f32[128,1024]{1,0:T(8,128)S(1)} %fusion.64, bf16[512,1024]{1,0:T(8,128)(2,1)S(1)} %copy-done, bf16[4,128,512]{2,1,0:T(8,128)(2,1)S(1)} %get-tuple-element.5), kind=kOutput, calls=%fused_computation.11 | convolution fusion | flops 134479872 | bytes 1966080 | tf_op jit(solution)/shard_map/lrj,jt->lrt/dot_general | solution.py:98
  11.7 1.3 %convolution_add_fusion = f32[3,128,512]{2,1,0:T(8,128)} fusion(f32[3,128,512]{2,1,0:T(8,128)S(1)} %fusion.15, bf16[4,128,512]{2,1,0:T(8,128)(2,1)S(1)} %get-tuple-element.5, bf16[512,1024]{1,0:T(8,128)(2,1)S(1)} %copy-done, s32[]{:T(128)S(6)} %select_n.69), kind=kOutput, calls=%fused_computation.6 | convolution fusion | flops 201523200 | bytes 2621444 | tf_op jit(solution)/shard_map/lrj,jt->lrt/dot_general | solution.py:98
  14.2 0.9 %slice_add_fusion = f32[256,128]{1,0:T(8,128)S(1)} fusion(f32[256,128]{1,0:T(8,128)S(1)} %fusion.84, f32[1024,128]{1,0:T(8,128)} %collective-permute-done), kind=kLoop, calls=%fused_computation.100 | loop fusion | flops 32768 | bytes 393216 | tf_op jit(solution)/shard_map/add | solution.py:77
  15.1 0.8 %slice_add_fusion.2 = f32[128,128]{1,0:T(8,128)S(1)} fusion(f32[128,128]{1,0:T(8,128)S(1)} %fusion.80, f32[1024,128]{1,0:T(8,128)} %collective-permute-done), kind=kLoop, calls=%fused_computation.161 | loop fusion | flops 16384 | bytes 196608 | tf_op jit(solution)/shard_map/add | solution.py:77
  16.0 1.6 %collective-permute-start.2 = (f32[640,128]{1,0:T(8,128)S(1)}, f32[640,128]{1,0:T(8,128)S(1)}, u32[]{:S(2)}, u32[]{:S(2)}) collective-permute-start(f32[640,128]{1,0:T(8,128)S(1)} %pad_maximum_fusion.2), channel_id=1, source_target_pairs={{0,2},{2,0},{1,3},{3,1},{4,6},{6,4},{5,7},{7,5},{8,10},{10,8},{9,1... | collective-permute-start | bytes 983048 | tf_op jit(solution)/shard_map/ppermute | solution.py:21
  17.6 0.9 %slice.308 = f32[384,128]{1,0:T(8,128)S(1)} slice(f32[1024,128]{1,0:T(8,128)} %collective-permute-done), slice={[256:640], [0:128]} | slice | bytes 393216 | tf_op jit(solution)/shard_map/slice | solution.py:72
  18.5 0.9 %fusion.126 = (bf16[128,128]{1,0:T(8,128)(2,1)S(1)}, bf16[128,128]{1,0:T(8,128)(2,1)S(1)}) fusion(f32[1024,128]{1,0:T(8,128)} %collective-permute-done), kind=kLoop, calls=%fused_computation.198 | loop fusion | bytes 131072 | tf_op jit(solution)/shard_map/slice | solution.py:68
  19.5 1.3 %convolution_convert_fusion = bf16[256,1024]{1,0:T(8,128)(2,1)S(1)} fusion(bf16[128,1024]{1,0:T(8,128)(2,1)} %collective-permute-done.1, bf16[128,1024]{1,0:T(8,128)(2,1)} %fusion.3, bf16[256,128]{1,0:T(8,128)(2,1)S(1)} %get-tuple-element.32, bf16[256,128]{1,0:T(8,128)(2,1)S(1)} %get-tuple-element.31), kind=kOutput, calls=%fused_computation.5 | convolution fusion | flops 135528448 | bytes 1179648 | tf_op jit(solution)/shard_map/dot_general | solution.py:137
  21.6 1.5 %fusion.2 = f32[3,128,512]{2,1,0:T(8,128)S(1)} fusion(f32[3,128,512]{2,1,0:T(8,128)S(1)} %bitcast.124, f32[3,128,512]{2,1,0:T(8,128)} %collective-permute-done.3, f32[3,128,512]{2,1,0:T(8,128)S(1)} %fusion.18, bf16[4,128,512]{2,1,0:T(8,128)(2,1)S(1)} %get-tuple-element.5, bf16[512,1024]{1,0:T(8,128)(2,1)S(1)} %copy-done, s32[]{:T(128)S(6)} %select_n.68), kind=kOutput, calls=%fused_computation.9 | convolution fusion | flops 201916416 | bytes 4194308 | tf_op jit(solution)/shard_map/lrj,jt->lrt/dot_general | solution.py:98
  23.9 2.3 %collective-permute-done.2 = f32[640,128]{1,0:T(8,128)S(1)} collective-permute-done((f32[640,128]{1,0:T(8,128)S(1)}, f32[640,128]{1,0:T(8,128)S(1)}, u32[]{:S(2)}, u32[]{:S(2)}) %collective-permute-start.2) | collective-permute-done | bytes 327712 | tf_op jit(solution)/shard_map/ppermute | solution.py:21
  26.2 1.6 %collective-permute-start.5 = (f32[384,128]{1,0:T(8,128)S(1)}, f32[384,128]{1,0:T(8,128)S(1)}, u32[]{:S(2)}, u32[]{:S(2)}) collective-permute-start(f32[384,128]{1,0:T(8,128)S(1)} %pad_maximum_fusion.4), channel_id=1, source_target_pairs={{0,4},{4,0},{8,12},{12,8},{1,5},{5,1},{9,13},{13,9},{2,6},{6,2},{1... | collective-permute-start | bytes 589832 | tf_op jit(solution)/shard_map/ppermute | solution.py:21
  27.9 3.9 %collective-permute-done.4 = bf16[512,256]{1,0:T(8,128)(2,1)S(1)} collective-permute-done((bf16[512,256]{1,0:T(8,128)(2,1)S(1)}, bf16[512,256]{1,0:T(8,128)(2,1)S(1)}, u32[]{:S(2)}, u32[]{:S(2)}) %collective-permute-start.4) | collective-permute-done | bytes 262176 | tf_op jit(solution)/shard_map/ppermute | solution.py:21
  32.5 1.6 %collective-permute-start.6 = (bf16[512,128]{1,0:T(8,128)(2,1)S(1)}, bf16[512,128]{1,0:T(8,128)(2,1)S(1)}, u32[]{:S(2)}, u32[]{:S(2)}) collective-permute-start(bf16[512,128]{1,0:T(8,128)(2,1)S(1)} %pad_maximum_fusion.11), channel_id=1, source_target_pairs={{0,4},{4,0},{8,12},{12,8},{1,5},{5,1},{9,13},{13,9},{2,6},{6,2},{1... | collective-permute-start | bytes 393224 | tf_op jit(solution)/shard_map/ppermute | solution.py:21
  34.2 3.3 %collective-permute-done.6 = bf16[512,128]{1,0:T(8,128)(2,1)S(1)} collective-permute-done((bf16[512,128]{1,0:T(8,128)(2,1)S(1)}, bf16[512,128]{1,0:T(8,128)(2,1)S(1)}, u32[]{:S(2)}, u32[]{:S(2)}) %collective-permute-start.6) | collective-permute-done | bytes 131104 | tf_op jit(solution)/shard_map/ppermute | solution.py:21
  38.5 4.8 %collective-permute-done.8 = bf16[256,128]{1,0:T(8,128)(2,1)S(1)} collective-permute-done((bf16[256,128]{1,0:T(8,128)(2,1)S(1)}, bf16[256,128]{1,0:T(8,128)(2,1)S(1)}, u32[]{:S(2)}, u32[]{:S(2)}) %collective-permute-start.8) | collective-permute-done | bytes 65568 | tf_op jit(solution)/shard_map/ppermute | solution.py:21
  43.6 1.7 %collective-permute-start.9 = (bf16[2,128,256]{1,2,0:T(8,128)(2,1)S(1)}, bf16[2,128,256]{1,2,0:T(8,128)(2,1)S(1)}, u32[]{:S(2)}, u32[]{:S(2)}) collective-permute-start(bf16[2,128,256]{1,2,0:T(8,128)(2,1)S(1)} %pad_maximum_fusion.14), channel_id=1, source_target_pairs={{0,2},{2,0},{1,3},{3,1},{4,6},{6,4},{5,7},{7,5},{8,10},{10,8},{9,1... | collective-permute-start | bytes 393224 | tf_op jit(solution)/shard_map/ppermute | solution.py:21
  45.5 3.2 %collective-permute-done.9 = bf16[2,128,256]{1,2,0:T(8,128)(2,1)S(1)} collective-permute-done((bf16[2,128,256]{1,2,0:T(8,128)(2,1)S(1)}, bf16[2,128,256]{1,2,0:T(8,128)(2,1)S(1)}, u32[]{:S(2)}, u32[]{:S(2)}) %collective-permute-start.9) | collective-permute-done | bytes 131104 | tf_op jit(solution)/shard_map/ppermute | solution.py:21
  49.8 1.3 %collective-permute-done.10 = bf16[3,128,512]{1,2,0:T(8,128)(2,1)S(1)} collective-permute-done((bf16[3,128,512]{1,2,0:T(8,128)(2,1)S(1)}, bf16[3,128,512]{1,2,0:T(8,128)(2,1)S(1)}, u32[]{:S(2)}, u32[]{:S(2)}) %collective-permute-start.10) | collective-permute-done | bytes 393248 | tf_op jit(solution)/shard_map/ppermute | solution.py:21
  51.1 1.2 %fusion.9 = bf16[3,128,1024]{1,2,0:T(8,128)(2,1)S(1)} fusion(s32[]{:T(128)S(6)} %select_n.79, bf16[1,128,512]{1,2,0:T(8,128)(2,1)S(1)} %copy.16, bf16[2,128,512]{1,2,0:T(8,128)(2,1)S(1)} %fusion.32, bf16[3,128,512]{1,2,0:T(8,128)(2,1)S(1)} %collective-permute-done.10), kind=kLoop, calls=%fused_computation.26 | loop fusion | flops 3932160 | bytes 1572868 | tf_op jit(solution)/shard_map/concatenate | solution.py:44
  53.8 1.8 %fusion = bf16[512,1024]{1,0:T(8,128)(2,1)} fusion(f32[1024,512]{0,1:T(8,128)S(1)} %fusion.34, f32[1024,512]{0,1:T(8,128)S(1)} %fusion.35, f32[1024,512]{0,1:T(8,128)S(1)} %fusion.36, f32[1024,512]{0,1:T(8,128)S(1)} %fusion.37, bf16[512,512]{1,0:T(8,128)(2,1)S(1)} %copy-done.2, bf16[512,1024]{1,0:T(8,128)(2,1)S(1)} %copy-done), kind=kOutput, calls=%fused_computation.1 | convolution fusion | flops 539492352 | bytes 11010048 | tf_op jit(solution)/shard_map/dot_general | solution.py:52
  (104 shorter events, 10.3 us)
Async XLA Ops:
  0.0 9.4 %copy-start = (bf16[512,1024]{1,0:T(8,128)(2,1)S(1)}, bf16[512,1024]{1,0:T(8,128)(2,1)}, u32[]{:S(2)}) copy-start(bf16[512,1024]{1,0:T(8,128)(2,1)} %param.5) | copy-start | bytes 3145732
  0.0 5.9 %copy-start.1 = (bf16[4,512,128]{2,1,0:T(8,128)(2,1)S(1)}, bf16[4,512,128]{2,1,0:T(8,128)(2,1)}, u32[]{:S(2)}) copy-start(bf16[4,512,128]{2,1,0:T(8,128)(2,1)} %param.7) | copy-start | bytes 1572868
  0.0 6.1 %slice-start = ((bf16[4,512,128]{2,1,0:T(8,128)(2,1)}), bf16[2,512,128]{2,1,0:T(8,128)(2,1)S(1)}, s32[]{:S(2)}) async-start(bf16[4,512,128]{2,1,0:T(8,128)(2,1)} %param.7), calls=%async_computation | async-start | bytes 524288 | tf_op jit(solution)/shard_map/slice | solution.py:57
  0.0 6.5 %slice-start.1 = ((bf16[4,512,128]{2,1,0:T(8,128)(2,1)}), bf16[3,512,128]{2,1,0:T(8,128)(2,1)S(1)}, s32[]{:S(2)}) async-start(bf16[4,512,128]{2,1,0:T(8,128)(2,1)} %param.7), calls=%async_computation.1 | async-start | bytes 786432 | tf_op jit(solution)/shard_map/slice | solution.py:57
  0.0 5.9 %copy-start.3 = (bf16[4,512,128]{2,1,0:T(8,128)(2,1)S(1)}, bf16[4,512,128]{2,1,0:T(8,128)(2,1)}, u32[]{:S(2)}) copy-start(bf16[4,512,128]{2,1,0:T(8,128)(2,1)} %param.8) | copy-start | bytes 1572868
  1.2 5.1 %copy-start.11 = (bf16[128,128]{1,0:T(8,128)(2,1)}, bf16[128,128]{1,0:T(8,128)(2,1)S(1)}, u32[]{:S(2)}) copy-start(bf16[128,128]{1,0:T(8,128)(2,1)S(1)} %get-tuple-element.39) | copy-start | bytes 98308
  1.2 5.1 %copy-start.13 = (bf16[128,128]{1,0:T(8,128)(2,1)}, bf16[128,128]{1,0:T(8,128)(2,1)S(1)}, u32[]{:S(2)}) copy-start(bf16[128,128]{1,0:T(8,128)(2,1)S(1)} %get-tuple-element.40) | copy-start | bytes 98308
  1.8 11.5 %collective-permute-start.7 = (bf16[256,128]{1,0:T(8,128)(2,1)}, bf16[256,128]{1,0:T(8,128)(2,1)}, u32[]{:S(2)}, u32[]{:S(2)}) collective-permute-start(bf16[256,128]{1,0:T(8,128)(2,1)} %maximum_convert_fusion.3), channel_id=1, source_target_pairs={{0,8},{4,12},{8,0},{12,4},{1,9},{5,13},{9,1},{13,5},{2,10},{6,14},... | collective-permute-start | bytes 196616 | tf_op jit(solution)/shard_map/ppermute | solution.py:21
  7.0 2.7 %copy-start.7 = (bf16[128,128]{1,0:T(8,128)(2,1)}, bf16[128,128]{1,0:T(8,128)(2,1)S(1)}, u32[]{:S(2)}) copy-start(bf16[128,128]{1,0:T(8,128)(2,1)S(1)} %get-tuple-element.53) | copy-start | bytes 98308
  7.0 2.7 %copy-start.9 = (bf16[128,128]{1,0:T(8,128)(2,1)}, bf16[128,128]{1,0:T(8,128)(2,1)S(1)}, u32[]{:S(2)}) copy-start(bf16[128,128]{1,0:T(8,128)(2,1)S(1)} %get-tuple-element.54) | copy-start | bytes 98308
  7.9 6.3 %collective-permute-start = (f32[1024,128]{1,0:T(8,128)}, f32[1024,128]{1,0:T(8,128)}, u32[]{:S(2)}, u32[]{:S(2)}) collective-permute-start(f32[1024,128]{1,0:T(8,128)} %pad_maximum_fusion), channel_id=1, source_target_pairs={{0,1},{1,0},{2,3},{3,2},{4,5},{5,4},{6,7},{7,6},{8,9},{9,8},{10,11... | collective-permute-start | bytes 1572872 | tf_op jit(solution)/shard_map/ppermute | solution.py:21
  10.8 8.7 %collective-permute-start.1 = (bf16[128,1024]{1,0:T(8,128)(2,1)}, bf16[128,1024]{1,0:T(8,128)(2,1)}, u32[]{:S(2)}, u32[]{:S(2)}) collective-permute-start(bf16[128,1024]{1,0:T(8,128)(2,1)} %fusion.3), channel_id=1, source_target_pairs={{0,1},{1,0},{2,3},{3,2},{4,5},{5,4},{6,7},{7,6},{8,9},{9,8},{10,11... | collective-permute-start | bytes 786440 | tf_op jit(solution)/shard_map/ppermute | solution.py:21
  12.9 8.4 %collective-permute-start.3 = (f32[3,128,512]{2,1,0:T(8,128)}, f32[3,128,512]{2,1,0:T(8,128)}, u32[]{:S(2)}, u32[]{:S(2)}) collective-permute-start(f32[3,128,512]{2,1,0:T(8,128)} %convolution_add_fusion), channel_id=1, source_target_pairs={{0,1},{1,0},{2,3},{3,2},{4,5},{5,4},{6,7},{7,6},{8,9},{9,8},{10,11... | collective-permute-start | bytes 2359304 | tf_op jit(solution)/shard_map/ppermute | solution.py:21
  12.9 6.5 %copy-start.8 = (bf16[128,128]{1,0:T(8,128)(2,1)S(1)}, bf16[128,128]{1,0:T(8,128)(2,1)}, u32[]{:S(2)}) copy-start(bf16[128,128]{1,0:T(8,128)(2,1)} %copy-done.7) | copy-start | bytes 98308
  12.9 6.5 %copy-start.10 = (bf16[128,128]{1,0:T(8,128)(2,1)S(1)}, bf16[128,128]{1,0:T(8,128)(2,1)}, u32[]{:S(2)}) copy-start(bf16[128,128]{1,0:T(8,128)(2,1)} %copy-done.9) | copy-start | bytes 98308
  16.0 10.2 %collective-permute-start.2 = (f32[640,128]{1,0:T(8,128)S(1)}, f32[640,128]{1,0:T(8,128)S(1)}, u32[]{:S(2)}, u32[]{:S(2)}) collective-permute-start(f32[640,128]{1,0:T(8,128)S(1)} %pad_maximum_fusion.2), channel_id=1, source_target_pairs={{0,2},{2,0},{1,3},{3,1},{4,6},{6,4},{5,7},{7,5},{8,10},{10,8},{9,1... | collective-permute-start | bytes 983048 | tf_op jit(solution)/shard_map/ppermute | solution.py:21
  23.3 8.5 %collective-permute-start.4 = (bf16[512,256]{1,0:T(8,128)(2,1)S(1)}, bf16[512,256]{1,0:T(8,128)(2,1)S(1)}, u32[]{:S(2)}, u32[]{:S(2)}) collective-permute-start(bf16[512,256]{1,0:T(8,128)(2,1)S(1)} %pad_maximum_fusion.3), channel_id=1, source_target_pairs={{0,2},{2,0},{1,3},{3,1},{4,6},{6,4},{5,7},{7,5},{8,10},{10,8},{9,1... | collective-permute-start | bytes 786440 | tf_op jit(solution)/shard_map/ppermute | solution.py:21
  26.2 7.9 %collective-permute-start.5 = (f32[384,128]{1,0:T(8,128)S(1)}, f32[384,128]{1,0:T(8,128)S(1)}, u32[]{:S(2)}, u32[]{:S(2)}) collective-permute-start(f32[384,128]{1,0:T(8,128)S(1)} %pad_maximum_fusion.4), channel_id=1, source_target_pairs={{0,4},{4,0},{8,12},{12,8},{1,5},{5,1},{9,13},{13,9},{2,6},{6,2},{1... | collective-permute-start | bytes 589832 | tf_op jit(solution)/shard_map/ppermute | solution.py:21
  32.5 5.0 %collective-permute-start.6 = (bf16[512,128]{1,0:T(8,128)(2,1)S(1)}, bf16[512,128]{1,0:T(8,128)(2,1)S(1)}, u32[]{:S(2)}, u32[]{:S(2)}) collective-permute-start(bf16[512,128]{1,0:T(8,128)(2,1)S(1)} %pad_maximum_fusion.11), channel_id=1, source_target_pairs={{0,4},{4,0},{8,12},{12,8},{1,5},{5,1},{9,13},{13,9},{2,6},{6,2},{1... | collective-permute-start | bytes 393224 | tf_op jit(solution)/shard_map/ppermute | solution.py:21
  37.5 11.9 %copy-start.4 = (bf16[4,512,128]{2,1,0:T(8,128)(2,1)S(1)}, bf16[4,512,128]{2,1,0:T(8,128)(2,1)}, u32[]{:S(2)}) copy-start(bf16[4,512,128]{2,1,0:T(8,128)(2,1)} %param.8) | copy-start | bytes 1572868
  37.5 11.9 %copy-start.6 = (bf16[256,1024]{1,0:T(8,128)(2,1)S(1)}, bf16[256,1024]{1,0:T(8,128)(2,1)}, u32[]{:S(2)}) copy-start(bf16[256,1024]{1,0:T(8,128)(2,1)} %copy-done.5) | copy-start | bytes 1572868
  38.1 5.2 %collective-permute-start.8 = (bf16[256,128]{1,0:T(8,128)(2,1)S(1)}, bf16[256,128]{1,0:T(8,128)(2,1)S(1)}, u32[]{:S(2)}, u32[]{:S(2)}) collective-permute-start(bf16[256,128]{1,0:T(8,128)(2,1)S(1)} %pad_maximum_fusion.15), channel_id=1, source_target_pairs={{0,8},{4,12},{8,0},{12,4},{1,9},{5,13},{9,1},{13,5},{2,10},{6,14},... | collective-permute-start | bytes 196616 | tf_op jit(solution)/shard_map/ppermute | solution.py:21
  43.6 5.0 %collective-permute-start.9 = (bf16[2,128,256]{1,2,0:T(8,128)(2,1)S(1)}, bf16[2,128,256]{1,2,0:T(8,128)(2,1)S(1)}, u32[]{:S(2)}, u32[]{:S(2)}) collective-permute-start(bf16[2,128,256]{1,2,0:T(8,128)(2,1)S(1)} %pad_maximum_fusion.14), channel_id=1, source_target_pairs={{0,2},{2,0},{1,3},{3,1},{4,6},{6,4},{5,7},{7,5},{8,10},{10,8},{9,1... | collective-permute-start | bytes 393224 | tf_op jit(solution)/shard_map/ppermute | solution.py:21
  49.3 1.8 %collective-permute-start.10 = (bf16[3,128,512]{1,2,0:T(8,128)(2,1)S(1)}, bf16[3,128,512]{1,2,0:T(8,128)(2,1)S(1)}, u32[]{:S(2)}, u32[]{:S(2)}) collective-permute-start(bf16[3,128,512]{1,2,0:T(8,128)(2,1)S(1)} %pad_maximum_fusion.1), channel_id=1, source_target_pairs={{0,1},{1,0},{2,3},{3,2},{4,5},{5,4},{6,7},{7,6},{8,9},{9,8},{10,11... | collective-permute-start | bytes 1179656 | tf_op jit(solution)/shard_map/ppermute | solution.py:21
  (4 other events, 6.8 us)

commit v24 on v23

--- a/solution.py
+++ b/solution.py
@@ -72,7 +72,7 @@
             recv = got[at : at + n]
             at += n
             if s == b:
-                w_own[s] = jnp.concatenate([partial[s], recv], axis=1)
+                w_own[s] = (partial[s], recv)
             else:
                 partial[s] = partial[s] + recv
     couple = []
@@ -142,8 +142,12 @@
                 piece = coefs.astype(F32)
             else:
                 piece = cols(coefs, side(s, bits) * w, w).astype(F32)
+            own_w, sib_w = w_own[s]
             fix = jnp.dot(
-                w_own[s], piece, preferred_element_type=F32,
+                own_w, piece[:rank], preferred_element_type=F32,
+                precision=lax.Precision.HIGHEST,
+            ) + jnp.dot(
+                sib_w, piece[rank:], preferred_element_type=F32,
                 precision=lax.Precision.HIGHEST,
             )
             rest = rest - fix.reshape(rest.shape)

time: 56.1 us -> 59 us (1.052)
  matrix products: 13.6 us -> 15.5 us
  other arithmetic: 5.39 us -> 6.92 us
  starting transfers between devices: 12.2 us -> 11.1 us
  waiting for transfers between devices: 18.8 us -> 19.9 us
  local copies, waits for them, and re-layouts: 4.95 us -> 4.32 us
    dot_general x3 -> x6, matrix products: 1.06 us -> 2.88 us  [the longest x3 1.91 us: on_device(): jnp.dot(sib_w, piece[rank:], preferred_element_type=F32, precision=lax.Pr...]
    select_n x4, other arithmetic: 0.13 us -> 1.68 us  [on_device(): jnp.where(lower, first, second)]
    ppermute x11, starting transfers between devices: 12.2 us -> 11.1 us  [swap(): return lax.ppermute(x, axis, [(i, i ^ 1 << stride) for i in range(n)])]
    ppermute x11, waiting for transfers between devices: 18.8 us -> 19.9 us  [swap(): return lax.ppermute(x, axis, [(i, i ^ 1 << stride) for i in range(n)])]
    slice x3 -> x0, local copies, waits for them, and re-layouts: 0.96 us -> none  [on_device(): recv = got[at:at + n]]
    slice x2, local copies, waits for them, and re-layouts: 0.05 us -> 0.67 us  [on_device(): first = jnp.concatenate([mine[:, :rank], theirs[:, :rank]], axis=0)]
  transfers between devices with their start and end apart: 11 -> 11, of which waited for: 6 -> 6; matrix products, arithmetic and copies ran while one was open for 29% -> 32% of each run, Pallas kernels for 0% -> 0%
where the time goes in v24:
time: 59 us; the launch traced here: 58.3 us
  waiting for transfers between devices  19.9 us (34%)
  matrix products  15.5 us (26%)
  starting transfers between devices  11.1 us (19%)
  other arithmetic  6.92 us (12%)
  local copies, waits for them, and re-layouts  4.32 us (7%)
  between operations  0.67 us (1%)
    ppermute x11, waiting for transfers between devices, swap(): return lax.ppermute(x, axis, [(i, i ^ 1 << stride) for i in range(n)])  19.9 us
    ppermute x11, starting transfers between devices, swap(): return lax.ppermute(x, axis, [(i, i ^ 1 << stride) for i in range(n)])  11.1 us
    dot_general x3, matrix products, project(): jnp.einsum('lrj,jt->lrt', vl_lo[lv], x, preferred_element_type=F32)  3.81 us
    dot_general x4, matrix products, on_device(): coefs = jnp.dot(couple[s], stacked, preferred_element_type=F32).astype(BF16)  2.01 us
    dot_general x3, matrix products, on_device(): jnp.dot(sib_w, piece[rank:], preferred_element_type=F32, precision=lax.Pr...  1.91 us
    dot_general x1, matrix products, on_device(): c0 = jnp.dot(leaf_inverse, templates, preferred_element_type=F32)  1.83 us
    concatenate x2, other arithmetic, gather_half(): both = jnp.concatenate([x, swap(x, bit, bits), x], axis=-1)  1.79 us
    add x3, other arithmetic, on_device(): partial[s] = partial[s] + recv  1.78 us
  transfers between devices with their start and end apart: 11, of which 6 were waited for; matrix products, arithmetic and copies ran while one was open for 32% of the time, Pallas kernels for 0%

profile of v24, /device:TPU:0, one launch (start us, length us, event | category | flops | bytes accessed | tf_op | source)
XLA Modules:
  0.0 58.3 jit_solution(431489328683095657)
XLA Ops:
  0.0 1.1 %slice_bitcast_fusion.11 = (bf16[128,256]{1,0:T(8,128)(2,1)S(1)}, bf16[128,256]{1,0:T(8,128)(2,1)S(1)}, bf16[128,256]{1,0:T(8,128)(2,1)S(1)}, bf16[128,256]{1,0:T(8,128)(2,1)S(1)}) fusion(bf16[4,1,128,256]{3,2,1,0:T(8,128)(2,1)} %param.9), kind=kLoop, calls=%fused_computation.167 | loop fusion | bytes 524288 | tf_op jit(solution)/shard_map/squeeze | solution.py:81
  1.8 4.0 %collective-permute-start.7 = (bf16[256,128]{1,0:T(8,128)(2,1)}, bf16[256,128]{1,0:T(8,128)(2,1)}, u32[]{:S(2)}, u32[]{:S(2)}) collective-permute-start(bf16[256,128]{1,0:T(8,128)(2,1)} %maximum_convert_fusion.3), channel_id=1, source_target_pairs={{0,8},{4,12},{8,0},{12,4},{1,9},{5,13},{9,1},{13,5},{2,10},{6,14},... | collective-permute-start | bytes 196616 | tf_op jit(solution)/shard_map/ppermute | solution.py:21
  7.6 0.8 %pad_maximum_fusion = f32[1024,128]{1,0:T(8,128)} fusion(f32[128,128]{1,0:T(8,128)S(1)} %fusion.75, f32[256,128]{1,0:T(8,128)S(1)} %fusion.79, f32[384,128]{1,0:T(8,128)S(1)} %fusion.82, f32[256,128]{1,0:T(8,128)S(1)} %maximum_convert_fusion), kind=kLoop, calls=%fused_computation.31 | loop fusion | flops 393216 | bytes 1048576 | tf_op jit(solution)/shard_map/concatenate | solution.py:66
  8.4 1.5 %subtract_convert_fusion = (bf16[4,128,512]{2,1,0:T(8,128)(2,1)S(1)}, bf16[4,128,512]{2,1,0:T(8,128)(2,1)S(1)}) fusion(bf16[4,512,128]{2,1,0:T(8,128)(2,1)S(1)} %copy-done.1, bf16[512,512]{1,0:T(8,128)(2,1)} %param.6), kind=kOutput, calls=%fused_computation.26 | convolution fusion | flops 269484032 | bytes 2097152 | tf_op jit(solution)/shard_map/lir,ij->lrj/dot_general | solution.py:91
  10.3 1.0 %fusion.3 = bf16[128,1024]{1,0:T(8,128)(2,1)} fusion(f32[128,1024]{1,0:T(8,128)S(1)} %fusion.62, bf16[512,1024]{1,0:T(8,128)(2,1)S(1)} %copy-done, bf16[4,128,512]{2,1,0:T(8,128)(2,1)S(1)} %get-tuple-element.5), kind=kOutput, calls=%fused_computation.12 | convolution fusion | flops 134479872 | bytes 1966080 | tf_op jit(solution)/shard_map/lrj,jt->lrt/dot_general | solution.py:98
  12.2 1.3 %convolution_add_fusion = f32[3,128,512]{2,1,0:T(8,128)} fusion(f32[3,128,512]{2,1,0:T(8,128)S(1)} %fusion.16, bf16[4,128,512]{2,1,0:T(8,128)(2,1)S(1)} %get-tuple-element.5, bf16[512,1024]{1,0:T(8,128)(2,1)S(1)} %copy-done, s32[]{:T(128)S(6)} %select_n.69), kind=kOutput, calls=%fused_computation.6 | convolution fusion | flops 201523200 | bytes 2621444 | tf_op jit(solution)/shard_map/lrj,jt->lrt/dot_general | solution.py:98
  15.5 0.8 %slice_add_fusion.2 = f32[128,128]{1,0:T(8,128)S(1)} fusion(f32[128,128]{1,0:T(8,128)S(1)} %fusion.75, f32[1024,128]{1,0:T(8,128)} %collective-permute-done), kind=kLoop, calls=%fused_computation.161 | loop fusion | flops 16384 | bytes 196608 | tf_op jit(solution)/shard_map/add | solution.py:77
  16.4 0.9 %slice_add_fusion = f32[256,128]{1,0:T(8,128)S(1)} fusion(f32[256,128]{1,0:T(8,128)S(1)} %fusion.79, f32[1024,128]{1,0:T(8,128)} %collective-permute-done), kind=kLoop, calls=%fused_computation.100 | loop fusion | flops 32768 | bytes 393216 | tf_op jit(solution)/shard_map/add | solution.py:77
  17.4 1.6 %collective-permute-start.2 = (f32[640,128]{1,0:T(8,128)S(1)}, f32[640,128]{1,0:T(8,128)S(1)}, u32[]{:S(2)}, u32[]{:S(2)}) collective-permute-start(f32[640,128]{1,0:T(8,128)S(1)} %pad_maximum_fusion.2), channel_id=1, source_target_pairs={{0,2},{2,0},{1,3},{3,1},{4,6},{6,4},{5,7},{7,5},{8,10},{10,8},{9,1... | collective-permute-start | bytes 983048 | tf_op jit(solution)/shard_map/ppermute | solution.py:21
  18.9 0.9 %fusion.123 = (bf16[128,128]{1,0:T(8,128)(2,1)S(1)}, bf16[128,128]{1,0:T(8,128)(2,1)S(1)}) fusion(f32[1024,128]{1,0:T(8,128)} %collective-permute-done), kind=kLoop, calls=%fused_computation.197 | loop fusion | bytes 131072 | tf_op jit(solution)/shard_map/slice | solution.py:68
  19.8 0.8 %fusion.99 = (bf16[256,128]{1,0:T(8,128)(2,1)S(1)}, bf16[256,128]{1,0:T(8,128)(2,1)S(1)}) fusion(bf16[128,128]{1,0:T(8,128)(2,1)S(1)} %get-tuple-element.8, bf16[128,128]{1,0:T(8,128)(2,1)} %copy-done.12, bf16[128,128]{1,0:T(8,128)(2,1)S(1)} %get-tuple-element.7, bf16[128,128]{1,0:T(8,128)(2,1)} %copy-done.11, pred[]{:T(512)S(6)} %eq.12), kind=kLoop, calls=%fused_computation.151 | loop fusion | flops 327680 | bytes 262145 | tf_op jit(solution)/shard_map/jit(_where)/select_n | solution.py:86
  20.6 1.3 %convolution_convert_fusion = bf16[256,1024]{1,0:T(8,128)(2,1)S(1)} fusion(bf16[128,1024]{1,0:T(8,128)(2,1)} %collective-permute-done.1, bf16[128,1024]{1,0:T(8,128)(2,1)} %fusion.3, bf16[256,128]{1,0:T(8,128)(2,1)S(1)} %get-tuple-element.32, bf16[256,128]{1,0:T(8,128)(2,1)S(1)} %get-tuple-element.31), kind=kOutput, calls=%fused_computation.5 | convolution fusion | flops 135528448 | bytes 1179648 | tf_op jit(solution)/shard_map/dot_general | solution.py:137
  22.5 1.4 %convolution_add_fusion.2 = f32[384,512]{1,0:T(8,128)S(1)} fusion(f32[384,512]{1,0:T(8,128)S(1)} %fusion.60, f32[1024,128]{1,0:T(8,128)} %collective-permute-done, bf16[256,1024]{1,0:T(8,128)(2,1)S(1)} %convolution_convert_fusion, s32[]{:T(128)S(6)} %add.75, s32[]{:T(128)S(6)} %select_n.68), kind=kOutput, calls=%fused_computation.10 | convolution fusion | flops 302186496 | bytes 1900552 | tf_op jit(solution)/shard_map/dot_general | solution.py:149
  23.9 1.5 %fusion.2 = f32[3,128,512]{2,1,0:T(8,128)S(1)} fusion(f32[3,128,512]{2,1,0:T(8,128)S(1)} %bitcast.126, f32[3,128,512]{2,1,0:T(8,128)} %collective-permute-done.3, f32[3,128,512]{2,1,0:T(8,128)S(1)} %fusion.19, bf16[4,128,512]{2,1,0:T(8,128)(2,1)S(1)} %get-tuple-element.5, bf16[512,1024]{1,0:T(8,128)(2,1)S(1)} %copy-done, s32[]{:T(128)S(6)} %select_n.68), kind=kOutput, calls=%fused_computation.9 | convolution fusion | flops 201916416 | bytes 4194308 | tf_op jit(solution)/shard_map/lrj,jt->lrt/dot_general | solution.py:98
  26.2 1.3 %collective-permute-done.2 = f32[640,128]{1,0:T(8,128)S(1)} collective-permute-done((f32[640,128]{1,0:T(8,128)S(1)}, f32[640,128]{1,0:T(8,128)S(1)}, u32[]{:S(2)}, u32[]{:S(2)}) %collective-permute-start.2) | collective-permute-done | bytes 327712 | tf_op jit(solution)/shard_map/ppermute | solution.py:21
  27.6 1.7 %collective-permute-start.5 = (f32[384,128]{1,0:T(8,128)S(1)}, f32[384,128]{1,0:T(8,128)S(1)}, u32[]{:S(2)}, u32[]{:S(2)}) collective-permute-start(f32[384,128]{1,0:T(8,128)S(1)} %pad_maximum_fusion.4), channel_id=1, source_target_pairs={{0,4},{4,0},{8,12},{12,8},{1,5},{5,1},{9,13},{13,9},{2,6},{6,2},{1... | collective-permute-start | bytes 589832 | tf_op jit(solution)/shard_map/ppermute | solution.py:21
  29.3 4.8 %collective-permute-done.4 = bf16[512,256]{1,0:T(8,128)(2,1)S(1)} collective-permute-done((bf16[512,256]{1,0:T(8,128)(2,1)S(1)}, bf16[512,256]{1,0:T(8,128)(2,1)S(1)}, u32[]{:S(2)}, u32[]{:S(2)}) %collective-permute-start.4) | collective-permute-done | bytes 262176 | tf_op jit(solution)/shard_map/ppermute | solution.py:21
  35.0 1.6 %collective-permute-start.6 = (bf16[512,128]{1,0:T(8,128)(2,1)S(1)}, bf16[512,128]{1,0:T(8,128)(2,1)S(1)}, u32[]{:S(2)}, u32[]{:S(2)}) collective-permute-start(bf16[512,128]{1,0:T(8,128)(2,1)S(1)} %pad_maximum_fusion.11), channel_id=1, source_target_pairs={{0,4},{4,0},{8,12},{12,8},{1,5},{5,1},{9,13},{13,9},{2,6},{6,2},{1... | collective-permute-start | bytes 393224 | tf_op jit(solution)/shard_map/ppermute | solution.py:21
  36.7 3.3 %collective-permute-done.6 = bf16[512,128]{1,0:T(8,128)(2,1)S(1)} collective-permute-done((bf16[512,128]{1,0:T(8,128)(2,1)S(1)}, bf16[512,128]{1,0:T(8,128)(2,1)S(1)}, u32[]{:S(2)}, u32[]{:S(2)}) %collective-permute-start.6) | collective-permute-done | bytes 131104 | tf_op jit(solution)/shard_map/ppermute | solution.py:21
  41.3 4.8 %collective-permute-done.8 = bf16[256,128]{1,0:T(8,128)(2,1)S(1)} collective-permute-done((bf16[256,128]{1,0:T(8,128)(2,1)S(1)}, bf16[256,128]{1,0:T(8,128)(2,1)S(1)}, u32[]{:S(2)}, u32[]{:S(2)}) %collective-permute-start.8) | collective-permute-done | bytes 65568 | tf_op jit(solution)/shard_map/ppermute | solution.py:21
  47.1 4.3 %collective-permute-done.9 = bf16[2,128,256]{1,2,0:T(8,128)(2,1)S(1)} collective-permute-done((bf16[2,128,256]{1,2,0:T(8,128)(2,1)S(1)}, bf16[2,128,256]{1,2,0:T(8,128)(2,1)S(1)}, u32[]{:S(2)}, u32[]{:S(2)}) %collective-permute-start.9) | collective-permute-done | bytes 131104 | tf_op jit(solution)/shard_map/ppermute | solution.py:21
  52.6 1.3 %collective-permute-done.10 = bf16[3,128,512]{1,2,0:T(8,128)(2,1)S(1)} collective-permute-done((bf16[3,128,512]{1,2,0:T(8,128)(2,1)S(1)}, bf16[3,128,512]{1,2,0:T(8,128)(2,1)S(1)}, u32[]{:S(2)}, u32[]{:S(2)}) %collective-permute-start.10) | collective-permute-done | bytes 393248 | tf_op jit(solution)/shard_map/ppermute | solution.py:21
  53.8 1.2 %fusion.10 = bf16[3,128,1024]{1,2,0:T(8,128)(2,1)S(1)} fusion(s32[]{:T(128)S(6)} %select_n.79, bf16[1,128,512]{1,2,0:T(8,128)(2,1)S(1)} %copy.16, bf16[2,128,512]{1,2,0:T(8,128)(2,1)S(1)} %fusion.29, bf16[3,128,512]{1,2,0:T(8,128)(2,1)S(1)} %collective-permute-done.10), kind=kLoop, calls=%fused_computation.29 | loop fusion | flops 3932160 | bytes 1572868 | tf_op jit(solution)/shard_map/concatenate | solution.py:44
  56.5 1.8 %fusion = bf16[512,1024]{1,0:T(8,128)(2,1)} fusion(f32[1024,512]{0,1:T(8,128)S(1)} %fusion.31, f32[1024,512]{0,1:T(8,128)S(1)} %fusion.32, f32[1024,512]{0,1:T(8,128)S(1)} %fusion.33, f32[1024,512]{0,1:T(8,128)S(1)} %fusion.34, bf16[512,512]{1,0:T(8,128)(2,1)S(1)} %copy-done.2, bf16[512,1024]{1,0:T(8,128)(2,1)S(1)} %copy-done), kind=kOutput, calls=%fused_computation.1 | convolution fusion | flops 539492352 | bytes 11010048 | tf_op jit(solution)/shard_map/dot_general | solution.py:52
  (104 shorter events, 12.5 us)
Async XLA Ops:
  0.0 10.0 %copy-start = (bf16[512,1024]{1,0:T(8,128)(2,1)S(1)}, bf16[512,1024]{1,0:T(8,128)(2,1)}, u32[]{:S(2)}) copy-start(bf16[512,1024]{1,0:T(8,128)(2,1)} %param.5) | copy-start | bytes 3145732
  0.0 5.9 %copy-start.1 = (bf16[4,512,128]{2,1,0:T(8,128)(2,1)S(1)}, bf16[4,512,128]{2,1,0:T(8,128)(2,1)}, u32[]{:S(2)}) copy-start(bf16[4,512,128]{2,1,0:T(8,128)(2,1)} %param.7) | copy-start | bytes 1572868
  0.0 6.1 %slice-start = ((bf16[4,512,128]{2,1,0:T(8,128)(2,1)}), bf16[2,512,128]{2,1,0:T(8,128)(2,1)S(1)}, s32[]{:S(2)}) async-start(bf16[4,512,128]{2,1,0:T(8,128)(2,1)} %param.7), calls=%async_computation | async-start | bytes 524288 | tf_op jit(solution)/shard_map/slice | solution.py:57
  0.0 6.5 %slice-start.1 = ((bf16[4,512,128]{2,1,0:T(8,128)(2,1)}), bf16[3,512,128]{2,1,0:T(8,128)(2,1)S(1)}, s32[]{:S(2)}) async-start(bf16[4,512,128]{2,1,0:T(8,128)(2,1)} %param.7), calls=%async_computation.1 | async-start | bytes 786432 | tf_op jit(solution)/shard_map/slice | solution.py:57
  0.0 5.9 %copy-start.3 = (bf16[4,512,128]{2,1,0:T(8,128)(2,1)S(1)}, bf16[4,512,128]{2,1,0:T(8,128)(2,1)}, u32[]{:S(2)}) copy-start(bf16[4,512,128]{2,1,0:T(8,128)(2,1)} %param.8) | copy-start | bytes 1572868
  1.2 5.1 %copy-start.13 = (bf16[128,128]{1,0:T(8,128)(2,1)}, bf16[128,128]{1,0:T(8,128)(2,1)S(1)}, u32[]{:S(2)}) copy-start(bf16[128,128]{1,0:T(8,128)(2,1)S(1)} %get-tuple-element.39) | copy-start | bytes 98308
  1.2 5.1 %copy-start.14 = (bf16[128,128]{1,0:T(8,128)(2,1)}, bf16[128,128]{1,0:T(8,128)(2,1)S(1)}, u32[]{:S(2)}) copy-start(bf16[128,128]{1,0:T(8,128)(2,1)S(1)} %get-tuple-element.40) | copy-start | bytes 98308
  1.8 12.1 %collective-permute-start.7 = (bf16[256,128]{1,0:T(8,128)(2,1)}, bf16[256,128]{1,0:T(8,128)(2,1)}, u32[]{:S(2)}, u32[]{:S(2)}) collective-permute-start(bf16[256,128]{1,0:T(8,128)(2,1)} %maximum_convert_fusion.3), channel_id=1, source_target_pairs={{0,8},{4,12},{8,0},{12,4},{1,9},{5,13},{9,1},{13,5},{2,10},{6,14},... | collective-permute-start | bytes 196616 | tf_op jit(solution)/shard_map/ppermute | solution.py:21
  7.6 2.7 %copy-start.11 = (bf16[128,128]{1,0:T(8,128)(2,1)}, bf16[128,128]{1,0:T(8,128)(2,1)S(1)}, u32[]{:S(2)}) copy-start(bf16[128,128]{1,0:T(8,128)(2,1)S(1)} %get-tuple-element.53) | copy-start | bytes 98308
  7.6 2.7 %copy-start.12 = (bf16[128,128]{1,0:T(8,128)(2,1)}, bf16[128,128]{1,0:T(8,128)(2,1)S(1)}, u32[]{:S(2)}) copy-start(bf16[128,128]{1,0:T(8,128)(2,1)S(1)} %get-tuple-element.54) | copy-start | bytes 98308
  8.4 7.1 %collective-permute-start = (f32[1024,128]{1,0:T(8,128)}, f32[1024,128]{1,0:T(8,128)}, u32[]{:S(2)}, u32[]{:S(2)}) collective-permute-start(f32[1024,128]{1,0:T(8,128)} %pad_maximum_fusion), channel_id=1, source_target_pairs={{0,1},{1,0},{2,3},{3,2},{4,5},{5,4},{6,7},{7,6},{8,9},{9,8},{10,11... | collective-permute-start | bytes 1572872 | tf_op jit(solution)/shard_map/ppermute | solution.py:21
  11.3 9.3 %collective-permute-start.1 = (bf16[128,1024]{1,0:T(8,128)(2,1)}, bf16[128,1024]{1,0:T(8,128)(2,1)}, u32[]{:S(2)}, u32[]{:S(2)}) collective-permute-start(bf16[128,1024]{1,0:T(8,128)(2,1)} %fusion.3), channel_id=1, source_target_pairs={{0,1},{1,0},{2,3},{3,2},{4,5},{5,4},{6,7},{7,6},{8,9},{9,8},{10,11... | collective-permute-start | bytes 786440 | tf_op jit(solution)/shard_map/ppermute | solution.py:21
  13.5 10.4 %collective-permute-start.3 = (f32[3,128,512]{2,1,0:T(8,128)}, f32[3,128,512]{2,1,0:T(8,128)}, u32[]{:S(2)}, u32[]{:S(2)}) collective-permute-start(f32[3,128,512]{2,1,0:T(8,128)} %convolution_add_fusion), channel_id=1, source_target_pairs={{0,1},{1,0},{2,3},{3,2},{4,5},{5,4},{6,7},{7,6},{8,9},{9,8},{10,11... | collective-permute-start | bytes 2359304 | tf_op jit(solution)/shard_map/ppermute | solution.py:21
  17.4 10.2 %collective-permute-start.2 = (f32[640,128]{1,0:T(8,128)S(1)}, f32[640,128]{1,0:T(8,128)S(1)}, u32[]{:S(2)}, u32[]{:S(2)}) collective-permute-start(f32[640,128]{1,0:T(8,128)S(1)} %pad_maximum_fusion.2), channel_id=1, source_target_pairs={{0,2},{2,0},{1,3},{3,1},{4,6},{6,4},{5,7},{7,5},{8,10},{10,8},{9,1... | collective-permute-start | bytes 983048 | tf_op jit(solution)/shard_map/ppermute | solution.py:21
  25.4 3.8 %copy-start.8 = (bf16[128,128]{1,0:T(8,128)(2,1)S(1)}, bf16[128,128]{1,0:T(8,128)(2,1)}, u32[]{:S(2)}) copy-start(bf16[128,128]{1,0:T(8,128)(2,1)} %get-tuple-element.65) | copy-start | bytes 98308
  25.4 3.8 %copy-start.10 = (bf16[128,128]{1,0:T(8,128)(2,1)S(1)}, bf16[128,128]{1,0:T(8,128)(2,1)}, u32[]{:S(2)}) copy-start(bf16[128,128]{1,0:T(8,128)(2,1)} %get-tuple-element.66) | copy-start | bytes 98308
  25.6 8.5 %collective-permute-start.4 = (bf16[512,256]{1,0:T(8,128)(2,1)S(1)}, bf16[512,256]{1,0:T(8,128)(2,1)S(1)}, u32[]{:S(2)}, u32[]{:S(2)}) collective-permute-start(bf16[512,256]{1,0:T(8,128)(2,1)S(1)} %pad_maximum_fusion.3), channel_id=1, source_target_pairs={{0,2},{2,0},{1,3},{3,1},{4,6},{6,4},{5,7},{7,5},{8,10},{10,8},{9,1... | collective-permute-start | bytes 786440 | tf_op jit(solution)/shard_map/ppermute | solution.py:21
  27.6 9.1 %collective-permute-start.5 = (f32[384,128]{1,0:T(8,128)S(1)}, f32[384,128]{1,0:T(8,128)S(1)}, u32[]{:S(2)}, u32[]{:S(2)}) collective-permute-start(f32[384,128]{1,0:T(8,128)S(1)} %pad_maximum_fusion.4), channel_id=1, source_target_pairs={{0,4},{4,0},{8,12},{12,8},{1,5},{5,1},{9,13},{13,9},{2,6},{6,2},{1... | collective-permute-start | bytes 589832 | tf_op jit(solution)/shard_map/ppermute | solution.py:21
  35.0 5.0 %collective-permute-start.6 = (bf16[512,128]{1,0:T(8,128)(2,1)S(1)}, bf16[512,128]{1,0:T(8,128)(2,1)S(1)}, u32[]{:S(2)}, u32[]{:S(2)}) collective-permute-start(bf16[512,128]{1,0:T(8,128)(2,1)S(1)} %pad_maximum_fusion.11), channel_id=1, source_target_pairs={{0,4},{4,0},{8,12},{12,8},{1,5},{5,1},{9,13},{13,9},{2,6},{6,2},{1... | collective-permute-start | bytes 393224 | tf_op jit(solution)/shard_map/ppermute | solution.py:21
  40.3 11.8 %copy-start.4 = (bf16[4,512,128]{2,1,0:T(8,128)(2,1)S(1)}, bf16[4,512,128]{2,1,0:T(8,128)(2,1)}, u32[]{:S(2)}) copy-start(bf16[4,512,128]{2,1,0:T(8,128)(2,1)} %param.8) | copy-start | bytes 1572868
  40.3 11.8 %copy-start.6 = (bf16[256,1024]{1,0:T(8,128)(2,1)S(1)}, bf16[256,1024]{1,0:T(8,128)(2,1)}, u32[]{:S(2)}) copy-start(bf16[256,1024]{1,0:T(8,128)(2,1)} %copy-done.5) | copy-start | bytes 1572868
  40.8 5.2 %collective-permute-start.8 = (bf16[256,128]{1,0:T(8,128)(2,1)S(1)}, bf16[256,128]{1,0:T(8,128)(2,1)S(1)}, u32[]{:S(2)}, u32[]{:S(2)}) collective-permute-start(bf16[256,128]{1,0:T(8,128)(2,1)S(1)} %pad_maximum_fusion.15), channel_id=1, source_target_pairs={{0,8},{4,12},{8,0},{12,4},{1,9},{5,13},{9,1},{13,5},{2,10},{6,14},... | collective-permute-start | bytes 196616 | tf_op jit(solution)/shard_map/ppermute | solution.py:21
  46.4 5.0 %collective-permute-start.9 = (bf16[2,128,256]{1,2,0:T(8,128)(2,1)S(1)}, bf16[2,128,256]{1,2,0:T(8,128)(2,1)S(1)}, u32[]{:S(2)}, u32[]{:S(2)}) collective-permute-start(bf16[2,128,256]{1,2,0:T(8,128)(2,1)S(1)} %pad_maximum_fusion.14), channel_id=1, source_target_pairs={{0,2},{2,0},{1,3},{3,1},{4,6},{6,4},{5,7},{7,5},{8,10},{10,8},{9,1... | collective-permute-start | bytes 393224 | tf_op jit(solution)/shard_map/ppermute | solution.py:21
  52.0 1.8 %collective-permute-start.10 = (bf16[3,128,512]{1,2,0:T(8,128)(2,1)S(1)}, bf16[3,128,512]{1,2,0:T(8,128)(2,1)S(1)}, u32[]{:S(2)}, u32[]{:S(2)}) collective-permute-start(bf16[3,128,512]{1,2,0:T(8,128)(2,1)S(1)} %pad_maximum_fusion.1), channel_id=1, source_target_pairs={{0,1},{1,0},{2,3},{3,2},{4,5},{5,4},{6,7},{7,6},{8,9},{9,8},{10,11... | collective-permute-start | bytes 1179656 | tf_op jit(solution)/shard_map/ppermute | solution.py:21
  (4 other events, 6.4 us)

commit v25 on v23

--- a/solution.py
+++ b/solution.py
@@ -75,18 +75,10 @@
                 w_own[s] = jnp.concatenate([partial[s], recv], axis=1)
             else:
                 partial[s] = partial[s] + recv
-    couple = []
-    for s in range(levels):
-        lower = side(s, bits) == 0
-        mine, theirs = mine_c[s], theirs_c[s]
-        first = jnp.concatenate([mine[:, :rank], theirs[:, :rank]], axis=0)
-        second = jnp.concatenate([mine[:, rank:], theirs[:, rank:]], axis=0)
-        couple.append(
-            jnp.concatenate(
-                [jnp.where(lower, first, second), jnp.where(lower, second, first)],
-                axis=1,
-            )
-        )
+    couple = [
+        jnp.concatenate([mine_c[s].astype(F32), theirs_c[s]], axis=0)
+        for s in range(levels)
+    ]
 
     vl = jnp.einsum("lir,ij->lrj", v_basis, leaf_inverse, preferred_element_type=F32)
     vl_hi = vl.astype(BF16)
@@ -133,7 +125,12 @@
             elif n > 0:
                 recv = got[2 * rank :].reshape(n, rank, w).astype(F32)
                 rest = keep + recv
-        stacked = jnp.concatenate([mine_b, theirs_b], axis=0)
+        lower = side(s, bits) == 0
+        stacked = jnp.where(
+            lower,
+            jnp.concatenate([mine_b, theirs_b], axis=0),
+            jnp.concatenate([theirs_b, mine_b], axis=0),
+        )
         coefs = jnp.dot(couple[s], stacked, preferred_element_type=F32).astype(BF16)
         own_coefs.append(coefs[:rank])
         if s < levels - 1:

time: 56.1 us -> 56.9 us (1.014)
  local copies, waits for them, and re-layouts: 4.95 us -> 5.6 us
    convert_element_type x0 -> x1, local copies, waits for them, and re-layouts: none -> 1.12 us  [on_device(): mine_c[s].astype(F32)]
    squeeze x1 -> x0, local copies, waits for them, and re-layouts: 1.12 us -> none  [on_device(): mine, theirs = (mine_c[s], theirs_c[s])]
    slice x2, local copies, waits for them, and re-layouts: 0.05 us -> 0.7 us  [on_device(): parts = [jnp.concatenate([c[:, :rank], c[:, rank:]], axis=0).astype(F32)]]
where the time goes in v25:
time: 56.9 us; the launch traced here: 56.5 us
  waiting for transfers between devices  19 us (33%)
  matrix products  13.9 us (24%)
  starting transfers between devices  12 us (21%)
  local copies, waits for them, and re-layouts  5.6 us (10%)
  other arithmetic  5.26 us (9%)
  between operations  0.66 us (1%)
    ppermute x11, waiting for transfers between devices, swap(): return lax.ppermute(x, axis, [(i, i ^ 1 << stride) for i in range(n)])  19 us
    ppermute x11, starting transfers between devices, swap(): return lax.ppermute(x, axis, [(i, i ^ 1 << stride) for i in range(n)])  12 us
    dot_general x3, matrix products, project(): jnp.einsum('lrj,jt->lrt', vl_lo[lv], x, preferred_element_type=F32)  3.78 us
    dot_general x4, matrix products, on_device(): coefs = jnp.dot(couple[s], stacked, preferred_element_type=F32).astype(BF16)  2.29 us
    dot_general x1, matrix products, on_device(): c0 = jnp.dot(leaf_inverse, templates, preferred_element_type=F32)  1.83 us
    concatenate x2, other arithmetic, gather_half(): both = jnp.concatenate([x, swap(x, bit, bits), x], axis=-1)  1.79 us
    add x3, other arithmetic, on_device(): partial[s] = partial[s] + recv  1.78 us
    dot_general x4, matrix products, on_device(): current = current - jnp.dot(u_basis[s], full[s], preferred_element_type=F32)  1.73 us
  transfers between devices with their start and end apart: 11, of which 6 were waited for; matrix products, arithmetic and copies ran while one was open for 29% of the time, Pallas kernels for 0%

profile of v25, /device:TPU:0, one launch (start us, length us, event | category | flops | bytes accessed | tf_op | source)
XLA Modules:
  0.0 56.5 jit_solution(10217011421942609217)
XLA Ops:
  0.0 1.1 %fusion.147 = (bf16[128,256]{1,0:T(8,128)(2,1)S(1)}, bf16[128,256]{1,0:T(8,128)(2,1)S(1)}, bf16[128,256]{1,0:T(8,128)(2,1)S(1)}, bf16[128,256]{1,0:T(8,128)(2,1)S(1)}) fusion(bf16[4,1,128,256]{3,2,1,0:T(8,128)(2,1)} %param.9), kind=kLoop, calls=%fused_computation.207 | loop fusion | bytes 524288 | tf_op jit(solution)/shard_map/convert_element_type | solution.py:79
  2.5 4.0 %collective-permute-start.7 = (bf16[256,128]{1,0:T(8,128)(2,1)}, bf16[256,128]{1,0:T(8,128)(2,1)}, u32[]{:S(2)}, u32[]{:S(2)}) collective-permute-start(bf16[256,128]{1,0:T(8,128)(2,1)} %maximum_convert_fusion.3), channel_id=1, source_target_pairs={{0,8},{4,12},{8,0},{12,4},{1,9},{5,13},{9,1},{13,5},{2,10},{6,14},... | collective-permute-start | bytes 196616 | tf_op jit(solution)/shard_map/ppermute | solution.py:21
  7.7 0.8 %pad_maximum_fusion = f32[1024,128]{1,0:T(8,128)} fusion(f32[128,128]{1,0:T(8,128)S(1)} %fusion.104, f32[256,128]{1,0:T(8,128)S(1)} %fusion.108, f32[384,128]{1,0:T(8,128)S(1)} %fusion.111, f32[256,128]{1,0:T(8,128)S(1)} %maximum_convert_fusion), kind=kLoop, calls=%fused_computation.28 | loop fusion | flops 393216 | bytes 1048576 | tf_op jit(solution)/shard_map/concatenate | solution.py:66
  8.5 1.5 %subtract_convert_fusion = (bf16[4,128,512]{2,1,0:T(8,128)(2,1)S(1)}, bf16[4,128,512]{2,1,0:T(8,128)(2,1)S(1)}) fusion(bf16[4,512,128]{2,1,0:T(8,128)(2,1)S(1)} %copy-done.1, bf16[512,512]{1,0:T(8,128)(2,1)} %param.6), kind=kOutput, calls=%fused_computation.23 | convolution fusion | flops 269484032 | bytes 2097152 | tf_op jit(solution)/shard_map/lir,ij->lrj/dot_general | solution.py:83
  10.4 1.0 %fusion.3 = bf16[128,1024]{1,0:T(8,128)(2,1)} fusion(f32[128,1024]{1,0:T(8,128)S(1)} %fusion.80, bf16[512,1024]{1,0:T(8,128)(2,1)S(1)} %copy-done, bf16[4,128,512]{2,1,0:T(8,128)(2,1)S(1)} %get-tuple-element.5), kind=kOutput, calls=%fused_computation.11 | convolution fusion | flops 134479872 | bytes 1966080 | tf_op jit(solution)/shard_map/lrj,jt->lrt/dot_general | solution.py:90
  12.3 1.3 %convolution_add_fusion = f32[3,128,512]{2,1,0:T(8,128)} fusion(f32[3,128,512]{2,1,0:T(8,128)S(1)} %fusion.17, bf16[4,128,512]{2,1,0:T(8,128)(2,1)S(1)} %get-tuple-element.5, bf16[512,1024]{1,0:T(8,128)(2,1)S(1)} %copy-done, s32[]{:T(128)S(6)} %select_n.54), kind=kOutput, calls=%fused_computation.6 | convolution fusion | flops 201523200 | bytes 2621444 | tf_op jit(solution)/shard_map/lrj,jt->lrt/dot_general | solution.py:90
  14.8 0.9 %slice_add_fusion = f32[256,128]{1,0:T(8,128)S(1)} fusion(f32[256,128]{1,0:T(8,128)S(1)} %fusion.108, f32[1024,128]{1,0:T(8,128)} %collective-permute-done), kind=kLoop, calls=%fused_computation.118 | loop fusion | flops 32768 | bytes 393216 | tf_op jit(solution)/shard_map/add | solution.py:77
  15.7 0.8 %slice_add_fusion.2 = f32[128,128]{1,0:T(8,128)S(1)} fusion(f32[128,128]{1,0:T(8,128)S(1)} %fusion.104, f32[1024,128]{1,0:T(8,128)} %collective-permute-done), kind=kLoop, calls=%fused_computation.175 | loop fusion | flops 16384 | bytes 196608 | tf_op jit(solution)/shard_map/add | solution.py:77
  16.6 1.6 %collective-permute-start.2 = (f32[640,128]{1,0:T(8,128)S(1)}, f32[640,128]{1,0:T(8,128)S(1)}, u32[]{:S(2)}, u32[]{:S(2)}) collective-permute-start(f32[640,128]{1,0:T(8,128)S(1)} %pad_maximum_fusion.2), channel_id=1, source_target_pairs={{0,2},{2,0},{1,3},{3,1},{4,6},{6,4},{5,7},{7,5},{8,10},{10,8},{9,1... | collective-permute-start | bytes 983048 | tf_op jit(solution)/shard_map/ppermute | solution.py:21
  18.1 0.9 %slice.300 = f32[384,128]{1,0:T(8,128)S(1)} slice(f32[1024,128]{1,0:T(8,128)} %collective-permute-done), slice={[256:640], [0:128]} | slice | bytes 393216 | tf_op jit(solution)/shard_map/slice | solution.py:72
  19.1 0.9 %fusion.148 = (bf16[128,128]{1,0:T(8,128)(2,1)S(1)}, bf16[128,128]{1,0:T(8,128)(2,1)S(1)}) fusion(f32[1024,128]{1,0:T(8,128)} %collective-permute-done), kind=kLoop, calls=%fused_computation.208 | loop fusion | bytes 131072 | tf_op jit(solution)/shard_map/slice | solution.py:68
  20.0 1.6 %convolution_convert_fusion = bf16[256,1024]{1,0:T(8,128)(2,1)S(1)} fusion(bf16[128,1024]{1,0:T(8,128)(2,1)} %collective-permute-done.1, bf16[128,1024]{1,0:T(8,128)(2,1)} %fusion.3, pred[]{:T(512)S(6)} %eq.12, bf16[128,128]{1,0:T(8,128)(2,1)S(1)} %get-tuple-element.8, bf16[128,128]{1,0:T(8,128)(2,1)S(1)} %get-tuple-element.7, ...), kind=kOutput, calls=%fused_computation.5 | convolution fusion | flops 136970240 | bytes 1179649 | tf_op jit(solution)/shard_map/dot_general | solution.py:134
  22.4 1.5 %fusion.2 = f32[3,128,512]{2,1,0:T(8,128)S(1)} fusion(f32[3,128,512]{2,1,0:T(8,128)S(1)} %bitcast.132, f32[3,128,512]{2,1,0:T(8,128)} %collective-permute-done.3, f32[3,128,512]{2,1,0:T(8,128)S(1)} %fusion.20, bf16[4,128,512]{2,1,0:T(8,128)(2,1)S(1)} %get-tuple-element.5, bf16[512,1024]{1,0:T(8,128)(2,1)S(1)} %copy-done, s32[]{:T(128)S(6)} %select_n.53), kind=kOutput, calls=%fused_computation.9 | convolution fusion | flops 201916416 | bytes 4194308 | tf_op jit(solution)/shard_map/lrj,jt->lrt/dot_general | solution.py:90
  24.7 2.1 %collective-permute-done.2 = f32[640,128]{1,0:T(8,128)S(1)} collective-permute-done((f32[640,128]{1,0:T(8,128)S(1)}, f32[640,128]{1,0:T(8,128)S(1)}, u32[]{:S(2)}, u32[]{:S(2)}) %collective-permute-start.2) | collective-permute-done | bytes 327712 | tf_op jit(solution)/shard_map/ppermute | solution.py:21
  26.8 1.6 %collective-permute-start.5 = (f32[384,128]{1,0:T(8,128)S(1)}, f32[384,128]{1,0:T(8,128)S(1)}, u32[]{:S(2)}, u32[]{:S(2)}) collective-permute-start(f32[384,128]{1,0:T(8,128)S(1)} %pad_maximum_fusion.4), channel_id=1, source_target_pairs={{0,4},{4,0},{8,12},{12,8},{1,5},{5,1},{9,13},{13,9},{2,6},{6,2},{1... | collective-permute-start | bytes 589832 | tf_op jit(solution)/shard_map/ppermute | solution.py:21
  28.5 4.1 %collective-permute-done.4 = bf16[512,256]{1,0:T(8,128)(2,1)S(1)} collective-permute-done((bf16[512,256]{1,0:T(8,128)(2,1)S(1)}, bf16[512,256]{1,0:T(8,128)(2,1)S(1)}, u32[]{:S(2)}, u32[]{:S(2)}) %collective-permute-start.4) | collective-permute-done | bytes 262176 | tf_op jit(solution)/shard_map/ppermute | solution.py:21
  33.3 1.6 %collective-permute-start.6 = (bf16[512,128]{1,0:T(8,128)(2,1)S(1)}, bf16[512,128]{1,0:T(8,128)(2,1)S(1)}, u32[]{:S(2)}, u32[]{:S(2)}) collective-permute-start(bf16[512,128]{1,0:T(8,128)(2,1)S(1)} %pad_maximum_fusion.5), channel_id=1, source_target_pairs={{0,4},{4,0},{8,12},{12,8},{1,5},{5,1},{9,13},{13,9},{2,6},{6,2},{1... | collective-permute-start | bytes 393224 | tf_op jit(solution)/shard_map/ppermute | solution.py:21
  35.0 3.4 %collective-permute-done.6 = bf16[512,128]{1,0:T(8,128)(2,1)S(1)} collective-permute-done((bf16[512,128]{1,0:T(8,128)(2,1)S(1)}, bf16[512,128]{1,0:T(8,128)(2,1)S(1)}, u32[]{:S(2)}, u32[]{:S(2)}) %collective-permute-start.6) | collective-permute-done | bytes 131104 | tf_op jit(solution)/shard_map/ppermute | solution.py:21
  39.4 4.8 %collective-permute-done.8 = bf16[256,128]{1,0:T(8,128)(2,1)S(1)} collective-permute-done((bf16[256,128]{1,0:T(8,128)(2,1)S(1)}, bf16[256,128]{1,0:T(8,128)(2,1)S(1)}, u32[]{:S(2)}, u32[]{:S(2)}) %collective-permute-start.8) | collective-permute-done | bytes 65568 | tf_op jit(solution)/shard_map/ppermute | solution.py:21
  44.5 1.5 %collective-permute-start.9 = (bf16[2,128,256]{1,2,0:T(8,128)(2,1)S(1)}, bf16[2,128,256]{1,2,0:T(8,128)(2,1)S(1)}, u32[]{:S(2)}, u32[]{:S(2)}) collective-permute-start(bf16[2,128,256]{1,2,0:T(8,128)(2,1)S(1)} %pad_maximum_fusion.6), channel_id=1, source_target_pairs={{0,2},{2,0},{1,3},{3,1},{4,6},{6,4},{5,7},{7,5},{8,10},{10,8},{9,1... | collective-permute-start | bytes 393224 | tf_op jit(solution)/shard_map/ppermute | solution.py:21
  46.2 3.4 %collective-permute-done.9 = bf16[2,128,256]{1,2,0:T(8,128)(2,1)S(1)} collective-permute-done((bf16[2,128,256]{1,2,0:T(8,128)(2,1)S(1)}, bf16[2,128,256]{1,2,0:T(8,128)(2,1)S(1)}, u32[]{:S(2)}, u32[]{:S(2)}) %collective-permute-start.9) | collective-permute-done | bytes 131104 | tf_op jit(solution)/shard_map/ppermute | solution.py:21
  50.7 1.3 %collective-permute-done.10 = bf16[3,128,512]{1,2,0:T(8,128)(2,1)S(1)} collective-permute-done((bf16[3,128,512]{1,2,0:T(8,128)(2,1)S(1)}, bf16[3,128,512]{1,2,0:T(8,128)(2,1)S(1)}, u32[]{:S(2)}, u32[]{:S(2)}) %collective-permute-start.10) | collective-permute-done | bytes 393248 | tf_op jit(solution)/shard_map/ppermute | solution.py:21
  51.9 1.2 %fusion.9 = bf16[3,128,1024]{1,2,0:T(8,128)(2,1)S(1)} fusion(s32[]{:T(128)S(6)} %select_n.63, bf16[1,128,512]{1,2,0:T(8,128)(2,1)S(1)} %copy.16, bf16[2,128,512]{1,2,0:T(8,128)(2,1)S(1)} %fusion.35, bf16[3,128,512]{1,2,0:T(8,128)(2,1)S(1)} %collective-permute-done.10), kind=kLoop, calls=%fused_computation.26 | loop fusion | flops 3932160 | bytes 1572868 | tf_op jit(solution)/shard_map/concatenate | solution.py:44
  54.6 1.8 %fusion = bf16[512,1024]{1,0:T(8,128)(2,1)} fusion(f32[1024,512]{0,1:T(8,128)S(1)} %fusion.37, f32[1024,512]{0,1:T(8,128)S(1)} %fusion.38, f32[1024,512]{0,1:T(8,128)S(1)} %fusion.39, f32[1024,512]{0,1:T(8,128)S(1)} %fusion.40, bf16[512,512]{1,0:T(8,128)(2,1)S(1)} %copy-done.2, bf16[512,1024]{1,0:T(8,128)(2,1)S(1)} %copy-done), kind=kOutput, calls=%fused_computation.1 | convolution fusion | flops 539492352 | bytes 11010048 | tf_op jit(solution)/shard_map/dot_general | solution.py:52
  (100 shorter events, 10.9 us)
Async XLA Ops:
  0.0 10.0 %copy-start = (bf16[512,1024]{1,0:T(8,128)(2,1)S(1)}, bf16[512,1024]{1,0:T(8,128)(2,1)}, u32[]{:S(2)}) copy-start(bf16[512,1024]{1,0:T(8,128)(2,1)} %param.5) | copy-start | bytes 3145732
  0.0 6.5 %copy-start.1 = (bf16[4,512,128]{2,1,0:T(8,128)(2,1)S(1)}, bf16[4,512,128]{2,1,0:T(8,128)(2,1)}, u32[]{:S(2)}) copy-start(bf16[4,512,128]{2,1,0:T(8,128)(2,1)} %param.7) | copy-start | bytes 1572868
  0.0 6.7 %slice-start = ((bf16[4,512,128]{2,1,0:T(8,128)(2,1)}), bf16[2,512,128]{2,1,0:T(8,128)(2,1)S(1)}, s32[]{:S(2)}) async-start(bf16[4,512,128]{2,1,0:T(8,128)(2,1)} %param.7), calls=%async_computation | async-start | bytes 524288 | tf_op jit(solution)/shard_map/slice | solution.py:57
  0.0 7.1 %slice-start.1 = ((bf16[4,512,128]{2,1,0:T(8,128)(2,1)}), bf16[3,512,128]{2,1,0:T(8,128)(2,1)S(1)}, s32[]{:S(2)}) async-start(bf16[4,512,128]{2,1,0:T(8,128)(2,1)} %param.7), calls=%async_computation.1 | async-start | bytes 786432 | tf_op jit(solution)/shard_map/slice | solution.py:57
  0.0 6.5 %copy-start.3 = (bf16[4,512,128]{2,1,0:T(8,128)(2,1)S(1)}, bf16[4,512,128]{2,1,0:T(8,128)(2,1)}, u32[]{:S(2)}) copy-start(bf16[4,512,128]{2,1,0:T(8,128)(2,1)} %param.8) | copy-start | bytes 1572868
  1.1 5.8 %copy-start.7 = (bf16[128,256]{1,0:T(8,128)(2,1)}, bf16[128,256]{1,0:T(8,128)(2,1)S(1)}, u32[]{:S(2)}) copy-start(bf16[128,256]{1,0:T(8,128)(2,1)S(1)} %get-tuple-element.12) | copy-start | bytes 196612
  1.2 6.4 %copy-start.9 = (bf16[128,256]{1,0:T(8,128)(2,1)}, bf16[128,256]{1,0:T(8,128)(2,1)S(1)}, u32[]{:S(2)}) copy-start(bf16[128,256]{1,0:T(8,128)(2,1)S(1)} %get-tuple-element.13) | copy-start | bytes 196612
  1.2 6.4 %copy-start.11 = (bf16[128,256]{1,0:T(8,128)(2,1)}, bf16[128,256]{1,0:T(8,128)(2,1)S(1)}, u32[]{:S(2)}) copy-start(bf16[128,256]{1,0:T(8,128)(2,1)S(1)} %get-tuple-element.14) | copy-start | bytes 196612
  2.5 11.5 %collective-permute-start.7 = (bf16[256,128]{1,0:T(8,128)(2,1)}, bf16[256,128]{1,0:T(8,128)(2,1)}, u32[]{:S(2)}, u32[]{:S(2)}) collective-permute-start(bf16[256,128]{1,0:T(8,128)(2,1)} %maximum_convert_fusion.3), channel_id=1, source_target_pairs={{0,8},{4,12},{8,0},{12,4},{1,9},{5,13},{9,1},{13,5},{2,10},{6,14},... | collective-permute-start | bytes 196616 | tf_op jit(solution)/shard_map/ppermute | solution.py:21
  8.5 6.3 %collective-permute-start = (f32[1024,128]{1,0:T(8,128)}, f32[1024,128]{1,0:T(8,128)}, u32[]{:S(2)}, u32[]{:S(2)}) collective-permute-start(f32[1024,128]{1,0:T(8,128)} %pad_maximum_fusion), channel_id=1, source_target_pairs={{0,1},{1,0},{2,3},{3,2},{4,5},{5,4},{6,7},{7,6},{8,9},{9,8},{10,11... | collective-permute-start | bytes 1572872 | tf_op jit(solution)/shard_map/ppermute | solution.py:21
  11.4 8.6 %collective-permute-start.1 = (bf16[128,1024]{1,0:T(8,128)(2,1)}, bf16[128,1024]{1,0:T(8,128)(2,1)}, u32[]{:S(2)}, u32[]{:S(2)}) collective-permute-start(bf16[128,1024]{1,0:T(8,128)(2,1)} %fusion.3), channel_id=1, source_target_pairs={{0,1},{1,0},{2,3},{3,2},{4,5},{5,4},{6,7},{7,6},{8,9},{9,8},{10,11... | collective-permute-start | bytes 786440 | tf_op jit(solution)/shard_map/ppermute | solution.py:21
  13.5 8.6 %collective-permute-start.3 = (f32[3,128,512]{2,1,0:T(8,128)}, f32[3,128,512]{2,1,0:T(8,128)}, u32[]{:S(2)}, u32[]{:S(2)}) collective-permute-start(f32[3,128,512]{2,1,0:T(8,128)} %convolution_add_fusion), channel_id=1, source_target_pairs={{0,1},{1,0},{2,3},{3,2},{4,5},{5,4},{6,7},{7,6},{8,9},{9,8},{10,11... | collective-permute-start | bytes 2359304 | tf_op jit(solution)/shard_map/ppermute | solution.py:21
  13.5 6.5 %copy-start.12 = (bf16[128,256]{1,0:T(8,128)(2,1)S(1)}, bf16[128,256]{1,0:T(8,128)(2,1)}, u32[]{:S(2)}) copy-start(bf16[128,256]{1,0:T(8,128)(2,1)} %copy-done.11) | copy-start | bytes 196612
  16.6 10.2 %collective-permute-start.2 = (f32[640,128]{1,0:T(8,128)S(1)}, f32[640,128]{1,0:T(8,128)S(1)}, u32[]{:S(2)}, u32[]{:S(2)}) collective-permute-start(f32[640,128]{1,0:T(8,128)S(1)} %pad_maximum_fusion.2), channel_id=1, source_target_pairs={{0,2},{2,0},{1,3},{3,1},{4,6},{6,4},{5,7},{7,5},{8,10},{10,8},{9,1... | collective-permute-start | bytes 983048 | tf_op jit(solution)/shard_map/ppermute | solution.py:21
  23.9 8.7 %copy-start.10 = (bf16[128,256]{1,0:T(8,128)(2,1)S(1)}, bf16[128,256]{1,0:T(8,128)(2,1)}, u32[]{:S(2)}) copy-start(bf16[128,256]{1,0:T(8,128)(2,1)} %copy-done.9) | copy-start | bytes 196612
  24.1 8.5 %collective-permute-start.4 = (bf16[512,256]{1,0:T(8,128)(2,1)S(1)}, bf16[512,256]{1,0:T(8,128)(2,1)S(1)}, u32[]{:S(2)}, u32[]{:S(2)}) collective-permute-start(bf16[512,256]{1,0:T(8,128)(2,1)S(1)} %pad_maximum_fusion.3), channel_id=1, source_target_pairs={{0,2},{2,0},{1,3},{3,1},{4,6},{6,4},{5,7},{7,5},{8,10},{10,8},{9,1... | collective-permute-start | bytes 786440 | tf_op jit(solution)/shard_map/ppermute | solution.py:21
  26.8 8.1 %collective-permute-start.5 = (f32[384,128]{1,0:T(8,128)S(1)}, f32[384,128]{1,0:T(8,128)S(1)}, u32[]{:S(2)}, u32[]{:S(2)}) collective-permute-start(f32[384,128]{1,0:T(8,128)S(1)} %pad_maximum_fusion.4), channel_id=1, source_target_pairs={{0,4},{4,0},{8,12},{12,8},{1,5},{5,1},{9,13},{13,9},{2,6},{6,2},{1... | collective-permute-start | bytes 589832 | tf_op jit(solution)/shard_map/ppermute | solution.py:21
  32.6 5.8 %copy-start.8 = (bf16[128,256]{1,0:T(8,128)(2,1)S(1)}, bf16[128,256]{1,0:T(8,128)(2,1)}, u32[]{:S(2)}) copy-start(bf16[128,256]{1,0:T(8,128)(2,1)} %copy-done.7) | copy-start | bytes 196612
  33.3 5.0 %collective-permute-start.6 = (bf16[512,128]{1,0:T(8,128)(2,1)S(1)}, bf16[512,128]{1,0:T(8,128)(2,1)S(1)}, u32[]{:S(2)}, u32[]{:S(2)}) collective-permute-start(bf16[512,128]{1,0:T(8,128)(2,1)S(1)} %pad_maximum_fusion.5), channel_id=1, source_target_pairs={{0,4},{4,0},{8,12},{12,8},{1,5},{5,1},{9,13},{13,9},{2,6},{6,2},{1... | collective-permute-start | bytes 393224 | tf_op jit(solution)/shard_map/ppermute | solution.py:21
  38.6 11.6 %copy-start.4 = (bf16[4,512,128]{2,1,0:T(8,128)(2,1)S(1)}, bf16[4,512,128]{2,1,0:T(8,128)(2,1)}, u32[]{:S(2)}) copy-start(bf16[4,512,128]{2,1,0:T(8,128)(2,1)} %param.8) | copy-start | bytes 1572868
  38.6 11.6 %copy-start.6 = (bf16[256,1024]{1,0:T(8,128)(2,1)S(1)}, bf16[256,1024]{1,0:T(8,128)(2,1)}, u32[]{:S(2)}) copy-start(bf16[256,1024]{1,0:T(8,128)(2,1)} %copy-done.5) | copy-start | bytes 1572868
  39.0 5.2 %collective-permute-start.8 = (bf16[256,128]{1,0:T(8,128)(2,1)S(1)}, bf16[256,128]{1,0:T(8,128)(2,1)S(1)}, u32[]{:S(2)}, u32[]{:S(2)}) collective-permute-start(bf16[256,128]{1,0:T(8,128)(2,1)S(1)} %pad_maximum_fusion.7), channel_id=1, source_target_pairs={{0,8},{4,12},{8,0},{12,4},{1,9},{5,13},{9,1},{13,5},{2,10},{6,14},... | collective-permute-start | bytes 196616 | tf_op jit(solution)/shard_map/ppermute | solution.py:21
  44.5 5.0 %collective-permute-start.9 = (bf16[2,128,256]{1,2,0:T(8,128)(2,1)S(1)}, bf16[2,128,256]{1,2,0:T(8,128)(2,1)S(1)}, u32[]{:S(2)}, u32[]{:S(2)}) collective-permute-start(bf16[2,128,256]{1,2,0:T(8,128)(2,1)S(1)} %pad_maximum_fusion.6), channel_id=1, source_target_pairs={{0,2},{2,0},{1,3},{3,1},{4,6},{6,4},{5,7},{7,5},{8,10},{10,8},{9,1... | collective-permute-start | bytes 393224 | tf_op jit(solution)/shard_map/ppermute | solution.py:21
  50.2 1.8 %collective-permute-start.10 = (bf16[3,128,512]{1,2,0:T(8,128)(2,1)S(1)}, bf16[3,128,512]{1,2,0:T(8,128)(2,1)S(1)}, u32[]{:S(2)}, u32[]{:S(2)}) collective-permute-start(bf16[3,128,512]{1,2,0:T(8,128)(2,1)S(1)} %pad_maximum_fusion.1), channel_id=1, source_target_pairs={{0,1},{1,0},{2,3},{3,2},{4,5},{5,4},{6,7},{7,6},{8,9},{9,8},{10,11... | collective-permute-start | bytes 1179656 | tf_op jit(solution)/shard_map/ppermute | solution.py:21
  (4 other events, 5.3 us)

commit v26 on v23

--- a/solution.py
+++ b/solution.py
@@ -61,6 +61,9 @@
     w_own, theirs_c = [None] * levels, []
     for b in range(levels):
         c = mine_c[b]
+        if b == levels - 1:
+            theirs_c.append(swap(c, b, bits))
+            continue
         parts = [jnp.concatenate([c[:, :rank], c[:, rank:]], axis=0).astype(F32)]
         parts += partial[b:]
         got = swap(jnp.concatenate(parts, axis=0), b, bits)

time: 56.1 us -> 59.5 us (1.061)
  local copies, waits for them, and re-layouts: 4.95 us -> 7.86 us
  matrix products: 13.6 us -> 14.6 us
  other arithmetic: 5.39 us -> 4.77 us
    slice x2 -> x3, local copies, waits for them, and re-layouts: 0.05 us -> 3.04 us  [on_device(): first = jnp.concatenate([mine[:, :rank], theirs[:, :rank]], axis=0)]
    dot_general x3, matrix products: 0.68 us -> 1.66 us  [on_device(): jnp.einsum('lir,is->lrs', v_basis[s + 1:], u_basis[s], preferred_element_...]
    slice x4 -> x3, local copies, waits for them, and re-layouts: 1.69 us -> 0.91 us  [on_device(): theirs_c.append(jnp.concatenate([theirs[:rank], theirs[rank:]], axis=1))]
    squeeze x1, local copies, waits for them, and re-layouts: 1.12 us -> 1.79 us  [on_device(): mine, theirs = (mine_c[s], theirs_c[s])]
    convert_element_type x4 -> x3, other arithmetic: 0.66 us -> 0.03 us  [on_device(): parts = [jnp.concatenate([c[:, :rank], c[:, rank:]], axis=0).astype(F32)]]
  transfers between devices with their start and end apart: 11 -> 11, of which waited for: 6 -> 6; matrix products, arithmetic and copies ran while one was open for 29% -> 33% of each run, Pallas kernels for 0% -> 0%
where the time goes in v26:
time: 59.5 us; the launch traced here: 58.9 us
  waiting for transfers between devices  18.7 us (31%)
  matrix products  14.6 us (25%)
  starting transfers between devices  12.1 us (20%)
  local copies, waits for them, and re-layouts  7.86 us (13%)
  other arithmetic  4.77 us (8%)
  between operations  0.74 us (1%)
    ppermute x11, waiting for transfers between devices, swap(): return lax.ppermute(x, axis, [(i, i ^ 1 << stride) for i in range(n)])  18.7 us
    ppermute x11, starting transfers between devices, swap(): return lax.ppermute(x, axis, [(i, i ^ 1 << stride) for i in range(n)])  12.1 us
    dot_general x3, matrix products, project(): jnp.einsum('lrj,jt->lrt', vl_lo[lv], x, preferred_element_type=F32)  3.79 us
    slice x3, local copies, waits for them, and re-layouts, on_device(): first = jnp.concatenate([mine[:, :rank], theirs[:, :rank]], axis=0)  3.04 us
    dot_general x4, matrix products, on_device(): coefs = jnp.dot(couple[s], stacked, preferred_element_type=F32).astype(BF16)  2.01 us
    dot_general x1, matrix products, on_device(): c0 = jnp.dot(leaf_inverse, templates, preferred_element_type=F32)  1.83 us
    concatenate x2, other arithmetic, gather_half(): both = jnp.concatenate([x, swap(x, bit, bits), x], axis=-1)  1.79 us
    squeeze x1, local copies, waits for them, and re-layouts, on_device(): mine, theirs = (mine_c[s], theirs_c[s])  1.79 us
  transfers between devices with their start and end apart: 11, of which 6 were waited for; matrix products, arithmetic and copies ran while one was open for 33% of the time, Pallas kernels for 0%

profile of v26, /device:TPU:0, one launch (start us, length us, event | category | flops | bytes accessed | tf_op | source)
XLA Modules:
  0.0 58.9 jit_solution(16395869368525121050)
XLA Ops:
  0.0 1.8 %slice_bitcast_fusion.12 = (bf16[128,256]{1,0:T(8,128)(2,1)}, bf16[128,256]{1,0:T(8,128)(2,1)}, bf16[128,256]{1,0:T(8,128)(2,1)}, bf16[128,256]{1,0:T(8,128)(2,1)}) fusion(bf16[4,1,128,256]{3,2,1,0:T(8,128)(2,1)} %param.9), kind=kLoop, calls=%fused_computation.164 | loop fusion | bytes 524288 | tf_op jit(solution)/shard_map/squeeze | solution.py:84
  1.8 4.0 %collective-permute-start.7 = (bf16[128,256]{1,0:T(8,128)(2,1)}, bf16[128,256]{1,0:T(8,128)(2,1)}, u32[]{:S(2)}, u32[]{:S(2)}) collective-permute-start(bf16[128,256]{1,0:T(8,128)(2,1)} %get-tuple-element.11), channel_id=1, source_target_pairs={{0,8},{4,12},{8,0},{12,4},{1,9},{5,13},{9,1},{13,5},{2,10},{6,14},... | collective-permute-start | bytes 196616 | tf_op jit(solution)/shard_map/ppermute | solution.py:21
  5.9 1.2 %fusion.80 = f32[128,128]{1,0:T(8,128)S(1)} fusion(bf16[4,512,128]{2,1,0:T(8,128)(2,1)} %param.7, bf16[4,512,128]{2,1,0:T(8,128)(2,1)} %param.8), kind=kOutput, calls=%fused_computation.127 | convolution fusion | flops 16777216 | bytes 327680 | tf_op jit(solution)/shard_map/lir,is->lrs/dot_general | solution.py:56
  7.9 1.4 %fusion.135 = (bf16[128,128]{1,0:T(8,128)(2,1)S(1)}, bf16[128,128]{1,0:T(8,128)(2,1)S(1)}, bf16[128,128]{1,0:T(8,128)(2,1)}, bf16[128,128]{1,0:T(8,128)(2,1)}) fusion(bf16[128,256]{1,0:T(8,128)(2,1)} %get-tuple-element.13, bf16[128,256]{1,0:T(8,128)(2,1)} %get-tuple-element.12), kind=kLoop, calls=%fused_computation.206 | loop fusion | bytes 262144 | tf_op jit(solution)/shard_map/slice | solution.py:85
  10.2 1.5 %subtract_convert_fusion = (bf16[4,128,512]{2,1,0:T(8,128)(2,1)S(1)}, bf16[4,128,512]{2,1,0:T(8,128)(2,1)S(1)}) fusion(bf16[4,512,128]{2,1,0:T(8,128)(2,1)S(1)} %copy-done.1, bf16[512,512]{1,0:T(8,128)(2,1)} %param.6), kind=kOutput, calls=%fused_computation.23 | convolution fusion | flops 269484032 | bytes 2097152 | tf_op jit(solution)/shard_map/lir,ij->lrj/dot_general | solution.py:94
  12.1 1.0 %fusion.3 = bf16[128,1024]{1,0:T(8,128)(2,1)} fusion(f32[128,1024]{1,0:T(8,128)S(1)} %fusion.60, bf16[512,1024]{1,0:T(8,128)(2,1)S(1)} %copy-done, bf16[4,128,512]{2,1,0:T(8,128)(2,1)S(1)} %get-tuple-element.5), kind=kOutput, calls=%fused_computation.11 | convolution fusion | flops 134479872 | bytes 1966080 | tf_op jit(solution)/shard_map/lrj,jt->lrt/dot_general | solution.py:101
  14.0 1.3 %convolution_add_fusion = f32[3,128,512]{2,1,0:T(8,128)} fusion(f32[3,128,512]{2,1,0:T(8,128)S(1)} %fusion.15, bf16[4,128,512]{2,1,0:T(8,128)(2,1)S(1)} %get-tuple-element.5, bf16[512,1024]{1,0:T(8,128)(2,1)S(1)} %copy-done, s32[]{:T(128)S(6)} %select_n.71), kind=kOutput, calls=%fused_computation.6 | convolution fusion | flops 201523200 | bytes 2621444 | tf_op jit(solution)/shard_map/lrj,jt->lrt/dot_general | solution.py:101
  17.5 0.9 %slice_add_fusion = f32[256,128]{1,0:T(8,128)S(1)} fusion(f32[256,128]{1,0:T(8,128)S(1)} %copy-done.6, f32[1024,128]{1,0:T(8,128)} %collective-permute-done), kind=kLoop, calls=%fused_computation.96 | loop fusion | flops 32768 | bytes 393216 | tf_op jit(solution)/shard_map/add | solution.py:80
  19.3 1.6 %collective-permute-start.2 = (f32[640,128]{1,0:T(8,128)S(1)}, f32[640,128]{1,0:T(8,128)S(1)}, u32[]{:S(2)}, u32[]{:S(2)}) collective-permute-start(f32[640,128]{1,0:T(8,128)S(1)} %pad_maximum_fusion.2), channel_id=1, source_target_pairs={{0,2},{2,0},{1,3},{3,1},{4,6},{6,4},{5,7},{7,5},{8,10},{10,8},{9,1... | collective-permute-start | bytes 983048 | tf_op jit(solution)/shard_map/ppermute | solution.py:21
  20.8 0.9 %slice.306 = f32[384,128]{1,0:T(8,128)S(1)} slice(f32[1024,128]{1,0:T(8,128)} %collective-permute-done), slice={[256:640], [0:128]} | slice | bytes 393216 | tf_op jit(solution)/shard_map/slice | solution.py:75
  21.8 0.9 %fusion.123 = (bf16[128,128]{1,0:T(8,128)(2,1)S(1)}, bf16[128,128]{1,0:T(8,128)(2,1)S(1)}) fusion(f32[1024,128]{1,0:T(8,128)} %collective-permute-done), kind=kLoop, calls=%fused_computation.194 | loop fusion | bytes 131072 | tf_op jit(solution)/shard_map/slice | solution.py:71
  22.7 1.3 %convolution_convert_fusion = bf16[256,1024]{1,0:T(8,128)(2,1)S(1)} fusion(bf16[128,1024]{1,0:T(8,128)(2,1)} %collective-permute-done.1, bf16[128,1024]{1,0:T(8,128)(2,1)} %fusion.3, bf16[256,128]{1,0:T(8,128)(2,1)S(1)} %get-tuple-element.32, bf16[256,128]{1,0:T(8,128)(2,1)S(1)} %get-tuple-element.31), kind=kOutput, calls=%fused_computation.5 | convolution fusion | flops 135528448 | bytes 1179648 | tf_op jit(solution)/shard_map/dot_general | solution.py:140
  24.9 1.5 %fusion.2 = f32[3,128,512]{2,1,0:T(8,128)S(1)} fusion(f32[3,128,512]{2,1,0:T(8,128)S(1)} %bitcast.124, f32[3,128,512]{2,1,0:T(8,128)} %collective-permute-done.3, f32[3,128,512]{2,1,0:T(8,128)S(1)} %fusion.18, bf16[4,128,512]{2,1,0:T(8,128)(2,1)S(1)} %get-tuple-element.5, bf16[512,1024]{1,0:T(8,128)(2,1)S(1)} %copy-done, s32[]{:T(128)S(6)} %select_n.70), kind=kOutput, calls=%fused_computation.9 | convolution fusion | flops 201916416 | bytes 4194308 | tf_op jit(solution)/shard_map/lrj,jt->lrt/dot_general | solution.py:101
  27.1 2.3 %collective-permute-done.2 = f32[640,128]{1,0:T(8,128)S(1)} collective-permute-done((f32[640,128]{1,0:T(8,128)S(1)}, f32[640,128]{1,0:T(8,128)S(1)}, u32[]{:S(2)}, u32[]{:S(2)}) %collective-permute-start.2) | collective-permute-done | bytes 327712 | tf_op jit(solution)/shard_map/ppermute | solution.py:21
  29.4 1.6 %collective-permute-start.5 = (f32[384,128]{1,0:T(8,128)S(1)}, f32[384,128]{1,0:T(8,128)S(1)}, u32[]{:S(2)}, u32[]{:S(2)}) collective-permute-start(f32[384,128]{1,0:T(8,128)S(1)} %pad_maximum_fusion.4), channel_id=1, source_target_pairs={{0,4},{4,0},{8,12},{12,8},{1,5},{5,1},{9,13},{13,9},{2,6},{6,2},{1... | collective-permute-start | bytes 589832 | tf_op jit(solution)/shard_map/ppermute | solution.py:21
  31.2 3.8 %collective-permute-done.4 = bf16[512,256]{1,0:T(8,128)(2,1)S(1)} collective-permute-done((bf16[512,256]{1,0:T(8,128)(2,1)S(1)}, bf16[512,256]{1,0:T(8,128)(2,1)S(1)}, u32[]{:S(2)}, u32[]{:S(2)}) %collective-permute-start.4) | collective-permute-done | bytes 262176 | tf_op jit(solution)/shard_map/ppermute | solution.py:21
  35.7 1.6 %collective-permute-start.6 = (bf16[512,128]{1,0:T(8,128)(2,1)S(1)}, bf16[512,128]{1,0:T(8,128)(2,1)S(1)}, u32[]{:S(2)}, u32[]{:S(2)}) collective-permute-start(bf16[512,128]{1,0:T(8,128)(2,1)S(1)} %pad_maximum_fusion.11), channel_id=1, source_target_pairs={{0,4},{4,0},{8,12},{12,8},{1,5},{5,1},{9,13},{13,9},{2,6},{6,2},{1... | collective-permute-start | bytes 393224 | tf_op jit(solution)/shard_map/ppermute | solution.py:21
  37.5 3.3 %collective-permute-done.6 = bf16[512,128]{1,0:T(8,128)(2,1)S(1)} collective-permute-done((bf16[512,128]{1,0:T(8,128)(2,1)S(1)}, bf16[512,128]{1,0:T(8,128)(2,1)S(1)}, u32[]{:S(2)}, u32[]{:S(2)}) %collective-permute-start.6) | collective-permute-done | bytes 131104 | tf_op jit(solution)/shard_map/ppermute | solution.py:21
  41.7 4.9 %collective-permute-done.8 = bf16[256,128]{1,0:T(8,128)(2,1)S(1)} collective-permute-done((bf16[256,128]{1,0:T(8,128)(2,1)S(1)}, bf16[256,128]{1,0:T(8,128)(2,1)S(1)}, u32[]{:S(2)}, u32[]{:S(2)}) %collective-permute-start.8) | collective-permute-done | bytes 65568 | tf_op jit(solution)/shard_map/ppermute | solution.py:21
  46.9 1.7 %collective-permute-start.9 = (bf16[2,128,256]{1,2,0:T(8,128)(2,1)S(1)}, bf16[2,128,256]{1,2,0:T(8,128)(2,1)S(1)}, u32[]{:S(2)}, u32[]{:S(2)}) collective-permute-start(bf16[2,128,256]{1,2,0:T(8,128)(2,1)S(1)} %pad_maximum_fusion.12), channel_id=1, source_target_pairs={{0,2},{2,0},{1,3},{3,1},{4,6},{6,4},{5,7},{7,5},{8,10},{10,8},{9,1... | collective-permute-start | bytes 393224 | tf_op jit(solution)/shard_map/ppermute | solution.py:21
  48.7 3.2 %collective-permute-done.9 = bf16[2,128,256]{1,2,0:T(8,128)(2,1)S(1)} collective-permute-done((bf16[2,128,256]{1,2,0:T(8,128)(2,1)S(1)}, bf16[2,128,256]{1,2,0:T(8,128)(2,1)S(1)}, u32[]{:S(2)}, u32[]{:S(2)}) %collective-permute-start.9) | collective-permute-done | bytes 131104 | tf_op jit(solution)/shard_map/ppermute | solution.py:21
  53.1 1.3 %collective-permute-done.10 = bf16[3,128,512]{1,2,0:T(8,128)(2,1)S(1)} collective-permute-done((bf16[3,128,512]{1,2,0:T(8,128)(2,1)S(1)}, bf16[3,128,512]{1,2,0:T(8,128)(2,1)S(1)}, u32[]{:S(2)}, u32[]{:S(2)}) %collective-permute-start.10) | collective-permute-done | bytes 393248 | tf_op jit(solution)/shard_map/ppermute | solution.py:21
  54.3 1.2 %fusion.9 = bf16[3,128,1024]{1,2,0:T(8,128)(2,1)S(1)} fusion(s32[]{:T(128)S(6)} %select_n.81, bf16[1,128,512]{1,2,0:T(8,128)(2,1)S(1)} %copy.16, bf16[2,128,512]{1,2,0:T(8,128)(2,1)S(1)} %fusion.32, bf16[3,128,512]{1,2,0:T(8,128)(2,1)S(1)} %collective-permute-done.10), kind=kLoop, calls=%fused_computation.26 | loop fusion | flops 3932160 | bytes 1572868 | tf_op jit(solution)/shard_map/concatenate | solution.py:44
  57.0 1.8 %fusion = bf16[512,1024]{1,0:T(8,128)(2,1)} fusion(f32[1024,512]{0,1:T(8,128)S(1)} %fusion.34, f32[1024,512]{0,1:T(8,128)S(1)} %fusion.35, f32[1024,512]{0,1:T(8,128)S(1)} %fusion.36, f32[1024,512]{0,1:T(8,128)S(1)} %fusion.37, bf16[512,512]{1,0:T(8,128)(2,1)S(1)} %copy-done.2, bf16[512,1024]{1,0:T(8,128)(2,1)S(1)} %copy-done), kind=kOutput, calls=%fused_computation.1 | convolution fusion | flops 539492352 | bytes 11010048 | tf_op jit(solution)/shard_map/dot_general | solution.py:52
  (117 shorter events, 12.0 us)
Async XLA Ops:
  0.0 11.7 %copy-start = (bf16[512,1024]{1,0:T(8,128)(2,1)S(1)}, bf16[512,1024]{1,0:T(8,128)(2,1)}, u32[]{:S(2)}) copy-start(bf16[512,1024]{1,0:T(8,128)(2,1)} %param.5) | copy-start | bytes 3145732
  0.0 7.0 %slice-start = ((bf16[4,512,128]{2,1,0:T(8,128)(2,1)}), bf16[2,512,128]{2,1,0:T(8,128)(2,1)S(1)}, s32[]{:S(2)}) async-start(bf16[4,512,128]{2,1,0:T(8,128)(2,1)} %param.7), calls=%async_computation | async-start | bytes 524288 | tf_op jit(solution)/shard_map/slice | solution.py:57
  0.0 7.4 %slice-start.1 = ((bf16[4,512,128]{2,1,0:T(8,128)(2,1)}), bf16[3,512,128]{2,1,0:T(8,128)(2,1)S(1)}, s32[]{:S(2)}) async-start(bf16[4,512,128]{2,1,0:T(8,128)(2,1)} %param.7), calls=%async_computation.1 | async-start | bytes 786432 | tf_op jit(solution)/shard_map/slice | solution.py:57
  0.0 7.2 %copy-start.3 = (bf16[4,512,128]{2,1,0:T(8,128)(2,1)S(1)}, bf16[4,512,128]{2,1,0:T(8,128)(2,1)}, u32[]{:S(2)}) copy-start(bf16[4,512,128]{2,1,0:T(8,128)(2,1)} %param.8) | copy-start | bytes 1572868
  1.8 14.8 %collective-permute-start.7 = (bf16[128,256]{1,0:T(8,128)(2,1)}, bf16[128,256]{1,0:T(8,128)(2,1)}, u32[]{:S(2)}, u32[]{:S(2)}) collective-permute-start(bf16[128,256]{1,0:T(8,128)(2,1)} %get-tuple-element.11), channel_id=1, source_target_pairs={{0,8},{4,12},{8,0},{12,4},{1,9},{5,13},{9,1},{13,5},{2,10},{6,14},... | collective-permute-start | bytes 196616 | tf_op jit(solution)/shard_map/ppermute | solution.py:21
  7.1 3.2 %copy-start.1 = (bf16[4,512,128]{2,1,0:T(8,128)(2,1)S(1)}, bf16[4,512,128]{2,1,0:T(8,128)(2,1)}, u32[]{:S(2)}) copy-start(bf16[4,512,128]{2,1,0:T(8,128)(2,1)} %param.7) | copy-start | bytes 1572868
  10.2 7.2 %collective-permute-start = (f32[1024,128]{1,0:T(8,128)}, f32[1024,128]{1,0:T(8,128)}, u32[]{:S(2)}, u32[]{:S(2)}) collective-permute-start(f32[1024,128]{1,0:T(8,128)} %pad_maximum_fusion), channel_id=1, source_target_pairs={{0,1},{1,0},{2,3},{3,2},{4,5},{5,4},{6,7},{7,6},{8,9},{9,8},{10,11... | collective-permute-start | bytes 1572872 | tf_op jit(solution)/shard_map/ppermute | solution.py:21
  13.1 9.6 %collective-permute-start.1 = (bf16[128,1024]{1,0:T(8,128)(2,1)}, bf16[128,1024]{1,0:T(8,128)(2,1)}, u32[]{:S(2)}, u32[]{:S(2)}) collective-permute-start(bf16[128,1024]{1,0:T(8,128)(2,1)} %fusion.3), channel_id=1, source_target_pairs={{0,1},{1,0},{2,3},{3,2},{4,5},{5,4},{6,7},{7,6},{8,9},{9,8},{10,11... | collective-permute-start | bytes 786440 | tf_op jit(solution)/shard_map/ppermute | solution.py:21
  15.3 9.3 %collective-permute-start.3 = (f32[3,128,512]{2,1,0:T(8,128)}, f32[3,128,512]{2,1,0:T(8,128)}, u32[]{:S(2)}, u32[]{:S(2)}) collective-permute-start(f32[3,128,512]{2,1,0:T(8,128)} %convolution_add_fusion), channel_id=1, source_target_pairs={{0,1},{1,0},{2,3},{3,2},{4,5},{5,4},{6,7},{7,6},{8,9},{9,8},{10,11... | collective-permute-start | bytes 2359304 | tf_op jit(solution)/shard_map/ppermute | solution.py:21
  16.5 6.1 %copy-start.18 = (bf16[128,128]{1,0:T(8,128)(2,1)S(1)}, bf16[128,128]{1,0:T(8,128)(2,1)}, u32[]{:S(2)}) copy-start(bf16[128,128]{1,0:T(8,128)(2,1)} %copy-done.17) | copy-start | bytes 98308
  16.5 6.1 %copy-start.20 = (bf16[128,128]{1,0:T(8,128)(2,1)S(1)}, bf16[128,128]{1,0:T(8,128)(2,1)}, u32[]{:S(2)}) copy-start(bf16[128,128]{1,0:T(8,128)(2,1)} %copy-done.19) | copy-start | bytes 98308
  19.3 10.1 %collective-permute-start.2 = (f32[640,128]{1,0:T(8,128)S(1)}, f32[640,128]{1,0:T(8,128)S(1)}, u32[]{:S(2)}, u32[]{:S(2)}) collective-permute-start(f32[640,128]{1,0:T(8,128)S(1)} %pad_maximum_fusion.2), channel_id=1, source_target_pairs={{0,2},{2,0},{1,3},{3,1},{4,6},{6,4},{5,7},{7,5},{8,10},{10,8},{9,1... | collective-permute-start | bytes 983048 | tf_op jit(solution)/shard_map/ppermute | solution.py:21
  26.4 4.8 %copy-start.10 = (bf16[128,128]{1,0:T(8,128)(2,1)S(1)}, bf16[128,128]{1,0:T(8,128)(2,1)}, u32[]{:S(2)}) copy-start(bf16[128,128]{1,0:T(8,128)(2,1)} %get-tuple-element.63) | copy-start | bytes 98308
  26.4 4.8 %copy-start.12 = (bf16[128,128]{1,0:T(8,128)(2,1)S(1)}, bf16[128,128]{1,0:T(8,128)(2,1)}, u32[]{:S(2)}) copy-start(bf16[128,128]{1,0:T(8,128)(2,1)} %get-tuple-element.64) | copy-start | bytes 98308
  26.5 8.5 %collective-permute-start.4 = (bf16[512,256]{1,0:T(8,128)(2,1)S(1)}, bf16[512,256]{1,0:T(8,128)(2,1)S(1)}, u32[]{:S(2)}, u32[]{:S(2)}) collective-permute-start(bf16[512,256]{1,0:T(8,128)(2,1)S(1)} %pad_maximum_fusion.3), channel_id=1, source_target_pairs={{0,2},{2,0},{1,3},{3,1},{4,6},{6,4},{5,7},{7,5},{8,10},{10,8},{9,1... | collective-permute-start | bytes 786440 | tf_op jit(solution)/shard_map/ppermute | solution.py:21
  29.4 7.9 %collective-permute-start.5 = (f32[384,128]{1,0:T(8,128)S(1)}, f32[384,128]{1,0:T(8,128)S(1)}, u32[]{:S(2)}, u32[]{:S(2)}) collective-permute-start(f32[384,128]{1,0:T(8,128)S(1)} %pad_maximum_fusion.4), channel_id=1, source_target_pairs={{0,4},{4,0},{8,12},{12,8},{1,5},{5,1},{9,13},{13,9},{2,6},{6,2},{1... | collective-permute-start | bytes 589832 | tf_op jit(solution)/shard_map/ppermute | solution.py:21
  31.2 6.2 %copy-start.14 = (bf16[128,128]{1,0:T(8,128)(2,1)S(1)}, bf16[128,128]{1,0:T(8,128)(2,1)}, u32[]{:S(2)}) copy-start(bf16[128,128]{1,0:T(8,128)(2,1)} %copy-done.13) | copy-start | bytes 98308
  31.2 6.2 %copy-start.16 = (bf16[128,128]{1,0:T(8,128)(2,1)S(1)}, bf16[128,128]{1,0:T(8,128)(2,1)}, u32[]{:S(2)}) copy-start(bf16[128,128]{1,0:T(8,128)(2,1)} %copy-done.15) | copy-start | bytes 98308
  35.7 5.0 %collective-permute-start.6 = (bf16[512,128]{1,0:T(8,128)(2,1)S(1)}, bf16[512,128]{1,0:T(8,128)(2,1)S(1)}, u32[]{:S(2)}, u32[]{:S(2)}) collective-permute-start(bf16[512,128]{1,0:T(8,128)(2,1)S(1)} %pad_maximum_fusion.11), channel_id=1, source_target_pairs={{0,4},{4,0},{8,12},{12,8},{1,5},{5,1},{9,13},{13,9},{2,6},{6,2},{1... | collective-permute-start | bytes 393224 | tf_op jit(solution)/shard_map/ppermute | solution.py:21
  40.8 11.9 %copy-start.4 = (bf16[4,512,128]{2,1,0:T(8,128)(2,1)S(1)}, bf16[4,512,128]{2,1,0:T(8,128)(2,1)}, u32[]{:S(2)}) copy-start(bf16[4,512,128]{2,1,0:T(8,128)(2,1)} %param.8) | copy-start | bytes 1572868
  40.8 11.9 %copy-start.8 = (bf16[256,1024]{1,0:T(8,128)(2,1)S(1)}, bf16[256,1024]{1,0:T(8,128)(2,1)}, u32[]{:S(2)}) copy-start(bf16[256,1024]{1,0:T(8,128)(2,1)} %copy-done.7) | copy-start | bytes 1572868
  41.4 5.2 %collective-permute-start.8 = (bf16[256,128]{1,0:T(8,128)(2,1)S(1)}, bf16[256,128]{1,0:T(8,128)(2,1)S(1)}, u32[]{:S(2)}, u32[]{:S(2)}) collective-permute-start(bf16[256,128]{1,0:T(8,128)(2,1)S(1)} %pad_maximum_fusion.15), channel_id=1, source_target_pairs={{0,8},{4,12},{8,0},{12,4},{1,9},{5,13},{9,1},{13,5},{2,10},{6,14},... | collective-permute-start | bytes 196616 | tf_op jit(solution)/shard_map/ppermute | solution.py:21
  46.9 5.0 %collective-permute-start.9 = (bf16[2,128,256]{1,2,0:T(8,128)(2,1)S(1)}, bf16[2,128,256]{1,2,0:T(8,128)(2,1)S(1)}, u32[]{:S(2)}, u32[]{:S(2)}) collective-permute-start(bf16[2,128,256]{1,2,0:T(8,128)(2,1)S(1)} %pad_maximum_fusion.12), channel_id=1, source_target_pairs={{0,2},{2,0},{1,3},{3,1},{4,6},{6,4},{5,7},{7,5},{8,10},{10,8},{9,1... | collective-permute-start | bytes 393224 | tf_op jit(solution)/shard_map/ppermute | solution.py:21
  52.5 1.8 %collective-permute-start.10 = (bf16[3,128,512]{1,2,0:T(8,128)(2,1)S(1)}, bf16[3,128,512]{1,2,0:T(8,128)(2,1)S(1)}, u32[]{:S(2)}, u32[]{:S(2)}) collective-permute-start(bf16[3,128,512]{1,2,0:T(8,128)(2,1)S(1)} %pad_maximum_fusion.1), channel_id=1, source_target_pairs={{0,1},{1,0},{2,3},{3,2},{4,5},{5,4},{6,7},{7,6},{8,9},{9,8},{10,11... | collective-permute-start | bytes 1179656 | tf_op jit(solution)/shard_map/ppermute | solution.py:21
  (11 other events, 21.6 us)

commit v27 on v23

--- a/solution.py
+++ b/solution.py
@@ -61,12 +61,12 @@
     w_own, theirs_c = [None] * levels, []
     for b in range(levels):
         c = mine_c[b]
-        parts = [jnp.concatenate([c[:, :rank], c[:, rank:]], axis=0).astype(F32)]
-        parts += partial[b:]
+        parts = list(partial[b:])
+        parts.append(jnp.concatenate([c[:, :rank], c[:, rank:]], axis=0).astype(F32))
         got = swap(jnp.concatenate(parts, axis=0), b, bits)
-        theirs = got[: 2 * rank]
+        theirs = got[got.shape[0] - 2 * rank :]
         theirs_c.append(jnp.concatenate([theirs[:rank], theirs[rank:]], axis=1))
-        at = 2 * rank
+        at = 0
         for s in range(b, levels - 1):
             n = partial[s].shape[0]
             recv = got[at : at + n]

time: 56.1 us -> 56.1 us (level)
  no operation moved by 1% of the time
where the time goes in v27:
time: 56.1 us; the launch traced here: 55.6 us
  waiting for transfers between devices  18.8 us (34%)
  matrix products  13.6 us (24%)
  starting transfers between devices  12.2 us (22%)
  other arithmetic  5.39 us (10%)
  local copies, waits for them, and re-layouts  4.95 us (9%)
  between operations  0.66 us (1%)
    ppermute x11, waiting for transfers between devices, swap(): return lax.ppermute(x, axis, [(i, i ^ 1 << stride) for i in range(n)])  18.8 us
    ppermute x11, starting transfers between devices, swap(): return lax.ppermute(x, axis, [(i, i ^ 1 << stride) for i in range(n)])  12.2 us
    dot_general x3, matrix products, project(): jnp.einsum('lrj,jt->lrt', vl_lo[lv], x, preferred_element_type=F32)  3.8 us
    dot_general x4, matrix products, on_device(): coefs = jnp.dot(couple[s], stacked, preferred_element_type=F32).astype(BF16)  2.01 us
    dot_general x1, matrix products, on_device(): c0 = jnp.dot(leaf_inverse, templates, preferred_element_type=F32)  1.83 us
    concatenate x2, other arithmetic, gather_half(): both = jnp.concatenate([x, swap(x, bit, bits), x], axis=-1)  1.79 us
    add x3, other arithmetic, on_device(): partial[s] = partial[s] + recv  1.78 us
    dot_general x4, matrix products, on_device(): current = current - jnp.dot(u_basis[s], full[s], preferred_element_type=F32)  1.73 us
  transfers between devices with their start and end apart: 11, of which 6 were waited for; matrix products, arithmetic and copies ran while one was open for 29% of the time, Pallas kernels for 0%

profile of v27, /device:TPU:0, one launch (start us, length us, event | category | flops | bytes accessed | tf_op | source)
XLA Modules:
  0.0 55.6 jit_solution(13954368664218409150)
XLA Ops:
  0.0 1.1 %slice_bitcast_fusion.12 = (bf16[128,256]{1,0:T(8,128)(2,1)S(1)}, bf16[128,256]{1,0:T(8,128)(2,1)S(1)}, bf16[128,256]{1,0:T(8,128)(2,1)S(1)}, bf16[128,256]{1,0:T(8,128)(2,1)S(1)}) fusion(bf16[4,1,128,256]{3,2,1,0:T(8,128)(2,1)} %param.9), kind=kLoop, calls=%fused_computation.167 | loop fusion | bytes 524288 | tf_op jit(solution)/shard_map/squeeze | solution.py:81
  1.8 4.0 %collective-permute-start.7 = (bf16[256,128]{1,0:T(8,128)(2,1)}, bf16[256,128]{1,0:T(8,128)(2,1)}, u32[]{:S(2)}, u32[]{:S(2)}) collective-permute-start(bf16[256,128]{1,0:T(8,128)(2,1)} %maximum_convert_fusion.3), channel_id=1, source_target_pairs={{0,8},{4,12},{8,0},{12,4},{1,9},{5,13},{9,1},{13,5},{2,10},{6,14},... | collective-permute-start | bytes 196616 | tf_op jit(solution)/shard_map/ppermute | solution.py:21
  7.0 0.8 %pad_maximum_fusion = f32[1024,128]{1,0:T(8,128)} fusion(f32[256,128]{1,0:T(8,128)S(1)} %maximum_convert_fusion, f32[128,128]{1,0:T(8,128)S(1)} %fusion.80, f32[256,128]{1,0:T(8,128)S(1)} %fusion.84, f32[384,128]{1,0:T(8,128)S(1)} %fusion.87), kind=kLoop, calls=%fused_computation.28 | loop fusion | flops 393216 | bytes 1048576 | tf_op jit(solution)/shard_map/concatenate | solution.py:66
  7.9 1.5 %subtract_convert_fusion = (bf16[4,128,512]{2,1,0:T(8,128)(2,1)S(1)}, bf16[4,128,512]{2,1,0:T(8,128)(2,1)S(1)}) fusion(bf16[4,512,128]{2,1,0:T(8,128)(2,1)S(1)} %copy-done.1, bf16[512,512]{1,0:T(8,128)(2,1)} %param.6), kind=kOutput, calls=%fused_computation.23 | convolution fusion | flops 269484032 | bytes 2097152 | tf_op jit(solution)/shard_map/lir,ij->lrj/dot_general | solution.py:91
  9.7 1.0 %fusion.3 = bf16[128,1024]{1,0:T(8,128)(2,1)} fusion(f32[128,1024]{1,0:T(8,128)S(1)} %fusion.64, bf16[512,1024]{1,0:T(8,128)(2,1)S(1)} %copy-done, bf16[4,128,512]{2,1,0:T(8,128)(2,1)S(1)} %get-tuple-element.5), kind=kOutput, calls=%fused_computation.11 | convolution fusion | flops 134479872 | bytes 1966080 | tf_op jit(solution)/shard_map/lrj,jt->lrt/dot_general | solution.py:98
  11.7 1.3 %convolution_add_fusion = f32[3,128,512]{2,1,0:T(8,128)} fusion(f32[3,128,512]{2,1,0:T(8,128)S(1)} %fusion.15, bf16[4,128,512]{2,1,0:T(8,128)(2,1)S(1)} %get-tuple-element.5, bf16[512,1024]{1,0:T(8,128)(2,1)S(1)} %copy-done, s32[]{:T(128)S(6)} %select_n.69), kind=kOutput, calls=%fused_computation.6 | convolution fusion | flops 201523200 | bytes 2621444 | tf_op jit(solution)/shard_map/lrj,jt->lrt/dot_general | solution.py:98
  14.2 0.9 %slice_add_fusion = f32[256,128]{1,0:T(8,128)S(1)} fusion(f32[256,128]{1,0:T(8,128)S(1)} %fusion.84, f32[1024,128]{1,0:T(8,128)} %collective-permute-done), kind=kLoop, calls=%fused_computation.100 | loop fusion | flops 32768 | bytes 393216 | tf_op jit(solution)/shard_map/add | solution.py:77
  15.1 0.8 %slice_add_fusion.2 = f32[128,128]{1,0:T(8,128)S(1)} fusion(f32[128,128]{1,0:T(8,128)S(1)} %fusion.80, f32[1024,128]{1,0:T(8,128)} %collective-permute-done), kind=kLoop, calls=%fused_computation.161 | loop fusion | flops 16384 | bytes 196608 | tf_op jit(solution)/shard_map/add | solution.py:77
  16.0 1.6 %collective-permute-start.2 = (f32[640,128]{1,0:T(8,128)S(1)}, f32[640,128]{1,0:T(8,128)S(1)}, u32[]{:S(2)}, u32[]{:S(2)}) collective-permute-start(f32[640,128]{1,0:T(8,128)S(1)} %pad_maximum_fusion.2), channel_id=1, source_target_pairs={{0,2},{2,0},{1,3},{3,1},{4,6},{6,4},{5,7},{7,5},{8,10},{10,8},{9,1... | collective-permute-start | bytes 983048 | tf_op jit(solution)/shard_map/ppermute | solution.py:21
  17.6 0.9 %slice.308 = f32[384,128]{1,0:T(8,128)S(1)} slice(f32[1024,128]{1,0:T(8,128)} %collective-permute-done), slice={[0:384], [0:128]} | slice | bytes 393216 | tf_op jit(solution)/shard_map/slice | solution.py:72
  18.5 0.9 %fusion.126 = (bf16[128,128]{1,0:T(8,128)(2,1)S(1)}, bf16[128,128]{1,0:T(8,128)(2,1)S(1)}) fusion(f32[1024,128]{1,0:T(8,128)} %collective-permute-done), kind=kLoop, calls=%fused_computation.198 | loop fusion | bytes 131072 | tf_op jit(solution)/shard_map/slice | solution.py:68
  19.5 1.3 %convolution_convert_fusion = bf16[256,1024]{1,0:T(8,128)(2,1)S(1)} fusion(bf16[128,1024]{1,0:T(8,128)(2,1)} %collective-permute-done.1, bf16[128,1024]{1,0:T(8,128)(2,1)} %fusion.3, bf16[256,128]{1,0:T(8,128)(2,1)S(1)} %get-tuple-element.32, bf16[256,128]{1,0:T(8,128)(2,1)S(1)} %get-tuple-element.31), kind=kOutput, calls=%fused_computation.5 | convolution fusion | flops 135528448 | bytes 1179648 | tf_op jit(solution)/shard_map/dot_general | solution.py:137
  21.6 1.5 %fusion.2 = f32[3,128,512]{2,1,0:T(8,128)S(1)} fusion(f32[3,128,512]{2,1,0:T(8,128)S(1)} %bitcast.124, f32[3,128,512]{2,1,0:T(8,128)} %collective-permute-done.3, f32[3,128,512]{2,1,0:T(8,128)S(1)} %fusion.18, bf16[4,128,512]{2,1,0:T(8,128)(2,1)S(1)} %get-tuple-element.5, bf16[512,1024]{1,0:T(8,128)(2,1)S(1)} %copy-done, s32[]{:T(128)S(6)} %select_n.68), kind=kOutput, calls=%fused_computation.9 | convolution fusion | flops 201916416 | bytes 4194308 | tf_op jit(solution)/shard_map/lrj,jt->lrt/dot_general | solution.py:98
  23.9 2.3 %collective-permute-done.2 = f32[640,128]{1,0:T(8,128)S(1)} collective-permute-done((f32[640,128]{1,0:T(8,128)S(1)}, f32[640,128]{1,0:T(8,128)S(1)}, u32[]{:S(2)}, u32[]{:S(2)}) %collective-permute-start.2) | collective-permute-done | bytes 327712 | tf_op jit(solution)/shard_map/ppermute | solution.py:21
  26.2 1.6 %collective-permute-start.5 = (f32[384,128]{1,0:T(8,128)S(1)}, f32[384,128]{1,0:T(8,128)S(1)}, u32[]{:S(2)}, u32[]{:S(2)}) collective-permute-start(f32[384,128]{1,0:T(8,128)S(1)} %pad_maximum_fusion.4), channel_id=1, source_target_pairs={{0,4},{4,0},{8,12},{12,8},{1,5},{5,1},{9,13},{13,9},{2,6},{6,2},{1... | collective-permute-start | bytes 589832 | tf_op jit(solution)/shard_map/ppermute | solution.py:21
  27.9 3.9 %collective-permute-done.4 = bf16[512,256]{1,0:T(8,128)(2,1)S(1)} collective-permute-done((bf16[512,256]{1,0:T(8,128)(2,1)S(1)}, bf16[512,256]{1,0:T(8,128)(2,1)S(1)}, u32[]{:S(2)}, u32[]{:S(2)}) %collective-permute-start.4) | collective-permute-done | bytes 262176 | tf_op jit(solution)/shard_map/ppermute | solution.py:21
  32.5 1.6 %collective-permute-start.6 = (bf16[512,128]{1,0:T(8,128)(2,1)S(1)}, bf16[512,128]{1,0:T(8,128)(2,1)S(1)}, u32[]{:S(2)}, u32[]{:S(2)}) collective-permute-start(bf16[512,128]{1,0:T(8,128)(2,1)S(1)} %pad_maximum_fusion.11), channel_id=1, source_target_pairs={{0,4},{4,0},{8,12},{12,8},{1,5},{5,1},{9,13},{13,9},{2,6},{6,2},{1... | collective-permute-start | bytes 393224 | tf_op jit(solution)/shard_map/ppermute | solution.py:21
  34.2 3.3 %collective-permute-done.6 = bf16[512,128]{1,0:T(8,128)(2,1)S(1)} collective-permute-done((bf16[512,128]{1,0:T(8,128)(2,1)S(1)}, bf16[512,128]{1,0:T(8,128)(2,1)S(1)}, u32[]{:S(2)}, u32[]{:S(2)}) %collective-permute-start.6) | collective-permute-done | bytes 131104 | tf_op jit(solution)/shard_map/ppermute | solution.py:21
  38.5 4.8 %collective-permute-done.8 = bf16[256,128]{1,0:T(8,128)(2,1)S(1)} collective-permute-done((bf16[256,128]{1,0:T(8,128)(2,1)S(1)}, bf16[256,128]{1,0:T(8,128)(2,1)S(1)}, u32[]{:S(2)}, u32[]{:S(2)}) %collective-permute-start.8) | collective-permute-done | bytes 65568 | tf_op jit(solution)/shard_map/ppermute | solution.py:21
  43.6 1.7 %collective-permute-start.9 = (bf16[2,128,256]{1,2,0:T(8,128)(2,1)S(1)}, bf16[2,128,256]{1,2,0:T(8,128)(2,1)S(1)}, u32[]{:S(2)}, u32[]{:S(2)}) collective-permute-start(bf16[2,128,256]{1,2,0:T(8,128)(2,1)S(1)} %pad_maximum_fusion.14), channel_id=1, source_target_pairs={{0,2},{2,0},{1,3},{3,1},{4,6},{6,4},{5,7},{7,5},{8,10},{10,8},{9,1... | collective-permute-start | bytes 393224 | tf_op jit(solution)/shard_map/ppermute | solution.py:21
  45.5 3.2 %collective-permute-done.9 = bf16[2,128,256]{1,2,0:T(8,128)(2,1)S(1)} collective-permute-done((bf16[2,128,256]{1,2,0:T(8,128)(2,1)S(1)}, bf16[2,128,256]{1,2,0:T(8,128)(2,1)S(1)}, u32[]{:S(2)}, u32[]{:S(2)}) %collective-permute-start.9) | collective-permute-done | bytes 131104 | tf_op jit(solution)/shard_map/ppermute | solution.py:21
  49.8 1.3 %collective-permute-done.10 = bf16[3,128,512]{1,2,0:T(8,128)(2,1)S(1)} collective-permute-done((bf16[3,128,512]{1,2,0:T(8,128)(2,1)S(1)}, bf16[3,128,512]{1,2,0:T(8,128)(2,1)S(1)}, u32[]{:S(2)}, u32[]{:S(2)}) %collective-permute-start.10) | collective-permute-done | bytes 393248 | tf_op jit(solution)/shard_map/ppermute | solution.py:21
  51.1 1.2 %fusion.9 = bf16[3,128,1024]{1,2,0:T(8,128)(2,1)S(1)} fusion(s32[]{:T(128)S(6)} %select_n.79, bf16[1,128,512]{1,2,0:T(8,128)(2,1)S(1)} %copy.16, bf16[2,128,512]{1,2,0:T(8,128)(2,1)S(1)} %fusion.32, bf16[3,128,512]{1,2,0:T(8,128)(2,1)S(1)} %collective-permute-done.10), kind=kLoop, calls=%fused_computation.26 | loop fusion | flops 3932160 | bytes 1572868 | tf_op jit(solution)/shard_map/concatenate | solution.py:44
  53.8 1.8 %fusion = bf16[512,1024]{1,0:T(8,128)(2,1)} fusion(f32[1024,512]{0,1:T(8,128)S(1)} %fusion.34, f32[1024,512]{0,1:T(8,128)S(1)} %fusion.35, f32[1024,512]{0,1:T(8,128)S(1)} %fusion.36, f32[1024,512]{0,1:T(8,128)S(1)} %fusion.37, bf16[512,512]{1,0:T(8,128)(2,1)S(1)} %copy-done.2, bf16[512,1024]{1,0:T(8,128)(2,1)S(1)} %copy-done), kind=kOutput, calls=%fused_computation.1 | convolution fusion | flops 539492352 | bytes 11010048 | tf_op jit(solution)/shard_map/dot_general | solution.py:52
  (104 shorter events, 10.3 us)
Async XLA Ops:
  0.0 9.4 %copy-start = (bf16[512,1024]{1,0:T(8,128)(2,1)S(1)}, bf16[512,1024]{1,0:T(8,128)(2,1)}, u32[]{:S(2)}) copy-start(bf16[512,1024]{1,0:T(8,128)(2,1)} %param.5) | copy-start | bytes 3145732
  0.0 5.9 %copy-start.1 = (bf16[4,512,128]{2,1,0:T(8,128)(2,1)S(1)}, bf16[4,512,128]{2,1,0:T(8,128)(2,1)}, u32[]{:S(2)}) copy-start(bf16[4,512,128]{2,1,0:T(8,128)(2,1)} %param.7) | copy-start | bytes 1572868
  0.0 6.1 %slice-start = ((bf16[4,512,128]{2,1,0:T(8,128)(2,1)}), bf16[2,512,128]{2,1,0:T(8,128)(2,1)S(1)}, s32[]{:S(2)}) async-start(bf16[4,512,128]{2,1,0:T(8,128)(2,1)} %param.7), calls=%async_computation | async-start | bytes 524288 | tf_op jit(solution)/shard_map/slice | solution.py:57
  0.0 6.5 %slice-start.1 = ((bf16[4,512,128]{2,1,0:T(8,128)(2,1)}), bf16[3,512,128]{2,1,0:T(8,128)(2,1)S(1)}, s32[]{:S(2)}) async-start(bf16[4,512,128]{2,1,0:T(8,128)(2,1)} %param.7), calls=%async_computation.1 | async-start | bytes 786432 | tf_op jit(solution)/shard_map/slice | solution.py:57
  0.0 5.9 %copy-start.3 = (bf16[4,512,128]{2,1,0:T(8,128)(2,1)S(1)}, bf16[4,512,128]{2,1,0:T(8,128)(2,1)}, u32[]{:S(2)}) copy-start(bf16[4,512,128]{2,1,0:T(8,128)(2,1)} %param.8) | copy-start | bytes 1572868
  1.2 5.1 %copy-start.11 = (bf16[128,128]{1,0:T(8,128)(2,1)}, bf16[128,128]{1,0:T(8,128)(2,1)S(1)}, u32[]{:S(2)}) copy-start(bf16[128,128]{1,0:T(8,128)(2,1)S(1)} %get-tuple-element.39) | copy-start | bytes 98308
  1.2 5.1 %copy-start.13 = (bf16[128,128]{1,0:T(8,128)(2,1)}, bf16[128,128]{1,0:T(8,128)(2,1)S(1)}, u32[]{:S(2)}) copy-start(bf16[128,128]{1,0:T(8,128)(2,1)S(1)} %get-tuple-element.40) | copy-start | bytes 98308
  1.8 11.5 %collective-permute-start.7 = (bf16[256,128]{1,0:T(8,128)(2,1)}, bf16[256,128]{1,0:T(8,128)(2,1)}, u32[]{:S(2)}, u32[]{:S(2)}) collective-permute-start(bf16[256,128]{1,0:T(8,128)(2,1)} %maximum_convert_fusion.3), channel_id=1, source_target_pairs={{0,8},{4,12},{8,0},{12,4},{1,9},{5,13},{9,1},{13,5},{2,10},{6,14},... | collective-permute-start | bytes 196616 | tf_op jit(solution)/shard_map/ppermute | solution.py:21
  7.0 2.7 %copy-start.7 = (bf16[128,128]{1,0:T(8,128)(2,1)}, bf16[128,128]{1,0:T(8,128)(2,1)S(1)}, u32[]{:S(2)}) copy-start(bf16[128,128]{1,0:T(8,128)(2,1)S(1)} %get-tuple-element.53) | copy-start | bytes 98308
  7.0 2.7 %copy-start.9 = (bf16[128,128]{1,0:T(8,128)(2,1)}, bf16[128,128]{1,0:T(8,128)(2,1)S(1)}, u32[]{:S(2)}) copy-start(bf16[128,128]{1,0:T(8,128)(2,1)S(1)} %get-tuple-element.54) | copy-start | bytes 98308
  7.9 6.3 %collective-permute-start = (f32[1024,128]{1,0:T(8,128)}, f32[1024,128]{1,0:T(8,128)}, u32[]{:S(2)}, u32[]{:S(2)}) collective-permute-start(f32[1024,128]{1,0:T(8,128)} %pad_maximum_fusion), channel_id=1, source_target_pairs={{0,1},{1,0},{2,3},{3,2},{4,5},{5,4},{6,7},{7,6},{8,9},{9,8},{10,11... | collective-permute-start | bytes 1572872 | tf_op jit(solution)/shard_map/ppermute | solution.py:21
  10.8 8.7 %collective-permute-start.1 = (bf16[128,1024]{1,0:T(8,128)(2,1)}, bf16[128,1024]{1,0:T(8,128)(2,1)}, u32[]{:S(2)}, u32[]{:S(2)}) collective-permute-start(bf16[128,1024]{1,0:T(8,128)(2,1)} %fusion.3), channel_id=1, source_target_pairs={{0,1},{1,0},{2,3},{3,2},{4,5},{5,4},{6,7},{7,6},{8,9},{9,8},{10,11... | collective-permute-start | bytes 786440 | tf_op jit(solution)/shard_map/ppermute | solution.py:21
  12.9 8.4 %collective-permute-start.3 = (f32[3,128,512]{2,1,0:T(8,128)}, f32[3,128,512]{2,1,0:T(8,128)}, u32[]{:S(2)}, u32[]{:S(2)}) collective-permute-start(f32[3,128,512]{2,1,0:T(8,128)} %convolution_add_fusion), channel_id=1, source_target_pairs={{0,1},{1,0},{2,3},{3,2},{4,5},{5,4},{6,7},{7,6},{8,9},{9,8},{10,11... | collective-permute-start | bytes 2359304 | tf_op jit(solution)/shard_map/ppermute | solution.py:21
  12.9 6.5 %copy-start.8 = (bf16[128,128]{1,0:T(8,128)(2,1)S(1)}, bf16[128,128]{1,0:T(8,128)(2,1)}, u32[]{:S(2)}) copy-start(bf16[128,128]{1,0:T(8,128)(2,1)} %copy-done.7) | copy-start | bytes 98308
  12.9 6.5 %copy-start.10 = (bf16[128,128]{1,0:T(8,128)(2,1)S(1)}, bf16[128,128]{1,0:T(8,128)(2,1)}, u32[]{:S(2)}) copy-start(bf16[128,128]{1,0:T(8,128)(2,1)} %copy-done.9) | copy-start | bytes 98308
  16.0 10.2 %collective-permute-start.2 = (f32[640,128]{1,0:T(8,128)S(1)}, f32[640,128]{1,0:T(8,128)S(1)}, u32[]{:S(2)}, u32[]{:S(2)}) collective-permute-start(f32[640,128]{1,0:T(8,128)S(1)} %pad_maximum_fusion.2), channel_id=1, source_target_pairs={{0,2},{2,0},{1,3},{3,1},{4,6},{6,4},{5,7},{7,5},{8,10},{10,8},{9,1... | collective-permute-start | bytes 983048 | tf_op jit(solution)/shard_map/ppermute | solution.py:21
  23.3 8.5 %collective-permute-start.4 = (bf16[512,256]{1,0:T(8,128)(2,1)S(1)}, bf16[512,256]{1,0:T(8,128)(2,1)S(1)}, u32[]{:S(2)}, u32[]{:S(2)}) collective-permute-start(bf16[512,256]{1,0:T(8,128)(2,1)S(1)} %pad_maximum_fusion.3), channel_id=1, source_target_pairs={{0,2},{2,0},{1,3},{3,1},{4,6},{6,4},{5,7},{7,5},{8,10},{10,8},{9,1... | collective-permute-start | bytes 786440 | tf_op jit(solution)/shard_map/ppermute | solution.py:21
  26.2 7.9 %collective-permute-start.5 = (f32[384,128]{1,0:T(8,128)S(1)}, f32[384,128]{1,0:T(8,128)S(1)}, u32[]{:S(2)}, u32[]{:S(2)}) collective-permute-start(f32[384,128]{1,0:T(8,128)S(1)} %pad_maximum_fusion.4), channel_id=1, source_target_pairs={{0,4},{4,0},{8,12},{12,8},{1,5},{5,1},{9,13},{13,9},{2,6},{6,2},{1... | collective-permute-start | bytes 589832 | tf_op jit(solution)/shard_map/ppermute | solution.py:21
  32.5 5.0 %collective-permute-start.6 = (bf16[512,128]{1,0:T(8,128)(2,1)S(1)}, bf16[512,128]{1,0:T(8,128)(2,1)S(1)}, u32[]{:S(2)}, u32[]{:S(2)}) collective-permute-start(bf16[512,128]{1,0:T(8,128)(2,1)S(1)} %pad_maximum_fusion.11), channel_id=1, source_target_pairs={{0,4},{4,0},{8,12},{12,8},{1,5},{5,1},{9,13},{13,9},{2,6},{6,2},{1... | collective-permute-start | bytes 393224 | tf_op jit(solution)/shard_map/ppermute | solution.py:21
  37.5 11.9 %copy-start.4 = (bf16[4,512,128]{2,1,0:T(8,128)(2,1)S(1)}, bf16[4,512,128]{2,1,0:T(8,128)(2,1)}, u32[]{:S(2)}) copy-start(bf16[4,512,128]{2,1,0:T(8,128)(2,1)} %param.8) | copy-start | bytes 1572868
  37.5 11.9 %copy-start.6 = (bf16[256,1024]{1,0:T(8,128)(2,1)S(1)}, bf16[256,1024]{1,0:T(8,128)(2,1)}, u32[]{:S(2)}) copy-start(bf16[256,1024]{1,0:T(8,128)(2,1)} %copy-done.5) | copy-start | bytes 1572868
  38.1 5.2 %collective-permute-start.8 = (bf16[256,128]{1,0:T(8,128)(2,1)S(1)}, bf16[256,128]{1,0:T(8,128)(2,1)S(1)}, u32[]{:S(2)}, u32[]{:S(2)}) collective-permute-start(bf16[256,128]{1,0:T(8,128)(2,1)S(1)} %pad_maximum_fusion.15), channel_id=1, source_target_pairs={{0,8},{4,12},{8,0},{12,4},{1,9},{5,13},{9,1},{13,5},{2,10},{6,14},... | collective-permute-start | bytes 196616 | tf_op jit(solution)/shard_map/ppermute | solution.py:21
  43.6 5.0 %collective-permute-start.9 = (bf16[2,128,256]{1,2,0:T(8,128)(2,1)S(1)}, bf16[2,128,256]{1,2,0:T(8,128)(2,1)S(1)}, u32[]{:S(2)}, u32[]{:S(2)}) collective-permute-start(bf16[2,128,256]{1,2,0:T(8,128)(2,1)S(1)} %pad_maximum_fusion.14), channel_id=1, source_target_pairs={{0,2},{2,0},{1,3},{3,1},{4,6},{6,4},{5,7},{7,5},{8,10},{10,8},{9,1... | collective-permute-start | bytes 393224 | tf_op jit(solution)/shard_map/ppermute | solution.py:21
  49.3 1.8 %collective-permute-start.10 = (bf16[3,128,512]{1,2,0:T(8,128)(2,1)S(1)}, bf16[3,128,512]{1,2,0:T(8,128)(2,1)S(1)}, u32[]{:S(2)}, u32[]{:S(2)}) collective-permute-start(bf16[3,128,512]{1,2,0:T(8,128)(2,1)S(1)} %pad_maximum_fusion.1), channel_id=1, source_target_pairs={{0,1},{1,0},{2,3},{3,2},{4,5},{5,4},{6,7},{7,6},{8,9},{9,8},{10,11... | collective-permute-start | bytes 1179656 | tf_op jit(solution)/shard_map/ppermute | solution.py:21
  (4 other events, 6.8 us)

commit v28 on v23

--- a/solution.py
+++ b/solution.py
@@ -66,15 +66,19 @@
         got = swap(jnp.concatenate(parts, axis=0), b, bits)
         theirs = got[: 2 * rank]
         theirs_c.append(jnp.concatenate([theirs[:rank], theirs[rank:]], axis=1))
-        at = 2 * rank
-        for s in range(b, levels - 1):
-            n = partial[s].shape[0]
-            recv = got[at : at + n]
-            at += n
-            if s == b:
-                w_own[s] = jnp.concatenate([partial[s], recv], axis=1)
-            else:
-                partial[s] = partial[s] + recv
+        if b < levels - 1:
+            n = partial[b].shape[0]
+            w_own[b] = jnp.concatenate(
+                [partial[b], got[2 * rank : 2 * rank + n]], axis=1
+            )
+            if b + 1 < levels - 1:
+                later = jnp.concatenate(partial[b + 1 :], axis=0)
+                later = later + got[2 * rank + n :]
+                at = 0
+                for s in range(b + 1, levels - 1):
+                    k = partial[s].shape[0]
+                    partial[s] = later[at : at + k]
+                    at += k
     couple = []
     for s in range(levels):
         lower = side(s, bits) == 0

time: 56.1 us -> 55.6 us (level)
  waiting for transfers between devices: 18.8 us -> 20.2 us
  local copies, waits for them, and re-layouts: 4.95 us -> 4.03 us
  other arithmetic: 5.39 us -> 4.69 us
    add x3 -> x1, other arithmetic: 1.78 us -> 0.01 us  [on_device(): later = later + got[2 * rank + n:]]
    ppermute x11, waiting for transfers between devices: 18.8 us -> 20.2 us  [swap(): return lax.ppermute(x, axis, [(i, i ^ 1 << stride) for i in range(n)])]
    slice x0 -> x1, other arithmetic: none -> 1.06 us  [on_device(): w_own[b] = jnp.concatenate([partial[b], got[2 * rank:2 * rank + n]], axis=1)]
    slice x3, local copies, waits for them, and re-layouts: 0.96 us -> 0.03 us  [the longest x2 0.02 us: on_device(): w_own[b] = jnp.concatenate([partial[b], got[2 * rank:2 * rank + n]], axis=1)]
  transfers between devices with their start and end apart: 11 -> 11, of which waited for: 6 -> 6; matrix products, arithmetic and copies ran while one was open for 29% -> 26% of each run, Pallas kernels for 0% -> 0%
where the time goes in v28:
time: 55.6 us; the launch traced here: 55.2 us
  waiting for transfers between devices  20.2 us (36%)
  matrix products  13.7 us (25%)
  starting transfers between devices  11.9 us (21%)
  other arithmetic  4.69 us (8%)
  local copies, waits for them, and re-layouts  4.03 us (7%)
  between operations  0.74 us (1%)
    ppermute x11, waiting for transfers between devices, swap(): return lax.ppermute(x, axis, [(i, i ^ 1 << stride) for i in range(n)])  20.2 us
    ppermute x11, starting transfers between devices, swap(): return lax.ppermute(x, axis, [(i, i ^ 1 << stride) for i in range(n)])  11.9 us
    dot_general x3, matrix products, project(): jnp.einsum('lrj,jt->lrt', vl_lo[lv], x, preferred_element_type=F32)  3.79 us
    dot_general x4, matrix products, on_device(): coefs = jnp.dot(couple[s], stacked, preferred_element_type=F32).astype(BF16)  2.01 us
    dot_general x1, matrix products, on_device(): c0 = jnp.dot(leaf_inverse, templates, preferred_element_type=F32)  1.83 us
    concatenate x2, other arithmetic, gather_half(): both = jnp.concatenate([x, swap(x, bit, bits), x], axis=-1)  1.79 us
    dot_general x4, matrix products, on_device(): current = current - jnp.dot(u_basis[s], full[s], preferred_element_type=F32)  1.73 us
    slice x4, local copies, waits for them, and re-layouts, on_device(): theirs_c.append(jnp.concatenate([theirs[:rank], theirs[rank:]], axis=1))  1.69 us
  transfers between devices with their start and end apart: 11, of which 6 were waited for; matrix products, arithmetic and copies ran while one was open for 26% of the time, Pallas kernels for 0%

profile of v28, /device:TPU:0, one launch (start us, length us, event | category | flops | bytes accessed | tf_op | source)
XLA Modules:
  0.0 55.2 jit_solution(2505782334135882237)
XLA Ops:
  0.0 1.1 %slice_bitcast_fusion.12 = (bf16[128,256]{1,0:T(8,128)(2,1)S(1)}, bf16[128,256]{1,0:T(8,128)(2,1)S(1)}, bf16[128,256]{1,0:T(8,128)(2,1)S(1)}, bf16[128,256]{1,0:T(8,128)(2,1)S(1)}) fusion(bf16[4,1,128,256]{3,2,1,0:T(8,128)(2,1)} %param.9), kind=kLoop, calls=%fused_computation.166 | loop fusion | bytes 524288 | tf_op jit(solution)/shard_map/squeeze | solution.py:85
  1.2 0.6 %maximum_convert_fusion.3 = bf16[256,128]{1,0:T(8,128)(2,1)} fusion(bf16[128,128]{1,0:T(8,128)(2,1)S(1)} %get-tuple-element.42, bf16[128,128]{1,0:T(8,128)(2,1)S(1)} %get-tuple-element.41), kind=kLoop, calls=%fused_computation.164 | loop fusion | flops 131072 | bytes 131072 | tf_op jit(solution)/shard_map/convert_element_type | solution.py:64
  1.8 4.0 %collective-permute-start.7 = (bf16[256,128]{1,0:T(8,128)(2,1)}, bf16[256,128]{1,0:T(8,128)(2,1)}, u32[]{:S(2)}, u32[]{:S(2)}) collective-permute-start(bf16[256,128]{1,0:T(8,128)(2,1)} %maximum_convert_fusion.3), channel_id=1, source_target_pairs={{0,8},{4,12},{8,0},{12,4},{1,9},{5,13},{9,1},{13,5},{2,10},{6,14},... | collective-permute-start | bytes 196616 | tf_op jit(solution)/shard_map/ppermute | solution.py:21
  7.1 0.8 %pad_maximum_fusion = f32[1024,128]{1,0:T(8,128)} fusion(f32[128,128]{1,0:T(8,128)S(1)} %fusion.80, f32[256,128]{1,0:T(8,128)S(1)} %fusion.84, f32[384,128]{1,0:T(8,128)S(1)} %fusion.87, f32[256,128]{1,0:T(8,128)S(1)} %maximum_convert_fusion), kind=kLoop, calls=%fused_computation.28 | loop fusion | flops 393216 | bytes 1048576 | tf_op jit(solution)/shard_map/concatenate | solution.py:66
  7.9 1.5 %subtract_convert_fusion = (bf16[4,128,512]{2,1,0:T(8,128)(2,1)S(1)}, bf16[4,128,512]{2,1,0:T(8,128)(2,1)S(1)}) fusion(bf16[4,512,128]{2,1,0:T(8,128)(2,1)S(1)} %copy-done.1, bf16[512,512]{1,0:T(8,128)(2,1)} %param.6), kind=kOutput, calls=%fused_computation.23 | convolution fusion | flops 269484032 | bytes 2097152 | tf_op jit(solution)/shard_map/lir,ij->lrj/dot_general | solution.py:95
  9.8 1.0 %fusion.3 = bf16[128,1024]{1,0:T(8,128)(2,1)} fusion(f32[128,1024]{1,0:T(8,128)S(1)} %fusion.64, bf16[512,1024]{1,0:T(8,128)(2,1)S(1)} %copy-done, bf16[4,128,512]{2,1,0:T(8,128)(2,1)S(1)} %get-tuple-element.5), kind=kOutput, calls=%fused_computation.11 | convolution fusion | flops 134479872 | bytes 1966080 | tf_op jit(solution)/shard_map/lrj,jt->lrt/dot_general | solution.py:102
  11.7 1.3 %convolution_add_fusion = f32[3,128,512]{2,1,0:T(8,128)} fusion(f32[3,128,512]{2,1,0:T(8,128)S(1)} %fusion.15, bf16[4,128,512]{2,1,0:T(8,128)(2,1)S(1)} %get-tuple-element.5, bf16[512,1024]{1,0:T(8,128)(2,1)S(1)} %copy-done, s32[]{:T(128)S(6)} %select_n.69), kind=kOutput, calls=%fused_computation.6 | convolution fusion | flops 201523200 | bytes 2621444 | tf_op jit(solution)/shard_map/lrj,jt->lrt/dot_general | solution.py:102
  13.4 0.8 %fusion.135 = (bf16[128,128]{1,0:T(8,128)(2,1)S(1)}, bf16[128,128]{1,0:T(8,128)(2,1)S(1)}) fusion(bf16[256,128]{1,0:T(8,128)(2,1)} %collective-permute-done.7), kind=kLoop, calls=%fused_computation.206 | loop fusion | bytes 131072 | tf_op jit(solution)/shard_map/slice | solution.py:68
  14.2 1.1 %fusion.127 = (f32[384,128]{1,0:T(8,128)S(1)}, f32[384,128]{1,0:T(8,128)S(1)}) fusion(f32[1024,128]{1,0:T(8,128)} %collective-permute-done, f32[128,128]{1,0:T(8,128)S(1)} %fusion.80, f32[256,128]{1,0:T(8,128)S(1)} %fusion.84), kind=kLoop, calls=%fused_computation.198 | loop fusion | flops 98304 | bytes 983040 | tf_op jit(solution)/shard_map/slice | solution.py:72
  15.4 1.6 %collective-permute-start.2 = (f32[640,128]{1,0:T(8,128)S(1)}, f32[640,128]{1,0:T(8,128)S(1)}, u32[]{:S(2)}, u32[]{:S(2)}) collective-permute-start(f32[640,128]{1,0:T(8,128)S(1)} %pad_maximum_fusion.2), channel_id=1, source_target_pairs={{0,2},{2,0},{1,3},{3,1},{4,6},{6,4},{5,7},{7,5},{8,10},{10,8},{9,1... | collective-permute-start | bytes 983048 | tf_op jit(solution)/shard_map/ppermute | solution.py:21
  16.9 0.9 %fusion.126 = (bf16[128,128]{1,0:T(8,128)(2,1)S(1)}, bf16[128,128]{1,0:T(8,128)(2,1)S(1)}) fusion(f32[1024,128]{1,0:T(8,128)} %collective-permute-done), kind=kLoop, calls=%fused_computation.197 | loop fusion | bytes 131072 | tf_op jit(solution)/shard_map/slice | solution.py:68
  17.9 1.3 %convolution_convert_fusion = bf16[256,1024]{1,0:T(8,128)(2,1)S(1)} fusion(bf16[128,1024]{1,0:T(8,128)(2,1)} %collective-permute-done.1, bf16[128,1024]{1,0:T(8,128)(2,1)} %fusion.3, bf16[256,128]{1,0:T(8,128)(2,1)S(1)} %get-tuple-element.34, bf16[256,128]{1,0:T(8,128)(2,1)S(1)} %get-tuple-element.33), kind=kOutput, calls=%fused_computation.5 | convolution fusion | flops 135528448 | bytes 1179648 | tf_op jit(solution)/shard_map/dot_general | solution.py:141
  20.0 1.5 %fusion.2 = f32[3,128,512]{2,1,0:T(8,128)S(1)} fusion(f32[3,128,512]{2,1,0:T(8,128)S(1)} %bitcast.124, f32[3,128,512]{2,1,0:T(8,128)} %collective-permute-done.3, f32[3,128,512]{2,1,0:T(8,128)S(1)} %fusion.18, bf16[4,128,512]{2,1,0:T(8,128)(2,1)S(1)} %get-tuple-element.5, bf16[512,1024]{1,0:T(8,128)(2,1)S(1)} %copy-done, s32[]{:T(128)S(6)} %select_n.68), kind=kOutput, calls=%fused_computation.9 | convolution fusion | flops 201916416 | bytes 4194308 | tf_op jit(solution)/shard_map/lrj,jt->lrt/dot_general | solution.py:102
  22.3 3.6 %collective-permute-done.2 = f32[640,128]{1,0:T(8,128)S(1)} collective-permute-done((f32[640,128]{1,0:T(8,128)S(1)}, f32[640,128]{1,0:T(8,128)S(1)}, u32[]{:S(2)}, u32[]{:S(2)}) %collective-permute-start.2) | collective-permute-done | bytes 327712 | tf_op jit(solution)/shard_map/ppermute | solution.py:21
  26.0 1.6 %collective-permute-start.5 = (f32[384,128]{1,0:T(8,128)S(1)}, f32[384,128]{1,0:T(8,128)S(1)}, u32[]{:S(2)}, u32[]{:S(2)}) collective-permute-start(f32[384,128]{1,0:T(8,128)S(1)} %pad_maximum_fusion.4), channel_id=1, source_target_pairs={{0,4},{4,0},{8,12},{12,8},{1,5},{5,1},{9,13},{13,9},{2,6},{6,2},{1... | collective-permute-start | bytes 589832 | tf_op jit(solution)/shard_map/ppermute | solution.py:21
  27.7 3.5 %collective-permute-done.4 = bf16[512,256]{1,0:T(8,128)(2,1)S(1)} collective-permute-done((bf16[512,256]{1,0:T(8,128)(2,1)S(1)}, bf16[512,256]{1,0:T(8,128)(2,1)S(1)}, u32[]{:S(2)}, u32[]{:S(2)}) %collective-permute-start.4) | collective-permute-done | bytes 262176 | tf_op jit(solution)/shard_map/ppermute | solution.py:21
  31.9 1.6 %collective-permute-start.6 = (bf16[512,128]{1,0:T(8,128)(2,1)S(1)}, bf16[512,128]{1,0:T(8,128)(2,1)S(1)}, u32[]{:S(2)}, u32[]{:S(2)}) collective-permute-start(bf16[512,128]{1,0:T(8,128)(2,1)S(1)} %pad_maximum_fusion.11), channel_id=1, source_target_pairs={{0,4},{4,0},{8,12},{12,8},{1,5},{5,1},{9,13},{13,9},{2,6},{6,2},{1... | collective-permute-start | bytes 393224 | tf_op jit(solution)/shard_map/ppermute | solution.py:21
  33.6 3.5 %collective-permute-done.6 = bf16[512,128]{1,0:T(8,128)(2,1)S(1)} collective-permute-done((bf16[512,128]{1,0:T(8,128)(2,1)S(1)}, bf16[512,128]{1,0:T(8,128)(2,1)S(1)}, u32[]{:S(2)}, u32[]{:S(2)}) %collective-permute-start.6) | collective-permute-done | bytes 131104 | tf_op jit(solution)/shard_map/ppermute | solution.py:21
  37.9 5.0 %collective-permute-done.8 = bf16[256,128]{1,0:T(8,128)(2,1)S(1)} collective-permute-done((bf16[256,128]{1,0:T(8,128)(2,1)S(1)}, bf16[256,128]{1,0:T(8,128)(2,1)S(1)}, u32[]{:S(2)}, u32[]{:S(2)}) %collective-permute-start.8) | collective-permute-done | bytes 65568 | tf_op jit(solution)/shard_map/ppermute | solution.py:21
  43.2 1.5 %collective-permute-start.9 = (bf16[2,128,256]{1,2,0:T(8,128)(2,1)S(1)}, bf16[2,128,256]{1,2,0:T(8,128)(2,1)S(1)}, u32[]{:S(2)}, u32[]{:S(2)}) collective-permute-start(bf16[2,128,256]{1,2,0:T(8,128)(2,1)S(1)} %pad_maximum_fusion.14), channel_id=1, source_target_pairs={{0,2},{2,0},{1,3},{3,1},{4,6},{6,4},{5,7},{7,5},{8,10},{10,8},{9,1... | collective-permute-start | bytes 393224 | tf_op jit(solution)/shard_map/ppermute | solution.py:21
  44.8 3.4 %collective-permute-done.9 = bf16[2,128,256]{1,2,0:T(8,128)(2,1)S(1)} collective-permute-done((bf16[2,128,256]{1,2,0:T(8,128)(2,1)S(1)}, bf16[2,128,256]{1,2,0:T(8,128)(2,1)S(1)}, u32[]{:S(2)}, u32[]{:S(2)}) %collective-permute-start.9) | collective-permute-done | bytes 131104 | tf_op jit(solution)/shard_map/ppermute | solution.py:21
  49.4 1.3 %collective-permute-done.10 = bf16[3,128,512]{1,2,0:T(8,128)(2,1)S(1)} collective-permute-done((bf16[3,128,512]{1,2,0:T(8,128)(2,1)S(1)}, bf16[3,128,512]{1,2,0:T(8,128)(2,1)S(1)}, u32[]{:S(2)}, u32[]{:S(2)}) %collective-permute-start.10) | collective-permute-done | bytes 393248 | tf_op jit(solution)/shard_map/ppermute | solution.py:21
  50.6 1.2 %fusion.9 = bf16[3,128,1024]{1,2,0:T(8,128)(2,1)S(1)} fusion(s32[]{:T(128)S(6)} %select_n.79, bf16[1,128,512]{1,2,0:T(8,128)(2,1)S(1)} %copy.16, bf16[2,128,512]{1,2,0:T(8,128)(2,1)S(1)} %fusion.32, bf16[3,128,512]{1,2,0:T(8,128)(2,1)S(1)} %collective-permute-done.10), kind=kLoop, calls=%fused_computation.26 | loop fusion | flops 3932160 | bytes 1572868 | tf_op jit(solution)/shard_map/concatenate | solution.py:44
  53.3 1.8 %fusion = bf16[512,1024]{1,0:T(8,128)(2,1)} fusion(f32[1024,512]{0,1:T(8,128)S(1)} %fusion.34, f32[1024,512]{0,1:T(8,128)S(1)} %fusion.35, f32[1024,512]{0,1:T(8,128)S(1)} %fusion.36, f32[1024,512]{0,1:T(8,128)S(1)} %fusion.37, bf16[512,512]{1,0:T(8,128)(2,1)S(1)} %copy-done.2, bf16[512,1024]{1,0:T(8,128)(2,1)S(1)} %copy-done), kind=kOutput, calls=%fused_computation.1 | convolution fusion | flops 539492352 | bytes 11010048 | tf_op jit(solution)/shard_map/dot_general | solution.py:52
  (111 shorter events, 8.9 us)
Async XLA Ops:
  0.0 9.4 %copy-start = (bf16[512,1024]{1,0:T(8,128)(2,1)S(1)}, bf16[512,1024]{1,0:T(8,128)(2,1)}, u32[]{:S(2)}) copy-start(bf16[512,1024]{1,0:T(8,128)(2,1)} %param.5) | copy-start | bytes 3145732
  0.0 5.9 %copy-start.1 = (bf16[4,512,128]{2,1,0:T(8,128)(2,1)S(1)}, bf16[4,512,128]{2,1,0:T(8,128)(2,1)}, u32[]{:S(2)}) copy-start(bf16[4,512,128]{2,1,0:T(8,128)(2,1)} %param.7) | copy-start | bytes 1572868
  0.0 6.1 %slice-start = ((bf16[4,512,128]{2,1,0:T(8,128)(2,1)}), bf16[2,512,128]{2,1,0:T(8,128)(2,1)S(1)}, s32[]{:S(2)}) async-start(bf16[4,512,128]{2,1,0:T(8,128)(2,1)} %param.7), calls=%async_computation | async-start | bytes 524288 | tf_op jit(solution)/shard_map/slice | solution.py:57
  0.0 6.5 %slice-start.1 = ((bf16[4,512,128]{2,1,0:T(8,128)(2,1)}), bf16[3,512,128]{2,1,0:T(8,128)(2,1)S(1)}, s32[]{:S(2)}) async-start(bf16[4,512,128]{2,1,0:T(8,128)(2,1)} %param.7), calls=%async_computation.1 | async-start | bytes 786432 | tf_op jit(solution)/shard_map/slice | solution.py:57
  0.0 5.9 %copy-start.3 = (bf16[4,512,128]{2,1,0:T(8,128)(2,1)S(1)}, bf16[4,512,128]{2,1,0:T(8,128)(2,1)}, u32[]{:S(2)}) copy-start(bf16[4,512,128]{2,1,0:T(8,128)(2,1)} %param.8) | copy-start | bytes 1572868
  1.2 5.1 %copy-start.15 = (bf16[128,128]{1,0:T(8,128)(2,1)}, bf16[128,128]{1,0:T(8,128)(2,1)S(1)}, u32[]{:S(2)}) copy-start(bf16[128,128]{1,0:T(8,128)(2,1)S(1)} %get-tuple-element.41) | copy-start | bytes 98308
  1.2 5.1 %copy-start.17 = (bf16[128,128]{1,0:T(8,128)(2,1)}, bf16[128,128]{1,0:T(8,128)(2,1)S(1)}, u32[]{:S(2)}) copy-start(bf16[128,128]{1,0:T(8,128)(2,1)S(1)} %get-tuple-element.42) | copy-start | bytes 98308
  1.8 11.6 %collective-permute-start.7 = (bf16[256,128]{1,0:T(8,128)(2,1)}, bf16[256,128]{1,0:T(8,128)(2,1)}, u32[]{:S(2)}, u32[]{:S(2)}) collective-permute-start(bf16[256,128]{1,0:T(8,128)(2,1)} %maximum_convert_fusion.3), channel_id=1, source_target_pairs={{0,8},{4,12},{8,0},{12,4},{1,9},{5,13},{9,1},{13,5},{2,10},{6,14},... | collective-permute-start | bytes 196616 | tf_op jit(solution)/shard_map/ppermute | solution.py:21
  7.0 6.3 %copy-start.7 = (bf16[128,128]{1,0:T(8,128)(2,1)}, bf16[128,128]{1,0:T(8,128)(2,1)S(1)}, u32[]{:S(2)}) copy-start(bf16[128,128]{1,0:T(8,128)(2,1)S(1)} %get-tuple-element.67) | copy-start | bytes 98308
  7.0 6.3 %copy-start.9 = (bf16[128,128]{1,0:T(8,128)(2,1)}, bf16[128,128]{1,0:T(8,128)(2,1)S(1)}, u32[]{:S(2)}) copy-start(bf16[128,128]{1,0:T(8,128)(2,1)S(1)} %get-tuple-element.68) | copy-start | bytes 98308
  7.9 6.3 %collective-permute-start = (f32[1024,128]{1,0:T(8,128)}, f32[1024,128]{1,0:T(8,128)}, u32[]{:S(2)}, u32[]{:S(2)}) collective-permute-start(f32[1024,128]{1,0:T(8,128)} %pad_maximum_fusion), channel_id=1, source_target_pairs={{0,1},{1,0},{2,3},{3,2},{4,5},{5,4},{6,7},{7,6},{8,9},{9,8},{10,11... | collective-permute-start | bytes 1572872 | tf_op jit(solution)/shard_map/ppermute | solution.py:21
  10.8 7.1 %collective-permute-start.1 = (bf16[128,1024]{1,0:T(8,128)(2,1)}, bf16[128,1024]{1,0:T(8,128)(2,1)}, u32[]{:S(2)}, u32[]{:S(2)}) collective-permute-start(bf16[128,1024]{1,0:T(8,128)(2,1)} %fusion.3), channel_id=1, source_target_pairs={{0,1},{1,0},{2,3},{3,2},{4,5},{5,4},{6,7},{7,6},{8,9},{9,8},{10,11... | collective-permute-start | bytes 786440 | tf_op jit(solution)/shard_map/ppermute | solution.py:21
  12.9 6.8 %collective-permute-start.3 = (f32[3,128,512]{2,1,0:T(8,128)}, f32[3,128,512]{2,1,0:T(8,128)}, u32[]{:S(2)}, u32[]{:S(2)}) collective-permute-start(f32[3,128,512]{2,1,0:T(8,128)} %convolution_add_fusion), channel_id=1, source_target_pairs={{0,1},{1,0},{2,3},{3,2},{4,5},{5,4},{6,7},{7,6},{8,9},{9,8},{10,11... | collective-permute-start | bytes 2359304 | tf_op jit(solution)/shard_map/ppermute | solution.py:21
  15.4 10.6 %collective-permute-start.2 = (f32[640,128]{1,0:T(8,128)S(1)}, f32[640,128]{1,0:T(8,128)S(1)}, u32[]{:S(2)}, u32[]{:S(2)}) collective-permute-start(f32[640,128]{1,0:T(8,128)S(1)} %pad_maximum_fusion.2), channel_id=1, source_target_pairs={{0,2},{2,0},{1,3},{3,1},{4,6},{6,4},{5,7},{7,5},{8,10},{10,8},{9,1... | collective-permute-start | bytes 983048 | tf_op jit(solution)/shard_map/ppermute | solution.py:21
  21.5 6.1 %copy-start.8 = (bf16[128,128]{1,0:T(8,128)(2,1)S(1)}, bf16[128,128]{1,0:T(8,128)(2,1)}, u32[]{:S(2)}) copy-start(bf16[128,128]{1,0:T(8,128)(2,1)} %copy-done.7) | copy-start | bytes 98308
  21.5 6.1 %copy-start.10 = (bf16[128,128]{1,0:T(8,128)(2,1)S(1)}, bf16[128,128]{1,0:T(8,128)(2,1)}, u32[]{:S(2)}) copy-start(bf16[128,128]{1,0:T(8,128)(2,1)} %copy-done.9) | copy-start | bytes 98308
  21.7 9.5 %collective-permute-start.4 = (bf16[512,256]{1,0:T(8,128)(2,1)S(1)}, bf16[512,256]{1,0:T(8,128)(2,1)S(1)}, u32[]{:S(2)}, u32[]{:S(2)}) collective-permute-start(bf16[512,256]{1,0:T(8,128)(2,1)S(1)} %pad_maximum_fusion.3), channel_id=1, source_target_pairs={{0,2},{2,0},{1,3},{3,1},{4,6},{6,4},{5,7},{7,5},{8,10},{10,8},{9,1... | collective-permute-start | bytes 786440 | tf_op jit(solution)/shard_map/ppermute | solution.py:21
  26.0 7.5 %collective-permute-start.5 = (f32[384,128]{1,0:T(8,128)S(1)}, f32[384,128]{1,0:T(8,128)S(1)}, u32[]{:S(2)}, u32[]{:S(2)}) collective-permute-start(f32[384,128]{1,0:T(8,128)S(1)} %pad_maximum_fusion.4), channel_id=1, source_target_pairs={{0,4},{4,0},{8,12},{12,8},{1,5},{5,1},{9,13},{13,9},{2,6},{6,2},{1... | collective-permute-start | bytes 589832 | tf_op jit(solution)/shard_map/ppermute | solution.py:21
  31.9 5.2 %collective-permute-start.6 = (bf16[512,128]{1,0:T(8,128)(2,1)S(1)}, bf16[512,128]{1,0:T(8,128)(2,1)S(1)}, u32[]{:S(2)}, u32[]{:S(2)}) collective-permute-start(bf16[512,128]{1,0:T(8,128)(2,1)S(1)} %pad_maximum_fusion.11), channel_id=1, source_target_pairs={{0,4},{4,0},{8,12},{12,8},{1,5},{5,1},{9,13},{13,9},{2,6},{6,2},{1... | collective-permute-start | bytes 393224 | tf_op jit(solution)/shard_map/ppermute | solution.py:21
  37.1 11.9 %copy-start.4 = (bf16[4,512,128]{2,1,0:T(8,128)(2,1)S(1)}, bf16[4,512,128]{2,1,0:T(8,128)(2,1)}, u32[]{:S(2)}) copy-start(bf16[4,512,128]{2,1,0:T(8,128)(2,1)} %param.8) | copy-start | bytes 1572868
  37.1 11.9 %copy-start.6 = (bf16[256,1024]{1,0:T(8,128)(2,1)S(1)}, bf16[256,1024]{1,0:T(8,128)(2,1)}, u32[]{:S(2)}) copy-start(bf16[256,1024]{1,0:T(8,128)(2,1)} %copy-done.5) | copy-start | bytes 1572868
  37.7 5.2 %collective-permute-start.8 = (bf16[256,128]{1,0:T(8,128)(2,1)S(1)}, bf16[256,128]{1,0:T(8,128)(2,1)S(1)}, u32[]{:S(2)}, u32[]{:S(2)}) collective-permute-start(bf16[256,128]{1,0:T(8,128)(2,1)S(1)} %pad_maximum_fusion.15), channel_id=1, source_target_pairs={{0,8},{4,12},{8,0},{12,4},{1,9},{5,13},{9,1},{13,5},{2,10},{6,14},... | collective-permute-start | bytes 196616 | tf_op jit(solution)/shard_map/ppermute | solution.py:21
  43.2 5.0 %collective-permute-start.9 = (bf16[2,128,256]{1,2,0:T(8,128)(2,1)S(1)}, bf16[2,128,256]{1,2,0:T(8,128)(2,1)S(1)}, u32[]{:S(2)}, u32[]{:S(2)}) collective-permute-start(bf16[2,128,256]{1,2,0:T(8,128)(2,1)S(1)} %pad_maximum_fusion.14), channel_id=1, source_target_pairs={{0,2},{2,0},{1,3},{3,1},{4,6},{6,4},{5,7},{7,5},{8,10},{10,8},{9,1... | collective-permute-start | bytes 393224 | tf_op jit(solution)/shard_map/ppermute | solution.py:21
  48.8 1.8 %collective-permute-start.10 = (bf16[3,128,512]{1,2,0:T(8,128)(2,1)S(1)}, bf16[3,128,512]{1,2,0:T(8,128)(2,1)S(1)}, u32[]{:S(2)}, u32[]{:S(2)}) collective-permute-start(bf16[3,128,512]{1,2,0:T(8,128)(2,1)S(1)} %pad_maximum_fusion.1), channel_id=1, source_target_pairs={{0,1},{1,0},{2,3},{3,2},{4,5},{5,4},{6,7},{7,6},{8,9},{9,8},{10,11... | collective-permute-start | bytes 1179656 | tf_op jit(solution)/shard_map/ppermute | solution.py:21
  (8 other events, 21.4 us)

commit v29 on v28

--- a/solution.py
+++ b/solution.py
@@ -61,19 +61,20 @@
     w_own, theirs_c = [None] * levels, []
     for b in range(levels):
         c = mine_c[b]
-        parts = [jnp.concatenate([c[:, :rank], c[:, rank:]], axis=0).astype(F32)]
-        parts += partial[b:]
+        parts = list(partial[b:])
+        parts.append(jnp.concatenate([c[:, :rank], c[:, rank:]], axis=0).astype(F32))
         got = swap(jnp.concatenate(parts, axis=0), b, bits)
-        theirs = got[: 2 * rank]
+        theirs = got[got.shape[0] - 2 * rank :]
+        got = got[: got.shape[0] - 2 * rank]
         theirs_c.append(jnp.concatenate([theirs[:rank], theirs[rank:]], axis=1))
         if b < levels - 1:
             n = partial[b].shape[0]
             w_own[b] = jnp.concatenate(
-                [partial[b], got[2 * rank : 2 * rank + n]], axis=1
+                [partial[b], got[:n]], axis=1
             )
             if b + 1 < levels - 1:
                 later = jnp.concatenate(partial[b + 1 :], axis=0)
-                later = later + got[2 * rank + n :]
+                later = later + got[n:]
                 at = 0
                 for s in range(b + 1, levels - 1):
                     k = partial[s].shape[0]

time: 55.6 us -> 55.6 us (level)
  no operation moved by 1% of the time
where the time goes in v29:
time: 55.6 us; the launch traced here: 55.2 us
  waiting for transfers between devices  20.1 us (36%)
  matrix products  13.6 us (24%)
  starting transfers between devices  11.9 us (21%)
  other arithmetic  4.69 us (8%)
  local copies, waits for them, and re-layouts  4.04 us (7%)
  between operations  0.74 us (1%)
    ppermute x11, waiting for transfers between devices, swap(): return lax.ppermute(x, axis, [(i, i ^ 1 << stride) for i in range(n)])  20.1 us
    ppermute x11, starting transfers between devices, swap(): return lax.ppermute(x, axis, [(i, i ^ 1 << stride) for i in range(n)])  11.9 us
    dot_general x3, matrix products, project(): jnp.einsum('lrj,jt->lrt', vl_lo[lv], x, preferred_element_type=F32)  3.79 us
    dot_general x4, matrix products, on_device(): coefs = jnp.dot(couple[s], stacked, preferred_element_type=F32).astype(BF16)  2.01 us
    dot_general x1, matrix products, on_device(): c0 = jnp.dot(leaf_inverse, templates, preferred_element_type=F32)  1.83 us
    concatenate x2, other arithmetic, gather_half(): both = jnp.concatenate([x, swap(x, bit, bits), x], axis=-1)  1.79 us
    dot_general x4, matrix products, on_device(): current = current - jnp.dot(u_basis[s], full[s], preferred_element_type=F32)  1.73 us
    slice x4, local copies, waits for them, and re-layouts, on_device(): theirs_c.append(jnp.concatenate([theirs[:rank], theirs[rank:]], axis=1))  1.69 us
  transfers between devices with their start and end apart: 11, of which 6 were waited for; matrix products, arithmetic and copies ran while one was open for 26% of the time, Pallas kernels for 0%

profile of v29, /device:TPU:0, one launch (start us, length us, event | category | flops | bytes accessed | tf_op | source)
XLA Modules:
  0.0 55.2 jit_solution(12742477353215145048)
XLA Ops:
  0.0 1.1 %slice_bitcast_fusion.12 = (bf16[128,256]{1,0:T(8,128)(2,1)S(1)}, bf16[128,256]{1,0:T(8,128)(2,1)S(1)}, bf16[128,256]{1,0:T(8,128)(2,1)S(1)}, bf16[128,256]{1,0:T(8,128)(2,1)S(1)}) fusion(bf16[4,1,128,256]{3,2,1,0:T(8,128)(2,1)} %param.9), kind=kLoop, calls=%fused_computation.166 | loop fusion | bytes 524288 | tf_op jit(solution)/shard_map/squeeze | solution.py:86
  1.2 0.6 %maximum_convert_fusion.3 = bf16[256,128]{1,0:T(8,128)(2,1)} fusion(bf16[128,128]{1,0:T(8,128)(2,1)S(1)} %get-tuple-element.42, bf16[128,128]{1,0:T(8,128)(2,1)S(1)} %get-tuple-element.41), kind=kLoop, calls=%fused_computation.164 | loop fusion | flops 131072 | bytes 131072 | tf_op jit(solution)/shard_map/convert_element_type | solution.py:65
  1.8 4.0 %collective-permute-start.7 = (bf16[256,128]{1,0:T(8,128)(2,1)}, bf16[256,128]{1,0:T(8,128)(2,1)}, u32[]{:S(2)}, u32[]{:S(2)}) collective-permute-start(bf16[256,128]{1,0:T(8,128)(2,1)} %maximum_convert_fusion.3), channel_id=1, source_target_pairs={{0,8},{4,12},{8,0},{12,4},{1,9},{5,13},{9,1},{13,5},{2,10},{6,14},... | collective-permute-start | bytes 196616 | tf_op jit(solution)/shard_map/ppermute | solution.py:21
  7.1 0.8 %pad_maximum_fusion = f32[1024,128]{1,0:T(8,128)} fusion(f32[256,128]{1,0:T(8,128)S(1)} %maximum_convert_fusion, f32[128,128]{1,0:T(8,128)S(1)} %fusion.80, f32[256,128]{1,0:T(8,128)S(1)} %fusion.84, f32[384,128]{1,0:T(8,128)S(1)} %fusion.87), kind=kLoop, calls=%fused_computation.28 | loop fusion | flops 393216 | bytes 1048576 | tf_op jit(solution)/shard_map/concatenate | solution.py:66
  7.9 1.5 %subtract_convert_fusion = (bf16[4,128,512]{2,1,0:T(8,128)(2,1)S(1)}, bf16[4,128,512]{2,1,0:T(8,128)(2,1)S(1)}) fusion(bf16[4,512,128]{2,1,0:T(8,128)(2,1)S(1)} %copy-done.1, bf16[512,512]{1,0:T(8,128)(2,1)} %param.6), kind=kOutput, calls=%fused_computation.23 | convolution fusion | flops 269484032 | bytes 2097152 | tf_op jit(solution)/shard_map/lir,ij->lrj/dot_general | solution.py:96
  9.8 1.0 %fusion.3 = bf16[128,1024]{1,0:T(8,128)(2,1)} fusion(f32[128,1024]{1,0:T(8,128)S(1)} %fusion.64, bf16[512,1024]{1,0:T(8,128)(2,1)S(1)} %copy-done, bf16[4,128,512]{2,1,0:T(8,128)(2,1)S(1)} %get-tuple-element.5), kind=kOutput, calls=%fused_computation.11 | convolution fusion | flops 134479872 | bytes 1966080 | tf_op jit(solution)/shard_map/lrj,jt->lrt/dot_general | solution.py:103
  11.7 1.3 %convolution_add_fusion = f32[3,128,512]{2,1,0:T(8,128)} fusion(f32[3,128,512]{2,1,0:T(8,128)S(1)} %fusion.15, bf16[4,128,512]{2,1,0:T(8,128)(2,1)S(1)} %get-tuple-element.5, bf16[512,1024]{1,0:T(8,128)(2,1)S(1)} %copy-done, s32[]{:T(128)S(6)} %select_n.69), kind=kOutput, calls=%fused_computation.6 | convolution fusion | flops 201523200 | bytes 2621444 | tf_op jit(solution)/shard_map/lrj,jt->lrt/dot_general | solution.py:103
  13.4 0.8 %fusion.135 = (bf16[128,128]{1,0:T(8,128)(2,1)S(1)}, bf16[128,128]{1,0:T(8,128)(2,1)S(1)}) fusion(bf16[256,128]{1,0:T(8,128)(2,1)} %collective-permute-done.7), kind=kLoop, calls=%fused_computation.206 | loop fusion | bytes 131072 | tf_op jit(solution)/shard_map/slice | solution.py:69
  14.2 1.1 %fusion.127 = (f32[384,128]{1,0:T(8,128)S(1)}, f32[384,128]{1,0:T(8,128)S(1)}) fusion(f32[1024,128]{1,0:T(8,128)} %collective-permute-done, f32[128,128]{1,0:T(8,128)S(1)} %fusion.80, f32[256,128]{1,0:T(8,128)S(1)} %fusion.84), kind=kLoop, calls=%fused_computation.198 | loop fusion | flops 98304 | bytes 983040 | tf_op jit(solution)/shard_map/slice | solution.py:73
  15.4 1.6 %collective-permute-start.2 = (f32[640,128]{1,0:T(8,128)S(1)}, f32[640,128]{1,0:T(8,128)S(1)}, u32[]{:S(2)}, u32[]{:S(2)}) collective-permute-start(f32[640,128]{1,0:T(8,128)S(1)} %pad_maximum_fusion.2), channel_id=1, source_target_pairs={{0,2},{2,0},{1,3},{3,1},{4,6},{6,4},{5,7},{7,5},{8,10},{10,8},{9,1... | collective-permute-start | bytes 983048 | tf_op jit(solution)/shard_map/ppermute | solution.py:21
  16.9 0.9 %fusion.126 = (bf16[128,128]{1,0:T(8,128)(2,1)S(1)}, bf16[128,128]{1,0:T(8,128)(2,1)S(1)}) fusion(f32[1024,128]{1,0:T(8,128)} %collective-permute-done), kind=kLoop, calls=%fused_computation.197 | loop fusion | bytes 131072 | tf_op jit(solution)/shard_map/slice | solution.py:69
  17.9 1.3 %convolution_convert_fusion = bf16[256,1024]{1,0:T(8,128)(2,1)S(1)} fusion(bf16[128,1024]{1,0:T(8,128)(2,1)} %collective-permute-done.1, bf16[128,1024]{1,0:T(8,128)(2,1)} %fusion.3, bf16[256,128]{1,0:T(8,128)(2,1)S(1)} %get-tuple-element.34, bf16[256,128]{1,0:T(8,128)(2,1)S(1)} %get-tuple-element.33), kind=kOutput, calls=%fused_computation.5 | convolution fusion | flops 135528448 | bytes 1179648 | tf_op jit(solution)/shard_map/dot_general | solution.py:142
  20.0 1.5 %fusion.2 = f32[3,128,512]{2,1,0:T(8,128)S(1)} fusion(f32[3,128,512]{2,1,0:T(8,128)S(1)} %bitcast.124, f32[3,128,512]{2,1,0:T(8,128)} %collective-permute-done.3, f32[3,128,512]{2,1,0:T(8,128)S(1)} %fusion.18, bf16[4,128,512]{2,1,0:T(8,128)(2,1)S(1)} %get-tuple-element.5, bf16[512,1024]{1,0:T(8,128)(2,1)S(1)} %copy-done, s32[]{:T(128)S(6)} %select_n.68), kind=kOutput, calls=%fused_computation.9 | convolution fusion | flops 201916416 | bytes 4194308 | tf_op jit(solution)/shard_map/lrj,jt->lrt/dot_general | solution.py:103
  22.3 3.6 %collective-permute-done.2 = f32[640,128]{1,0:T(8,128)S(1)} collective-permute-done((f32[640,128]{1,0:T(8,128)S(1)}, f32[640,128]{1,0:T(8,128)S(1)}, u32[]{:S(2)}, u32[]{:S(2)}) %collective-permute-start.2) | collective-permute-done | bytes 327712 | tf_op jit(solution)/shard_map/ppermute | solution.py:21
  26.0 1.6 %collective-permute-start.5 = (f32[384,128]{1,0:T(8,128)S(1)}, f32[384,128]{1,0:T(8,128)S(1)}, u32[]{:S(2)}, u32[]{:S(2)}) collective-permute-start(f32[384,128]{1,0:T(8,128)S(1)} %pad_maximum_fusion.4), channel_id=1, source_target_pairs={{0,4},{4,0},{8,12},{12,8},{1,5},{5,1},{9,13},{13,9},{2,6},{6,2},{1... | collective-permute-start | bytes 589832 | tf_op jit(solution)/shard_map/ppermute | solution.py:21
  27.7 3.5 %collective-permute-done.4 = bf16[512,256]{1,0:T(8,128)(2,1)S(1)} collective-permute-done((bf16[512,256]{1,0:T(8,128)(2,1)S(1)}, bf16[512,256]{1,0:T(8,128)(2,1)S(1)}, u32[]{:S(2)}, u32[]{:S(2)}) %collective-permute-start.4) | collective-permute-done | bytes 262176 | tf_op jit(solution)/shard_map/ppermute | solution.py:21
  31.9 1.6 %collective-permute-start.6 = (bf16[512,128]{1,0:T(8,128)(2,1)S(1)}, bf16[512,128]{1,0:T(8,128)(2,1)S(1)}, u32[]{:S(2)}, u32[]{:S(2)}) collective-permute-start(bf16[512,128]{1,0:T(8,128)(2,1)S(1)} %pad_maximum_fusion.11), channel_id=1, source_target_pairs={{0,4},{4,0},{8,12},{12,8},{1,5},{5,1},{9,13},{13,9},{2,6},{6,2},{1... | collective-permute-start | bytes 393224 | tf_op jit(solution)/shard_map/ppermute | solution.py:21
  33.6 3.5 %collective-permute-done.6 = bf16[512,128]{1,0:T(8,128)(2,1)S(1)} collective-permute-done((bf16[512,128]{1,0:T(8,128)(2,1)S(1)}, bf16[512,128]{1,0:T(8,128)(2,1)S(1)}, u32[]{:S(2)}, u32[]{:S(2)}) %collective-permute-start.6) | collective-permute-done | bytes 131104 | tf_op jit(solution)/shard_map/ppermute | solution.py:21
  37.9 5.0 %collective-permute-done.8 = bf16[256,128]{1,0:T(8,128)(2,1)S(1)} collective-permute-done((bf16[256,128]{1,0:T(8,128)(2,1)S(1)}, bf16[256,128]{1,0:T(8,128)(2,1)S(1)}, u32[]{:S(2)}, u32[]{:S(2)}) %collective-permute-start.8) | collective-permute-done | bytes 65568 | tf_op jit(solution)/shard_map/ppermute | solution.py:21
  43.2 1.5 %collective-permute-start.9 = (bf16[2,128,256]{1,2,0:T(8,128)(2,1)S(1)}, bf16[2,128,256]{1,2,0:T(8,128)(2,1)S(1)}, u32[]{:S(2)}, u32[]{:S(2)}) collective-permute-start(bf16[2,128,256]{1,2,0:T(8,128)(2,1)S(1)} %pad_maximum_fusion.14), channel_id=1, source_target_pairs={{0,2},{2,0},{1,3},{3,1},{4,6},{6,4},{5,7},{7,5},{8,10},{10,8},{9,1... | collective-permute-start | bytes 393224 | tf_op jit(solution)/shard_map/ppermute | solution.py:21
  44.8 3.4 %collective-permute-done.9 = bf16[2,128,256]{1,2,0:T(8,128)(2,1)S(1)} collective-permute-done((bf16[2,128,256]{1,2,0:T(8,128)(2,1)S(1)}, bf16[2,128,256]{1,2,0:T(8,128)(2,1)S(1)}, u32[]{:S(2)}, u32[]{:S(2)}) %collective-permute-start.9) | collective-permute-done | bytes 131104 | tf_op jit(solution)/shard_map/ppermute | solution.py:21
  49.4 1.3 %collective-permute-done.10 = bf16[3,128,512]{1,2,0:T(8,128)(2,1)S(1)} collective-permute-done((bf16[3,128,512]{1,2,0:T(8,128)(2,1)S(1)}, bf16[3,128,512]{1,2,0:T(8,128)(2,1)S(1)}, u32[]{:S(2)}, u32[]{:S(2)}) %collective-permute-start.10) | collective-permute-done | bytes 393248 | tf_op jit(solution)/shard_map/ppermute | solution.py:21
  50.6 1.2 %fusion.9 = bf16[3,128,1024]{1,2,0:T(8,128)(2,1)S(1)} fusion(s32[]{:T(128)S(6)} %select_n.79, bf16[1,128,512]{1,2,0:T(8,128)(2,1)S(1)} %copy.16, bf16[2,128,512]{1,2,0:T(8,128)(2,1)S(1)} %fusion.32, bf16[3,128,512]{1,2,0:T(8,128)(2,1)S(1)} %collective-permute-done.10), kind=kLoop, calls=%fused_computation.26 | loop fusion | flops 3932160 | bytes 1572868 | tf_op jit(solution)/shard_map/concatenate | solution.py:44
  53.3 1.8 %fusion = bf16[512,1024]{1,0:T(8,128)(2,1)} fusion(f32[1024,512]{0,1:T(8,128)S(1)} %fusion.34, f32[1024,512]{0,1:T(8,128)S(1)} %fusion.35, f32[1024,512]{0,1:T(8,128)S(1)} %fusion.36, f32[1024,512]{0,1:T(8,128)S(1)} %fusion.37, bf16[512,512]{1,0:T(8,128)(2,1)S(1)} %copy-done.2, bf16[512,1024]{1,0:T(8,128)(2,1)S(1)} %copy-done), kind=kOutput, calls=%fused_computation.1 | convolution fusion | flops 539492352 | bytes 11010048 | tf_op jit(solution)/shard_map/dot_general | solution.py:52
  (111 shorter events, 8.9 us)
Async XLA Ops:
  0.0 9.4 %copy-start = (bf16[512,1024]{1,0:T(8,128)(2,1)S(1)}, bf16[512,1024]{1,0:T(8,128)(2,1)}, u32[]{:S(2)}) copy-start(bf16[512,1024]{1,0:T(8,128)(2,1)} %param.5) | copy-start | bytes 3145732
  0.0 5.9 %copy-start.1 = (bf16[4,512,128]{2,1,0:T(8,128)(2,1)S(1)}, bf16[4,512,128]{2,1,0:T(8,128)(2,1)}, u32[]{:S(2)}) copy-start(bf16[4,512,128]{2,1,0:T(8,128)(2,1)} %param.7) | copy-start | bytes 1572868
  0.0 6.1 %slice-start = ((bf16[4,512,128]{2,1,0:T(8,128)(2,1)}), bf16[2,512,128]{2,1,0:T(8,128)(2,1)S(1)}, s32[]{:S(2)}) async-start(bf16[4,512,128]{2,1,0:T(8,128)(2,1)} %param.7), calls=%async_computation | async-start | bytes 524288 | tf_op jit(solution)/shard_map/slice | solution.py:57
  0.0 6.5 %slice-start.1 = ((bf16[4,512,128]{2,1,0:T(8,128)(2,1)}), bf16[3,512,128]{2,1,0:T(8,128)(2,1)S(1)}, s32[]{:S(2)}) async-start(bf16[4,512,128]{2,1,0:T(8,128)(2,1)} %param.7), calls=%async_computation.1 | async-start | bytes 786432 | tf_op jit(solution)/shard_map/slice | solution.py:57
  0.0 5.9 %copy-start.3 = (bf16[4,512,128]{2,1,0:T(8,128)(2,1)S(1)}, bf16[4,512,128]{2,1,0:T(8,128)(2,1)}, u32[]{:S(2)}) copy-start(bf16[4,512,128]{2,1,0:T(8,128)(2,1)} %param.8) | copy-start | bytes 1572868
  1.2 5.1 %copy-start.15 = (bf16[128,128]{1,0:T(8,128)(2,1)}, bf16[128,128]{1,0:T(8,128)(2,1)S(1)}, u32[]{:S(2)}) copy-start(bf16[128,128]{1,0:T(8,128)(2,1)S(1)} %get-tuple-element.41) | copy-start | bytes 98308
  1.2 5.1 %copy-start.17 = (bf16[128,128]{1,0:T(8,128)(2,1)}, bf16[128,128]{1,0:T(8,128)(2,1)S(1)}, u32[]{:S(2)}) copy-start(bf16[128,128]{1,0:T(8,128)(2,1)S(1)} %get-tuple-element.42) | copy-start | bytes 98308
  1.8 11.6 %collective-permute-start.7 = (bf16[256,128]{1,0:T(8,128)(2,1)}, bf16[256,128]{1,0:T(8,128)(2,1)}, u32[]{:S(2)}, u32[]{:S(2)}) collective-permute-start(bf16[256,128]{1,0:T(8,128)(2,1)} %maximum_convert_fusion.3), channel_id=1, source_target_pairs={{0,8},{4,12},{8,0},{12,4},{1,9},{5,13},{9,1},{13,5},{2,10},{6,14},... | collective-permute-start | bytes 196616 | tf_op jit(solution)/shard_map/ppermute | solution.py:21
  7.0 6.3 %copy-start.7 = (bf16[128,128]{1,0:T(8,128)(2,1)}, bf16[128,128]{1,0:T(8,128)(2,1)S(1)}, u32[]{:S(2)}) copy-start(bf16[128,128]{1,0:T(8,128)(2,1)S(1)} %get-tuple-element.67) | copy-start | bytes 98308
  7.0 6.3 %copy-start.9 = (bf16[128,128]{1,0:T(8,128)(2,1)}, bf16[128,128]{1,0:T(8,128)(2,1)S(1)}, u32[]{:S(2)}) copy-start(bf16[128,128]{1,0:T(8,128)(2,1)S(1)} %get-tuple-element.68) | copy-start | bytes 98308
  7.9 6.3 %collective-permute-start = (f32[1024,128]{1,0:T(8,128)}, f32[1024,128]{1,0:T(8,128)}, u32[]{:S(2)}, u32[]{:S(2)}) collective-permute-start(f32[1024,128]{1,0:T(8,128)} %pad_maximum_fusion), channel_id=1, source_target_pairs={{0,1},{1,0},{2,3},{3,2},{4,5},{5,4},{6,7},{7,6},{8,9},{9,8},{10,11... | collective-permute-start | bytes 1572872 | tf_op jit(solution)/shard_map/ppermute | solution.py:21
  10.8 7.1 %collective-permute-start.1 = (bf16[128,1024]{1,0:T(8,128)(2,1)}, bf16[128,1024]{1,0:T(8,128)(2,1)}, u32[]{:S(2)}, u32[]{:S(2)}) collective-permute-start(bf16[128,1024]{1,0:T(8,128)(2,1)} %fusion.3), channel_id=1, source_target_pairs={{0,1},{1,0},{2,3},{3,2},{4,5},{5,4},{6,7},{7,6},{8,9},{9,8},{10,11... | collective-permute-start | bytes 786440 | tf_op jit(solution)/shard_map/ppermute | solution.py:21
  12.9 6.8 %collective-permute-start.3 = (f32[3,128,512]{2,1,0:T(8,128)}, f32[3,128,512]{2,1,0:T(8,128)}, u32[]{:S(2)}, u32[]{:S(2)}) collective-permute-start(f32[3,128,512]{2,1,0:T(8,128)} %convolution_add_fusion), channel_id=1, source_target_pairs={{0,1},{1,0},{2,3},{3,2},{4,5},{5,4},{6,7},{7,6},{8,9},{9,8},{10,11... | collective-permute-start | bytes 2359304 | tf_op jit(solution)/shard_map/ppermute | solution.py:21
  15.4 10.6 %collective-permute-start.2 = (f32[640,128]{1,0:T(8,128)S(1)}, f32[640,128]{1,0:T(8,128)S(1)}, u32[]{:S(2)}, u32[]{:S(2)}) collective-permute-start(f32[640,128]{1,0:T(8,128)S(1)} %pad_maximum_fusion.2), channel_id=1, source_target_pairs={{0,2},{2,0},{1,3},{3,1},{4,6},{6,4},{5,7},{7,5},{8,10},{10,8},{9,1... | collective-permute-start | bytes 983048 | tf_op jit(solution)/shard_map/ppermute | solution.py:21
  21.5 6.1 %copy-start.8 = (bf16[128,128]{1,0:T(8,128)(2,1)S(1)}, bf16[128,128]{1,0:T(8,128)(2,1)}, u32[]{:S(2)}) copy-start(bf16[128,128]{1,0:T(8,128)(2,1)} %copy-done.7) | copy-start | bytes 98308
  21.5 6.1 %copy-start.10 = (bf16[128,128]{1,0:T(8,128)(2,1)S(1)}, bf16[128,128]{1,0:T(8,128)(2,1)}, u32[]{:S(2)}) copy-start(bf16[128,128]{1,0:T(8,128)(2,1)} %copy-done.9) | copy-start | bytes 98308
  21.7 9.5 %collective-permute-start.4 = (bf16[512,256]{1,0:T(8,128)(2,1)S(1)}, bf16[512,256]{1,0:T(8,128)(2,1)S(1)}, u32[]{:S(2)}, u32[]{:S(2)}) collective-permute-start(bf16[512,256]{1,0:T(8,128)(2,1)S(1)} %pad_maximum_fusion.3), channel_id=1, source_target_pairs={{0,2},{2,0},{1,3},{3,1},{4,6},{6,4},{5,7},{7,5},{8,10},{10,8},{9,1... | collective-permute-start | bytes 786440 | tf_op jit(solution)/shard_map/ppermute | solution.py:21
  26.0 7.5 %collective-permute-start.5 = (f32[384,128]{1,0:T(8,128)S(1)}, f32[384,128]{1,0:T(8,128)S(1)}, u32[]{:S(2)}, u32[]{:S(2)}) collective-permute-start(f32[384,128]{1,0:T(8,128)S(1)} %pad_maximum_fusion.4), channel_id=1, source_target_pairs={{0,4},{4,0},{8,12},{12,8},{1,5},{5,1},{9,13},{13,9},{2,6},{6,2},{1... | collective-permute-start | bytes 589832 | tf_op jit(solution)/shard_map/ppermute | solution.py:21
  31.9 5.2 %collective-permute-start.6 = (bf16[512,128]{1,0:T(8,128)(2,1)S(1)}, bf16[512,128]{1,0:T(8,128)(2,1)S(1)}, u32[]{:S(2)}, u32[]{:S(2)}) collective-permute-start(bf16[512,128]{1,0:T(8,128)(2,1)S(1)} %pad_maximum_fusion.11), channel_id=1, source_target_pairs={{0,4},{4,0},{8,12},{12,8},{1,5},{5,1},{9,13},{13,9},{2,6},{6,2},{1... | collective-permute-start | bytes 393224 | tf_op jit(solution)/shard_map/ppermute | solution.py:21
  37.1 11.9 %copy-start.4 = (bf16[4,512,128]{2,1,0:T(8,128)(2,1)S(1)}, bf16[4,512,128]{2,1,0:T(8,128)(2,1)}, u32[]{:S(2)}) copy-start(bf16[4,512,128]{2,1,0:T(8,128)(2,1)} %param.8) | copy-start | bytes 1572868
  37.1 11.9 %copy-start.6 = (bf16[256,1024]{1,0:T(8,128)(2,1)S(1)}, bf16[256,1024]{1,0:T(8,128)(2,1)}, u32[]{:S(2)}) copy-start(bf16[256,1024]{1,0:T(8,128)(2,1)} %copy-done.5) | copy-start | bytes 1572868
  37.7 5.2 %collective-permute-start.8 = (bf16[256,128]{1,0:T(8,128)(2,1)S(1)}, bf16[256,128]{1,0:T(8,128)(2,1)S(1)}, u32[]{:S(2)}, u32[]{:S(2)}) collective-permute-start(bf16[256,128]{1,0:T(8,128)(2,1)S(1)} %pad_maximum_fusion.15), channel_id=1, source_target_pairs={{0,8},{4,12},{8,0},{12,4},{1,9},{5,13},{9,1},{13,5},{2,10},{6,14},... | collective-permute-start | bytes 196616 | tf_op jit(solution)/shard_map/ppermute | solution.py:21
  43.2 5.0 %collective-permute-start.9 = (bf16[2,128,256]{1,2,0:T(8,128)(2,1)S(1)}, bf16[2,128,256]{1,2,0:T(8,128)(2,1)S(1)}, u32[]{:S(2)}, u32[]{:S(2)}) collective-permute-start(bf16[2,128,256]{1,2,0:T(8,128)(2,1)S(1)} %pad_maximum_fusion.14), channel_id=1, source_target_pairs={{0,2},{2,0},{1,3},{3,1},{4,6},{6,4},{5,7},{7,5},{8,10},{10,8},{9,1... | collective-permute-start | bytes 393224 | tf_op jit(solution)/shard_map/ppermute | solution.py:21
  48.8 1.8 %collective-permute-start.10 = (bf16[3,128,512]{1,2,0:T(8,128)(2,1)S(1)}, bf16[3,128,512]{1,2,0:T(8,128)(2,1)S(1)}, u32[]{:S(2)}, u32[]{:S(2)}) collective-permute-start(bf16[3,128,512]{1,2,0:T(8,128)(2,1)S(1)} %pad_maximum_fusion.1), channel_id=1, source_target_pairs={{0,1},{1,0},{2,3},{3,2},{4,5},{5,4},{6,7},{7,6},{8,9},{9,8},{10,11... | collective-permute-start | bytes 1179656 | tf_op jit(solution)/shard_map/ppermute | solution.py:21
  (8 other events, 21.4 us)

commit v30 on v28

--- a/solution.py
+++ b/solution.py
@@ -138,7 +138,8 @@
                 recv = got[2 * rank :].reshape(n, rank, w).astype(F32)
                 rest = keep + recv
         stacked = jnp.concatenate([mine_b, theirs_b], axis=0)
-        coefs = jnp.dot(couple[s], stacked, preferred_element_type=F32).astype(BF16)
+        rows = couple[s] if s < levels - 1 else couple[s][:rank]
+        coefs = jnp.dot(rows, stacked, preferred_element_type=F32).astype(BF16)
         own_coefs.append(coefs[:rank])
         if s < levels - 1:
             w = coefs.shape[1] // 2

time: 55.6 us -> 55.6 us (level)
  no operation moved by 1% of the time
where the time goes in v30:
time: 55.6 us; the launch traced here: 55.1 us
  waiting for transfers between devices  20.2 us (36%)
  matrix products  13.7 us (25%)
  starting transfers between devices  11.9 us (21%)
  other arithmetic  4.69 us (8%)
  local copies, waits for them, and re-layouts  4.03 us (7%)
  between operations  0.73 us (1%)
    ppermute x11, waiting for transfers between devices, swap(): return lax.ppermute(x, axis, [(i, i ^ 1 << stride) for i in range(n)])  20.2 us
    ppermute x11, starting transfers between devices, swap(): return lax.ppermute(x, axis, [(i, i ^ 1 << stride) for i in range(n)])  11.9 us
    dot_general x3, matrix products, project(): jnp.einsum('lrj,jt->lrt', vl_lo[lv], x, preferred_element_type=F32)  3.79 us
    dot_general x4, matrix products, on_device(): coefs = jnp.dot(rows, stacked, preferred_element_type=F32).astype(BF16)  2.01 us
    dot_general x1, matrix products, on_device(): c0 = jnp.dot(leaf_inverse, templates, preferred_element_type=F32)  1.83 us
    concatenate x2, other arithmetic, gather_half(): both = jnp.concatenate([x, swap(x, bit, bits), x], axis=-1)  1.79 us
    dot_general x4, matrix products, on_device(): current = current - jnp.dot(u_basis[s], full[s], preferred_element_type=F32)  1.73 us
    slice x4, local copies, waits for them, and re-layouts, on_device(): theirs_c.append(jnp.concatenate([theirs[:rank], theirs[rank:]], axis=1))  1.69 us
  transfers between devices with their start and end apart: 11, of which 6 were waited for; matrix products, arithmetic and copies ran while one was open for 26% of the time, Pallas kernels for 0%

profile of v30, /device:TPU:0, one launch (start us, length us, event | category | flops | bytes accessed | tf_op | source)
XLA Modules:
  0.0 55.1 jit_solution(1311867959521704686)
XLA Ops:
  0.0 1.1 %slice_bitcast_fusion.12 = (bf16[128,256]{1,0:T(8,128)(2,1)S(1)}, bf16[128,256]{1,0:T(8,128)(2,1)S(1)}, bf16[128,256]{1,0:T(8,128)(2,1)S(1)}, bf16[128,256]{1,0:T(8,128)(2,1)S(1)}) fusion(bf16[4,1,128,256]{3,2,1,0:T(8,128)(2,1)} %param.9), kind=kLoop, calls=%fused_computation.164 | loop fusion | bytes 524288 | tf_op jit(solution)/shard_map/squeeze | solution.py:85
  1.2 0.6 %maximum_convert_fusion.3 = bf16[256,128]{1,0:T(8,128)(2,1)} fusion(bf16[128,128]{1,0:T(8,128)(2,1)S(1)} %get-tuple-element.42, bf16[128,128]{1,0:T(8,128)(2,1)S(1)} %get-tuple-element.41), kind=kLoop, calls=%fused_computation.162 | loop fusion | flops 131072 | bytes 131072 | tf_op jit(solution)/shard_map/convert_element_type | solution.py:64
  1.8 4.0 %collective-permute-start.7 = (bf16[256,128]{1,0:T(8,128)(2,1)}, bf16[256,128]{1,0:T(8,128)(2,1)}, u32[]{:S(2)}, u32[]{:S(2)}) collective-permute-start(bf16[256,128]{1,0:T(8,128)(2,1)} %maximum_convert_fusion.3), channel_id=1, source_target_pairs={{0,8},{4,12},{8,0},{12,4},{1,9},{5,13},{9,1},{13,5},{2,10},{6,14},... | collective-permute-start | bytes 196616 | tf_op jit(solution)/shard_map/ppermute | solution.py:21
  7.1 0.8 %pad_maximum_fusion = f32[1024,128]{1,0:T(8,128)} fusion(f32[128,128]{1,0:T(8,128)S(1)} %fusion.78, f32[256,128]{1,0:T(8,128)S(1)} %fusion.82, f32[384,128]{1,0:T(8,128)S(1)} %fusion.85, f32[256,128]{1,0:T(8,128)S(1)} %maximum_convert_fusion), kind=kLoop, calls=%fused_computation.30 | loop fusion | flops 393216 | bytes 1048576 | tf_op jit(solution)/shard_map/concatenate | solution.py:66
  7.9 1.5 %subtract_convert_fusion = (bf16[4,128,512]{2,1,0:T(8,128)(2,1)S(1)}, bf16[4,128,512]{2,1,0:T(8,128)(2,1)S(1)}) fusion(bf16[4,512,128]{2,1,0:T(8,128)(2,1)S(1)} %copy-done.1, bf16[512,512]{1,0:T(8,128)(2,1)} %param.6), kind=kOutput, calls=%fused_computation.25 | convolution fusion | flops 269484032 | bytes 2097152 | tf_op jit(solution)/shard_map/lir,ij->lrj/dot_general | solution.py:95
  9.8 1.0 %fusion.3 = bf16[128,1024]{1,0:T(8,128)(2,1)} fusion(f32[128,1024]{1,0:T(8,128)S(1)} %fusion.62, bf16[512,1024]{1,0:T(8,128)(2,1)S(1)} %copy-done, bf16[4,128,512]{2,1,0:T(8,128)(2,1)S(1)} %get-tuple-element.5), kind=kOutput, calls=%fused_computation.11 | convolution fusion | flops 134479872 | bytes 1966080 | tf_op jit(solution)/shard_map/lrj,jt->lrt/dot_general | solution.py:102
  11.7 1.3 %convolution_add_fusion = f32[3,128,512]{2,1,0:T(8,128)} fusion(f32[3,128,512]{2,1,0:T(8,128)S(1)} %fusion.16, bf16[4,128,512]{2,1,0:T(8,128)(2,1)S(1)} %get-tuple-element.5, bf16[512,1024]{1,0:T(8,128)(2,1)S(1)} %copy-done, s32[]{:T(128)S(6)} %select_n.69), kind=kOutput, calls=%fused_computation.6 | convolution fusion | flops 201523200 | bytes 2621444 | tf_op jit(solution)/shard_map/lrj,jt->lrt/dot_general | solution.py:102
  13.4 0.8 %fusion.132 = (bf16[128,128]{1,0:T(8,128)(2,1)S(1)}, bf16[128,128]{1,0:T(8,128)(2,1)S(1)}) fusion(bf16[256,128]{1,0:T(8,128)(2,1)} %collective-permute-done.7), kind=kLoop, calls=%fused_computation.204 | loop fusion | bytes 131072 | tf_op jit(solution)/shard_map/slice | solution.py:68
  14.2 1.1 %fusion.124 = (f32[384,128]{1,0:T(8,128)S(1)}, f32[384,128]{1,0:T(8,128)S(1)}) fusion(f32[1024,128]{1,0:T(8,128)} %collective-permute-done, f32[128,128]{1,0:T(8,128)S(1)} %fusion.78, f32[256,128]{1,0:T(8,128)S(1)} %fusion.82), kind=kLoop, calls=%fused_computation.196 | loop fusion | flops 98304 | bytes 983040 | tf_op jit(solution)/shard_map/slice | solution.py:72
  15.4 1.6 %collective-permute-start.2 = (f32[640,128]{1,0:T(8,128)S(1)}, f32[640,128]{1,0:T(8,128)S(1)}, u32[]{:S(2)}, u32[]{:S(2)}) collective-permute-start(f32[640,128]{1,0:T(8,128)S(1)} %pad_maximum_fusion.2), channel_id=1, source_target_pairs={{0,2},{2,0},{1,3},{3,1},{4,6},{6,4},{5,7},{7,5},{8,10},{10,8},{9,1... | collective-permute-start | bytes 983048 | tf_op jit(solution)/shard_map/ppermute | solution.py:21
  16.9 0.9 %fusion.123 = (bf16[128,128]{1,0:T(8,128)(2,1)S(1)}, bf16[128,128]{1,0:T(8,128)(2,1)S(1)}) fusion(f32[1024,128]{1,0:T(8,128)} %collective-permute-done), kind=kLoop, calls=%fused_computation.195 | loop fusion | bytes 131072 | tf_op jit(solution)/shard_map/slice | solution.py:68
  17.9 1.3 %convolution_convert_fusion = bf16[256,1024]{1,0:T(8,128)(2,1)S(1)} fusion(bf16[128,1024]{1,0:T(8,128)(2,1)} %collective-permute-done.1, bf16[128,1024]{1,0:T(8,128)(2,1)} %fusion.3, bf16[256,128]{1,0:T(8,128)(2,1)S(1)} %get-tuple-element.34, bf16[256,128]{1,0:T(8,128)(2,1)S(1)} %get-tuple-element.33), kind=kOutput, calls=%fused_computation.5 | convolution fusion | flops 135528448 | bytes 1179648 | tf_op jit(solution)/shard_map/dot_general | solution.py:142
  20.0 1.5 %fusion.2 = f32[3,128,512]{2,1,0:T(8,128)S(1)} fusion(f32[3,128,512]{2,1,0:T(8,128)S(1)} %bitcast.124, f32[3,128,512]{2,1,0:T(8,128)} %collective-permute-done.3, f32[3,128,512]{2,1,0:T(8,128)S(1)} %fusion.19, bf16[4,128,512]{2,1,0:T(8,128)(2,1)S(1)} %get-tuple-element.5, bf16[512,1024]{1,0:T(8,128)(2,1)S(1)} %copy-done, s32[]{:T(128)S(6)} %select_n.68), kind=kOutput, calls=%fused_computation.9 | convolution fusion | flops 201916416 | bytes 4194308 | tf_op jit(solution)/shard_map/lrj,jt->lrt/dot_general | solution.py:102
  22.3 3.6 %collective-permute-done.2 = f32[640,128]{1,0:T(8,128)S(1)} collective-permute-done((f32[640,128]{1,0:T(8,128)S(1)}, f32[640,128]{1,0:T(8,128)S(1)}, u32[]{:S(2)}, u32[]{:S(2)}) %collective-permute-start.2) | collective-permute-done | bytes 327712 | tf_op jit(solution)/shard_map/ppermute | solution.py:21
  26.0 1.6 %collective-permute-start.5 = (f32[384,128]{1,0:T(8,128)S(1)}, f32[384,128]{1,0:T(8,128)S(1)}, u32[]{:S(2)}, u32[]{:S(2)}) collective-permute-start(f32[384,128]{1,0:T(8,128)S(1)} %pad_maximum_fusion.4), channel_id=1, source_target_pairs={{0,4},{4,0},{8,12},{12,8},{1,5},{5,1},{9,13},{13,9},{2,6},{6,2},{1... | collective-permute-start | bytes 589832 | tf_op jit(solution)/shard_map/ppermute | solution.py:21
  27.7 3.5 %collective-permute-done.4 = bf16[512,256]{1,0:T(8,128)(2,1)S(1)} collective-permute-done((bf16[512,256]{1,0:T(8,128)(2,1)S(1)}, bf16[512,256]{1,0:T(8,128)(2,1)S(1)}, u32[]{:S(2)}, u32[]{:S(2)}) %collective-permute-start.4) | collective-permute-done | bytes 262176 | tf_op jit(solution)/shard_map/ppermute | solution.py:21
  31.9 1.6 %collective-permute-start.6 = (bf16[512,128]{1,0:T(8,128)(2,1)S(1)}, bf16[512,128]{1,0:T(8,128)(2,1)S(1)}, u32[]{:S(2)}, u32[]{:S(2)}) collective-permute-start(bf16[512,128]{1,0:T(8,128)(2,1)S(1)} %pad_maximum_fusion.13), channel_id=1, source_target_pairs={{0,4},{4,0},{8,12},{12,8},{1,5},{5,1},{9,13},{13,9},{2,6},{6,2},{1... | collective-permute-start | bytes 393224 | tf_op jit(solution)/shard_map/ppermute | solution.py:21
  33.6 3.5 %collective-permute-done.6 = bf16[512,128]{1,0:T(8,128)(2,1)S(1)} collective-permute-done((bf16[512,128]{1,0:T(8,128)(2,1)S(1)}, bf16[512,128]{1,0:T(8,128)(2,1)S(1)}, u32[]{:S(2)}, u32[]{:S(2)}) %collective-permute-start.6) | collective-permute-done | bytes 131104 | tf_op jit(solution)/shard_map/ppermute | solution.py:21
  37.9 5.0 %collective-permute-done.8 = bf16[256,128]{1,0:T(8,128)(2,1)S(1)} collective-permute-done((bf16[256,128]{1,0:T(8,128)(2,1)S(1)}, bf16[256,128]{1,0:T(8,128)(2,1)S(1)}, u32[]{:S(2)}, u32[]{:S(2)}) %collective-permute-start.8) | collective-permute-done | bytes 65568 | tf_op jit(solution)/shard_map/ppermute | solution.py:21
  43.1 1.5 %collective-permute-start.9 = (bf16[2,128,256]{1,2,0:T(8,128)(2,1)S(1)}, bf16[2,128,256]{1,2,0:T(8,128)(2,1)S(1)}, u32[]{:S(2)}, u32[]{:S(2)}) collective-permute-start(bf16[2,128,256]{1,2,0:T(8,128)(2,1)S(1)} %pad_maximum_fusion.16), channel_id=1, source_target_pairs={{0,2},{2,0},{1,3},{3,1},{4,6},{6,4},{5,7},{7,5},{8,10},{10,8},{9,1... | collective-permute-start | bytes 393224 | tf_op jit(solution)/shard_map/ppermute | solution.py:21
  44.8 3.4 %collective-permute-done.9 = bf16[2,128,256]{1,2,0:T(8,128)(2,1)S(1)} collective-permute-done((bf16[2,128,256]{1,2,0:T(8,128)(2,1)S(1)}, bf16[2,128,256]{1,2,0:T(8,128)(2,1)S(1)}, u32[]{:S(2)}, u32[]{:S(2)}) %collective-permute-start.9) | collective-permute-done | bytes 131104 | tf_op jit(solution)/shard_map/ppermute | solution.py:21
  49.4 1.3 %collective-permute-done.10 = bf16[3,128,512]{1,2,0:T(8,128)(2,1)S(1)} collective-permute-done((bf16[3,128,512]{1,2,0:T(8,128)(2,1)S(1)}, bf16[3,128,512]{1,2,0:T(8,128)(2,1)S(1)}, u32[]{:S(2)}, u32[]{:S(2)}) %collective-permute-start.10) | collective-permute-done | bytes 393248 | tf_op jit(solution)/shard_map/ppermute | solution.py:21
  50.6 1.2 %fusion.10 = bf16[3,128,1024]{1,2,0:T(8,128)(2,1)S(1)} fusion(s32[]{:T(128)S(6)} %select_n.79, bf16[1,128,512]{1,2,0:T(8,128)(2,1)S(1)} %copy.18, bf16[2,128,512]{1,2,0:T(8,128)(2,1)S(1)} %fusion.33, bf16[3,128,512]{1,2,0:T(8,128)(2,1)S(1)} %collective-permute-done.10), kind=kLoop, calls=%fused_computation.28 | loop fusion | flops 3932160 | bytes 1572868 | tf_op jit(solution)/shard_map/concatenate | solution.py:44
  53.3 1.8 %fusion = bf16[512,1024]{1,0:T(8,128)(2,1)} fusion(f32[1024,512]{0,1:T(8,128)S(1)} %fusion.35, f32[1024,512]{0,1:T(8,128)S(1)} %fusion.36, f32[1024,512]{0,1:T(8,128)S(1)} %fusion.37, f32[1024,512]{0,1:T(8,128)S(1)} %fusion.38, bf16[512,512]{1,0:T(8,128)(2,1)S(1)} %copy-done.2, bf16[512,1024]{1,0:T(8,128)(2,1)S(1)} %copy-done), kind=kOutput, calls=%fused_computation.1 | convolution fusion | flops 539492352 | bytes 11010048 | tf_op jit(solution)/shard_map/dot_general | solution.py:52
  (110 shorter events, 8.9 us)
Async XLA Ops:
  0.0 9.4 %copy-start = (bf16[512,1024]{1,0:T(8,128)(2,1)S(1)}, bf16[512,1024]{1,0:T(8,128)(2,1)}, u32[]{:S(2)}) copy-start(bf16[512,1024]{1,0:T(8,128)(2,1)} %param.5) | copy-start | bytes 3145732
  0.0 5.9 %copy-start.1 = (bf16[4,512,128]{2,1,0:T(8,128)(2,1)S(1)}, bf16[4,512,128]{2,1,0:T(8,128)(2,1)}, u32[]{:S(2)}) copy-start(bf16[4,512,128]{2,1,0:T(8,128)(2,1)} %param.7) | copy-start | bytes 1572868
  0.0 6.1 %slice-start = ((bf16[4,512,128]{2,1,0:T(8,128)(2,1)}), bf16[2,512,128]{2,1,0:T(8,128)(2,1)S(1)}, s32[]{:S(2)}) async-start(bf16[4,512,128]{2,1,0:T(8,128)(2,1)} %param.7), calls=%async_computation | async-start | bytes 524288 | tf_op jit(solution)/shard_map/slice | solution.py:57
  0.0 6.5 %slice-start.1 = ((bf16[4,512,128]{2,1,0:T(8,128)(2,1)}), bf16[3,512,128]{2,1,0:T(8,128)(2,1)S(1)}, s32[]{:S(2)}) async-start(bf16[4,512,128]{2,1,0:T(8,128)(2,1)} %param.7), calls=%async_computation.1 | async-start | bytes 786432 | tf_op jit(solution)/shard_map/slice | solution.py:57
  0.0 5.9 %copy-start.3 = (bf16[4,512,128]{2,1,0:T(8,128)(2,1)S(1)}, bf16[4,512,128]{2,1,0:T(8,128)(2,1)}, u32[]{:S(2)}) copy-start(bf16[4,512,128]{2,1,0:T(8,128)(2,1)} %param.8) | copy-start | bytes 1572868
  1.2 5.1 %copy-start.15 = (bf16[128,128]{1,0:T(8,128)(2,1)}, bf16[128,128]{1,0:T(8,128)(2,1)S(1)}, u32[]{:S(2)}) copy-start(bf16[128,128]{1,0:T(8,128)(2,1)S(1)} %get-tuple-element.41) | copy-start | bytes 98308
  1.2 5.1 %copy-start.17 = (bf16[128,128]{1,0:T(8,128)(2,1)}, bf16[128,128]{1,0:T(8,128)(2,1)S(1)}, u32[]{:S(2)}) copy-start(bf16[128,128]{1,0:T(8,128)(2,1)S(1)} %get-tuple-element.42) | copy-start | bytes 98308
  1.8 11.6 %collective-permute-start.7 = (bf16[256,128]{1,0:T(8,128)(2,1)}, bf16[256,128]{1,0:T(8,128)(2,1)}, u32[]{:S(2)}, u32[]{:S(2)}) collective-permute-start(bf16[256,128]{1,0:T(8,128)(2,1)} %maximum_convert_fusion.3), channel_id=1, source_target_pairs={{0,8},{4,12},{8,0},{12,4},{1,9},{5,13},{9,1},{13,5},{2,10},{6,14},... | collective-permute-start | bytes 196616 | tf_op jit(solution)/shard_map/ppermute | solution.py:21
  7.0 6.3 %copy-start.7 = (bf16[128,128]{1,0:T(8,128)(2,1)}, bf16[128,128]{1,0:T(8,128)(2,1)S(1)}, u32[]{:S(2)}) copy-start(bf16[128,128]{1,0:T(8,128)(2,1)S(1)} %get-tuple-element.67) | copy-start | bytes 98308
  7.0 6.3 %copy-start.9 = (bf16[128,128]{1,0:T(8,128)(2,1)}, bf16[128,128]{1,0:T(8,128)(2,1)S(1)}, u32[]{:S(2)}) copy-start(bf16[128,128]{1,0:T(8,128)(2,1)S(1)} %get-tuple-element.68) | copy-start | bytes 98308
  7.9 6.3 %collective-permute-start = (f32[1024,128]{1,0:T(8,128)}, f32[1024,128]{1,0:T(8,128)}, u32[]{:S(2)}, u32[]{:S(2)}) collective-permute-start(f32[1024,128]{1,0:T(8,128)} %pad_maximum_fusion), channel_id=1, source_target_pairs={{0,1},{1,0},{2,3},{3,2},{4,5},{5,4},{6,7},{7,6},{8,9},{9,8},{10,11... | collective-permute-start | bytes 1572872 | tf_op jit(solution)/shard_map/ppermute | solution.py:21
  10.8 7.1 %collective-permute-start.1 = (bf16[128,1024]{1,0:T(8,128)(2,1)}, bf16[128,1024]{1,0:T(8,128)(2,1)}, u32[]{:S(2)}, u32[]{:S(2)}) collective-permute-start(bf16[128,1024]{1,0:T(8,128)(2,1)} %fusion.3), channel_id=1, source_target_pairs={{0,1},{1,0},{2,3},{3,2},{4,5},{5,4},{6,7},{7,6},{8,9},{9,8},{10,11... | collective-permute-start | bytes 786440 | tf_op jit(solution)/shard_map/ppermute | solution.py:21
  12.9 6.8 %collective-permute-start.3 = (f32[3,128,512]{2,1,0:T(8,128)}, f32[3,128,512]{2,1,0:T(8,128)}, u32[]{:S(2)}, u32[]{:S(2)}) collective-permute-start(f32[3,128,512]{2,1,0:T(8,128)} %convolution_add_fusion), channel_id=1, source_target_pairs={{0,1},{1,0},{2,3},{3,2},{4,5},{5,4},{6,7},{7,6},{8,9},{9,8},{10,11... | collective-permute-start | bytes 2359304 | tf_op jit(solution)/shard_map/ppermute | solution.py:21
  15.4 10.6 %collective-permute-start.2 = (f32[640,128]{1,0:T(8,128)S(1)}, f32[640,128]{1,0:T(8,128)S(1)}, u32[]{:S(2)}, u32[]{:S(2)}) collective-permute-start(f32[640,128]{1,0:T(8,128)S(1)} %pad_maximum_fusion.2), channel_id=1, source_target_pairs={{0,2},{2,0},{1,3},{3,1},{4,6},{6,4},{5,7},{7,5},{8,10},{10,8},{9,1... | collective-permute-start | bytes 983048 | tf_op jit(solution)/shard_map/ppermute | solution.py:21
  21.5 6.1 %copy-start.8 = (bf16[128,128]{1,0:T(8,128)(2,1)S(1)}, bf16[128,128]{1,0:T(8,128)(2,1)}, u32[]{:S(2)}) copy-start(bf16[128,128]{1,0:T(8,128)(2,1)} %copy-done.7) | copy-start | bytes 98308
  21.5 6.1 %copy-start.10 = (bf16[128,128]{1,0:T(8,128)(2,1)S(1)}, bf16[128,128]{1,0:T(8,128)(2,1)}, u32[]{:S(2)}) copy-start(bf16[128,128]{1,0:T(8,128)(2,1)} %copy-done.9) | copy-start | bytes 98308
  21.7 9.5 %collective-permute-start.4 = (bf16[512,256]{1,0:T(8,128)(2,1)S(1)}, bf16[512,256]{1,0:T(8,128)(2,1)S(1)}, u32[]{:S(2)}, u32[]{:S(2)}) collective-permute-start(bf16[512,256]{1,0:T(8,128)(2,1)S(1)} %pad_maximum_fusion.3), channel_id=1, source_target_pairs={{0,2},{2,0},{1,3},{3,1},{4,6},{6,4},{5,7},{7,5},{8,10},{10,8},{9,1... | collective-permute-start | bytes 786440 | tf_op jit(solution)/shard_map/ppermute | solution.py:21
  26.0 7.5 %collective-permute-start.5 = (f32[384,128]{1,0:T(8,128)S(1)}, f32[384,128]{1,0:T(8,128)S(1)}, u32[]{:S(2)}, u32[]{:S(2)}) collective-permute-start(f32[384,128]{1,0:T(8,128)S(1)} %pad_maximum_fusion.4), channel_id=1, source_target_pairs={{0,4},{4,0},{8,12},{12,8},{1,5},{5,1},{9,13},{13,9},{2,6},{6,2},{1... | collective-permute-start | bytes 589832 | tf_op jit(solution)/shard_map/ppermute | solution.py:21
  31.9 5.2 %collective-permute-start.6 = (bf16[512,128]{1,0:T(8,128)(2,1)S(1)}, bf16[512,128]{1,0:T(8,128)(2,1)S(1)}, u32[]{:S(2)}, u32[]{:S(2)}) collective-permute-start(bf16[512,128]{1,0:T(8,128)(2,1)S(1)} %pad_maximum_fusion.13), channel_id=1, source_target_pairs={{0,4},{4,0},{8,12},{12,8},{1,5},{5,1},{9,13},{13,9},{2,6},{6,2},{1... | collective-permute-start | bytes 393224 | tf_op jit(solution)/shard_map/ppermute | solution.py:21
  37.1 11.8 %copy-start.4 = (bf16[4,512,128]{2,1,0:T(8,128)(2,1)S(1)}, bf16[4,512,128]{2,1,0:T(8,128)(2,1)}, u32[]{:S(2)}) copy-start(bf16[4,512,128]{2,1,0:T(8,128)(2,1)} %param.8) | copy-start | bytes 1572868
  37.1 11.8 %copy-start.6 = (bf16[256,1024]{1,0:T(8,128)(2,1)S(1)}, bf16[256,1024]{1,0:T(8,128)(2,1)}, u32[]{:S(2)}) copy-start(bf16[256,1024]{1,0:T(8,128)(2,1)} %copy-done.5) | copy-start | bytes 1572868
  37.7 5.2 %collective-permute-start.8 = (bf16[256,128]{1,0:T(8,128)(2,1)S(1)}, bf16[256,128]{1,0:T(8,128)(2,1)S(1)}, u32[]{:S(2)}, u32[]{:S(2)}) collective-permute-start(bf16[256,128]{1,0:T(8,128)(2,1)S(1)} %pad_maximum_fusion.17), channel_id=1, source_target_pairs={{0,8},{4,12},{8,0},{12,4},{1,9},{5,13},{9,1},{13,5},{2,10},{6,14},... | collective-permute-start | bytes 196616 | tf_op jit(solution)/shard_map/ppermute | solution.py:21
  43.1 5.0 %collective-permute-start.9 = (bf16[2,128,256]{1,2,0:T(8,128)(2,1)S(1)}, bf16[2,128,256]{1,2,0:T(8,128)(2,1)S(1)}, u32[]{:S(2)}, u32[]{:S(2)}) collective-permute-start(bf16[2,128,256]{1,2,0:T(8,128)(2,1)S(1)} %pad_maximum_fusion.16), channel_id=1, source_target_pairs={{0,2},{2,0},{1,3},{3,1},{4,6},{6,4},{5,7},{7,5},{8,10},{10,8},{9,1... | collective-permute-start | bytes 393224 | tf_op jit(solution)/shard_map/ppermute | solution.py:21
  48.8 1.8 %collective-permute-start.10 = (bf16[3,128,512]{1,2,0:T(8,128)(2,1)S(1)}, bf16[3,128,512]{1,2,0:T(8,128)(2,1)S(1)}, u32[]{:S(2)}, u32[]{:S(2)}) collective-permute-start(bf16[3,128,512]{1,2,0:T(8,128)(2,1)S(1)} %pad_maximum_fusion.1), channel_id=1, source_target_pairs={{0,1},{1,0},{2,3},{3,2},{4,5},{5,4},{6,7},{7,6},{8,9},{9,8},{10,11... | collective-permute-start | bytes 1179656 | tf_op jit(solution)/shard_map/ppermute | solution.py:21
  (8 other events, 21.4 us)
